TPU v7x, 32 devices: a whole 2x2x4 slice. The times are simulated.
32 devices in a mesh: day: 4 (over z), dom: 8 (over y, x, core).
Axes of the slice: x: 2, y: 2, z: 4, core: 2. Of those that a mesh axis runs over, the one named last changes fastest.
Arguments:
- node_states: bfloat16 [16, 2048, 256], P('day', 'dom'), may hold values from -12 to 12
- edge_source: int32 [16, 8192], P('day', 'dom'), may hold values from 0 to 383
- edge_target: int32 [16, 8192], P('day', 'dom'), may hold values from 0 to 255
- halo_rows: int32 [16, 1024], P('day', 'dom'), may hold values from 0 to 255
- halo_count: int32 [16, 8], P('day', 'dom'), may hold values from 1 to 128, 640 in all within a row
- w_message: bfloat16 [256, 256], replicated, may hold values from -0.375 to 0.375
- w_query: bfloat16 [256, 256], replicated, may hold values from -1 to 1, as said below
- w_key: bfloat16 [256, 256], replicated, may hold values from -1 to 1, as said below
- w_value: bfloat16 [256, 256], replicated, may hold values from -0.375 to 0.375
- cotangent: bfloat16 [16, 8, 4, 64, 256], P(None, 'dom', 'day'), may hold values from -6 to 6
Outputs:
- state_grad: float32 [16, 2048, 256], P('day', 'dom')
- grad_message: float32 [256, 256], replicated
- grad_query: float32 [256, 256], replicated
- grad_key: float32 [256, 256], replicated
- grad_value: float32 [256, 256], replicated
Inputs may be any that keep to these rules, and one draw needn't show every extreme that they name: `edge_source`: indices of the extended rows: below 256 a partition's own account, from 256 on a received halo slot. `halo_rows`: rows of the sending partition's own block; repeats allowed. `halo_count`: on every day some partition has all 128 slots live. `w_query`: entries of order 256 ** -0.5. `w_key`: entries of order 256 ** -0.5.
All inputs are finite; a program needn't handle non-finite values. No bound on the sum of `halo_count` on one device may be relied on, other than what follows from the above.
Results may differ from a plain program's by a relative error of at most 0.004.
The roundings to bfloat16 on the way count: a program that leaves them out, or rounds other values in their place, can miss the bound.
Values may be sent and summed in bfloat16 or wider, within the bound.
No kernel may reach another device: no remote copies, remote signals or barrier semaphores. Data moves between devices by JAX's collectives and lax.ppermute only.
A program may use at most 64 MiB of HBM per device.

v0:
```python
import jax
import jax.numpy as jnp
from jax import lax
from jax.sharding import PartitionSpec as P

HEADS = 4


def from_behind(value, axis, steps):
    count = lax.axis_size(axis)
    pairs = [(source, (source + steps) % count) for source in range(count)]
    return lax.ppermute(value, axis, pairs)


def adjacency(sources, targets, count_rows, total_rows):
    target_hot = (targets[:, None] == jnp.arange(count_rows, dtype=jnp.int32)[None, :]).astype(
        jnp.bfloat16
    )
    source_hot = (sources[:, None] == jnp.arange(total_rows, dtype=jnp.int32)[None, :]).astype(
        jnp.bfloat16
    )
    counts = lax.dot_general(
        target_hot, source_hot, (((0,), (0,)), ((), ())), preferred_element_type=jnp.float32
    )
    return counts.astype(jnp.bfloat16)


def gnn_forward(states, received, adjacent, w_message):
    extended = jnp.concatenate([states, received], axis=0)
    neighbours = jnp.dot(adjacent, extended, preferred_element_type=jnp.float32)
    counted = jnp.sum(adjacent.astype(jnp.float32), axis=1)
    inverse = 1.0 / (counted + 1.0)
    aggregate = ((states.astype(jnp.float32) + neighbours) * inverse[:, None]).astype(jnp.bfloat16)
    preact = jnp.dot(aggregate, w_message, preferred_element_type=jnp.float32)
    hidden = (states.astype(jnp.float32) + jax.nn.silu(preact)).astype(jnp.bfloat16)
    return (aggregate, preact, inverse, hidden)


def gnn_backward(upstream, aggregate, preact, inverse, adjacent, w_message):
    count_rows = aggregate.shape[0]
    up_float = upstream.astype(jnp.float32)
    sigmoid_val = jax.nn.sigmoid(preact)
    pre_grad = (up_float * sigmoid_val * (1.0 + preact * (1.0 - sigmoid_val))).astype(jnp.bfloat16)
    message_part = lax.dot_general(
        aggregate, pre_grad, (((0,), (0,)), ((), ())), preferred_element_type=jnp.float32
    )
    agg_grad = lax.dot_general(
        pre_grad, w_message, (((1,), (1,)), ((), ())), preferred_element_type=jnp.float32
    )
    term_grad = agg_grad * inverse[:, None]
    ext_grad = lax.dot_general(
        adjacent.astype(jnp.float32),
        term_grad,
        (((0,), (0,)), ((), ())),
        precision=lax.Precision.HIGHEST,
        preferred_element_type=jnp.float32,
    )
    local_grad = up_float + term_grad + ext_grad[:count_rows]
    halo_grad = ext_grad[count_rows:].astype(jnp.bfloat16)
    return (message_part, local_grad, halo_grad)


def attend(states, upstream, w_query, w_key, w_value):
    steps_all, nodes_here, width = states.shape
    head_dim = width // HEADS
    scale_factor = head_dim ** (-0.5)
    flat = states.reshape(steps_all * nodes_here, width)

    def project(weight):
        return jnp.dot(flat, weight, preferred_element_type=jnp.float32).astype(jnp.bfloat16)

    def splitter(matrix):
        return matrix.reshape(steps_all, nodes_here, HEADS, head_dim).astype(jnp.float32)

    queries = project(w_query)
    key_rows = project(w_key)
    value_rows = project(w_value)
    query_f = splitter(queries)
    key_f = splitter(key_rows)
    value_f = splitter(value_rows)
    scores = jnp.einsum("tnhd,snhd->nhts", query_f, key_f) * scale_factor
    causal = jnp.arange(steps_all)[:, None] >= jnp.arange(steps_all)[None, :]
    scores = jnp.where(causal, scores, -jnp.inf)
    highest = jnp.max(scores, axis=-1, keepdims=True)
    exponent = jnp.exp(scores - highest)
    probs = exponent / jnp.sum(exponent, axis=-1, keepdims=True)
    probs_low = probs.astype(jnp.bfloat16).astype(jnp.float32)
    up_heads = splitter(upstream)
    value_grad = jnp.einsum("nhts,tnhd->snhd", probs_low, up_heads).astype(jnp.bfloat16)
    prob_grad = jnp.einsum("tnhd,snhd->nhts", up_heads, value_f)
    score_grad = (
        probs * (prob_grad - jnp.sum(prob_grad * probs, axis=-1, keepdims=True)) * scale_factor
    ).astype(jnp.bfloat16)
    score_f = score_grad.astype(jnp.float32)
    query_grad = jnp.einsum("nhts,snhd->tnhd", score_f, key_f).astype(jnp.bfloat16)
    key_grad = jnp.einsum("nhts,tnhd->snhd", score_f, query_f).astype(jnp.bfloat16)
    query_flat = query_grad.reshape(steps_all * nodes_here, width)
    key_flat = key_grad.reshape(steps_all * nodes_here, width)
    value_flat = value_grad.reshape(steps_all * nodes_here, width)

    def weight_grad(grad_rows):
        return lax.dot_general(
            flat, grad_rows, (((0,), (0,)), ((), ())), preferred_element_type=jnp.float32
        )

    def input_grad(grad_rows, weight):
        return lax.dot_general(
            grad_rows, weight, (((1,), (1,)), ((), ())), preferred_element_type=jnp.float32
        )

    back = upstream.reshape(steps_all * nodes_here, width).astype(jnp.float32)
    back = (
        back
        + input_grad(query_flat, w_query)
        + input_grad(key_flat, w_key)
        + input_grad(value_flat, w_value)
    )
    back = back.astype(jnp.bfloat16).reshape(steps_all, nodes_here, width)
    return ((weight_grad(query_flat), weight_grad(key_flat), weight_grad(value_flat)), back)


def local(
    node_states,
    edge_source,
    edge_target,
    halo_rows,
    halo_count,
    w_message,
    w_query,
    w_key,
    w_value,
    cotangent,
):
    days_local, node_local, width = node_states.shape
    halo_slots = halo_rows.shape[1]
    live = jnp.arange(halo_slots)[None, :] < halo_count
    picked = jnp.take_along_axis(node_states, halo_rows[:, :, None], axis=1)
    sent = jnp.where(live[:, :, None], picked, jnp.zeros_like(picked))
    received = from_behind(sent, "dom", 1)

    def forward_one(items):
        adjacent = adjacency(items[2], items[3], node_local, node_local + halo_slots)
        aggregate, preact, inverse, hidden = gnn_forward(items[0], items[1], adjacent, w_message)
        return (aggregate, preact, inverse, hidden, adjacent)

    aggregate, preact, inverse, hidden, adjacent = lax.map(
        forward_one, (node_states, received, edge_source, edge_target)
    )
    node_major = lax.all_to_all(hidden, "day", split_axis=1, concat_axis=0, tiled=True)
    upstream = cotangent.reshape(cotangent.shape[0], -1, width)
    attn_grads, back = attend(node_major, upstream, w_query, w_key, w_value)
    back_days = lax.all_to_all(back, "day", split_axis=0, concat_axis=1, tiled=True)

    def backward_one(items):
        return gnn_backward(items[0], items[1], items[2], items[3], items[4], w_message)

    message_parts, local_grad, halo_grad = lax.map(
        backward_one, (back_days, aggregate, preact, inverse, adjacent)
    )
    grad_message = jnp.sum(message_parts, axis=0)
    returned = from_behind(halo_grad, "dom", -1)
    slot_hot = jnp.logical_and(
        halo_rows[:, :, None] == jnp.arange(node_local, dtype=jnp.int32)[None, None, :],
        live[:, :, None],
    ).astype(jnp.bfloat16)
    scattered = jnp.einsum("dsn,dsh->dnh", slot_hot, returned, preferred_element_type=jnp.float32)
    state_grad = local_grad + scattered
    grad_message, grad_query, grad_key, grad_value = lax.psum(
        (grad_message, attn_grads[0], attn_grads[1], attn_grads[2]), ("day", "dom")
    )
    return (state_grad, grad_message, grad_query, grad_key, grad_value)


def solution(mesh):
    return jax.shard_map(
        local,
        mesh=mesh,
        in_specs=(
            P("day", "dom", None),
            P("day", "dom"),
            P("day", "dom"),
            P("day", "dom"),
            P("day", "dom"),
            P(),
            P(),
            P(),
            P(),
            P(None, "dom", "day", None, None),
        ),
        out_specs=(P("day", "dom", None), P(), P(), P(), P()),
        check_vma=False,
    )
```

profile of v0, /device:TPU:0, one launch (start us, length us, event | category | flops | bytes accessed | tf_op | source)
XLA Modules:
  0.0 277.3 jit_solution(9602864403409959612)
XLA Ops:
  8.7 7.0 %gather_fusion = bf16[512,256]{1,0:T(8,128)(2,1)S(1)} fusion(bf16[4,256,256]{2,1,0:T(8,128)(2,1)} %param.14, s32[512]{0:T(512)S(1)} %fusion.70), kind=kCustom, calls=%fused_computation | custom fusion | bytes 528384 | tf_op jit(solution)/shard_map/jit(take_along_axis)/gather | solution.py:137
  16.4 6.9 %collective-permute-done = bf16[4,128,256]{2,1,0:T(8,128)(2,1)S(1)} collective-permute-done((bf16[4,128,256]{2,1,0:T(8,128)(2,1)S(1)}, bf16[4,128,256]{2,1,0:T(8,128)(2,1)S(1)}, u32[]{:S(2)}, u32[]{:S(2)}) %collective-permute-start) | collective-permute-done | bytes 262176 | tf_op jit(solution)/shard_map/ppermute | solution.py:12
  23.4 12.2 %while.34 = (s32[]{:T(128)}, bf16[4,256,256]{2,1,0:T(8,128)(2,1)S(1)}, f32[4,256,256]{2,1,0:T(8,128)S(1)}, f32[4,256]{1,0:T(4,128)S(1)}, bf16[4,256,256]{2,1,0:T...) while((s32[]{:T(128)}, ...), condition=%wide.region_2.3_spmd.clone, body=%wide.region_0.2_spmd.sunk.clone | while | flops 287277312 | bytes 3111561 | solution.py:146
  24.2 1.0 convert_reduce_fusion.3
  27.3 1.0 convert_reduce_fusion.3
  30.3 1.0 convert_reduce_fusion.3
  33.3 1.0 convert_reduce_fusion.3
  35.6 1.2 copy.52
  36.9 5.6 %all-to-all-start = ((bf16[4,256,256]{2,0,1:T(4,128)(2,1)}), bf16[4,256,256]{2,0,1:T(4,128)(2,1)S(1)}, u32[]{:S(2)}, u32[]{:S(2)}) async-start(bf16[4,256,256]{2,0,1:T(4,128)(2,1)} %copy.52), calls=%async_computation | async-start | bytes 1048576 | tf_op jit(solution)/shard_map/all_to_all | solution.py:149
  42.9 12.5 %all-to-all-done = bf16[4,256,256]{2,0,1:T(4,128)(2,1)S(1)} async-done(((bf16[4,256,256]{2,0,1:T(4,128)(2,1)}), bf16[4,256,256]{2,0,1:T(4,128)(2,1)S(1)}, u32[]{:S(2)}, u32[]{:S(2)}) %all-to-all-start) | async-done | bytes 524320 | tf_op jit(solution)/shard_map/all_to_all | solution.py:149
  55.8 1.4 reshape.100
  57.5 1.4 reshape.99
  59.6 2.6 fusion.52
  62.3 4.9 %fusion.77 = (f32[64,4,16]{2,1,0:T(4,128)S(1)}, f32[64,4,16,16]{2,3,1,0:T(8,128)}) fusion(pred[16,16]{0,1:T(8,128)(4,1)S(1)} %iota_compare_fusion.7, bf16[16,64,4,64]{3,2,1,0:T(4,128)(2,1)} %reshape.99, bf16[16,64,4,64]{3,2,1,0:T(4,128)(2,1)} %reshape.100), kind=kOutput, calls=%fused_computation.119 | convolution fusion | flops 8650767 | bytes 1327360 | tf_op jit(solution)/shard_map/sub | solution.py:85
  67.2 5.8 %fusion.50 = bf16[16,64,4,64]{3,0,2,1:T(8,128)(2,1)} fusion(f32[64,4,16,16]{3,2,1,0:T(8,128)} %fusion.52, bf16[16,64,4,64]{3,2,1,0:T(4,128)(2,1)S(1)} %copy-done.5, f32[64,4,16,16]{2,3,1,0:T(8,128)} %get-tuple-element.183, f32[64,4,16]{2,1,0:T(4,128)S(1)} %get-tuple-element.182), kind=kOutput, calls=%fused_computation.78 | convolution fusion | flops 9113615 | bytes 1589248 | tf_op jit(solution)/shard_map/nhts,tnhd->snhd/dot_general | solution.py:96
  73.0 6.1 %fusion.48 = bf16[16,64,4,64]{3,0,2,1:T(8,128)(2,1)} fusion(f32[64,4,16,16]{3,2,1,0:T(8,128)} %fusion.52, bf16[16,64,4,64]{3,2,1,0:T(4,128)(2,1)} %reshape.99, f32[64,4,16,16]{2,3,1,0:T(8,128)} %get-tuple-element.183, f32[64,4,16]{2,1,0:T(4,128)S(1)} %get-tuple-element.182), kind=kOutput, calls=%fused_computation.76 | convolution fusion | flops 9113615 | bytes 1589248 | tf_op jit(solution)/shard_map/nhts,snhd->tnhd/dot_general | solution.py:95
  79.2 3.5 %fusion.49 = bf16[16,64,4,64]{3,0,2,1:T(8,128)(2,1)} fusion(bf16[16,64,4,64]{3,2,1,0:T(4,128)(2,1)S(1)} %reshape_reshape.4, f32[64,4,16,16]{2,3,1,0:T(8,128)} %get-tuple-element.183, f32[64,4,16]{2,1,0:T(4,128)} %copy-done.13), kind=kOutput, calls=%fused_computation.77 | convolution fusion | flops 8781824 | bytes 1327104 | tf_op jit(solution)/shard_map/nhts,tnhd->snhd/dot_general | solution.py:89
  82.7 1.7 copy.63
  85.2 3.1 %copy.61 = bf16[16,64,4,64]{1,0,3,2:T(8,128)(2,1)S(1)} copy(bf16[16,64,4,64]{3,0,2,1:T(8,128)(2,1)} %fusion.48) | data formatting | bytes 1048576 | tf_op jit(solution)/shard_map/convert_element_type | solution.py:95
  89.0 2.9 %copy.65 = bf16[16,64,4,64]{1,0,3,2:T(8,128)(2,1)S(1)} copy(bf16[16,64,4,64]{3,0,2,1:T(8,128)(2,1)} %fusion.49) | data formatting | bytes 1048576 | tf_op jit(solution)/shard_map/convert_element_type | solution.py:89
  92.7 1.4 convolution_add_fusion.3
  94.5 1.2 fusion.51
  95.6 3.5 %all-to-all-start.1 = ((bf16[16,64,256]{2,1,0:T(8,128)(2,1)}), bf16[16,64,256]{2,1,0:T(8,128)(2,1)S(1)}, u32[]{:S(2)}, u32[]{:S(2)}) async-start(bf16[16,64,256]{2,1,0:T(8,128)(2,1)} %bitcast.30), calls=%async_computation.1 | async-start | bytes 1048576 | tf_op jit(solution)/shard_map/all_to_all | solution.py:152
  99.2 1.0 fusion.87
  100.2 1.0 fusion.86
  101.3 10.9 %all-to-all-done.1 = bf16[16,64,256]{2,1,0:T(8,128)(2,1)S(1)} async-done(((bf16[16,64,256]{2,1,0:T(8,128)(2,1)}), bf16[16,64,256]{2,1,0:T(8,128)(2,1)S(1)}, u32[]{:S(2)}, u32[]{:S(2)}) %all-to-all-start.1) | async-done | bytes 524320 | tf_op jit(solution)/shard_map/all_to_all | solution.py:152
  112.1 0.8 copy.66
  113.1 18.6 %while.35 = (s32[]{:T(128)}, f32[4,256,256]{2,1,0:T(8,128)S(1)}, f32[4,256,256]{2,1,0:T(8,128)S(1)}, bf16[4,128,256]{2,1,0:T(8,128)(2,1)}, bf16[4,256,256]{2,1,0...) while((s32[]{:T(128)}, f32[4,256,256]{2,1,0:T(8,128)S(1)}, ...), condition=%wide.region_7.8_spmd.clone, body=%wide.region_6.7_spmd.sunk.clone | while | flops 370671616 | bytes 5576841 | solution.py:157
  113.2 1.3 convolution_multiply_fusion.3
  114.5 1.3 fusion.149
  116.5 1.3 fusion.148
  117.8 1.3 convolution_multiply_fusion.3
  119.1 1.3 fusion.149
  121.1 1.3 fusion.148
  122.5 1.3 convolution_multiply_fusion.3
  123.8 1.3 fusion.149
  125.8 1.3 fusion.148
  127.1 1.3 convolution_multiply_fusion.3
  128.4 1.3 fusion.149
  130.4 1.3 fusion.148
  131.8 1.1 fusion.88
  133.7 2.3 collective-permute-done.1
  136.0 2.4 convolution_add_fusion.4
  138.5 125.3 %all-reduce.3.cloned.1.call-done = (f32[256,256]{1,0:T(8,128)}, f32[256,256]{1,0:T(8,128)}, f32[256,256]{1,0:T(8,128)}, f32[256,256]{1,0:T(8,128)}) async-done(((f32[256,256]{1,0:T(8,128)}, f32[256,256]{1,0:T(8,128)}, f32[256,256]{1,0:T(8,128)}, f32[256,256]{1,0:T(8,128)}), (f32[256,256]{1,0:T(8,128)}, f32[256,256]{1,0:T(8,128)}, f32[256,256]{1,0:T(8,128)}, ...) | async-done | bytes 1048592 | tf_op jit(solution)/shard_map/psum | solution.py:168
  263.8 1.7 copy.137
  265.5 1.7 copy.138
  267.1 1.7 copy.139
  268.8 1.7 copy.140
  (110 shorter events, 18.7 us)
Async XLA Ops:
  7.2 48.3 %copy-start = (bf16[256,256]{1,0:T(8,128)(2,1)S(1)}, bf16[256,256]{1,0:T(8,128)(2,1)}, u32[]{:S(2)}) copy-start(bf16[256,256]{1,0:T(8,128)(2,1)} %param.20) | copy-start | bytes 393220
  8.7 14.8 %copy-start.1 = (bf16[4,256,256]{2,1,0:T(8,128)(2,1)S(1)}, bf16[4,256,256]{2,1,0:T(8,128)(2,1)}, u32[]{:S(2)}) copy-start(bf16[4,256,256]{2,1,0:T(8,128)(2,1)} %param.14) | copy-start | bytes 1572868
  8.7 14.8 %copy-start.2 = (bf16[256,256]{1,0:T(8,128)(2,1)S(1)}, bf16[256,256]{1,0:T(8,128)(2,1)}, u32[]{:S(2)}) copy-start(bf16[256,256]{1,0:T(8,128)(2,1)} %param.19) | copy-start | bytes 393220
  15.9 7.4 %collective-permute-start = (bf16[4,128,256]{2,1,0:T(8,128)(2,1)S(1)}, bf16[4,128,256]{2,1,0:T(8,128)(2,1)S(1)}, u32[]{:S(2)}, u32[]{:S(2)}) collective-permute-start(bf16[4,128,256]{2,1,0:T(8,128)(2,1)S(1)} %select_select_fusion), channel_id=1, source_target_pairs={{0,1},{1,2},{2,3},{3,4},{4,5},{5,6},{6,7},{7,0},{8,9},{9,10},{10,1... | collective-permute-start | bytes 786440 | tf_op jit(solution)/shard_map/ppermute | solution.py:12
  35.6 1.2 copy-start.6
  35.6 19.8 %copy-start.12 = (bf16[4,256,256]{2,1,0:T(8,128)(2,1)}, bf16[4,256,256]{2,1,0:T(8,128)(2,1)S(1)}, u32[]{:S(2)}) copy-start(bf16[4,256,256]{2,1,0:T(8,128)(2,1)S(1)} %get-tuple-element.422) | copy-start | bytes 1572868
  35.6 6.8 %copy-start.4 = (bf16[16,1,1,64,256]{4,3,2,1,0:T(8,128)(2,1)S(1)}, bf16[16,1,1,64,256]{4,3,2,1,0:T(8,128)(2,1)}, u32[]{:S(2)}) copy-start(bf16[16,1,1,64,256]{4,3,2,1,0:T(8,128)(2,1)} %param.23) | copy-start | bytes 1572868
  36.9 18.5 %all-to-all-start = ((bf16[4,256,256]{2,0,1:T(4,128)(2,1)}), bf16[4,256,256]{2,0,1:T(4,128)(2,1)S(1)}, u32[]{:S(2)}, u32[]{:S(2)}) async-start(bf16[4,256,256]{2,0,1:T(4,128)(2,1)} %copy.52), calls=%async_computation | async-start | bytes 1048576 | tf_op jit(solution)/shard_map/all_to_all | solution.py:149
  55.4 1.8 copy-start.9
  55.8 3.1 %copy-start.8 = (bf16[256,256]{1,0:T(8,128)(2,1)S(1)}, bf16[256,256]{1,0:T(8,128)(2,1)}, u32[]{:S(2)}) copy-start(bf16[256,256]{1,0:T(8,128)(2,1)} %param.22) | copy-start | bytes 393220
  62.3 5.0 %copy-start.5 = (bf16[16,64,4,64]{3,2,1,0:T(4,128)(2,1)S(1)}, bf16[16,64,4,64]{3,2,1,0:T(4,128)(2,1)}, u32[]{:S(2)}) copy-start(bf16[16,64,4,64]{3,2,1,0:T(4,128)(2,1)} %reshape.100) | copy-start | bytes 1572868
  67.2 5.8 %copy-start.13 = (f32[64,4,16]{2,1,0:T(4,128)}, f32[64,4,16]{2,1,0:T(4,128)S(1)}, u32[]{:S(2)}) copy-start(f32[64,4,16]{2,1,0:T(4,128)S(1)} %get-tuple-element.182) | copy-start | bytes 49156
  79.2 3.5 %copy-start.7 = (bf16[16,64,4,64]{3,0,2,1:T(8,128)(2,1)S(1)}, bf16[16,64,4,64]{3,0,2,1:T(8,128)(2,1)}, u32[]{:S(2)}) copy-start(bf16[16,64,4,64]{3,0,2,1:T(8,128)(2,1)} %fusion.50) | copy-start | bytes 1572868
  92.7 1.5 copy-start.10
  95.6 16.5 %all-to-all-start.1 = ((bf16[16,64,256]{2,1,0:T(8,128)(2,1)}), bf16[16,64,256]{2,1,0:T(8,128)(2,1)S(1)}, u32[]{:S(2)}, u32[]{:S(2)}) async-start(bf16[16,64,256]{2,1,0:T(8,128)(2,1)} %bitcast.30), calls=%async_computation.1 | async-start | bytes 1048576 | tf_op jit(solution)/shard_map/all_to_all | solution.py:152
  99.1 164.7 %all-reduce.3.cloned.1.call-start = ((), (), s32[]{:S(2)}) async-start(), calls=%async_computation.2 | async-start | bytes 2097152 | tf_op jit(solution)/shard_map/psum | solution.py:168
  113.2 2.6 copy-start.3
  117.8 2.6 copy-start.3
  122.5 2.6 copy-start.3
  127.1 2.6 copy-start.3
  131.8 4.3 %copy-start.11 = (s32[4,128]{1,0:T(4,128)S(1)}, s32[4,128]{1,0:T(4,128)}, u32[]{:S(2)}) copy-start(s32[4,128]{1,0:T(4,128)} %param.17) | copy-start | bytes 6148
  131.8 4.3 %collective-permute-start.1 = (bf16[4,128,256]{2,1,0:T(8,128)(2,1)}, bf16[4,128,256]{2,1,0:T(8,128)(2,1)}, u32[]{:S(2)}, u32[]{:S(2)}) collective-permute-start(bf16[4,128,256]{2,1,0:T(8,128)(2,1)} %get-tuple-element.126), channel_id=1, source_target_pairs={{0,7},{1,0},{2,1},{3,2},{4,3},{5,4},{6,5},{7,6},{8,15},{9,8},{10,9... | collective-permute-start | bytes 786440 | tf_op jit(solution)/shard_map/ppermute | solution.py:12
Sparse Core Ops, SparseCore 0:
  133.8 129.9 all-reduce.2
where the time goes:
time: 278 us; the launch traced here: 277 us
  waiting for transfers between devices  158 us (57%)
  matrix products  53.5 us (19%)
  local copies, waits for them, and re-layouts  38.3 us (14%)
  between operations  14.4 us (5%)
  starting transfers between devices  9.7 us (3%)
  other arithmetic  3.06 us (1%)
    psum x1, waiting for transfers between devices, local(): lax.psum((grad_message, attn_grads[0], attn_grads[1], attn_grads[2]), ('d...  125 us
    all_to_all x1, waiting for transfers between devices, local(): lax.all_to_all(hidden, 'day', split_axis=1, concat_axis=0, tiled=True)  12.5 us
    all_to_all x1, waiting for transfers between devices, local(): lax.all_to_all(back, 'day', split_axis=0, concat_axis=1, tiled=True)  10.9 us
    ppermute x2, waiting for transfers between devices, from_behind(): return lax.ppermute(value, axis, pairs)  9.28 us
    gather x1, local copies, waits for them, and re-layouts, local(): picked = jnp.take_along_axis(node_states, halo_rows[:, :, None], axis=1)  7 us
    unnamed x30, local copies, waits for them, and re-layouts  6.74 us
    dot_general x1, matrix products, attend(): jnp.einsum('nhts,snhd->tnhd', score_f, key_f).astype(jnp.bfloat16)  6.14 us
    dot_general x1, matrix products, attend(): jnp.einsum('nhts,tnhd->snhd', score_f, query_f).astype(jnp.bfloat16)  5.79 us
  transfers between devices with their start and end apart: 5, of which 5 were waited for; matrix products, arithmetic and copies ran while one was open for 2% of the time, Pallas kernels for 0%

commit v1 on v0

--- a/solution.py
+++ b/solution.py
@@ -10,6 +10,38 @@
     count = lax.axis_size(axis)
     pairs = [(source, (source + steps) % count) for source in range(count)]
     return lax.ppermute(value, axis, pairs)
+
+
+def _power_of_two(count):
+    return count > 0 and count & (count - 1) == 0
+
+
+def tree_sum(values, axes):
+    sizes = [lax.axis_size(axis) for axis in axes]
+    flat = jnp.concatenate([value.reshape(-1) for value in values])
+    total = 1
+    for size in sizes:
+        total *= size
+    if not all(_power_of_two(size) for size in sizes) or flat.shape[0] % total:
+        return lax.psum(tuple(values), axes)
+    steps = [(axis, bit) for axis, size in zip(axes, sizes) for bit in [1 << k for k in range(size.bit_length() - 1)]]
+    for axis, bit in steps:
+        side = (lax.axis_index(axis) // bit) % 2
+        halves = flat.reshape(2, -1)
+        keep = jnp.where(side == 0, halves[0], halves[1])
+        send = jnp.where(side == 0, halves[1], halves[0])
+        pairs = [(source, source ^ bit) for source in range(lax.axis_size(axis))]
+        flat = keep + lax.ppermute(send, axis, pairs)
+    for axis, bit in reversed(steps):
+        side = (lax.axis_index(axis) // bit) % 2
+        pairs = [(source, source ^ bit) for source in range(lax.axis_size(axis))]
+        other = lax.ppermute(flat, axis, pairs)
+        flat = jnp.where(side == 0, jnp.concatenate([flat, other]), jnp.concatenate([other, flat]))
+    results, start = [], 0
+    for value in values:
+        results.append(flat[start : start + value.size].reshape(value.shape))
+        start += value.size
+    return tuple(results)
 
 
 def adjacency(sources, targets, count_rows, total_rows):
@@ -165,8 +197,8 @@
     ).astype(jnp.bfloat16)
     scattered = jnp.einsum("dsn,dsh->dnh", slot_hot, returned, preferred_element_type=jnp.float32)
     state_grad = local_grad + scattered
-    grad_message, grad_query, grad_key, grad_value = lax.psum(
-        (grad_message, attn_grads[0], attn_grads[1], attn_grads[2]), ("day", "dom")
+    grad_message, grad_query, grad_key, grad_value = tree_sum(
+        (grad_message, attn_grads[0], attn_grads[1], attn_grads[2]), ("dom", "day")
     )
     return (state_grad, grad_message, grad_query, grad_key, grad_value)
 

time: 278 us -> 186 us (0.67)
  waiting for transfers between devices: 158 us -> 73.4 us
  between operations: 14.4 us -> 1.26 us
  starting transfers between devices: 9.7 us -> 15.7 us
    psum x1 -> x0, waiting for transfers between devices: 125 us -> none  [local(): lax.psum((grad_message, attn_grads[0], attn_grads[1], attn_grads[2]), ('d...]
    ppermute x0 -> x10, waiting for transfers between devices: none -> 40.4 us  [the longest x5 22.3 us: tree_sum(): flat = keep + lax.ppermute(send, axis, pairs)]
    ppermute x0 -> x10, starting transfers between devices: none -> 6.14 us  [the longest x5 3.6 us: tree_sum(): flat = keep + lax.ppermute(send, axis, pairs)]
    unnamed x30 -> x34, local copies, waits for them, and re-layouts: 6.74 us -> 2.04 us
  transfers between devices with their start and end apart: 5 -> 14, of which waited for: 5 -> 13; matrix products, arithmetic and copies ran while one was open for 2% -> 2% of each run, Pallas kernels for 0% -> 0%
where the time goes in v1:
time: 186 us; the launch traced here: 185 us
  waiting for transfers between devices  73.4 us (39%)
  matrix products  54.4 us (29%)
  local copies, waits for them, and re-layouts  36.9 us (20%)
  starting transfers between devices  15.7 us (8%)
  other arithmetic  2.89 us (2%)
    ppermute x5, waiting for transfers between devices, tree_sum(): flat = keep + lax.ppermute(send, axis, pairs)  22.3 us
    ppermute x5, waiting for transfers between devices, tree_sum(): other = lax.ppermute(flat, axis, pairs)  18.1 us
    all_to_all x1, waiting for transfers between devices, local(): lax.all_to_all(hidden, 'day', split_axis=1, concat_axis=0, tiled=True)  12.4 us
    all_to_all x1, waiting for transfers between devices, local(): lax.all_to_all(back, 'day', split_axis=0, concat_axis=1, tiled=True)  11.9 us
    ppermute x2, waiting for transfers between devices, from_behind(): return lax.ppermute(value, axis, pairs)  8.72 us
    gather x1, local copies, waits for them, and re-layouts, local(): picked = jnp.take_along_axis(node_states, halo_rows[:, :, None], axis=1)  7 us
    dot_general x1, matrix products, attend(): jnp.einsum('nhts,tnhd->snhd', score_f, query_f).astype(jnp.bfloat16)  6.16 us
    dot_general x1, matrix products, attend(): jnp.einsum('nhts,snhd->tnhd', score_f, key_f).astype(jnp.bfloat16)  5.9 us
  transfers between devices with their start and end apart: 14, of which 13 were waited for; matrix products, arithmetic and copies ran while one was open for 2% of the time, Pallas kernels for 0%

profile of v1, /device:TPU:0, one launch (start us, length us, event | category | flops | bytes accessed | tf_op | source)
XLA Modules:
  0.0 184.9 jit_solution(11964779627345640827)
XLA Ops:
  2.1 7.0 %gather_fusion = bf16[512,256]{1,0:T(8,128)(2,1)S(1)} fusion(bf16[4,256,256]{2,1,0:T(8,128)(2,1)} %param.14, s32[512]{0:T(512)S(1)} %fusion.70), kind=kCustom, calls=%fused_computation | custom fusion | bytes 528384 | tf_op jit(solution)/shard_map/jit(take_along_axis)/gather | solution.py:169
  9.9 6.9 %collective-permute-done = bf16[4,128,256]{2,1,0:T(8,128)(2,1)S(1)} collective-permute-done((bf16[4,128,256]{2,1,0:T(8,128)(2,1)S(1)}, bf16[4,128,256]{2,1,0:T(8,128)(2,1)S(1)}, u32[]{:S(2)}, u32[]{:S(2)}) %collective-permute-start) | collective-permute-done | bytes 262176 | tf_op jit(solution)/shard_map/ppermute | solution.py:12
  16.9 14.8 %while.34 = (s32[]{:T(128)}, bf16[4,256,256]{2,1,0:T(8,128)(2,1)}, f32[4,256,256]{2,1,0:T(8,128)S(1)}, f32[4,256]{1,0:T(4,128)S(1)}, bf16[4,256,256]{2,1,0:T(8,1...) while((s32[]{:T(128)}, bf16[4,256,256]{2,1,0:T(8,128)(2,1)}, ...), condition=%wide.region_2.3_spmd.clone, body=%wide.region_0.2_spmd.sunk.clone | while | flops 287277312 | bytes 3112069 | solution.py:178
  31.7 1.2 copy.52
  32.9 5.6 %all-to-all-start = ((bf16[4,256,256]{2,0,1:T(4,128)(2,1)}), bf16[4,256,256]{2,0,1:T(4,128)(2,1)S(1)}, u32[]{:S(2)}, u32[]{:S(2)}) async-start(bf16[4,256,256]{2,0,1:T(4,128)(2,1)} %copy.52), calls=%async_computation | async-start | bytes 1048576 | tf_op jit(solution)/shard_map/all_to_all | solution.py:181
  39.0 12.4 %all-to-all-done = bf16[4,256,256]{2,0,1:T(4,128)(2,1)S(1)} async-done(((bf16[4,256,256]{2,0,1:T(4,128)(2,1)}), bf16[4,256,256]{2,0,1:T(4,128)(2,1)S(1)}, u32[]{:S(2)}, u32[]{:S(2)}) %all-to-all-start) | async-done | bytes 524320 | tf_op jit(solution)/shard_map/all_to_all | solution.py:181
  51.9 1.4 reshape.172
  53.5 1.4 reshape.173
  54.9 1.1 convolution_convert_fusion.3
  56.0 2.0 %reshape.174 = bf16[16,64,4,64]{3,2,1,0:T(4,128)(2,1)S(1)} reshape(bf16[1024,256]{1,0:T(8,128)(2,1)} %convolution_convert_fusion.3) | data formatting | bytes 1048576 | tf_op jit(solution)/shard_map/reshape | solution.py:105
  58.1 2.6 %fusion.52 = f32[64,4,16,16]{3,2,1,0:T(8,128)} fusion(bf16[16,64,4,64]{3,2,1,0:T(4,128)(2,1)S(1)} %reshape.174, bf16[16,64,4,64]{3,2,1,0:T(4,128)(2,1)S(1)} %reshape_reshape.4), kind=kOutput, calls=%fused_computation.91 | convolution fusion | flops 8388608 | bytes 1310720 | tf_op jit(solution)/shard_map/tnhd,snhd->nhts/dot_general | solution.py:122
  60.7 5.5 %fusion.78 = (f32[64,4,16]{2,1,0:T(4,128)}, f32[64,4,16,16]{2,3,1,0:T(8,128)}) fusion(pred[16,16]{0,1:T(8,128)(4,1)S(1)} %iota_compare_fusion.7, bf16[16,64,4,64]{3,2,1,0:T(4,128)(2,1)} %reshape.172, bf16[16,64,4,64]{3,2,1,0:T(4,128)(2,1)} %reshape.173), kind=kOutput, calls=%fused_computation.145 | convolution fusion | flops 8650767 | bytes 1327360 | tf_op jit(solution)/shard_map/sub | solution.py:117
  66.2 6.2 %fusion.50 = bf16[16,64,4,64]{3,0,2,1:T(8,128)(2,1)} fusion(f32[64,4,16,16]{3,2,1,0:T(8,128)} %fusion.52, bf16[16,64,4,64]{3,2,1,0:T(4,128)(2,1)} %reshape.173, f32[64,4,16,16]{2,3,1,0:T(8,128)} %get-tuple-element.183, f32[64,4,16]{2,1,0:T(4,128)} %get-tuple-element.182), kind=kOutput, calls=%fused_computation.78 | convolution fusion | flops 9113615 | bytes 1589248 | tf_op jit(solution)/shard_map/nhts,tnhd->snhd/dot_general | solution.py:128
  72.3 5.9 %fusion.48 = bf16[16,64,4,64]{3,0,2,1:T(8,128)(2,1)} fusion(f32[64,4,16,16]{3,2,1,0:T(8,128)} %fusion.52, bf16[16,64,4,64]{3,2,1,0:T(4,128)(2,1)S(1)} %copy-done.6, f32[64,4,16,16]{2,3,1,0:T(8,128)} %get-tuple-element.183, f32[64,4,16]{2,1,0:T(4,128)} %get-tuple-element.182), kind=kOutput, calls=%fused_computation.76 | convolution fusion | flops 9113615 | bytes 1589248 | tf_op jit(solution)/shard_map/nhts,snhd->tnhd/dot_general | solution.py:127
  78.2 3.5 %fusion.49 = bf16[16,64,4,64]{3,0,2,1:T(8,128)(2,1)} fusion(bf16[16,64,4,64]{3,2,1,0:T(4,128)(2,1)S(1)} %reshape_reshape.4, f32[64,4,16,16]{2,3,1,0:T(8,128)} %get-tuple-element.183, f32[64,4,16]{2,1,0:T(4,128)} %get-tuple-element.182), kind=kOutput, calls=%fused_computation.77 | convolution fusion | flops 8781824 | bytes 1327104 | tf_op jit(solution)/shard_map/nhts,tnhd->snhd/dot_general | solution.py:121
  81.7 2.9 %copy.63 = bf16[16,64,4,64]{1,0,3,2:T(8,128)(2,1)S(1)} copy(bf16[16,64,4,64]{3,0,2,1:T(8,128)(2,1)} %fusion.50) | data formatting | bytes 1048576 | tf_op jit(solution)/shard_map/convert_element_type | solution.py:128
  85.3 3.1 %copy.61 = bf16[16,64,4,64]{1,0,3,2:T(8,128)(2,1)S(1)} copy(bf16[16,64,4,64]{3,0,2,1:T(8,128)(2,1)} %fusion.48) | data formatting | bytes 1048576 | tf_op jit(solution)/shard_map/convert_element_type | solution.py:127
  90.6 1.1 convolution_bitcast_fusion.2
  92.0 2.9 %copy.65 = bf16[16,64,4,64]{1,0,3,2:T(8,128)(2,1)S(1)} copy(bf16[16,64,4,64]{3,0,2,1:T(8,128)(2,1)} %fusion.49) | data formatting | bytes 1048576 | tf_op jit(solution)/shard_map/convert_element_type | solution.py:121
  96.0 1.1 fusion.51
  97.2 3.5 %all-to-all-start.1 = ((bf16[16,64,256]{2,1,0:T(8,128)(2,1)}), bf16[16,64,256]{2,1,0:T(8,128)(2,1)S(1)}, u32[]{:S(2)}, u32[]{:S(2)}) async-start(bf16[16,64,256]{2,1,0:T(8,128)(2,1)} %bitcast.30), calls=%async_computation.1 | async-start | bytes 1048576 | tf_op jit(solution)/shard_map/all_to_all | solution.py:184
  101.8 11.9 %all-to-all-done.1 = bf16[16,64,256]{2,1,0:T(8,128)(2,1)S(1)} async-done(((bf16[16,64,256]{2,1,0:T(8,128)(2,1)}), bf16[16,64,256]{2,1,0:T(8,128)(2,1)S(1)}, u32[]{:S(2)}, u32[]{:S(2)}) %all-to-all-start.1) | async-done | bytes 524320 | tf_op jit(solution)/shard_map/all_to_all | solution.py:184
  113.9 18.2 %while.35 = (s32[]{:T(128)}, f32[4,256,256]{2,1,0:T(8,128)S(1)}, f32[4,256,256]{2,1,0:T(8,128)S(1)}, bf16[4,128,256]{2,1,0:T(8,128)(2,1)}, bf16[4,256,256]{2,1,0...) while((s32[]{:T(128)}, f32[4,256,256]{2,1,0:T(8,128)S(1)}, ...), condition=%wide.region_7.8_spmd.clone, body=%wide.region_6.7_spmd.sunk.clone | while | flops 370671616 | bytes 3479661 | solution.py:189
  113.9 1.2 convolution_multiply_fusion.3
  115.1 1.3 fusion.147
  117.1 1.3 fusion.146
  118.5 1.2 convolution_multiply_fusion.3
  119.7 1.3 fusion.147
  121.7 1.3 fusion.146
  123.0 1.2 convolution_multiply_fusion.3
  124.2 1.3 fusion.147
  126.2 1.3 fusion.146
  127.6 1.2 convolution_multiply_fusion.3
  128.8 1.3 fusion.147
  130.8 1.3 fusion.146
  133.2 1.9 %collective-permute-done.2 = f32[131072]{0:T(1024)S(1)} collective-permute-done((f32[131072]{0:T(1024)S(1)}, f32[131072]{0:T(1024)S(1)}, u32[]{:S(2)}, u32[]{:S(2)}) %collective-permute-start.2) | collective-permute-done | bytes 524320 | tf_op jit(solution)/shard_map/ppermute | solution.py:34
  135.2 2.5 %collective-permute-start.3 = (f32[65536]{0:T(1024)S(1)}, f32[65536]{0:T(1024)S(1)}, u32[]{:S(2)}, u32[]{:S(2)}) collective-permute-start(f32[65536]{0:T(1024)S(1)} %slice_select_fusion), channel_id=1, source_target_pairs={{0,2},{1,3},{2,0},{3,1},{4,6},{5,7},{6,4},{7,5},{8,10},{9,11},{10,... | collective-permute-start | bytes 786440 | tf_op jit(solution)/shard_map/ppermute | solution.py:34
  137.7 6.6 %collective-permute-done.3 = f32[65536]{0:T(1024)S(1)} collective-permute-done((f32[65536]{0:T(1024)S(1)}, f32[65536]{0:T(1024)S(1)}, u32[]{:S(2)}, u32[]{:S(2)}) %collective-permute-start.3) | collective-permute-done | bytes 262176 | tf_op jit(solution)/shard_map/ppermute | solution.py:34
  145.3 4.2 %collective-permute-done.4 = f32[32768]{0:T(1024)S(1)} collective-permute-done((f32[32768]{0:T(1024)S(1)}, f32[32768]{0:T(1024)S(1)}, u32[]{:S(2)}, u32[]{:S(2)}) %collective-permute-start.4) | collective-permute-done | bytes 131104 | tf_op jit(solution)/shard_map/ppermute | solution.py:34
  149.6 4.2 %collective-permute-done.5 = f32[16384]{0:T(1024)S(1)} collective-permute-done((f32[16384]{0:T(1024)S(1)}, f32[16384]{0:T(1024)S(1)}, u32[]{:S(2)}, u32[]{:S(2)}) %collective-permute-start.5) | collective-permute-done | bytes 65568 | tf_op jit(solution)/shard_map/ppermute | solution.py:34
  154.0 5.4 %collective-permute-done.6 = f32[8192]{0:T(1024)S(1)} collective-permute-done((f32[8192]{0:T(1024)S(1)}, f32[8192]{0:T(1024)S(1)}, u32[]{:S(2)}, u32[]{:S(2)}) %collective-permute-start.6) | collective-permute-done | bytes 32800 | tf_op jit(solution)/shard_map/ppermute | solution.py:34
  159.4 4.8 %collective-permute-done.7 = f32[8192]{0:T(1024)S(1)} collective-permute-done((f32[8192]{0:T(1024)S(1)}, f32[8192]{0:T(1024)S(1)}, u32[]{:S(2)}, u32[]{:S(2)}) %collective-permute-start.7) | collective-permute-done | bytes 32800 | tf_op jit(solution)/shard_map/ppermute | solution.py:38
  164.3 4.3 %collective-permute-done.8 = f32[16384]{0:T(1024)S(1)} collective-permute-done((f32[16384]{0:T(1024)S(1)}, f32[16384]{0:T(1024)S(1)}, u32[]{:S(2)}, u32[]{:S(2)}) %collective-permute-start.8) | collective-permute-done | bytes 65568 | tf_op jit(solution)/shard_map/ppermute | solution.py:38
  169.3 4.3 %collective-permute-done.9 = f32[32768]{0:T(1024)S(1)} collective-permute-done((f32[32768]{0:T(1024)S(1)}, f32[32768]{0:T(1024)S(1)}, u32[]{:S(2)}, u32[]{:S(2)}) %collective-permute-start.9) | collective-permute-done | bytes 131104 | tf_op jit(solution)/shard_map/ppermute | solution.py:38
  173.6 1.6 collective-permute-start.10
  175.2 4.8 %collective-permute-done.10 = f32[65536]{0:T(1024)S(1)} collective-permute-done((f32[65536]{0:T(1024)S(1)}, f32[65536]{0:T(1024)S(1)}, u32[]{:S(2)}, u32[]{:S(2)}) %collective-permute-start.10) | collective-permute-done | bytes 262176 | tf_op jit(solution)/shard_map/ppermute | solution.py:38
  180.1 1.8 collective-permute-done.1
  181.9 1.5 convolution_add_fusion.4
  (149 shorter events, 31.2 us)
Async XLA Ops:
  0.6 52.6 %copy-start = (bf16[256,256]{1,0:T(8,128)(2,1)S(1)}, bf16[256,256]{1,0:T(8,128)(2,1)}, u32[]{:S(2)}) copy-start(bf16[256,256]{1,0:T(8,128)(2,1)} %param.20) | copy-start | bytes 393220
  2.1 14.8 %copy-start.1 = (bf16[4,256,256]{2,1,0:T(8,128)(2,1)S(1)}, bf16[4,256,256]{2,1,0:T(8,128)(2,1)}, u32[]{:S(2)}) copy-start(bf16[4,256,256]{2,1,0:T(8,128)(2,1)} %param.14) | copy-start | bytes 1572868
  2.1 14.8 %copy-start.2 = (bf16[256,256]{1,0:T(8,128)(2,1)S(1)}, bf16[256,256]{1,0:T(8,128)(2,1)}, u32[]{:S(2)}) copy-start(bf16[256,256]{1,0:T(8,128)(2,1)} %param.19) | copy-start | bytes 393220
  9.4 7.4 %collective-permute-start = (bf16[4,128,256]{2,1,0:T(8,128)(2,1)S(1)}, bf16[4,128,256]{2,1,0:T(8,128)(2,1)S(1)}, u32[]{:S(2)}, u32[]{:S(2)}) collective-permute-start(bf16[4,128,256]{2,1,0:T(8,128)(2,1)S(1)} %select_select_fusion), channel_id=1, source_target_pairs={{0,1},{1,2},{2,3},{3,4},{4,5},{5,6},{6,7},{7,0},{8,9},{9,10},{10,1... | collective-permute-start | bytes 786440 | tf_op jit(solution)/shard_map/ppermute | solution.py:12
  31.7 6.8 %copy-start.7 = (f32[4,256,256]{2,1,0:T(8,128)}, f32[4,256,256]{2,1,0:T(8,128)S(1)}, u32[]{:S(2)}) copy-start(f32[4,256,256]{2,1,0:T(8,128)S(1)} %get-tuple-element.424) | copy-start | bytes 3145732
  31.7 6.8 %copy-start.3 = (bf16[16,1,1,64,256]{4,3,2,1,0:T(8,128)(2,1)S(1)}, bf16[16,1,1,64,256]{4,3,2,1,0:T(8,128)(2,1)}, u32[]{:S(2)}) copy-start(bf16[16,1,1,64,256]{4,3,2,1,0:T(8,128)(2,1)} %param.23) | copy-start | bytes 1572868
  32.9 18.5 %all-to-all-start = ((bf16[4,256,256]{2,0,1:T(4,128)(2,1)}), bf16[4,256,256]{2,0,1:T(4,128)(2,1)S(1)}, u32[]{:S(2)}, u32[]{:S(2)}) async-start(bf16[4,256,256]{2,0,1:T(4,128)(2,1)} %copy.52), calls=%async_computation | async-start | bytes 1048576 | tf_op jit(solution)/shard_map/all_to_all | solution.py:181
  38.5 13.0 %copy-start.10 = (bf16[256,256]{1,0:T(8,128)(2,1)S(1)}, bf16[256,256]{1,0:T(8,128)(2,1)}, u32[]{:S(2)}) copy-start(bf16[256,256]{1,0:T(8,128)(2,1)} %param.21) | copy-start | bytes 393220
  51.8 3.1 %copy-start.9 = (bf16[256,256]{1,0:T(8,128)(2,1)S(1)}, bf16[256,256]{1,0:T(8,128)(2,1)}, u32[]{:S(2)}) copy-start(bf16[256,256]{1,0:T(8,128)(2,1)} %param.22) | copy-start | bytes 393220
  66.2 6.2 %copy-start.6 = (bf16[16,64,4,64]{3,2,1,0:T(4,128)(2,1)S(1)}, bf16[16,64,4,64]{3,2,1,0:T(4,128)(2,1)}, u32[]{:S(2)}) copy-start(bf16[16,64,4,64]{3,2,1,0:T(4,128)(2,1)} %reshape.172) | copy-start | bytes 1572868
  90.2 1.4 copy-start.11
  95.6 5.0 %copy-start.4 = (f32[32,2,8,128]{3,2,1,0:T(8,128)S(1)}, f32[32,2,8,128]{3,2,1,0:T(8,128)}, u32[]{:S(2)}) copy-start(f32[32,2,8,128]{3,2,1,0:T(8,128)} %convolution_bitcast_fusion.3) | copy-start | bytes 786436
  96.0 5.5 %copy-start.5 = (f32[32,2,8,128]{3,2,1,0:T(8,128)S(1)}, f32[32,2,8,128]{3,2,1,0:T(8,128)}, u32[]{:S(2)}) copy-start(f32[32,2,8,128]{3,2,1,0:T(8,128)} %convolution_bitcast_fusion.2) | copy-start | bytes 786436
  97.2 16.5 %all-to-all-start.1 = ((bf16[16,64,256]{2,1,0:T(8,128)(2,1)}), bf16[16,64,256]{2,1,0:T(8,128)(2,1)S(1)}, u32[]{:S(2)}, u32[]{:S(2)}) async-start(bf16[16,64,256]{2,1,0:T(8,128)(2,1)} %bitcast.30), calls=%async_computation.1 | async-start | bytes 1048576 | tf_op jit(solution)/shard_map/all_to_all | solution.py:184
  132.1 1.0 copy-start.8
  133.1 2.0 %collective-permute-start.2 = (f32[131072]{0:T(1024)S(1)}, f32[131072]{0:T(1024)S(1)}, u32[]{:S(2)}, u32[]{:S(2)}) collective-permute-start(f32[131072]{0:T(1024)S(1)} %broadcast_select_fusion), channel_id=1, source_target_pairs={{0,1},{1,0},{2,3},{3,2},{4,5},{5,4},{6,7},{7,6},{8,9},{9,8},{10,11... | collective-permute-start | bytes 1572872 | tf_op jit(solution)/shard_map/ppermute | solution.py:34
  135.2 40.1 %copy-start.13 = (bf16[4,128,256]{2,1,0:T(8,128)(2,1)S(1)}, bf16[4,128,256]{2,1,0:T(8,128)(2,1)}, u32[]{:S(2)}) copy-start(bf16[4,128,256]{2,1,0:T(8,128)(2,1)} %get-tuple-element.126) | copy-start | bytes 786436
  135.2 9.1 %collective-permute-start.3 = (f32[65536]{0:T(1024)S(1)}, f32[65536]{0:T(1024)S(1)}, u32[]{:S(2)}, u32[]{:S(2)}) collective-permute-start(f32[65536]{0:T(1024)S(1)} %slice_select_fusion), channel_id=1, source_target_pairs={{0,2},{1,3},{2,0},{3,1},{4,6},{5,7},{6,4},{7,5},{8,10},{9,11},{10,... | collective-permute-start | bytes 786440 | tf_op jit(solution)/shard_map/ppermute | solution.py:34
  137.7 44.2 %copy-start.12 = (s32[4,128]{1,0:T(4,128)S(1)}, s32[4,128]{1,0:T(4,128)}, u32[]{:S(2)}) copy-start(s32[4,128]{1,0:T(4,128)} %param.17) | copy-start | bytes 6148
  144.4 5.1 %collective-permute-start.4 = (f32[32768]{0:T(1024)S(1)}, f32[32768]{0:T(1024)S(1)}, u32[]{:S(2)}, u32[]{:S(2)}) collective-permute-start(f32[32768]{0:T(1024)S(1)} %slice_select_fusion.1), channel_id=1, source_target_pairs={{0,4},{1,5},{2,6},{3,7},{4,0},{5,1},{6,2},{7,3},{8,12},{9,13},{10,... | collective-permute-start | bytes 393224 | tf_op jit(solution)/shard_map/ppermute | solution.py:34
  149.5 4.3 %collective-permute-start.5 = (f32[16384]{0:T(1024)S(1)}, f32[16384]{0:T(1024)S(1)}, u32[]{:S(2)}, u32[]{:S(2)}) collective-permute-start(f32[16384]{0:T(1024)S(1)} %slice_select_fusion.2), channel_id=1, source_target_pairs={{0,8},{8,0},{16,24},{24,16},{1,9},{9,1},{17,25},{25,17},{2,10},{10... | collective-permute-start | bytes 196616 | tf_op jit(solution)/shard_map/ppermute | solution.py:34
  153.9 5.5 %collective-permute-start.6 = (f32[8192]{0:T(1024)S(1)}, f32[8192]{0:T(1024)S(1)}, u32[]{:S(2)}, u32[]{:S(2)}) collective-permute-start(f32[8192]{0:T(1024)S(1)} %slice_select_fusion.3), channel_id=1, source_target_pairs={{0,16},{8,24},{16,0},{24,8},{1,17},{9,25},{17,1},{25,9},{2,18},{10... | collective-permute-start | bytes 98312 | tf_op jit(solution)/shard_map/ppermute | solution.py:34
  159.4 4.8 %collective-permute-start.7 = (f32[8192]{0:T(1024)S(1)}, f32[8192]{0:T(1024)S(1)}, u32[]{:S(2)}, u32[]{:S(2)}) collective-permute-start(f32[8192]{0:T(1024)S(1)} %select_add_fusion.4), channel_id=1, source_target_pairs={{0,16},{8,24},{16,0},{24,8},{1,17},{9,25},{17,1},{25,9},{2,18},{10... | collective-permute-start | bytes 98312 | tf_op jit(solution)/shard_map/ppermute | solution.py:38
  164.2 4.3 %collective-permute-start.8 = (f32[16384]{0:T(1024)S(1)}, f32[16384]{0:T(1024)S(1)}, u32[]{:S(2)}, u32[]{:S(2)}) collective-permute-start(f32[16384]{0:T(1024)S(1)} %maximum_select_fusion.7), channel_id=1, source_target_pairs={{0,8},{8,0},{16,24},{24,16},{1,9},{9,1},{17,25},{25,17},{2,10},{10... | collective-permute-start | bytes 196616 | tf_op jit(solution)/shard_map/ppermute | solution.py:38
  168.5 5.0 %collective-permute-start.9 = (f32[32768]{0:T(1024)S(1)}, f32[32768]{0:T(1024)S(1)}, u32[]{:S(2)}, u32[]{:S(2)}) collective-permute-start(f32[32768]{0:T(1024)S(1)} %maximum_select_fusion.6), channel_id=1, source_target_pairs={{0,4},{1,5},{2,6},{3,7},{4,0},{5,1},{6,2},{7,3},{8,12},{9,13},{10,... | collective-permute-start | bytes 393224 | tf_op jit(solution)/shard_map/ppermute | solution.py:38
  173.6 6.4 %collective-permute-start.10 = (f32[65536]{0:T(1024)S(1)}, f32[65536]{0:T(1024)S(1)}, u32[]{:S(2)}, u32[]{:S(2)}) collective-permute-start(f32[65536]{0:T(1024)S(1)} %maximum_select_fusion.4), channel_id=1, source_target_pairs={{0,2},{1,3},{2,0},{3,1},{4,6},{5,7},{6,4},{7,5},{8,10},{9,11},{10,... | collective-permute-start | bytes 786440 | tf_op jit(solution)/shard_map/ppermute | solution.py:38
  175.2 6.7 %collective-permute-start.1 = (bf16[4,128,256]{2,1,0:T(8,128)(2,1)S(1)}, bf16[4,128,256]{2,1,0:T(8,128)(2,1)S(1)}, u32[]{:S(2)}, u32[]{:S(2)}) collective-permute-start(bf16[4,128,256]{2,1,0:T(8,128)(2,1)S(1)} %copy-done.13), channel_id=1, source_target_pairs={{0,7},{1,0},{2,1},{3,2},{4,3},{5,4},{6,5},{7,6},{8,15},{9,8},{10,9... | collective-permute-start | bytes 786440 | tf_op jit(solution)/shard_map/ppermute | solution.py:12
  180.1 3.6 %collective-permute-start.11 = (f32[131072]{0:T(1024)S(1)}, f32[131072]{0:T(1024)S(1)}, u32[]{:S(2)}, u32[]{:S(2)}) collective-permute-start(f32[131072]{0:T(1024)S(1)} %maximum_select_fusion.2), channel_id=1, source_target_pairs={{0,1},{1,0},{2,3},{3,2},{4,5},{5,4},{6,7},{7,6},{8,9},{9,8},{10,11... | collective-permute-start | bytes 1572872 | tf_op jit(solution)/shard_map/ppermute | solution.py:38

commit v2 on v1

--- a/solution.py
+++ b/solution.py
@@ -166,40 +166,73 @@
     days_local, node_local, width = node_states.shape
     halo_slots = halo_rows.shape[1]
     live = jnp.arange(halo_slots)[None, :] < halo_count
-    picked = jnp.take_along_axis(node_states, halo_rows[:, :, None], axis=1)
-    sent = jnp.where(live[:, :, None], picked, jnp.zeros_like(picked))
+    rows = jnp.arange(node_local, dtype=jnp.int32)
+    slot_hot = jnp.logical_and(
+        halo_rows[:, :, None] == rows[None, None, :], live[:, :, None]
+    ).astype(jnp.bfloat16)
+    sent = jnp.einsum(
+        "dsn,dnh->dsh", slot_hot, node_states, preferred_element_type=jnp.float32
+    ).astype(jnp.bfloat16)
     received = from_behind(sent, "dom", 1)
 
-    def forward_one(items):
-        adjacent = adjacency(items[2], items[3], node_local, node_local + halo_slots)
-        aggregate, preact, inverse, hidden = gnn_forward(items[0], items[1], adjacent, w_message)
-        return (aggregate, preact, inverse, hidden, adjacent)
-
-    aggregate, preact, inverse, hidden, adjacent = lax.map(
-        forward_one, (node_states, received, edge_source, edge_target)
-    )
+    target_hot = (edge_target[:, :, None] == rows[None, None, :]).astype(jnp.bfloat16)
+    local_hot = (edge_source[:, :, None] == rows[None, None, :]).astype(jnp.bfloat16)
+    halo_ids = node_local + jnp.arange(halo_slots, dtype=jnp.int32)
+    halo_hot = (edge_source[:, :, None] == halo_ids[None, None, :]).astype(jnp.bfloat16)
+    adjacent_local = jnp.einsum(
+        "der,des->drs", target_hot, local_hot, preferred_element_type=jnp.float32
+    ).astype(jnp.bfloat16)
+    adjacent_halo = jnp.einsum(
+        "der,des->drs", target_hot, halo_hot, preferred_element_type=jnp.float32
+    ).astype(jnp.bfloat16)
+    counted = jnp.sum(target_hot.astype(jnp.float32), axis=1)
+    inverse = 1.0 / (counted + 1.0)
+
+    states_f = node_states.astype(jnp.float32)
+    neighbours = jnp.einsum(
+        "drs,dsh->drh", adjacent_local, node_states, preferred_element_type=jnp.float32
+    ) + jnp.einsum("drs,dsh->drh", adjacent_halo, received, preferred_element_type=jnp.float32)
+    aggregate = ((states_f + neighbours) * inverse[:, :, None]).astype(jnp.bfloat16)
+    preact = jnp.einsum("drh,hk->drk", aggregate, w_message, preferred_element_type=jnp.float32)
+    hidden = (states_f + jax.nn.silu(preact)).astype(jnp.bfloat16)
+
     node_major = lax.all_to_all(hidden, "day", split_axis=1, concat_axis=0, tiled=True)
     upstream = cotangent.reshape(cotangent.shape[0], -1, width)
     attn_grads, back = attend(node_major, upstream, w_query, w_key, w_value)
     back_days = lax.all_to_all(back, "day", split_axis=0, concat_axis=1, tiled=True)
 
-    def backward_one(items):
-        return gnn_backward(items[0], items[1], items[2], items[3], items[4], w_message)
-
-    message_parts, local_grad, halo_grad = lax.map(
-        backward_one, (back_days, aggregate, preact, inverse, adjacent)
-    )
-    grad_message = jnp.sum(message_parts, axis=0)
-    returned = from_behind(halo_grad, "dom", -1)
-    slot_hot = jnp.logical_and(
-        halo_rows[:, :, None] == jnp.arange(node_local, dtype=jnp.int32)[None, None, :],
-        live[:, :, None],
-    ).astype(jnp.bfloat16)
-    scattered = jnp.einsum("dsn,dsh->dnh", slot_hot, returned, preferred_element_type=jnp.float32)
-    state_grad = local_grad + scattered
+    sigmoid_val = jax.nn.sigmoid(preact)
+    pre_grad = (
+        back_days.astype(jnp.float32) * sigmoid_val * (1.0 + preact * (1.0 - sigmoid_val))
+    ).astype(jnp.bfloat16)
+    grad_message = lax.dot_general(
+        aggregate.reshape(-1, width),
+        pre_grad.reshape(-1, width),
+        (((0,), (0,)), ((), ())),
+        preferred_element_type=jnp.float32,
+    )
     grad_message, grad_query, grad_key, grad_value = tree_sum(
         (grad_message, attn_grads[0], attn_grads[1], attn_grads[2]), ("dom", "day")
     )
+    agg_grad = jnp.einsum("drk,hk->drh", pre_grad, w_message, preferred_element_type=jnp.float32)
+    term_grad = agg_grad * inverse[:, :, None]
+    halo_grad = jnp.einsum(
+        "drs,drh->dsh",
+        adjacent_halo.astype(jnp.float32),
+        term_grad,
+        precision=lax.Precision.HIGHEST,
+        preferred_element_type=jnp.float32,
+    ).astype(jnp.bfloat16)
+    returned = from_behind(halo_grad, "dom", -1)
+    own_grad = jnp.einsum(
+        "drs,drh->dsh",
+        adjacent_local.astype(jnp.float32),
+        term_grad,
+        precision=lax.Precision.HIGHEST,
+        preferred_element_type=jnp.float32,
+    )
+    scattered = jnp.einsum("dsn,dsh->dnh", slot_hot, returned, preferred_element_type=jnp.float32)
+    state_grad = back_days.astype(jnp.float32) + term_grad + own_grad + scattered
     return (state_grad, grad_message, grad_query, grad_key, grad_value)
 
 

time: 186 us -> 154 us (0.83)
  local copies, waits for them, and re-layouts: 36.9 us -> 20.4 us
  matrix products: 54.4 us -> 40.4 us
  waiting for transfers between devices: 73.4 us -> 67.4 us
  starting transfers between devices: 15.7 us -> 18.4 us
  other arithmetic: 2.89 us -> 5.35 us
    dot_general x24 -> x10, matrix products: 23.3 us -> 9.08 us  [the longest x1 2.37 us: local(): jnp.einsum('der,des->drs', target_hot, local_hot, preferred_element_type=...]
    ppermute x2, waiting for transfers between devices: 8.72 us -> 1.56 us  [from_behind(): return lax.ppermute(value, axis, pairs)]
    gather x1 -> x0, local copies, waits for them, and re-layouts: 7 us -> none  [local(): picked = jnp.take_along_axis(node_states, halo_rows[:, :, None], axis=1)]
    dynamic_update_slice x12 -> x0, local copies, waits for them, and re-layouts: 5.55 us -> none  [the longest x8 2.98 us: local(): lax.map(forward_one, (node_states, received, edge_source, edge_target))]
    dynamic_slice x8 -> x0, local copies, waits for them, and re-layouts: 3.03 us -> none  [the longest x4 3 us: local(): lax.map(forward_one, (node_states, received, edge_source, edge_target))]
    ppermute x5, starting transfers between devices: 2.54 us -> 5.23 us  [tree_sum(): other = lax.ppermute(flat, axis, pairs)]
    all_to_all x1, waiting for transfers between devices: 12.4 us -> 14.5 us  [local(): lax.all_to_all(hidden, 'day', split_axis=1, concat_axis=0, tiled=True)]
    ppermute x5, waiting for transfers between devices: 18.1 us -> 16.1 us  [tree_sum(): other = lax.ppermute(flat, axis, pairs)]
  transfers between devices with their start and end apart: 14 -> 14, of which waited for: 13 -> 13; matrix products, arithmetic and copies ran while one was open for 2% -> 7% of each run, Pallas kernels for 0% -> 0%
where the time goes in v2:
time: 154 us; the launch traced here: 153 us
  waiting for transfers between devices  67.4 us (44%)
  matrix products  40.4 us (26%)
  local copies, waits for them, and re-layouts  20.4 us (13%)
  starting transfers between devices  18.4 us (12%)
  other arithmetic  5.35 us (3%)
    ppermute x5, waiting for transfers between devices, tree_sum(): flat = keep + lax.ppermute(send, axis, pairs)  22.3 us
    ppermute x5, waiting for transfers between devices, tree_sum(): other = lax.ppermute(flat, axis, pairs)  16.1 us
    all_to_all x1, waiting for transfers between devices, local(): lax.all_to_all(hidden, 'day', split_axis=1, concat_axis=0, tiled=True)  14.5 us
    all_to_all x1, waiting for transfers between devices, local(): lax.all_to_all(back, 'day', split_axis=0, concat_axis=1, tiled=True)  12.9 us
    dot_general x1, matrix products, attend(): jnp.einsum('nhts,tnhd->snhd', score_f, query_f).astype(jnp.bfloat16)  6.11 us
    dot_general x1, matrix products, attend(): jnp.einsum('nhts,snhd->tnhd', score_f, key_f).astype(jnp.bfloat16)  5.89 us
    all_to_all x1, starting transfers between devices, local(): lax.all_to_all(hidden, 'day', split_axis=1, concat_axis=0, tiled=True)  5.62 us
    ppermute x5, starting transfers between devices, tree_sum(): other = lax.ppermute(flat, axis, pairs)  5.23 us
  transfers between devices with their start and end apart: 14, of which 13 were waited for; matrix products, arithmetic and copies ran while one was open for 7% of the time, Pallas kernels for 0%

profile of v2, /device:TPU:0, one launch (start us, length us, event | category | flops | bytes accessed | tf_op | source)
XLA Modules:
  0.0 153.5 jit_solution(13134923585445658555)
XLA Ops:
  0.6 0.8 iota_compare_fusion.13
  1.4 1.4 convolution_convert_fusion.7
  3.3 1.2 convert_reduce_fusion
  4.6 2.4 %fusion.20 = bf16[4,256,256]{2,1,0:T(8,128)(2,1)S(1)} fusion(s32[4,1024]{1,0:T(4,128)} %param.11, s32[4,1024]{1,0:T(4,128)} %param.12), kind=kOutput, calls=%fused_computation.41 | convolution fusion | flops 539230208 | bytes 557056 | tf_op jit(solution)/shard_map/der,des->drs/dot_general | solution.py:182
  7.0 1.3 fusion.21
  8.7 1.6 %collective-permute-done = bf16[4,128,256]{2,1,0:T(8,128)(2,1)S(1)} collective-permute-done((bf16[4,128,256]{2,1,0:T(8,128)(2,1)S(1)}, bf16[4,128,256]{2,1,0:T(8,128)(2,1)S(1)}, u32[]{:S(2)}, u32[]{:S(2)}) %collective-permute-start) | collective-permute-done | bytes 262176 | tf_op jit(solution)/shard_map/ppermute | solution.py:12
  10.6 1.3 fusion.24
  12.0 1.2 copy.58
  13.2 5.6 %all-to-all-start = ((bf16[4,256,256]{2,0,1:T(4,128)(2,1)}), bf16[4,256,256]{2,0,1:T(4,128)(2,1)S(1)}, u32[]{:S(2)}, u32[]{:S(2)}) async-start(bf16[4,256,256]{2,0,1:T(4,128)(2,1)} %copy.58), calls=%async_computation | async-start | bytes 1048576 | tf_op jit(solution)/shard_map/all_to_all | solution.py:199
  19.2 14.5 %all-to-all-done = bf16[4,256,256]{2,0,1:T(4,128)(2,1)S(1)} async-done(((bf16[4,256,256]{2,0,1:T(4,128)(2,1)}), bf16[4,256,256]{2,0,1:T(4,128)(2,1)S(1)}, u32[]{:S(2)}, u32[]{:S(2)}) %all-to-all-start) | async-done | bytes 524320 | tf_op jit(solution)/shard_map/all_to_all | solution.py:199
  34.2 1.4 reshape.153
  35.9 1.4 reshape.154
  37.3 1.1 convolution_convert_fusion.3
  38.4 2.0 %reshape.155 = bf16[16,64,4,64]{3,2,1,0:T(4,128)(2,1)S(1)} reshape(bf16[1024,256]{1,0:T(8,128)(2,1)} %convolution_convert_fusion.3) | data formatting | bytes 1048576 | tf_op jit(solution)/shard_map/reshape | solution.py:105
  40.5 2.6 %fusion.27 = f32[64,4,16,16]{3,2,1,0:T(8,128)} fusion(bf16[16,64,4,64]{3,2,1,0:T(4,128)(2,1)S(1)} %reshape.155, bf16[16,64,4,64]{3,2,1,0:T(4,128)(2,1)S(1)} %reshape_reshape.4), kind=kOutput, calls=%fused_computation.56 | convolution fusion | flops 8388608 | bytes 1310720 | tf_op jit(solution)/shard_map/tnhd,snhd->nhts/dot_general | solution.py:122
  43.1 4.9 %fusion.60 = (f32[64,4,16]{2,1,0:T(4,128)S(1)}, f32[64,4,16,16]{2,3,1,0:T(8,128)}) fusion(pred[16,16]{0,1:T(8,128)(4,1)S(1)} %iota_compare_fusion.12, bf16[16,64,4,64]{3,2,1,0:T(4,128)(2,1)} %reshape.153, bf16[16,64,4,64]{3,2,1,0:T(4,128)(2,1)} %reshape.154), kind=kOutput, calls=%fused_computation.115 | convolution fusion | flops 8650767 | bytes 1327360 | tf_op jit(solution)/shard_map/sub | solution.py:117
  47.9 6.1 %fusion.15 = bf16[16,64,4,64]{3,0,2,1:T(8,128)(2,1)} fusion(f32[64,4,16,16]{3,2,1,0:T(8,128)} %fusion.27, bf16[16,64,4,64]{3,2,1,0:T(4,128)(2,1)} %reshape.154, f32[64,4,16,16]{2,3,1,0:T(8,128)} %get-tuple-element.12, f32[64,4,16]{2,1,0:T(4,128)S(1)} %get-tuple-element.11), kind=kOutput, calls=%fused_computation.25 | convolution fusion | flops 9113615 | bytes 1589248 | tf_op jit(solution)/shard_map/nhts,tnhd->snhd/dot_general | solution.py:128
  54.0 5.9 %fusion.13 = bf16[16,64,4,64]{3,0,2,1:T(8,128)(2,1)} fusion(f32[64,4,16,16]{3,2,1,0:T(8,128)} %fusion.27, bf16[16,64,4,64]{3,2,1,0:T(4,128)(2,1)S(1)} %copy-done.8, f32[64,4,16,16]{2,3,1,0:T(8,128)} %get-tuple-element.12, f32[64,4,16]{2,1,0:T(4,128)S(1)} %get-tuple-element.11), kind=kOutput, calls=%fused_computation.23 | convolution fusion | flops 9113615 | bytes 1589248 | tf_op jit(solution)/shard_map/nhts,snhd->tnhd/dot_general | solution.py:127
  59.9 3.5 %fusion.14 = bf16[16,64,4,64]{3,0,2,1:T(8,128)(2,1)} fusion(bf16[16,64,4,64]{3,2,1,0:T(4,128)(2,1)S(1)} %reshape_reshape.4, f32[64,4,16,16]{2,3,1,0:T(8,128)} %get-tuple-element.12, f32[64,4,16]{2,1,0:T(4,128)S(1)} %get-tuple-element.11), kind=kOutput, calls=%fused_computation.24 | convolution fusion | flops 8781824 | bytes 1327104 | tf_op jit(solution)/shard_map/nhts,tnhd->snhd/dot_general | solution.py:121
  63.4 2.9 %copy.69 = bf16[16,64,4,64]{1,0,3,2:T(8,128)(2,1)S(1)} copy(bf16[16,64,4,64]{3,0,2,1:T(8,128)(2,1)} %fusion.15) | data formatting | bytes 1048576 | tf_op jit(solution)/shard_map/convert_element_type | solution.py:128
  66.3 0.7 reshape.157
  67.1 3.1 %copy.67 = bf16[16,64,4,64]{1,0,3,2:T(8,128)(2,1)S(1)} copy(bf16[16,64,4,64]{3,0,2,1:T(8,128)(2,1)} %fusion.13) | data formatting | bytes 1048576 | tf_op jit(solution)/shard_map/convert_element_type | solution.py:127
  70.2 0.7 reshape.156
  71.3 1.3 convolution_add_fusion.3
  72.6 1.1 convolution_bitcast_fusion.1
  74.0 2.9 %copy.71 = bf16[16,64,4,64]{1,0,3,2:T(8,128)(2,1)S(1)} copy(bf16[16,64,4,64]{3,0,2,1:T(8,128)(2,1)} %fusion.14) | data formatting | bytes 1048576 | tf_op jit(solution)/shard_map/convert_element_type | solution.py:121
  78.0 2.1 %fusion.19 = bf16[1024,256]{1,0:T(8,128)(2,1)} fusion(f32[1024,256]{1,0:T(8,128)S(1)} %convolution_add_fusion.2, bf16[1024,256]{0,1:T(8,128)(2,1)S(1)} %reshape.158, bf16[256,256]{1,0:T(8,128)(2,1)} %param.18), kind=kOutput, calls=%fused_computation.40 | convolution fusion | flops 134742016 | bytes 2228224 | tf_op jit(solution)/shard_map/dot_general | solution.py:139
  80.1 3.5 %all-to-all-start.1 = ((bf16[16,64,256]{2,1,0:T(8,128)(2,1)}), bf16[16,64,256]{2,1,0:T(8,128)(2,1)S(1)}, u32[]{:S(2)}, u32[]{:S(2)}) async-start(bf16[16,64,256]{2,1,0:T(8,128)(2,1)} %bitcast.10), calls=%async_computation.1 | async-start | bytes 1048576 | tf_op jit(solution)/shard_map/all_to_all | solution.py:202
  83.7 0.8 copy.82
  84.7 12.9 %all-to-all-done.1 = bf16[16,64,256]{2,1,0:T(8,128)(2,1)S(1)} async-done(((bf16[16,64,256]{2,1,0:T(8,128)(2,1)}), bf16[16,64,256]{2,1,0:T(8,128)(2,1)S(1)}, u32[]{:S(2)}, u32[]{:S(2)}) %all-to-all-start.1) | async-done | bytes 524320 | tf_op jit(solution)/shard_map/all_to_all | solution.py:202
  97.9 1.7 %fusion.26 = bf16[4,256,256]{2,1,0:T(8,128)(2,1)S(1)} fusion(f32[4,4,64,256]{3,2,1,0:T(8,128)S(1)} %copy.72, f32[4,256,256]{2,1,0:T(8,128)} %get-tuple-element.10), kind=kLoop, calls=%fused_computation.55 | loop fusion | flops 2359296 | bytes 2621440 | tf_op jit(solution)/shard_map/convert_element_type | solution.py:207
  100.3 2.0 %collective-permute-done.2 = f32[131072]{0:T(1024)} collective-permute-done((f32[131072]{0:T(1024)S(1)}, f32[131072]{0:T(1024)}, u32[]{:S(2)}, u32[]{:S(2)}) %collective-permute-start.2) | collective-permute-done | bytes 524320 | tf_op jit(solution)/shard_map/ppermute | solution.py:34
  102.3 1.1 select_add_fusion
  103.5 2.4 %collective-permute-start.3 = (f32[65536]{0:T(1024)S(1)}, f32[65536]{0:T(1024)S(1)}, u32[]{:S(2)}, u32[]{:S(2)}) collective-permute-start(f32[65536]{0:T(1024)S(1)} %slice_select_fusion), channel_id=1, source_target_pairs={{0,2},{1,3},{2,0},{3,1},{4,6},{5,7},{6,4},{7,5},{8,10},{9,11},{10,... | collective-permute-start | bytes 786440 | tf_op jit(solution)/shard_map/ppermute | solution.py:34
  105.9 6.6 %collective-permute-done.3 = f32[65536]{0:T(1024)S(1)} collective-permute-done((f32[65536]{0:T(1024)S(1)}, f32[65536]{0:T(1024)S(1)}, u32[]{:S(2)}, u32[]{:S(2)}) %collective-permute-start.3) | collective-permute-done | bytes 262176 | tf_op jit(solution)/shard_map/ppermute | solution.py:34
  112.6 0.9 collective-permute-start.4
  113.5 4.2 %collective-permute-done.4 = f32[32768]{0:T(1024)S(1)} collective-permute-done((f32[32768]{0:T(1024)S(1)}, f32[32768]{0:T(1024)S(1)}, u32[]{:S(2)}, u32[]{:S(2)}) %collective-permute-start.4) | collective-permute-done | bytes 131104 | tf_op jit(solution)/shard_map/ppermute | solution.py:34
  117.8 4.2 %collective-permute-done.5 = f32[16384]{0:T(1024)S(1)} collective-permute-done((f32[16384]{0:T(1024)S(1)}, f32[16384]{0:T(1024)S(1)}, u32[]{:S(2)}, u32[]{:S(2)}) %collective-permute-start.5) | collective-permute-done | bytes 65568 | tf_op jit(solution)/shard_map/ppermute | solution.py:34
  122.1 5.3 %collective-permute-done.6 = f32[8192]{0:T(1024)S(1)} collective-permute-done((f32[8192]{0:T(1024)S(1)}, f32[8192]{0:T(1024)S(1)}, u32[]{:S(2)}, u32[]{:S(2)}) %collective-permute-start.6) | collective-permute-done | bytes 32800 | tf_op jit(solution)/shard_map/ppermute | solution.py:34
  127.6 4.8 %collective-permute-done.7 = f32[8192]{0:T(1024)S(1)} collective-permute-done((f32[8192]{0:T(1024)S(1)}, f32[8192]{0:T(1024)S(1)}, u32[]{:S(2)}, u32[]{:S(2)}) %collective-permute-start.7) | collective-permute-done | bytes 32800 | tf_op jit(solution)/shard_map/ppermute | solution.py:38
  132.8 3.9 %collective-permute-done.8 = f32[16384]{0:T(1024)S(1)} collective-permute-done((f32[16384]{0:T(1024)S(1)}, f32[16384]{0:T(1024)S(1)}, u32[]{:S(2)}, u32[]{:S(2)}) %collective-permute-start.8) | collective-permute-done | bytes 65568 | tf_op jit(solution)/shard_map/ppermute | solution.py:38
  136.7 0.9 collective-permute-start.9
  138.3 3.5 %collective-permute-done.9 = f32[32768]{0:T(1024)S(1)} collective-permute-done((f32[32768]{0:T(1024)S(1)}, f32[32768]{0:T(1024)S(1)}, u32[]{:S(2)}, u32[]{:S(2)}) %collective-permute-start.9) | collective-permute-done | bytes 131104 | tf_op jit(solution)/shard_map/ppermute | solution.py:38
  141.8 4.1 %collective-permute-start.10 = (f32[65536]{0:T(1024)S(1)}, f32[65536]{0:T(1024)S(1)}, u32[]{:S(2)}, u32[]{:S(2)}) collective-permute-start(f32[65536]{0:T(1024)S(1)} %maximum_select_fusion.4), channel_id=1, source_target_pairs={{0,2},{1,3},{2,0},{3,1},{4,6},{5,7},{6,4},{7,5},{8,10},{9,11},{10,... | collective-permute-start | bytes 786440 | tf_op jit(solution)/shard_map/ppermute | solution.py:38
  145.9 0.8 convolution_add_fusion
  146.6 3.6 %collective-permute-done.10 = f32[65536]{0:T(1024)S(1)} collective-permute-done((f32[65536]{0:T(1024)S(1)}, f32[65536]{0:T(1024)S(1)}, u32[]{:S(2)}, u32[]{:S(2)}) %collective-permute-start.10) | collective-permute-done | bytes 262176 | tf_op jit(solution)/shard_map/ppermute | solution.py:38
  150.4 1.3 convolution_add_fusion.4
  152.5 1.0 fusion.59
  (95 shorter events, 7.6 us)
Async XLA Ops:
  0.6 10.0 %copy-start = (bf16[256,256]{1,0:T(8,128)(2,1)S(1)}, bf16[256,256]{1,0:T(8,128)(2,1)}, u32[]{:S(2)}) copy-start(bf16[256,256]{1,0:T(8,128)(2,1)} %param.15) | copy-start | bytes 393220
  2.8 7.4 %collective-permute-start = (bf16[4,128,256]{2,1,0:T(8,128)(2,1)S(1)}, bf16[4,128,256]{2,1,0:T(8,128)(2,1)S(1)}, u32[]{:S(2)}, u32[]{:S(2)}) collective-permute-start(bf16[4,128,256]{2,1,0:T(8,128)(2,1)S(1)} %convolution_convert_fusion.7), channel_id=1, source_target_pairs={{0,1},{1,2},{2,3},{3,4},{4,5},{5,6},{6,7},{7,0},{8,9},{9,10},{10,1... | collective-permute-start | bytes 786440 | tf_op jit(solution)/shard_map/ppermute | solution.py:12
  4.5 2.4 %copy-start.16 = (s32[4,1024]{1,0:T(4,128)S(1)}, s32[4,1024]{1,0:T(4,128)}, u32[]{:S(2)}) copy-start(s32[4,1024]{1,0:T(4,128)} %param.12) | copy-start | bytes 49156
  4.6 2.4 %copy-start.18 = (s32[4,1024]{1,0:T(4,128)S(1)}, s32[4,1024]{1,0:T(4,128)}, u32[]{:S(2)}) copy-start(s32[4,1024]{1,0:T(4,128)} %param.11) | copy-start | bytes 49156
  7.0 1.7 %copy-start.5 = (bf16[4,256,256]{2,1,0:T(8,128)(2,1)}, bf16[4,256,256]{2,1,0:T(8,128)(2,1)S(1)}, u32[]{:S(2)}) copy-start(bf16[4,256,256]{2,1,0:T(8,128)(2,1)S(1)} %fusion.20) | copy-start | bytes 1572868
  7.0 1.4 copy-start.1
  8.3 2.2 %copy-start.9 = (bf16[4,256,128]{2,1,0:T(8,128)(2,1)}, bf16[4,256,128]{2,1,0:T(8,128)(2,1)S(1)}, u32[]{:S(2)}) copy-start(bf16[4,256,128]{2,1,0:T(8,128)(2,1)S(1)} %fusion.21) | copy-start | bytes 786436
  10.6 1.4 copy-start.3
  12.0 6.8 %copy-start.2 = (bf16[16,1,1,64,256]{4,3,2,1,0:T(8,128)(2,1)S(1)}, bf16[16,1,1,64,256]{4,3,2,1,0:T(8,128)(2,1)}, u32[]{:S(2)}) copy-start(bf16[16,1,1,64,256]{4,3,2,1,0:T(8,128)(2,1)} %param.19) | copy-start | bytes 1572868
  13.2 20.6 %all-to-all-start = ((bf16[4,256,256]{2,0,1:T(4,128)(2,1)}), bf16[4,256,256]{2,0,1:T(4,128)(2,1)S(1)}, u32[]{:S(2)}, u32[]{:S(2)}) async-start(bf16[4,256,256]{2,0,1:T(4,128)(2,1)} %copy.58), calls=%async_computation | async-start | bytes 1048576 | tf_op jit(solution)/shard_map/all_to_all | solution.py:199
  18.8 15.1 %copy-start.14 = (bf16[256,256]{1,0:T(8,128)(2,1)S(1)}, bf16[256,256]{1,0:T(8,128)(2,1)}, u32[]{:S(2)}) copy-start(bf16[256,256]{1,0:T(8,128)(2,1)} %param.17) | copy-start | bytes 393220
  33.8 1.8 %copy-start.12 = (bf16[256,256]{1,0:T(8,128)(2,1)S(1)}, bf16[256,256]{1,0:T(8,128)(2,1)}, u32[]{:S(2)}) copy-start(bf16[256,256]{1,0:T(8,128)(2,1)} %param.16) | copy-start | bytes 393220
  34.2 3.1 %copy-start.13 = (bf16[256,256]{1,0:T(8,128)(2,1)S(1)}, bf16[256,256]{1,0:T(8,128)(2,1)}, u32[]{:S(2)}) copy-start(bf16[256,256]{1,0:T(8,128)(2,1)} %param.18) | copy-start | bytes 393220
  47.9 6.1 %copy-start.8 = (bf16[16,64,4,64]{3,2,1,0:T(4,128)(2,1)S(1)}, bf16[16,64,4,64]{3,2,1,0:T(4,128)(2,1)}, u32[]{:S(2)}) copy-start(bf16[16,64,4,64]{3,2,1,0:T(4,128)(2,1)} %reshape.153) | copy-start | bytes 1572868
  71.3 2.4 %copy-start.15 = (bf16[256,256]{1,0:T(8,128)(2,1)S(1)}, bf16[256,256]{1,0:T(8,128)(2,1)}, u32[]{:S(2)}) copy-start(bf16[256,256]{1,0:T(8,128)(2,1)} %param.17) | copy-start | bytes 393220
  77.6 5.9 %copy-start.7 = (f32[32,2,8,128]{3,2,1,0:T(8,128)S(1)}, f32[32,2,8,128]{3,2,1,0:T(8,128)}, u32[]{:S(2)}) copy-start(f32[32,2,8,128]{3,2,1,0:T(8,128)} %convolution_bitcast_fusion.1) | copy-start | bytes 786436
  80.1 17.6 %all-to-all-start.1 = ((bf16[16,64,256]{2,1,0:T(8,128)(2,1)}), bf16[16,64,256]{2,1,0:T(8,128)(2,1)S(1)}, u32[]{:S(2)}, u32[]{:S(2)}) async-start(bf16[16,64,256]{2,1,0:T(8,128)(2,1)} %bitcast.10), calls=%async_computation.1 | async-start | bytes 1048576 | tf_op jit(solution)/shard_map/all_to_all | solution.py:202
  97.7 1.8 %copy-start.4 = (bf16[4,256,256]{2,1,0:T(8,128)(2,1)S(1)}, bf16[4,256,256]{2,1,0:T(8,128)(2,1)}, u32[]{:S(2)}) copy-start(bf16[4,256,256]{2,1,0:T(8,128)(2,1)} %copy-done.3) | copy-start | bytes 1572868
  97.8 2.2 %copy-start.11 = (f32[32,2,8,128]{3,1,2,0:T(2,128)S(1)}, f32[32,2,8,128]{3,1,2,0:T(2,128)}, u32[]{:S(2)}) copy-start(f32[32,2,8,128]{3,1,2,0:T(2,128)} %copy.82) | copy-start | bytes 786436
  100.2 2.1 %collective-permute-start.2 = (f32[131072]{0:T(1024)S(1)}, f32[131072]{0:T(1024)}, u32[]{:S(2)}, u32[]{:S(2)}) collective-permute-start(f32[131072]{0:T(1024)S(1)} %broadcast_select_fusion), channel_id=1, source_target_pairs={{0,1},{1,0},{2,3},{3,2},{4,5},{5,4},{6,7},{7,6},{8,9},{9,8},{10,11... | collective-permute-start | bytes 1572872 | tf_op jit(solution)/shard_map/ppermute | solution.py:34
  103.5 9.0 %collective-permute-start.3 = (f32[65536]{0:T(1024)S(1)}, f32[65536]{0:T(1024)S(1)}, u32[]{:S(2)}, u32[]{:S(2)}) collective-permute-start(f32[65536]{0:T(1024)S(1)} %slice_select_fusion), channel_id=1, source_target_pairs={{0,2},{1,3},{2,0},{3,1},{4,6},{5,7},{6,4},{7,5},{8,10},{9,11},{10,... | collective-permute-start | bytes 786440 | tf_op jit(solution)/shard_map/ppermute | solution.py:34
  112.6 5.1 %collective-permute-start.4 = (f32[32768]{0:T(1024)S(1)}, f32[32768]{0:T(1024)S(1)}, u32[]{:S(2)}, u32[]{:S(2)}) collective-permute-start(f32[32768]{0:T(1024)S(1)} %slice_select_fusion.1), channel_id=1, source_target_pairs={{0,4},{1,5},{2,6},{3,7},{4,0},{5,1},{6,2},{7,3},{8,12},{9,13},{10,... | collective-permute-start | bytes 393224 | tf_op jit(solution)/shard_map/ppermute | solution.py:34
  117.7 4.3 %collective-permute-start.5 = (f32[16384]{0:T(1024)S(1)}, f32[16384]{0:T(1024)S(1)}, u32[]{:S(2)}, u32[]{:S(2)}) collective-permute-start(f32[16384]{0:T(1024)S(1)} %slice_select_fusion.2), channel_id=1, source_target_pairs={{0,8},{8,0},{16,24},{24,16},{1,9},{9,1},{17,25},{25,17},{2,10},{10... | collective-permute-start | bytes 196616 | tf_op jit(solution)/shard_map/ppermute | solution.py:34
  122.1 5.4 %collective-permute-start.6 = (f32[8192]{0:T(1024)S(1)}, f32[8192]{0:T(1024)S(1)}, u32[]{:S(2)}, u32[]{:S(2)}) collective-permute-start(f32[8192]{0:T(1024)S(1)} %slice_select_fusion.3), channel_id=1, source_target_pairs={{0,16},{8,24},{16,0},{24,8},{1,17},{9,25},{17,1},{25,9},{2,18},{10... | collective-permute-start | bytes 98312 | tf_op jit(solution)/shard_map/ppermute | solution.py:34
  127.5 10.2 %copy-start.10 = (bf16[4,256,128]{2,1,0:T(8,128)(2,1)S(1)}, bf16[4,256,128]{2,1,0:T(8,128)(2,1)}, u32[]{:S(2)}) copy-start(bf16[4,256,128]{2,1,0:T(8,128)(2,1)} %copy-done.9) | copy-start | bytes 786436
  127.5 4.9 %collective-permute-start.7 = (f32[8192]{0:T(1024)S(1)}, f32[8192]{0:T(1024)S(1)}, u32[]{:S(2)}, u32[]{:S(2)}) collective-permute-start(f32[8192]{0:T(1024)S(1)} %select_add_fusion.4), channel_id=1, source_target_pairs={{0,16},{8,24},{16,0},{24,8},{1,17},{9,25},{17,1},{25,9},{2,18},{10... | collective-permute-start | bytes 98312 | tf_op jit(solution)/shard_map/ppermute | solution.py:38
  132.4 4.3 %collective-permute-start.8 = (f32[16384]{0:T(1024)S(1)}, f32[16384]{0:T(1024)S(1)}, u32[]{:S(2)}, u32[]{:S(2)}) collective-permute-start(f32[16384]{0:T(1024)S(1)} %maximum_select_fusion.7), channel_id=1, source_target_pairs={{0,8},{8,0},{16,24},{24,16},{1,9},{9,1},{17,25},{25,17},{2,10},{10... | collective-permute-start | bytes 196616 | tf_op jit(solution)/shard_map/ppermute | solution.py:38
  132.8 13.1 %copy-start.6 = (bf16[4,256,256]{2,1,0:T(8,128)(2,1)S(1)}, bf16[4,256,256]{2,1,0:T(8,128)(2,1)}, u32[]{:S(2)}) copy-start(bf16[4,256,256]{2,1,0:T(8,128)(2,1)} %copy-done.5) | copy-start | bytes 1572868
  136.7 5.0 %collective-permute-start.9 = (f32[32768]{0:T(1024)S(1)}, f32[32768]{0:T(1024)S(1)}, u32[]{:S(2)}, u32[]{:S(2)}) collective-permute-start(f32[32768]{0:T(1024)S(1)} %maximum_select_fusion.6), channel_id=1, source_target_pairs={{0,4},{1,5},{2,6},{3,7},{4,0},{5,1},{6,2},{7,3},{8,12},{9,13},{10,... | collective-permute-start | bytes 393224 | tf_op jit(solution)/shard_map/ppermute | solution.py:38
  138.2 12.2 %collective-permute-start.1 = (bf16[4,128,256]{2,1,0:T(8,128)(2,1)S(1)}, bf16[4,128,256]{2,1,0:T(8,128)(2,1)S(1)}, u32[]{:S(2)}, u32[]{:S(2)}) collective-permute-start(bf16[4,128,256]{2,1,0:T(8,128)(2,1)S(1)} %convolution_convert_fusion.6), channel_id=1, source_target_pairs={{0,7},{1,0},{2,1},{3,2},{4,3},{5,4},{6,5},{7,6},{8,15},{9,8},{10,9... | collective-permute-start | bytes 786440 | tf_op jit(solution)/shard_map/ppermute | solution.py:12
  141.8 8.5 %collective-permute-start.10 = (f32[65536]{0:T(1024)S(1)}, f32[65536]{0:T(1024)S(1)}, u32[]{:S(2)}, u32[]{:S(2)}) collective-permute-start(f32[65536]{0:T(1024)S(1)} %maximum_select_fusion.4), channel_id=1, source_target_pairs={{0,2},{1,3},{2,0},{3,1},{4,6},{5,7},{6,4},{7,5},{8,10},{9,11},{10,... | collective-permute-start | bytes 786440 | tf_op jit(solution)/shard_map/ppermute | solution.py:38
  145.9 4.5 %copy-start.17 = (s32[4,128]{1,0:T(4,128)S(1)}, s32[4,128]{1,0:T(4,128)}, u32[]{:S(2)}) copy-start(s32[4,128]{1,0:T(4,128)} %param.13) | copy-start | bytes 6148
  150.3 2.0 %collective-permute-start.11 = (f32[131072]{0:T(1024)S(1)}, f32[131072]{0:T(1024)S(1)}, u32[]{:S(2)}, u32[]{:S(2)}) collective-permute-start(f32[131072]{0:T(1024)S(1)} %maximum_select_fusion.2), channel_id=1, source_target_pairs={{0,1},{1,0},{2,3},{3,2},{4,5},{5,4},{6,7},{7,6},{8,9},{9,8},{10,11... | collective-permute-start | bytes 1572872 | tf_op jit(solution)/shard_map/ppermute | solution.py:38

commit v3 on v2

--- a/solution.py
+++ b/solution.py
@@ -151,6 +151,72 @@
     return ((weight_grad(query_flat), weight_grad(key_flat), weight_grad(value_flat)), back)
 
 
+def attend_blocked(states, upstream, w_query, w_key, w_value):
+    steps_all, nodes_here, width = states.shape
+    head_dim = width // HEADS
+    scale_factor = head_dim ** (-0.5)
+    per_group = max(1, 128 // steps_all)
+    if nodes_here % per_group:
+        per_group = 1
+    groups = nodes_here // per_group
+    block = per_group * steps_all
+    flat = jnp.swapaxes(states, 0, 1).reshape(nodes_here * steps_all, width)
+    up_flat = jnp.swapaxes(upstream, 0, 1).reshape(nodes_here * steps_all, width)
+
+    def project(weight):
+        return jnp.dot(flat, weight, preferred_element_type=jnp.float32).astype(jnp.bfloat16)
+
+    def blocks(matrix):
+        return matrix.reshape(groups, block, HEADS, head_dim)
+
+    queries = blocks(project(w_query))
+    key_rows = blocks(project(w_key))
+    value_rows = blocks(project(w_value))
+    up_heads = blocks(up_flat)
+    position = jnp.arange(block)
+    same = (position[:, None] // steps_all) == (position[None, :] // steps_all)
+    causal = jnp.logical_and(same, (position[:, None] % steps_all) >= (position[None, :] % steps_all))
+
+    def contract(spec, left, right):
+        return jnp.einsum(spec, left, right, preferred_element_type=jnp.float32)
+
+    scores = contract("gihd,gjhd->ghij", queries, key_rows) * scale_factor
+    scores = jnp.where(causal, scores, -jnp.inf)
+    highest = jnp.max(scores, axis=-1, keepdims=True)
+    exponent = jnp.exp(scores - highest)
+    probs = exponent / jnp.sum(exponent, axis=-1, keepdims=True)
+    probs_low = probs.astype(jnp.bfloat16)
+    value_grad = contract("ghij,gihd->gjhd", probs_low, up_heads).astype(jnp.bfloat16)
+    prob_grad = contract("gihd,gjhd->ghij", up_heads, value_rows)
+    score_grad = (
+        probs * (prob_grad - jnp.sum(prob_grad * probs, axis=-1, keepdims=True)) * scale_factor
+    ).astype(jnp.bfloat16)
+    query_grad = contract("ghij,gjhd->gihd", score_grad, key_rows).astype(jnp.bfloat16)
+    key_grad = contract("ghij,gihd->gjhd", score_grad, queries).astype(jnp.bfloat16)
+    query_flat = query_grad.reshape(-1, width)
+    key_flat = key_grad.reshape(-1, width)
+    value_flat = value_grad.reshape(-1, width)
+
+    def weight_grad(grad_rows):
+        return lax.dot_general(
+            flat, grad_rows, (((0,), (0,)), ((), ())), preferred_element_type=jnp.float32
+        )
+
+    def input_grad(grad_rows, weight):
+        return lax.dot_general(
+            grad_rows, weight, (((1,), (1,)), ((), ())), preferred_element_type=jnp.float32
+        )
+
+    back = (
+        up_flat.astype(jnp.float32)
+        + input_grad(query_flat, w_query)
+        + input_grad(key_flat, w_key)
+        + input_grad(value_flat, w_value)
+    )
+    back = jnp.swapaxes(back.astype(jnp.bfloat16).reshape(nodes_here, steps_all, width), 0, 1)
+    return ((weight_grad(query_flat), weight_grad(key_flat), weight_grad(value_flat)), back)
+
+
 def local(
     node_states,
     edge_source,
@@ -198,7 +264,7 @@
 
     node_major = lax.all_to_all(hidden, "day", split_axis=1, concat_axis=0, tiled=True)
     upstream = cotangent.reshape(cotangent.shape[0], -1, width)
-    attn_grads, back = attend(node_major, upstream, w_query, w_key, w_value)
+    attn_grads, back = attend_blocked(node_major, upstream, w_query, w_key, w_value)
     back_days = lax.all_to_all(back, "day", split_axis=0, concat_axis=1, tiled=True)
 
     sigmoid_val = jax.nn.sigmoid(preact)

time: 154 us -> 144 us (0.935)
  matrix products: 40.4 us -> 36 us
  local copies, waits for them, and re-layouts: 20.4 us -> 17.7 us
  waiting for transfers between devices: 67.4 us -> 65.2 us
    convert_element_type x3 -> x4, local copies, waits for them, and re-layouts: 8.93 us -> 1.65 us  [the longest x1 0.61 us: attend_blocked(): up_flat.astype(jnp.float32) + input_grad(query_flat, w_query)]
    dot_general x4, matrix products: 18.1 us -> 14.4 us  [contract(): return jnp.einsum(spec, left, right, preferred_element_type=jnp.float32)]
    dot_general x3, matrix products: 1.68 us -> 5.13 us  [project(): jnp.dot(flat, weight, preferred_element_type=jnp.float32)]
    reshape x6, local copies, waits for them, and re-layouts: 6.98 us -> 9.65 us  [the longest x5 8.68 us: blocks(): return matrix.reshape(groups, block, HEADS, head_dim)]
    dot_general x3, matrix products: 3.71 us -> 1.06 us  [input_grad(): lax.dot_general(grad_rows, weight, (((1,), (1,)), ((), ())), preferred_el...]
    all_to_all x1, waiting for transfers between devices: 14.5 us -> 12.2 us  [local(): lax.all_to_all(hidden, 'day', split_axis=1, concat_axis=0, tiled=True)]
  transfers between devices with their start and end apart: 14 -> 14, of which waited for: 13 -> 13; matrix products, arithmetic and copies ran while one was open for 7% -> 9% of each run, Pallas kernels for 0% -> 0%
where the time goes in v3:
time: 144 us; the launch traced here: 143 us
  waiting for transfers between devices  65.2 us (45%)
  matrix products  36 us (25%)
  starting transfers between devices  17.9 us (12%)
  local copies, waits for them, and re-layouts  17.7 us (12%)
  other arithmetic  4.81 us (3%)
    ppermute x5, waiting for transfers between devices, tree_sum(): flat = keep + lax.ppermute(send, axis, pairs)  22.3 us
    ppermute x5, waiting for transfers between devices, tree_sum(): other = lax.ppermute(flat, axis, pairs)  16.2 us
    dot_general x4, matrix products, contract(): return jnp.einsum(spec, left, right, preferred_element_type=jnp.float32)  14.4 us
    all_to_all x1, waiting for transfers between devices, local(): lax.all_to_all(back, 'day', split_axis=0, concat_axis=1, tiled=True)  12.9 us
    all_to_all x1, waiting for transfers between devices, local(): lax.all_to_all(hidden, 'day', split_axis=1, concat_axis=0, tiled=True)  12.2 us
    reshape x5, local copies, waits for them, and re-layouts, blocks(): return matrix.reshape(groups, block, HEADS, head_dim)  8.68 us
    all_to_all x1, starting transfers between devices, local(): lax.all_to_all(hidden, 'day', split_axis=1, concat_axis=0, tiled=True)  5.62 us
    dot_general x3, matrix products, project(): jnp.dot(flat, weight, preferred_element_type=jnp.float32)  5.13 us
  transfers between devices with their start and end apart: 14, of which 13 were waited for; matrix products, arithmetic and copies ran while one was open for 9% of the time, Pallas kernels for 0%

profile of v3, /device:TPU:0, one launch (start us, length us, event | category | flops | bytes accessed | tf_op | source)
XLA Modules:
  0.0 143.0 jit_solution(8215435144741459609)
XLA Ops:
  0.6 0.8 iota_compare_fusion.12
  1.4 1.4 convolution_convert_fusion.7
  3.3 1.2 convert_reduce_fusion
  4.6 2.4 %fusion.17 = bf16[4,256,256]{2,1,0:T(8,128)(2,1)S(1)} fusion(s32[4,1024]{1,0:T(4,128)} %param.11, s32[4,1024]{1,0:T(4,128)} %param.12), kind=kOutput, calls=%fused_computation.38 | convolution fusion | flops 539230208 | bytes 557056 | tf_op jit(solution)/shard_map/der,des->drs/dot_general | solution.py:248
  7.0 1.3 fusion.21
  8.7 1.6 %collective-permute-done = bf16[4,128,256]{2,1,0:T(8,128)(2,1)S(1)} collective-permute-done((bf16[4,128,256]{2,1,0:T(8,128)(2,1)S(1)}, bf16[4,128,256]{2,1,0:T(8,128)(2,1)S(1)}, u32[]{:S(2)}, u32[]{:S(2)}) %collective-permute-start) | collective-permute-done | bytes 262176 | tf_op jit(solution)/shard_map/ppermute | solution.py:12
  10.6 1.3 fusion.24
  12.0 1.2 copy.78
  13.2 5.6 %all-to-all-start = ((bf16[4,256,256]{2,0,1:T(4,128)(2,1)}), bf16[4,256,256]{2,0,1:T(4,128)(2,1)S(1)}, u32[]{:S(2)}, u32[]{:S(2)}) async-start(bf16[4,256,256]{2,0,1:T(4,128)(2,1)} %copy.78), calls=%async_computation | async-start | bytes 1048576 | tf_op jit(solution)/shard_map/all_to_all | solution.py:265
  19.5 0.6 copy.89
  20.2 0.6 copy.76
  20.8 0.7 compare_and_fusion
  21.6 12.2 %all-to-all-done = bf16[4,256,256]{2,0,1:T(4,128)(2,1)S(1)} async-done(((bf16[4,256,256]{2,0,1:T(4,128)(2,1)}), bf16[4,256,256]{2,0,1:T(4,128)(2,1)S(1)}, u32[]{:S(2)}, u32[]{:S(2)}) %all-to-all-start) | async-done | bytes 524320 | tf_op jit(solution)/shard_map/all_to_all | solution.py:265
  34.2 1.1 convolution_convert_fusion.1
  35.3 2.0 %reshape.279 = bf16[8,128,4,64]{3,2,1,0:T(4,128)(2,1)S(1)} reshape(bf16[1024,256]{1,0:T(8,128)(2,1)} %convolution_convert_fusion.1) | data formatting | bytes 1048576 | tf_op jit(solution)/shard_map/reshape | solution.py:170
  37.3 1.2 copy.84
  38.5 2.0 %convolution_convert_fusion.2 = bf16[1024,256]{1,0:T(8,128)(2,1)} fusion(bf16[1024,256]{1,0:T(8,128)(2,1)S(1)} %bitcast.135, bf16[256,256]{1,0:T(8,128)(2,1)} %param.17), kind=kOutput, calls=%fused_computation.33 | convolution fusion | flops 134479872 | bytes 1179648 | tf_op jit(solution)/shard_map/dot_general | solution.py:167
  40.5 2.0 %reshape.278 = bf16[8,128,4,64]{3,2,1,0:T(4,128)(2,1)S(1)} reshape(bf16[1024,256]{1,0:T(8,128)(2,1)} %convolution_convert_fusion.2) | data formatting | bytes 1048576 | tf_op jit(solution)/shard_map/reshape | solution.py:170
  42.6 1.2 copy.90
  43.8 2.0 %convolution_convert_fusion = bf16[1024,256]{1,0:T(8,128)(2,1)} fusion(bf16[1024,256]{1,0:T(8,128)(2,1)S(1)} %bitcast.136, bf16[256,256]{1,0:T(8,128)(2,1)} %param.18), kind=kOutput, calls=%fused_computation.31 | convolution fusion | flops 134479872 | bytes 1179648 | tf_op jit(solution)/shard_map/dot_general | solution.py:167
  45.8 2.2 %reshape.277 = bf16[8,128,4,64]{3,2,1,0:T(4,128)(2,1)S(1)} reshape(bf16[1024,256]{1,0:T(8,128)(2,1)} %convolution_convert_fusion) | data formatting | bytes 1048576 | tf_op jit(solution)/shard_map/reshape | solution.py:170
  48.0 1.7 %fusion.27 = f32[8,4,128,128]{3,2,1,0:T(8,128)} fusion(bf16[8,128,4,64]{1,3,2,0:T(8,128)(2,1)S(1)} %copy.89, bf16[8,128,4,64]{3,2,1,0:T(4,128)(2,1)S(1)} %reshape.277), kind=kOutput, calls=%fused_computation.56 | convolution fusion | flops 67108864 | bytes 3145728 | tf_op jit(solution)/shard_map/gihd,gjhd->ghij/dot_general | solution.py:181
  49.8 4.0 %fusion.67 = (f32[8,4,128]{2,1,0:T(4,128)}, f32[8,4,128,128]{2,3,1,0:T(8,128)}) fusion(pred[128,128]{0,1:T(8,128)(4,1)} %compare_and_fusion, bf16[8,128,4,64]{1,3,2,0:T(8,128)(2,1)} %copy.84, bf16[8,128,4,64]{1,3,2,0:T(8,128)(2,1)} %copy.90), kind=kOutput, calls=%fused_computation.128 | convolution fusion | flops 69206144 | bytes 3178496 | tf_op jit(solution)/shard_map/sub | solution.py:186
  53.8 5.1 %fusion.19 = bf16[8,128,4,64]{1,3,2,0:T(8,128)(2,1)} fusion(bf16[8,128,4,64]{1,3,2,0:T(8,128)(2,1)S(1)} %copy-done.9, f32[8,4,128,128]{3,2,1,0:T(8,128)} %fusion.27, f32[8,4,128,128]{2,3,1,0:T(8,128)} %get-tuple-element.12, f32[8,4,128]{2,1,0:T(4,128)} %get-tuple-element.11), kind=kOutput, calls=%fused_computation.40 | convolution fusion | flops 71045248 | bytes 5259264 | tf_op jit(solution)/shard_map/ghij,gihd->gjhd/dot_general | solution.py:181
  58.9 5.0 %fusion.18 = bf16[8,128,4,64]{1,3,2,0:T(8,128)(2,1)} fusion(bf16[8,128,4,64]{1,3,2,0:T(8,128)(2,1)S(1)} %copy-done.10, f32[8,4,128,128]{3,2,1,0:T(8,128)} %fusion.27, f32[8,4,128,128]{2,3,1,0:T(8,128)} %get-tuple-element.12, f32[8,4,128]{2,1,0:T(4,128)} %get-tuple-element.11), kind=kOutput, calls=%fused_computation.39 | convolution fusion | flops 71045248 | bytes 5259264 | tf_op jit(solution)/shard_map/ghij,gjhd->gihd/dot_general | solution.py:181
  63.9 2.5 %fusion.20 = bf16[8,128,4,64]{1,3,2,0:T(8,128)(2,1)S(1)} fusion(bf16[8,128,4,64]{1,3,2,0:T(8,128)(2,1)S(1)} %copy.89, f32[8,4,128,128]{2,3,1,0:T(8,128)} %get-tuple-element.12, f32[8,4,128]{2,1,0:T(4,128)S(1)} %copy-done.20), kind=kOutput, calls=%fused_computation.41 | convolution fusion | flops 68419584 | bytes 3162112 | tf_op jit(solution)/shard_map/ghij,gihd->gjhd/dot_general | solution.py:181
  69.9 1.0 copy.151
  70.8 3.5 %all-to-all-start.1 = ((bf16[16,64,256]{2,1,0:T(8,128)(2,1)}), bf16[16,64,256]{2,1,0:T(8,128)(2,1)S(1)}, u32[]{:S(2)}, u32[]{:S(2)}) async-start(bf16[16,64,256]{2,1,0:T(8,128)(2,1)} %bitcast.133), calls=%async_computation.1 | async-start | bytes 1048576 | tf_op jit(solution)/shard_map/all_to_all | solution.py:268
  74.3 0.8 copy.121
  75.5 12.9 %all-to-all-done.1 = bf16[16,64,256]{2,1,0:T(8,128)(2,1)S(1)} async-done(((bf16[16,64,256]{2,1,0:T(8,128)(2,1)}), bf16[16,64,256]{2,1,0:T(8,128)(2,1)S(1)}, u32[]{:S(2)}, u32[]{:S(2)}) %all-to-all-start.1) | async-done | bytes 524320 | tf_op jit(solution)/shard_map/all_to_all | solution.py:268
  90.2 2.0 %collective-permute-done.2 = f32[131072]{0:T(1024)} collective-permute-done((f32[131072]{0:T(1024)S(1)}, f32[131072]{0:T(1024)}, u32[]{:S(2)}, u32[]{:S(2)}) %collective-permute-start.2) | collective-permute-done | bytes 524320 | tf_op jit(solution)/shard_map/ppermute | solution.py:34
  92.2 1.1 select_add_fusion
  93.4 2.5 %collective-permute-start.3 = (f32[65536]{0:T(1024)S(1)}, f32[65536]{0:T(1024)S(1)}, u32[]{:S(2)}, u32[]{:S(2)}) collective-permute-start(f32[65536]{0:T(1024)S(1)} %slice_select_fusion), channel_id=1, source_target_pairs={{0,2},{1,3},{2,0},{3,1},{4,6},{5,7},{6,4},{7,5},{8,10},{9,11},{10,... | collective-permute-start | bytes 786440 | tf_op jit(solution)/shard_map/ppermute | solution.py:34
  95.9 6.6 %collective-permute-done.3 = f32[65536]{0:T(1024)S(1)} collective-permute-done((f32[65536]{0:T(1024)S(1)}, f32[65536]{0:T(1024)S(1)}, u32[]{:S(2)}, u32[]{:S(2)}) %collective-permute-start.3) | collective-permute-done | bytes 262176 | tf_op jit(solution)/shard_map/ppermute | solution.py:34
  102.5 1.0 collective-permute-start.4
  103.5 4.1 %collective-permute-done.4 = f32[32768]{0:T(1024)S(1)} collective-permute-done((f32[32768]{0:T(1024)S(1)}, f32[32768]{0:T(1024)S(1)}, u32[]{:S(2)}, u32[]{:S(2)}) %collective-permute-start.4) | collective-permute-done | bytes 131104 | tf_op jit(solution)/shard_map/ppermute | solution.py:34
  107.8 4.2 %collective-permute-done.5 = f32[16384]{0:T(1024)S(1)} collective-permute-done((f32[16384]{0:T(1024)S(1)}, f32[16384]{0:T(1024)S(1)}, u32[]{:S(2)}, u32[]{:S(2)}) %collective-permute-start.5) | collective-permute-done | bytes 65568 | tf_op jit(solution)/shard_map/ppermute | solution.py:34
  112.1 5.4 %collective-permute-done.6 = f32[8192]{0:T(1024)S(1)} collective-permute-done((f32[8192]{0:T(1024)S(1)}, f32[8192]{0:T(1024)S(1)}, u32[]{:S(2)}, u32[]{:S(2)}) %collective-permute-start.6) | collective-permute-done | bytes 32800 | tf_op jit(solution)/shard_map/ppermute | solution.py:34
  117.5 4.8 %collective-permute-done.7 = f32[8192]{0:T(1024)S(1)} collective-permute-done((f32[8192]{0:T(1024)S(1)}, f32[8192]{0:T(1024)S(1)}, u32[]{:S(2)}, u32[]{:S(2)}) %collective-permute-start.7) | collective-permute-done | bytes 32800 | tf_op jit(solution)/shard_map/ppermute | solution.py:38
  122.8 3.9 %collective-permute-done.8 = f32[16384]{0:T(1024)S(1)} collective-permute-done((f32[16384]{0:T(1024)S(1)}, f32[16384]{0:T(1024)S(1)}, u32[]{:S(2)}, u32[]{:S(2)}) %collective-permute-start.8) | collective-permute-done | bytes 65568 | tf_op jit(solution)/shard_map/ppermute | solution.py:38
  126.7 0.8 collective-permute-start.9
  127.5 0.6 convolution_convert_fusion.6
  128.1 3.6 %collective-permute-done.9 = f32[32768]{0:T(1024)S(1)} collective-permute-done((f32[32768]{0:T(1024)S(1)}, f32[32768]{0:T(1024)S(1)}, u32[]{:S(2)}, u32[]{:S(2)}) %collective-permute-start.9) | collective-permute-done | bytes 131104 | tf_op jit(solution)/shard_map/ppermute | solution.py:38
  131.7 3.7 %collective-permute-start.10 = (f32[65536]{0:T(1024)S(1)}, f32[65536]{0:T(1024)S(1)}, u32[]{:S(2)}, u32[]{:S(2)}) collective-permute-start(f32[65536]{0:T(1024)S(1)} %maximum_select_fusion.4), channel_id=1, source_target_pairs={{0,2},{1,3},{2,0},{3,1},{4,6},{5,7},{6,4},{7,5},{8,10},{9,11},{10,... | collective-permute-start | bytes 786440 | tf_op jit(solution)/shard_map/ppermute | solution.py:38
  135.4 0.8 convolution_add_fusion
  136.2 3.6 %collective-permute-done.10 = f32[65536]{0:T(1024)S(1)} collective-permute-done((f32[65536]{0:T(1024)S(1)}, f32[65536]{0:T(1024)S(1)}, u32[]{:S(2)}, u32[]{:S(2)}) %collective-permute-start.10) | collective-permute-done | bytes 262176 | tf_op jit(solution)/shard_map/ppermute | solution.py:38
  139.9 1.3 convolution_add_fusion.4
  142.0 1.0 fusion.66
  (106 shorter events, 9.5 us)
Async XLA Ops:
  0.6 10.0 %copy-start = (bf16[256,256]{1,0:T(8,128)(2,1)S(1)}, bf16[256,256]{1,0:T(8,128)(2,1)}, u32[]{:S(2)}) copy-start(bf16[256,256]{1,0:T(8,128)(2,1)} %param.15) | copy-start | bytes 393220
  2.8 7.4 %collective-permute-start = (bf16[4,128,256]{2,1,0:T(8,128)(2,1)S(1)}, bf16[4,128,256]{2,1,0:T(8,128)(2,1)S(1)}, u32[]{:S(2)}, u32[]{:S(2)}) collective-permute-start(bf16[4,128,256]{2,1,0:T(8,128)(2,1)S(1)} %convolution_convert_fusion.7), channel_id=1, source_target_pairs={{0,1},{1,2},{2,3},{3,4},{4,5},{5,6},{6,7},{7,0},{8,9},{9,10},{10,1... | collective-permute-start | bytes 786440 | tf_op jit(solution)/shard_map/ppermute | solution.py:12
  4.5 2.4 %copy-start.17 = (s32[4,1024]{1,0:T(4,128)S(1)}, s32[4,1024]{1,0:T(4,128)}, u32[]{:S(2)}) copy-start(s32[4,1024]{1,0:T(4,128)} %param.12) | copy-start | bytes 49156
  4.6 2.4 %copy-start.19 = (s32[4,1024]{1,0:T(4,128)S(1)}, s32[4,1024]{1,0:T(4,128)}, u32[]{:S(2)}) copy-start(s32[4,1024]{1,0:T(4,128)} %param.11) | copy-start | bytes 49156
  7.0 1.7 %copy-start.5 = (bf16[4,256,256]{2,1,0:T(8,128)(2,1)}, bf16[4,256,256]{2,1,0:T(8,128)(2,1)S(1)}, u32[]{:S(2)}) copy-start(bf16[4,256,256]{2,1,0:T(8,128)(2,1)S(1)} %fusion.17) | copy-start | bytes 1572868
  7.0 1.4 copy-start.1
  10.6 1.4 copy-start.3
  12.0 6.8 %copy-start.2 = (bf16[16,1,1,64,256]{4,3,2,1,0:T(8,128)(2,1)S(1)}, bf16[16,1,1,64,256]{4,3,2,1,0:T(8,128)(2,1)}, u32[]{:S(2)}) copy-start(bf16[16,1,1,64,256]{4,3,2,1,0:T(8,128)(2,1)} %param.19) | copy-start | bytes 1572868
  13.2 20.6 %all-to-all-start = ((bf16[4,256,256]{2,0,1:T(4,128)(2,1)}), bf16[4,256,256]{2,0,1:T(4,128)(2,1)S(1)}, u32[]{:S(2)}, u32[]{:S(2)}) async-start(bf16[4,256,256]{2,0,1:T(4,128)(2,1)} %copy.78), calls=%async_computation | async-start | bytes 1048576 | tf_op jit(solution)/shard_map/all_to_all | solution.py:265
  20.8 13.4 %copy-start.14 = (bf16[256,256]{1,0:T(8,128)(2,1)S(1)}, bf16[256,256]{1,0:T(8,128)(2,1)}, u32[]{:S(2)}) copy-start(bf16[256,256]{1,0:T(8,128)(2,1)} %param.16) | copy-start | bytes 393220
  49.8 4.0 %copy-start.9 = (bf16[8,128,4,64]{1,3,2,0:T(8,128)(2,1)S(1)}, bf16[8,128,4,64]{1,3,2,0:T(8,128)(2,1)}, u32[]{:S(2)}) copy-start(bf16[8,128,4,64]{1,3,2,0:T(8,128)(2,1)} %copy.84) | copy-start | bytes 1572868
  53.8 5.1 %copy-start.10 = (bf16[8,128,4,64]{1,3,2,0:T(8,128)(2,1)S(1)}, bf16[8,128,4,64]{1,3,2,0:T(8,128)(2,1)}, u32[]{:S(2)}) copy-start(bf16[8,128,4,64]{1,3,2,0:T(8,128)(2,1)} %copy.90) | copy-start | bytes 1572868
  58.9 5.0 %copy-start.20 = (f32[8,4,128]{2,1,0:T(4,128)S(1)}, f32[8,4,128]{2,1,0:T(4,128)}, u32[]{:S(2)}) copy-start(f32[8,4,128]{2,1,0:T(4,128)} %get-tuple-element.11) | copy-start | bytes 49156
  63.9 2.5 %copy-start.12 = (bf16[8,128,4,64]{1,3,2,0:T(8,128)(2,1)S(1)}, bf16[8,128,4,64]{1,3,2,0:T(8,128)(2,1)}, u32[]{:S(2)}) copy-start(bf16[8,128,4,64]{1,3,2,0:T(8,128)(2,1)} %fusion.19) | copy-start | bytes 1572868
  63.9 2.9 %copy-start.13 = (bf16[8,128,4,64]{1,3,2,0:T(8,128)(2,1)S(1)}, bf16[8,128,4,64]{1,3,2,0:T(8,128)(2,1)}, u32[]{:S(2)}) copy-start(bf16[8,128,4,64]{1,3,2,0:T(8,128)(2,1)} %fusion.18) | copy-start | bytes 1572868
  66.5 1.1 copy-start.15
  67.5 0.9 copy-start.16
  68.4 1.1 copy-start.11
  70.8 17.5 %all-to-all-start.1 = ((bf16[16,64,256]{2,1,0:T(8,128)(2,1)}), bf16[16,64,256]{2,1,0:T(8,128)(2,1)S(1)}, u32[]{:S(2)}, u32[]{:S(2)}) async-start(bf16[16,64,256]{2,1,0:T(8,128)(2,1)} %bitcast.133), calls=%async_computation.1 | async-start | bytes 1048576 | tf_op jit(solution)/shard_map/all_to_all | solution.py:268
  75.5 13.1 %copy-start.7 = (f32[4,256,256]{2,1,0:T(8,128)S(1)}, f32[4,256,256]{2,1,0:T(8,128)}, u32[]{:S(2)}) copy-start(f32[4,256,256]{2,1,0:T(8,128)} %get-tuple-element.10) | copy-start | bytes 3145732
  88.5 1.0 copy-start.4
  88.6 1.4 %copy-start.8 = (f32[32,2,8,128]{3,1,2,0:T(2,128)S(1)}, f32[32,2,8,128]{3,1,2,0:T(2,128)}, u32[]{:S(2)}) copy-start(f32[32,2,8,128]{3,1,2,0:T(2,128)} %copy.121) | copy-start | bytes 786436
  90.1 2.1 %collective-permute-start.2 = (f32[131072]{0:T(1024)S(1)}, f32[131072]{0:T(1024)}, u32[]{:S(2)}, u32[]{:S(2)}) collective-permute-start(f32[131072]{0:T(1024)S(1)} %broadcast_select_fusion), channel_id=1, source_target_pairs={{0,1},{1,0},{2,3},{3,2},{4,5},{5,4},{6,7},{7,6},{8,9},{9,8},{10,11... | collective-permute-start | bytes 1572872 | tf_op jit(solution)/shard_map/ppermute | solution.py:34
  93.4 9.1 %collective-permute-start.3 = (f32[65536]{0:T(1024)S(1)}, f32[65536]{0:T(1024)S(1)}, u32[]{:S(2)}, u32[]{:S(2)}) collective-permute-start(f32[65536]{0:T(1024)S(1)} %slice_select_fusion), channel_id=1, source_target_pairs={{0,2},{1,3},{2,0},{3,1},{4,6},{5,7},{6,4},{7,5},{8,10},{9,11},{10,... | collective-permute-start | bytes 786440 | tf_op jit(solution)/shard_map/ppermute | solution.py:34
  102.5 5.1 %collective-permute-start.4 = (f32[32768]{0:T(1024)S(1)}, f32[32768]{0:T(1024)S(1)}, u32[]{:S(2)}, u32[]{:S(2)}) collective-permute-start(f32[32768]{0:T(1024)S(1)} %slice_select_fusion.1), channel_id=1, source_target_pairs={{0,4},{1,5},{2,6},{3,7},{4,0},{5,1},{6,2},{7,3},{8,12},{9,13},{10,... | collective-permute-start | bytes 393224 | tf_op jit(solution)/shard_map/ppermute | solution.py:34
  107.7 4.3 %collective-permute-start.5 = (f32[16384]{0:T(1024)S(1)}, f32[16384]{0:T(1024)S(1)}, u32[]{:S(2)}, u32[]{:S(2)}) collective-permute-start(f32[16384]{0:T(1024)S(1)} %slice_select_fusion.2), channel_id=1, source_target_pairs={{0,8},{8,0},{16,24},{24,16},{1,9},{9,1},{17,25},{25,17},{2,10},{10... | collective-permute-start | bytes 196616 | tf_op jit(solution)/shard_map/ppermute | solution.py:34
  112.0 5.5 %collective-permute-start.6 = (f32[8192]{0:T(1024)S(1)}, f32[8192]{0:T(1024)S(1)}, u32[]{:S(2)}, u32[]{:S(2)}) collective-permute-start(f32[8192]{0:T(1024)S(1)} %slice_select_fusion.3), channel_id=1, source_target_pairs={{0,16},{8,24},{16,0},{24,8},{1,17},{9,25},{17,1},{25,9},{2,18},{10... | collective-permute-start | bytes 98312 | tf_op jit(solution)/shard_map/ppermute | solution.py:34
  117.5 4.8 %collective-permute-start.7 = (f32[8192]{0:T(1024)S(1)}, f32[8192]{0:T(1024)S(1)}, u32[]{:S(2)}, u32[]{:S(2)}) collective-permute-start(f32[8192]{0:T(1024)S(1)} %select_add_fusion.4), channel_id=1, source_target_pairs={{0,16},{8,24},{16,0},{24,8},{1,17},{9,25},{17,1},{25,9},{2,18},{10... | collective-permute-start | bytes 98312 | tf_op jit(solution)/shard_map/ppermute | solution.py:38
  122.3 4.3 %collective-permute-start.8 = (f32[16384]{0:T(1024)S(1)}, f32[16384]{0:T(1024)S(1)}, u32[]{:S(2)}, u32[]{:S(2)}) collective-permute-start(f32[16384]{0:T(1024)S(1)} %maximum_select_fusion.7), channel_id=1, source_target_pairs={{0,8},{8,0},{16,24},{24,16},{1,9},{9,1},{17,25},{25,17},{2,10},{10... | collective-permute-start | bytes 196616 | tf_op jit(solution)/shard_map/ppermute | solution.py:38
  122.8 12.7 %copy-start.6 = (bf16[4,256,256]{2,1,0:T(8,128)(2,1)S(1)}, bf16[4,256,256]{2,1,0:T(8,128)(2,1)}, u32[]{:S(2)}) copy-start(bf16[4,256,256]{2,1,0:T(8,128)(2,1)} %copy-done.5) | copy-start | bytes 1572868
  126.7 5.0 %collective-permute-start.9 = (f32[32768]{0:T(1024)S(1)}, f32[32768]{0:T(1024)S(1)}, u32[]{:S(2)}, u32[]{:S(2)}) collective-permute-start(f32[32768]{0:T(1024)S(1)} %maximum_select_fusion.6), channel_id=1, source_target_pairs={{0,4},{1,5},{2,6},{3,7},{4,0},{5,1},{6,2},{7,3},{8,12},{9,13},{10,... | collective-permute-start | bytes 393224 | tf_op jit(solution)/shard_map/ppermute | solution.py:38
  128.1 11.8 %collective-permute-start.1 = (bf16[4,128,256]{2,1,0:T(8,128)(2,1)S(1)}, bf16[4,128,256]{2,1,0:T(8,128)(2,1)S(1)}, u32[]{:S(2)}, u32[]{:S(2)}) collective-permute-start(bf16[4,128,256]{2,1,0:T(8,128)(2,1)S(1)} %convolution_convert_fusion.6), channel_id=1, source_target_pairs={{0,7},{1,0},{2,1},{3,2},{4,3},{5,4},{6,5},{7,6},{8,15},{9,8},{10,9... | collective-permute-start | bytes 786440 | tf_op jit(solution)/shard_map/ppermute | solution.py:12
  131.7 8.0 %collective-permute-start.10 = (f32[65536]{0:T(1024)S(1)}, f32[65536]{0:T(1024)S(1)}, u32[]{:S(2)}, u32[]{:S(2)}) collective-permute-start(f32[65536]{0:T(1024)S(1)} %maximum_select_fusion.4), channel_id=1, source_target_pairs={{0,2},{1,3},{2,0},{3,1},{4,6},{5,7},{6,4},{7,5},{8,10},{9,11},{10,... | collective-permute-start | bytes 786440 | tf_op jit(solution)/shard_map/ppermute | solution.py:38
  135.4 4.5 %copy-start.18 = (s32[4,128]{1,0:T(4,128)S(1)}, s32[4,128]{1,0:T(4,128)}, u32[]{:S(2)}) copy-start(s32[4,128]{1,0:T(4,128)} %param.13) | copy-start | bytes 6148
  139.8 2.0 %collective-permute-start.11 = (f32[131072]{0:T(1024)S(1)}, f32[131072]{0:T(1024)S(1)}, u32[]{:S(2)}, u32[]{:S(2)}) collective-permute-start(f32[131072]{0:T(1024)S(1)} %maximum_select_fusion.2), channel_id=1, source_target_pairs={{0,1},{1,0},{2,3},{3,2},{4,5},{5,4},{6,7},{7,6},{8,9},{9,8},{10,11... | collective-permute-start | bytes 1572872 | tf_op jit(solution)/shard_map/ppermute | solution.py:38

commit v4 on v3

--- a/solution.py
+++ b/solution.py
@@ -14,6 +14,40 @@
 
 def _power_of_two(count):
     return count > 0 and count & (count - 1) == 0
+
+
+def _group_pairs(axis, stride, group, shift):
+    pairs = []
+    for source in range(lax.axis_size(axis)):
+        digit = (source // stride) % group
+        pairs.append((source, source + ((digit + shift) % group - digit) * stride))
+    return pairs
+
+
+def _scatter_step(flat, axis, stride, group):
+    digit = (lax.axis_index(axis) // stride) % group
+    chunks = flat.reshape(group, -1)
+    total = lax.dynamic_index_in_dim(chunks, digit, 0, keepdims=False)
+    for shift in range(1, group):
+        send = lax.dynamic_index_in_dim(chunks, (digit + shift) % group, 0, keepdims=False)
+        total = total + lax.ppermute(send, axis, _group_pairs(axis, stride, group, shift))
+    return total
+
+
+def _gather_step(flat, axis, stride, group):
+    digit = (lax.axis_index(axis) // stride) % group
+    got = [flat] + [
+        lax.ppermute(flat, axis, _group_pairs(axis, stride, group, shift)) for shift in range(1, group)
+    ]
+    stacked = jnp.stack(got)
+    order = (digit - jnp.arange(group)) % group
+    return jnp.take(stacked, order, axis=0).reshape(-1)
+
+
+def _factors(size):
+    if size <= 4:
+        return [size]
+    return [2] + _factors(size // 2)
 
 
 def tree_sum(values, axes):
@@ -24,24 +58,36 @@
         total *= size
     if not all(_power_of_two(size) for size in sizes) or flat.shape[0] % total:
         return lax.psum(tuple(values), axes)
-    steps = [(axis, bit) for axis, size in zip(axes, sizes) for bit in [1 << k for k in range(size.bit_length() - 1)]]
-    for axis, bit in steps:
-        side = (lax.axis_index(axis) // bit) % 2
-        halves = flat.reshape(2, -1)
-        keep = jnp.where(side == 0, halves[0], halves[1])
-        send = jnp.where(side == 0, halves[1], halves[0])
-        pairs = [(source, source ^ bit) for source in range(lax.axis_size(axis))]
-        flat = keep + lax.ppermute(send, axis, pairs)
-    for axis, bit in reversed(steps):
-        side = (lax.axis_index(axis) // bit) % 2
-        pairs = [(source, source ^ bit) for source in range(lax.axis_size(axis))]
-        other = lax.ppermute(flat, axis, pairs)
-        flat = jnp.where(side == 0, jnp.concatenate([flat, other]), jnp.concatenate([other, flat]))
+    steps = []
+    for axis, size in zip(axes, sizes):
+        stride = 1
+        for group in _factors(size):
+            if group > 1:
+                steps.append((axis, stride, group))
+            stride *= group
+    for axis, stride, group in steps:
+        flat = _scatter_step(flat, axis, stride, group)
+    for axis, stride, group in reversed(steps):
+        flat = _gather_step(flat, axis, stride, group)
     results, start = [], 0
     for value in values:
         results.append(flat[start : start + value.size].reshape(value.shape))
         start += value.size
     return tuple(results)
+
+
+def exchange(value, axis, split_axis, concat_axis):
+    count = lax.axis_size(axis)
+    mine = lax.axis_index(axis)
+    pieces = jnp.stack(jnp.split(value, count, axis=split_axis))
+    got = []
+    for shift in range(count):
+        send = lax.dynamic_index_in_dim(pieces, (mine + shift) % count, 0, keepdims=False)
+        if shift:
+            send = lax.ppermute(send, axis, [(i, (i + shift) % count) for i in range(count)])
+        got.append(send)
+    stacked = jnp.take(jnp.stack(got), (mine - jnp.arange(count)) % count, axis=0)
+    return jnp.concatenate([stacked[k] for k in range(count)], axis=concat_axis)
 
 
 def adjacency(sources, targets, count_rows, total_rows):
@@ -262,10 +308,10 @@
     preact = jnp.einsum("drh,hk->drk", aggregate, w_message, preferred_element_type=jnp.float32)
     hidden = (states_f + jax.nn.silu(preact)).astype(jnp.bfloat16)
 
-    node_major = lax.all_to_all(hidden, "day", split_axis=1, concat_axis=0, tiled=True)
+    node_major = exchange(hidden, "day", 1, 0)
     upstream = cotangent.reshape(cotangent.shape[0], -1, width)
     attn_grads, back = attend_blocked(node_major, upstream, w_query, w_key, w_value)
-    back_days = lax.all_to_all(back, "day", split_axis=0, concat_axis=1, tiled=True)
+    back_days = exchange(back, "day", 0, 1)
 
     sigmoid_val = jax.nn.sigmoid(preact)
     pre_grad = (

time: 144 us -> 126 us (0.88); the launches traced: 143 us -> 124 us
  waiting for transfers between devices: 65.2 us -> 26.9 us
  starting transfers between devices: 17.9 us -> 31.1 us
  local copies, waits for them, and re-layouts: 17.7 us -> 22.5 us
  other arithmetic: 4.81 us -> 8.24 us
  matrix products: 36 us -> 33.1 us
    all_to_all x2 -> x0, waiting for transfers between devices: 25.1 us -> none  [the longest x1 12.9 us: local(): lax.all_to_all(back, 'day', split_axis=0, concat_axis=1, tiled=True)]
    ppermute x10 -> x20, starting transfers between devices: 8.26 us -> 30.7 us  [the longest x6 12.1 us: exchange(): lax.ppermute(send, axis, [(i, (i + shift) % count) for i in range(count)])]
    ppermute x10 -> x20, waiting for transfers between devices: 38.6 us -> 26.4 us  [the longest x6 11.8 us: exchange(): lax.ppermute(send, axis, [(i, (i + shift) % count) for i in range(count)])]
    all_to_all x2 -> x0, starting transfers between devices: 9.09 us -> none  [the longest x1 5.62 us: local(): lax.all_to_all(hidden, 'day', split_axis=1, concat_axis=0, tiled=True)]
    reshape x5, local copies, waits for them, and re-layouts: 8.68 us -> 2.99 us  [blocks(): return matrix.reshape(groups, block, HEADS, head_dim)]
    gather x0 -> x7, local copies, waits for them, and re-layouts: none -> 5.3 us  [the longest x5 4.14 us: _gather_step(): return jnp.take(stacked, order, axis=0).reshape(-1)]
    unnamed x48 -> x54, local copies, waits for them, and re-layouts: 2.11 us -> 5.39 us
    another operation x0 -> x7, other arithmetic: none -> 2.88 us  [the longest x3 1.57 us: _gather_step(): stacked = jnp.stack(got)]
  transfers between devices with their start and end apart: 14 -> 22, of which waited for: 13 -> 16; matrix products, arithmetic and copies ran while one was open for 9% -> 14% of each run, Pallas kernels for 0% -> 0%
where the time goes in v4:
time: 126 us; the launch traced here: 124 us
  matrix products  33.1 us (26%)
  starting transfers between devices  31.1 us (25%)
  waiting for transfers between devices  26.9 us (21%)
  local copies, waits for them, and re-layouts  22.5 us (18%)
  other arithmetic  8.24 us (7%)
  between operations  1.56 us (1%)
    dot_general x4, matrix products, contract(): return jnp.einsum(spec, left, right, preferred_element_type=jnp.float32)  12.7 us
    ppermute x6, starting transfers between devices, exchange(): lax.ppermute(send, axis, [(i, (i + shift) % count) for i in range(count)])  12.1 us
    ppermute x6, waiting for transfers between devices, exchange(): lax.ppermute(send, axis, [(i, (i + shift) % count) for i in range(count)])  11.8 us
    ppermute x7, waiting for transfers between devices, _scatter_step(): lax.ppermute(send, axis, _group_pairs(axis, stride, group, shift))  10.5 us
    ppermute x7, starting transfers between devices, _scatter_step(): lax.ppermute(send, axis, _group_pairs(axis, stride, group, shift))  9.45 us
    ppermute x7, starting transfers between devices, _gather_step(): lax.ppermute(flat, axis, _group_pairs(axis, stride, group, shift))  9.1 us
    unnamed x54, local copies, waits for them, and re-layouts  5.39 us
    ppermute x7, waiting for transfers between devices, _gather_step(): lax.ppermute(flat, axis, _group_pairs(axis, stride, group, shift))  4.15 us
  transfers between devices with their start and end apart: 22, of which 16 were waited for; matrix products, arithmetic and copies ran while one was open for 14% of the time, Pallas kernels for 0%

profile of v4, /device:TPU:0, one launch (start us, length us, event | category | flops | bytes accessed | tf_op | source)
XLA Modules:
  0.0 123.5 jit_solution(16312335596590983377)
XLA Ops:
  2.0 2.1 %convolution_convert_fusion.7 = bf16[4,128,256]{2,1,0:T(8,128)(2,1)} fusion(bf16[4,256,256]{2,1,0:T(8,128)(2,1)} %param.12, s32[4,128]{1,0:T(4,128)} %param.15, pred[4,128]{1,0:T(4,128)(4,1)S(1)} %iota_compare_fusion.12), kind=kOutput, calls=%fused_computation.52 | convolution fusion | flops 67502080 | bytes 788992 | tf_op jit(solution)/shard_map/dsn,dnh->dsh/dot_general | solution.py:285
  4.5 1.2 convert_reduce_fusion
  5.8 2.4 %fusion.17 = bf16[4,256,256]{2,1,0:T(8,128)(2,1)S(1)} fusion(s32[4,1024]{1,0:T(4,128)} %param.13, s32[4,1024]{1,0:T(4,128)} %param.14), kind=kOutput, calls=%fused_computation.46 | convolution fusion | flops 539230208 | bytes 557056 | tf_op jit(solution)/shard_map/der,des->drs/dot_general | solution.py:294
  9.0 1.3 %fusion.21 = bf16[4,256,128]{2,1,0:T(8,128)(2,1)S(1)} fusion(s32[4,1024]{1,0:T(4,128)S(1)} %copy-done.16, s32[128]{0:T(128)S(1)} %iota_add_fusion, s32[4,1024]{1,0:T(4,128)S(1)} %copy-done.21), kind=kOutput, calls=%fused_computation.50 | convolution fusion | flops 270139392 | bytes 295424 | tf_op jit(solution)/shard_map/der,des->drs/dot_general | solution.py:297
  11.8 1.3 %fusion.15 = bf16[4,256,256]{2,1,0:T(8,128)(2,1)S(1)} fusion(f32[4,256,256]{2,1,0:T(8,128)S(1)} %fusion.79, bf16[4,256,128]{2,1,0:T(8,128)(2,1)S(1)} %fusion.21, bf16[4,128,256]{2,1,0:T(8,128)(2,1)} %collective-permute-done, bf16[4,256,256]{2,1,0:T(8,128)(2,1)S(1)} %copy-done.1, f32[4,256]{1,0:T(4,128)S(1)} %add_divide_fusion.1), kind=kOutput, calls=%fused_computation.38 | convolution fusion | flops 68419584 | bytes 2625536 | tf_op jit(solution)/shard_map/drs,dsh->drh/dot_general | solution.py:306
  13.1 1.3 %fusion.24 = (bf16[4,256,256]{2,1,0:T(8,128)(2,1)S(1)}, f32[4,256,256]{2,1,0:T(8,128)}) fusion(bf16[4,256,256]{2,1,0:T(8,128)(2,1)S(1)} %copy-done.1, bf16[4,256,256]{2,1,0:T(8,128)(2,1)S(1)} %fusion.15, bf16[256,256]{1,0:T(8,128)(2,1)S(1)} %copy-done), kind=kOutput, calls=%fused_computation.57 | convolution fusion | flops 136052736 | bytes 2752512 | tf_op jit(solution)/shard_map/drh,hk->drk/dot_general | solution.py:308
  15.3 2.3 %collective-permute-start.1 = (bf16[4,64,256]{2,1,0:T(8,128)(2,1)}, bf16[4,64,256]{2,1,0:T(8,128)(2,1)}, u32[]{:S(2)}, u32[]{:S(2)}) collective-permute-start(bf16[4,64,256]{2,1,0:T(8,128)(2,1)} %get-tuple-element.39), channel_id=1, source_target_pairs={{0,8},{8,16},{16,24},{24,0},{1,9},{9,17},{17,25},{25,1},{2,10},{10... | collective-permute-start | bytes 393224 | tf_op jit(solution)/shard_map/ppermute | solution.py:87
  17.7 2.6 %collective-permute-start.2 = (bf16[4,64,256]{2,1,0:T(8,128)(2,1)}, bf16[4,64,256]{2,1,0:T(8,128)(2,1)}, u32[]{:S(2)}, u32[]{:S(2)}) collective-permute-start(bf16[4,64,256]{2,1,0:T(8,128)(2,1)} %get-tuple-element.38), channel_id=1, source_target_pairs={{0,16},{8,24},{16,0},{24,8},{1,17},{9,25},{17,1},{25,9},{2,18},{10... | collective-permute-start | bytes 393224 | tf_op jit(solution)/shard_map/ppermute | solution.py:87
  20.3 1.3 %collective-permute-start.3 = (bf16[4,64,256]{2,1,0:T(8,128)(2,1)}, bf16[4,64,256]{2,1,0:T(8,128)(2,1)}, u32[]{:S(2)}, u32[]{:S(2)}) collective-permute-start(bf16[4,64,256]{2,1,0:T(8,128)(2,1)} %get-tuple-element.37), channel_id=1, source_target_pairs={{0,24},{8,0},{16,8},{24,16},{1,25},{9,1},{17,9},{25,17},{2,26},{10... | collective-permute-start | bytes 393224 | tf_op jit(solution)/shard_map/ppermute | solution.py:87
  23.5 1.6 %copy.26 = f32[64,16,256]{2,1,0:T(8,128)} copy(f32[64,16,256]{2,0,1:T(8,128)S(1)} %bitcast_convert_fusion) | data formatting | bytes 2097152 | tf_op jit(solution)/shard_map/convert_element_type | solution.py:257
  25.1 4.9 %collective-permute-done.2 = bf16[4,64,256]{2,1,0:T(8,128)(2,1)} collective-permute-done((bf16[4,64,256]{2,1,0:T(8,128)(2,1)}, bf16[4,64,256]{2,1,0:T(8,128)(2,1)}, u32[]{:S(2)}, u32[]{:S(2)}) %collective-permute-start.2) | collective-permute-done | bytes 131104 | tf_op jit(solution)/shard_map/ppermute | solution.py:87
  30.0 1.1 pad_maximum_fusion.4
  33.9 1.2 convolution_convert_fusion.2
  35.5 1.2 copy.36
  36.7 1.2 convolution_convert_fusion
  38.3 1.8 %fusion.27 = f32[8,4,128,128]{3,2,1,0:T(8,128)} fusion(bf16[8,128,4,64]{1,3,2,0:T(8,128)(2,1)S(1)} %copy.35, bf16[8,128,4,64]{3,2,1,0:T(4,128)(2,1)S(1)} %reshape.518), kind=kOutput, calls=%fused_computation.64 | convolution fusion | flops 67108864 | bytes 3145728 | tf_op jit(solution)/shard_map/gihd,gjhd->ghij/dot_general | solution.py:227
  40.1 2.9 %fusion.78 = (f32[8,4,128]{2,1,0:T(4,128)S(1)}, f32[8,4,128,128]{2,3,1,0:T(8,128)}) fusion(pred[128,128]{0,1:T(8,128)(4,1)} %compare_and_fusion, bf16[8,128,4,64]{1,3,2,0:T(8,128)(2,1)S(1)} %copy.30, bf16[8,128,4,64]{1,3,2,0:T(8,128)(2,1)S(1)} %copy-done.10), kind=kOutput, calls=%fused_computation.214 | convolution fusion | flops 69206144 | bytes 3178496 | tf_op jit(solution)/shard_map/sub | solution.py:232
  43.6 2.4 %fusion.20 = bf16[8,128,4,64]{1,3,2,0:T(8,128)(2,1)S(1)} fusion(bf16[8,128,4,64]{1,3,2,0:T(8,128)(2,1)S(1)} %copy.35, f32[8,4,128,128]{2,3,1,0:T(8,128)} %get-tuple-element.53, f32[8,4,128]{2,1,0:T(4,128)S(1)} %get-tuple-element.52), kind=kOutput, calls=%fused_computation.49 | convolution fusion | flops 68419584 | bytes 3162112 | tf_op jit(solution)/shard_map/ghij,gihd->gjhd/dot_general | solution.py:227
  46.0 4.3 %fusion.19 = bf16[8,128,4,64]{1,3,2,0:T(8,128)(2,1)S(1)} fusion(bf16[8,128,4,64]{1,3,2,0:T(8,128)(2,1)S(1)} %copy.30, f32[8,4,128,128]{3,2,1,0:T(8,128)} %fusion.27, f32[8,4,128,128]{2,3,1,0:T(8,128)} %get-tuple-element.53, f32[8,4,128]{2,1,0:T(4,128)} %copy-done.22), kind=kOutput, calls=%fused_computation.48 | convolution fusion | flops 71045248 | bytes 5259264 | tf_op jit(solution)/shard_map/ghij,gihd->gjhd/dot_general | solution.py:227
  50.3 4.2 %fusion.18 = bf16[8,128,4,64]{1,3,2,0:T(8,128)(2,1)S(1)} fusion(bf16[8,128,4,64]{1,3,2,0:T(8,128)(2,1)S(1)} %copy-done.10, f32[8,4,128,128]{3,2,1,0:T(8,128)} %fusion.27, f32[8,4,128,128]{2,3,1,0:T(8,128)} %get-tuple-element.53, f32[8,4,128]{2,1,0:T(4,128)} %copy-done.22), kind=kOutput, calls=%fused_computation.47 | convolution fusion | flops 71045248 | bytes 5259264 | tf_op jit(solution)/shard_map/ghij,gjhd->gihd/dot_general | solution.py:227
  58.2 3.4 %collective-permute-start.4 = (bf16[4,64,256]{2,1,0:T(8,128)(2,1)S(1)}, bf16[4,64,256]{2,1,0:T(8,128)(2,1)S(1)}, u32[]{:S(2)}, u32[]{:S(2)}) collective-permute-start(bf16[4,64,256]{2,1,0:T(8,128)(2,1)S(1)} %get-tuple-element.27), channel_id=1, source_target_pairs={{0,8},{8,16},{16,24},{24,0},{1,9},{9,17},{17,25},{25,1},{2,10},{10... | collective-permute-start | bytes 393224 | tf_op jit(solution)/shard_map/ppermute | solution.py:87
  61.6 1.6 %collective-permute-start.5 = (bf16[4,64,256]{2,1,0:T(8,128)(2,1)S(1)}, bf16[4,64,256]{2,1,0:T(8,128)(2,1)S(1)}, u32[]{:S(2)}, u32[]{:S(2)}) collective-permute-start(bf16[4,64,256]{2,1,0:T(8,128)(2,1)S(1)} %get-tuple-element.26), channel_id=1, source_target_pairs={{0,16},{8,24},{16,0},{24,8},{1,17},{9,25},{17,1},{25,9},{2,18},{10... | collective-permute-start | bytes 393224 | tf_op jit(solution)/shard_map/ppermute | solution.py:87
  65.3 1.8 %collective-permute-done.4 = bf16[4,64,256]{2,1,0:T(8,128)(2,1)S(1)} collective-permute-done((bf16[4,64,256]{2,1,0:T(8,128)(2,1)S(1)}, bf16[4,64,256]{2,1,0:T(8,128)(2,1)S(1)}, u32[]{:S(2)}, u32[]{:S(2)}) %collective-permute-start.4) | collective-permute-done | bytes 131104 | tf_op jit(solution)/shard_map/ppermute | solution.py:87
  67.0 5.1 %collective-permute-done.5 = bf16[4,64,256]{2,1,0:T(8,128)(2,1)S(1)} collective-permute-done((bf16[4,64,256]{2,1,0:T(8,128)(2,1)S(1)}, bf16[4,64,256]{2,1,0:T(8,128)(2,1)S(1)}, u32[]{:S(2)}, u32[]{:S(2)}) %collective-permute-start.5) | collective-permute-done | bytes 131104 | tf_op jit(solution)/shard_map/ppermute | solution.py:87
  76.3 1.8 %collective-permute-done.8 = f32[131072]{0:T(1024)S(1)} collective-permute-done((f32[131072]{0:T(1024)S(1)}, f32[131072]{0:T(1024)S(1)}, u32[]{:S(2)}, u32[]{:S(2)}) %collective-permute-start.8) | collective-permute-done | bytes 524320 | tf_op jit(solution)/shard_map/ppermute | solution.py:33
  78.8 1.6 %collective-permute-start.10 = (f32[32768]{0:T(1024)S(1)}, f32[32768]{0:T(1024)S(1)}, u32[]{:S(2)}, u32[]{:S(2)}) collective-permute-start(f32[32768]{0:T(1024)S(1)} %bitcast.239), channel_id=1, source_target_pairs={{0,4},{1,5},{2,6},{3,7},{4,0},{5,1},{6,2},{7,3},{8,12},{9,13},{10,... | collective-permute-start | bytes 393224 | tf_op jit(solution)/shard_map/ppermute | solution.py:33
  80.4 1.1 collective-permute-start.11
  82.5 1.9 %collective-permute-done.10 = f32[32768]{0:T(1024)S(1)} collective-permute-done((f32[32768]{0:T(1024)S(1)}, f32[32768]{0:T(1024)S(1)}, u32[]{:S(2)}, u32[]{:S(2)}) %collective-permute-start.10) | collective-permute-done | bytes 131104 | tf_op jit(solution)/shard_map/ppermute | solution.py:33
  84.4 2.4 %collective-permute-done.11 = f32[32768]{0:T(1024)S(1)} collective-permute-done((f32[32768]{0:T(1024)S(1)}, f32[32768]{0:T(1024)S(1)}, u32[]{:S(2)}, u32[]{:S(2)}) %collective-permute-start.11) | collective-permute-done | bytes 131104 | tf_op jit(solution)/shard_map/ppermute | solution.py:33
  86.8 1.6 %collective-permute-done.9 = f32[32768]{0:T(1024)S(1)} collective-permute-done((f32[32768]{0:T(1024)S(1)}, f32[32768]{0:T(1024)S(1)}, u32[]{:S(2)}, u32[]{:S(2)}) %collective-permute-start.9) | collective-permute-done | bytes 131104 | tf_op jit(solution)/shard_map/ppermute | solution.py:33
  88.7 3.3 %collective-permute-start.12 = (f32[8192]{0:T(1024)S(1)}, f32[8192]{0:T(1024)S(1)}, u32[]{:S(2)}, u32[]{:S(2)}) collective-permute-start(f32[8192]{0:T(1024)S(1)} %bitcast.248), channel_id=1, source_target_pairs={{0,8},{8,16},{16,24},{24,0},{1,9},{9,17},{17,25},{25,1},{2,10},{10... | collective-permute-start | bytes 98312 | tf_op jit(solution)/shard_map/ppermute | solution.py:33
  92.0 1.4 %collective-permute-start.13 = (f32[8192]{0:T(1024)S(1)}, f32[8192]{0:T(1024)S(1)}, u32[]{:S(2)}, u32[]{:S(2)}) collective-permute-start(f32[8192]{0:T(1024)S(1)} %bitcast.247), channel_id=1, source_target_pairs={{0,16},{8,24},{16,0},{24,8},{1,17},{9,25},{17,1},{25,9},{2,18},{10... | collective-permute-start | bytes 98312 | tf_op jit(solution)/shard_map/ppermute | solution.py:33
  93.4 1.1 collective-permute-start.14
  94.8 2.0 %collective-permute-done.13 = f32[8192]{0:T(1024)S(1)} collective-permute-done((f32[8192]{0:T(1024)S(1)}, f32[8192]{0:T(1024)S(1)}, u32[]{:S(2)}, u32[]{:S(2)}) %collective-permute-start.13) | collective-permute-done | bytes 32800 | tf_op jit(solution)/shard_map/ppermute | solution.py:33
  97.8 3.1 %collective-permute-start.16 = (f32[8192]{0:T(1024)S(1)}, f32[8192]{0:T(1024)S(1)}, u32[]{:S(2)}, u32[]{:S(2)}) collective-permute-start(f32[8192]{0:T(1024)S(1)} %add_add_fusion.1), channel_id=1, source_target_pairs={{0,16},{8,24},{16,0},{24,8},{1,17},{9,25},{17,1},{25,9},{2,18},{10... | collective-permute-start | bytes 98312 | tf_op jit(solution)/shard_map/ppermute | solution.py:40
  100.9 0.9 collective-permute-start.17
  102.2 1.0 collective-permute-done.15
  103.1 1.7 %collective-permute-done.17 = f32[8192]{0:T(1024)S(1)} collective-permute-done((f32[8192]{0:T(1024)S(1)}, f32[8192]{0:T(1024)S(1)}, u32[]{:S(2)}, u32[]{:S(2)}) %collective-permute-start.17) | collective-permute-done | bytes 32800 | tf_op jit(solution)/shard_map/ppermute | solution.py:40
  105.7 1.3 %collective-permute-start.18 = (f32[32768]{0:T(1024)S(1)}, f32[32768]{0:T(1024)S(1)}, u32[]{:S(2)}, u32[]{:S(2)}) collective-permute-start(f32[32768]{0:T(1024)S(1)} %bitcast.232), channel_id=1, source_target_pairs={{0,2},{1,3},{2,4},{3,5},{4,6},{5,7},{6,0},{7,1},{8,10},{9,11},{10,... | collective-permute-start | bytes 393224 | tf_op jit(solution)/shard_map/ppermute | solution.py:40
  106.9 1.1 collective-permute-start.19
  108.1 2.1 %collective-permute-start.20 = (f32[32768]{0:T(1024)S(1)}, f32[32768]{0:T(1024)S(1)}, u32[]{:S(2)}, u32[]{:S(2)}) collective-permute-start(f32[32768]{0:T(1024)S(1)} %bitcast.234), channel_id=1, source_target_pairs={{0,6},{1,7},{2,0},{3,1},{4,2},{5,3},{6,4},{7,5},{8,14},{9,15},{10,... | collective-permute-start | bytes 393224 | tf_op jit(solution)/shard_map/ppermute | solution.py:40
  110.2 1.3 %convolution_convert_fusion.6 = bf16[4,128,256]{2,1,0:T(8,128)(2,1)} fusion(bf16[4,256,128]{2,1,0:T(8,128)(2,1)S(1)} %fusion.21, f32[4,256,256]{2,1,0:T(8,128)S(1)} %convolution_multiply_fusion), kind=kOutput, calls=%fused_computation.51 | convolution fusion | flops 402784256 | bytes 1572864 | tf_op jit(solution)/shard_map/drs,drh->dsh/dot_general | solution.py:331
  111.7 1.3 %collective-permute-done.19 = f32[32768]{0:T(1024)S(1)} collective-permute-done((f32[32768]{0:T(1024)S(1)}, f32[32768]{0:T(1024)S(1)}, u32[]{:S(2)}, u32[]{:S(2)}) %collective-permute-start.19) | collective-permute-done | bytes 131104 | tf_op jit(solution)/shard_map/ppermute | solution.py:40
  116.4 1.3 %convolution_add_fusion.4 = f32[4,256,256]{2,1,0:T(8,128)} fusion(f32[4,256,256]{2,1,0:T(8,128)S(1)} %convolution_add_fusion, bf16[4,128,256]{2,1,0:T(8,128)(2,1)S(1)} %collective-permute-done.7, s32[4,128]{1,0:T(4,128)S(1)} %copy-done.17, pred[4,128]{1,0:T(4,128)(4,1)S(1)} %copy-done.19), kind=kOutput, calls=%fused_computation.31 | convolution fusion | flops 67633152 | bytes 2361856 | tf_op jit(solution)/shard_map/dsn,dsh->dnh/dot_general | solution.py:346
  118.2 0.9 fusion.36
  119.1 0.9 gather_fusion.2
  120.1 0.9 gather_fusion.3
  122.6 1.0 fusion.77
  (148 shorter events, 30.5 us)
Async XLA Ops:
  0.6 12.4 %copy-start = (bf16[256,256]{1,0:T(8,128)(2,1)S(1)}, bf16[256,256]{1,0:T(8,128)(2,1)}, u32[]{:S(2)}) copy-start(bf16[256,256]{1,0:T(8,128)(2,1)} %param.17) | copy-start | bytes 393220
  1.4 0.5 copy-start.18
  4.1 7.7 %collective-permute-start = (bf16[4,128,256]{2,1,0:T(8,128)(2,1)}, bf16[4,128,256]{2,1,0:T(8,128)(2,1)}, u32[]{:S(2)}, u32[]{:S(2)}) collective-permute-start(bf16[4,128,256]{2,1,0:T(8,128)(2,1)} %convolution_convert_fusion.7), channel_id=1, source_target_pairs={{0,1},{1,2},{2,3},{3,4},{4,5},{5,6},{6,7},{7,0},{8,9},{9,10},{10,1... | collective-permute-start | bytes 786440 | tf_op jit(solution)/shard_map/ppermute | solution.py:12
  5.8 2.4 %copy-start.1 = (bf16[4,256,256]{2,1,0:T(8,128)(2,1)S(1)}, bf16[4,256,256]{2,1,0:T(8,128)(2,1)}, u32[]{:S(2)}) copy-start(bf16[4,256,256]{2,1,0:T(8,128)(2,1)} %param.12) | copy-start | bytes 1572868
  8.2 2.2 %copy-start.6 = (bf16[4,256,256]{2,1,0:T(8,128)(2,1)}, bf16[4,256,256]{2,1,0:T(8,128)(2,1)S(1)}, u32[]{:S(2)}) copy-start(bf16[4,256,256]{2,1,0:T(8,128)(2,1)S(1)} %fusion.17) | copy-start | bytes 1572868
  8.2 0.7 copy-start.16
  8.2 0.8 copy-start.21
  9.0 2.1 %copy-start.3 = (bf16[16,1,1,64,256]{4,3,2,1,0:T(8,128)(2,1)S(1)}, bf16[16,1,1,64,256]{4,3,2,1,0:T(8,128)(2,1)}, u32[]{:S(2)}) copy-start(bf16[16,1,1,64,256]{4,3,2,1,0:T(8,128)(2,1)} %param.21) | copy-start | bytes 1572868
  13.1 1.4 %copy-start.4 = (bf16[4,256,256]{2,1,0:T(8,128)(2,1)}, bf16[4,256,256]{2,1,0:T(8,128)(2,1)S(1)}, u32[]{:S(2)}) copy-start(bf16[4,256,256]{2,1,0:T(8,128)(2,1)S(1)} %fusion.15) | copy-start | bytes 1572868
  15.3 9.8 %collective-permute-start.1 = (bf16[4,64,256]{2,1,0:T(8,128)(2,1)}, bf16[4,64,256]{2,1,0:T(8,128)(2,1)}, u32[]{:S(2)}, u32[]{:S(2)}) collective-permute-start(bf16[4,64,256]{2,1,0:T(8,128)(2,1)} %get-tuple-element.39), channel_id=1, source_target_pairs={{0,8},{8,16},{16,24},{24,0},{1,9},{9,17},{17,25},{25,1},{2,10},{10... | collective-permute-start | bytes 393224 | tf_op jit(solution)/shard_map/ppermute | solution.py:87
  17.7 12.3 %collective-permute-start.2 = (bf16[4,64,256]{2,1,0:T(8,128)(2,1)}, bf16[4,64,256]{2,1,0:T(8,128)(2,1)}, u32[]{:S(2)}, u32[]{:S(2)}) collective-permute-start(bf16[4,64,256]{2,1,0:T(8,128)(2,1)} %get-tuple-element.38), channel_id=1, source_target_pairs={{0,16},{8,24},{16,0},{24,8},{1,17},{9,25},{17,1},{25,9},{2,18},{10... | collective-permute-start | bytes 393224 | tf_op jit(solution)/shard_map/ppermute | solution.py:87
  20.3 9.7 %collective-permute-start.3 = (bf16[4,64,256]{2,1,0:T(8,128)(2,1)}, bf16[4,64,256]{2,1,0:T(8,128)(2,1)}, u32[]{:S(2)}, u32[]{:S(2)}) collective-permute-start(bf16[4,64,256]{2,1,0:T(8,128)(2,1)} %get-tuple-element.37), channel_id=1, source_target_pairs={{0,24},{8,0},{16,8},{24,16},{1,25},{9,1},{17,9},{25,17},{2,26},{10... | collective-permute-start | bytes 393224 | tf_op jit(solution)/shard_map/ppermute | solution.py:87
  22.9 2.2 %copy-start.20 = (s32[4]{0:T(128)S(1)}, s32[4]{0:T(128)}, u32[]{:S(2)}) copy-start(s32[4]{0:T(128)} %compare_select_fusion) | copy-start | bytes 52
  22.9 7.1 %copy-start.15 = (bf16[1,4,64,256]{3,2,1,0:T(8,128)(2,1)S(1)}, bf16[1,4,64,256]{3,2,1,0:T(8,128)(2,1)}, u32[]{:S(2)}) copy-start(bf16[1,4,64,256]{3,2,1,0:T(8,128)(2,1)} %get-tuple-element.36) | copy-start | bytes 393220
  31.7 0.9 copy-start.12
  38.3 1.8 %copy-start.10 = (bf16[8,128,4,64]{1,3,2,0:T(8,128)(2,1)S(1)}, bf16[8,128,4,64]{1,3,2,0:T(8,128)(2,1)}, u32[]{:S(2)}) copy-start(bf16[8,128,4,64]{1,3,2,0:T(8,128)(2,1)} %copy.36) | copy-start | bytes 1572868
  43.0 0.6 copy-start.22
  55.3 1.2 copy-start.2
  55.4 1.2 copy-start.13
  56.1 1.0 copy-start.14
  56.6 0.9 copy-start.11
  58.2 8.8 %collective-permute-start.4 = (bf16[4,64,256]{2,1,0:T(8,128)(2,1)S(1)}, bf16[4,64,256]{2,1,0:T(8,128)(2,1)S(1)}, u32[]{:S(2)}, u32[]{:S(2)}) collective-permute-start(bf16[4,64,256]{2,1,0:T(8,128)(2,1)S(1)} %get-tuple-element.27), channel_id=1, source_target_pairs={{0,8},{8,16},{16,24},{24,0},{1,9},{9,17},{17,25},{25,1},{2,10},{10... | collective-permute-start | bytes 393224 | tf_op jit(solution)/shard_map/ppermute | solution.py:87
  61.6 10.5 %collective-permute-start.5 = (bf16[4,64,256]{2,1,0:T(8,128)(2,1)S(1)}, bf16[4,64,256]{2,1,0:T(8,128)(2,1)S(1)}, u32[]{:S(2)}, u32[]{:S(2)}) collective-permute-start(bf16[4,64,256]{2,1,0:T(8,128)(2,1)S(1)} %get-tuple-element.26), channel_id=1, source_target_pairs={{0,16},{8,24},{16,0},{24,8},{1,17},{9,25},{17,1},{25,9},{2,18},{10... | collective-permute-start | bytes 393224 | tf_op jit(solution)/shard_map/ppermute | solution.py:87
  63.2 9.0 %collective-permute-start.6 = (bf16[4,64,256]{2,1,0:T(8,128)(2,1)S(1)}, bf16[4,64,256]{2,1,0:T(8,128)(2,1)S(1)}, u32[]{:S(2)}, u32[]{:S(2)}) collective-permute-start(bf16[4,64,256]{2,1,0:T(8,128)(2,1)S(1)} %get-tuple-element.25), channel_id=1, source_target_pairs={{0,24},{8,0},{16,8},{24,16},{1,25},{9,1},{17,9},{25,17},{2,26},{10... | collective-permute-start | bytes 393224 | tf_op jit(solution)/shard_map/ppermute | solution.py:87
  72.2 1.2 copy-start.8
  72.9 1.1 copy-start.5
  73.0 1.4 %copy-start.9 = (f32[32,2,8,128]{3,1,2,0:T(2,128)S(1)}, f32[32,2,8,128]{3,1,2,0:T(2,128)}, u32[]{:S(2)}) copy-start(f32[32,2,8,128]{3,1,2,0:T(2,128)} %copy.63) | copy-start | bytes 786436
  76.1 2.0 %collective-permute-start.8 = (f32[131072]{0:T(1024)S(1)}, f32[131072]{0:T(1024)S(1)}, u32[]{:S(2)}, u32[]{:S(2)}) collective-permute-start(f32[131072]{0:T(1024)S(1)} %bitcast.229), channel_id=1, source_target_pairs={{0,1},{1,0},{2,3},{3,2},{4,5},{5,4},{6,7},{7,6},{8,9},{9,8},{10,11... | collective-permute-start | bytes 1572872 | tf_op jit(solution)/shard_map/ppermute | solution.py:33
  78.8 5.6 %collective-permute-start.10 = (f32[32768]{0:T(1024)S(1)}, f32[32768]{0:T(1024)S(1)}, u32[]{:S(2)}, u32[]{:S(2)}) collective-permute-start(f32[32768]{0:T(1024)S(1)} %bitcast.239), channel_id=1, source_target_pairs={{0,4},{1,5},{2,6},{3,7},{4,0},{5,1},{6,2},{7,3},{8,12},{9,13},{10,... | collective-permute-start | bytes 393224 | tf_op jit(solution)/shard_map/ppermute | solution.py:33
  80.4 6.4 %collective-permute-start.11 = (f32[32768]{0:T(1024)S(1)}, f32[32768]{0:T(1024)S(1)}, u32[]{:S(2)}, u32[]{:S(2)}) collective-permute-start(f32[32768]{0:T(1024)S(1)} %bitcast.238), channel_id=1, source_target_pairs={{0,6},{1,7},{2,0},{3,1},{4,2},{5,3},{6,4},{7,5},{8,14},{9,15},{10,... | collective-permute-start | bytes 393224 | tf_op jit(solution)/shard_map/ppermute | solution.py:33
  81.5 6.9 %collective-permute-start.9 = (f32[32768]{0:T(1024)S(1)}, f32[32768]{0:T(1024)S(1)}, u32[]{:S(2)}, u32[]{:S(2)}) collective-permute-start(f32[32768]{0:T(1024)S(1)} %bitcast.237), channel_id=1, source_target_pairs={{0,2},{1,3},{2,4},{3,5},{4,6},{5,7},{6,0},{7,1},{8,10},{9,11},{10,... | collective-permute-start | bytes 393224 | tf_op jit(solution)/shard_map/ppermute | solution.py:33
  88.7 6.2 %collective-permute-start.12 = (f32[8192]{0:T(1024)S(1)}, f32[8192]{0:T(1024)S(1)}, u32[]{:S(2)}, u32[]{:S(2)}) collective-permute-start(f32[8192]{0:T(1024)S(1)} %bitcast.248), channel_id=1, source_target_pairs={{0,8},{8,16},{16,24},{24,0},{1,9},{9,17},{17,25},{25,1},{2,10},{10... | collective-permute-start | bytes 98312 | tf_op jit(solution)/shard_map/ppermute | solution.py:33
  92.0 4.8 %collective-permute-start.13 = (f32[8192]{0:T(1024)S(1)}, f32[8192]{0:T(1024)S(1)}, u32[]{:S(2)}, u32[]{:S(2)}) collective-permute-start(f32[8192]{0:T(1024)S(1)} %bitcast.247), channel_id=1, source_target_pairs={{0,16},{8,24},{16,0},{24,8},{1,17},{9,25},{17,1},{25,9},{2,18},{10... | collective-permute-start | bytes 98312 | tf_op jit(solution)/shard_map/ppermute | solution.py:33
  93.4 3.9 %collective-permute-start.14 = (f32[8192]{0:T(1024)S(1)}, f32[8192]{0:T(1024)S(1)}, u32[]{:S(2)}, u32[]{:S(2)}) collective-permute-start(f32[8192]{0:T(1024)S(1)} %bitcast.246), channel_id=1, source_target_pairs={{0,24},{8,0},{16,8},{24,16},{1,25},{9,1},{17,9},{25,17},{2,26},{10... | collective-permute-start | bytes 98312 | tf_op jit(solution)/shard_map/ppermute | solution.py:33
  97.3 5.8 %collective-permute-start.15 = (f32[8192]{0:T(1024)S(1)}, f32[8192]{0:T(1024)S(1)}, u32[]{:S(2)}, u32[]{:S(2)}) collective-permute-start(f32[8192]{0:T(1024)S(1)} %add_add_fusion.1), channel_id=1, source_target_pairs={{0,8},{8,16},{16,24},{24,0},{1,9},{9,17},{17,25},{25,1},{2,10},{10... | collective-permute-start | bytes 98312 | tf_op jit(solution)/shard_map/ppermute | solution.py:40
  97.8 5.3 %collective-permute-start.16 = (f32[8192]{0:T(1024)S(1)}, f32[8192]{0:T(1024)S(1)}, u32[]{:S(2)}, u32[]{:S(2)}) collective-permute-start(f32[8192]{0:T(1024)S(1)} %add_add_fusion.1), channel_id=1, source_target_pairs={{0,16},{8,24},{16,0},{24,8},{1,17},{9,25},{17,1},{25,9},{2,18},{10... | collective-permute-start | bytes 98312 | tf_op jit(solution)/shard_map/ppermute | solution.py:40
  100.9 3.9 %collective-permute-start.17 = (f32[8192]{0:T(1024)S(1)}, f32[8192]{0:T(1024)S(1)}, u32[]{:S(2)}, u32[]{:S(2)}) collective-permute-start(f32[8192]{0:T(1024)S(1)} %add_add_fusion.1), channel_id=1, source_target_pairs={{0,24},{8,0},{16,8},{24,16},{1,25},{9,1},{17,9},{25,17},{2,26},{10... | collective-permute-start | bytes 98312 | tf_op jit(solution)/shard_map/ppermute | solution.py:40
  105.7 6.0 %collective-permute-start.18 = (f32[32768]{0:T(1024)S(1)}, f32[32768]{0:T(1024)S(1)}, u32[]{:S(2)}, u32[]{:S(2)}) collective-permute-start(f32[32768]{0:T(1024)S(1)} %bitcast.232), channel_id=1, source_target_pairs={{0,2},{1,3},{2,4},{3,5},{4,6},{5,7},{6,0},{7,1},{8,10},{9,11},{10,... | collective-permute-start | bytes 393224 | tf_op jit(solution)/shard_map/ppermute | solution.py:40
  106.9 6.0 %collective-permute-start.19 = (f32[32768]{0:T(1024)S(1)}, f32[32768]{0:T(1024)S(1)}, u32[]{:S(2)}, u32[]{:S(2)}) collective-permute-start(f32[32768]{0:T(1024)S(1)} %bitcast.233), channel_id=1, source_target_pairs={{0,4},{1,5},{2,6},{3,7},{4,0},{5,1},{6,2},{7,3},{8,12},{9,13},{10,... | collective-permute-start | bytes 393224 | tf_op jit(solution)/shard_map/ppermute | solution.py:40
  108.1 5.0 %collective-permute-start.20 = (f32[32768]{0:T(1024)S(1)}, f32[32768]{0:T(1024)S(1)}, u32[]{:S(2)}, u32[]{:S(2)}) collective-permute-start(f32[32768]{0:T(1024)S(1)} %bitcast.234), channel_id=1, source_target_pairs={{0,6},{1,7},{2,0},{3,1},{4,2},{5,3},{6,4},{7,5},{8,14},{9,15},{10,... | collective-permute-start | bytes 393224 | tf_op jit(solution)/shard_map/ppermute | solution.py:40
  111.4 4.9 %collective-permute-start.7 = (bf16[4,128,256]{2,1,0:T(8,128)(2,1)}, bf16[4,128,256]{2,1,0:T(8,128)(2,1)S(1)}, u32[]{:S(2)}, u32[]{:S(2)}) collective-permute-start(bf16[4,128,256]{2,1,0:T(8,128)(2,1)} %convolution_convert_fusion.6), channel_id=1, source_target_pairs={{0,7},{1,0},{2,1},{3,2},{4,3},{5,4},{6,5},{7,6},{8,15},{9,8},{10,9... | collective-permute-start | bytes 786440 | tf_op jit(solution)/shard_map/ppermute | solution.py:12
  114.4 1.0 copy-start.7
  114.6 1.7 %copy-start.17 = (s32[4,128]{1,0:T(4,128)S(1)}, s32[4,128]{1,0:T(4,128)}, u32[]{:S(2)}) copy-start(s32[4,128]{1,0:T(4,128)} %param.15) | copy-start | bytes 6148
  114.7 1.7 %copy-start.19 = (pred[4,128]{1,0:T(4,128)(4,1)S(1)}, pred[4,128]{1,0:T(4,128)(4,1)}, u32[]{:S(2)}) copy-start(pred[4,128]{1,0:T(4,128)(4,1)} %copy-done.18) | copy-start | bytes 1540
  114.7 3.5 %collective-permute-start.21 = (f32[131072]{0:T(1024)S(1)}, f32[131072]{0:T(1024)S(1)}, u32[]{:S(2)}, u32[]{:S(2)}) collective-permute-start(f32[131072]{0:T(1024)S(1)} %bitcast.227), channel_id=1, source_target_pairs={{0,1},{1,0},{2,3},{3,2},{4,5},{5,4},{6,7},{7,6},{8,9},{9,8},{10,11... | collective-permute-start | bytes 1572872 | tf_op jit(solution)/shard_map/ppermute | solution.py:40

commit v5 on v4

--- a/solution.py
+++ b/solution.py
@@ -311,6 +311,7 @@
     node_major = exchange(hidden, "day", 1, 0)
     upstream = cotangent.reshape(cotangent.shape[0], -1, width)
     attn_grads, back = attend_blocked(node_major, upstream, w_query, w_key, w_value)
+    grad_query, grad_key, grad_value = tree_sum(attn_grads, ("dom", "day"))
     back_days = exchange(back, "day", 0, 1)
 
     sigmoid_val = jax.nn.sigmoid(preact)
@@ -323,9 +324,7 @@
         (((0,), (0,)), ((), ())),
         preferred_element_type=jnp.float32,
     )
-    grad_message, grad_query, grad_key, grad_value = tree_sum(
-        (grad_message, attn_grads[0], attn_grads[1], attn_grads[2]), ("dom", "day")
-    )
+    (grad_message,) = tree_sum((grad_message,), ("dom", "day"))
     agg_grad = jnp.einsum("drk,hk->drh", pre_grad, w_message, preferred_element_type=jnp.float32)
     term_grad = agg_grad * inverse[:, :, None]
     halo_grad = jnp.einsum(

time: 126 us -> 152 us (1.21); the launches traced: 124 us -> 151 us
  waiting for transfers between devices: 26.9 us -> 35.8 us
  starting transfers between devices: 31.1 us -> 39.6 us
  other arithmetic: 8.24 us -> 12.6 us
  local copies, waits for them, and re-layouts: 22.5 us -> 26.7 us
  matrix products: 33.1 us -> 35 us
    ppermute x7 -> x14, waiting for transfers between devices: 4.15 us -> 11.4 us  [_gather_step(): lax.ppermute(flat, axis, _group_pairs(axis, stride, group, shift))]
    ppermute x7 -> x14, starting transfers between devices: 9.1 us -> 14.9 us  [_gather_step(): lax.ppermute(flat, axis, _group_pairs(axis, stride, group, shift))]
    ppermute x6, waiting for transfers between devices: 11.8 us -> 17.2 us  [exchange(): lax.ppermute(send, axis, [(i, (i + shift) % count) for i in range(count)])]
    ppermute x7 -> x14, starting transfers between devices: 9.45 us -> 14.1 us  [_scatter_step(): lax.ppermute(send, axis, _group_pairs(axis, stride, group, shift))]
    reshape x5, local copies, waits for them, and re-layouts: 2.99 us -> 6.87 us  [blocks(): return matrix.reshape(groups, block, HEADS, head_dim)]
    ppermute x7 -> x14, waiting for transfers between devices: 10.5 us -> 7.2 us  [_scatter_step(): lax.ppermute(send, axis, _group_pairs(axis, stride, group, shift))]
    unnamed x54 -> x71, local copies, waits for them, and re-layouts: 5.39 us -> 2.38 us
    ppermute x6, starting transfers between devices: 12.1 us -> 10.1 us  [exchange(): lax.ppermute(send, axis, [(i, (i + shift) % count) for i in range(count)])]
  transfers between devices with their start and end apart: 22 -> 36, of which waited for: 16 -> 17; matrix products, arithmetic and copies ran while one was open for 14% -> 19% of each run, Pallas kernels for 0% -> 0%
where the time goes in v5:
time: 152 us; the launch traced here: 151 us
  starting transfers between devices  39.6 us (26%)
  waiting for transfers between devices  35.8 us (24%)
  matrix products  35 us (23%)
  local copies, waits for them, and re-layouts  26.7 us (18%)
  other arithmetic  12.6 us (8%)
  between operations  1.72 us (1%)
    ppermute x6, waiting for transfers between devices, exchange(): lax.ppermute(send, axis, [(i, (i + shift) % count) for i in range(count)])  17.2 us
    ppermute x14, starting transfers between devices, _gather_step(): lax.ppermute(flat, axis, _group_pairs(axis, stride, group, shift))  14.9 us
    ppermute x14, starting transfers between devices, _scatter_step(): lax.ppermute(send, axis, _group_pairs(axis, stride, group, shift))  14.1 us
    dot_general x4, matrix products, contract(): return jnp.einsum(spec, left, right, preferred_element_type=jnp.float32)  12.7 us
    ppermute x14, waiting for transfers between devices, _gather_step(): lax.ppermute(flat, axis, _group_pairs(axis, stride, group, shift))  11.4 us
    ppermute x6, starting transfers between devices, exchange(): lax.ppermute(send, axis, [(i, (i + shift) % count) for i in range(count)])  10.1 us
    ppermute x14, waiting for transfers between devices, _scatter_step(): lax.ppermute(send, axis, _group_pairs(axis, stride, group, shift))  7.2 us
    reshape x5, local copies, waits for them, and re-layouts, blocks(): return matrix.reshape(groups, block, HEADS, head_dim)  6.87 us
  transfers between devices with their start and end apart: 36, of which 17 were waited for; matrix products, arithmetic and copies ran while one was open for 19% of the time, Pallas kernels for 0%

profile of v5, /device:TPU:0, one launch (start us, length us, event | category | flops | bytes accessed | tf_op | source)
XLA Modules:
  0.0 151.5 jit_solution(921872315970281633)
XLA Ops:
  2.0 2.1 %convolution_convert_fusion.7 = bf16[4,128,256]{2,1,0:T(8,128)(2,1)} fusion(bf16[4,256,256]{2,1,0:T(8,128)(2,1)} %param.12, s32[4,128]{1,0:T(4,128)} %param.15, pred[4,128]{1,0:T(4,128)(4,1)S(1)} %iota_compare_fusion.12), kind=kOutput, calls=%fused_computation.54 | convolution fusion | flops 67502080 | bytes 788992 | tf_op jit(solution)/shard_map/dsn,dnh->dsh/dot_general | solution.py:285
  6.9 1.2 convert_reduce_fusion
  8.2 2.4 %fusion.17 = bf16[4,256,256]{2,1,0:T(8,128)(2,1)S(1)} fusion(s32[4,1024]{1,0:T(4,128)} %param.13, s32[4,1024]{1,0:T(4,128)} %param.14), kind=kOutput, calls=%fused_computation.48 | convolution fusion | flops 539230208 | bytes 557056 | tf_op jit(solution)/shard_map/der,des->drs/dot_general | solution.py:294
  10.6 1.3 fusion.21
  13.2 1.3 fusion.15
  14.5 1.3 fusion.24
  16.7 4.6 %collective-permute-start.3 = (bf16[4,64,256]{2,1,0:T(8,128)(2,1)}, bf16[4,64,256]{2,1,0:T(8,128)(2,1)}, u32[]{:S(2)}, u32[]{:S(2)}) collective-permute-start(bf16[4,64,256]{2,1,0:T(8,128)(2,1)} %get-tuple-element.28), channel_id=1, source_target_pairs={{0,24},{8,0},{16,8},{24,16},{1,25},{9,1},{17,9},{25,17},{2,26},{10... | collective-permute-start | bytes 393224 | tf_op jit(solution)/shard_map/ppermute | solution.py:87
  25.0 1.6 %copy.26 = f32[64,16,256]{2,1,0:T(8,128)} copy(f32[64,16,256]{2,0,1:T(8,128)S(1)} %bitcast_convert_fusion) | data formatting | bytes 2097152 | tf_op jit(solution)/shard_map/convert_element_type | solution.py:257
  26.6 7.6 %collective-permute-done.2 = bf16[4,64,256]{2,1,0:T(8,128)(2,1)} collective-permute-done((bf16[4,64,256]{2,1,0:T(8,128)(2,1)}, bf16[4,64,256]{2,1,0:T(8,128)(2,1)}, u32[]{:S(2)}, u32[]{:S(2)}) %collective-permute-start.2) | collective-permute-done | bytes 131104 | tf_op jit(solution)/shard_map/ppermute | solution.py:87
  37.6 1.1 convolution_convert_fusion.1
  38.7 2.0 %reshape.589 = bf16[8,128,4,64]{3,2,1,0:T(4,128)(2,1)S(1)} reshape(bf16[1024,256]{1,0:T(8,128)(2,1)} %convolution_convert_fusion.1) | data formatting | bytes 1048576 | tf_op jit(solution)/shard_map/reshape | solution.py:216
  40.7 1.2 copy.30
  41.9 2.0 %convolution_convert_fusion.2 = bf16[1024,256]{1,0:T(8,128)(2,1)} fusion(bf16[1024,256]{1,0:T(8,128)(2,1)S(1)} %bitcast.239, bf16[256,256]{1,0:T(8,128)(2,1)} %param.19), kind=kOutput, calls=%fused_computation.43 | convolution fusion | flops 134479872 | bytes 1179648 | tf_op jit(solution)/shard_map/dot_general | solution.py:213
  43.9 2.0 %reshape.588 = bf16[8,128,4,64]{3,2,1,0:T(4,128)(2,1)S(1)} reshape(bf16[1024,256]{1,0:T(8,128)(2,1)} %convolution_convert_fusion.2) | data formatting | bytes 1048576 | tf_op jit(solution)/shard_map/reshape | solution.py:216
  45.9 1.2 copy.36
  47.1 1.7 %fusion.27 = f32[8,4,128,128]{3,2,1,0:T(8,128)} fusion(bf16[8,128,4,64]{1,3,2,0:T(8,128)(2,1)S(1)} %copy.35, bf16[8,128,4,64]{3,2,1,0:T(4,128)(2,1)S(1)} %reshape.587), kind=kOutput, calls=%fused_computation.62 | convolution fusion | flops 67108864 | bytes 3145728 | tf_op jit(solution)/shard_map/gihd,gjhd->ghij/dot_general | solution.py:227
  48.9 2.9 %fusion.77 = (f32[8,4,128]{2,1,0:T(4,128)S(1)}, f32[8,4,128,128]{2,3,1,0:T(8,128)}) fusion(pred[128,128]{0,1:T(8,128)(4,1)} %compare_and_fusion, bf16[8,128,4,64]{1,3,2,0:T(8,128)(2,1)S(1)} %copy-done.10, bf16[8,128,4,64]{1,3,2,0:T(8,128)(2,1)S(1)} %copy-done.11), kind=kOutput, calls=%fused_computation.233 | convolution fusion | flops 69206144 | bytes 3178496 | tf_op jit(solution)/shard_map/sub | solution.py:232
  51.8 2.4 %fusion.20 = bf16[8,128,4,64]{1,3,2,0:T(8,128)(2,1)S(1)} fusion(bf16[8,128,4,64]{1,3,2,0:T(8,128)(2,1)S(1)} %copy.35, f32[8,4,128,128]{2,3,1,0:T(8,128)} %get-tuple-element.64, f32[8,4,128]{2,1,0:T(4,128)S(1)} %get-tuple-element.63), kind=kOutput, calls=%fused_computation.51 | convolution fusion | flops 68419584 | bytes 3162112 | tf_op jit(solution)/shard_map/ghij,gihd->gjhd/dot_general | solution.py:227
  54.2 4.3 %fusion.19 = bf16[8,128,4,64]{1,3,2,0:T(8,128)(2,1)S(1)} fusion(bf16[8,128,4,64]{1,3,2,0:T(8,128)(2,1)S(1)} %copy-done.10, f32[8,4,128,128]{3,2,1,0:T(8,128)} %fusion.27, f32[8,4,128,128]{2,3,1,0:T(8,128)} %get-tuple-element.64, f32[8,4,128]{2,1,0:T(4,128)S(1)} %get-tuple-element.63), kind=kOutput, calls=%fused_computation.50 | convolution fusion | flops 71045248 | bytes 5259264 | tf_op jit(solution)/shard_map/ghij,gihd->gjhd/dot_general | solution.py:227
  58.5 4.3 %fusion.18 = bf16[8,128,4,64]{1,3,2,0:T(8,128)(2,1)S(1)} fusion(bf16[8,128,4,64]{1,3,2,0:T(8,128)(2,1)S(1)} %copy-done.11, f32[8,4,128,128]{3,2,1,0:T(8,128)} %fusion.27, f32[8,4,128,128]{2,3,1,0:T(8,128)} %get-tuple-element.64, f32[8,4,128]{2,1,0:T(4,128)} %copy-done.29), kind=kOutput, calls=%fused_computation.49 | convolution fusion | flops 71045248 | bytes 5259264 | tf_op jit(solution)/shard_map/ghij,gjhd->gihd/dot_general | solution.py:227
  67.6 2.0 %collective-permute-start.5 = (bf16[4,64,256]{2,1,0:T(8,128)(2,1)S(1)}, bf16[4,64,256]{2,1,0:T(8,128)(2,1)S(1)}, u32[]{:S(2)}, u32[]{:S(2)}) collective-permute-start(bf16[4,64,256]{2,1,0:T(8,128)(2,1)S(1)} %get-tuple-element.17), channel_id=1, source_target_pairs={{0,16},{8,24},{16,0},{24,8},{1,17},{9,25},{17,1},{25,9},{2,18},{10... | collective-permute-start | bytes 393224 | tf_op jit(solution)/shard_map/ppermute | solution.py:87
  69.6 1.9 %collective-permute-start.4 = (bf16[4,64,256]{2,1,0:T(8,128)(2,1)S(1)}, bf16[4,64,256]{2,1,0:T(8,128)(2,1)S(1)}, u32[]{:S(2)}, u32[]{:S(2)}) collective-permute-start(bf16[4,64,256]{2,1,0:T(8,128)(2,1)S(1)} %get-tuple-element.18), channel_id=1, source_target_pairs={{0,8},{8,16},{16,24},{24,0},{1,9},{9,17},{17,25},{25,1},{2,10},{10... | collective-permute-start | bytes 393224 | tf_op jit(solution)/shard_map/ppermute | solution.py:87
  72.6 9.1 %collective-permute-done.5 = bf16[4,64,256]{2,1,0:T(8,128)(2,1)S(1)} collective-permute-done((bf16[4,64,256]{2,1,0:T(8,128)(2,1)S(1)}, bf16[4,64,256]{2,1,0:T(8,128)(2,1)S(1)}, u32[]{:S(2)}, u32[]{:S(2)}) %collective-permute-start.5) | collective-permute-done | bytes 131104 | tf_op jit(solution)/shard_map/ppermute | solution.py:87
  82.5 1.7 %fusion.26 = bf16[4,256,256]{2,1,0:T(8,128)(2,1)S(1)} fusion(f32[4,256,256]{2,1,0:T(8,128)} %get-tuple-element.62, bf16[4,64,256]{2,1,0:T(8,128)(2,1)S(1)} %get-tuple-element.12, bf16[4,64,256]{2,1,0:T(8,128)(2,1)S(1)} %get-tuple-element.13, bf16[4,64,256]{2,1,0:T(8,128)(2,1)S(1)} %get-tuple-element.14, bf16[4,64,256]{2,1,0:T(8,128)(2,1)S(1)} %get-tuple-element.11), kind=kLoop, calls=%fused_computation.61 | loop fusion | flops 4456448 | bytes 2097152 | tf_op jit(solution)/shard_map/convert_element_type | solution.py:320
  85.1 1.4 constant_dynamic-slice_fusion.8
  87.2 1.5 collective-permute-start.11
  89.3 1.5 collective-permute-start.10
  91.2 2.4 %collective-permute-done.9 = f32[8192]{0:T(1024)S(1)} collective-permute-done((f32[8192]{0:T(1024)S(1)}, f32[8192]{0:T(1024)S(1)}, u32[]{:S(2)}, u32[]{:S(2)}) %collective-permute-start.9) | collective-permute-done | bytes 32800 | tf_op jit(solution)/shard_map/ppermute | solution.py:33
  93.7 2.0 %collective-permute-start.12 = (f32[2048]{0:T(1024)S(1)}, f32[2048]{0:T(1024)S(1)}, u32[]{:S(2)}, u32[]{:S(2)}) collective-permute-start(f32[2048]{0:T(1024)S(1)} %bitcast.301), channel_id=1, source_target_pairs={{0,8},{8,16},{16,24},{24,0},{1,9},{9,17},{17,25},{25,1},{2,10},{10... | collective-permute-start | bytes 24584 | tf_op jit(solution)/shard_map/ppermute | solution.py:33
  95.7 1.3 collective-permute-start.13
  97.0 1.7 %convolution_add_fusion = f32[4,256,256]{2,1,0:T(8,128)S(1)} fusion(bf16[4,256,256]{2,1,0:T(8,128)(2,1)S(1)} %copy-done.7, f32[4,256,256]{2,1,0:T(8,128)S(1)} %convolution_multiply_fusion, bf16[4,64,256]{2,1,0:T(8,128)(2,1)S(1)} %get-tuple-element.12, bf16[4,64,256]{2,1,0:T(8,128)(2,1)S(1)} %get-tuple-element.13, bf16[4,64,256]{2,1,0:T(8,128)(2,1)} %copy-done.8, ...), kind=kOutput, calls=%fused_computation.28 | convolution fusion | flops 807927808 | bytes 3145728 | tf_op jit(solution)/shard_map/drs,drh->dsh/dot_general | solution.py:338
  99.2 1.1 collective-permute-done.13
  100.3 1.8 %collective-permute-start.17 = (f32[2048]{0:T(1024)S(1)}, f32[2048]{0:T(1024)S(1)}, u32[]{:S(2)}, u32[]{:S(2)}) collective-permute-start(f32[2048]{0:T(1024)S(1)} %add_add_fusion.3), channel_id=1, source_target_pairs={{0,24},{8,0},{16,8},{24,16},{1,25},{9,1},{17,9},{25,17},{2,26},{10... | collective-permute-start | bytes 24584 | tf_op jit(solution)/shard_map/ppermute | solution.py:40
  102.1 1.4 collective-permute-start.15
  103.6 1.5 convolution_convert_fusion.6
  105.2 1.5 collective-permute-done.16
  109.8 2.0 %collective-permute-start.25 = (f32[24576]{0:T(1024)S(1)}, f32[24576]{0:T(1024)S(1)}, u32[]{:S(2)}, u32[]{:S(2)}) collective-permute-start(f32[24576]{0:T(1024)S(1)} %bitcast.274), channel_id=1, source_target_pairs={{0,6},{1,7},{2,0},{3,1},{4,2},{5,3},{6,4},{7,5},{8,14},{9,15},{10,... | collective-permute-start | bytes 294920 | tf_op jit(solution)/shard_map/ppermute | solution.py:33
  112.0 1.4 collective-permute-start.24
  113.5 2.9 %collective-permute-start.20 = (f32[8192]{0:T(1024)S(1)}, f32[8192]{0:T(1024)S(1)}, u32[]{:S(2)}, u32[]{:S(2)}) collective-permute-start(f32[8192]{0:T(1024)S(1)} %bitcast.284), channel_id=1, source_target_pairs={{0,6},{1,7},{2,0},{3,1},{4,2},{5,3},{6,4},{7,5},{8,14},{9,15},{10,... | collective-permute-start | bytes 98312 | tf_op jit(solution)/shard_map/ppermute | solution.py:40
  118.6 1.3 collective-permute-start.28
  123.2 2.5 %collective-permute-done.26 = f32[6144]{0:T(1024)S(1)} collective-permute-done((f32[6144]{0:T(1024)S(1)}, f32[6144]{0:T(1024)S(1)}, u32[]{:S(2)}, u32[]{:S(2)}) %collective-permute-start.26) | collective-permute-done | bytes 24608 | tf_op jit(solution)/shard_map/ppermute | solution.py:33
  125.9 2.6 %collective-permute-start.31 = (f32[6144]{0:T(1024)S(1)}, f32[6144]{0:T(1024)S(1)}, u32[]{:S(2)}, u32[]{:S(2)}) collective-permute-start(f32[6144]{0:T(1024)S(1)} %add_add_fusion.2), channel_id=1, source_target_pairs={{0,24},{8,0},{16,8},{24,16},{1,25},{9,1},{17,9},{25,17},{2,26},{10... | collective-permute-start | bytes 73736 | tf_op jit(solution)/shard_map/ppermute | solution.py:40
  130.0 3.2 %collective-permute-done.30 = f32[6144]{0:T(1024)S(1)} collective-permute-done((f32[6144]{0:T(1024)S(1)}, f32[6144]{0:T(1024)S(1)}, u32[]{:S(2)}, u32[]{:S(2)}) %collective-permute-start.30) | collective-permute-done | bytes 24608 | tf_op jit(solution)/shard_map/ppermute | solution.py:40
  135.0 2.0 %collective-permute-start.34 = (f32[24576]{0:T(1024)S(1)}, f32[24576]{0:T(1024)S(1)}, u32[]{:S(2)}, u32[]{:S(2)}) collective-permute-start(f32[24576]{0:T(1024)S(1)} %bitcast.278), channel_id=1, source_target_pairs={{0,6},{1,7},{2,0},{3,1},{4,2},{5,3},{6,4},{7,5},{8,14},{9,15},{10,... | collective-permute-start | bytes 294920 | tf_op jit(solution)/shard_map/ppermute | solution.py:40
  137.0 1.4 collective-permute-start.33
  138.9 1.3 convolution_add_fusion.4
  140.3 1.3 collective-permute-done.33
  141.6 2.3 %collective-permute-done.32 = f32[24576]{0:T(1024)S(1)} collective-permute-done((f32[24576]{0:T(1024)S(1)}, f32[24576]{0:T(1024)S(1)}, u32[]{:S(2)}, u32[]{:S(2)}) %collective-permute-start.32) | collective-permute-done | bytes 98336 | tf_op jit(solution)/shard_map/ppermute | solution.py:40
  (211 shorter events, 43.0 us)
Async XLA Ops:
  0.6 13.8 %copy-start = (bf16[256,256]{1,0:T(8,128)(2,1)S(1)}, bf16[256,256]{1,0:T(8,128)(2,1)}, u32[]{:S(2)}) copy-start(bf16[256,256]{1,0:T(8,128)(2,1)} %param.17) | copy-start | bytes 393220
  4.1 9.1 %collective-permute-start = (bf16[4,128,256]{2,1,0:T(8,128)(2,1)}, bf16[4,128,256]{2,1,0:T(8,128)(2,1)}, u32[]{:S(2)}, u32[]{:S(2)}) collective-permute-start(bf16[4,128,256]{2,1,0:T(8,128)(2,1)} %convolution_convert_fusion.7), channel_id=1, source_target_pairs={{0,1},{1,2},{2,3},{3,4},{4,5},{5,6},{6,7},{7,0},{8,9},{9,10},{10,1... | collective-permute-start | bytes 786440 | tf_op jit(solution)/shard_map/ppermute | solution.py:12
  4.5 3.6 %copy-start.26 = (pred[2]{0:T(512)(128)(4,1)}, pred[2]{0:T(512)(128)(4,1)S(1)}, u32[]{:S(2)}) copy-start(pred[2]{0:T(512)(128)(4,1)S(1)} %compare_and_fusion.4) | copy-start | bytes 10
  12.0 2.5 %copy-start.9 = (bf16[4,256,128]{2,1,0:T(8,128)(2,1)}, bf16[4,256,128]{2,1,0:T(8,128)(2,1)S(1)}, u32[]{:S(2)}) copy-start(bf16[4,256,128]{2,1,0:T(8,128)(2,1)S(1)} %fusion.21) | copy-start | bytes 786436
  15.8 7.0 %copy-start.27 = (pred[2]{0:T(512)(128)(4,1)S(1)}, pred[2]{0:T(512)(128)(4,1)}, u32[]{:S(2)}) copy-start(pred[2]{0:T(512)(128)(4,1)} %copy-done.26) | copy-start | bytes 10
  16.7 9.9 %collective-permute-start.3 = (bf16[4,64,256]{2,1,0:T(8,128)(2,1)}, bf16[4,64,256]{2,1,0:T(8,128)(2,1)}, u32[]{:S(2)}, u32[]{:S(2)}) collective-permute-start(bf16[4,64,256]{2,1,0:T(8,128)(2,1)} %get-tuple-element.28), channel_id=1, source_target_pairs={{0,24},{8,0},{16,8},{24,16},{1,25},{9,1},{17,9},{25,17},{2,26},{10... | collective-permute-start | bytes 393224 | tf_op jit(solution)/shard_map/ppermute | solution.py:87
  21.3 12.9 %collective-permute-start.2 = (bf16[4,64,256]{2,1,0:T(8,128)(2,1)}, bf16[4,64,256]{2,1,0:T(8,128)(2,1)}, u32[]{:S(2)}, u32[]{:S(2)}) collective-permute-start(bf16[4,64,256]{2,1,0:T(8,128)(2,1)} %get-tuple-element.29), channel_id=1, source_target_pairs={{0,16},{8,24},{16,0},{24,8},{1,17},{9,25},{17,1},{25,9},{2,18},{10... | collective-permute-start | bytes 393224 | tf_op jit(solution)/shard_map/ppermute | solution.py:87
  21.3 12.9 %collective-permute-start.1 = (bf16[4,64,256]{2,1,0:T(8,128)(2,1)S(1)}, bf16[4,64,256]{2,1,0:T(8,128)(2,1)}, u32[]{:S(2)}, u32[]{:S(2)}) collective-permute-start(bf16[4,64,256]{2,1,0:T(8,128)(2,1)S(1)} %get-tuple-element.30), channel_id=1, source_target_pairs={{0,8},{8,16},{16,24},{24,0},{1,9},{9,17},{17,25},{25,1},{2,10},{10... | collective-permute-start | bytes 393224 | tf_op jit(solution)/shard_map/ppermute | solution.py:87
  25.0 11.0 %copy-start.18 = (pred[4]{0:T(512)(128)(4,1)S(1)}, pred[4]{0:T(512)(128)(4,1)}, u32[]{:S(2)}) copy-start(pred[4]{0:T(512)(128)(4,1)} %get-tuple-element.65) | copy-start | bytes 16
  67.0 5.6 %collective-permute-start.6 = (bf16[4,64,256]{2,1,0:T(8,128)(2,1)S(1)}, bf16[4,64,256]{2,1,0:T(8,128)(2,1)S(1)}, u32[]{:S(2)}, u32[]{:S(2)}) collective-permute-start(bf16[4,64,256]{2,1,0:T(8,128)(2,1)S(1)} %get-tuple-element.16), channel_id=1, source_target_pairs={{0,24},{8,0},{16,8},{24,16},{1,25},{9,1},{17,9},{25,17},{2,26},{10... | collective-permute-start | bytes 393224 | tf_op jit(solution)/shard_map/ppermute | solution.py:87
  67.6 14.1 %collective-permute-start.5 = (bf16[4,64,256]{2,1,0:T(8,128)(2,1)S(1)}, bf16[4,64,256]{2,1,0:T(8,128)(2,1)S(1)}, u32[]{:S(2)}, u32[]{:S(2)}) collective-permute-start(bf16[4,64,256]{2,1,0:T(8,128)(2,1)S(1)} %get-tuple-element.17), channel_id=1, source_target_pairs={{0,16},{8,24},{16,0},{24,8},{1,17},{9,25},{17,1},{25,9},{2,18},{10... | collective-permute-start | bytes 393224 | tf_op jit(solution)/shard_map/ppermute | solution.py:87
  69.6 12.1 %collective-permute-start.4 = (bf16[4,64,256]{2,1,0:T(8,128)(2,1)S(1)}, bf16[4,64,256]{2,1,0:T(8,128)(2,1)S(1)}, u32[]{:S(2)}, u32[]{:S(2)}) collective-permute-start(bf16[4,64,256]{2,1,0:T(8,128)(2,1)S(1)} %get-tuple-element.18), channel_id=1, source_target_pairs={{0,8},{8,16},{16,24},{24,0},{1,9},{9,17},{17,25},{25,1},{2,10},{10... | collective-permute-start | bytes 393224 | tf_op jit(solution)/shard_map/ppermute | solution.py:87
  71.6 10.8 %copy-start.19 = (pred[4]{0:T(512)(128)(4,1)S(1)}, pred[4]{0:T(512)(128)(4,1)}, u32[]{:S(2)}) copy-start(pred[4]{0:T(512)(128)(4,1)} %get-tuple-element.65) | copy-start | bytes 16
  82.5 2.5 %copy-start.8 = (bf16[4,64,256]{2,1,0:T(8,128)(2,1)}, bf16[4,64,256]{2,1,0:T(8,128)(2,1)S(1)}, u32[]{:S(2)}) copy-start(bf16[4,64,256]{2,1,0:T(8,128)(2,1)S(1)} %get-tuple-element.14) | copy-start | bytes 393220
  85.0 12.0 %copy-start.7 = (bf16[4,256,256]{2,1,0:T(8,128)(2,1)S(1)}, bf16[4,256,256]{2,1,0:T(8,128)(2,1)}, u32[]{:S(2)}) copy-start(bf16[4,256,256]{2,1,0:T(8,128)(2,1)} %copy-done.6) | copy-start | bytes 1572868
  85.0 2.0 %collective-permute-start.8 = (f32[32768]{0:T(1024)S(1)}, f32[32768]{0:T(1024)S(1)}, u32[]{:S(2)}, u32[]{:S(2)}) collective-permute-start(f32[32768]{0:T(1024)S(1)} %bitcast.266), channel_id=1, source_target_pairs={{0,1},{1,0},{2,3},{3,2},{4,5},{5,4},{6,7},{7,6},{8,9},{9,8},{10,11... | collective-permute-start | bytes 393224 | tf_op jit(solution)/shard_map/ppermute | solution.py:33
  86.5 21.7 %collective-permute-start.22 = (f32[98304]{0:T(1024)}, f32[98304]{0:T(1024)}, u32[]{:S(2)}, u32[]{:S(2)}) collective-permute-start(f32[98304]{0:T(1024)} %bitcast.66), channel_id=1, source_target_pairs={{0,1},{1,0},{2,3},{3,2},{4,5},{5,4},{6,7},{7,6},{8,9},{9,8},{10,11... | collective-permute-start | bytes 1179656 | tf_op jit(solution)/shard_map/ppermute | solution.py:33
  87.2 4.0 %collective-permute-start.11 = (f32[8192]{0:T(1024)S(1)}, f32[8192]{0:T(1024)S(1)}, u32[]{:S(2)}, u32[]{:S(2)}) collective-permute-start(f32[8192]{0:T(1024)S(1)} %bitcast.293), channel_id=1, source_target_pairs={{0,6},{1,7},{2,0},{3,1},{4,2},{5,3},{6,4},{7,5},{8,14},{9,15},{10,... | collective-permute-start | bytes 98312 | tf_op jit(solution)/shard_map/ppermute | solution.py:33
  88.7 4.8 %collective-permute-start.9 = (f32[8192]{0:T(1024)S(1)}, f32[8192]{0:T(1024)S(1)}, u32[]{:S(2)}, u32[]{:S(2)}) collective-permute-start(f32[8192]{0:T(1024)S(1)} %bitcast.292), channel_id=1, source_target_pairs={{0,2},{1,3},{2,4},{3,5},{4,6},{5,7},{6,0},{7,1},{8,10},{9,11},{10,... | collective-permute-start | bytes 98312 | tf_op jit(solution)/shard_map/ppermute | solution.py:33
  89.3 4.3 %collective-permute-start.10 = (f32[8192]{0:T(1024)S(1)}, f32[8192]{0:T(1024)S(1)}, u32[]{:S(2)}, u32[]{:S(2)}) collective-permute-start(f32[8192]{0:T(1024)S(1)} %bitcast.291), channel_id=1, source_target_pairs={{0,4},{1,5},{2,6},{3,7},{4,0},{5,1},{6,2},{7,3},{8,12},{9,13},{10,... | collective-permute-start | bytes 98312 | tf_op jit(solution)/shard_map/ppermute | solution.py:33
  93.6 5.1 %collective-permute-start.14 = (f32[2048]{0:T(1024)S(1)}, f32[2048]{0:T(1024)S(1)}, u32[]{:S(2)}, u32[]{:S(2)}) collective-permute-start(f32[2048]{0:T(1024)S(1)} %bitcast.302), channel_id=1, source_target_pairs={{0,24},{8,0},{16,8},{24,16},{1,25},{9,1},{17,9},{25,17},{2,26},{10... | collective-permute-start | bytes 24584 | tf_op jit(solution)/shard_map/ppermute | solution.py:33
  93.7 5.5 %collective-permute-start.12 = (f32[2048]{0:T(1024)S(1)}, f32[2048]{0:T(1024)S(1)}, u32[]{:S(2)}, u32[]{:S(2)}) collective-permute-start(f32[2048]{0:T(1024)S(1)} %bitcast.301), channel_id=1, source_target_pairs={{0,8},{8,16},{16,24},{24,0},{1,9},{9,17},{17,25},{25,1},{2,10},{10... | collective-permute-start | bytes 24584 | tf_op jit(solution)/shard_map/ppermute | solution.py:33
  95.7 4.6 %collective-permute-start.13 = (f32[2048]{0:T(1024)S(1)}, f32[2048]{0:T(1024)S(1)}, u32[]{:S(2)}, u32[]{:S(2)}) collective-permute-start(f32[2048]{0:T(1024)S(1)} %bitcast.300), channel_id=1, source_target_pairs={{0,16},{8,24},{16,0},{24,8},{1,17},{9,25},{17,1},{25,9},{2,18},{10... | collective-permute-start | bytes 24584 | tf_op jit(solution)/shard_map/ppermute | solution.py:33
  100.3 13.1 %copy-start.17 = (pred[4]{0:T(512)(128)(4,1)S(1)}, pred[4]{0:T(512)(128)(4,1)}, u32[]{:S(2)}) copy-start(pred[4]{0:T(512)(128)(4,1)} %get-tuple-element.66) | copy-start | bytes 16
  100.3 4.8 %collective-permute-start.17 = (f32[2048]{0:T(1024)S(1)}, f32[2048]{0:T(1024)S(1)}, u32[]{:S(2)}, u32[]{:S(2)}) collective-permute-start(f32[2048]{0:T(1024)S(1)} %add_add_fusion.3), channel_id=1, source_target_pairs={{0,24},{8,0},{16,8},{24,16},{1,25},{9,1},{17,9},{25,17},{2,26},{10... | collective-permute-start | bytes 24584 | tf_op jit(solution)/shard_map/ppermute | solution.py:40
  102.1 4.5 %collective-permute-start.16 = (f32[2048]{0:T(1024)S(1)}, f32[2048]{0:T(1024)S(1)}, u32[]{:S(2)}, u32[]{:S(2)}) collective-permute-start(f32[2048]{0:T(1024)S(1)} %add_add_fusion.3), channel_id=1, source_target_pairs={{0,16},{8,24},{16,0},{24,8},{1,17},{9,25},{17,1},{25,9},{2,18},{10... | collective-permute-start | bytes 24584 | tf_op jit(solution)/shard_map/ppermute | solution.py:40
  102.1 5.4 %collective-permute-start.15 = (f32[2048]{0:T(1024)S(1)}, f32[2048]{0:T(1024)S(1)}, u32[]{:S(2)}, u32[]{:S(2)}) collective-permute-start(f32[2048]{0:T(1024)S(1)} %add_add_fusion.3), channel_id=1, source_target_pairs={{0,8},{8,16},{16,24},{24,0},{1,9},{9,17},{17,25},{25,1},{2,10},{10... | collective-permute-start | bytes 24584 | tf_op jit(solution)/shard_map/ppermute | solution.py:40
  105.1 33.8 %collective-permute-start.7 = (bf16[4,128,256]{2,1,0:T(8,128)(2,1)S(1)}, bf16[4,128,256]{2,1,0:T(8,128)(2,1)S(1)}, u32[]{:S(2)}, u32[]{:S(2)}) collective-permute-start(bf16[4,128,256]{2,1,0:T(8,128)(2,1)S(1)} %convolution_convert_fusion.6), channel_id=1, source_target_pairs={{0,7},{1,0},{2,1},{3,2},{4,3},{5,4},{6,5},{7,6},{8,15},{9,8},{10,9... | collective-permute-start | bytes 786440 | tf_op jit(solution)/shard_map/ppermute | solution.py:12
  109.3 19.9 %copy-start.21 = (pred[4]{0:T(512)(128)(4,1)S(1)}, pred[4]{0:T(512)(128)(4,1)}, u32[]{:S(2)}) copy-start(pred[4]{0:T(512)(128)(4,1)} %compare_and_fusion.3) | copy-start | bytes 16
  109.8 6.7 %collective-permute-start.25 = (f32[24576]{0:T(1024)S(1)}, f32[24576]{0:T(1024)S(1)}, u32[]{:S(2)}, u32[]{:S(2)}) collective-permute-start(f32[24576]{0:T(1024)S(1)} %bitcast.274), channel_id=1, source_target_pairs={{0,6},{1,7},{2,0},{3,1},{4,2},{5,3},{6,4},{7,5},{8,14},{9,15},{10,... | collective-permute-start | bytes 294920 | tf_op jit(solution)/shard_map/ppermute | solution.py:33
  111.8 5.6 %collective-permute-start.23 = (f32[24576]{0:T(1024)S(1)}, f32[24576]{0:T(1024)S(1)}, u32[]{:S(2)}, u32[]{:S(2)}) collective-permute-start(f32[24576]{0:T(1024)S(1)} %bitcast.273), channel_id=1, source_target_pairs={{0,2},{1,3},{2,4},{3,5},{4,6},{5,7},{6,0},{7,1},{8,10},{9,11},{10,... | collective-permute-start | bytes 294920 | tf_op jit(solution)/shard_map/ppermute | solution.py:33
  112.0 6.4 %collective-permute-start.24 = (f32[24576]{0:T(1024)S(1)}, f32[24576]{0:T(1024)S(1)}, u32[]{:S(2)}, u32[]{:S(2)}) collective-permute-start(f32[24576]{0:T(1024)S(1)} %bitcast.272), channel_id=1, source_target_pairs={{0,4},{1,5},{2,6},{3,7},{4,0},{5,1},{6,2},{7,3},{8,12},{9,13},{10,... | collective-permute-start | bytes 294920 | tf_op jit(solution)/shard_map/ppermute | solution.py:33
  113.5 6.4 %collective-permute-start.20 = (f32[8192]{0:T(1024)S(1)}, f32[8192]{0:T(1024)S(1)}, u32[]{:S(2)}, u32[]{:S(2)}) collective-permute-start(f32[8192]{0:T(1024)S(1)} %bitcast.284), channel_id=1, source_target_pairs={{0,6},{1,7},{2,0},{3,1},{4,2},{5,3},{6,4},{7,5},{8,14},{9,15},{10,... | collective-permute-start | bytes 98312 | tf_op jit(solution)/shard_map/ppermute | solution.py:40
  116.5 4.2 %collective-permute-start.19 = (f32[8192]{0:T(1024)S(1)}, f32[8192]{0:T(1024)S(1)}, u32[]{:S(2)}, u32[]{:S(2)}) collective-permute-start(f32[8192]{0:T(1024)S(1)} %bitcast.285), channel_id=1, source_target_pairs={{0,4},{1,5},{2,6},{3,7},{4,0},{5,1},{6,2},{7,3},{8,12},{9,13},{10,... | collective-permute-start | bytes 98312 | tf_op jit(solution)/shard_map/ppermute | solution.py:40
  117.5 4.8 %collective-permute-start.18 = (f32[8192]{0:T(1024)S(1)}, f32[8192]{0:T(1024)S(1)}, u32[]{:S(2)}, u32[]{:S(2)}) collective-permute-start(f32[8192]{0:T(1024)S(1)} %bitcast.286), channel_id=1, source_target_pairs={{0,2},{1,3},{2,4},{3,5},{4,6},{5,7},{6,0},{7,1},{8,10},{9,11},{10,... | collective-permute-start | bytes 98312 | tf_op jit(solution)/shard_map/ppermute | solution.py:40
  118.5 20.4 %copy-start.16 = (s32[4,128]{1,0:T(4,128)S(1)}, s32[4,128]{1,0:T(4,128)}, u32[]{:S(2)}) copy-start(s32[4,128]{1,0:T(4,128)} %param.15) | copy-start | bytes 6148
  118.5 20.4 %copy-start.23 = (pred[4,128]{1,0:T(4,128)(4,1)S(1)}, pred[4,128]{1,0:T(4,128)(4,1)}, u32[]{:S(2)}) copy-start(pred[4,128]{1,0:T(4,128)(4,1)} %copy-done.22) | copy-start | bytes 1540
  118.6 4.6 %collective-permute-start.28 = (f32[6144]{0:T(1024)S(1)}, f32[6144]{0:T(1024)S(1)}, u32[]{:S(2)}, u32[]{:S(2)}) collective-permute-start(f32[6144]{0:T(1024)S(1)} %bitcast.296), channel_id=1, source_target_pairs={{0,24},{8,0},{16,8},{24,16},{1,25},{9,1},{17,9},{25,17},{2,26},{10... | collective-permute-start | bytes 73736 | tf_op jit(solution)/shard_map/ppermute | solution.py:33
  119.9 5.7 %collective-permute-start.26 = (f32[6144]{0:T(1024)S(1)}, f32[6144]{0:T(1024)S(1)}, u32[]{:S(2)}, u32[]{:S(2)}) collective-permute-start(f32[6144]{0:T(1024)S(1)} %bitcast.295), channel_id=1, source_target_pairs={{0,8},{8,16},{16,24},{24,0},{1,9},{9,17},{17,25},{25,1},{2,10},{10... | collective-permute-start | bytes 73736 | tf_op jit(solution)/shard_map/ppermute | solution.py:33
  120.6 5.3 %collective-permute-start.27 = (f32[6144]{0:T(1024)S(1)}, f32[6144]{0:T(1024)S(1)}, u32[]{:S(2)}, u32[]{:S(2)}) collective-permute-start(f32[6144]{0:T(1024)S(1)} %bitcast.294), channel_id=1, source_target_pairs={{0,16},{8,24},{16,0},{24,8},{1,17},{9,25},{17,1},{25,9},{2,18},{10... | collective-permute-start | bytes 73736 | tf_op jit(solution)/shard_map/ppermute | solution.py:33
  125.9 4.1 %collective-permute-start.31 = (f32[6144]{0:T(1024)S(1)}, f32[6144]{0:T(1024)S(1)}, u32[]{:S(2)}, u32[]{:S(2)}) collective-permute-start(f32[6144]{0:T(1024)S(1)} %add_add_fusion.2), channel_id=1, source_target_pairs={{0,24},{8,0},{16,8},{24,16},{1,25},{9,1},{17,9},{25,17},{2,26},{10... | collective-permute-start | bytes 73736 | tf_op jit(solution)/shard_map/ppermute | solution.py:40
  128.5 4.7 %collective-permute-start.30 = (f32[6144]{0:T(1024)S(1)}, f32[6144]{0:T(1024)S(1)}, u32[]{:S(2)}, u32[]{:S(2)}) collective-permute-start(f32[6144]{0:T(1024)S(1)} %add_add_fusion.2), channel_id=1, source_target_pairs={{0,16},{8,24},{16,0},{24,8},{1,17},{9,25},{17,1},{25,9},{2,18},{10... | collective-permute-start | bytes 73736 | tf_op jit(solution)/shard_map/ppermute | solution.py:40
  128.5 5.6 %collective-permute-start.29 = (f32[6144]{0:T(1024)S(1)}, f32[6144]{0:T(1024)S(1)}, u32[]{:S(2)}, u32[]{:S(2)}) collective-permute-start(f32[6144]{0:T(1024)S(1)} %add_add_fusion.2), channel_id=1, source_target_pairs={{0,8},{8,16},{16,24},{24,0},{1,9},{9,17},{17,25},{25,1},{2,10},{10... | collective-permute-start | bytes 73736 | tf_op jit(solution)/shard_map/ppermute | solution.py:40
  129.4 16.0 %collective-permute-start.21 = (f32[32768]{0:T(1024)S(1)}, f32[32768]{0:T(1024)S(1)}, u32[]{:S(2)}, u32[]{:S(2)}) collective-permute-start(f32[32768]{0:T(1024)S(1)} %bitcast.264), channel_id=1, source_target_pairs={{0,1},{1,0},{2,3},{3,2},{4,5},{5,4},{6,7},{7,6},{8,9},{9,8},{10,11... | collective-permute-start | bytes 393224 | tf_op jit(solution)/shard_map/ppermute | solution.py:40
  135.0 5.3 %collective-permute-start.34 = (f32[24576]{0:T(1024)S(1)}, f32[24576]{0:T(1024)S(1)}, u32[]{:S(2)}, u32[]{:S(2)}) collective-permute-start(f32[24576]{0:T(1024)S(1)} %bitcast.278), channel_id=1, source_target_pairs={{0,6},{1,7},{2,0},{3,1},{4,2},{5,3},{6,4},{7,5},{8,14},{9,15},{10,... | collective-permute-start | bytes 294920 | tf_op jit(solution)/shard_map/ppermute | solution.py:40
  137.0 4.6 %collective-permute-start.33 = (f32[24576]{0:T(1024)S(1)}, f32[24576]{0:T(1024)S(1)}, u32[]{:S(2)}, u32[]{:S(2)}) collective-permute-start(f32[24576]{0:T(1024)S(1)} %bitcast.279), channel_id=1, source_target_pairs={{0,4},{1,5},{2,6},{3,7},{4,0},{5,1},{6,2},{7,3},{8,12},{9,13},{10,... | collective-permute-start | bytes 294920 | tf_op jit(solution)/shard_map/ppermute | solution.py:40
  138.3 5.5 %collective-permute-start.32 = (f32[24576]{0:T(1024)S(1)}, f32[24576]{0:T(1024)S(1)}, u32[]{:S(2)}, u32[]{:S(2)}) collective-permute-start(f32[24576]{0:T(1024)S(1)} %bitcast.280), channel_id=1, source_target_pairs={{0,2},{1,3},{2,4},{3,5},{4,6},{5,7},{6,0},{7,1},{8,10},{9,11},{10,... | collective-permute-start | bytes 294920 | tf_op jit(solution)/shard_map/ppermute | solution.py:40
  145.3 2.5 %collective-permute-start.35 = (f32[98304]{0:T(1024)S(1)}, f32[98304]{0:T(1024)S(1)}, u32[]{:S(2)}, u32[]{:S(2)}) collective-permute-start(f32[98304]{0:T(1024)S(1)} %bitcast.260), channel_id=1, source_target_pairs={{0,1},{1,0},{2,3},{3,2},{4,5},{5,4},{6,7},{7,6},{8,9},{9,8},{10,11... | collective-permute-start | bytes 1179656 | tf_op jit(solution)/shard_map/ppermute | solution.py:40
  (18 other events, 30.0 us)

commit v6 on v4

--- a/solution.py
+++ b/solution.py
@@ -34,14 +34,30 @@
     return total
 
 
+def _by_source(got, digit):
+    group = len(got)
+    turned = jnp.stack([got[0]] + got[:0:-1] + [got[0]] + got[:0:-1])
+    return lax.dynamic_slice_in_dim(turned, group - digit, group, axis=0)
+
+
 def _gather_step(flat, axis, stride, group):
     digit = (lax.axis_index(axis) // stride) % group
     got = [flat] + [
         lax.ppermute(flat, axis, _group_pairs(axis, stride, group, shift)) for shift in range(1, group)
     ]
-    stacked = jnp.stack(got)
-    order = (digit - jnp.arange(group)) % group
-    return jnp.take(stacked, order, axis=0).reshape(-1)
+    return _by_source(got, digit).reshape(-1)
+
+
+def _reduce_step(flat, axis, stride, group):
+    digit = (lax.axis_index(axis) // stride) % group
+    got = [flat] + [
+        lax.ppermute(flat, axis, _group_pairs(axis, stride, group, shift)) for shift in range(1, group)
+    ]
+    ordered = _by_source(got, digit)
+    total = ordered[0]
+    for source in range(1, group):
+        total = total + ordered[source]
+    return total
 
 
 def _factors(size):
@@ -65,9 +81,10 @@
             if group > 1:
                 steps.append((axis, stride, group))
             stride *= group
-    for axis, stride, group in steps:
+    for axis, stride, group in steps[:-1]:
         flat = _scatter_step(flat, axis, stride, group)
-    for axis, stride, group in reversed(steps):
+    flat = _reduce_step(flat, *steps[-1])
+    for axis, stride, group in reversed(steps[:-1]):
         flat = _gather_step(flat, axis, stride, group)
     results, start = [], 0
     for value in values:
@@ -86,7 +103,7 @@
         if shift:
             send = lax.ppermute(send, axis, [(i, (i + shift) % count) for i in range(count)])
         got.append(send)
-    stacked = jnp.take(jnp.stack(got), (mine - jnp.arange(count)) % count, axis=0)
+    stacked = _by_source(got, mine)
     return jnp.concatenate([stacked[k] for k in range(count)], axis=concat_axis)
 
 
@@ -237,6 +254,7 @@
     score_grad = (
         probs * (prob_grad - jnp.sum(prob_grad * probs, axis=-1, keepdims=True)) * scale_factor
     ).astype(jnp.bfloat16)
+    score_grad = lax.optimization_barrier(score_grad)
     query_grad = contract("ghij,gjhd->gihd", score_grad, key_rows).astype(jnp.bfloat16)
     key_grad = contract("ghij,gihd->gjhd", score_grad, queries).astype(jnp.bfloat16)
     query_flat = query_grad.reshape(-1, width)

time: 126 us -> 132 us (1.048)
  waiting for transfers between devices: 26.9 us -> 41.3 us
  starting transfers between devices: 31.1 us -> 21.2 us
  local copies, waits for them, and re-layouts: 22.5 us -> 26.7 us
  matrix products: 33.1 us -> 31.6 us
    ppermute x6, waiting for transfers between devices: 11.8 us -> 20.9 us  [exchange(): lax.ppermute(send, axis, [(i, (i + shift) % count) for i in range(count)])]
    ppermute x0 -> x3, waiting for transfers between devices: none -> 9.08 us  [_reduce_step(): lax.ppermute(flat, axis, _group_pairs(axis, stride, group, shift))]
    dot_general x4, matrix products: 12.7 us -> 5.57 us  [contract(): return jnp.einsum(spec, left, right, preferred_element_type=jnp.float32)]
    ppermute x7 -> x4, starting transfers between devices: 9.45 us -> 3.67 us  [_scatter_step(): lax.ppermute(send, axis, _group_pairs(axis, stride, group, shift))]
    another operation x0 -> x4, local copies, waits for them, and re-layouts: none -> 5.74 us  [_by_source(): turned = jnp.stack([got[0]] + got[:0:-1] + [got[0]] + got[:0:-1])]
    reshape x5, local copies, waits for them, and re-layouts: 2.99 us -> 8.5 us  [blocks(): return matrix.reshape(groups, block, HEADS, head_dim)]
    ppermute x7 -> x4, starting transfers between devices: 9.1 us -> 3.6 us  [_gather_step(): lax.ppermute(flat, axis, _group_pairs(axis, stride, group, shift))]
    gather x7 -> x0, local copies, waits for them, and re-layouts: 5.3 us -> none  [the longest x5 4.14 us: _gather_step(): return jnp.take(stacked, order, axis=0).reshape(-1)]
  transfers between devices with their start and end apart: 22 -> 19, of which waited for: 16 -> 11; matrix products, arithmetic and copies ran while one was open for 14% -> 15% of each run, Pallas kernels for 0% -> 0%
where the time goes in v6:
time: 132 us; the launch traced here: 131 us
  waiting for transfers between devices  41.3 us (31%)
  matrix products  31.6 us (24%)
  local copies, waits for them, and re-layouts  26.7 us (20%)
  starting transfers between devices  21.2 us (16%)
  other arithmetic  8.38 us (6%)
  between operations  1.5 us (1%)
    ppermute x6, waiting for transfers between devices, exchange(): lax.ppermute(send, axis, [(i, (i + shift) % count) for i in range(count)])  20.9 us
    ppermute x6, starting transfers between devices, exchange(): lax.ppermute(send, axis, [(i, (i + shift) % count) for i in range(count)])  10.5 us
    ppermute x3, waiting for transfers between devices, _reduce_step(): lax.ppermute(flat, axis, _group_pairs(axis, stride, group, shift))  9.08 us
    reshape x5, local copies, waits for them, and re-layouts, blocks(): return matrix.reshape(groups, block, HEADS, head_dim)  8.5 us
    ppermute x4, waiting for transfers between devices, _scatter_step(): lax.ppermute(send, axis, _group_pairs(axis, stride, group, shift))  7.8 us
    another operation x4, local copies, waits for them, and re-layouts, _by_source(): turned = jnp.stack([got[0]] + got[:0:-1] + [got[0]] + got[:0:-1])  5.74 us
    dot_general x4, matrix products, contract(): return jnp.einsum(spec, left, right, preferred_element_type=jnp.float32)  5.57 us
    unnamed x63, local copies, waits for them, and re-layouts  4.67 us
  transfers between devices with their start and end apart: 19, of which 11 were waited for; matrix products, arithmetic and copies ran while one was open for 15% of the time, Pallas kernels for 0%

profile of v6, /device:TPU:0, one launch (start us, length us, event | category | flops | bytes accessed | tf_op | source)
XLA Modules:
  0.0 130.6 jit_solution(5107666039315338829)
XLA Ops:
  1.4 2.1 %convolution_convert_fusion.7 = bf16[4,128,256]{2,1,0:T(8,128)(2,1)} fusion(bf16[4,256,256]{2,1,0:T(8,128)(2,1)} %param.10, s32[4,128]{1,0:T(4,128)} %param.13, pred[4,128]{1,0:T(4,128)(4,1)S(1)} %iota_compare_fusion.12), kind=kOutput, calls=%fused_computation.50 | convolution fusion | flops 67502080 | bytes 788992 | tf_op jit(solution)/shard_map/dsn,dnh->dsh/dot_general | solution.py:303
  4.0 1.2 convert_reduce_fusion
  5.2 3.1 %fusion.17 = bf16[4,256,256]{2,1,0:T(8,128)(2,1)} fusion(s32[4,1024]{1,0:T(4,128)} %param.11, s32[4,1024]{1,0:T(4,128)} %param.12), kind=kOutput, calls=%fused_computation.44 | convolution fusion | flops 539230208 | bytes 557056 | tf_op jit(solution)/shard_map/der,des->drs/dot_general | solution.py:312
  8.3 1.3 %fusion.21 = bf16[4,256,128]{2,1,0:T(8,128)(2,1)S(1)} fusion(s32[4,1024]{1,0:T(4,128)S(1)} %copy-done.18, s32[128]{0:T(128)S(1)} %iota_add_fusion, s32[4,1024]{1,0:T(4,128)S(1)} %copy-done.20), kind=kOutput, calls=%fused_computation.48 | convolution fusion | flops 270139392 | bytes 295424 | tf_op jit(solution)/shard_map/der,des->drs/dot_general | solution.py:315
  11.8 1.3 %fusion.67 = f32[4,256,256]{2,1,0:T(8,128)S(1)} fusion(bf16[4,256,256]{2,1,0:T(8,128)(2,1)} %fusion.17, bf16[4,256,256]{2,1,0:T(8,128)(2,1)S(1)} %copy-done.1), kind=kOutput, calls=%fused_computation.164 | convolution fusion | flops 134217728 | bytes 2097152 | tf_op jit(solution)/shard_map/drs,dsh->drh/dot_general | solution.py:322
  13.1 1.3 fusion.15
  14.4 1.3 %fusion.24 = (bf16[4,256,256]{2,1,0:T(8,128)(2,1)S(1)}, f32[4,256,256]{2,1,0:T(8,128)}) fusion(bf16[4,256,256]{2,1,0:T(8,128)(2,1)S(1)} %copy-done.1, bf16[4,256,256]{2,1,0:T(8,128)(2,1)S(1)} %fusion.15, bf16[256,256]{1,0:T(8,128)(2,1)S(1)} %copy-done), kind=kOutput, calls=%fused_computation.55 | convolution fusion | flops 136052736 | bytes 2752512 | tf_op jit(solution)/shard_map/drh,hk->drk/dot_general | solution.py:326
  15.9 4.7 %collective-permute-start.1 = (bf16[4,64,256]{2,1,0:T(8,128)(2,1)S(1)}, bf16[4,64,256]{2,1,0:T(8,128)(2,1)S(1)}, u32[]{:S(2)}, u32[]{:S(2)}) collective-permute-start(bf16[4,64,256]{2,1,0:T(8,128)(2,1)S(1)} %get-tuple-element.36), channel_id=1, source_target_pairs={{0,24},{8,0},{16,8},{24,16},{1,25},{9,1},{17,9},{25,17},{2,26},{10... | collective-permute-start | bytes 393224 | tf_op jit(solution)/shard_map/ppermute | solution.py:104
  21.3 1.0 collective-permute-start.3
  22.3 1.7 %collective-permute-done.1 = bf16[4,64,256]{2,1,0:T(8,128)(2,1)S(1)} collective-permute-done((bf16[4,64,256]{2,1,0:T(8,128)(2,1)S(1)}, bf16[4,64,256]{2,1,0:T(8,128)(2,1)S(1)}, u32[]{:S(2)}, u32[]{:S(2)}) %collective-permute-start.1) | collective-permute-done | bytes 131104 | tf_op jit(solution)/shard_map/ppermute | solution.py:104
  24.0 9.6 %collective-permute-done.2 = bf16[4,64,256]{2,1,0:T(8,128)(2,1)S(1)} collective-permute-done((bf16[4,64,256]{2,1,0:T(8,128)(2,1)S(1)}, bf16[4,64,256]{2,1,0:T(8,128)(2,1)S(1)}, u32[]{:S(2)}, u32[]{:S(2)}) %collective-permute-start.2) | collective-permute-done | bytes 131104 | tf_op jit(solution)/shard_map/ppermute | solution.py:104
  34.5 1.1 convolution_convert_fusion.1
  35.6 2.0 %reshape.240 = bf16[8,128,4,64]{3,2,1,0:T(4,128)(2,1)S(1)} reshape(bf16[1024,256]{1,0:T(8,128)(2,1)} %convolution_convert_fusion.1) | data formatting | bytes 1048576 | tf_op jit(solution)/shard_map/reshape | solution.py:233
  37.6 1.2 copy.30
  38.8 2.0 %convolution_convert_fusion.2 = bf16[1024,256]{1,0:T(8,128)(2,1)} fusion(bf16[1024,256]{1,0:T(8,128)(2,1)S(1)} %bitcast.197, bf16[256,256]{1,0:T(8,128)(2,1)} %param.17), kind=kOutput, calls=%fused_computation.39 | convolution fusion | flops 134479872 | bytes 1179648 | tf_op jit(solution)/shard_map/dot_general | solution.py:230
  40.8 2.0 %reshape.239 = bf16[8,128,4,64]{3,2,1,0:T(4,128)(2,1)S(1)} reshape(bf16[1024,256]{1,0:T(8,128)(2,1)} %convolution_convert_fusion.2) | data formatting | bytes 1048576 | tf_op jit(solution)/shard_map/reshape | solution.py:233
  42.9 1.2 copy.36
  44.1 1.1 convolution_convert_fusion
  45.2 2.0 %reshape.238 = bf16[8,128,4,64]{3,2,1,0:T(4,128)(2,1)S(1)} reshape(bf16[1024,256]{1,0:T(8,128)(2,1)} %convolution_convert_fusion) | data formatting | bytes 1048576 | tf_op jit(solution)/shard_map/reshape | solution.py:233
  47.2 1.8 %fusion.30 = f32[8,4,128,128]{3,2,1,0:T(8,128)} fusion(bf16[8,128,4,64]{1,3,2,0:T(8,128)(2,1)S(1)} %copy.35, bf16[8,128,4,64]{3,2,1,0:T(4,128)(2,1)S(1)} %reshape.238), kind=kOutput, calls=%fused_computation.62 | convolution fusion | flops 67108864 | bytes 3145728 | tf_op jit(solution)/shard_map/gihd,gjhd->ghij/dot_general | solution.py:244
  49.0 3.4 %fusion.66 = (f32[8,4,128]{2,1,0:T(4,128)S(1)}, f32[8,4,128,128]{2,3,1,0:T(8,128)}) fusion(pred[128,128]{0,1:T(8,128)(4,1)} %compare_and_fusion, bf16[8,128,4,64]{1,3,2,0:T(8,128)(2,1)} %copy.30, bf16[8,128,4,64]{1,3,2,0:T(8,128)(2,1)} %copy.36), kind=kOutput, calls=%fused_computation.163 | convolution fusion | flops 69206144 | bytes 3178496 | tf_op jit(solution)/shard_map/sub | solution.py:249
  52.4 2.6 %fusion.20 = bf16[8,128,4,64]{1,3,2,0:T(8,128)(2,1)S(1)} fusion(bf16[8,128,4,64]{1,3,2,0:T(8,128)(2,1)S(1)} %copy.35, f32[8,4,128,128]{2,3,1,0:T(8,128)} %get-tuple-element.44, f32[8,4,128]{2,1,0:T(4,128)S(1)} %get-tuple-element.43), kind=kOutput, calls=%fused_computation.47 | convolution fusion | flops 68419584 | bytes 3162112 | tf_op jit(solution)/shard_map/ghij,gihd->gjhd/dot_general | solution.py:244
  56.3 0.8 fusion.19
  61.3 0.9 collective-permute-start.4
  62.1 2.0 %collective-permute-start.5 = (bf16[4,64,256]{2,1,0:T(8,128)(2,1)S(1)}, bf16[4,64,256]{2,1,0:T(8,128)(2,1)S(1)}, u32[]{:S(2)}, u32[]{:S(2)}) collective-permute-start(bf16[4,64,256]{2,1,0:T(8,128)(2,1)S(1)} %get-tuple-element.27), channel_id=1, source_target_pairs={{0,16},{8,24},{16,0},{24,8},{1,17},{9,25},{17,1},{25,9},{2,18},{10... | collective-permute-start | bytes 393224 | tf_op jit(solution)/shard_map/ppermute | solution.py:104
  64.1 1.9 %collective-permute-start.6 = (bf16[4,64,256]{2,1,0:T(8,128)(2,1)S(1)}, bf16[4,64,256]{2,1,0:T(8,128)(2,1)S(1)}, u32[]{:S(2)}, u32[]{:S(2)}) collective-permute-start(bf16[4,64,256]{2,1,0:T(8,128)(2,1)S(1)} %get-tuple-element.25), channel_id=1, source_target_pairs={{0,8},{8,16},{16,24},{24,0},{1,9},{9,17},{17,25},{25,1},{2,10},{10... | collective-permute-start | bytes 393224 | tf_op jit(solution)/shard_map/ppermute | solution.py:104
  66.8 9.4 %collective-permute-done.5 = bf16[4,64,256]{2,1,0:T(8,128)(2,1)S(1)} collective-permute-done((bf16[4,64,256]{2,1,0:T(8,128)(2,1)S(1)}, bf16[4,64,256]{2,1,0:T(8,128)(2,1)S(1)}, u32[]{:S(2)}, u32[]{:S(2)}) %collective-permute-start.5) | collective-permute-done | bytes 131104 | tf_op jit(solution)/shard_map/ppermute | solution.py:104
  78.5 0.9 constant_dynamic-slice_fusion.4
  79.6 1.8 %collective-permute-done.8 = f32[131072]{0:T(1024)S(1)} collective-permute-done((f32[131072]{0:T(1024)S(1)}, f32[131072]{0:T(1024)S(1)}, u32[]{:S(2)}, u32[]{:S(2)}) %collective-permute-start.8) | collective-permute-done | bytes 524320 | tf_op jit(solution)/shard_map/ppermute | solution.py:33
  82.1 1.6 %collective-permute-start.10 = (f32[32768]{0:T(1024)S(1)}, f32[32768]{0:T(1024)S(1)}, u32[]{:S(2)}, u32[]{:S(2)}) collective-permute-start(f32[32768]{0:T(1024)S(1)} %bitcast.241), channel_id=1, source_target_pairs={{0,4},{1,5},{2,6},{3,7},{4,0},{5,1},{6,2},{7,3},{8,12},{9,13},{10,... | collective-permute-start | bytes 393224 | tf_op jit(solution)/shard_map/ppermute | solution.py:33
  83.7 1.4 %collective-permute-start.11 = (f32[32768]{0:T(1024)S(1)}, f32[32768]{0:T(1024)S(1)}, u32[]{:S(2)}, u32[]{:S(2)}) collective-permute-start(f32[32768]{0:T(1024)S(1)} %bitcast.240), channel_id=1, source_target_pairs={{0,6},{1,7},{2,0},{3,1},{4,2},{5,3},{6,4},{7,5},{8,14},{9,15},{10,... | collective-permute-start | bytes 393224 | tf_op jit(solution)/shard_map/ppermute | solution.py:33
  85.7 2.0 %collective-permute-done.10 = f32[32768]{0:T(1024)S(1)} collective-permute-done((f32[32768]{0:T(1024)S(1)}, f32[32768]{0:T(1024)S(1)}, u32[]{:S(2)}, u32[]{:S(2)}) %collective-permute-start.10) | collective-permute-done | bytes 131104 | tf_op jit(solution)/shard_map/ppermute | solution.py:33
  87.7 2.4 %collective-permute-done.11 = f32[32768]{0:T(1024)S(1)} collective-permute-done((f32[32768]{0:T(1024)S(1)}, f32[32768]{0:T(1024)S(1)}, u32[]{:S(2)}, u32[]{:S(2)}) %collective-permute-start.11) | collective-permute-done | bytes 131104 | tf_op jit(solution)/shard_map/ppermute | solution.py:33
  90.1 1.6 %collective-permute-done.9 = f32[32768]{0:T(1024)S(1)} collective-permute-done((f32[32768]{0:T(1024)S(1)}, f32[32768]{0:T(1024)S(1)}, u32[]{:S(2)}, u32[]{:S(2)}) %collective-permute-start.9) | collective-permute-done | bytes 131104 | tf_op jit(solution)/shard_map/ppermute | solution.py:33
  92.6 1.9 %collective-permute-start.14 = (f32[32768]{0:T(1024)S(1)}, f32[32768]{0:T(1024)S(1)}, u32[]{:S(2)}, u32[]{:S(2)}) collective-permute-start(f32[32768]{0:T(1024)S(1)} %add_add_fusion), channel_id=1, source_target_pairs={{0,8},{8,16},{16,24},{24,0},{1,9},{9,17},{17,25},{25,1},{2,10},{10... | collective-permute-start | bytes 393224 | tf_op jit(solution)/shard_map/ppermute | solution.py:54
  94.9 3.0 %collective-permute-done.12 = f32[32768]{0:T(1024)S(1)} collective-permute-done((f32[32768]{0:T(1024)S(1)}, f32[32768]{0:T(1024)S(1)}, u32[]{:S(2)}, u32[]{:S(2)}) %collective-permute-start.12) | collective-permute-done | bytes 131104 | tf_op jit(solution)/shard_map/ppermute | solution.py:54
  97.9 6.1 %collective-permute-done.13 = f32[32768]{0:T(1024)S(1)} collective-permute-done((f32[32768]{0:T(1024)S(1)}, f32[32768]{0:T(1024)S(1)}, u32[]{:S(2)}, u32[]{:S(2)}) %collective-permute-start.13) | collective-permute-done | bytes 131104 | tf_op jit(solution)/shard_map/ppermute | solution.py:54
  104.7 2.8 %stack.129 = f32[8,32768]{1,0:T(8,128)S(1)} concatenate(f32[1,32768]{1,0:T(1,128)S(1)} %bitcast.217, f32[1,32768]{1,0:T(1,128)S(1)} %bitcast.226, f32[1,32768]{1,0:T(1,128)} %bitcast.230, f32[1,32768]{1,0:T(1,128)} %bitcast.234, f32[1,32768]{1,0:T(1,128)S(1)} %bitcast.218, f32[1,32768]{1,0:T(1,128)S(1)} %bitcast.227, f32[1,32768]{1,0:T(1,128)} %bitcast.231, f32[1,32768]{1,0:T(1,128)} %bitcast.235), dimensions={0} | concatenate | bytes 2097152 | tf_op jit(solution)/shard_map/stack | solution.py:39
  107.9 2.0 %collective-permute-start.15 = (f32[32768]{0:T(1024)S(1)}, f32[32768]{0:T(1024)S(1)}, u32[]{:S(2)}, u32[]{:S(2)}) collective-permute-start(f32[32768]{0:T(1024)S(1)} %bitcast.214), channel_id=1, source_target_pairs={{0,6},{1,7},{2,0},{3,1},{4,2},{5,3},{6,4},{7,5},{8,14},{9,15},{10,... | collective-permute-start | bytes 393224 | tf_op jit(solution)/shard_map/ppermute | solution.py:46
  109.9 1.0 collective-permute-start.16
  111.5 2.2 %convolution_convert_fusion.6 = bf16[4,128,256]{2,1,0:T(8,128)(2,1)} fusion(bf16[4,256,128]{2,1,0:T(8,128)(2,1)} %copy-done.10, f32[4,256,256]{2,1,0:T(8,128)S(1)} %convolution_multiply_fusion), kind=kOutput, calls=%fused_computation.49 | convolution fusion | flops 402784256 | bytes 1572864 | tf_op jit(solution)/shard_map/drs,drh->dsh/dot_general | solution.py:349
  113.9 3.5 %collective-permute-done.16 = f32[32768]{0:T(1024)S(1)} collective-permute-done((f32[32768]{0:T(1024)S(1)}, f32[32768]{0:T(1024)S(1)}, u32[]{:S(2)}, u32[]{:S(2)}) %collective-permute-start.16) | collective-permute-done | bytes 131104 | tf_op jit(solution)/shard_map/ppermute | solution.py:46
  118.0 2.9 %stack.133 = f32[8,32768]{1,0:T(8,128)S(1)} concatenate(f32[1,32768]{1,0:T(1,128)S(1)} %dynamic-slice_add_fusion, f32[1,32768]{1,0:T(1,128)S(1)} %bitcast.224, f32[1,32768]{1,0:T(1,128)} %bitcast.228, f32[1,32768]{1,0:T(1,128)} %bitcast.232, f32[1,32768]{1,0:T(1,128)S(1)} %dynamic-slice_add_fusion, f32[1,32768]{1,0:T(1,128)S(1)} %bitcast.225, f32[1,32768]{1,0:T(1,128)} %bitcast.229, ...), dimensions={0} | concatenate | bytes 2097152 | tf_op jit(solution)/shard_map/stack | solution.py:39
  121.2 0.9 convolution_add_fusion
  122.1 2.2 %convolution_add_fusion.4 = f32[4,256,256]{2,1,0:T(8,128)} fusion(f32[4,256,256]{2,1,0:T(8,128)S(1)} %convolution_add_fusion, bf16[4,128,256]{2,1,0:T(8,128)(2,1)} %collective-permute-done.7, s32[4,128]{1,0:T(4,128)S(1)} %copy-done.19, pred[4,128]{1,0:T(4,128)(4,1)S(1)} %iota_compare_fusion.12), kind=kOutput, calls=%fused_computation.29 | convolution fusion | flops 67633152 | bytes 2361856 | tf_op jit(solution)/shard_map/dsn,dsh->dnh/dot_general | solution.py:364
  124.9 3.8 %fusion.29 = f32[2,131072]{1,0:T(2,128)S(1)} fusion(s32[]{:T(128)S(6)} %select_n.184, f32[1,131072]{1,0:T(1,128)S(1)} %bitcast.210, f32[1,131072]{1,0:T(1,128)S(1)} %bitcast.223), kind=kLoop, calls=%fused_computation.60 | loop fusion | flops 786432 | bytes 2097156 | tf_op jit(solution)/shard_map/stack | solution.py:39
  128.7 0.9 slice.66
  129.6 1.0 fusion.65
  (125 shorter events, 19.2 us)
Async XLA Ops:
  0.6 13.8 %copy-start = (bf16[256,256]{1,0:T(8,128)(2,1)S(1)}, bf16[256,256]{1,0:T(8,128)(2,1)}, u32[]{:S(2)}) copy-start(bf16[256,256]{1,0:T(8,128)(2,1)} %param.15) | copy-start | bytes 393220
  3.5 9.6 %collective-permute-start = (bf16[4,128,256]{2,1,0:T(8,128)(2,1)}, bf16[4,128,256]{2,1,0:T(8,128)(2,1)}, u32[]{:S(2)}, u32[]{:S(2)}) collective-permute-start(bf16[4,128,256]{2,1,0:T(8,128)(2,1)} %convolution_convert_fusion.7), channel_id=1, source_target_pairs={{0,1},{1,2},{2,3},{3,4},{4,5},{5,6},{6,7},{7,0},{8,9},{9,10},{10,1... | collective-permute-start | bytes 786440 | tf_op jit(solution)/shard_map/ppermute | solution.py:12
  5.2 3.1 %copy-start.18 = (s32[4,1024]{1,0:T(4,128)S(1)}, s32[4,1024]{1,0:T(4,128)}, u32[]{:S(2)}) copy-start(s32[4,1024]{1,0:T(4,128)} %param.12) | copy-start | bytes 49156
  5.2 3.1 %copy-start.20 = (s32[4,1024]{1,0:T(4,128)S(1)}, s32[4,1024]{1,0:T(4,128)}, u32[]{:S(2)}) copy-start(s32[4,1024]{1,0:T(4,128)} %param.11) | copy-start | bytes 49156
  8.3 1.4 %copy-start.3 = (bf16[16,1,1,64,256]{4,3,2,1,0:T(8,128)(2,1)S(1)}, bf16[16,1,1,64,256]{4,3,2,1,0:T(8,128)(2,1)}, u32[]{:S(2)}) copy-start(bf16[16,1,1,64,256]{4,3,2,1,0:T(8,128)(2,1)} %param.19) | copy-start | bytes 1572868
  9.7 3.5 %copy-start.10 = (bf16[4,256,128]{2,1,0:T(8,128)(2,1)}, bf16[4,256,128]{2,1,0:T(8,128)(2,1)S(1)}, u32[]{:S(2)}) copy-start(bf16[4,256,128]{2,1,0:T(8,128)(2,1)S(1)} %fusion.21) | copy-start | bytes 786436
  10.5 1.2 copy-start.1
  14.4 1.4 %copy-start.4 = (bf16[4,256,256]{2,1,0:T(8,128)(2,1)}, bf16[4,256,256]{2,1,0:T(8,128)(2,1)S(1)}, u32[]{:S(2)}) copy-start(bf16[4,256,256]{2,1,0:T(8,128)(2,1)S(1)} %fusion.15) | copy-start | bytes 1572868
  15.9 8.0 %collective-permute-start.1 = (bf16[4,64,256]{2,1,0:T(8,128)(2,1)S(1)}, bf16[4,64,256]{2,1,0:T(8,128)(2,1)S(1)}, u32[]{:S(2)}, u32[]{:S(2)}) collective-permute-start(bf16[4,64,256]{2,1,0:T(8,128)(2,1)S(1)} %get-tuple-element.36), channel_id=1, source_target_pairs={{0,24},{8,0},{16,8},{24,16},{1,25},{9,1},{17,9},{25,17},{2,26},{10... | collective-permute-start | bytes 393224 | tf_op jit(solution)/shard_map/ppermute | solution.py:104
  21.3 12.2 %collective-permute-start.2 = (bf16[4,64,256]{2,1,0:T(8,128)(2,1)S(1)}, bf16[4,64,256]{2,1,0:T(8,128)(2,1)S(1)}, u32[]{:S(2)}, u32[]{:S(2)}) collective-permute-start(bf16[4,64,256]{2,1,0:T(8,128)(2,1)S(1)} %get-tuple-element.35), channel_id=1, source_target_pairs={{0,16},{8,24},{16,0},{24,8},{1,17},{9,25},{17,1},{25,9},{2,18},{10... | collective-permute-start | bytes 393224 | tf_op jit(solution)/shard_map/ppermute | solution.py:104
  21.3 12.3 %collective-permute-start.3 = (bf16[4,64,256]{2,1,0:T(8,128)(2,1)S(1)}, bf16[4,64,256]{2,1,0:T(8,128)(2,1)S(1)}, u32[]{:S(2)}, u32[]{:S(2)}) collective-permute-start(bf16[4,64,256]{2,1,0:T(8,128)(2,1)S(1)} %get-tuple-element.33), channel_id=1, source_target_pairs={{0,8},{8,16},{16,24},{24,0},{1,9},{9,17},{17,25},{25,1},{2,10},{10... | collective-permute-start | bytes 393224 | tf_op jit(solution)/shard_map/ppermute | solution.py:104
  33.6 0.9 copy-start.16
  38.8 5.3 %copy-start.11 = (bf16[256,256]{1,0:T(8,128)(2,1)S(1)}, bf16[256,256]{1,0:T(8,128)(2,1)}, u32[]{:S(2)}) copy-start(bf16[256,256]{1,0:T(8,128)(2,1)} %param.18) | copy-start | bytes 393220
  52.4 2.6 %copy-start.2 = (f32[8,4,128,128]{3,2,1,0:T(8,128)S(1)}, f32[8,4,128,128]{3,2,1,0:T(8,128)}, u32[]{:S(2)}) copy-start(f32[8,4,128,128]{3,2,1,0:T(8,128)} %fusion.30) | copy-start | bytes 6291460
  52.4 2.9 %copy-start.21 = (f32[8,4,128,128]{2,3,1,0:T(8,128)S(1)}, f32[8,4,128,128]{2,3,1,0:T(8,128)}, u32[]{:S(2)}) copy-start(f32[8,4,128,128]{2,3,1,0:T(8,128)} %get-tuple-element.44) | copy-start | bytes 6291460
  55.2 1.0 copy-start.6
  56.3 1.0 copy-start.7
  59.3 0.9 copy-start.17
  61.3 5.6 %collective-permute-start.4 = (bf16[4,64,256]{2,1,0:T(8,128)(2,1)S(1)}, bf16[4,64,256]{2,1,0:T(8,128)(2,1)S(1)}, u32[]{:S(2)}, u32[]{:S(2)}) collective-permute-start(bf16[4,64,256]{2,1,0:T(8,128)(2,1)S(1)} %get-tuple-element.28), channel_id=1, source_target_pairs={{0,24},{8,0},{16,8},{24,16},{1,25},{9,1},{17,9},{25,17},{2,26},{10... | collective-permute-start | bytes 393224 | tf_op jit(solution)/shard_map/ppermute | solution.py:104
  62.1 14.1 %collective-permute-start.5 = (bf16[4,64,256]{2,1,0:T(8,128)(2,1)S(1)}, bf16[4,64,256]{2,1,0:T(8,128)(2,1)S(1)}, u32[]{:S(2)}, u32[]{:S(2)}) collective-permute-start(bf16[4,64,256]{2,1,0:T(8,128)(2,1)S(1)} %get-tuple-element.27), channel_id=1, source_target_pairs={{0,16},{8,24},{16,0},{24,8},{1,17},{9,25},{17,1},{25,9},{2,18},{10... | collective-permute-start | bytes 393224 | tf_op jit(solution)/shard_map/ppermute | solution.py:104
  64.1 12.3 %copy-start.9 = (f32[4,256,256]{2,1,0:T(8,128)S(1)}, f32[4,256,256]{2,1,0:T(8,128)}, u32[]{:S(2)}) copy-start(f32[4,256,256]{2,1,0:T(8,128)} %get-tuple-element.42) | copy-start | bytes 3145732
  64.1 12.1 %collective-permute-start.6 = (bf16[4,64,256]{2,1,0:T(8,128)(2,1)S(1)}, bf16[4,64,256]{2,1,0:T(8,128)(2,1)S(1)}, u32[]{:S(2)}, u32[]{:S(2)}) collective-permute-start(bf16[4,64,256]{2,1,0:T(8,128)(2,1)S(1)} %get-tuple-element.25), channel_id=1, source_target_pairs={{0,8},{8,16},{16,24},{24,0},{1,9},{9,17},{17,25},{25,1},{2,10},{10... | collective-permute-start | bytes 393224 | tf_op jit(solution)/shard_map/ppermute | solution.py:104
  76.2 1.0 copy-start.5
  79.4 2.0 %collective-permute-start.8 = (f32[131072]{0:T(1024)S(1)}, f32[131072]{0:T(1024)S(1)}, u32[]{:S(2)}, u32[]{:S(2)}) collective-permute-start(f32[131072]{0:T(1024)S(1)} %bitcast.237), channel_id=1, source_target_pairs={{0,1},{1,0},{2,3},{3,2},{4,5},{5,4},{6,7},{7,6},{8,9},{9,8},{10,11... | collective-permute-start | bytes 1572872 | tf_op jit(solution)/shard_map/ppermute | solution.py:33
  82.1 5.6 %collective-permute-start.10 = (f32[32768]{0:T(1024)S(1)}, f32[32768]{0:T(1024)S(1)}, u32[]{:S(2)}, u32[]{:S(2)}) collective-permute-start(f32[32768]{0:T(1024)S(1)} %bitcast.241), channel_id=1, source_target_pairs={{0,4},{1,5},{2,6},{3,7},{4,0},{5,1},{6,2},{7,3},{8,12},{9,13},{10,... | collective-permute-start | bytes 393224 | tf_op jit(solution)/shard_map/ppermute | solution.py:33
  83.7 6.4 %collective-permute-start.11 = (f32[32768]{0:T(1024)S(1)}, f32[32768]{0:T(1024)S(1)}, u32[]{:S(2)}, u32[]{:S(2)}) collective-permute-start(f32[32768]{0:T(1024)S(1)} %bitcast.240), channel_id=1, source_target_pairs={{0,6},{1,7},{2,0},{3,1},{4,2},{5,3},{6,4},{7,5},{8,14},{9,15},{10,... | collective-permute-start | bytes 393224 | tf_op jit(solution)/shard_map/ppermute | solution.py:33
  85.2 6.6 %collective-permute-start.9 = (f32[32768]{0:T(1024)S(1)}, f32[32768]{0:T(1024)S(1)}, u32[]{:S(2)}, u32[]{:S(2)}) collective-permute-start(f32[32768]{0:T(1024)S(1)} %bitcast.239), channel_id=1, source_target_pairs={{0,2},{1,3},{2,4},{3,5},{4,6},{5,7},{6,0},{7,1},{8,10},{9,11},{10,... | collective-permute-start | bytes 393224 | tf_op jit(solution)/shard_map/ppermute | solution.py:33
  91.8 6.2 %collective-permute-start.12 = (f32[32768]{0:T(1024)S(1)}, f32[32768]{0:T(1024)S(1)}, u32[]{:S(2)}, u32[]{:S(2)}) collective-permute-start(f32[32768]{0:T(1024)S(1)} %add_add_fusion), channel_id=1, source_target_pairs={{0,24},{8,0},{16,8},{24,16},{1,25},{9,1},{17,9},{25,17},{2,26},{10... | collective-permute-start | bytes 393224 | tf_op jit(solution)/shard_map/ppermute | solution.py:54
  91.8 12.2 %collective-permute-start.13 = (f32[32768]{0:T(1024)S(1)}, f32[32768]{0:T(1024)S(1)}, u32[]{:S(2)}, u32[]{:S(2)}) collective-permute-start(f32[32768]{0:T(1024)S(1)} %add_add_fusion), channel_id=1, source_target_pairs={{0,16},{8,24},{16,0},{24,8},{1,17},{9,25},{17,1},{25,9},{2,18},{10... | collective-permute-start | bytes 393224 | tf_op jit(solution)/shard_map/ppermute | solution.py:54
  92.6 11.4 %collective-permute-start.14 = (f32[32768]{0:T(1024)S(1)}, f32[32768]{0:T(1024)S(1)}, u32[]{:S(2)}, u32[]{:S(2)}) collective-permute-start(f32[32768]{0:T(1024)S(1)} %add_add_fusion), channel_id=1, source_target_pairs={{0,8},{8,16},{16,24},{24,0},{1,9},{9,17},{17,25},{25,1},{2,10},{10... | collective-permute-start | bytes 393224 | tf_op jit(solution)/shard_map/ppermute | solution.py:54
  104.0 0.7 copy-start.13
  104.0 0.7 copy-start.15
  107.9 5.9 %collective-permute-start.15 = (f32[32768]{0:T(1024)S(1)}, f32[32768]{0:T(1024)S(1)}, u32[]{:S(2)}, u32[]{:S(2)}) collective-permute-start(f32[32768]{0:T(1024)S(1)} %bitcast.214), channel_id=1, source_target_pairs={{0,6},{1,7},{2,0},{3,1},{4,2},{5,3},{6,4},{7,5},{8,14},{9,15},{10,... | collective-permute-start | bytes 393224 | tf_op jit(solution)/shard_map/ppermute | solution.py:46
  109.9 7.4 %collective-permute-start.16 = (f32[32768]{0:T(1024)S(1)}, f32[32768]{0:T(1024)S(1)}, u32[]{:S(2)}, u32[]{:S(2)}) collective-permute-start(f32[32768]{0:T(1024)S(1)} %bitcast.215), channel_id=1, source_target_pairs={{0,4},{1,5},{2,6},{3,7},{4,0},{5,1},{6,2},{7,3},{8,12},{9,13},{10,... | collective-permute-start | bytes 393224 | tf_op jit(solution)/shard_map/ppermute | solution.py:46
  110.9 6.4 %collective-permute-start.17 = (f32[32768]{0:T(1024)S(1)}, f32[32768]{0:T(1024)S(1)}, u32[]{:S(2)}, u32[]{:S(2)}) collective-permute-start(f32[32768]{0:T(1024)S(1)} %bitcast.216), channel_id=1, source_target_pairs={{0,2},{1,3},{2,4},{3,5},{4,6},{5,7},{6,0},{7,1},{8,10},{9,11},{10,... | collective-permute-start | bytes 393224 | tf_op jit(solution)/shard_map/ppermute | solution.py:46
  113.7 8.4 %collective-permute-start.7 = (bf16[4,128,256]{2,1,0:T(8,128)(2,1)}, bf16[4,128,256]{2,1,0:T(8,128)(2,1)}, u32[]{:S(2)}, u32[]{:S(2)}) collective-permute-start(bf16[4,128,256]{2,1,0:T(8,128)(2,1)} %convolution_convert_fusion.6), channel_id=1, source_target_pairs={{0,7},{1,0},{2,1},{3,2},{4,3},{5,4},{6,5},{7,6},{8,15},{9,8},{10,9... | collective-permute-start | bytes 786440 | tf_op jit(solution)/shard_map/ppermute | solution.py:12
  117.3 0.7 copy-start.12
  117.4 0.7 copy-start.14
  118.0 3.2 %copy-start.8 = (bf16[4,256,256]{2,1,0:T(8,128)(2,1)S(1)}, bf16[4,256,256]{2,1,0:T(8,128)(2,1)}, u32[]{:S(2)}) copy-start(bf16[4,256,256]{2,1,0:T(8,128)(2,1)} %fusion.17) | copy-start | bytes 1572868
  121.1 1.1 copy-start.19
  121.1 3.8 %collective-permute-start.18 = (f32[131072]{0:T(1024)S(1)}, f32[131072]{0:T(1024)S(1)}, u32[]{:S(2)}, u32[]{:S(2)}) collective-permute-start(f32[131072]{0:T(1024)S(1)} %bitcast.236), channel_id=1, source_target_pairs={{0,1},{1,0},{2,3},{3,2},{4,5},{5,4},{6,7},{7,6},{8,9},{9,8},{10,11... | collective-permute-start | bytes 1572872 | tf_op jit(solution)/shard_map/ppermute | solution.py:46

commit v7 on v4

--- a/solution.py
+++ b/solution.py
@@ -237,6 +237,7 @@
     score_grad = (
         probs * (prob_grad - jnp.sum(prob_grad * probs, axis=-1, keepdims=True)) * scale_factor
     ).astype(jnp.bfloat16)
+    score_grad = lax.optimization_barrier(score_grad)
     query_grad = contract("ghij,gjhd->gihd", score_grad, key_rows).astype(jnp.bfloat16)
     key_grad = contract("ghij,gihd->gjhd", score_grad, queries).astype(jnp.bfloat16)
     query_flat = query_grad.reshape(-1, width)

time: 126 us -> 120 us (0.952)
  matrix products: 33.1 us -> 26.8 us
    dot_general x4, matrix products: 12.7 us -> 5.53 us  [contract(): return jnp.einsum(spec, left, right, preferred_element_type=jnp.float32)]
    unnamed x54 -> x64, local copies, waits for them, and re-layouts: 5.39 us -> 5.79 us
where the time goes in v7:
time: 120 us; the launch traced here: 118 us
  starting transfers between devices  31.2 us (26%)
  waiting for transfers between devices  27 us (22%)
  matrix products  26.8 us (22%)
  local copies, waits for them, and re-layouts  22.9 us (19%)
  other arithmetic  8.77 us (7%)
  between operations  1.57 us (1%)
    ppermute x6, starting transfers between devices, exchange(): lax.ppermute(send, axis, [(i, (i + shift) % count) for i in range(count)])  12.1 us
    ppermute x6, waiting for transfers between devices, exchange(): lax.ppermute(send, axis, [(i, (i + shift) % count) for i in range(count)])  11.9 us
    ppermute x7, waiting for transfers between devices, _scatter_step(): lax.ppermute(send, axis, _group_pairs(axis, stride, group, shift))  10.4 us
    ppermute x7, starting transfers between devices, _scatter_step(): lax.ppermute(send, axis, _group_pairs(axis, stride, group, shift))  9.47 us
    ppermute x7, starting transfers between devices, _gather_step(): lax.ppermute(flat, axis, _group_pairs(axis, stride, group, shift))  9.11 us
    unnamed x64, local copies, waits for them, and re-layouts  5.79 us
    dot_general x4, matrix products, contract(): return jnp.einsum(spec, left, right, preferred_element_type=jnp.float32)  5.53 us
    ppermute x7, waiting for transfers between devices, _gather_step(): lax.ppermute(flat, axis, _group_pairs(axis, stride, group, shift))  4.15 us
  transfers between devices with their start and end apart: 22, of which 16 were waited for; matrix products, arithmetic and copies ran while one was open for 14% of the time, Pallas kernels for 0%

profile of v7, /device:TPU:0, one launch (start us, length us, event | category | flops | bytes accessed | tf_op | source)
XLA Modules:
  0.0 118.2 jit_solution(5848766533430506226)
XLA Ops:
  2.0 2.1 %convolution_convert_fusion.7 = bf16[4,128,256]{2,1,0:T(8,128)(2,1)} fusion(bf16[4,256,256]{2,1,0:T(8,128)(2,1)} %param.12, s32[4,128]{1,0:T(4,128)} %param.15, pred[4,128]{1,0:T(4,128)(4,1)S(1)} %iota_compare_fusion.12), kind=kOutput, calls=%fused_computation.52 | convolution fusion | flops 67502080 | bytes 788992 | tf_op jit(solution)/shard_map/dsn,dnh->dsh/dot_general | solution.py:286
  4.6 1.2 %convert_reduce_fusion = f32[4,256]{1,0:T(4,128)S(1)} fusion(s32[4,1024]{1,0:T(4,128)} %param.14), kind=kLoop, calls=%fused_computation.8 | loop fusion | flops 4193280 | bytes 20480 | tf_op jit(solution)/shard_map/reduce_sum | solution.py:301
  5.8 2.4 %fusion.17 = bf16[4,256,256]{2,1,0:T(8,128)(2,1)S(1)} fusion(s32[4,1024]{1,0:T(4,128)} %param.13, s32[4,1024]{1,0:T(4,128)} %param.14), kind=kOutput, calls=%fused_computation.46 | convolution fusion | flops 539230208 | bytes 557056 | tf_op jit(solution)/shard_map/der,des->drs/dot_general | solution.py:295
  9.1 1.3 %fusion.21 = bf16[4,256,128]{2,1,0:T(8,128)(2,1)S(1)} fusion(s32[4,1024]{1,0:T(4,128)S(1)} %copy-done.20, s32[128]{0:T(128)S(1)} %iota_add_fusion, s32[4,1024]{1,0:T(4,128)S(1)} %copy-done.25), kind=kOutput, calls=%fused_computation.50 | convolution fusion | flops 270139392 | bytes 295424 | tf_op jit(solution)/shard_map/der,des->drs/dot_general | solution.py:298
  11.8 1.3 %fusion.15 = bf16[4,256,256]{2,1,0:T(8,128)(2,1)S(1)} fusion(f32[4,256,256]{2,1,0:T(8,128)S(1)} %fusion.75, bf16[4,256,128]{2,1,0:T(8,128)(2,1)S(1)} %fusion.21, bf16[4,128,256]{2,1,0:T(8,128)(2,1)} %collective-permute-done, bf16[4,256,256]{2,1,0:T(8,128)(2,1)S(1)} %copy-done.1, f32[4,256]{1,0:T(4,128)S(1)} %add_divide_fusion.1), kind=kOutput, calls=%fused_computation.38 | convolution fusion | flops 68419584 | bytes 2625536 | tf_op jit(solution)/shard_map/drs,dsh->drh/dot_general | solution.py:307
  13.1 1.3 %fusion.24 = (bf16[4,256,256]{2,1,0:T(8,128)(2,1)S(1)}, f32[4,256,256]{2,1,0:T(8,128)}) fusion(bf16[4,256,256]{2,1,0:T(8,128)(2,1)S(1)} %copy-done.1, bf16[4,256,256]{2,1,0:T(8,128)(2,1)S(1)} %fusion.15, bf16[256,256]{1,0:T(8,128)(2,1)S(1)} %copy-done), kind=kOutput, calls=%fused_computation.57 | convolution fusion | flops 136052736 | bytes 2752512 | tf_op jit(solution)/shard_map/drh,hk->drk/dot_general | solution.py:309
  15.4 2.3 %collective-permute-start.1 = (bf16[4,64,256]{2,1,0:T(8,128)(2,1)}, bf16[4,64,256]{2,1,0:T(8,128)(2,1)}, u32[]{:S(2)}, u32[]{:S(2)}) collective-permute-start(bf16[4,64,256]{2,1,0:T(8,128)(2,1)} %get-tuple-element.39), channel_id=1, source_target_pairs={{0,8},{8,16},{16,24},{24,0},{1,9},{9,17},{17,25},{25,1},{2,10},{10... | collective-permute-start | bytes 393224 | tf_op jit(solution)/shard_map/ppermute | solution.py:87
  17.7 2.6 %collective-permute-start.2 = (bf16[4,64,256]{2,1,0:T(8,128)(2,1)}, bf16[4,64,256]{2,1,0:T(8,128)(2,1)}, u32[]{:S(2)}, u32[]{:S(2)}) collective-permute-start(bf16[4,64,256]{2,1,0:T(8,128)(2,1)} %get-tuple-element.38), channel_id=1, source_target_pairs={{0,16},{8,24},{16,0},{24,8},{1,17},{9,25},{17,1},{25,9},{2,18},{10... | collective-permute-start | bytes 393224 | tf_op jit(solution)/shard_map/ppermute | solution.py:87
  20.3 1.3 %collective-permute-start.3 = (bf16[4,64,256]{2,1,0:T(8,128)(2,1)}, bf16[4,64,256]{2,1,0:T(8,128)(2,1)}, u32[]{:S(2)}, u32[]{:S(2)}) collective-permute-start(bf16[4,64,256]{2,1,0:T(8,128)(2,1)} %get-tuple-element.37), channel_id=1, source_target_pairs={{0,24},{8,0},{16,8},{24,16},{1,25},{9,1},{17,9},{25,17},{2,26},{10... | collective-permute-start | bytes 393224 | tf_op jit(solution)/shard_map/ppermute | solution.py:87
  23.4 1.6 %copy.26 = f32[64,16,256]{2,1,0:T(8,128)} copy(f32[64,16,256]{2,0,1:T(8,128)S(1)} %bitcast_convert_fusion) | data formatting | bytes 2097152 | tf_op jit(solution)/shard_map/convert_element_type | solution.py:258
  25.1 5.0 %collective-permute-done.2 = bf16[4,64,256]{2,1,0:T(8,128)(2,1)} collective-permute-done((bf16[4,64,256]{2,1,0:T(8,128)(2,1)}, bf16[4,64,256]{2,1,0:T(8,128)(2,1)}, u32[]{:S(2)}, u32[]{:S(2)}) %collective-permute-start.2) | collective-permute-done | bytes 131104 | tf_op jit(solution)/shard_map/ppermute | solution.py:87
  30.0 1.1 pad_maximum_fusion.4
  33.9 1.3 %convolution_convert_fusion.2 = bf16[1024,256]{1,0:T(8,128)(2,1)S(1)} fusion(bf16[1024,256]{1,0:T(8,128)(2,1)S(1)} %bitcast.201, bf16[256,256]{1,0:T(8,128)(2,1)} %param.19), kind=kOutput, calls=%fused_computation.41 | convolution fusion | flops 134479872 | bytes 1179648 | tf_op jit(solution)/shard_map/dot_general | solution.py:213
  35.7 1.2 %copy.36 = bf16[8,128,4,64]{1,3,2,0:T(8,128)(2,1)} copy(bf16[8,128,4,64]{3,2,1,0:T(4,128)(2,1)S(1)} %reshape.519) | data formatting | bytes 1048576 | tf_op jit(solution)/shard_map/reshape | solution.py:216
  36.9 1.2 %convolution_convert_fusion = bf16[1024,256]{1,0:T(8,128)(2,1)S(1)} fusion(bf16[1024,256]{1,0:T(8,128)(2,1)S(1)} %bitcast.202, bf16[256,256]{1,0:T(8,128)(2,1)} %param.20), kind=kOutput, calls=%fused_computation.39 | convolution fusion | flops 134479872 | bytes 1179648 | tf_op jit(solution)/shard_map/dot_general | solution.py:213
  38.5 1.8 %fusion.27 = f32[8,4,128,128]{3,2,1,0:T(8,128)} fusion(bf16[8,128,4,64]{1,3,2,0:T(8,128)(2,1)S(1)} %copy.35, bf16[8,128,4,64]{3,2,1,0:T(4,128)(2,1)S(1)} %reshape.518), kind=kOutput, calls=%fused_computation.64 | convolution fusion | flops 67108864 | bytes 3145728 | tf_op jit(solution)/shard_map/gihd,gjhd->ghij/dot_general | solution.py:227
  40.2 3.5 %fusion.74 = (f32[8,4,128]{2,1,0:T(4,128)}, f32[8,4,128,128]{2,3,1,0:T(8,128)}) fusion(pred[128,128]{0,1:T(8,128)(4,1)} %compare_and_fusion, bf16[8,128,4,64]{1,3,2,0:T(8,128)(2,1)S(1)} %copy.30, bf16[8,128,4,64]{1,3,2,0:T(8,128)(2,1)S(1)} %copy-done.9), kind=kOutput, calls=%fused_computation.210 | convolution fusion | flops 69206144 | bytes 3178496 | tf_op jit(solution)/shard_map/sub | solution.py:232
  43.8 2.6 %fusion.20 = bf16[8,128,4,64]{1,3,2,0:T(8,128)(2,1)S(1)} fusion(bf16[8,128,4,64]{1,3,2,0:T(8,128)(2,1)S(1)} %copy.35, f32[8,4,128,128]{2,3,1,0:T(8,128)} %get-tuple-element.53, f32[8,4,128]{2,1,0:T(4,128)} %get-tuple-element.52), kind=kOutput, calls=%fused_computation.49 | convolution fusion | flops 68419584 | bytes 3162112 | tf_op jit(solution)/shard_map/ghij,gihd->gjhd/dot_general | solution.py:227
  52.9 3.4 %collective-permute-start.4 = (bf16[4,64,256]{2,1,0:T(8,128)(2,1)S(1)}, bf16[4,64,256]{2,1,0:T(8,128)(2,1)S(1)}, u32[]{:S(2)}, u32[]{:S(2)}) collective-permute-start(bf16[4,64,256]{2,1,0:T(8,128)(2,1)S(1)} %get-tuple-element.27), channel_id=1, source_target_pairs={{0,8},{8,16},{16,24},{24,0},{1,9},{9,17},{17,25},{25,1},{2,10},{10... | collective-permute-start | bytes 393224 | tf_op jit(solution)/shard_map/ppermute | solution.py:87
  56.3 1.6 %collective-permute-start.5 = (bf16[4,64,256]{2,1,0:T(8,128)(2,1)S(1)}, bf16[4,64,256]{2,1,0:T(8,128)(2,1)S(1)}, u32[]{:S(2)}, u32[]{:S(2)}) collective-permute-start(bf16[4,64,256]{2,1,0:T(8,128)(2,1)S(1)} %get-tuple-element.26), channel_id=1, source_target_pairs={{0,16},{8,24},{16,0},{24,8},{1,17},{9,25},{17,1},{25,9},{2,18},{10... | collective-permute-start | bytes 393224 | tf_op jit(solution)/shard_map/ppermute | solution.py:87
  59.9 1.8 %collective-permute-done.4 = bf16[4,64,256]{2,1,0:T(8,128)(2,1)S(1)} collective-permute-done((bf16[4,64,256]{2,1,0:T(8,128)(2,1)S(1)}, bf16[4,64,256]{2,1,0:T(8,128)(2,1)S(1)}, u32[]{:S(2)}, u32[]{:S(2)}) %collective-permute-start.4) | collective-permute-done | bytes 131104 | tf_op jit(solution)/shard_map/ppermute | solution.py:87
  61.7 5.1 %collective-permute-done.5 = bf16[4,64,256]{2,1,0:T(8,128)(2,1)S(1)} collective-permute-done((bf16[4,64,256]{2,1,0:T(8,128)(2,1)S(1)}, bf16[4,64,256]{2,1,0:T(8,128)(2,1)S(1)}, u32[]{:S(2)}, u32[]{:S(2)}) %collective-permute-start.5) | collective-permute-done | bytes 131104 | tf_op jit(solution)/shard_map/ppermute | solution.py:87
  69.8 0.9 constant_dynamic-slice_fusion.8
  70.9 1.8 %collective-permute-done.8 = f32[131072]{0:T(1024)S(1)} collective-permute-done((f32[131072]{0:T(1024)S(1)}, f32[131072]{0:T(1024)S(1)}, u32[]{:S(2)}, u32[]{:S(2)}) %collective-permute-start.8) | collective-permute-done | bytes 524320 | tf_op jit(solution)/shard_map/ppermute | solution.py:33
  73.5 1.6 %collective-permute-start.10 = (f32[32768]{0:T(1024)S(1)}, f32[32768]{0:T(1024)S(1)}, u32[]{:S(2)}, u32[]{:S(2)}) collective-permute-start(f32[32768]{0:T(1024)S(1)} %bitcast.234), channel_id=1, source_target_pairs={{0,4},{1,5},{2,6},{3,7},{4,0},{5,1},{6,2},{7,3},{8,12},{9,13},{10,... | collective-permute-start | bytes 393224 | tf_op jit(solution)/shard_map/ppermute | solution.py:33
  75.1 1.1 collective-permute-start.11
  77.2 1.9 %collective-permute-done.10 = f32[32768]{0:T(1024)S(1)} collective-permute-done((f32[32768]{0:T(1024)S(1)}, f32[32768]{0:T(1024)S(1)}, u32[]{:S(2)}, u32[]{:S(2)}) %collective-permute-start.10) | collective-permute-done | bytes 131104 | tf_op jit(solution)/shard_map/ppermute | solution.py:33
  79.1 2.4 %collective-permute-done.11 = f32[32768]{0:T(1024)S(1)} collective-permute-done((f32[32768]{0:T(1024)S(1)}, f32[32768]{0:T(1024)S(1)}, u32[]{:S(2)}, u32[]{:S(2)}) %collective-permute-start.11) | collective-permute-done | bytes 131104 | tf_op jit(solution)/shard_map/ppermute | solution.py:33
  81.5 1.6 %collective-permute-done.9 = f32[32768]{0:T(1024)S(1)} collective-permute-done((f32[32768]{0:T(1024)S(1)}, f32[32768]{0:T(1024)S(1)}, u32[]{:S(2)}, u32[]{:S(2)}) %collective-permute-start.9) | collective-permute-done | bytes 131104 | tf_op jit(solution)/shard_map/ppermute | solution.py:33
  83.3 3.3 %collective-permute-start.12 = (f32[8192]{0:T(1024)S(1)}, f32[8192]{0:T(1024)S(1)}, u32[]{:S(2)}, u32[]{:S(2)}) collective-permute-start(f32[8192]{0:T(1024)S(1)} %bitcast.243), channel_id=1, source_target_pairs={{0,8},{8,16},{16,24},{24,0},{1,9},{9,17},{17,25},{25,1},{2,10},{10... | collective-permute-start | bytes 98312 | tf_op jit(solution)/shard_map/ppermute | solution.py:33
  86.6 1.4 %collective-permute-start.13 = (f32[8192]{0:T(1024)S(1)}, f32[8192]{0:T(1024)S(1)}, u32[]{:S(2)}, u32[]{:S(2)}) collective-permute-start(f32[8192]{0:T(1024)S(1)} %bitcast.242), channel_id=1, source_target_pairs={{0,16},{8,24},{16,0},{24,8},{1,17},{9,25},{17,1},{25,9},{2,18},{10... | collective-permute-start | bytes 98312 | tf_op jit(solution)/shard_map/ppermute | solution.py:33
  88.0 1.1 collective-permute-start.14
  89.5 1.9 %collective-permute-done.13 = f32[8192]{0:T(1024)S(1)} collective-permute-done((f32[8192]{0:T(1024)S(1)}, f32[8192]{0:T(1024)S(1)}, u32[]{:S(2)}, u32[]{:S(2)}) %collective-permute-start.13) | collective-permute-done | bytes 32800 | tf_op jit(solution)/shard_map/ppermute | solution.py:33
  92.4 3.1 %collective-permute-start.16 = (f32[8192]{0:T(1024)S(1)}, f32[8192]{0:T(1024)S(1)}, u32[]{:S(2)}, u32[]{:S(2)}) collective-permute-start(f32[8192]{0:T(1024)S(1)} %add_add_fusion.1), channel_id=1, source_target_pairs={{0,16},{8,24},{16,0},{24,8},{1,17},{9,25},{17,1},{25,9},{2,18},{10... | collective-permute-start | bytes 98312 | tf_op jit(solution)/shard_map/ppermute | solution.py:40
  95.5 0.9 collective-permute-start.17
  96.8 1.0 collective-permute-done.15
  97.8 1.7 %collective-permute-done.17 = f32[8192]{0:T(1024)S(1)} collective-permute-done((f32[8192]{0:T(1024)S(1)}, f32[8192]{0:T(1024)S(1)}, u32[]{:S(2)}, u32[]{:S(2)}) %collective-permute-start.17) | collective-permute-done | bytes 32800 | tf_op jit(solution)/shard_map/ppermute | solution.py:40
  100.3 1.3 %collective-permute-start.18 = (f32[32768]{0:T(1024)S(1)}, f32[32768]{0:T(1024)S(1)}, u32[]{:S(2)}, u32[]{:S(2)}) collective-permute-start(f32[32768]{0:T(1024)S(1)} %bitcast.227), channel_id=1, source_target_pairs={{0,2},{1,3},{2,4},{3,5},{4,6},{5,7},{6,0},{7,1},{8,10},{9,11},{10,... | collective-permute-start | bytes 393224 | tf_op jit(solution)/shard_map/ppermute | solution.py:40
  101.6 1.1 collective-permute-start.19
  102.7 2.1 %collective-permute-start.20 = (f32[32768]{0:T(1024)S(1)}, f32[32768]{0:T(1024)S(1)}, u32[]{:S(2)}, u32[]{:S(2)}) collective-permute-start(f32[32768]{0:T(1024)S(1)} %bitcast.229), channel_id=1, source_target_pairs={{0,6},{1,7},{2,0},{3,1},{4,2},{5,3},{6,4},{7,5},{8,14},{9,15},{10,... | collective-permute-start | bytes 393224 | tf_op jit(solution)/shard_map/ppermute | solution.py:40
  104.8 1.3 %convolution_convert_fusion.6 = bf16[4,128,256]{2,1,0:T(8,128)(2,1)} fusion(bf16[4,256,128]{2,1,0:T(8,128)(2,1)S(1)} %fusion.21, f32[4,256,256]{2,1,0:T(8,128)S(1)} %convolution_multiply_fusion), kind=kOutput, calls=%fused_computation.51 | convolution fusion | flops 402784256 | bytes 1572864 | tf_op jit(solution)/shard_map/drs,drh->dsh/dot_general | solution.py:332
  106.3 1.3 %collective-permute-done.19 = f32[32768]{0:T(1024)S(1)} collective-permute-done((f32[32768]{0:T(1024)S(1)}, f32[32768]{0:T(1024)S(1)}, u32[]{:S(2)}, u32[]{:S(2)}) %collective-permute-start.19) | collective-permute-done | bytes 131104 | tf_op jit(solution)/shard_map/ppermute | solution.py:40
  111.0 1.3 %convolution_add_fusion.4 = f32[4,256,256]{2,1,0:T(8,128)} fusion(f32[4,256,256]{2,1,0:T(8,128)S(1)} %convolution_add_fusion, bf16[4,128,256]{2,1,0:T(8,128)(2,1)S(1)} %collective-permute-done.7, s32[4,128]{1,0:T(4,128)S(1)} %copy-done.21, pred[4,128]{1,0:T(4,128)(4,1)S(1)} %copy-done.23), kind=kOutput, calls=%fused_computation.31 | convolution fusion | flops 67633152 | bytes 2361856 | tf_op jit(solution)/shard_map/dsn,dsh->dnh/dot_general | solution.py:347
  112.9 0.9 fusion.36
  113.8 0.9 gather_fusion.2
  114.7 0.9 gather_fusion.3
  116.1 0.9 gather.20
  117.2 1.0 fusion.73
  (159 shorter events, 30.8 us)
Async XLA Ops:
  0.6 12.5 %copy-start = (bf16[256,256]{1,0:T(8,128)(2,1)S(1)}, bf16[256,256]{1,0:T(8,128)(2,1)}, u32[]{:S(2)}) copy-start(bf16[256,256]{1,0:T(8,128)(2,1)} %param.17) | copy-start | bytes 393220
  4.1 7.7 %collective-permute-start = (bf16[4,128,256]{2,1,0:T(8,128)(2,1)}, bf16[4,128,256]{2,1,0:T(8,128)(2,1)}, u32[]{:S(2)}, u32[]{:S(2)}) collective-permute-start(bf16[4,128,256]{2,1,0:T(8,128)(2,1)} %convolution_convert_fusion.7), channel_id=1, source_target_pairs={{0,1},{1,2},{2,3},{3,4},{4,5},{5,6},{6,7},{7,0},{8,9},{9,10},{10,1... | collective-permute-start | bytes 786440 | tf_op jit(solution)/shard_map/ppermute | solution.py:12
  5.8 2.4 %copy-start.1 = (bf16[4,256,256]{2,1,0:T(8,128)(2,1)S(1)}, bf16[4,256,256]{2,1,0:T(8,128)(2,1)}, u32[]{:S(2)}) copy-start(bf16[4,256,256]{2,1,0:T(8,128)(2,1)} %param.12) | copy-start | bytes 1572868
  8.2 2.2 %copy-start.11 = (bf16[4,256,256]{2,1,0:T(8,128)(2,1)}, bf16[4,256,256]{2,1,0:T(8,128)(2,1)S(1)}, u32[]{:S(2)}) copy-start(bf16[4,256,256]{2,1,0:T(8,128)(2,1)S(1)} %fusion.17) | copy-start | bytes 1572868
  8.3 0.8 copy-start.25
  9.1 2.1 %copy-start.4 = (bf16[16,1,1,64,256]{4,3,2,1,0:T(8,128)(2,1)S(1)}, bf16[16,1,1,64,256]{4,3,2,1,0:T(8,128)(2,1)}, u32[]{:S(2)}) copy-start(bf16[16,1,1,64,256]{4,3,2,1,0:T(8,128)(2,1)} %param.21) | copy-start | bytes 1572868
  13.1 1.4 %copy-start.5 = (bf16[4,256,256]{2,1,0:T(8,128)(2,1)}, bf16[4,256,256]{2,1,0:T(8,128)(2,1)S(1)}, u32[]{:S(2)}) copy-start(bf16[4,256,256]{2,1,0:T(8,128)(2,1)S(1)} %fusion.15) | copy-start | bytes 1572868
  15.4 9.7 %collective-permute-start.1 = (bf16[4,64,256]{2,1,0:T(8,128)(2,1)}, bf16[4,64,256]{2,1,0:T(8,128)(2,1)}, u32[]{:S(2)}, u32[]{:S(2)}) collective-permute-start(bf16[4,64,256]{2,1,0:T(8,128)(2,1)} %get-tuple-element.39), channel_id=1, source_target_pairs={{0,8},{8,16},{16,24},{24,0},{1,9},{9,17},{17,25},{25,1},{2,10},{10... | collective-permute-start | bytes 393224 | tf_op jit(solution)/shard_map/ppermute | solution.py:87
  17.7 12.3 %collective-permute-start.2 = (bf16[4,64,256]{2,1,0:T(8,128)(2,1)}, bf16[4,64,256]{2,1,0:T(8,128)(2,1)}, u32[]{:S(2)}, u32[]{:S(2)}) collective-permute-start(bf16[4,64,256]{2,1,0:T(8,128)(2,1)} %get-tuple-element.38), channel_id=1, source_target_pairs={{0,16},{8,24},{16,0},{24,8},{1,17},{9,25},{17,1},{25,9},{2,18},{10... | collective-permute-start | bytes 393224 | tf_op jit(solution)/shard_map/ppermute | solution.py:87
  20.3 9.7 %collective-permute-start.3 = (bf16[4,64,256]{2,1,0:T(8,128)(2,1)}, bf16[4,64,256]{2,1,0:T(8,128)(2,1)}, u32[]{:S(2)}, u32[]{:S(2)}) collective-permute-start(bf16[4,64,256]{2,1,0:T(8,128)(2,1)} %get-tuple-element.37), channel_id=1, source_target_pairs={{0,24},{8,0},{16,8},{24,16},{1,25},{9,1},{17,9},{25,17},{2,26},{10... | collective-permute-start | bytes 393224 | tf_op jit(solution)/shard_map/ppermute | solution.py:87
  22.9 2.2 %copy-start.24 = (s32[4]{0:T(128)S(1)}, s32[4]{0:T(128)}, u32[]{:S(2)}) copy-start(s32[4]{0:T(128)} %compare_select_fusion) | copy-start | bytes 52
  22.9 7.2 %copy-start.19 = (bf16[1,4,64,256]{3,2,1,0:T(8,128)(2,1)S(1)}, bf16[1,4,64,256]{3,2,1,0:T(8,128)(2,1)}, u32[]{:S(2)}) copy-start(bf16[1,4,64,256]{3,2,1,0:T(8,128)(2,1)} %get-tuple-element.36) | copy-start | bytes 393220
  31.7 0.9 copy-start.16
  33.9 6.3 %copy-start.7 = (bf16[8,128,4,64]{1,3,2,0:T(8,128)(2,1)}, bf16[8,128,4,64]{1,3,2,0:T(8,128)(2,1)S(1)}, u32[]{:S(2)}) copy-start(bf16[8,128,4,64]{1,3,2,0:T(8,128)(2,1)S(1)} %copy.30) | copy-start | bytes 1572868
  38.5 1.8 %copy-start.9 = (bf16[8,128,4,64]{1,3,2,0:T(8,128)(2,1)S(1)}, bf16[8,128,4,64]{1,3,2,0:T(8,128)(2,1)}, u32[]{:S(2)}) copy-start(bf16[8,128,4,64]{1,3,2,0:T(8,128)(2,1)} %copy.36) | copy-start | bytes 1572868
  43.8 2.6 %copy-start.3 = (f32[8,4,128,128]{3,2,1,0:T(8,128)S(1)}, f32[8,4,128,128]{3,2,1,0:T(8,128)}, u32[]{:S(2)}) copy-start(f32[8,4,128,128]{3,2,1,0:T(8,128)} %fusion.27) | copy-start | bytes 6291460
  43.8 2.9 %copy-start.26 = (f32[8,4,128,128]{2,3,1,0:T(8,128)S(1)}, f32[8,4,128,128]{2,3,1,0:T(8,128)}, u32[]{:S(2)}) copy-start(f32[8,4,128,128]{2,3,1,0:T(8,128)} %get-tuple-element.53) | copy-start | bytes 6291460
  43.8 2.9 %copy-start.27 = (f32[8,4,128]{2,1,0:T(4,128)S(1)}, f32[8,4,128]{2,1,0:T(4,128)}, u32[]{:S(2)}) copy-start(f32[8,4,128]{2,1,0:T(4,128)} %get-tuple-element.52) | copy-start | bytes 49156
  46.7 1.0 copy-start.8
  47.7 1.0 copy-start.10
  50.0 1.2 %copy-start.2 = (f32[64,16,256]{2,1,0:T(8,128)S(1)}, f32[64,16,256]{2,1,0:T(8,128)}, u32[]{:S(2)}) copy-start(f32[64,16,256]{2,1,0:T(8,128)} %copy.26) | copy-start | bytes 3145732
  50.0 1.2 %copy-start.17 = (bf16[256,256]{1,0:T(8,128)(2,1)S(1)}, bf16[256,256]{1,0:T(8,128)(2,1)}, u32[]{:S(2)}) copy-start(bf16[256,256]{1,0:T(8,128)(2,1)} %param.18) | copy-start | bytes 393220
  50.7 1.0 copy-start.18
  51.2 0.9 copy-start.15
  52.9 8.8 %collective-permute-start.4 = (bf16[4,64,256]{2,1,0:T(8,128)(2,1)S(1)}, bf16[4,64,256]{2,1,0:T(8,128)(2,1)S(1)}, u32[]{:S(2)}, u32[]{:S(2)}) collective-permute-start(bf16[4,64,256]{2,1,0:T(8,128)(2,1)S(1)} %get-tuple-element.27), channel_id=1, source_target_pairs={{0,8},{8,16},{16,24},{24,0},{1,9},{9,17},{17,25},{25,1},{2,10},{10... | collective-permute-start | bytes 393224 | tf_op jit(solution)/shard_map/ppermute | solution.py:87
  56.3 10.5 %collective-permute-start.5 = (bf16[4,64,256]{2,1,0:T(8,128)(2,1)S(1)}, bf16[4,64,256]{2,1,0:T(8,128)(2,1)S(1)}, u32[]{:S(2)}, u32[]{:S(2)}) collective-permute-start(bf16[4,64,256]{2,1,0:T(8,128)(2,1)S(1)} %get-tuple-element.26), channel_id=1, source_target_pairs={{0,16},{8,24},{16,0},{24,8},{1,17},{9,25},{17,1},{25,9},{2,18},{10... | collective-permute-start | bytes 393224 | tf_op jit(solution)/shard_map/ppermute | solution.py:87
  57.9 9.0 %collective-permute-start.6 = (bf16[4,64,256]{2,1,0:T(8,128)(2,1)S(1)}, bf16[4,64,256]{2,1,0:T(8,128)(2,1)S(1)}, u32[]{:S(2)}, u32[]{:S(2)}) collective-permute-start(bf16[4,64,256]{2,1,0:T(8,128)(2,1)S(1)} %get-tuple-element.25), channel_id=1, source_target_pairs={{0,24},{8,0},{16,8},{24,16},{1,25},{9,1},{17,9},{25,17},{2,26},{10... | collective-permute-start | bytes 393224 | tf_op jit(solution)/shard_map/ppermute | solution.py:87
  66.8 1.2 %copy-start.13 = (f32[4,256,256]{2,1,0:T(8,128)S(1)}, f32[4,256,256]{2,1,0:T(8,128)}, u32[]{:S(2)}) copy-start(f32[4,256,256]{2,1,0:T(8,128)} %get-tuple-element.51) | copy-start | bytes 3145732
  67.5 1.1 copy-start.6
  67.7 1.4 %copy-start.14 = (f32[32,2,8,128]{3,1,2,0:T(2,128)S(1)}, f32[32,2,8,128]{3,1,2,0:T(2,128)}, u32[]{:S(2)}) copy-start(f32[32,2,8,128]{3,1,2,0:T(2,128)} %copy.63) | copy-start | bytes 786436
  70.7 2.0 %collective-permute-start.8 = (f32[131072]{0:T(1024)S(1)}, f32[131072]{0:T(1024)S(1)}, u32[]{:S(2)}, u32[]{:S(2)}) collective-permute-start(f32[131072]{0:T(1024)S(1)} %bitcast.224), channel_id=1, source_target_pairs={{0,1},{1,0},{2,3},{3,2},{4,5},{5,4},{6,7},{7,6},{8,9},{9,8},{10,11... | collective-permute-start | bytes 1572872 | tf_op jit(solution)/shard_map/ppermute | solution.py:33
  73.5 5.6 %collective-permute-start.10 = (f32[32768]{0:T(1024)S(1)}, f32[32768]{0:T(1024)S(1)}, u32[]{:S(2)}, u32[]{:S(2)}) collective-permute-start(f32[32768]{0:T(1024)S(1)} %bitcast.234), channel_id=1, source_target_pairs={{0,4},{1,5},{2,6},{3,7},{4,0},{5,1},{6,2},{7,3},{8,12},{9,13},{10,... | collective-permute-start | bytes 393224 | tf_op jit(solution)/shard_map/ppermute | solution.py:33
  75.1 6.4 %collective-permute-start.11 = (f32[32768]{0:T(1024)S(1)}, f32[32768]{0:T(1024)S(1)}, u32[]{:S(2)}, u32[]{:S(2)}) collective-permute-start(f32[32768]{0:T(1024)S(1)} %bitcast.233), channel_id=1, source_target_pairs={{0,6},{1,7},{2,0},{3,1},{4,2},{5,3},{6,4},{7,5},{8,14},{9,15},{10,... | collective-permute-start | bytes 393224 | tf_op jit(solution)/shard_map/ppermute | solution.py:33
  76.2 6.8 %collective-permute-start.9 = (f32[32768]{0:T(1024)S(1)}, f32[32768]{0:T(1024)S(1)}, u32[]{:S(2)}, u32[]{:S(2)}) collective-permute-start(f32[32768]{0:T(1024)S(1)} %bitcast.232), channel_id=1, source_target_pairs={{0,2},{1,3},{2,4},{3,5},{4,6},{5,7},{6,0},{7,1},{8,10},{9,11},{10,... | collective-permute-start | bytes 393224 | tf_op jit(solution)/shard_map/ppermute | solution.py:33
  83.3 6.2 %collective-permute-start.12 = (f32[8192]{0:T(1024)S(1)}, f32[8192]{0:T(1024)S(1)}, u32[]{:S(2)}, u32[]{:S(2)}) collective-permute-start(f32[8192]{0:T(1024)S(1)} %bitcast.243), channel_id=1, source_target_pairs={{0,8},{8,16},{16,24},{24,0},{1,9},{9,17},{17,25},{25,1},{2,10},{10... | collective-permute-start | bytes 98312 | tf_op jit(solution)/shard_map/ppermute | solution.py:33
  86.6 4.8 %collective-permute-start.13 = (f32[8192]{0:T(1024)S(1)}, f32[8192]{0:T(1024)S(1)}, u32[]{:S(2)}, u32[]{:S(2)}) collective-permute-start(f32[8192]{0:T(1024)S(1)} %bitcast.242), channel_id=1, source_target_pairs={{0,16},{8,24},{16,0},{24,8},{1,17},{9,25},{17,1},{25,9},{2,18},{10... | collective-permute-start | bytes 98312 | tf_op jit(solution)/shard_map/ppermute | solution.py:33
  88.0 3.9 %collective-permute-start.14 = (f32[8192]{0:T(1024)S(1)}, f32[8192]{0:T(1024)S(1)}, u32[]{:S(2)}, u32[]{:S(2)}) collective-permute-start(f32[8192]{0:T(1024)S(1)} %bitcast.241), channel_id=1, source_target_pairs={{0,24},{8,0},{16,8},{24,16},{1,25},{9,1},{17,9},{25,17},{2,26},{10... | collective-permute-start | bytes 98312 | tf_op jit(solution)/shard_map/ppermute | solution.py:33
  91.9 5.8 %collective-permute-start.15 = (f32[8192]{0:T(1024)S(1)}, f32[8192]{0:T(1024)S(1)}, u32[]{:S(2)}, u32[]{:S(2)}) collective-permute-start(f32[8192]{0:T(1024)S(1)} %add_add_fusion.1), channel_id=1, source_target_pairs={{0,8},{8,16},{16,24},{24,0},{1,9},{9,17},{17,25},{25,1},{2,10},{10... | collective-permute-start | bytes 98312 | tf_op jit(solution)/shard_map/ppermute | solution.py:40
  92.4 5.3 %collective-permute-start.16 = (f32[8192]{0:T(1024)S(1)}, f32[8192]{0:T(1024)S(1)}, u32[]{:S(2)}, u32[]{:S(2)}) collective-permute-start(f32[8192]{0:T(1024)S(1)} %add_add_fusion.1), channel_id=1, source_target_pairs={{0,16},{8,24},{16,0},{24,8},{1,17},{9,25},{17,1},{25,9},{2,18},{10... | collective-permute-start | bytes 98312 | tf_op jit(solution)/shard_map/ppermute | solution.py:40
  95.5 3.9 %collective-permute-start.17 = (f32[8192]{0:T(1024)S(1)}, f32[8192]{0:T(1024)S(1)}, u32[]{:S(2)}, u32[]{:S(2)}) collective-permute-start(f32[8192]{0:T(1024)S(1)} %add_add_fusion.1), channel_id=1, source_target_pairs={{0,24},{8,0},{16,8},{24,16},{1,25},{9,1},{17,9},{25,17},{2,26},{10... | collective-permute-start | bytes 98312 | tf_op jit(solution)/shard_map/ppermute | solution.py:40
  100.3 6.0 %collective-permute-start.18 = (f32[32768]{0:T(1024)S(1)}, f32[32768]{0:T(1024)S(1)}, u32[]{:S(2)}, u32[]{:S(2)}) collective-permute-start(f32[32768]{0:T(1024)S(1)} %bitcast.227), channel_id=1, source_target_pairs={{0,2},{1,3},{2,4},{3,5},{4,6},{5,7},{6,0},{7,1},{8,10},{9,11},{10,... | collective-permute-start | bytes 393224 | tf_op jit(solution)/shard_map/ppermute | solution.py:40
  101.6 6.0 %collective-permute-start.19 = (f32[32768]{0:T(1024)S(1)}, f32[32768]{0:T(1024)S(1)}, u32[]{:S(2)}, u32[]{:S(2)}) collective-permute-start(f32[32768]{0:T(1024)S(1)} %bitcast.228), channel_id=1, source_target_pairs={{0,4},{1,5},{2,6},{3,7},{4,0},{5,1},{6,2},{7,3},{8,12},{9,13},{10,... | collective-permute-start | bytes 393224 | tf_op jit(solution)/shard_map/ppermute | solution.py:40
  102.7 5.0 %collective-permute-start.20 = (f32[32768]{0:T(1024)S(1)}, f32[32768]{0:T(1024)S(1)}, u32[]{:S(2)}, u32[]{:S(2)}) collective-permute-start(f32[32768]{0:T(1024)S(1)} %bitcast.229), channel_id=1, source_target_pairs={{0,6},{1,7},{2,0},{3,1},{4,2},{5,3},{6,4},{7,5},{8,14},{9,15},{10,... | collective-permute-start | bytes 393224 | tf_op jit(solution)/shard_map/ppermute | solution.py:40
  106.1 4.9 %collective-permute-start.7 = (bf16[4,128,256]{2,1,0:T(8,128)(2,1)}, bf16[4,128,256]{2,1,0:T(8,128)(2,1)S(1)}, u32[]{:S(2)}, u32[]{:S(2)}) collective-permute-start(bf16[4,128,256]{2,1,0:T(8,128)(2,1)} %convolution_convert_fusion.6), channel_id=1, source_target_pairs={{0,7},{1,0},{2,1},{3,2},{4,3},{5,4},{6,5},{7,6},{8,15},{9,8},{10,9... | collective-permute-start | bytes 786440 | tf_op jit(solution)/shard_map/ppermute | solution.py:12
  109.1 1.0 copy-start.12
  109.3 1.7 %copy-start.21 = (s32[4,128]{1,0:T(4,128)S(1)}, s32[4,128]{1,0:T(4,128)}, u32[]{:S(2)}) copy-start(s32[4,128]{1,0:T(4,128)} %param.15) | copy-start | bytes 6148
  109.3 1.7 %copy-start.23 = (pred[4,128]{1,0:T(4,128)(4,1)S(1)}, pred[4,128]{1,0:T(4,128)(4,1)}, u32[]{:S(2)}) copy-start(pred[4,128]{1,0:T(4,128)(4,1)} %copy-done.22) | copy-start | bytes 1540
  109.4 3.5 %collective-permute-start.21 = (f32[131072]{0:T(1024)S(1)}, f32[131072]{0:T(1024)S(1)}, u32[]{:S(2)}, u32[]{:S(2)}) collective-permute-start(f32[131072]{0:T(1024)S(1)} %bitcast.222), channel_id=1, source_target_pairs={{0,1},{1,0},{2,3},{3,2},{4,5},{5,4},{6,7},{7,6},{8,9},{9,8},{10,11... | collective-permute-start | bytes 1572872 | tf_op jit(solution)/shard_map/ppermute | solution.py:40
  (2 other events, 1.3 us)

commit v8 on v7

--- a/solution.py
+++ b/solution.py
@@ -50,14 +50,14 @@
     return [2] + _factors(size // 2)
 
 
-def tree_sum(values, axes):
+def tree_sum(values, axes, companion=None):
     sizes = [lax.axis_size(axis) for axis in axes]
     flat = jnp.concatenate([value.reshape(-1) for value in values])
     total = 1
     for size in sizes:
         total *= size
     if not all(_power_of_two(size) for size in sizes) or flat.shape[0] % total:
-        return lax.psum(tuple(values), axes)
+        return lax.psum(tuple(values), axes), companion
     steps = []
     for axis, size in zip(axes, sizes):
         stride = 1
@@ -67,13 +67,14 @@
             stride *= group
     for axis, stride, group in steps:
         flat = _scatter_step(flat, axis, stride, group)
+    flat, companion = lax.optimization_barrier((flat, companion))
     for axis, stride, group in reversed(steps):
         flat = _gather_step(flat, axis, stride, group)
     results, start = [], 0
     for value in values:
         results.append(flat[start : start + value.size].reshape(value.shape))
         start += value.size
-    return tuple(results)
+    return tuple(results), companion
 
 
 def exchange(value, axis, split_axis, concat_axis):
@@ -324,9 +325,6 @@
         (((0,), (0,)), ((), ())),
         preferred_element_type=jnp.float32,
     )
-    grad_message, grad_query, grad_key, grad_value = tree_sum(
-        (grad_message, attn_grads[0], attn_grads[1], attn_grads[2]), ("dom", "day")
-    )
     agg_grad = jnp.einsum("drk,hk->drh", pre_grad, w_message, preferred_element_type=jnp.float32)
     term_grad = agg_grad * inverse[:, :, None]
     halo_grad = jnp.einsum(
@@ -346,6 +344,9 @@
     )
     scattered = jnp.einsum("dsn,dsh->dnh", slot_hot, returned, preferred_element_type=jnp.float32)
     state_grad = back_days.astype(jnp.float32) + term_grad + own_grad + scattered
+    (grad_message, grad_query, grad_key, grad_value), state_grad = tree_sum(
+        (grad_message, attn_grads[0], attn_grads[1], attn_grads[2]), ("dom", "day"), state_grad
+    )
     return (state_grad, grad_message, grad_query, grad_key, grad_value)
 
 

time: 120 us -> 117 us (0.975); the launches traced: 118 us -> 117 us
  matrix products: 26.8 us -> 23 us
  other arithmetic: 8.77 us -> 11.7 us
  waiting for transfers between devices: 27 us -> 24.7 us
    ppermute x7, waiting for transfers between devices: 10.4 us -> 7.16 us  [_scatter_step(): lax.ppermute(send, axis, _group_pairs(axis, stride, group, shift))]
    ppermute x7, waiting for transfers between devices: 4.15 us -> 6.82 us  [_gather_step(): lax.ppermute(flat, axis, _group_pairs(axis, stride, group, shift))]
    sub x1, other arithmetic: 0.61 us -> 2.94 us  [attend_blocked(): prob_grad - jnp.sum(prob_grad * probs, axis=-1, keepdims=True)]
    dot_general x3, matrix products: 2.82 us -> 0.86 us  [project(): jnp.dot(flat, weight, preferred_element_type=jnp.float32)]
    dot_general x4, matrix products: 5.53 us -> 3.83 us  [contract(): return jnp.einsum(spec, left, right, preferred_element_type=jnp.float32)]
    ppermute x6, waiting for transfers between devices: 11.9 us -> 10.2 us  [exchange(): lax.ppermute(send, axis, [(i, (i + shift) % count) for i in range(count)])]
    unnamed x64 -> x70, local copies, waits for them, and re-layouts: 5.79 us -> 6.17 us
  transfers between devices with their start and end apart: 22 -> 22, of which waited for: 16 -> 15; matrix products, arithmetic and copies ran while one was open for 14% -> 15% of each run, Pallas kernels for 0% -> 0%
where the time goes in v8:
time: 117 us
  starting transfers between devices  31.9 us (27%)
  waiting for transfers between devices  24.7 us (21%)
  local copies, waits for them, and re-layouts  23.9 us (20%)
  matrix products  23 us (20%)
  other arithmetic  11.7 us (10%)
  between operations  1.54 us (1%)
    ppermute x6, starting transfers between devices, exchange(): lax.ppermute(send, axis, [(i, (i + shift) % count) for i in range(count)])  12 us
    ppermute x6, waiting for transfers between devices, exchange(): lax.ppermute(send, axis, [(i, (i + shift) % count) for i in range(count)])  10.2 us
    ppermute x7, starting transfers between devices, _scatter_step(): lax.ppermute(send, axis, _group_pairs(axis, stride, group, shift))  9.46 us
    ppermute x7, starting transfers between devices, _gather_step(): lax.ppermute(flat, axis, _group_pairs(axis, stride, group, shift))  8.83 us
    ppermute x7, waiting for transfers between devices, _scatter_step(): lax.ppermute(send, axis, _group_pairs(axis, stride, group, shift))  7.16 us
    ppermute x7, waiting for transfers between devices, _gather_step(): lax.ppermute(flat, axis, _group_pairs(axis, stride, group, shift))  6.82 us
    unnamed x70, local copies, waits for them, and re-layouts  6.17 us
    sub x1, matrix products, attend_blocked(): exponent = jnp.exp(scores - highest)  4.15 us
  transfers between devices with their start and end apart: 22, of which 15 were waited for; matrix products, arithmetic and copies ran while one was open for 15% of the time, Pallas kernels for 0%

profile of v8, /device:TPU:0, one launch (start us, length us, event | category | flops | bytes accessed | tf_op | source)
XLA Modules:
  0.0 116.7 jit_solution(14850664461317833977)
XLA Ops:
  1.9 2.1 %convolution_convert_fusion.7 = bf16[4,128,256]{2,1,0:T(8,128)(2,1)} fusion(bf16[4,256,256]{2,1,0:T(8,128)(2,1)} %param.12, s32[4,128]{1,0:T(4,128)} %param.15, pred[4,128]{1,0:T(4,128)(4,1)S(1)} %iota_compare_fusion.12), kind=kOutput, calls=%fused_computation.52 | convolution fusion | flops 67502080 | bytes 788992 | tf_op jit(solution)/shard_map/dsn,dnh->dsh/dot_general | solution.py:287
  5.1 1.2 %convert_reduce_fusion = f32[4,256]{1,0:T(4,128)S(1)} fusion(s32[4,1024]{1,0:T(4,128)} %param.14), kind=kLoop, calls=%fused_computation.8 | loop fusion | flops 4193280 | bytes 20480 | tf_op jit(solution)/shard_map/reduce_sum | solution.py:302
  6.3 2.4 %fusion.17 = bf16[4,256,256]{2,1,0:T(8,128)(2,1)S(1)} fusion(s32[4,1024]{1,0:T(4,128)} %param.13, s32[4,1024]{1,0:T(4,128)} %param.14), kind=kOutput, calls=%fused_computation.46 | convolution fusion | flops 539230208 | bytes 557056 | tf_op jit(solution)/shard_map/der,des->drs/dot_general | solution.py:296
  9.1 1.3 %fusion.21 = bf16[4,256,128]{2,1,0:T(8,128)(2,1)S(1)} fusion(s32[4,1024]{1,0:T(4,128)S(1)} %copy-done.22, s32[128]{0:T(128)S(1)} %iota_add_fusion, s32[4,1024]{1,0:T(4,128)S(1)} %copy-done.28), kind=kOutput, calls=%fused_computation.50 | convolution fusion | flops 270139392 | bytes 295424 | tf_op jit(solution)/shard_map/der,des->drs/dot_general | solution.py:299
  11.7 1.3 %fusion.15 = bf16[4,256,256]{2,1,0:T(8,128)(2,1)S(1)} fusion(f32[4,256,256]{2,1,0:T(8,128)S(1)} %fusion.75, bf16[4,256,128]{2,1,0:T(8,128)(2,1)S(1)} %fusion.21, bf16[4,128,256]{2,1,0:T(8,128)(2,1)} %collective-permute-done, bf16[4,256,256]{2,1,0:T(8,128)(2,1)S(1)} %copy-done.1, f32[4,256]{1,0:T(4,128)S(1)} %add_divide_fusion.1), kind=kOutput, calls=%fused_computation.38 | convolution fusion | flops 68419584 | bytes 2625536 | tf_op jit(solution)/shard_map/drs,dsh->drh/dot_general | solution.py:308
  13.0 1.3 %fusion.24 = (bf16[4,256,256]{2,1,0:T(8,128)(2,1)S(1)}, f32[4,256,256]{2,1,0:T(8,128)}) fusion(bf16[4,256,256]{2,1,0:T(8,128)(2,1)S(1)} %copy-done.1, bf16[4,256,256]{2,1,0:T(8,128)(2,1)S(1)} %fusion.15, bf16[256,256]{1,0:T(8,128)(2,1)S(1)} %copy-done), kind=kOutput, calls=%fused_computation.57 | convolution fusion | flops 136052736 | bytes 2752512 | tf_op jit(solution)/shard_map/drh,hk->drk/dot_general | solution.py:310
  15.3 2.3 %collective-permute-start.1 = (bf16[4,64,256]{2,1,0:T(8,128)(2,1)}, bf16[4,64,256]{2,1,0:T(8,128)(2,1)}, u32[]{:S(2)}, u32[]{:S(2)}) collective-permute-start(bf16[4,64,256]{2,1,0:T(8,128)(2,1)} %get-tuple-element.43), channel_id=1, source_target_pairs={{0,8},{8,16},{16,24},{24,0},{1,9},{9,17},{17,25},{25,1},{2,10},{10... | collective-permute-start | bytes 393224 | tf_op jit(solution)/shard_map/ppermute | solution.py:88
  17.7 2.6 %collective-permute-start.2 = (bf16[4,64,256]{2,1,0:T(8,128)(2,1)}, bf16[4,64,256]{2,1,0:T(8,128)(2,1)}, u32[]{:S(2)}, u32[]{:S(2)}) collective-permute-start(bf16[4,64,256]{2,1,0:T(8,128)(2,1)} %get-tuple-element.42), channel_id=1, source_target_pairs={{0,16},{8,24},{16,0},{24,8},{1,17},{9,25},{17,1},{25,9},{2,18},{10... | collective-permute-start | bytes 393224 | tf_op jit(solution)/shard_map/ppermute | solution.py:88
  20.2 1.3 %collective-permute-start.3 = (bf16[4,64,256]{2,1,0:T(8,128)(2,1)}, bf16[4,64,256]{2,1,0:T(8,128)(2,1)}, u32[]{:S(2)}, u32[]{:S(2)}) collective-permute-start(bf16[4,64,256]{2,1,0:T(8,128)(2,1)} %get-tuple-element.41), channel_id=1, source_target_pairs={{0,24},{8,0},{16,8},{24,16},{1,25},{9,1},{17,9},{25,17},{2,26},{10... | collective-permute-start | bytes 393224 | tf_op jit(solution)/shard_map/ppermute | solution.py:88
  23.4 1.6 %copy.26 = f32[64,16,256]{2,1,0:T(8,128)} copy(f32[64,16,256]{2,0,1:T(8,128)S(1)} %bitcast_convert_fusion) | data formatting | bytes 2097152 | tf_op jit(solution)/shard_map/convert_element_type | solution.py:259
  25.0 5.0 %collective-permute-done.2 = bf16[4,64,256]{2,1,0:T(8,128)(2,1)} collective-permute-done((bf16[4,64,256]{2,1,0:T(8,128)(2,1)}, bf16[4,64,256]{2,1,0:T(8,128)(2,1)}, u32[]{:S(2)}, u32[]{:S(2)}) %collective-permute-start.2) | collective-permute-done | bytes 131104 | tf_op jit(solution)/shard_map/ppermute | solution.py:88
  30.1 1.1 pad_maximum_fusion.4
  33.4 1.2 %copy.30 = bf16[8,128,4,64]{1,3,2,0:T(8,128)(2,1)} copy(bf16[8,128,4,64]{3,2,1,0:T(4,128)(2,1)S(1)} %reshape.520) | data formatting | bytes 1048576 | tf_op jit(solution)/shard_map/reshape | solution.py:217
  35.3 1.2 %copy.36 = bf16[8,128,4,64]{1,3,2,0:T(8,128)(2,1)} copy(bf16[8,128,4,64]{3,2,1,0:T(4,128)(2,1)S(1)} %reshape.519) | data formatting | bytes 1048576 | tf_op jit(solution)/shard_map/reshape | solution.py:217
  37.2 1.8 %fusion.27 = f32[8,4,128,128]{3,2,1,0:T(8,128)} fusion(bf16[8,128,4,64]{1,3,2,0:T(8,128)(2,1)S(1)} %copy.35, bf16[8,128,4,64]{3,2,1,0:T(4,128)(2,1)S(1)} %reshape.518), kind=kOutput, calls=%fused_computation.64 | convolution fusion | flops 67108864 | bytes 3145728 | tf_op jit(solution)/shard_map/gihd,gjhd->ghij/dot_general | solution.py:228
  39.0 4.1 %fusion.74 = (f32[8,4,128]{2,1,0:T(4,128)}, f32[8,4,128,128]{2,3,1,0:T(8,128)}) fusion(pred[128,128]{0,1:T(8,128)(4,1)} %compare_and_fusion, bf16[8,128,4,64]{1,3,2,0:T(8,128)(2,1)} %copy.30, bf16[8,128,4,64]{1,3,2,0:T(8,128)(2,1)} %copy.36), kind=kOutput, calls=%fused_computation.210 | convolution fusion | flops 69206144 | bytes 3178496 | tf_op jit(solution)/shard_map/sub | solution.py:233
  43.2 2.9 %fusion.7 = bf16[8,4,128,128]{2,3,1,0:T(8,128)(2,1)S(1)} fusion(f32[8,4,128,128]{3,2,1,0:T(8,128)S(1)} %copy-done.3, f32[8,4,128,128]{2,3,1,0:T(8,128)} %get-tuple-element.57, f32[8,4,128]{2,1,0:T(4,128)} %get-tuple-element.56), kind=kOutput, calls=%fused_computation.18 | output fusion | flops 3674239 | bytes 5259264 | tf_op jit(solution)/shard_map/sub | solution.py:239
  52.7 3.3 %collective-permute-start.4 = (bf16[4,64,256]{2,1,0:T(8,128)(2,1)S(1)}, bf16[4,64,256]{2,1,0:T(8,128)(2,1)S(1)}, u32[]{:S(2)}, u32[]{:S(2)}) collective-permute-start(bf16[4,64,256]{2,1,0:T(8,128)(2,1)S(1)} %get-tuple-element.31), channel_id=1, source_target_pairs={{0,8},{8,16},{16,24},{24,0},{1,9},{9,17},{17,25},{25,1},{2,10},{10... | collective-permute-start | bytes 393224 | tf_op jit(solution)/shard_map/ppermute | solution.py:88
  56.1 1.5 %collective-permute-start.5 = (bf16[4,64,256]{2,1,0:T(8,128)(2,1)S(1)}, bf16[4,64,256]{2,1,0:T(8,128)(2,1)S(1)}, u32[]{:S(2)}, u32[]{:S(2)}) collective-permute-start(bf16[4,64,256]{2,1,0:T(8,128)(2,1)S(1)} %get-tuple-element.30), channel_id=1, source_target_pairs={{0,16},{8,24},{16,0},{24,8},{1,17},{9,25},{17,1},{25,9},{2,18},{10... | collective-permute-start | bytes 393224 | tf_op jit(solution)/shard_map/ppermute | solution.py:88
  57.5 1.0 collective-permute-start.6
  60.5 0.8 copy.65
  61.4 5.2 %collective-permute-done.5 = bf16[4,64,256]{2,1,0:T(8,128)(2,1)S(1)} collective-permute-done((bf16[4,64,256]{2,1,0:T(8,128)(2,1)S(1)}, bf16[4,64,256]{2,1,0:T(8,128)(2,1)S(1)}, u32[]{:S(2)}, u32[]{:S(2)}) %collective-permute-start.5) | collective-permute-done | bytes 131104 | tf_op jit(solution)/shard_map/ppermute | solution.py:88
  69.6 0.9 constant_dynamic-slice_fusion.8
  70.9 0.8 convolution_add_fusion
  73.3 2.0 %collective-permute-start.10 = (f32[32768]{0:T(1024)S(1)}, f32[32768]{0:T(1024)S(1)}, u32[]{:S(2)}, u32[]{:S(2)}) collective-permute-start(f32[32768]{0:T(1024)S(1)} %bitcast.236), channel_id=1, source_target_pairs={{0,6},{1,7},{2,0},{3,1},{4,2},{5,3},{6,4},{7,5},{8,14},{9,15},{10,... | collective-permute-start | bytes 393224 | tf_op jit(solution)/shard_map/ppermute | solution.py:33
  75.4 1.6 %collective-permute-start.9 = (f32[32768]{0:T(1024)S(1)}, f32[32768]{0:T(1024)S(1)}, u32[]{:S(2)}, u32[]{:S(2)}) collective-permute-start(f32[32768]{0:T(1024)S(1)} %bitcast.232), channel_id=1, source_target_pairs={{0,4},{1,5},{2,6},{3,7},{4,0},{5,1},{6,2},{7,3},{8,12},{9,13},{10,... | collective-permute-start | bytes 393224 | tf_op jit(solution)/shard_map/ppermute | solution.py:33
  77.5 1.1 collective-permute-start.14
  78.6 1.1 collective-permute-done.10
  79.7 3.1 %collective-permute-done.8 = f32[32768]{0:T(1024)S(1)} collective-permute-done((f32[32768]{0:T(1024)S(1)}, f32[32768]{0:T(1024)S(1)}, u32[]{:S(2)}, u32[]{:S(2)}) %collective-permute-start.8) | collective-permute-done | bytes 131104 | tf_op jit(solution)/shard_map/ppermute | solution.py:33
  83.5 3.3 %collective-permute-start.11 = (f32[8192]{0:T(1024)S(1)}, f32[8192]{0:T(1024)S(1)}, u32[]{:S(2)}, u32[]{:S(2)}) collective-permute-start(f32[8192]{0:T(1024)S(1)} %bitcast.243), channel_id=1, source_target_pairs={{0,8},{8,16},{16,24},{24,0},{1,9},{9,17},{17,25},{25,1},{2,10},{10... | collective-permute-start | bytes 98312 | tf_op jit(solution)/shard_map/ppermute | solution.py:33
  86.9 1.5 %collective-permute-start.12 = (f32[8192]{0:T(1024)S(1)}, f32[8192]{0:T(1024)S(1)}, u32[]{:S(2)}, u32[]{:S(2)}) collective-permute-start(f32[8192]{0:T(1024)S(1)} %bitcast.242), channel_id=1, source_target_pairs={{0,16},{8,24},{16,0},{24,8},{1,17},{9,25},{17,1},{25,9},{2,18},{10... | collective-permute-start | bytes 98312 | tf_op jit(solution)/shard_map/ppermute | solution.py:33
  88.4 0.9 collective-permute-start.13
  89.3 1.3 %convolution_add_fusion.4 = f32[4,256,256]{2,1,0:T(8,128)} fusion(f32[4,256,256]{2,1,0:T(8,128)S(1)} %convolution_add_fusion, bf16[4,128,256]{2,1,0:T(8,128)(2,1)S(1)} %collective-permute-done.14, s32[4,128]{1,0:T(4,128)S(1)} %copy-done.23, pred[4,128]{1,0:T(4,128)(4,1)S(1)} %copy-done.26), kind=kOutput, calls=%fused_computation.31 | convolution fusion | flops 67633152 | bytes 2361856 | tf_op jit(solution)/shard_map/dsn,dsh->dnh/dot_general | solution.py:345
  90.6 1.1 collective-permute-done.12
  92.7 3.0 %collective-permute-start.16 = (f32[8192]{0:T(1024)S(1)}, f32[8192]{0:T(1024)S(1)}, u32[]{:S(2)}, u32[]{:S(2)}) collective-permute-start(f32[8192]{0:T(1024)S(1)} %add_add_fusion.1), channel_id=1, source_target_pairs={{0,16},{8,24},{16,0},{24,8},{1,17},{9,25},{17,1},{25,9},{2,18},{10... | collective-permute-start | bytes 98312 | tf_op jit(solution)/shard_map/ppermute | solution.py:40
  95.7 1.0 collective-permute-start.17
  96.7 1.4 %collective-permute-done.15 = f32[8192]{0:T(1024)S(1)} collective-permute-done((f32[8192]{0:T(1024)S(1)}, f32[8192]{0:T(1024)S(1)}, u32[]{:S(2)}, u32[]{:S(2)}) %collective-permute-start.15) | collective-permute-done | bytes 32800 | tf_op jit(solution)/shard_map/ppermute | solution.py:40
  98.1 1.5 %collective-permute-done.17 = f32[8192]{0:T(1024)S(1)} collective-permute-done((f32[8192]{0:T(1024)S(1)}, f32[8192]{0:T(1024)S(1)}, u32[]{:S(2)}, u32[]{:S(2)}) %collective-permute-start.17) | collective-permute-done | bytes 32800 | tf_op jit(solution)/shard_map/ppermute | solution.py:40
  101.1 1.1 collective-permute-start.19
  102.2 2.6 %collective-permute-start.20 = (f32[32768]{0:T(1024)S(1)}, f32[32768]{0:T(1024)S(1)}, u32[]{:S(2)}, u32[]{:S(2)}) collective-permute-start(f32[32768]{0:T(1024)S(1)} %bitcast.229), channel_id=1, source_target_pairs={{0,6},{1,7},{2,0},{3,1},{4,2},{5,3},{6,4},{7,5},{8,14},{9,15},{10,... | collective-permute-start | bytes 393224 | tf_op jit(solution)/shard_map/ppermute | solution.py:40
  105.0 1.5 %collective-permute-done.18 = f32[32768]{0:T(1024)S(1)} collective-permute-done((f32[32768]{0:T(1024)S(1)}, f32[32768]{0:T(1024)S(1)}, u32[]{:S(2)}, u32[]{:S(2)}) %collective-permute-start.18) | collective-permute-done | bytes 131104 | tf_op jit(solution)/shard_map/ppermute | solution.py:40
  106.5 1.0 collective-permute-done.19
  110.1 1.2 %collective-permute-done.21 = f32[131072]{0:T(1024)S(1)} collective-permute-done((f32[131072]{0:T(1024)S(1)}, f32[131072]{0:T(1024)S(1)}, u32[]{:S(2)}, u32[]{:S(2)}) %collective-permute-start.21) | collective-permute-done | bytes 524320 | tf_op jit(solution)/shard_map/ppermute | solution.py:40
  111.3 0.9 fusion.36
  112.3 0.9 gather_fusion.2
  113.2 0.9 gather_fusion.3
  114.6 0.9 gather.20
  115.7 1.0 fusion.73
  (165 shorter events, 30.8 us)
Async XLA Ops:
  0.6 12.4 %copy-start = (bf16[256,256]{1,0:T(8,128)(2,1)S(1)}, bf16[256,256]{1,0:T(8,128)(2,1)}, u32[]{:S(2)}) copy-start(bf16[256,256]{1,0:T(8,128)(2,1)} %param.17) | copy-start | bytes 393220
  4.0 7.7 %collective-permute-start = (bf16[4,128,256]{2,1,0:T(8,128)(2,1)}, bf16[4,128,256]{2,1,0:T(8,128)(2,1)}, u32[]{:S(2)}, u32[]{:S(2)}) collective-permute-start(bf16[4,128,256]{2,1,0:T(8,128)(2,1)} %convolution_convert_fusion.7), channel_id=1, source_target_pairs={{0,1},{1,2},{2,3},{3,4},{4,5},{5,6},{6,7},{7,0},{8,9},{9,10},{10,1... | collective-permute-start | bytes 786440 | tf_op jit(solution)/shard_map/ppermute | solution.py:12
  6.3 2.4 %copy-start.1 = (bf16[4,256,256]{2,1,0:T(8,128)(2,1)S(1)}, bf16[4,256,256]{2,1,0:T(8,128)(2,1)}, u32[]{:S(2)}) copy-start(bf16[4,256,256]{2,1,0:T(8,128)(2,1)} %param.12) | copy-start | bytes 1572868
  6.3 2.8 %copy-start.22 = (s32[4,1024]{1,0:T(4,128)S(1)}, s32[4,1024]{1,0:T(4,128)}, u32[]{:S(2)}) copy-start(s32[4,1024]{1,0:T(4,128)} %param.14) | copy-start | bytes 49156
  6.3 2.8 %copy-start.28 = (s32[4,1024]{1,0:T(4,128)S(1)}, s32[4,1024]{1,0:T(4,128)}, u32[]{:S(2)}) copy-start(s32[4,1024]{1,0:T(4,128)} %param.13) | copy-start | bytes 49156
  8.7 1.7 %copy-start.9 = (bf16[4,256,256]{2,1,0:T(8,128)(2,1)}, bf16[4,256,256]{2,1,0:T(8,128)(2,1)S(1)}, u32[]{:S(2)}) copy-start(bf16[4,256,256]{2,1,0:T(8,128)(2,1)S(1)} %fusion.17) | copy-start | bytes 1572868
  9.1 2.1 %copy-start.4 = (bf16[16,1,1,64,256]{4,3,2,1,0:T(8,128)(2,1)S(1)}, bf16[16,1,1,64,256]{4,3,2,1,0:T(8,128)(2,1)}, u32[]{:S(2)}) copy-start(bf16[16,1,1,64,256]{4,3,2,1,0:T(8,128)(2,1)} %param.21) | copy-start | bytes 1572868
  13.0 1.4 %copy-start.5 = (bf16[4,256,256]{2,1,0:T(8,128)(2,1)}, bf16[4,256,256]{2,1,0:T(8,128)(2,1)S(1)}, u32[]{:S(2)}) copy-start(bf16[4,256,256]{2,1,0:T(8,128)(2,1)S(1)} %fusion.15) | copy-start | bytes 1572868
  15.3 9.7 %collective-permute-start.1 = (bf16[4,64,256]{2,1,0:T(8,128)(2,1)}, bf16[4,64,256]{2,1,0:T(8,128)(2,1)}, u32[]{:S(2)}, u32[]{:S(2)}) collective-permute-start(bf16[4,64,256]{2,1,0:T(8,128)(2,1)} %get-tuple-element.43), channel_id=1, source_target_pairs={{0,8},{8,16},{16,24},{24,0},{1,9},{9,17},{17,25},{25,1},{2,10},{10... | collective-permute-start | bytes 393224 | tf_op jit(solution)/shard_map/ppermute | solution.py:88
  17.7 12.4 %collective-permute-start.2 = (bf16[4,64,256]{2,1,0:T(8,128)(2,1)}, bf16[4,64,256]{2,1,0:T(8,128)(2,1)}, u32[]{:S(2)}, u32[]{:S(2)}) collective-permute-start(bf16[4,64,256]{2,1,0:T(8,128)(2,1)} %get-tuple-element.42), channel_id=1, source_target_pairs={{0,16},{8,24},{16,0},{24,8},{1,17},{9,25},{17,1},{25,9},{2,18},{10... | collective-permute-start | bytes 393224 | tf_op jit(solution)/shard_map/ppermute | solution.py:88
  20.2 9.9 %collective-permute-start.3 = (bf16[4,64,256]{2,1,0:T(8,128)(2,1)}, bf16[4,64,256]{2,1,0:T(8,128)(2,1)}, u32[]{:S(2)}, u32[]{:S(2)}) collective-permute-start(bf16[4,64,256]{2,1,0:T(8,128)(2,1)} %get-tuple-element.41), channel_id=1, source_target_pairs={{0,24},{8,0},{16,8},{24,16},{1,25},{9,1},{17,9},{25,17},{2,26},{10... | collective-permute-start | bytes 393224 | tf_op jit(solution)/shard_map/ppermute | solution.py:88
  22.8 2.2 %copy-start.27 = (s32[4]{0:T(128)S(1)}, s32[4]{0:T(128)}, u32[]{:S(2)}) copy-start(s32[4]{0:T(128)} %fusion.68) | copy-start | bytes 52
  22.8 7.3 %copy-start.21 = (bf16[1,4,64,256]{3,2,1,0:T(8,128)(2,1)S(1)}, bf16[1,4,64,256]{3,2,1,0:T(8,128)(2,1)}, u32[]{:S(2)}) copy-start(bf16[1,4,64,256]{3,2,1,0:T(8,128)(2,1)} %get-tuple-element.40) | copy-start | bytes 393220
  32.7 1.9 %copy-start.19 = (bf16[256,256]{1,0:T(8,128)(2,1)S(1)}, bf16[256,256]{1,0:T(8,128)(2,1)}, u32[]{:S(2)}) copy-start(bf16[256,256]{1,0:T(8,128)(2,1)} %param.19) | copy-start | bytes 393220
  34.6 1.9 %copy-start.15 = (bf16[256,256]{1,0:T(8,128)(2,1)S(1)}, bf16[256,256]{1,0:T(8,128)(2,1)}, u32[]{:S(2)}) copy-start(bf16[256,256]{1,0:T(8,128)(2,1)} %param.20) | copy-start | bytes 393220
  39.0 4.2 %copy-start.3 = (f32[8,4,128,128]{3,2,1,0:T(8,128)S(1)}, f32[8,4,128,128]{3,2,1,0:T(8,128)}, u32[]{:S(2)}) copy-start(f32[8,4,128,128]{3,2,1,0:T(8,128)} %fusion.27) | copy-start | bytes 6291460
  43.2 2.9 %copy-start.8 = (bf16[8,128,4,64]{1,3,2,0:T(8,128)(2,1)S(1)}, bf16[8,128,4,64]{1,3,2,0:T(8,128)(2,1)}, u32[]{:S(2)}) copy-start(bf16[8,128,4,64]{1,3,2,0:T(8,128)(2,1)} %copy.36) | copy-start | bytes 1572868
  46.1 1.9 %copy-start.29 = (f32[8,4,128,128]{2,3,1,0:T(8,128)S(1)}, f32[8,4,128,128]{2,3,1,0:T(8,128)}, u32[]{:S(2)}) copy-start(f32[8,4,128,128]{2,3,1,0:T(8,128)} %get-tuple-element.57) | copy-start | bytes 6291460
  46.1 1.9 %copy-start.30 = (f32[8,4,128]{2,1,0:T(4,128)S(1)}, f32[8,4,128]{2,1,0:T(4,128)}, u32[]{:S(2)}) copy-start(f32[8,4,128]{2,1,0:T(4,128)} %get-tuple-element.56) | copy-start | bytes 49156
  48.8 1.2 %copy-start.2 = (f32[64,16,256]{2,1,0:T(8,128)S(1)}, f32[64,16,256]{2,1,0:T(8,128)}, u32[]{:S(2)}) copy-start(f32[64,16,256]{2,1,0:T(8,128)} %copy.26) | copy-start | bytes 3145732
  48.8 1.2 %copy-start.18 = (bf16[256,256]{1,0:T(8,128)(2,1)S(1)}, bf16[256,256]{1,0:T(8,128)(2,1)}, u32[]{:S(2)}) copy-start(bf16[256,256]{1,0:T(8,128)(2,1)} %param.18) | copy-start | bytes 393220
  52.7 8.6 %collective-permute-start.4 = (bf16[4,64,256]{2,1,0:T(8,128)(2,1)S(1)}, bf16[4,64,256]{2,1,0:T(8,128)(2,1)S(1)}, u32[]{:S(2)}, u32[]{:S(2)}) collective-permute-start(bf16[4,64,256]{2,1,0:T(8,128)(2,1)S(1)} %get-tuple-element.31), channel_id=1, source_target_pairs={{0,8},{8,16},{16,24},{24,0},{1,9},{9,17},{17,25},{25,1},{2,10},{10... | collective-permute-start | bytes 393224 | tf_op jit(solution)/shard_map/ppermute | solution.py:88
  56.1 10.5 %collective-permute-start.5 = (bf16[4,64,256]{2,1,0:T(8,128)(2,1)S(1)}, bf16[4,64,256]{2,1,0:T(8,128)(2,1)S(1)}, u32[]{:S(2)}, u32[]{:S(2)}) collective-permute-start(bf16[4,64,256]{2,1,0:T(8,128)(2,1)S(1)} %get-tuple-element.30), channel_id=1, source_target_pairs={{0,16},{8,24},{16,0},{24,8},{1,17},{9,25},{17,1},{25,9},{2,18},{10... | collective-permute-start | bytes 393224 | tf_op jit(solution)/shard_map/ppermute | solution.py:88
  57.5 9.0 %collective-permute-start.6 = (bf16[4,64,256]{2,1,0:T(8,128)(2,1)S(1)}, bf16[4,64,256]{2,1,0:T(8,128)(2,1)S(1)}, u32[]{:S(2)}, u32[]{:S(2)}) collective-permute-start(bf16[4,64,256]{2,1,0:T(8,128)(2,1)S(1)} %get-tuple-element.29), channel_id=1, source_target_pairs={{0,24},{8,0},{16,8},{24,16},{1,25},{9,1},{17,9},{25,17},{2,26},{10... | collective-permute-start | bytes 393224 | tf_op jit(solution)/shard_map/ppermute | solution.py:88
  66.6 1.2 %copy-start.11 = (f32[4,256,256]{2,1,0:T(8,128)S(1)}, f32[4,256,256]{2,1,0:T(8,128)}, u32[]{:S(2)}) copy-start(f32[4,256,256]{2,1,0:T(8,128)} %get-tuple-element.55) | copy-start | bytes 3145732
  67.2 1.1 copy-start.6
  67.4 1.4 %copy-start.12 = (f32[32,2,8,128]{3,1,2,0:T(2,128)S(1)}, f32[32,2,8,128]{3,1,2,0:T(2,128)}, u32[]{:S(2)}) copy-start(f32[32,2,8,128]{3,1,2,0:T(2,128)} %copy.63) | copy-start | bytes 786436
  67.4 1.4 %copy-start.13 = (f32[32,2,8,128]{3,1,2,0:T(2,128)S(1)}, f32[32,2,8,128]{3,1,2,0:T(2,128)}, u32[]{:S(2)}) copy-start(f32[32,2,8,128]{3,1,2,0:T(2,128)} %copy.64) | copy-start | bytes 786436
  67.4 1.4 %copy-start.14 = (f32[32,2,8,128]{3,1,2,0:T(2,128)S(1)}, f32[32,2,8,128]{3,1,2,0:T(2,128)}, u32[]{:S(2)}) copy-start(f32[32,2,8,128]{3,1,2,0:T(2,128)} %copy.65) | copy-start | bytes 786436
  69.6 1.3 %copy-start.10 = (bf16[4,256,256]{2,1,0:T(8,128)(2,1)S(1)}, bf16[4,256,256]{2,1,0:T(8,128)(2,1)}, u32[]{:S(2)}) copy-start(bf16[4,256,256]{2,1,0:T(8,128)(2,1)} %copy-done.9) | copy-start | bytes 1572868
  70.5 2.0 %collective-permute-start.7 = (f32[131072]{0:T(1024)S(1)}, f32[131072]{0:T(1024)S(1)}, u32[]{:S(2)}, u32[]{:S(2)}) collective-permute-start(f32[131072]{0:T(1024)S(1)} %bitcast.224), channel_id=1, source_target_pairs={{0,1},{1,0},{2,3},{3,2},{4,5},{5,4},{6,7},{7,6},{8,9},{9,8},{10,11... | collective-permute-start | bytes 1572872 | tf_op jit(solution)/shard_map/ppermute | solution.py:33
  72.8 16.5 %copy-start.23 = (s32[4,128]{1,0:T(4,128)S(1)}, s32[4,128]{1,0:T(4,128)}, u32[]{:S(2)}) copy-start(s32[4,128]{1,0:T(4,128)} %param.15) | copy-start | bytes 6148
  72.8 16.5 %copy-start.26 = (pred[4,128]{1,0:T(4,128)(4,1)S(1)}, pred[4,128]{1,0:T(4,128)(4,1)}, u32[]{:S(2)}) copy-start(pred[4,128]{1,0:T(4,128)(4,1)} %copy-done.25) | copy-start | bytes 1540
  73.3 6.4 %collective-permute-start.10 = (f32[32768]{0:T(1024)S(1)}, f32[32768]{0:T(1024)S(1)}, u32[]{:S(2)}, u32[]{:S(2)}) collective-permute-start(f32[32768]{0:T(1024)S(1)} %bitcast.236), channel_id=1, source_target_pairs={{0,6},{1,7},{2,0},{3,1},{4,2},{5,3},{6,4},{7,5},{8,14},{9,15},{10,... | collective-permute-start | bytes 393224 | tf_op jit(solution)/shard_map/ppermute | solution.py:33
  75.3 7.5 %collective-permute-start.8 = (f32[32768]{0:T(1024)S(1)}, f32[32768]{0:T(1024)S(1)}, u32[]{:S(2)}, u32[]{:S(2)}) collective-permute-start(f32[32768]{0:T(1024)S(1)} %bitcast.234), channel_id=1, source_target_pairs={{0,2},{1,3},{2,4},{3,5},{4,6},{5,7},{6,0},{7,1},{8,10},{9,11},{10,... | collective-permute-start | bytes 393224 | tf_op jit(solution)/shard_map/ppermute | solution.py:33
  75.4 8.0 %collective-permute-start.9 = (f32[32768]{0:T(1024)S(1)}, f32[32768]{0:T(1024)S(1)}, u32[]{:S(2)}, u32[]{:S(2)}) collective-permute-start(f32[32768]{0:T(1024)S(1)} %bitcast.232), channel_id=1, source_target_pairs={{0,4},{1,5},{2,6},{3,7},{4,0},{5,1},{6,2},{7,3},{8,12},{9,13},{10,... | collective-permute-start | bytes 393224 | tf_op jit(solution)/shard_map/ppermute | solution.py:33
  77.5 11.8 %collective-permute-start.14 = (bf16[4,128,256]{2,1,0:T(8,128)(2,1)S(1)}, bf16[4,128,256]{2,1,0:T(8,128)(2,1)S(1)}, u32[]{:S(2)}, u32[]{:S(2)}) collective-permute-start(bf16[4,128,256]{2,1,0:T(8,128)(2,1)S(1)} %convolution_convert_fusion.6), channel_id=1, source_target_pairs={{0,7},{1,0},{2,1},{3,2},{4,3},{5,4},{6,5},{7,6},{8,15},{9,8},{10,9... | collective-permute-start | bytes 786440 | tf_op jit(solution)/shard_map/ppermute | solution.py:12
  83.4 16.9 %copy-start.24 = (pred[4]{0:T(512)(128)(4,1)S(1)}, pred[4]{0:T(512)(128)(4,1)}, u32[]{:S(2)}) copy-start(pred[4]{0:T(512)(128)(4,1)} %get-tuple-element.59) | copy-start | bytes 16
  83.5 7.0 %collective-permute-start.11 = (f32[8192]{0:T(1024)S(1)}, f32[8192]{0:T(1024)S(1)}, u32[]{:S(2)}, u32[]{:S(2)}) collective-permute-start(f32[8192]{0:T(1024)S(1)} %bitcast.243), channel_id=1, source_target_pairs={{0,8},{8,16},{16,24},{24,0},{1,9},{9,17},{17,25},{25,1},{2,10},{10... | collective-permute-start | bytes 98312 | tf_op jit(solution)/shard_map/ppermute | solution.py:33
  86.9 4.8 %collective-permute-start.12 = (f32[8192]{0:T(1024)S(1)}, f32[8192]{0:T(1024)S(1)}, u32[]{:S(2)}, u32[]{:S(2)}) collective-permute-start(f32[8192]{0:T(1024)S(1)} %bitcast.242), channel_id=1, source_target_pairs={{0,16},{8,24},{16,0},{24,8},{1,17},{9,25},{17,1},{25,9},{2,18},{10... | collective-permute-start | bytes 98312 | tf_op jit(solution)/shard_map/ppermute | solution.py:33
  88.4 3.9 %collective-permute-start.13 = (f32[8192]{0:T(1024)S(1)}, f32[8192]{0:T(1024)S(1)}, u32[]{:S(2)}, u32[]{:S(2)}) collective-permute-start(f32[8192]{0:T(1024)S(1)} %bitcast.241), channel_id=1, source_target_pairs={{0,24},{8,0},{16,8},{24,16},{1,25},{9,1},{17,9},{25,17},{2,26},{10... | collective-permute-start | bytes 98312 | tf_op jit(solution)/shard_map/ppermute | solution.py:33
  92.3 5.8 %collective-permute-start.15 = (f32[8192]{0:T(1024)S(1)}, f32[8192]{0:T(1024)S(1)}, u32[]{:S(2)}, u32[]{:S(2)}) collective-permute-start(f32[8192]{0:T(1024)S(1)} %add_add_fusion.1), channel_id=1, source_target_pairs={{0,8},{8,16},{16,24},{24,0},{1,9},{9,17},{17,25},{25,1},{2,10},{10... | collective-permute-start | bytes 98312 | tf_op jit(solution)/shard_map/ppermute | solution.py:40
  92.7 5.4 %collective-permute-start.16 = (f32[8192]{0:T(1024)S(1)}, f32[8192]{0:T(1024)S(1)}, u32[]{:S(2)}, u32[]{:S(2)}) collective-permute-start(f32[8192]{0:T(1024)S(1)} %add_add_fusion.1), channel_id=1, source_target_pairs={{0,16},{8,24},{16,0},{24,8},{1,17},{9,25},{17,1},{25,9},{2,18},{10... | collective-permute-start | bytes 98312 | tf_op jit(solution)/shard_map/ppermute | solution.py:40
  95.7 3.9 %collective-permute-start.17 = (f32[8192]{0:T(1024)S(1)}, f32[8192]{0:T(1024)S(1)}, u32[]{:S(2)}, u32[]{:S(2)}) collective-permute-start(f32[8192]{0:T(1024)S(1)} %add_add_fusion.1), channel_id=1, source_target_pairs={{0,24},{8,0},{16,8},{24,16},{1,25},{9,1},{17,9},{25,17},{2,26},{10... | collective-permute-start | bytes 98312 | tf_op jit(solution)/shard_map/ppermute | solution.py:40
  100.5 6.0 %collective-permute-start.18 = (f32[32768]{0:T(1024)S(1)}, f32[32768]{0:T(1024)S(1)}, u32[]{:S(2)}, u32[]{:S(2)}) collective-permute-start(f32[32768]{0:T(1024)S(1)} %bitcast.227), channel_id=1, source_target_pairs={{0,2},{1,3},{2,4},{3,5},{4,6},{5,7},{6,0},{7,1},{8,10},{9,11},{10,... | collective-permute-start | bytes 393224 | tf_op jit(solution)/shard_map/ppermute | solution.py:40
  101.1 6.4 %collective-permute-start.19 = (f32[32768]{0:T(1024)S(1)}, f32[32768]{0:T(1024)S(1)}, u32[]{:S(2)}, u32[]{:S(2)}) collective-permute-start(f32[32768]{0:T(1024)S(1)} %bitcast.228), channel_id=1, source_target_pairs={{0,4},{1,5},{2,6},{3,7},{4,0},{5,1},{6,2},{7,3},{8,12},{9,13},{10,... | collective-permute-start | bytes 393224 | tf_op jit(solution)/shard_map/ppermute | solution.py:40
  102.2 5.5 %collective-permute-start.20 = (f32[32768]{0:T(1024)S(1)}, f32[32768]{0:T(1024)S(1)}, u32[]{:S(2)}, u32[]{:S(2)}) collective-permute-start(f32[32768]{0:T(1024)S(1)} %bitcast.229), channel_id=1, source_target_pairs={{0,6},{1,7},{2,0},{3,1},{4,2},{5,3},{6,4},{7,5},{8,14},{9,15},{10,... | collective-permute-start | bytes 393224 | tf_op jit(solution)/shard_map/ppermute | solution.py:40
  109.4 2.0 %collective-permute-start.21 = (f32[131072]{0:T(1024)S(1)}, f32[131072]{0:T(1024)S(1)}, u32[]{:S(2)}, u32[]{:S(2)}) collective-permute-start(f32[131072]{0:T(1024)S(1)} %bitcast.222), channel_id=1, source_target_pairs={{0,1},{1,0},{2,3},{3,2},{4,5},{5,4},{6,7},{7,6},{8,9},{9,8},{10,11... | collective-permute-start | bytes 1572872 | tf_op jit(solution)/shard_map/ppermute | solution.py:40
  (5 other events, 4.4 us)

commit v9 on v8

--- a/solution.py
+++ b/solution.py
@@ -34,14 +34,24 @@
     return total
 
 
+def _by_source(got, digit):
+    count = len(got)
+    ordered = []
+    for source in range(count):
+        place = (digit - source) % count
+        chosen = got[count - 1]
+        for shift in range(count - 2, -1, -1):
+            chosen = jnp.where(place == shift, got[shift], chosen)
+        ordered.append(chosen)
+    return ordered
+
+
 def _gather_step(flat, axis, stride, group):
     digit = (lax.axis_index(axis) // stride) % group
     got = [flat] + [
         lax.ppermute(flat, axis, _group_pairs(axis, stride, group, shift)) for shift in range(1, group)
     ]
-    stacked = jnp.stack(got)
-    order = (digit - jnp.arange(group)) % group
-    return jnp.take(stacked, order, axis=0).reshape(-1)
+    return jnp.concatenate(_by_source(got, digit))
 
 
 def _factors(size):
@@ -87,8 +97,7 @@
         if shift:
             send = lax.ppermute(send, axis, [(i, (i + shift) % count) for i in range(count)])
         got.append(send)
-    stacked = jnp.take(jnp.stack(got), (mine - jnp.arange(count)) % count, axis=0)
-    return jnp.concatenate([stacked[k] for k in range(count)], axis=concat_axis)
+    return jnp.concatenate(_by_source(got, mine), axis=concat_axis)
 
 
 def adjacency(sources, targets, count_rows, total_rows):

time: 117 us -> 119 us (1.017)
  matrix products: 23 us -> 28.2 us
  waiting for transfers between devices: 24.7 us -> 29.5 us
  local copies, waits for them, and re-layouts: 23.9 us -> 19.2 us
  other arithmetic: 11.7 us -> 8.12 us
    gather x7 -> x0, local copies, waits for them, and re-layouts: 5.3 us -> none  [the longest x5 4.14 us: _gather_step(): return jnp.take(stacked, order, axis=0).reshape(-1)]
    reshape x5, local copies, waits for them, and re-layouts: 3.61 us -> 8.5 us  [blocks(): return matrix.reshape(groups, block, HEADS, head_dim)]
    unnamed x70 -> x38, local copies, waits for them, and re-layouts: 6.17 us -> 1.64 us
    ppermute x6, waiting for transfers between devices: 10.2 us -> 14.8 us  [exchange(): lax.ppermute(send, axis, [(i, (i + shift) % count) for i in range(count)])]
    dot_general x3, matrix products: 0.86 us -> 5.06 us  [project(): jnp.dot(flat, weight, preferred_element_type=jnp.float32)]
    another operation x5 -> x0, other arithmetic: 2.74 us -> none  [the longest x3 1.57 us: _gather_step(): stacked = jnp.stack(got)]
    slice x1 -> x6, local copies, waits for them, and re-layouts: 0.98 us -> 3.18 us  [tree_sum(): results.append(flat[start:start + value.size].reshape(value.shape))]
    sub x1, other arithmetic: 2.94 us -> 4.15 us  [attend_blocked(): prob_grad - jnp.sum(prob_grad * probs, axis=-1, keepdims=True)]
  transfers between devices with their start and end apart: 22 -> 22, of which waited for: 15 -> 17; matrix products, arithmetic and copies ran while one was open for 15% -> 11% of each run, Pallas kernels for 0% -> 0%
where the time goes in v9:
time: 119 us
  starting transfers between devices  32.4 us (27%)
  waiting for transfers between devices  29.5 us (25%)
  matrix products  28.2 us (24%)
  local copies, waits for them, and re-layouts  19.2 us (16%)
  other arithmetic  8.12 us (7%)
  between operations  1.4 us (1%)
    ppermute x6, waiting for transfers between devices, exchange(): lax.ppermute(send, axis, [(i, (i + shift) % count) for i in range(count)])  14.8 us
    ppermute x6, starting transfers between devices, exchange(): lax.ppermute(send, axis, [(i, (i + shift) % count) for i in range(count)])  12.5 us
    ppermute x7, starting transfers between devices, _scatter_step(): lax.ppermute(send, axis, _group_pairs(axis, stride, group, shift))  9.43 us
    ppermute x7, starting transfers between devices, _gather_step(): lax.ppermute(flat, axis, _group_pairs(axis, stride, group, shift))  8.8 us
    reshape x5, local copies, waits for them, and re-layouts, blocks(): return matrix.reshape(groups, block, HEADS, head_dim)  8.5 us
    ppermute x7, waiting for transfers between devices, _gather_step(): lax.ppermute(flat, axis, _group_pairs(axis, stride, group, shift))  7.72 us
    ppermute x7, waiting for transfers between devices, _scatter_step(): lax.ppermute(send, axis, _group_pairs(axis, stride, group, shift))  7 us
    dot_general x3, matrix products, project(): jnp.dot(flat, weight, preferred_element_type=jnp.float32)  5.06 us
  transfers between devices with their start and end apart: 22, of which 17 were waited for; matrix products, arithmetic and copies ran while one was open for 11% of the time, Pallas kernels for 0%

profile of v9, /device:TPU:0, one launch (start us, length us, event | category | flops | bytes accessed | tf_op | source)
XLA Modules:
  0.0 118.8 jit_solution(9927726724177680575)
XLA Ops:
  1.4 2.1 %convolution_convert_fusion.7 = bf16[4,128,256]{2,1,0:T(8,128)(2,1)} fusion(bf16[4,256,256]{2,1,0:T(8,128)(2,1)} %param.10, s32[4,128]{1,0:T(4,128)} %param.13, pred[4,128]{1,0:T(4,128)(4,1)S(1)} %iota_compare_fusion.12), kind=kOutput, calls=%fused_computation.46 | convolution fusion | flops 67502080 | bytes 788992 | tf_op jit(solution)/shard_map/dsn,dnh->dsh/dot_general | solution.py:296
  4.0 1.2 %convert_reduce_fusion = f32[4,256]{1,0:T(4,128)S(1)} fusion(s32[4,1024]{1,0:T(4,128)} %param.12), kind=kLoop, calls=%fused_computation.2 | loop fusion | flops 4193280 | bytes 20480 | tf_op jit(solution)/shard_map/reduce_sum | solution.py:311
  5.2 3.1 %fusion.17 = bf16[4,256,256]{2,1,0:T(8,128)(2,1)} fusion(s32[4,1024]{1,0:T(4,128)} %param.11, s32[4,1024]{1,0:T(4,128)} %param.12), kind=kOutput, calls=%fused_computation.40 | convolution fusion | flops 539230208 | bytes 557056 | tf_op jit(solution)/shard_map/der,des->drs/dot_general | solution.py:305
  8.3 1.3 %fusion.21 = bf16[4,256,128]{2,1,0:T(8,128)(2,1)S(1)} fusion(s32[4,1024]{1,0:T(4,128)S(1)} %copy-done.13, s32[128]{0:T(128)S(1)} %iota_add_fusion, s32[4,1024]{1,0:T(4,128)S(1)} %copy-done.15), kind=kOutput, calls=%fused_computation.44 | convolution fusion | flops 270139392 | bytes 295424 | tf_op jit(solution)/shard_map/der,des->drs/dot_general | solution.py:308
  11.8 1.3 %fusion.65 = f32[4,256,256]{2,1,0:T(8,128)S(1)} fusion(bf16[4,256,256]{2,1,0:T(8,128)(2,1)} %fusion.17, bf16[4,256,256]{2,1,0:T(8,128)(2,1)S(1)} %copy-done.1), kind=kOutput, calls=%fused_computation.154 | convolution fusion | flops 134217728 | bytes 2097152 | tf_op jit(solution)/shard_map/drs,dsh->drh/dot_general | solution.py:315
  13.1 1.3 %fusion.15 = bf16[4,256,256]{2,1,0:T(8,128)(2,1)S(1)} fusion(f32[4,256,256]{2,1,0:T(8,128)S(1)} %fusion.65, bf16[4,256,128]{2,1,0:T(8,128)(2,1)S(1)} %fusion.21, bf16[4,128,256]{2,1,0:T(8,128)(2,1)} %collective-permute-done, bf16[4,256,256]{2,1,0:T(8,128)(2,1)S(1)} %copy-done.1, f32[4,256]{1,0:T(4,128)S(1)} %add_divide_fusion.1), kind=kOutput, calls=%fused_computation.32 | convolution fusion | flops 68419584 | bytes 2625536 | tf_op jit(solution)/shard_map/drs,dsh->drh/dot_general | solution.py:317
  14.4 1.3 %fusion.24 = (bf16[4,256,256]{2,1,0:T(8,128)(2,1)S(1)}, f32[4,256,256]{2,1,0:T(8,128)}) fusion(bf16[4,256,256]{2,1,0:T(8,128)(2,1)S(1)} %copy-done.1, bf16[4,256,256]{2,1,0:T(8,128)(2,1)S(1)} %fusion.15, bf16[256,256]{1,0:T(8,128)(2,1)S(1)} %copy-done), kind=kOutput, calls=%fused_computation.51 | convolution fusion | flops 136052736 | bytes 2752512 | tf_op jit(solution)/shard_map/drh,hk->drk/dot_general | solution.py:319
  16.0 2.8 %collective-permute-start.1 = (bf16[4,64,256]{2,1,0:T(8,128)(2,1)S(1)}, bf16[4,64,256]{2,1,0:T(8,128)(2,1)S(1)}, u32[]{:S(2)}, u32[]{:S(2)}) collective-permute-start(bf16[4,64,256]{2,1,0:T(8,128)(2,1)S(1)} %get-tuple-element.42), channel_id=1, source_target_pairs={{0,8},{8,16},{16,24},{24,0},{1,9},{9,17},{17,25},{25,1},{2,10},{10... | collective-permute-start | bytes 393224 | tf_op jit(solution)/shard_map/ppermute | solution.py:98
  18.7 2.6 %collective-permute-start.2 = (bf16[4,64,256]{2,1,0:T(8,128)(2,1)S(1)}, bf16[4,64,256]{2,1,0:T(8,128)(2,1)S(1)}, u32[]{:S(2)}, u32[]{:S(2)}) collective-permute-start(bf16[4,64,256]{2,1,0:T(8,128)(2,1)S(1)} %get-tuple-element.41), channel_id=1, source_target_pairs={{0,16},{8,24},{16,0},{24,8},{1,17},{9,25},{17,1},{25,9},{2,18},{10... | collective-permute-start | bytes 393224 | tf_op jit(solution)/shard_map/ppermute | solution.py:98
  21.3 1.3 %collective-permute-start.3 = (bf16[4,64,256]{2,1,0:T(8,128)(2,1)S(1)}, bf16[4,64,256]{2,1,0:T(8,128)(2,1)S(1)}, u32[]{:S(2)}, u32[]{:S(2)}) collective-permute-start(bf16[4,64,256]{2,1,0:T(8,128)(2,1)S(1)} %get-tuple-element.40), channel_id=1, source_target_pairs={{0,24},{8,0},{16,8},{24,16},{1,25},{9,1},{17,9},{25,17},{2,26},{10... | collective-permute-start | bytes 393224 | tf_op jit(solution)/shard_map/ppermute | solution.py:98
  23.4 1.1 collective-permute-done.1
  24.5 6.3 %collective-permute-done.2 = bf16[4,64,256]{2,1,0:T(8,128)(2,1)S(1)} collective-permute-done((bf16[4,64,256]{2,1,0:T(8,128)(2,1)S(1)}, bf16[4,64,256]{2,1,0:T(8,128)(2,1)S(1)}, u32[]{:S(2)}, u32[]{:S(2)}) %collective-permute-start.2) | collective-permute-done | bytes 131104 | tf_op jit(solution)/shard_map/ppermute | solution.py:98
  31.4 1.1 convolution_convert_fusion.1
  32.4 2.0 %reshape.260 = bf16[8,128,4,64]{3,2,1,0:T(4,128)(2,1)S(1)} reshape(bf16[1024,256]{1,0:T(8,128)(2,1)} %convolution_convert_fusion.1) | data formatting | bytes 1048576 | tf_op jit(solution)/shard_map/reshape | solution.py:226
  34.5 1.2 %copy.31 = bf16[8,128,4,64]{1,3,2,0:T(8,128)(2,1)} copy(bf16[8,128,4,64]{3,2,1,0:T(4,128)(2,1)S(1)} %reshape.260) | data formatting | bytes 1048576 | tf_op jit(solution)/shard_map/reshape | solution.py:226
  35.7 2.0 %convolution_convert_fusion.2 = bf16[1024,256]{1,0:T(8,128)(2,1)} fusion(bf16[1024,256]{1,0:T(8,128)(2,1)S(1)} %bitcast.161, bf16[256,256]{1,0:T(8,128)(2,1)} %param.17), kind=kOutput, calls=%fused_computation.35 | convolution fusion | flops 134479872 | bytes 1179648 | tf_op jit(solution)/shard_map/dot_general | solution.py:223
  37.7 2.0 %reshape.259 = bf16[8,128,4,64]{3,2,1,0:T(4,128)(2,1)S(1)} reshape(bf16[1024,256]{1,0:T(8,128)(2,1)} %convolution_convert_fusion.2) | data formatting | bytes 1048576 | tf_op jit(solution)/shard_map/reshape | solution.py:226
  39.7 1.2 %copy.37 = bf16[8,128,4,64]{1,3,2,0:T(8,128)(2,1)} copy(bf16[8,128,4,64]{3,2,1,0:T(4,128)(2,1)S(1)} %reshape.259) | data formatting | bytes 1048576 | tf_op jit(solution)/shard_map/reshape | solution.py:226
  40.9 2.0 %convolution_convert_fusion = bf16[1024,256]{1,0:T(8,128)(2,1)} fusion(bf16[1024,256]{1,0:T(8,128)(2,1)S(1)} %bitcast.162, bf16[256,256]{1,0:T(8,128)(2,1)} %param.18), kind=kOutput, calls=%fused_computation.33 | convolution fusion | flops 134479872 | bytes 1179648 | tf_op jit(solution)/shard_map/dot_general | solution.py:223
  42.9 2.0 %reshape.258 = bf16[8,128,4,64]{3,2,1,0:T(4,128)(2,1)S(1)} reshape(bf16[1024,256]{1,0:T(8,128)(2,1)} %convolution_convert_fusion) | data formatting | bytes 1048576 | tf_op jit(solution)/shard_map/reshape | solution.py:226
  45.0 1.8 %fusion.27 = f32[8,4,128,128]{3,2,1,0:T(8,128)} fusion(bf16[8,128,4,64]{1,3,2,0:T(8,128)(2,1)S(1)} %copy.36, bf16[8,128,4,64]{3,2,1,0:T(4,128)(2,1)S(1)} %reshape.258), kind=kOutput, calls=%fused_computation.55 | convolution fusion | flops 67108864 | bytes 3145728 | tf_op jit(solution)/shard_map/gihd,gjhd->ghij/dot_general | solution.py:237
  46.7 3.4 %fusion.64 = (f32[8,4,128]{2,1,0:T(4,128)S(1)}, f32[8,4,128,128]{2,3,1,0:T(8,128)}) fusion(pred[128,128]{0,1:T(8,128)(4,1)} %compare_and_fusion, bf16[8,128,4,64]{1,3,2,0:T(8,128)(2,1)} %copy.31, bf16[8,128,4,64]{1,3,2,0:T(8,128)(2,1)} %copy.37), kind=kOutput, calls=%fused_computation.153 | convolution fusion | flops 69206144 | bytes 3178496 | tf_op jit(solution)/shard_map/sub | solution.py:242
  50.1 4.2 %fusion.7 = bf16[8,4,128,128]{2,3,1,0:T(8,128)(2,1)S(1)} fusion(f32[8,4,128,128]{3,2,1,0:T(8,128)} %fusion.27, f32[8,4,128,128]{2,3,1,0:T(8,128)} %get-tuple-element.58, f32[8,4,128]{2,1,0:T(4,128)S(1)} %get-tuple-element.57), kind=kOutput, calls=%fused_computation.12 | output fusion | flops 3674239 | bytes 5259264 | tf_op jit(solution)/shard_map/sub | solution.py:248
  56.2 0.8 fusion.20
  60.6 3.3 %collective-permute-start.4 = (bf16[4,64,256]{2,1,0:T(8,128)(2,1)S(1)}, bf16[4,64,256]{2,1,0:T(8,128)(2,1)S(1)}, u32[]{:S(2)}, u32[]{:S(2)}) collective-permute-start(bf16[4,64,256]{2,1,0:T(8,128)(2,1)S(1)} %get-tuple-element.35), channel_id=1, source_target_pairs={{0,8},{8,16},{16,24},{24,0},{1,9},{9,17},{17,25},{25,1},{2,10},{10... | collective-permute-start | bytes 393224 | tf_op jit(solution)/shard_map/ppermute | solution.py:98
  63.9 1.5 %collective-permute-start.5 = (bf16[4,64,256]{2,1,0:T(8,128)(2,1)S(1)}, bf16[4,64,256]{2,1,0:T(8,128)(2,1)S(1)}, u32[]{:S(2)}, u32[]{:S(2)}) collective-permute-start(bf16[4,64,256]{2,1,0:T(8,128)(2,1)S(1)} %get-tuple-element.34), channel_id=1, source_target_pairs={{0,16},{8,24},{16,0},{24,8},{1,17},{9,25},{17,1},{25,9},{2,18},{10... | collective-permute-start | bytes 393224 | tf_op jit(solution)/shard_map/ppermute | solution.py:98
  65.4 1.0 collective-permute-start.6
  67.1 2.1 %collective-permute-done.4 = bf16[4,64,256]{2,1,0:T(8,128)(2,1)S(1)} collective-permute-done((bf16[4,64,256]{2,1,0:T(8,128)(2,1)S(1)}, bf16[4,64,256]{2,1,0:T(8,128)(2,1)S(1)}, u32[]{:S(2)}, u32[]{:S(2)}) %collective-permute-start.4) | collective-permute-done | bytes 131104 | tf_op jit(solution)/shard_map/ppermute | solution.py:98
  69.2 5.2 %collective-permute-done.5 = bf16[4,64,256]{2,1,0:T(8,128)(2,1)S(1)} collective-permute-done((bf16[4,64,256]{2,1,0:T(8,128)(2,1)S(1)}, bf16[4,64,256]{2,1,0:T(8,128)(2,1)S(1)}, u32[]{:S(2)}, u32[]{:S(2)}) %collective-permute-start.5) | collective-permute-done | bytes 131104 | tf_op jit(solution)/shard_map/ppermute | solution.py:98
  76.1 0.9 constant_dynamic-slice_fusion.8
  77.5 0.8 convolution_add_fusion
  79.8 1.8 %collective-permute-start.10 = (f32[32768]{0:T(1024)S(1)}, f32[32768]{0:T(1024)S(1)}, u32[]{:S(2)}, u32[]{:S(2)}) collective-permute-start(f32[32768]{0:T(1024)S(1)} %bitcast.186), channel_id=1, source_target_pairs={{0,6},{1,7},{2,0},{3,1},{4,2},{5,3},{6,4},{7,5},{8,14},{9,15},{10,... | collective-permute-start | bytes 393224 | tf_op jit(solution)/shard_map/ppermute | solution.py:33
  81.9 1.5 %collective-permute-start.9 = (f32[32768]{0:T(1024)S(1)}, f32[32768]{0:T(1024)S(1)}, u32[]{:S(2)}, u32[]{:S(2)}) collective-permute-start(f32[32768]{0:T(1024)S(1)} %bitcast.184), channel_id=1, source_target_pairs={{0,4},{1,5},{2,6},{3,7},{4,0},{5,1},{6,2},{7,3},{8,12},{9,13},{10,... | collective-permute-start | bytes 393224 | tf_op jit(solution)/shard_map/ppermute | solution.py:33
  84.0 1.3 %collective-permute-start.14 = (bf16[4,128,256]{2,1,0:T(8,128)(2,1)S(1)}, bf16[4,128,256]{2,1,0:T(8,128)(2,1)S(1)}, u32[]{:S(2)}, u32[]{:S(2)}) collective-permute-start(bf16[4,128,256]{2,1,0:T(8,128)(2,1)S(1)} %convolution_convert_fusion.6), channel_id=1, source_target_pairs={{0,7},{1,0},{2,1},{3,2},{4,3},{5,4},{6,5},{7,6},{8,15},{9,8},{10,9... | collective-permute-start | bytes 786440 | tf_op jit(solution)/shard_map/ppermute | solution.py:12
  86.0 3.2 %collective-permute-done.8 = f32[32768]{0:T(1024)S(1)} collective-permute-done((f32[32768]{0:T(1024)S(1)}, f32[32768]{0:T(1024)S(1)}, u32[]{:S(2)}, u32[]{:S(2)}) %collective-permute-start.8) | collective-permute-done | bytes 131104 | tf_op jit(solution)/shard_map/ppermute | solution.py:33
  89.9 3.3 %collective-permute-start.11 = (f32[8192]{0:T(1024)S(1)}, f32[8192]{0:T(1024)S(1)}, u32[]{:S(2)}, u32[]{:S(2)}) collective-permute-start(f32[8192]{0:T(1024)S(1)} %bitcast.189), channel_id=1, source_target_pairs={{0,8},{8,16},{16,24},{24,0},{1,9},{9,17},{17,25},{25,1},{2,10},{10... | collective-permute-start | bytes 98312 | tf_op jit(solution)/shard_map/ppermute | solution.py:33
  93.2 1.7 %collective-permute-start.12 = (f32[8192]{0:T(1024)S(1)}, f32[8192]{0:T(1024)S(1)}, u32[]{:S(2)}, u32[]{:S(2)}) collective-permute-start(f32[8192]{0:T(1024)S(1)} %bitcast.188), channel_id=1, source_target_pairs={{0,16},{8,24},{16,0},{24,8},{1,17},{9,25},{17,1},{25,9},{2,18},{10... | collective-permute-start | bytes 98312 | tf_op jit(solution)/shard_map/ppermute | solution.py:33
  95.7 1.3 %convolution_add_fusion.4 = f32[4,256,256]{2,1,0:T(8,128)} fusion(f32[4,256,256]{2,1,0:T(8,128)S(1)} %convolution_add_fusion, bf16[4,128,256]{2,1,0:T(8,128)(2,1)S(1)} %collective-permute-done.14, s32[4,128]{1,0:T(4,128)S(1)} %copy-done.14, pred[4,128]{1,0:T(4,128)(4,1)S(1)} %iota_compare_fusion.12), kind=kOutput, calls=%fused_computation.25 | convolution fusion | flops 67633152 | bytes 2361856 | tf_op jit(solution)/shard_map/dsn,dsh->dnh/dot_general | solution.py:354
  96.9 1.1 collective-permute-done.12
  99.0 3.1 %collective-permute-start.16 = (f32[8192]{0:T(1024)S(1)}, f32[8192]{0:T(1024)S(1)}, u32[]{:S(2)}, u32[]{:S(2)}) collective-permute-start(f32[8192]{0:T(1024)S(1)} %add_add_fusion.1), channel_id=1, source_target_pairs={{0,16},{8,24},{16,0},{24,8},{1,17},{9,25},{17,1},{25,9},{2,18},{10... | collective-permute-start | bytes 98312 | tf_op jit(solution)/shard_map/ppermute | solution.py:52
  102.1 1.0 collective-permute-start.17
  103.1 1.6 %collective-permute-done.15 = f32[8192]{0:T(1024)S(1)} collective-permute-done((f32[8192]{0:T(1024)S(1)}, f32[8192]{0:T(1024)S(1)}, u32[]{:S(2)}, u32[]{:S(2)}) %collective-permute-start.15) | collective-permute-done | bytes 32800 | tf_op jit(solution)/shard_map/ppermute | solution.py:52
  104.6 1.4 %collective-permute-done.17 = f32[8192]{0:T(1024)S(1)} collective-permute-done((f32[8192]{0:T(1024)S(1)}, f32[8192]{0:T(1024)S(1)}, u32[]{:S(2)}, u32[]{:S(2)}) %collective-permute-start.17) | collective-permute-done | bytes 32800 | tf_op jit(solution)/shard_map/ppermute | solution.py:52
  106.0 0.9 collective-permute-start.18
  107.8 2.8 %collective-permute-start.20 = (f32[32768]{0:T(1024)S(1)}, f32[32768]{0:T(1024)S(1)}, u32[]{:S(2)}, u32[]{:S(2)}) collective-permute-start(f32[32768]{0:T(1024)S(1)} %pad_maximum_fusion.5), channel_id=1, source_target_pairs={{0,6},{1,7},{2,0},{3,1},{4,2},{5,3},{6,4},{7,5},{8,14},{9,15},{10,... | collective-permute-start | bytes 393224 | tf_op jit(solution)/shard_map/ppermute | solution.py:52
  110.6 1.5 %collective-permute-done.18 = f32[32768]{0:T(1024)S(1)} collective-permute-done((f32[32768]{0:T(1024)S(1)}, f32[32768]{0:T(1024)S(1)}, u32[]{:S(2)}, u32[]{:S(2)}) %collective-permute-start.18) | collective-permute-done | bytes 131104 | tf_op jit(solution)/shard_map/ppermute | solution.py:52
  112.1 1.3 %collective-permute-done.19 = f32[32768]{0:T(1024)S(1)} collective-permute-done((f32[32768]{0:T(1024)S(1)}, f32[32768]{0:T(1024)S(1)}, u32[]{:S(2)}, u32[]{:S(2)}) %collective-permute-start.19) | collective-permute-done | bytes 131104 | tf_op jit(solution)/shard_map/ppermute | solution.py:52
  113.7 1.9 %collective-permute-done.21 = f32[131072]{0:T(1024)S(1)} collective-permute-done((f32[131072]{0:T(1024)S(1)}, f32[131072]{0:T(1024)S(1)}, u32[]{:S(2)}, u32[]{:S(2)}) %collective-permute-start.21) | collective-permute-done | bytes 524320 | tf_op jit(solution)/shard_map/ppermute | solution.py:52
  (113 shorter events, 22.6 us)
Async XLA Ops:
  0.6 13.8 %copy-start = (bf16[256,256]{1,0:T(8,128)(2,1)S(1)}, bf16[256,256]{1,0:T(8,128)(2,1)}, u32[]{:S(2)}) copy-start(bf16[256,256]{1,0:T(8,128)(2,1)} %param.15) | copy-start | bytes 393220
  3.5 9.6 %collective-permute-start = (bf16[4,128,256]{2,1,0:T(8,128)(2,1)}, bf16[4,128,256]{2,1,0:T(8,128)(2,1)}, u32[]{:S(2)}, u32[]{:S(2)}) collective-permute-start(bf16[4,128,256]{2,1,0:T(8,128)(2,1)} %convolution_convert_fusion.7), channel_id=1, source_target_pairs={{0,1},{1,2},{2,3},{3,4},{4,5},{5,6},{6,7},{7,0},{8,9},{9,10},{10,1... | collective-permute-start | bytes 786440 | tf_op jit(solution)/shard_map/ppermute | solution.py:12
  5.2 3.1 %copy-start.13 = (s32[4,1024]{1,0:T(4,128)S(1)}, s32[4,1024]{1,0:T(4,128)}, u32[]{:S(2)}) copy-start(s32[4,1024]{1,0:T(4,128)} %param.12) | copy-start | bytes 49156
  5.2 3.1 %copy-start.15 = (s32[4,1024]{1,0:T(4,128)S(1)}, s32[4,1024]{1,0:T(4,128)}, u32[]{:S(2)}) copy-start(s32[4,1024]{1,0:T(4,128)} %param.11) | copy-start | bytes 49156
  8.3 1.4 %copy-start.2 = (bf16[16,1,1,64,256]{4,3,2,1,0:T(8,128)(2,1)S(1)}, bf16[16,1,1,64,256]{4,3,2,1,0:T(8,128)(2,1)}, u32[]{:S(2)}) copy-start(bf16[16,1,1,64,256]{4,3,2,1,0:T(8,128)(2,1)} %param.19) | copy-start | bytes 1572868
  10.5 1.3 %copy-start.1 = (bf16[4,256,256]{2,1,0:T(8,128)(2,1)S(1)}, bf16[4,256,256]{2,1,0:T(8,128)(2,1)}, u32[]{:S(2)}) copy-start(bf16[4,256,256]{2,1,0:T(8,128)(2,1)} %param.10) | copy-start | bytes 1572868
  14.4 1.4 %copy-start.3 = (bf16[4,256,256]{2,1,0:T(8,128)(2,1)}, bf16[4,256,256]{2,1,0:T(8,128)(2,1)S(1)}, u32[]{:S(2)}) copy-start(bf16[4,256,256]{2,1,0:T(8,128)(2,1)S(1)} %fusion.15) | copy-start | bytes 1572868
  15.9 15.4 %copy-start.10 = (bf16[256,256]{1,0:T(8,128)(2,1)S(1)}, bf16[256,256]{1,0:T(8,128)(2,1)}, u32[]{:S(2)}) copy-start(bf16[256,256]{1,0:T(8,128)(2,1)} %param.16) | copy-start | bytes 393220
  16.0 8.5 %collective-permute-start.1 = (bf16[4,64,256]{2,1,0:T(8,128)(2,1)S(1)}, bf16[4,64,256]{2,1,0:T(8,128)(2,1)S(1)}, u32[]{:S(2)}, u32[]{:S(2)}) collective-permute-start(bf16[4,64,256]{2,1,0:T(8,128)(2,1)S(1)} %get-tuple-element.42), channel_id=1, source_target_pairs={{0,8},{8,16},{16,24},{24,0},{1,9},{9,17},{17,25},{25,1},{2,10},{10... | collective-permute-start | bytes 393224 | tf_op jit(solution)/shard_map/ppermute | solution.py:98
  18.7 12.1 %collective-permute-start.2 = (bf16[4,64,256]{2,1,0:T(8,128)(2,1)S(1)}, bf16[4,64,256]{2,1,0:T(8,128)(2,1)S(1)}, u32[]{:S(2)}, u32[]{:S(2)}) collective-permute-start(bf16[4,64,256]{2,1,0:T(8,128)(2,1)S(1)} %get-tuple-element.41), channel_id=1, source_target_pairs={{0,16},{8,24},{16,0},{24,8},{1,17},{9,25},{17,1},{25,9},{2,18},{10... | collective-permute-start | bytes 393224 | tf_op jit(solution)/shard_map/ppermute | solution.py:98
  21.3 9.6 %collective-permute-start.3 = (bf16[4,64,256]{2,1,0:T(8,128)(2,1)S(1)}, bf16[4,64,256]{2,1,0:T(8,128)(2,1)S(1)}, u32[]{:S(2)}, u32[]{:S(2)}) collective-permute-start(bf16[4,64,256]{2,1,0:T(8,128)(2,1)S(1)} %get-tuple-element.40), channel_id=1, source_target_pairs={{0,24},{8,0},{16,8},{24,16},{1,25},{9,1},{17,9},{25,17},{2,26},{10... | collective-permute-start | bytes 393224 | tf_op jit(solution)/shard_map/ppermute | solution.py:98
  50.1 4.2 %copy-start.6 = (bf16[8,128,4,64]{1,3,2,0:T(8,128)(2,1)S(1)}, bf16[8,128,4,64]{1,3,2,0:T(8,128)(2,1)}, u32[]{:S(2)}) copy-start(bf16[8,128,4,64]{1,3,2,0:T(8,128)(2,1)} %copy.37) | copy-start | bytes 1572868
  54.3 1.0 copy-start.5
  54.3 1.9 %copy-start.16 = (f32[8,4,128,128]{2,3,1,0:T(8,128)S(1)}, f32[8,4,128,128]{2,3,1,0:T(8,128)}, u32[]{:S(2)}) copy-start(f32[8,4,128,128]{2,3,1,0:T(8,128)} %get-tuple-element.58) | copy-start | bytes 6291460
  57.0 0.9 copy-start.11
  57.9 1.1 copy-start.12
  59.0 0.9 copy-start.9
  60.6 13.9 %copy-start.8 = (f32[4,256,256]{2,1,0:T(8,128)S(1)}, f32[4,256,256]{2,1,0:T(8,128)}, u32[]{:S(2)}) copy-start(f32[4,256,256]{2,1,0:T(8,128)} %get-tuple-element.56) | copy-start | bytes 3145732
  60.6 8.6 %collective-permute-start.4 = (bf16[4,64,256]{2,1,0:T(8,128)(2,1)S(1)}, bf16[4,64,256]{2,1,0:T(8,128)(2,1)S(1)}, u32[]{:S(2)}, u32[]{:S(2)}) collective-permute-start(bf16[4,64,256]{2,1,0:T(8,128)(2,1)S(1)} %get-tuple-element.35), channel_id=1, source_target_pairs={{0,8},{8,16},{16,24},{24,0},{1,9},{9,17},{17,25},{25,1},{2,10},{10... | collective-permute-start | bytes 393224 | tf_op jit(solution)/shard_map/ppermute | solution.py:98
  63.9 10.5 %collective-permute-start.5 = (bf16[4,64,256]{2,1,0:T(8,128)(2,1)S(1)}, bf16[4,64,256]{2,1,0:T(8,128)(2,1)S(1)}, u32[]{:S(2)}, u32[]{:S(2)}) collective-permute-start(bf16[4,64,256]{2,1,0:T(8,128)(2,1)S(1)} %get-tuple-element.34), channel_id=1, source_target_pairs={{0,16},{8,24},{16,0},{24,8},{1,17},{9,25},{17,1},{25,9},{2,18},{10... | collective-permute-start | bytes 393224 | tf_op jit(solution)/shard_map/ppermute | solution.py:98
  65.4 9.0 %collective-permute-start.6 = (bf16[4,64,256]{2,1,0:T(8,128)(2,1)S(1)}, bf16[4,64,256]{2,1,0:T(8,128)(2,1)S(1)}, u32[]{:S(2)}, u32[]{:S(2)}) collective-permute-start(bf16[4,64,256]{2,1,0:T(8,128)(2,1)S(1)} %get-tuple-element.33), channel_id=1, source_target_pairs={{0,24},{8,0},{16,8},{24,16},{1,25},{9,1},{17,9},{25,17},{2,26},{10... | collective-permute-start | bytes 393224 | tf_op jit(solution)/shard_map/ppermute | solution.py:98
  66.9 7.9 %copy-start.4 = (bf16[4,256,256]{2,1,0:T(8,128)(2,1)S(1)}, bf16[4,256,256]{2,1,0:T(8,128)(2,1)}, u32[]{:S(2)}) copy-start(bf16[4,256,256]{2,1,0:T(8,128)(2,1)} %copy-done.3) | copy-start | bytes 1572868
  76.1 1.3 %copy-start.7 = (bf16[4,256,256]{2,1,0:T(8,128)(2,1)S(1)}, bf16[4,256,256]{2,1,0:T(8,128)(2,1)}, u32[]{:S(2)}) copy-start(bf16[4,256,256]{2,1,0:T(8,128)(2,1)} %fusion.17) | copy-start | bytes 1572868
  77.0 2.0 %collective-permute-start.7 = (f32[131072]{0:T(1024)S(1)}, f32[131072]{0:T(1024)S(1)}, u32[]{:S(2)}, u32[]{:S(2)}) collective-permute-start(f32[131072]{0:T(1024)S(1)} %bitcast.181), channel_id=1, source_target_pairs={{0,1},{1,0},{2,3},{3,2},{4,5},{5,4},{6,7},{7,6},{8,9},{9,8},{10,11... | collective-permute-start | bytes 1572872 | tf_op jit(solution)/shard_map/ppermute | solution.py:33
  79.3 16.4 %copy-start.14 = (s32[4,128]{1,0:T(4,128)S(1)}, s32[4,128]{1,0:T(4,128)}, u32[]{:S(2)}) copy-start(s32[4,128]{1,0:T(4,128)} %param.13) | copy-start | bytes 6148
  79.8 6.2 %collective-permute-start.10 = (f32[32768]{0:T(1024)S(1)}, f32[32768]{0:T(1024)S(1)}, u32[]{:S(2)}, u32[]{:S(2)}) collective-permute-start(f32[32768]{0:T(1024)S(1)} %bitcast.186), channel_id=1, source_target_pairs={{0,6},{1,7},{2,0},{3,1},{4,2},{5,3},{6,4},{7,5},{8,14},{9,15},{10,... | collective-permute-start | bytes 393224 | tf_op jit(solution)/shard_map/ppermute | solution.py:33
  81.6 7.6 %collective-permute-start.8 = (f32[32768]{0:T(1024)S(1)}, f32[32768]{0:T(1024)S(1)}, u32[]{:S(2)}, u32[]{:S(2)}) collective-permute-start(f32[32768]{0:T(1024)S(1)} %bitcast.185), channel_id=1, source_target_pairs={{0,2},{1,3},{2,4},{3,5},{4,6},{5,7},{6,0},{7,1},{8,10},{9,11},{10,... | collective-permute-start | bytes 393224 | tf_op jit(solution)/shard_map/ppermute | solution.py:33
  81.9 7.8 %collective-permute-start.9 = (f32[32768]{0:T(1024)S(1)}, f32[32768]{0:T(1024)S(1)}, u32[]{:S(2)}, u32[]{:S(2)}) collective-permute-start(f32[32768]{0:T(1024)S(1)} %bitcast.184), channel_id=1, source_target_pairs={{0,4},{1,5},{2,6},{3,7},{4,0},{5,1},{6,2},{7,3},{8,12},{9,13},{10,... | collective-permute-start | bytes 393224 | tf_op jit(solution)/shard_map/ppermute | solution.py:33
  84.0 11.7 %collective-permute-start.14 = (bf16[4,128,256]{2,1,0:T(8,128)(2,1)S(1)}, bf16[4,128,256]{2,1,0:T(8,128)(2,1)S(1)}, u32[]{:S(2)}, u32[]{:S(2)}) collective-permute-start(bf16[4,128,256]{2,1,0:T(8,128)(2,1)S(1)} %convolution_convert_fusion.6), channel_id=1, source_target_pairs={{0,7},{1,0},{2,1},{3,2},{4,3},{5,4},{6,5},{7,6},{8,15},{9,8},{10,9... | collective-permute-start | bytes 786440 | tf_op jit(solution)/shard_map/ppermute | solution.py:12
  89.9 7.0 %collective-permute-start.11 = (f32[8192]{0:T(1024)S(1)}, f32[8192]{0:T(1024)S(1)}, u32[]{:S(2)}, u32[]{:S(2)}) collective-permute-start(f32[8192]{0:T(1024)S(1)} %bitcast.189), channel_id=1, source_target_pairs={{0,8},{8,16},{16,24},{24,0},{1,9},{9,17},{17,25},{25,1},{2,10},{10... | collective-permute-start | bytes 98312 | tf_op jit(solution)/shard_map/ppermute | solution.py:33
  93.2 4.8 %collective-permute-start.12 = (f32[8192]{0:T(1024)S(1)}, f32[8192]{0:T(1024)S(1)}, u32[]{:S(2)}, u32[]{:S(2)}) collective-permute-start(f32[8192]{0:T(1024)S(1)} %bitcast.188), channel_id=1, source_target_pairs={{0,16},{8,24},{16,0},{24,8},{1,17},{9,25},{17,1},{25,9},{2,18},{10... | collective-permute-start | bytes 98312 | tf_op jit(solution)/shard_map/ppermute | solution.py:33
  94.9 3.9 %collective-permute-start.13 = (f32[8192]{0:T(1024)S(1)}, f32[8192]{0:T(1024)S(1)}, u32[]{:S(2)}, u32[]{:S(2)}) collective-permute-start(f32[8192]{0:T(1024)S(1)} %bitcast.187), channel_id=1, source_target_pairs={{0,24},{8,0},{16,8},{24,16},{1,25},{9,1},{17,9},{25,17},{2,26},{10... | collective-permute-start | bytes 98312 | tf_op jit(solution)/shard_map/ppermute | solution.py:33
  98.8 5.8 %collective-permute-start.15 = (f32[8192]{0:T(1024)S(1)}, f32[8192]{0:T(1024)S(1)}, u32[]{:S(2)}, u32[]{:S(2)}) collective-permute-start(f32[8192]{0:T(1024)S(1)} %add_add_fusion.1), channel_id=1, source_target_pairs={{0,8},{8,16},{16,24},{24,0},{1,9},{9,17},{17,25},{25,1},{2,10},{10... | collective-permute-start | bytes 98312 | tf_op jit(solution)/shard_map/ppermute | solution.py:52
  99.0 5.6 %collective-permute-start.16 = (f32[8192]{0:T(1024)S(1)}, f32[8192]{0:T(1024)S(1)}, u32[]{:S(2)}, u32[]{:S(2)}) collective-permute-start(f32[8192]{0:T(1024)S(1)} %add_add_fusion.1), channel_id=1, source_target_pairs={{0,16},{8,24},{16,0},{24,8},{1,17},{9,25},{17,1},{25,9},{2,18},{10... | collective-permute-start | bytes 98312 | tf_op jit(solution)/shard_map/ppermute | solution.py:52
  102.1 3.9 %collective-permute-start.17 = (f32[8192]{0:T(1024)S(1)}, f32[8192]{0:T(1024)S(1)}, u32[]{:S(2)}, u32[]{:S(2)}) collective-permute-start(f32[8192]{0:T(1024)S(1)} %add_add_fusion.1), channel_id=1, source_target_pairs={{0,24},{8,0},{16,8},{24,16},{1,25},{9,1},{17,9},{25,17},{2,26},{10... | collective-permute-start | bytes 98312 | tf_op jit(solution)/shard_map/ppermute | solution.py:52
  106.0 6.0 %collective-permute-start.18 = (f32[32768]{0:T(1024)S(1)}, f32[32768]{0:T(1024)S(1)}, u32[]{:S(2)}, u32[]{:S(2)}) collective-permute-start(f32[32768]{0:T(1024)S(1)} %pad_maximum_fusion.5), channel_id=1, source_target_pairs={{0,2},{1,3},{2,4},{3,5},{4,6},{5,7},{6,0},{7,1},{8,10},{9,11},{10,... | collective-permute-start | bytes 393224 | tf_op jit(solution)/shard_map/ppermute | solution.py:52
  106.9 6.4 %collective-permute-start.19 = (f32[32768]{0:T(1024)S(1)}, f32[32768]{0:T(1024)S(1)}, u32[]{:S(2)}, u32[]{:S(2)}) collective-permute-start(f32[32768]{0:T(1024)S(1)} %pad_maximum_fusion.5), channel_id=1, source_target_pairs={{0,4},{1,5},{2,6},{3,7},{4,0},{5,1},{6,2},{7,3},{8,12},{9,13},{10,... | collective-permute-start | bytes 393224 | tf_op jit(solution)/shard_map/ppermute | solution.py:52
  107.8 5.7 %collective-permute-start.20 = (f32[32768]{0:T(1024)S(1)}, f32[32768]{0:T(1024)S(1)}, u32[]{:S(2)}, u32[]{:S(2)}) collective-permute-start(f32[32768]{0:T(1024)S(1)} %pad_maximum_fusion.5), channel_id=1, source_target_pairs={{0,6},{1,7},{2,0},{3,1},{4,2},{5,3},{6,4},{7,5},{8,14},{9,15},{10,... | collective-permute-start | bytes 393224 | tf_op jit(solution)/shard_map/ppermute | solution.py:52
  113.6 2.0 %collective-permute-start.21 = (f32[131072]{0:T(1024)S(1)}, f32[131072]{0:T(1024)S(1)}, u32[]{:S(2)}, u32[]{:S(2)}) collective-permute-start(f32[131072]{0:T(1024)S(1)} %pad_maximum_fusion.4), channel_id=1, source_target_pairs={{0,1},{1,0},{2,3},{3,2},{4,5},{5,4},{6,7},{7,6},{8,9},{9,8},{10,11... | collective-permute-start | bytes 1572872 | tf_op jit(solution)/shard_map/ppermute | solution.py:52

commit v10 on v8

--- a/solution.py
+++ b/solution.py
@@ -310,10 +310,23 @@
     preact = jnp.einsum("drh,hk->drk", aggregate, w_message, preferred_element_type=jnp.float32)
     hidden = (states_f + jax.nn.silu(preact)).astype(jnp.bfloat16)
 
-    node_major = exchange(hidden, "day", 1, 0)
+    day_count = lax.axis_size("day")
     upstream = cotangent.reshape(cotangent.shape[0], -1, width)
-    attn_grads, back = attend_blocked(node_major, upstream, w_query, w_key, w_value)
-    back_days = exchange(back, "day", 0, 1)
+    piece = node_local // day_count
+    halves = 2 if piece % 2 == 0 and (piece // 2) % max(1, 128 // upstream.shape[0]) == 0 else 1
+    part = piece // halves
+    split_hidden = hidden.reshape(days_local, day_count, halves, part, width)
+    attn_grads, backs = None, []
+    for half in range(halves):
+        node_major = exchange(
+            split_hidden[:, :, half].reshape(days_local, day_count * part, width), "day", 1, 0
+        )
+        grads, back = attend_blocked(
+            node_major, upstream[:, half * part : (half + 1) * part], w_query, w_key, w_value
+        )
+        attn_grads = grads if attn_grads is None else tuple(a + b for a, b in zip(attn_grads, grads))
+        backs.append(exchange(back, "day", 0, 1).reshape(days_local, day_count, part, width))
+    back_days = jnp.stack(backs, axis=2).reshape(days_local, node_local, width)
 
     sigmoid_val = jax.nn.sigmoid(preact)
     pre_grad = (

time: 117 us -> 139 us (1.19)
  local copies, waits for them, and re-layouts: 23.9 us -> 32.3 us
  matrix products: 23 us -> 30.9 us
  starting transfers between devices: 31.9 us -> 39.5 us
  waiting for transfers between devices: 24.7 us -> 21.1 us
    ppermute x6 -> x12, starting transfers between devices: 12 us -> 19.6 us  [exchange(): lax.ppermute(send, axis, [(i, (i + shift) % count) for i in range(count)])]
    dot_general x4 -> x8, matrix products: 3.83 us -> 8.84 us  [contract(): return jnp.einsum(spec, left, right, preferred_element_type=jnp.float32)]
    reshape x5 -> x10, local copies, waits for them, and re-layouts: 3.61 us -> 7.23 us  [blocks(): return matrix.reshape(groups, block, HEADS, head_dim)]
    ppermute x6 -> x12, waiting for transfers between devices: 10.2 us -> 6.85 us  [exchange(): lax.ppermute(send, axis, [(i, (i + shift) % count) for i in range(count)])]
    dot_general x3 -> x6, matrix products: 0.86 us -> 2.76 us  [project(): jnp.dot(flat, weight, preferred_element_type=jnp.float32)]
    ppermute x7, starting transfers between devices: 8.83 us -> 10.7 us  [_gather_step(): lax.ppermute(flat, axis, _group_pairs(axis, stride, group, shift))]
    gather x2 -> x4, local copies, waits for them, and re-layouts: 1.16 us -> 2.67 us  [exchange(): jnp.take(jnp.stack(got), (mine - jnp.arange(count)) % count, axis=0)]
    unnamed x70 -> x76, local copies, waits for them, and re-layouts: 6.17 us -> 7.1 us
  transfers between devices with their start and end apart: 22 -> 28, of which waited for: 15 -> 18; matrix products, arithmetic and copies ran while one was open for 15% -> 14% of each run, Pallas kernels for 0% -> 0%
where the time goes in v10:
time: 139 us; the launch traced here: 138 us
  starting transfers between devices  39.5 us (28%)
  local copies, waits for them, and re-layouts  32.3 us (23%)
  matrix products  30.9 us (22%)
  waiting for transfers between devices  21.1 us (15%)
  other arithmetic  12.7 us (9%)
  between operations  1.74 us (1%)
    ppermute x12, starting transfers between devices, exchange(): lax.ppermute(send, axis, [(i, (i + shift) % count) for i in range(count)])  19.6 us
    ppermute x7, starting transfers between devices, _gather_step(): lax.ppermute(flat, axis, _group_pairs(axis, stride, group, shift))  10.7 us
    dot_general x8, matrix products, contract(): return jnp.einsum(spec, left, right, preferred_element_type=jnp.float32)  8.84 us
    ppermute x7, starting transfers between devices, _scatter_step(): lax.ppermute(send, axis, _group_pairs(axis, stride, group, shift))  8.69 us
    ppermute x7, waiting for transfers between devices, _gather_step(): lax.ppermute(flat, axis, _group_pairs(axis, stride, group, shift))  7.5 us
    reshape x10, local copies, waits for them, and re-layouts, blocks(): return matrix.reshape(groups, block, HEADS, head_dim)  7.23 us
    unnamed x76, local copies, waits for them, and re-layouts  7.1 us
    ppermute x12, waiting for transfers between devices, exchange(): lax.ppermute(send, axis, [(i, (i + shift) % count) for i in range(count)])  6.85 us
  transfers between devices with their start and end apart: 28, of which 18 were waited for; matrix products, arithmetic and copies ran while one was open for 14% of the time, Pallas kernels for 0%

profile of v10, /device:TPU:0, one launch (start us, length us, event | category | flops | bytes accessed | tf_op | source)
XLA Modules:
  0.0 138.1 jit_solution(11152118872611359091)
XLA Ops:
  2.0 2.1 %convolution_convert_fusion.13 = bf16[4,128,256]{2,1,0:T(8,128)(2,1)} fusion(bf16[4,256,256]{2,1,0:T(8,128)(2,1)} %param.12, s32[4,128]{1,0:T(4,128)} %param.15, pred[4,128]{1,0:T(4,128)(4,1)S(1)} %iota_compare_fusion.12), kind=kOutput, calls=%fused_computation.71 | convolution fusion | flops 67502080 | bytes 788992 | tf_op jit(solution)/shard_map/dsn,dnh->dsh/dot_general | solution.py:287
  6.7 1.6 %fusion.28 = bf16[4,256,256]{2,1,0:T(8,128)(2,1)S(1)} fusion(s32[4,1024]{1,0:T(4,128)S(1)} %copy-done.32, s32[4,1024]{1,0:T(4,128)S(1)} %copy-done.22), kind=kOutput, calls=%fused_computation.50 | convolution fusion | flops 539230208 | bytes 557056 | tf_op jit(solution)/shard_map/der,des->drs/dot_general | solution.py:296
  8.3 2.0 %fusion.29 = bf16[4,256,128]{2,1,0:T(8,128)(2,1)} fusion(s32[4,1024]{1,0:T(4,128)S(1)} %copy-done.22, s32[128]{0:T(128)S(1)} %iota_add_fusion, s32[4,1024]{1,0:T(4,128)S(1)} %copy-done.32), kind=kOutput, calls=%fused_computation.57 | convolution fusion | flops 270139392 | bytes 295424 | tf_op jit(solution)/shard_map/der,des->drs/dot_general | solution.py:299
  11.9 1.1 copy.98
  15.7 1.3 fusion.25
  17.0 1.3 fusion.43
  18.5 2.6 %collective-permute-start.1 = (bf16[4,32,256]{2,1,0:T(8,128)(2,1)S(1)}, bf16[4,32,256]{2,1,0:T(8,128)(2,1)S(1)}, u32[]{:S(2)}, u32[]{:S(2)}) collective-permute-start(bf16[4,32,256]{2,1,0:T(8,128)(2,1)S(1)} %get-tuple-element.73), channel_id=1, source_target_pairs={{0,8},{8,16},{16,24},{24,0},{1,9},{9,17},{17,25},{25,1},{2,10},{10... | collective-permute-start | bytes 196616 | tf_op jit(solution)/shard_map/ppermute | solution.py:88
  21.1 2.6 %collective-permute-start.2 = (bf16[4,32,256]{2,1,0:T(8,128)(2,1)S(1)}, bf16[4,32,256]{2,1,0:T(8,128)(2,1)S(1)}, u32[]{:S(2)}, u32[]{:S(2)}) collective-permute-start(bf16[4,32,256]{2,1,0:T(8,128)(2,1)S(1)} %get-tuple-element.72), channel_id=1, source_target_pairs={{0,16},{8,24},{16,0},{24,8},{1,17},{9,25},{17,1},{25,9},{2,18},{10... | collective-permute-start | bytes 196616 | tf_op jit(solution)/shard_map/ppermute | solution.py:88
  23.7 1.3 collective-permute-start.3
  26.2 2.8 %collective-permute-start.9 = (bf16[4,32,256]{2,1,0:T(8,128)(2,1)S(1)}, bf16[4,32,256]{2,1,0:T(8,128)(2,1)S(1)}, u32[]{:S(2)}, u32[]{:S(2)}) collective-permute-start(bf16[4,32,256]{2,1,0:T(8,128)(2,1)S(1)} %get-tuple-element.59), channel_id=1, source_target_pairs={{0,24},{8,0},{16,8},{24,16},{1,25},{9,1},{17,9},{25,17},{2,26},{10... | collective-permute-start | bytes 196616 | tf_op jit(solution)/shard_map/ppermute | solution.py:88
  30.3 1.8 %collective-permute-done.7 = bf16[4,32,256]{2,1,0:T(8,128)(2,1)S(1)} collective-permute-done((bf16[4,32,256]{2,1,0:T(8,128)(2,1)S(1)}, bf16[4,32,256]{2,1,0:T(8,128)(2,1)S(1)}, u32[]{:S(2)}, u32[]{:S(2)}) %collective-permute-start.7) | collective-permute-done | bytes 65568 | tf_op jit(solution)/shard_map/ppermute | solution.py:88
  32.1 2.5 %collective-permute-done.8 = bf16[4,32,256]{2,1,0:T(8,128)(2,1)S(1)} collective-permute-done((bf16[4,32,256]{2,1,0:T(8,128)(2,1)S(1)}, bf16[4,32,256]{2,1,0:T(8,128)(2,1)S(1)}, u32[]{:S(2)}, u32[]{:S(2)}) %collective-permute-start.8) | collective-permute-done | bytes 65568 | tf_op jit(solution)/shard_map/ppermute | solution.py:88
  39.8 1.2 reshape.591
  42.0 1.3 convolution_bitcast_fusion
  43.3 1.5 %fusion.113 = (f32[4,4,128]{2,1,0:T(4,128)S(1)}, f32[4,4,128,128]{2,3,1,0:T(8,128)}) fusion(bf16[4,128,4,64]{1,3,2,0:T(8,128)(2,1)S(1)} %copy-done.13, bf16[4,128,4,64]{1,3,2,0:T(8,128)(2,1)S(1)} %copy-done.15, pred[128,128]{0,1:T(8,128)(4,1)S(1)} %copy-done.23), kind=kOutput, calls=%fused_computation.297 | convolution fusion | flops 34603136 | bytes 1597440 | tf_op jit(solution)/shard_map/sub | solution.py:233
  44.8 2.6 %fusion.26 = bf16[4,4,128,128]{2,3,1,0:T(8,128)(2,1)S(1)} fusion(f32[4,4,128,128]{2,3,1,0:T(8,128)} %convolution_bitcast_fusion, f32[4,4,128,128]{2,3,1,0:T(8,128)} %get-tuple-element.93, f32[4,4,128]{2,1,0:T(4,128)S(1)} %get-tuple-element.92), kind=kOutput, calls=%fused_computation.48 | output fusion | flops 1837183 | bytes 2629632 | tf_op jit(solution)/shard_map/sub | solution.py:239
  47.4 1.0 fusion.37
  48.4 1.2 fusion.38
  49.6 1.5 %fusion.39 = bf16[4,128,4,64]{1,3,2,0:T(8,128)(2,1)} fusion(bf16[4,128,4,64]{1,3,2,0:T(8,128)(2,1)S(1)} %copy-done.8, f32[4,4,128]{2,1,0:T(4,128)S(1)} %get-tuple-element.92, bf16[4,128,4,64]{1,3,2,0:T(8,128)(2,1)S(1)} %copy-done.13, bf16[4,128,4,64]{1,3,2,0:T(8,128)(2,1)S(1)} %copy-done.15, pred[128,128]{0,1:T(8,128)(4,1)S(1)} %copy-done.23), kind=kOutput, calls=%fused_computation.79 | convolution fusion | flops 68552832 | bytes 1073152 | tf_op jit(solution)/shard_map/ghij,gihd->gjhd/dot_general | solution.py:228
  52.7 1.2 reshape.590
  56.4 2.5 %fusion.112 = (f32[4,4,128]{2,1,0:T(4,128)S(1)}, f32[4,4,128,128]{2,3,1,0:T(8,128)}) fusion(bf16[4,128,4,64]{1,3,2,0:T(8,128)(2,1)S(1)} %copy-done.12, bf16[4,128,4,64]{1,3,2,0:T(8,128)(2,1)} %copy.88, pred[128,128]{0,1:T(8,128)(4,1)S(1)} %copy-done.24), kind=kOutput, calls=%fused_computation.296 | convolution fusion | flops 34603136 | bytes 1597440 | tf_op jit(solution)/shard_map/sub | solution.py:233
  62.0 1.2 fusion.35
  63.2 1.5 %fusion.36 = bf16[4,128,4,64]{1,3,2,0:T(8,128)(2,1)} fusion(bf16[4,128,4,64]{1,3,2,0:T(8,128)(2,1)S(1)} %copy.87, f32[4,4,128]{2,1,0:T(4,128)S(1)} %get-tuple-element.90, bf16[4,128,4,64]{1,3,2,0:T(8,128)(2,1)S(1)} %copy-done.12, bf16[4,128,4,64]{1,3,2,0:T(8,128)(2,1)S(1)} %copy-done.14, pred[128,128]{0,1:T(8,128)(4,1)S(1)} %copy-done.24), kind=kOutput, calls=%fused_computation.76 | convolution fusion | flops 68552832 | bytes 1073152 | tf_op jit(solution)/shard_map/ghij,gihd->gjhd/dot_general | solution.py:228
  64.6 1.2 copy.110
  65.9 1.2 copy.113
  68.6 2.0 %collective-permute-start.10 = (bf16[4,32,256]{2,0,1:T(4,128)(2,1)S(1)}, bf16[4,32,256]{2,0,1:T(4,128)(2,1)S(1)}, u32[]{:S(2)}, u32[]{:S(2)}) collective-permute-start(bf16[4,32,256]{2,0,1:T(4,128)(2,1)S(1)} %get-tuple-element.49), channel_id=1, source_target_pairs={{0,8},{8,16},{16,24},{24,0},{1,9},{9,17},{17,25},{25,1},{2,10},{10... | collective-permute-start | bytes 196616 | tf_op jit(solution)/shard_map/ppermute | solution.py:88
  70.6 1.7 %collective-permute-start.11 = (bf16[4,32,256]{2,0,1:T(4,128)(2,1)S(1)}, bf16[4,32,256]{2,0,1:T(4,128)(2,1)S(1)}, u32[]{:S(2)}, u32[]{:S(2)}) collective-permute-start(bf16[4,32,256]{2,0,1:T(4,128)(2,1)S(1)} %get-tuple-element.48), channel_id=1, source_target_pairs={{0,16},{8,24},{16,0},{24,8},{1,17},{9,25},{17,1},{25,9},{2,18},{10... | collective-permute-start | bytes 196616 | tf_op jit(solution)/shard_map/ppermute | solution.py:88
  76.6 1.6 %collective-permute-start.4 = (bf16[4,32,256]{2,0,1:T(4,128)(2,1)S(1)}, bf16[4,32,256]{2,0,1:T(4,128)(2,1)S(1)}, u32[]{:S(2)}, u32[]{:S(2)}) collective-permute-start(bf16[4,32,256]{2,0,1:T(4,128)(2,1)S(1)} %get-tuple-element.37), channel_id=1, source_target_pairs={{0,8},{8,16},{16,24},{24,0},{1,9},{9,17},{17,25},{25,1},{2,10},{10... | collective-permute-start | bytes 196616 | tf_op jit(solution)/shard_map/ppermute | solution.py:88
  78.2 1.2 collective-permute-start.5
  80.7 1.9 %collective-permute-start.6 = (bf16[4,32,256]{2,0,1:T(4,128)(2,1)S(1)}, bf16[4,32,256]{2,0,1:T(4,128)(2,1)S(1)}, u32[]{:S(2)}, u32[]{:S(2)}) collective-permute-start(bf16[4,32,256]{2,0,1:T(4,128)(2,1)S(1)} %get-tuple-element.35), channel_id=1, source_target_pairs={{0,24},{8,0},{16,8},{24,16},{1,25},{9,1},{17,9},{25,17},{2,26},{10... | collective-permute-start | bytes 196616 | tf_op jit(solution)/shard_map/ppermute | solution.py:88
  83.6 1.5 %collective-permute-done.5 = bf16[4,32,256]{2,0,1:T(4,128)(2,1)S(1)} collective-permute-done((bf16[4,32,256]{2,0,1:T(4,128)(2,1)S(1)}, bf16[4,32,256]{2,0,1:T(4,128)(2,1)S(1)}, u32[]{:S(2)}, u32[]{:S(2)}) %collective-permute-start.5) | collective-permute-done | bytes 65568 | tf_op jit(solution)/shard_map/ppermute | solution.py:88
  93.9 1.6 %collective-permute-start.14 = (f32[32768]{0:T(1024)S(1)}, f32[32768]{0:T(1024)S(1)}, u32[]{:S(2)}, u32[]{:S(2)}) collective-permute-start(f32[32768]{0:T(1024)S(1)} %bitcast.371), channel_id=1, source_target_pairs={{0,2},{1,3},{2,4},{3,5},{4,6},{5,7},{6,0},{7,1},{8,10},{9,11},{10,... | collective-permute-start | bytes 393224 | tf_op jit(solution)/shard_map/ppermute | solution.py:33
  95.4 1.2 collective-permute-start.15
  96.6 1.8 %collective-permute-start.16 = (f32[32768]{0:T(1024)S(1)}, f32[32768]{0:T(1024)S(1)}, u32[]{:S(2)}, u32[]{:S(2)}) collective-permute-start(f32[32768]{0:T(1024)S(1)} %bitcast.369), channel_id=1, source_target_pairs={{0,6},{1,7},{2,0},{3,1},{4,2},{5,3},{6,4},{7,5},{8,14},{9,15},{10,... | collective-permute-start | bytes 393224 | tf_op jit(solution)/shard_map/ppermute | solution.py:33
  99.0 2.1 %collective-permute-done.14 = f32[32768]{0:T(1024)S(1)} collective-permute-done((f32[32768]{0:T(1024)S(1)}, f32[32768]{0:T(1024)S(1)}, u32[]{:S(2)}, u32[]{:S(2)}) %collective-permute-start.14) | collective-permute-done | bytes 131104 | tf_op jit(solution)/shard_map/ppermute | solution.py:33
  101.2 2.0 %collective-permute-done.15 = f32[32768]{0:T(1024)S(1)} collective-permute-done((f32[32768]{0:T(1024)S(1)}, f32[32768]{0:T(1024)S(1)}, u32[]{:S(2)}, u32[]{:S(2)}) %collective-permute-start.15) | collective-permute-done | bytes 131104 | tf_op jit(solution)/shard_map/ppermute | solution.py:33
  103.5 1.5 %collective-permute-start.17 = (f32[8192]{0:T(1024)S(1)}, f32[8192]{0:T(1024)S(1)}, u32[]{:S(2)}, u32[]{:S(2)}) collective-permute-start(f32[8192]{0:T(1024)S(1)} %bitcast.389), channel_id=1, source_target_pairs={{0,8},{8,16},{16,24},{24,0},{1,9},{9,17},{17,25},{25,1},{2,10},{10... | collective-permute-start | bytes 98312 | tf_op jit(solution)/shard_map/ppermute | solution.py:33
  105.0 2.3 %collective-permute-start.18 = (f32[8192]{0:T(1024)S(1)}, f32[8192]{0:T(1024)S(1)}, u32[]{:S(2)}, u32[]{:S(2)}) collective-permute-start(f32[8192]{0:T(1024)S(1)} %bitcast.388), channel_id=1, source_target_pairs={{0,16},{8,24},{16,0},{24,8},{1,17},{9,25},{17,1},{25,9},{2,18},{10... | collective-permute-start | bytes 98312 | tf_op jit(solution)/shard_map/ppermute | solution.py:33
  107.6 1.3 convolution_add_fusion.1
  109.4 1.0 collective-permute-done.18
  111.9 2.1 %collective-permute-start.22 = (f32[8192]{0:T(1024)S(1)}, f32[8192]{0:T(1024)S(1)}, u32[]{:S(2)}, u32[]{:S(2)}) collective-permute-start(f32[8192]{0:T(1024)S(1)} %add_add_fusion.1), channel_id=1, source_target_pairs={{0,16},{8,24},{16,0},{24,8},{1,17},{9,25},{17,1},{25,9},{2,18},{10... | collective-permute-start | bytes 98312 | tf_op jit(solution)/shard_map/ppermute | solution.py:40
  114.0 1.1 collective-permute-start.23
  115.2 1.9 %collective-permute-done.21 = f32[8192]{0:T(1024)S(1)} collective-permute-done((f32[8192]{0:T(1024)S(1)}, f32[8192]{0:T(1024)S(1)}, u32[]{:S(2)}, u32[]{:S(2)}) %collective-permute-start.21) | collective-permute-done | bytes 32800 | tf_op jit(solution)/shard_map/ppermute | solution.py:40
  118.8 5.2 %collective-permute-start.24 = (f32[32768]{0:T(1024)S(1)}, f32[32768]{0:T(1024)S(1)}, u32[]{:S(2)}, u32[]{:S(2)}) collective-permute-start(f32[32768]{0:T(1024)S(1)} %bitcast.364), channel_id=1, source_target_pairs={{0,2},{1,3},{2,4},{3,5},{4,6},{5,7},{6,0},{7,1},{8,10},{9,11},{10,... | collective-permute-start | bytes 393224 | tf_op jit(solution)/shard_map/ppermute | solution.py:40
  124.3 1.3 collective-permute-start.26
  126.6 2.3 %collective-permute-done.25 = f32[32768]{0:T(1024)S(1)} collective-permute-done((f32[32768]{0:T(1024)S(1)}, f32[32768]{0:T(1024)S(1)}, u32[]{:S(2)}, u32[]{:S(2)}) %collective-permute-start.25) | collective-permute-done | bytes 131104 | tf_op jit(solution)/shard_map/ppermute | solution.py:40
  131.6 1.2 collective-permute-done.27
  137.2 1.0 fusion.110
  (229 shorter events, 53.5 us)
Async XLA Ops:
  0.6 16.4 %copy-start = (bf16[256,256]{1,0:T(8,128)(2,1)S(1)}, bf16[256,256]{1,0:T(8,128)(2,1)}, u32[]{:S(2)}) copy-start(bf16[256,256]{1,0:T(8,128)(2,1)} %param.17) | copy-start | bytes 393220
  0.6 5.6 %copy-start.22 = (s32[4,1024]{1,0:T(4,128)S(1)}, s32[4,1024]{1,0:T(4,128)}, u32[]{:S(2)}) copy-start(s32[4,1024]{1,0:T(4,128)} %param.14) | copy-start | bytes 49156
  0.7 6.1 %copy-start.32 = (s32[4,1024]{1,0:T(4,128)S(1)}, s32[4,1024]{1,0:T(4,128)}, u32[]{:S(2)}) copy-start(s32[4,1024]{1,0:T(4,128)} %param.13) | copy-start | bytes 49156
  4.1 11.0 %collective-permute-start = (bf16[4,128,256]{2,1,0:T(8,128)(2,1)}, bf16[4,128,256]{2,1,0:T(8,128)(2,1)}, u32[]{:S(2)}, u32[]{:S(2)}) collective-permute-start(bf16[4,128,256]{2,1,0:T(8,128)(2,1)} %convolution_convert_fusion.13), channel_id=1, source_target_pairs={{0,1},{1,2},{2,3},{3,4},{4,5},{5,6},{6,7},{7,0},{8,9},{9,10},{10,1... | collective-permute-start | bytes 786440 | tf_op jit(solution)/shard_map/ppermute | solution.py:12
  8.3 6.5 %copy-start.4 = (bf16[4,256,256]{2,1,0:T(8,128)(2,1)}, bf16[4,256,256]{2,1,0:T(8,128)(2,1)S(1)}, u32[]{:S(2)}) copy-start(bf16[4,256,256]{2,1,0:T(8,128)(2,1)S(1)} %fusion.28) | copy-start | bytes 1572868
  8.3 2.0 %copy-start.19 = (bf16[16,1,1,64,256]{4,3,2,1,0:T(8,128)(2,1)S(1)}, bf16[16,1,1,64,256]{4,3,2,1,0:T(8,128)(2,1)}, u32[]{:S(2)}) copy-start(bf16[16,1,1,64,256]{4,3,2,1,0:T(8,128)(2,1)} %param.21) | copy-start | bytes 1572868
  13.4 1.4 copy-start.1
  18.5 7.7 %collective-permute-start.1 = (bf16[4,32,256]{2,1,0:T(8,128)(2,1)S(1)}, bf16[4,32,256]{2,1,0:T(8,128)(2,1)S(1)}, u32[]{:S(2)}, u32[]{:S(2)}) collective-permute-start(bf16[4,32,256]{2,1,0:T(8,128)(2,1)S(1)} %get-tuple-element.73), channel_id=1, source_target_pairs={{0,8},{8,16},{16,24},{24,0},{1,9},{9,17},{17,25},{25,1},{2,10},{10... | collective-permute-start | bytes 196616 | tf_op jit(solution)/shard_map/ppermute | solution.py:88
  21.1 7.9 %collective-permute-start.2 = (bf16[4,32,256]{2,1,0:T(8,128)(2,1)S(1)}, bf16[4,32,256]{2,1,0:T(8,128)(2,1)S(1)}, u32[]{:S(2)}, u32[]{:S(2)}) collective-permute-start(bf16[4,32,256]{2,1,0:T(8,128)(2,1)S(1)} %get-tuple-element.72), channel_id=1, source_target_pairs={{0,16},{8,24},{16,0},{24,8},{1,17},{9,25},{17,1},{25,9},{2,18},{10... | collective-permute-start | bytes 196616 | tf_op jit(solution)/shard_map/ppermute | solution.py:88
  23.7 6.0 %collective-permute-start.3 = (bf16[4,32,256]{2,1,0:T(8,128)(2,1)S(1)}, bf16[4,32,256]{2,1,0:T(8,128)(2,1)S(1)}, u32[]{:S(2)}, u32[]{:S(2)}) collective-permute-start(bf16[4,32,256]{2,1,0:T(8,128)(2,1)S(1)} %get-tuple-element.71), channel_id=1, source_target_pairs={{0,24},{8,0},{16,8},{24,16},{1,25},{9,1},{17,9},{25,17},{2,26},{10... | collective-permute-start | bytes 196616 | tf_op jit(solution)/shard_map/ppermute | solution.py:88
  25.2 6.9 %collective-permute-start.7 = (bf16[4,32,256]{2,1,0:T(8,128)(2,1)S(1)}, bf16[4,32,256]{2,1,0:T(8,128)(2,1)S(1)}, u32[]{:S(2)}, u32[]{:S(2)}) collective-permute-start(bf16[4,32,256]{2,1,0:T(8,128)(2,1)S(1)} %get-tuple-element.61), channel_id=1, source_target_pairs={{0,8},{8,16},{16,24},{24,0},{1,9},{9,17},{17,25},{25,1},{2,10},{10... | collective-permute-start | bytes 196616 | tf_op jit(solution)/shard_map/ppermute | solution.py:88
  25.9 8.7 %collective-permute-start.8 = (bf16[4,32,256]{2,1,0:T(8,128)(2,1)S(1)}, bf16[4,32,256]{2,1,0:T(8,128)(2,1)S(1)}, u32[]{:S(2)}, u32[]{:S(2)}) collective-permute-start(bf16[4,32,256]{2,1,0:T(8,128)(2,1)S(1)} %get-tuple-element.60), channel_id=1, source_target_pairs={{0,16},{8,24},{16,0},{24,8},{1,17},{9,25},{17,1},{25,9},{2,18},{10... | collective-permute-start | bytes 196616 | tf_op jit(solution)/shard_map/ppermute | solution.py:88
  26.2 8.4 %collective-permute-start.9 = (bf16[4,32,256]{2,1,0:T(8,128)(2,1)S(1)}, bf16[4,32,256]{2,1,0:T(8,128)(2,1)S(1)}, u32[]{:S(2)}, u32[]{:S(2)}) collective-permute-start(bf16[4,32,256]{2,1,0:T(8,128)(2,1)S(1)} %get-tuple-element.59), channel_id=1, source_target_pairs={{0,24},{8,0},{16,8},{24,16},{1,25},{9,1},{17,9},{25,17},{2,26},{10... | collective-permute-start | bytes 196616 | tf_op jit(solution)/shard_map/ppermute | solution.py:88
  37.4 1.5 %copy-start.7 = (bf16[256,256]{1,0:T(8,128)(2,1)S(1)}, bf16[256,256]{1,0:T(8,128)(2,1)}, u32[]{:S(2)}) copy-start(bf16[256,256]{1,0:T(8,128)(2,1)} %param.19) | copy-start | bytes 393220
  38.9 3.1 %copy-start.8 = (bf16[4,128,4,64]{1,3,2,0:T(8,128)(2,1)S(1)}, bf16[4,128,4,64]{1,3,2,0:T(8,128)(2,1)}, u32[]{:S(2)}) copy-start(bf16[4,128,4,64]{1,3,2,0:T(8,128)(2,1)} %copy.107) | copy-start | bytes 786436
  42.0 1.3 copy-start.13
  42.0 1.3 copy-start.15
  42.0 1.3 copy-start.23
  49.6 1.5 %copy-start.17 = (bf16[4,4,32,256]{3,2,1,0:T(8,128)(2,1)S(1)}, bf16[4,4,32,256]{3,2,1,0:T(8,128)(2,1)}, u32[]{:S(2)}) copy-start(bf16[4,4,32,256]{3,2,1,0:T(8,128)(2,1)} %get-tuple-element.87) | copy-start | bytes 786436
  54.9 1.5 %copy-start.24 = (pred[128,128]{0,1:T(8,128)(4,1)S(1)}, pred[128,128]{0,1:T(8,128)(4,1)}, u32[]{:S(2)}) copy-start(pred[128,128]{0,1:T(8,128)(4,1)} %compare_and_fusion) | copy-start | bytes 49156
  64.6 2.4 %copy-start.21 = (bf16[4,128,4,64]{1,3,2,0:T(8,128)(2,1)S(1)}, bf16[4,128,4,64]{1,3,2,0:T(8,128)(2,1)}, u32[]{:S(2)}) copy-start(bf16[4,128,4,64]{1,3,2,0:T(8,128)(2,1)} %fusion.39) | copy-start | bytes 786436
  64.6 2.6 %copy-start.3 = (f32[32,16,256]{2,1,0:T(8,128)S(1)}, f32[32,16,256]{2,1,0:T(8,128)}, u32[]{:S(2)}) copy-start(f32[32,16,256]{2,1,0:T(8,128)} %copy.98) | copy-start | bytes 1572868
  68.1 4.9 %copy-start.18 = (bf16[4,128,4,64]{1,3,2,0:T(8,128)(2,1)S(1)}, bf16[4,128,4,64]{1,3,2,0:T(8,128)(2,1)}, u32[]{:S(2)}) copy-start(bf16[4,128,4,64]{1,3,2,0:T(8,128)(2,1)} %fusion.34) | copy-start | bytes 786436
  68.6 12.1 %collective-permute-start.10 = (bf16[4,32,256]{2,0,1:T(4,128)(2,1)S(1)}, bf16[4,32,256]{2,0,1:T(4,128)(2,1)S(1)}, u32[]{:S(2)}, u32[]{:S(2)}) collective-permute-start(bf16[4,32,256]{2,0,1:T(4,128)(2,1)S(1)} %get-tuple-element.49), channel_id=1, source_target_pairs={{0,8},{8,16},{16,24},{24,0},{1,9},{9,17},{17,25},{25,1},{2,10},{10... | collective-permute-start | bytes 196616 | tf_op jit(solution)/shard_map/ppermute | solution.py:88
  70.6 12.0 %collective-permute-start.11 = (bf16[4,32,256]{2,0,1:T(4,128)(2,1)S(1)}, bf16[4,32,256]{2,0,1:T(4,128)(2,1)S(1)}, u32[]{:S(2)}, u32[]{:S(2)}) collective-permute-start(bf16[4,32,256]{2,0,1:T(4,128)(2,1)S(1)} %get-tuple-element.48), channel_id=1, source_target_pairs={{0,16},{8,24},{16,0},{24,8},{1,17},{9,25},{17,1},{25,9},{2,18},{10... | collective-permute-start | bytes 196616 | tf_op jit(solution)/shard_map/ppermute | solution.py:88
  72.3 10.3 %collective-permute-start.12 = (bf16[4,32,256]{2,0,1:T(4,128)(2,1)S(1)}, bf16[4,32,256]{2,0,1:T(4,128)(2,1)S(1)}, u32[]{:S(2)}, u32[]{:S(2)}) collective-permute-start(bf16[4,32,256]{2,0,1:T(4,128)(2,1)S(1)} %get-tuple-element.47), channel_id=1, source_target_pairs={{0,24},{8,0},{16,8},{24,16},{1,25},{9,1},{17,9},{25,17},{2,26},{10... | collective-permute-start | bytes 196616 | tf_op jit(solution)/shard_map/ppermute | solution.py:88
  76.6 7.0 %collective-permute-start.4 = (bf16[4,32,256]{2,0,1:T(4,128)(2,1)S(1)}, bf16[4,32,256]{2,0,1:T(4,128)(2,1)S(1)}, u32[]{:S(2)}, u32[]{:S(2)}) collective-permute-start(bf16[4,32,256]{2,0,1:T(4,128)(2,1)S(1)} %get-tuple-element.37), channel_id=1, source_target_pairs={{0,8},{8,16},{16,24},{24,0},{1,9},{9,17},{17,25},{25,1},{2,10},{10... | collective-permute-start | bytes 196616 | tf_op jit(solution)/shard_map/ppermute | solution.py:88
  78.2 7.0 %collective-permute-start.5 = (bf16[4,32,256]{2,0,1:T(4,128)(2,1)S(1)}, bf16[4,32,256]{2,0,1:T(4,128)(2,1)S(1)}, u32[]{:S(2)}, u32[]{:S(2)}) collective-permute-start(bf16[4,32,256]{2,0,1:T(4,128)(2,1)S(1)} %get-tuple-element.36), channel_id=1, source_target_pairs={{0,16},{8,24},{16,0},{24,8},{1,17},{9,25},{17,1},{25,9},{2,18},{10... | collective-permute-start | bytes 196616 | tf_op jit(solution)/shard_map/ppermute | solution.py:88
  80.7 4.9 %collective-permute-start.6 = (bf16[4,32,256]{2,0,1:T(4,128)(2,1)S(1)}, bf16[4,32,256]{2,0,1:T(4,128)(2,1)S(1)}, u32[]{:S(2)}, u32[]{:S(2)}) collective-permute-start(bf16[4,32,256]{2,0,1:T(4,128)(2,1)S(1)} %get-tuple-element.35), channel_id=1, source_target_pairs={{0,24},{8,0},{16,8},{24,16},{1,25},{9,1},{17,9},{25,17},{2,26},{10... | collective-permute-start | bytes 196616 | tf_op jit(solution)/shard_map/ppermute | solution.py:88
  91.1 2.0 %collective-permute-start.13 = (f32[131072]{0:T(1024)S(1)}, f32[131072]{0:T(1024)S(1)}, u32[]{:S(2)}, u32[]{:S(2)}) collective-permute-start(f32[131072]{0:T(1024)S(1)} %bitcast.361), channel_id=1, source_target_pairs={{0,1},{1,0},{2,3},{3,2},{4,5},{5,4},{6,7},{7,6},{8,9},{9,8},{10,11... | collective-permute-start | bytes 1572872 | tf_op jit(solution)/shard_map/ppermute | solution.py:33
  93.2 5.3 %copy-start.11 = (bf16[4,256,128]{2,1,0:T(8,128)(2,1)S(1)}, bf16[4,256,128]{2,1,0:T(8,128)(2,1)}, u32[]{:S(2)}) copy-start(bf16[4,256,128]{2,1,0:T(8,128)(2,1)} %fusion.29) | copy-start | bytes 786436
  93.9 7.3 %collective-permute-start.14 = (f32[32768]{0:T(1024)S(1)}, f32[32768]{0:T(1024)S(1)}, u32[]{:S(2)}, u32[]{:S(2)}) collective-permute-start(f32[32768]{0:T(1024)S(1)} %bitcast.371), channel_id=1, source_target_pairs={{0,2},{1,3},{2,4},{3,5},{4,6},{5,7},{6,0},{7,1},{8,10},{9,11},{10,... | collective-permute-start | bytes 393224 | tf_op jit(solution)/shard_map/ppermute | solution.py:33
  95.4 7.7 %collective-permute-start.15 = (f32[32768]{0:T(1024)S(1)}, f32[32768]{0:T(1024)S(1)}, u32[]{:S(2)}, u32[]{:S(2)}) collective-permute-start(f32[32768]{0:T(1024)S(1)} %bitcast.370), channel_id=1, source_target_pairs={{0,4},{1,5},{2,6},{3,7},{4,0},{5,1},{6,2},{7,3},{8,12},{9,13},{10,... | collective-permute-start | bytes 393224 | tf_op jit(solution)/shard_map/ppermute | solution.py:33
  96.6 11.0 %copy-start.25 = (s32[4,128]{1,0:T(4,128)S(1)}, s32[4,128]{1,0:T(4,128)}, u32[]{:S(2)}) copy-start(s32[4,128]{1,0:T(4,128)} %param.15) | copy-start | bytes 6148
  96.6 11.0 %copy-start.30 = (pred[4,128]{1,0:T(4,128)(4,1)S(1)}, pred[4,128]{1,0:T(4,128)(4,1)}, u32[]{:S(2)}) copy-start(pred[4,128]{1,0:T(4,128)(4,1)} %copy-done.29) | copy-start | bytes 1540
  96.6 6.7 %collective-permute-start.16 = (f32[32768]{0:T(1024)S(1)}, f32[32768]{0:T(1024)S(1)}, u32[]{:S(2)}, u32[]{:S(2)}) collective-permute-start(f32[32768]{0:T(1024)S(1)} %bitcast.369), channel_id=1, source_target_pairs={{0,6},{1,7},{2,0},{3,1},{4,2},{5,3},{6,4},{7,5},{8,14},{9,15},{10,... | collective-permute-start | bytes 393224 | tf_op jit(solution)/shard_map/ppermute | solution.py:33
  99.0 8.6 %collective-permute-start.20 = (bf16[4,128,256]{2,1,0:T(8,128)(2,1)S(1)}, bf16[4,128,256]{2,1,0:T(8,128)(2,1)S(1)}, u32[]{:S(2)}, u32[]{:S(2)}) collective-permute-start(bf16[4,128,256]{2,1,0:T(8,128)(2,1)S(1)} %convolution_convert_fusion), channel_id=1, source_target_pairs={{0,7},{1,0},{2,1},{3,2},{4,3},{5,4},{6,5},{7,6},{8,15},{9,8},{10,9... | collective-permute-start | bytes 786440 | tf_op jit(solution)/shard_map/ppermute | solution.py:12
  103.5 5.9 %collective-permute-start.17 = (f32[8192]{0:T(1024)S(1)}, f32[8192]{0:T(1024)S(1)}, u32[]{:S(2)}, u32[]{:S(2)}) collective-permute-start(f32[8192]{0:T(1024)S(1)} %bitcast.389), channel_id=1, source_target_pairs={{0,8},{8,16},{16,24},{24,0},{1,9},{9,17},{17,25},{25,1},{2,10},{10... | collective-permute-start | bytes 98312 | tf_op jit(solution)/shard_map/ppermute | solution.py:33
  105.0 5.4 %collective-permute-start.18 = (f32[8192]{0:T(1024)S(1)}, f32[8192]{0:T(1024)S(1)}, u32[]{:S(2)}, u32[]{:S(2)}) collective-permute-start(f32[8192]{0:T(1024)S(1)} %bitcast.388), channel_id=1, source_target_pairs={{0,16},{8,24},{16,0},{24,8},{1,17},{9,25},{17,1},{25,9},{2,18},{10... | collective-permute-start | bytes 98312 | tf_op jit(solution)/shard_map/ppermute | solution.py:33
  107.3 3.9 %collective-permute-start.19 = (f32[8192]{0:T(1024)S(1)}, f32[8192]{0:T(1024)S(1)}, u32[]{:S(2)}, u32[]{:S(2)}) collective-permute-start(f32[8192]{0:T(1024)S(1)} %bitcast.387), channel_id=1, source_target_pairs={{0,24},{8,0},{16,8},{24,16},{1,25},{9,1},{17,9},{25,17},{2,26},{10... | collective-permute-start | bytes 98312 | tf_op jit(solution)/shard_map/ppermute | solution.py:33
  108.9 9.8 %copy-start.26 = (pred[4]{0:T(512)(128)(4,1)S(1)}, pred[4]{0:T(512)(128)(4,1)}, u32[]{:S(2)}) copy-start(pred[4]{0:T(512)(128)(4,1)} %get-tuple-element.95) | copy-start | bytes 16
  111.3 5.8 %collective-permute-start.21 = (f32[8192]{0:T(1024)S(1)}, f32[8192]{0:T(1024)S(1)}, u32[]{:S(2)}, u32[]{:S(2)}) collective-permute-start(f32[8192]{0:T(1024)S(1)} %add_add_fusion.1), channel_id=1, source_target_pairs={{0,8},{8,16},{16,24},{24,0},{1,9},{9,17},{17,25},{25,1},{2,10},{10... | collective-permute-start | bytes 98312 | tf_op jit(solution)/shard_map/ppermute | solution.py:40
  111.9 5.2 %collective-permute-start.22 = (f32[8192]{0:T(1024)S(1)}, f32[8192]{0:T(1024)S(1)}, u32[]{:S(2)}, u32[]{:S(2)}) collective-permute-start(f32[8192]{0:T(1024)S(1)} %add_add_fusion.1), channel_id=1, source_target_pairs={{0,16},{8,24},{16,0},{24,8},{1,17},{9,25},{17,1},{25,9},{2,18},{10... | collective-permute-start | bytes 98312 | tf_op jit(solution)/shard_map/ppermute | solution.py:40
  114.0 3.9 %collective-permute-start.23 = (f32[8192]{0:T(1024)S(1)}, f32[8192]{0:T(1024)S(1)}, u32[]{:S(2)}, u32[]{:S(2)}) collective-permute-start(f32[8192]{0:T(1024)S(1)} %add_add_fusion.1), channel_id=1, source_target_pairs={{0,24},{8,0},{16,8},{24,16},{1,25},{9,1},{17,9},{25,17},{2,26},{10... | collective-permute-start | bytes 98312 | tf_op jit(solution)/shard_map/ppermute | solution.py:40
  118.8 7.8 %collective-permute-start.24 = (f32[32768]{0:T(1024)S(1)}, f32[32768]{0:T(1024)S(1)}, u32[]{:S(2)}, u32[]{:S(2)}) collective-permute-start(f32[32768]{0:T(1024)S(1)} %bitcast.364), channel_id=1, source_target_pairs={{0,2},{1,3},{2,4},{3,5},{4,6},{5,7},{6,0},{7,1},{8,10},{9,11},{10,... | collective-permute-start | bytes 393224 | tf_op jit(solution)/shard_map/ppermute | solution.py:40
  124.0 5.0 %collective-permute-start.25 = (f32[32768]{0:T(1024)S(1)}, f32[32768]{0:T(1024)S(1)}, u32[]{:S(2)}, u32[]{:S(2)}) collective-permute-start(f32[32768]{0:T(1024)S(1)} %bitcast.365), channel_id=1, source_target_pairs={{0,4},{1,5},{2,6},{3,7},{4,0},{5,1},{6,2},{7,3},{8,12},{9,13},{10,... | collective-permute-start | bytes 393224 | tf_op jit(solution)/shard_map/ppermute | solution.py:40
  124.3 5.0 %collective-permute-start.26 = (f32[32768]{0:T(1024)S(1)}, f32[32768]{0:T(1024)S(1)}, u32[]{:S(2)}, u32[]{:S(2)}) collective-permute-start(f32[32768]{0:T(1024)S(1)} %bitcast.366), channel_id=1, source_target_pairs={{0,6},{1,7},{2,0},{3,1},{4,2},{5,3},{6,4},{7,5},{8,14},{9,15},{10,... | collective-permute-start | bytes 393224 | tf_op jit(solution)/shard_map/ppermute | solution.py:40
  130.8 2.0 %collective-permute-start.27 = (f32[131072]{0:T(1024)S(1)}, f32[131072]{0:T(1024)S(1)}, u32[]{:S(2)}, u32[]{:S(2)}) collective-permute-start(f32[131072]{0:T(1024)S(1)} %bitcast.357), channel_id=1, source_target_pairs={{0,1},{1,0},{2,3},{3,2},{4,5},{5,4},{6,7},{7,6},{8,9},{9,8},{10,11... | collective-permute-start | bytes 1572872 | tf_op jit(solution)/shard_map/ppermute | solution.py:40
  (14 other events, 13.2 us)

commit v11 on v8

--- a/solution.py
+++ b/solution.py
@@ -36,6 +36,11 @@
 
 def _gather_step(flat, axis, stride, group):
     digit = (lax.axis_index(axis) // stride) % group
+    if group == 2:
+        other = lax.ppermute(flat, axis, _group_pairs(axis, stride, group, 1))
+        return jnp.where(
+            digit == 0, jnp.concatenate([flat, other]), jnp.concatenate([other, flat])
+        )
     got = [flat] + [
         lax.ppermute(flat, axis, _group_pairs(axis, stride, group, shift)) for shift in range(1, group)
     ]

time: 117 us -> 113 us (0.966)
  local copies, waits for them, and re-layouts: 23.9 us -> 21.2 us
  other arithmetic: 11.7 us -> 10.3 us
    gather x5 -> x3, local copies, waits for them, and re-layouts: 4.14 us -> 1.78 us  [_gather_step(): return jnp.take(stacked, order, axis=0).reshape(-1)]
    ppermute x0 -> x1, waiting for transfers between devices: none -> 1.31 us  [_gather_step(): other = lax.ppermute(flat, axis, _group_pairs(axis, stride, group, 1))]
    ppermute x7 -> x6, waiting for transfers between devices: 6.82 us -> 5.61 us  [_gather_step(): lax.ppermute(flat, axis, _group_pairs(axis, stride, group, shift))]
    unnamed x70 -> x69, local copies, waits for them, and re-layouts: 6.17 us -> 5.68 us
    ppermute x7 -> x6, starting transfers between devices: 8.83 us -> 8.76 us  [_gather_step(): lax.ppermute(flat, axis, _group_pairs(axis, stride, group, shift))]
where the time goes in v11:
time: 113 us
  starting transfers between devices  31.9 us (28%)
  waiting for transfers between devices  24.7 us (22%)
  matrix products  23 us (20%)
  local copies, waits for them, and re-layouts  21.2 us (19%)
  other arithmetic  10.3 us (9%)
  between operations  1.51 us (1%)
    ppermute x6, starting transfers between devices, exchange(): lax.ppermute(send, axis, [(i, (i + shift) % count) for i in range(count)])  12 us
    ppermute x6, waiting for transfers between devices, exchange(): lax.ppermute(send, axis, [(i, (i + shift) % count) for i in range(count)])  10.2 us
    ppermute x7, starting transfers between devices, _scatter_step(): lax.ppermute(send, axis, _group_pairs(axis, stride, group, shift))  9.43 us
    ppermute x6, starting transfers between devices, _gather_step(): lax.ppermute(flat, axis, _group_pairs(axis, stride, group, shift))  8.76 us
    ppermute x7, waiting for transfers between devices, _scatter_step(): lax.ppermute(send, axis, _group_pairs(axis, stride, group, shift))  7.16 us
    unnamed x69, local copies, waits for them, and re-layouts  5.68 us
    ppermute x6, waiting for transfers between devices, _gather_step(): lax.ppermute(flat, axis, _group_pairs(axis, stride, group, shift))  5.61 us
    sub x1, matrix products, attend_blocked(): exponent = jnp.exp(scores - highest)  4.16 us
  transfers between devices with their start and end apart: 22, of which 15 were waited for; matrix products, arithmetic and copies ran while one was open for 15% of the time, Pallas kernels for 0%

profile of v11, /device:TPU:0, one launch (start us, length us, event | category | flops | bytes accessed | tf_op | source)
XLA Modules:
  0.0 112.6 jit_solution(6280409897535133715)
XLA Ops:
  2.0 2.1 %convolution_convert_fusion.7 = bf16[4,128,256]{2,1,0:T(8,128)(2,1)} fusion(bf16[4,256,256]{2,1,0:T(8,128)(2,1)} %param.12, s32[4,128]{1,0:T(4,128)} %param.15, pred[4,128]{1,0:T(4,128)(4,1)S(1)} %iota_compare_fusion.12), kind=kOutput, calls=%fused_computation.50 | convolution fusion | flops 67502080 | bytes 788992 | tf_op jit(solution)/shard_map/dsn,dnh->dsh/dot_general | solution.py:292
  5.1 1.2 %convert_reduce_fusion = f32[4,256]{1,0:T(4,128)S(1)} fusion(s32[4,1024]{1,0:T(4,128)} %param.14), kind=kLoop, calls=%fused_computation.6 | loop fusion | flops 4193280 | bytes 20480 | tf_op jit(solution)/shard_map/reduce_sum | solution.py:307
  6.4 2.4 %fusion.17 = bf16[4,256,256]{2,1,0:T(8,128)(2,1)S(1)} fusion(s32[4,1024]{1,0:T(4,128)} %param.13, s32[4,1024]{1,0:T(4,128)} %param.14), kind=kOutput, calls=%fused_computation.44 | convolution fusion | flops 539230208 | bytes 557056 | tf_op jit(solution)/shard_map/der,des->drs/dot_general | solution.py:301
  9.1 1.3 %fusion.21 = bf16[4,256,128]{2,1,0:T(8,128)(2,1)S(1)} fusion(s32[4,1024]{1,0:T(4,128)S(1)} %copy-done.22, s32[128]{0:T(128)S(1)} %iota_add_fusion, s32[4,1024]{1,0:T(4,128)S(1)} %copy-done.28), kind=kOutput, calls=%fused_computation.48 | convolution fusion | flops 270139392 | bytes 295424 | tf_op jit(solution)/shard_map/der,des->drs/dot_general | solution.py:304
  11.8 1.3 %fusion.15 = bf16[4,256,256]{2,1,0:T(8,128)(2,1)S(1)} fusion(f32[4,256,256]{2,1,0:T(8,128)S(1)} %fusion.71, bf16[4,256,128]{2,1,0:T(8,128)(2,1)S(1)} %fusion.21, bf16[4,128,256]{2,1,0:T(8,128)(2,1)} %collective-permute-done, bf16[4,256,256]{2,1,0:T(8,128)(2,1)S(1)} %copy-done.1, f32[4,256]{1,0:T(4,128)S(1)} %add_divide_fusion.1), kind=kOutput, calls=%fused_computation.36 | convolution fusion | flops 68419584 | bytes 2625536 | tf_op jit(solution)/shard_map/drs,dsh->drh/dot_general | solution.py:313
  13.1 1.3 %fusion.24 = (bf16[4,256,256]{2,1,0:T(8,128)(2,1)S(1)}, f32[4,256,256]{2,1,0:T(8,128)}) fusion(bf16[4,256,256]{2,1,0:T(8,128)(2,1)S(1)} %copy-done.1, bf16[4,256,256]{2,1,0:T(8,128)(2,1)S(1)} %fusion.15, bf16[256,256]{1,0:T(8,128)(2,1)S(1)} %copy-done), kind=kOutput, calls=%fused_computation.55 | convolution fusion | flops 136052736 | bytes 2752512 | tf_op jit(solution)/shard_map/drh,hk->drk/dot_general | solution.py:315
  15.4 2.3 %collective-permute-start.1 = (bf16[4,64,256]{2,1,0:T(8,128)(2,1)}, bf16[4,64,256]{2,1,0:T(8,128)(2,1)}, u32[]{:S(2)}, u32[]{:S(2)}) collective-permute-start(bf16[4,64,256]{2,1,0:T(8,128)(2,1)} %get-tuple-element.39), channel_id=1, source_target_pairs={{0,8},{8,16},{16,24},{24,0},{1,9},{9,17},{17,25},{25,1},{2,10},{10... | collective-permute-start | bytes 393224 | tf_op jit(solution)/shard_map/ppermute | solution.py:93
  17.7 2.6 %collective-permute-start.2 = (bf16[4,64,256]{2,1,0:T(8,128)(2,1)}, bf16[4,64,256]{2,1,0:T(8,128)(2,1)}, u32[]{:S(2)}, u32[]{:S(2)}) collective-permute-start(bf16[4,64,256]{2,1,0:T(8,128)(2,1)} %get-tuple-element.38), channel_id=1, source_target_pairs={{0,16},{8,24},{16,0},{24,8},{1,17},{9,25},{17,1},{25,9},{2,18},{10... | collective-permute-start | bytes 393224 | tf_op jit(solution)/shard_map/ppermute | solution.py:93
  20.3 1.3 %collective-permute-start.3 = (bf16[4,64,256]{2,1,0:T(8,128)(2,1)}, bf16[4,64,256]{2,1,0:T(8,128)(2,1)}, u32[]{:S(2)}, u32[]{:S(2)}) collective-permute-start(bf16[4,64,256]{2,1,0:T(8,128)(2,1)} %get-tuple-element.37), channel_id=1, source_target_pairs={{0,24},{8,0},{16,8},{24,16},{1,25},{9,1},{17,9},{25,17},{2,26},{10... | collective-permute-start | bytes 393224 | tf_op jit(solution)/shard_map/ppermute | solution.py:93
  23.5 1.6 %copy.26 = f32[64,16,256]{2,1,0:T(8,128)} copy(f32[64,16,256]{2,0,1:T(8,128)S(1)} %bitcast_convert_fusion) | data formatting | bytes 2097152 | tf_op jit(solution)/shard_map/convert_element_type | solution.py:264
  25.2 5.0 %collective-permute-done.2 = bf16[4,64,256]{2,1,0:T(8,128)(2,1)} collective-permute-done((bf16[4,64,256]{2,1,0:T(8,128)(2,1)}, bf16[4,64,256]{2,1,0:T(8,128)(2,1)}, u32[]{:S(2)}, u32[]{:S(2)}) %collective-permute-start.2) | collective-permute-done | bytes 131104 | tf_op jit(solution)/shard_map/ppermute | solution.py:93
  30.1 1.1 pad_maximum_fusion.2
  33.5 1.2 %copy.30 = bf16[8,128,4,64]{1,3,2,0:T(8,128)(2,1)} copy(bf16[8,128,4,64]{3,2,1,0:T(4,128)(2,1)S(1)} %reshape.433) | data formatting | bytes 1048576 | tf_op jit(solution)/shard_map/reshape | solution.py:222
  35.4 1.2 %copy.36 = bf16[8,128,4,64]{1,3,2,0:T(8,128)(2,1)} copy(bf16[8,128,4,64]{3,2,1,0:T(4,128)(2,1)S(1)} %reshape.432) | data formatting | bytes 1048576 | tf_op jit(solution)/shard_map/reshape | solution.py:222
  37.3 1.8 %fusion.27 = f32[8,4,128,128]{3,2,1,0:T(8,128)} fusion(bf16[8,128,4,64]{1,3,2,0:T(8,128)(2,1)S(1)} %copy.35, bf16[8,128,4,64]{3,2,1,0:T(4,128)(2,1)S(1)} %reshape.431), kind=kOutput, calls=%fused_computation.60 | convolution fusion | flops 67108864 | bytes 3145728 | tf_op jit(solution)/shard_map/gihd,gjhd->ghij/dot_general | solution.py:233
  39.1 4.2 %fusion.70 = (f32[8,4,128]{2,1,0:T(4,128)}, f32[8,4,128,128]{2,3,1,0:T(8,128)}) fusion(pred[128,128]{0,1:T(8,128)(4,1)} %compare_and_fusion, bf16[8,128,4,64]{1,3,2,0:T(8,128)(2,1)} %copy.30, bf16[8,128,4,64]{1,3,2,0:T(8,128)(2,1)} %copy.36), kind=kOutput, calls=%fused_computation.191 | convolution fusion | flops 69206144 | bytes 3178496 | tf_op jit(solution)/shard_map/sub | solution.py:238
  43.2 2.9 %fusion.7 = bf16[8,4,128,128]{2,3,1,0:T(8,128)(2,1)S(1)} fusion(f32[8,4,128,128]{3,2,1,0:T(8,128)S(1)} %copy-done.3, f32[8,4,128,128]{2,3,1,0:T(8,128)} %get-tuple-element.53, f32[8,4,128]{2,1,0:T(4,128)} %get-tuple-element.52), kind=kOutput, calls=%fused_computation.16 | output fusion | flops 3674239 | bytes 5259264 | tf_op jit(solution)/shard_map/sub | solution.py:244
  48.1 0.8 fusion.20
  52.8 3.3 %collective-permute-start.4 = (bf16[4,64,256]{2,1,0:T(8,128)(2,1)S(1)}, bf16[4,64,256]{2,1,0:T(8,128)(2,1)S(1)}, u32[]{:S(2)}, u32[]{:S(2)}) collective-permute-start(bf16[4,64,256]{2,1,0:T(8,128)(2,1)S(1)} %get-tuple-element.27), channel_id=1, source_target_pairs={{0,8},{8,16},{16,24},{24,0},{1,9},{9,17},{17,25},{25,1},{2,10},{10... | collective-permute-start | bytes 393224 | tf_op jit(solution)/shard_map/ppermute | solution.py:93
  56.1 1.5 %collective-permute-start.5 = (bf16[4,64,256]{2,1,0:T(8,128)(2,1)S(1)}, bf16[4,64,256]{2,1,0:T(8,128)(2,1)S(1)}, u32[]{:S(2)}, u32[]{:S(2)}) collective-permute-start(bf16[4,64,256]{2,1,0:T(8,128)(2,1)S(1)} %get-tuple-element.26), channel_id=1, source_target_pairs={{0,16},{8,24},{16,0},{24,8},{1,17},{9,25},{17,1},{25,9},{2,18},{10... | collective-permute-start | bytes 393224 | tf_op jit(solution)/shard_map/ppermute | solution.py:93
  57.6 0.9 collective-permute-start.6
  58.6 0.8 copy.63
  59.4 0.8 copy.64
  60.6 0.8 copy.65
  61.5 5.2 %collective-permute-done.5 = bf16[4,64,256]{2,1,0:T(8,128)(2,1)S(1)} collective-permute-done((bf16[4,64,256]{2,1,0:T(8,128)(2,1)S(1)}, bf16[4,64,256]{2,1,0:T(8,128)(2,1)S(1)}, u32[]{:S(2)}, u32[]{:S(2)}) %collective-permute-start.5) | collective-permute-done | bytes 131104 | tf_op jit(solution)/shard_map/ppermute | solution.py:93
  69.7 0.9 constant_dynamic-slice_fusion.8
  71.0 0.8 convolution_add_fusion
  73.4 1.9 %collective-permute-start.10 = (f32[32768]{0:T(1024)S(1)}, f32[32768]{0:T(1024)S(1)}, u32[]{:S(2)}, u32[]{:S(2)}) collective-permute-start(f32[32768]{0:T(1024)S(1)} %bitcast.229), channel_id=1, source_target_pairs={{0,6},{1,7},{2,0},{3,1},{4,2},{5,3},{6,4},{7,5},{8,14},{9,15},{10,... | collective-permute-start | bytes 393224 | tf_op jit(solution)/shard_map/ppermute | solution.py:33
  75.4 1.5 %collective-permute-start.9 = (f32[32768]{0:T(1024)S(1)}, f32[32768]{0:T(1024)S(1)}, u32[]{:S(2)}, u32[]{:S(2)}) collective-permute-start(f32[32768]{0:T(1024)S(1)} %bitcast.225), channel_id=1, source_target_pairs={{0,4},{1,5},{2,6},{3,7},{4,0},{5,1},{6,2},{7,3},{8,12},{9,13},{10,... | collective-permute-start | bytes 393224 | tf_op jit(solution)/shard_map/ppermute | solution.py:33
  77.5 1.1 collective-permute-start.14
  78.6 1.1 collective-permute-done.10
  79.8 3.1 %collective-permute-done.8 = f32[32768]{0:T(1024)S(1)} collective-permute-done((f32[32768]{0:T(1024)S(1)}, f32[32768]{0:T(1024)S(1)}, u32[]{:S(2)}, u32[]{:S(2)}) %collective-permute-start.8) | collective-permute-done | bytes 131104 | tf_op jit(solution)/shard_map/ppermute | solution.py:33
  83.6 3.3 %collective-permute-start.11 = (f32[8192]{0:T(1024)S(1)}, f32[8192]{0:T(1024)S(1)}, u32[]{:S(2)}, u32[]{:S(2)}) collective-permute-start(f32[8192]{0:T(1024)S(1)} %bitcast.236), channel_id=1, source_target_pairs={{0,8},{8,16},{16,24},{24,0},{1,9},{9,17},{17,25},{25,1},{2,10},{10... | collective-permute-start | bytes 98312 | tf_op jit(solution)/shard_map/ppermute | solution.py:33
  86.9 1.5 %collective-permute-start.12 = (f32[8192]{0:T(1024)S(1)}, f32[8192]{0:T(1024)S(1)}, u32[]{:S(2)}, u32[]{:S(2)}) collective-permute-start(f32[8192]{0:T(1024)S(1)} %bitcast.235), channel_id=1, source_target_pairs={{0,16},{8,24},{16,0},{24,8},{1,17},{9,25},{17,1},{25,9},{2,18},{10... | collective-permute-start | bytes 98312 | tf_op jit(solution)/shard_map/ppermute | solution.py:33
  88.5 0.9 collective-permute-start.13
  89.4 1.3 %convolution_add_fusion.4 = f32[4,256,256]{2,1,0:T(8,128)} fusion(f32[4,256,256]{2,1,0:T(8,128)S(1)} %convolution_add_fusion, bf16[4,128,256]{2,1,0:T(8,128)(2,1)S(1)} %collective-permute-done.14, s32[4,128]{1,0:T(4,128)S(1)} %copy-done.23, pred[4,128]{1,0:T(4,128)(4,1)S(1)} %copy-done.26), kind=kOutput, calls=%fused_computation.29 | convolution fusion | flops 67633152 | bytes 2361856 | tf_op jit(solution)/shard_map/dsn,dsh->dnh/dot_general | solution.py:350
  90.6 1.1 collective-permute-done.12
  92.7 3.0 %collective-permute-start.16 = (f32[8192]{0:T(1024)S(1)}, f32[8192]{0:T(1024)S(1)}, u32[]{:S(2)}, u32[]{:S(2)}) collective-permute-start(f32[8192]{0:T(1024)S(1)} %add_add_fusion.1), channel_id=1, source_target_pairs={{0,16},{8,24},{16,0},{24,8},{1,17},{9,25},{17,1},{25,9},{2,18},{10... | collective-permute-start | bytes 98312 | tf_op jit(solution)/shard_map/ppermute | solution.py:45
  95.7 1.0 collective-permute-start.17
  96.8 1.4 %collective-permute-done.15 = f32[8192]{0:T(1024)S(1)} collective-permute-done((f32[8192]{0:T(1024)S(1)}, f32[8192]{0:T(1024)S(1)}, u32[]{:S(2)}, u32[]{:S(2)}) %collective-permute-start.15) | collective-permute-done | bytes 32800 | tf_op jit(solution)/shard_map/ppermute | solution.py:45
  98.1 1.5 %collective-permute-done.17 = f32[8192]{0:T(1024)S(1)} collective-permute-done((f32[8192]{0:T(1024)S(1)}, f32[8192]{0:T(1024)S(1)}, u32[]{:S(2)}, u32[]{:S(2)}) %collective-permute-start.17) | collective-permute-done | bytes 32800 | tf_op jit(solution)/shard_map/ppermute | solution.py:45
  101.1 1.1 %collective-permute-start.19 = (f32[32768]{0:T(1024)S(1)}, f32[32768]{0:T(1024)S(1)}, u32[]{:S(2)}, u32[]{:S(2)}) collective-permute-start(f32[32768]{0:T(1024)S(1)} %bitcast.221), channel_id=1, source_target_pairs={{0,4},{1,5},{2,6},{3,7},{4,0},{5,1},{6,2},{7,3},{8,12},{9,13},{10,... | collective-permute-start | bytes 393224 | tf_op jit(solution)/shard_map/ppermute | solution.py:45
  102.3 2.6 %collective-permute-start.20 = (f32[32768]{0:T(1024)S(1)}, f32[32768]{0:T(1024)S(1)}, u32[]{:S(2)}, u32[]{:S(2)}) collective-permute-start(f32[32768]{0:T(1024)S(1)} %bitcast.222), channel_id=1, source_target_pairs={{0,6},{1,7},{2,0},{3,1},{4,2},{5,3},{6,4},{7,5},{8,14},{9,15},{10,... | collective-permute-start | bytes 393224 | tf_op jit(solution)/shard_map/ppermute | solution.py:45
  105.1 1.5 %collective-permute-done.18 = f32[32768]{0:T(1024)S(1)} collective-permute-done((f32[32768]{0:T(1024)S(1)}, f32[32768]{0:T(1024)S(1)}, u32[]{:S(2)}, u32[]{:S(2)}) %collective-permute-start.18) | collective-permute-done | bytes 131104 | tf_op jit(solution)/shard_map/ppermute | solution.py:45
  106.5 1.0 collective-permute-done.19
  108.3 0.8 gather_fusion.1
  110.0 1.3 %collective-permute-done.21 = f32[131072]{0:T(1024)S(1)} collective-permute-done((f32[131072]{0:T(1024)S(1)}, f32[131072]{0:T(1024)S(1)}, u32[]{:S(2)}, u32[]{:S(2)}) %collective-permute-start.21) | collective-permute-done | bytes 524320 | tf_op jit(solution)/shard_map/ppermute | solution.py:40
  111.6 1.0 fusion.69
  (158 shorter events, 27.1 us)
Async XLA Ops:
  0.6 12.4 %copy-start = (bf16[256,256]{1,0:T(8,128)(2,1)S(1)}, bf16[256,256]{1,0:T(8,128)(2,1)}, u32[]{:S(2)}) copy-start(bf16[256,256]{1,0:T(8,128)(2,1)} %param.17) | copy-start | bytes 393220
  4.1 7.7 %collective-permute-start = (bf16[4,128,256]{2,1,0:T(8,128)(2,1)}, bf16[4,128,256]{2,1,0:T(8,128)(2,1)}, u32[]{:S(2)}, u32[]{:S(2)}) collective-permute-start(bf16[4,128,256]{2,1,0:T(8,128)(2,1)} %convolution_convert_fusion.7), channel_id=1, source_target_pairs={{0,1},{1,2},{2,3},{3,4},{4,5},{5,6},{6,7},{7,0},{8,9},{9,10},{10,1... | collective-permute-start | bytes 786440 | tf_op jit(solution)/shard_map/ppermute | solution.py:12
  6.3 2.4 %copy-start.1 = (bf16[4,256,256]{2,1,0:T(8,128)(2,1)S(1)}, bf16[4,256,256]{2,1,0:T(8,128)(2,1)}, u32[]{:S(2)}) copy-start(bf16[4,256,256]{2,1,0:T(8,128)(2,1)} %param.12) | copy-start | bytes 1572868
  6.3 2.8 %copy-start.22 = (s32[4,1024]{1,0:T(4,128)S(1)}, s32[4,1024]{1,0:T(4,128)}, u32[]{:S(2)}) copy-start(s32[4,1024]{1,0:T(4,128)} %param.14) | copy-start | bytes 49156
  6.4 2.8 %copy-start.28 = (s32[4,1024]{1,0:T(4,128)S(1)}, s32[4,1024]{1,0:T(4,128)}, u32[]{:S(2)}) copy-start(s32[4,1024]{1,0:T(4,128)} %param.13) | copy-start | bytes 49156
  8.8 1.7 %copy-start.9 = (bf16[4,256,256]{2,1,0:T(8,128)(2,1)}, bf16[4,256,256]{2,1,0:T(8,128)(2,1)S(1)}, u32[]{:S(2)}) copy-start(bf16[4,256,256]{2,1,0:T(8,128)(2,1)S(1)} %fusion.17) | copy-start | bytes 1572868
  9.1 2.1 %copy-start.4 = (bf16[16,1,1,64,256]{4,3,2,1,0:T(8,128)(2,1)S(1)}, bf16[16,1,1,64,256]{4,3,2,1,0:T(8,128)(2,1)}, u32[]{:S(2)}) copy-start(bf16[16,1,1,64,256]{4,3,2,1,0:T(8,128)(2,1)} %param.21) | copy-start | bytes 1572868
  13.1 1.4 %copy-start.5 = (bf16[4,256,256]{2,1,0:T(8,128)(2,1)}, bf16[4,256,256]{2,1,0:T(8,128)(2,1)S(1)}, u32[]{:S(2)}) copy-start(bf16[4,256,256]{2,1,0:T(8,128)(2,1)S(1)} %fusion.15) | copy-start | bytes 1572868
  15.4 9.8 %collective-permute-start.1 = (bf16[4,64,256]{2,1,0:T(8,128)(2,1)}, bf16[4,64,256]{2,1,0:T(8,128)(2,1)}, u32[]{:S(2)}, u32[]{:S(2)}) collective-permute-start(bf16[4,64,256]{2,1,0:T(8,128)(2,1)} %get-tuple-element.39), channel_id=1, source_target_pairs={{0,8},{8,16},{16,24},{24,0},{1,9},{9,17},{17,25},{25,1},{2,10},{10... | collective-permute-start | bytes 393224 | tf_op jit(solution)/shard_map/ppermute | solution.py:93
  17.7 12.4 %collective-permute-start.2 = (bf16[4,64,256]{2,1,0:T(8,128)(2,1)}, bf16[4,64,256]{2,1,0:T(8,128)(2,1)}, u32[]{:S(2)}, u32[]{:S(2)}) collective-permute-start(bf16[4,64,256]{2,1,0:T(8,128)(2,1)} %get-tuple-element.38), channel_id=1, source_target_pairs={{0,16},{8,24},{16,0},{24,8},{1,17},{9,25},{17,1},{25,9},{2,18},{10... | collective-permute-start | bytes 393224 | tf_op jit(solution)/shard_map/ppermute | solution.py:93
  20.3 9.8 %collective-permute-start.3 = (bf16[4,64,256]{2,1,0:T(8,128)(2,1)}, bf16[4,64,256]{2,1,0:T(8,128)(2,1)}, u32[]{:S(2)}, u32[]{:S(2)}) collective-permute-start(bf16[4,64,256]{2,1,0:T(8,128)(2,1)} %get-tuple-element.37), channel_id=1, source_target_pairs={{0,24},{8,0},{16,8},{24,16},{1,25},{9,1},{17,9},{25,17},{2,26},{10... | collective-permute-start | bytes 393224 | tf_op jit(solution)/shard_map/ppermute | solution.py:93
  22.9 2.2 %copy-start.27 = (s32[4]{0:T(128)S(1)}, s32[4]{0:T(128)}, u32[]{:S(2)}) copy-start(s32[4]{0:T(128)} %fusion.65) | copy-start | bytes 52
  22.9 7.2 %copy-start.21 = (bf16[1,4,64,256]{3,2,1,0:T(8,128)(2,1)S(1)}, bf16[1,4,64,256]{3,2,1,0:T(8,128)(2,1)}, u32[]{:S(2)}) copy-start(bf16[1,4,64,256]{3,2,1,0:T(8,128)(2,1)} %get-tuple-element.36) | copy-start | bytes 393220
  32.7 1.9 %copy-start.19 = (bf16[256,256]{1,0:T(8,128)(2,1)S(1)}, bf16[256,256]{1,0:T(8,128)(2,1)}, u32[]{:S(2)}) copy-start(bf16[256,256]{1,0:T(8,128)(2,1)} %param.19) | copy-start | bytes 393220
  34.7 1.9 %copy-start.15 = (bf16[256,256]{1,0:T(8,128)(2,1)S(1)}, bf16[256,256]{1,0:T(8,128)(2,1)}, u32[]{:S(2)}) copy-start(bf16[256,256]{1,0:T(8,128)(2,1)} %param.20) | copy-start | bytes 393220
  39.1 4.2 %copy-start.3 = (f32[8,4,128,128]{3,2,1,0:T(8,128)S(1)}, f32[8,4,128,128]{3,2,1,0:T(8,128)}, u32[]{:S(2)}) copy-start(f32[8,4,128,128]{3,2,1,0:T(8,128)} %fusion.27) | copy-start | bytes 6291460
  43.2 2.9 %copy-start.8 = (bf16[8,128,4,64]{1,3,2,0:T(8,128)(2,1)S(1)}, bf16[8,128,4,64]{1,3,2,0:T(8,128)(2,1)}, u32[]{:S(2)}) copy-start(bf16[8,128,4,64]{1,3,2,0:T(8,128)(2,1)} %copy.36) | copy-start | bytes 1572868
  46.2 1.9 %copy-start.29 = (f32[8,4,128,128]{2,3,1,0:T(8,128)S(1)}, f32[8,4,128,128]{2,3,1,0:T(8,128)}, u32[]{:S(2)}) copy-start(f32[8,4,128,128]{2,3,1,0:T(8,128)} %get-tuple-element.53) | copy-start | bytes 6291460
  46.2 1.9 %copy-start.30 = (f32[8,4,128]{2,1,0:T(4,128)S(1)}, f32[8,4,128]{2,1,0:T(4,128)}, u32[]{:S(2)}) copy-start(f32[8,4,128]{2,1,0:T(4,128)} %get-tuple-element.52) | copy-start | bytes 49156
  48.9 1.2 %copy-start.2 = (f32[64,16,256]{2,1,0:T(8,128)S(1)}, f32[64,16,256]{2,1,0:T(8,128)}, u32[]{:S(2)}) copy-start(f32[64,16,256]{2,1,0:T(8,128)} %copy.26) | copy-start | bytes 3145732
  48.9 1.2 %copy-start.18 = (bf16[256,256]{1,0:T(8,128)(2,1)S(1)}, bf16[256,256]{1,0:T(8,128)(2,1)}, u32[]{:S(2)}) copy-start(bf16[256,256]{1,0:T(8,128)(2,1)} %param.18) | copy-start | bytes 393220
  52.8 8.7 %collective-permute-start.4 = (bf16[4,64,256]{2,1,0:T(8,128)(2,1)S(1)}, bf16[4,64,256]{2,1,0:T(8,128)(2,1)S(1)}, u32[]{:S(2)}, u32[]{:S(2)}) collective-permute-start(bf16[4,64,256]{2,1,0:T(8,128)(2,1)S(1)} %get-tuple-element.27), channel_id=1, source_target_pairs={{0,8},{8,16},{16,24},{24,0},{1,9},{9,17},{17,25},{25,1},{2,10},{10... | collective-permute-start | bytes 393224 | tf_op jit(solution)/shard_map/ppermute | solution.py:93
  56.1 10.5 %collective-permute-start.5 = (bf16[4,64,256]{2,1,0:T(8,128)(2,1)S(1)}, bf16[4,64,256]{2,1,0:T(8,128)(2,1)S(1)}, u32[]{:S(2)}, u32[]{:S(2)}) collective-permute-start(bf16[4,64,256]{2,1,0:T(8,128)(2,1)S(1)} %get-tuple-element.26), channel_id=1, source_target_pairs={{0,16},{8,24},{16,0},{24,8},{1,17},{9,25},{17,1},{25,9},{2,18},{10... | collective-permute-start | bytes 393224 | tf_op jit(solution)/shard_map/ppermute | solution.py:93
  57.6 9.0 %collective-permute-start.6 = (bf16[4,64,256]{2,1,0:T(8,128)(2,1)S(1)}, bf16[4,64,256]{2,1,0:T(8,128)(2,1)S(1)}, u32[]{:S(2)}, u32[]{:S(2)}) collective-permute-start(bf16[4,64,256]{2,1,0:T(8,128)(2,1)S(1)} %get-tuple-element.25), channel_id=1, source_target_pairs={{0,24},{8,0},{16,8},{24,16},{1,25},{9,1},{17,9},{25,17},{2,26},{10... | collective-permute-start | bytes 393224 | tf_op jit(solution)/shard_map/ppermute | solution.py:93
  66.6 1.2 %copy-start.11 = (f32[4,256,256]{2,1,0:T(8,128)S(1)}, f32[4,256,256]{2,1,0:T(8,128)}, u32[]{:S(2)}) copy-start(f32[4,256,256]{2,1,0:T(8,128)} %get-tuple-element.51) | copy-start | bytes 3145732
  67.3 1.1 copy-start.6
  67.5 1.4 %copy-start.12 = (f32[32,2,8,128]{3,1,2,0:T(2,128)S(1)}, f32[32,2,8,128]{3,1,2,0:T(2,128)}, u32[]{:S(2)}) copy-start(f32[32,2,8,128]{3,1,2,0:T(2,128)} %copy.63) | copy-start | bytes 786436
  67.5 1.4 %copy-start.13 = (f32[32,2,8,128]{3,1,2,0:T(2,128)S(1)}, f32[32,2,8,128]{3,1,2,0:T(2,128)}, u32[]{:S(2)}) copy-start(f32[32,2,8,128]{3,1,2,0:T(2,128)} %copy.64) | copy-start | bytes 786436
  67.5 1.4 %copy-start.14 = (f32[32,2,8,128]{3,1,2,0:T(2,128)S(1)}, f32[32,2,8,128]{3,1,2,0:T(2,128)}, u32[]{:S(2)}) copy-start(f32[32,2,8,128]{3,1,2,0:T(2,128)} %copy.65) | copy-start | bytes 786436
  69.7 1.3 %copy-start.10 = (bf16[4,256,256]{2,1,0:T(8,128)(2,1)S(1)}, bf16[4,256,256]{2,1,0:T(8,128)(2,1)}, u32[]{:S(2)}) copy-start(bf16[4,256,256]{2,1,0:T(8,128)(2,1)} %copy-done.9) | copy-start | bytes 1572868
  70.6 2.0 %collective-permute-start.7 = (f32[131072]{0:T(1024)S(1)}, f32[131072]{0:T(1024)S(1)}, u32[]{:S(2)}, u32[]{:S(2)}) collective-permute-start(f32[131072]{0:T(1024)S(1)} %bitcast.217), channel_id=1, source_target_pairs={{0,1},{1,0},{2,3},{3,2},{4,5},{5,4},{6,7},{7,6},{8,9},{9,8},{10,11... | collective-permute-start | bytes 1572872 | tf_op jit(solution)/shard_map/ppermute | solution.py:33
  72.9 16.5 %copy-start.23 = (s32[4,128]{1,0:T(4,128)S(1)}, s32[4,128]{1,0:T(4,128)}, u32[]{:S(2)}) copy-start(s32[4,128]{1,0:T(4,128)} %param.15) | copy-start | bytes 6148
  72.9 16.5 %copy-start.26 = (pred[4,128]{1,0:T(4,128)(4,1)S(1)}, pred[4,128]{1,0:T(4,128)(4,1)}, u32[]{:S(2)}) copy-start(pred[4,128]{1,0:T(4,128)(4,1)} %copy-done.25) | copy-start | bytes 1540
  73.4 6.4 %collective-permute-start.10 = (f32[32768]{0:T(1024)S(1)}, f32[32768]{0:T(1024)S(1)}, u32[]{:S(2)}, u32[]{:S(2)}) collective-permute-start(f32[32768]{0:T(1024)S(1)} %bitcast.229), channel_id=1, source_target_pairs={{0,6},{1,7},{2,0},{3,1},{4,2},{5,3},{6,4},{7,5},{8,14},{9,15},{10,... | collective-permute-start | bytes 393224 | tf_op jit(solution)/shard_map/ppermute | solution.py:33
  75.3 7.5 %collective-permute-start.8 = (f32[32768]{0:T(1024)S(1)}, f32[32768]{0:T(1024)S(1)}, u32[]{:S(2)}, u32[]{:S(2)}) collective-permute-start(f32[32768]{0:T(1024)S(1)} %bitcast.227), channel_id=1, source_target_pairs={{0,2},{1,3},{2,4},{3,5},{4,6},{5,7},{6,0},{7,1},{8,10},{9,11},{10,... | collective-permute-start | bytes 393224 | tf_op jit(solution)/shard_map/ppermute | solution.py:33
  75.4 7.9 %collective-permute-start.9 = (f32[32768]{0:T(1024)S(1)}, f32[32768]{0:T(1024)S(1)}, u32[]{:S(2)}, u32[]{:S(2)}) collective-permute-start(f32[32768]{0:T(1024)S(1)} %bitcast.225), channel_id=1, source_target_pairs={{0,4},{1,5},{2,6},{3,7},{4,0},{5,1},{6,2},{7,3},{8,12},{9,13},{10,... | collective-permute-start | bytes 393224 | tf_op jit(solution)/shard_map/ppermute | solution.py:33
  77.5 11.8 %collective-permute-start.14 = (bf16[4,128,256]{2,1,0:T(8,128)(2,1)S(1)}, bf16[4,128,256]{2,1,0:T(8,128)(2,1)S(1)}, u32[]{:S(2)}, u32[]{:S(2)}) collective-permute-start(bf16[4,128,256]{2,1,0:T(8,128)(2,1)S(1)} %convolution_convert_fusion.6), channel_id=1, source_target_pairs={{0,7},{1,0},{2,1},{3,2},{4,3},{5,4},{6,5},{7,6},{8,15},{9,8},{10,9... | collective-permute-start | bytes 786440 | tf_op jit(solution)/shard_map/ppermute | solution.py:12
  83.5 16.9 %copy-start.24 = (pred[4]{0:T(512)(128)(4,1)S(1)}, pred[4]{0:T(512)(128)(4,1)}, u32[]{:S(2)}) copy-start(pred[4]{0:T(512)(128)(4,1)} %get-tuple-element.55) | copy-start | bytes 16
  83.6 7.0 %collective-permute-start.11 = (f32[8192]{0:T(1024)S(1)}, f32[8192]{0:T(1024)S(1)}, u32[]{:S(2)}, u32[]{:S(2)}) collective-permute-start(f32[8192]{0:T(1024)S(1)} %bitcast.236), channel_id=1, source_target_pairs={{0,8},{8,16},{16,24},{24,0},{1,9},{9,17},{17,25},{25,1},{2,10},{10... | collective-permute-start | bytes 98312 | tf_op jit(solution)/shard_map/ppermute | solution.py:33
  86.9 4.8 %collective-permute-start.12 = (f32[8192]{0:T(1024)S(1)}, f32[8192]{0:T(1024)S(1)}, u32[]{:S(2)}, u32[]{:S(2)}) collective-permute-start(f32[8192]{0:T(1024)S(1)} %bitcast.235), channel_id=1, source_target_pairs={{0,16},{8,24},{16,0},{24,8},{1,17},{9,25},{17,1},{25,9},{2,18},{10... | collective-permute-start | bytes 98312 | tf_op jit(solution)/shard_map/ppermute | solution.py:33
  88.5 3.9 %collective-permute-start.13 = (f32[8192]{0:T(1024)S(1)}, f32[8192]{0:T(1024)S(1)}, u32[]{:S(2)}, u32[]{:S(2)}) collective-permute-start(f32[8192]{0:T(1024)S(1)} %bitcast.234), channel_id=1, source_target_pairs={{0,24},{8,0},{16,8},{24,16},{1,25},{9,1},{17,9},{25,17},{2,26},{10... | collective-permute-start | bytes 98312 | tf_op jit(solution)/shard_map/ppermute | solution.py:33
  92.4 5.8 %collective-permute-start.15 = (f32[8192]{0:T(1024)S(1)}, f32[8192]{0:T(1024)S(1)}, u32[]{:S(2)}, u32[]{:S(2)}) collective-permute-start(f32[8192]{0:T(1024)S(1)} %add_add_fusion.1), channel_id=1, source_target_pairs={{0,8},{8,16},{16,24},{24,0},{1,9},{9,17},{17,25},{25,1},{2,10},{10... | collective-permute-start | bytes 98312 | tf_op jit(solution)/shard_map/ppermute | solution.py:45
  92.7 5.4 %collective-permute-start.16 = (f32[8192]{0:T(1024)S(1)}, f32[8192]{0:T(1024)S(1)}, u32[]{:S(2)}, u32[]{:S(2)}) collective-permute-start(f32[8192]{0:T(1024)S(1)} %add_add_fusion.1), channel_id=1, source_target_pairs={{0,16},{8,24},{16,0},{24,8},{1,17},{9,25},{17,1},{25,9},{2,18},{10... | collective-permute-start | bytes 98312 | tf_op jit(solution)/shard_map/ppermute | solution.py:45
  95.7 3.9 %collective-permute-start.17 = (f32[8192]{0:T(1024)S(1)}, f32[8192]{0:T(1024)S(1)}, u32[]{:S(2)}, u32[]{:S(2)}) collective-permute-start(f32[8192]{0:T(1024)S(1)} %add_add_fusion.1), channel_id=1, source_target_pairs={{0,24},{8,0},{16,8},{24,16},{1,25},{9,1},{17,9},{25,17},{2,26},{10... | collective-permute-start | bytes 98312 | tf_op jit(solution)/shard_map/ppermute | solution.py:45
  100.5 6.0 %collective-permute-start.18 = (f32[32768]{0:T(1024)S(1)}, f32[32768]{0:T(1024)S(1)}, u32[]{:S(2)}, u32[]{:S(2)}) collective-permute-start(f32[32768]{0:T(1024)S(1)} %bitcast.220), channel_id=1, source_target_pairs={{0,2},{1,3},{2,4},{3,5},{4,6},{5,7},{6,0},{7,1},{8,10},{9,11},{10,... | collective-permute-start | bytes 393224 | tf_op jit(solution)/shard_map/ppermute | solution.py:45
  101.1 6.4 %collective-permute-start.19 = (f32[32768]{0:T(1024)S(1)}, f32[32768]{0:T(1024)S(1)}, u32[]{:S(2)}, u32[]{:S(2)}) collective-permute-start(f32[32768]{0:T(1024)S(1)} %bitcast.221), channel_id=1, source_target_pairs={{0,4},{1,5},{2,6},{3,7},{4,0},{5,1},{6,2},{7,3},{8,12},{9,13},{10,... | collective-permute-start | bytes 393224 | tf_op jit(solution)/shard_map/ppermute | solution.py:45
  102.3 5.5 %collective-permute-start.20 = (f32[32768]{0:T(1024)S(1)}, f32[32768]{0:T(1024)S(1)}, u32[]{:S(2)}, u32[]{:S(2)}) collective-permute-start(f32[32768]{0:T(1024)S(1)} %bitcast.222), channel_id=1, source_target_pairs={{0,6},{1,7},{2,0},{3,1},{4,2},{5,3},{6,4},{7,5},{8,14},{9,15},{10,... | collective-permute-start | bytes 393224 | tf_op jit(solution)/shard_map/ppermute | solution.py:45
  109.4 2.0 %collective-permute-start.21 = (f32[131072]{0:T(1024)S(1)}, f32[131072]{0:T(1024)S(1)}, u32[]{:S(2)}, u32[]{:S(2)}) collective-permute-start(f32[131072]{0:T(1024)S(1)} %bitcast.216), channel_id=1, source_target_pairs={{0,1},{1,0},{2,3},{3,2},{4,5},{5,4},{6,7},{7,6},{8,9},{9,8},{10,11... | collective-permute-start | bytes 1572872 | tf_op jit(solution)/shard_map/ppermute | solution.py:40
  (5 other events, 4.5 us)

commit v12 on v11

--- a/solution.py
+++ b/solution.py
@@ -27,6 +27,10 @@
 def _scatter_step(flat, axis, stride, group):
     digit = (lax.axis_index(axis) // stride) % group
     chunks = flat.reshape(group, -1)
+    if group == 2:
+        keep = jnp.where(digit == 0, chunks[0], chunks[1])
+        send = jnp.where(digit == 0, chunks[1], chunks[0])
+        return keep + lax.ppermute(send, axis, _group_pairs(axis, stride, group, 1))
     total = lax.dynamic_index_in_dim(chunks, digit, 0, keepdims=False)
     for shift in range(1, group):
         send = lax.dynamic_index_in_dim(chunks, (digit + shift) % group, 0, keepdims=False)
@@ -85,10 +89,10 @@
 def exchange(value, axis, split_axis, concat_axis):
     count = lax.axis_size(axis)
     mine = lax.axis_index(axis)
-    pieces = jnp.stack(jnp.split(value, count, axis=split_axis))
+    size = value.shape[split_axis] // count
     got = []
     for shift in range(count):
-        send = lax.dynamic_index_in_dim(pieces, (mine + shift) % count, 0, keepdims=False)
+        send = lax.dynamic_slice_in_dim(value, ((mine + shift) % count) * size, size, axis=split_axis)
         if shift:
             send = lax.ppermute(send, axis, [(i, (i + shift) % count) for i in range(count)])
         got.append(send)

time: 113 us -> 112 us (level)
  local copies, waits for them, and re-layouts: 21.2 us -> 17.6 us
    unnamed x69 -> x67, local copies, waits for them, and re-layouts: 5.68 us -> 3.64 us
    ppermute x6, waiting for transfers between devices: 10.2 us -> 12.1 us  [exchange(): lax.ppermute(send, axis, [(i, (i + shift) % count) for i in range(count)])]
    convert_element_type x1, other arithmetic: 0.42 us -> 1.63 us  [local(): pre_grad = (back_days.astype(jnp.float32) * sigmoid_val * (1.0 + preact *...]
    ppermute x7 -> x6, waiting for transfers between devices: 7.16 us -> 6.45 us  [_scatter_step(): lax.ppermute(send, axis, _group_pairs(axis, stride, group, shift))]
    ppermute x7 -> x6, starting transfers between devices: 9.43 us -> 9.36 us  [_scatter_step(): lax.ppermute(send, axis, _group_pairs(axis, stride, group, shift))]
  transfers between devices with their start and end apart: 22 -> 22, of which waited for: 15 -> 16; matrix products, arithmetic and copies ran while one was open for 15% -> 13% of each run, Pallas kernels for 0% -> 0%
where the time goes in v12:
time: 112 us; the launch traced here: 111 us
  starting transfers between devices  32.3 us (29%)
  waiting for transfers between devices  25.7 us (23%)
  matrix products  23 us (21%)
  local copies, waits for them, and re-layouts  17.6 us (16%)
  other arithmetic  11.3 us (10%)
  between operations  1.45 us (1%)
    ppermute x6, starting transfers between devices, exchange(): lax.ppermute(send, axis, [(i, (i + shift) % count) for i in range(count)])  12.4 us
    ppermute x6, waiting for transfers between devices, exchange(): lax.ppermute(send, axis, [(i, (i + shift) % count) for i in range(count)])  12.1 us
    ppermute x6, starting transfers between devices, _scatter_step(): lax.ppermute(send, axis, _group_pairs(axis, stride, group, shift))  9.36 us
    ppermute x6, starting transfers between devices, _gather_step(): lax.ppermute(flat, axis, _group_pairs(axis, stride, group, shift))  8.65 us
    ppermute x6, waiting for transfers between devices, _scatter_step(): lax.ppermute(send, axis, _group_pairs(axis, stride, group, shift))  6.45 us
    ppermute x6, waiting for transfers between devices, _gather_step(): lax.ppermute(flat, axis, _group_pairs(axis, stride, group, shift))  5.63 us
    sub x1, matrix products, attend_blocked(): exponent = jnp.exp(scores - highest)  4.14 us
    dot_general x4, matrix products, contract(): return jnp.einsum(spec, left, right, preferred_element_type=jnp.float32)  3.8 us
  transfers between devices with their start and end apart: 22, of which 16 were waited for; matrix products, arithmetic and copies ran while one was open for 13% of the time, Pallas kernels for 0%

profile of v12, /device:TPU:0, one launch (start us, length us, event | category | flops | bytes accessed | tf_op | source)
XLA Modules:
  0.0 111.3 jit_solution(8749947088567214265)
XLA Ops:
  1.9 2.1 %convolution_convert_fusion.7 = bf16[4,128,256]{2,1,0:T(8,128)(2,1)} fusion(bf16[4,256,256]{2,1,0:T(8,128)(2,1)} %param.12, s32[4,128]{1,0:T(4,128)} %param.15, pred[4,128]{1,0:T(4,128)(4,1)S(1)} %iota_compare_fusion.12), kind=kOutput, calls=%fused_computation.50 | convolution fusion | flops 67502080 | bytes 788992 | tf_op jit(solution)/shard_map/dsn,dnh->dsh/dot_general | solution.py:296
  5.0 1.2 %convert_reduce_fusion = f32[4,256]{1,0:T(4,128)S(1)} fusion(s32[4,1024]{1,0:T(4,128)} %param.14), kind=kLoop, calls=%fused_computation.6 | loop fusion | flops 4193280 | bytes 20480 | tf_op jit(solution)/shard_map/reduce_sum | solution.py:311
  6.3 2.4 %fusion.17 = bf16[4,256,256]{2,1,0:T(8,128)(2,1)S(1)} fusion(s32[4,1024]{1,0:T(4,128)} %param.13, s32[4,1024]{1,0:T(4,128)} %param.14), kind=kOutput, calls=%fused_computation.44 | convolution fusion | flops 539230208 | bytes 557056 | tf_op jit(solution)/shard_map/der,des->drs/dot_general | solution.py:305
  9.5 1.3 %fusion.21 = bf16[4,256,128]{2,1,0:T(8,128)(2,1)S(1)} fusion(s32[4,1024]{1,0:T(4,128)S(1)} %copy-done.18, s32[128]{0:T(128)S(1)} %iota_add_fusion, s32[4,1024]{1,0:T(4,128)S(1)} %copy-done.24), kind=kOutput, calls=%fused_computation.48 | convolution fusion | flops 270139392 | bytes 295424 | tf_op jit(solution)/shard_map/der,des->drs/dot_general | solution.py:308
  11.7 1.3 %fusion.15 = bf16[4,256,256]{2,1,0:T(8,128)(2,1)S(1)} fusion(f32[4,256,256]{2,1,0:T(8,128)S(1)} %fusion.71, bf16[4,256,128]{2,1,0:T(8,128)(2,1)S(1)} %fusion.21, bf16[4,128,256]{2,1,0:T(8,128)(2,1)} %collective-permute-done, bf16[4,256,256]{2,1,0:T(8,128)(2,1)S(1)} %copy-done.1, f32[4,256]{1,0:T(4,128)S(1)} %add_divide_fusion.1), kind=kOutput, calls=%fused_computation.36 | convolution fusion | flops 68419584 | bytes 2625536 | tf_op jit(solution)/shard_map/drs,dsh->drh/dot_general | solution.py:317
  13.0 1.3 %fusion.24 = (bf16[4,256,256]{2,1,0:T(8,128)(2,1)S(1)}, f32[4,256,256]{2,1,0:T(8,128)}) fusion(bf16[4,256,256]{2,1,0:T(8,128)(2,1)S(1)} %copy-done.1, bf16[4,256,256]{2,1,0:T(8,128)(2,1)S(1)} %fusion.15, bf16[256,256]{1,0:T(8,128)(2,1)S(1)} %copy-done), kind=kOutput, calls=%fused_computation.55 | convolution fusion | flops 136052736 | bytes 2752512 | tf_op jit(solution)/shard_map/drh,hk->drk/dot_general | solution.py:319
  14.4 0.8 dynamic-slice_bitcast_fusion
  15.2 2.6 %collective-permute-start.1 = (bf16[4,64,256]{2,1,0:T(8,128)(2,1)}, bf16[4,64,256]{2,1,0:T(8,128)(2,1)}, u32[]{:S(2)}, u32[]{:S(2)}) collective-permute-start(bf16[4,64,256]{2,1,0:T(8,128)(2,1)} %get-tuple-element.33), channel_id=1, source_target_pairs={{0,8},{8,16},{16,24},{24,0},{1,9},{9,17},{17,25},{25,1},{2,10},{10... | collective-permute-start | bytes 393224 | tf_op jit(solution)/shard_map/ppermute | solution.py:97
  17.7 2.6 %collective-permute-start.2 = (bf16[4,64,256]{2,1,0:T(8,128)(2,1)}, bf16[4,64,256]{2,1,0:T(8,128)(2,1)}, u32[]{:S(2)}, u32[]{:S(2)}) collective-permute-start(bf16[4,64,256]{2,1,0:T(8,128)(2,1)} %get-tuple-element.32), channel_id=1, source_target_pairs={{0,16},{8,24},{16,0},{24,8},{1,17},{9,25},{17,1},{25,9},{2,18},{10... | collective-permute-start | bytes 393224 | tf_op jit(solution)/shard_map/ppermute | solution.py:97
  20.3 1.3 %collective-permute-start.3 = (bf16[4,64,256]{2,1,0:T(8,128)(2,1)}, bf16[4,64,256]{2,1,0:T(8,128)(2,1)}, u32[]{:S(2)}, u32[]{:S(2)}) collective-permute-start(bf16[4,64,256]{2,1,0:T(8,128)(2,1)} %get-tuple-element.31), channel_id=1, source_target_pairs={{0,24},{8,0},{16,8},{24,16},{1,25},{9,1},{17,9},{25,17},{2,26},{10... | collective-permute-start | bytes 393224 | tf_op jit(solution)/shard_map/ppermute | solution.py:97
  23.5 1.6 %copy.26 = f32[64,16,256]{2,1,0:T(8,128)} copy(f32[64,16,256]{2,0,1:T(8,128)S(1)} %bitcast_convert_fusion) | data formatting | bytes 2097152 | tf_op jit(solution)/shard_map/convert_element_type | solution.py:268
  25.1 5.0 %collective-permute-done.2 = bf16[4,64,256]{2,1,0:T(8,128)(2,1)} collective-permute-done((bf16[4,64,256]{2,1,0:T(8,128)(2,1)}, bf16[4,64,256]{2,1,0:T(8,128)(2,1)}, u32[]{:S(2)}, u32[]{:S(2)}) %collective-permute-start.2) | collective-permute-done | bytes 131104 | tf_op jit(solution)/shard_map/ppermute | solution.py:97
  30.3 1.1 pad_maximum_fusion
  33.6 1.2 %copy.30 = bf16[8,128,4,64]{1,3,2,0:T(8,128)(2,1)} copy(bf16[8,128,4,64]{3,2,1,0:T(4,128)(2,1)S(1)} %reshape.434) | data formatting | bytes 1048576 | tf_op jit(solution)/shard_map/reshape | solution.py:226
  35.5 1.2 %copy.36 = bf16[8,128,4,64]{1,3,2,0:T(8,128)(2,1)} copy(bf16[8,128,4,64]{3,2,1,0:T(4,128)(2,1)S(1)} %reshape.433) | data formatting | bytes 1048576 | tf_op jit(solution)/shard_map/reshape | solution.py:226
  37.4 1.8 %fusion.27 = f32[8,4,128,128]{3,2,1,0:T(8,128)} fusion(bf16[8,128,4,64]{1,3,2,0:T(8,128)(2,1)S(1)} %copy.35, bf16[8,128,4,64]{3,2,1,0:T(4,128)(2,1)S(1)} %reshape.432), kind=kOutput, calls=%fused_computation.59 | convolution fusion | flops 67108864 | bytes 3145728 | tf_op jit(solution)/shard_map/gihd,gjhd->ghij/dot_general | solution.py:237
  39.2 4.1 %fusion.70 = (f32[8,4,128]{2,1,0:T(4,128)}, f32[8,4,128,128]{2,3,1,0:T(8,128)}) fusion(pred[128,128]{0,1:T(8,128)(4,1)} %compare_and_fusion, bf16[8,128,4,64]{1,3,2,0:T(8,128)(2,1)} %copy.30, bf16[8,128,4,64]{1,3,2,0:T(8,128)(2,1)} %copy.36), kind=kOutput, calls=%fused_computation.187 | convolution fusion | flops 69206144 | bytes 3178496 | tf_op jit(solution)/shard_map/sub | solution.py:242
  43.4 2.9 %fusion.7 = bf16[8,4,128,128]{2,3,1,0:T(8,128)(2,1)S(1)} fusion(f32[8,4,128,128]{3,2,1,0:T(8,128)S(1)} %copy-done.3, f32[8,4,128,128]{2,3,1,0:T(8,128)} %get-tuple-element.43, f32[8,4,128]{2,1,0:T(4,128)} %get-tuple-element.42), kind=kOutput, calls=%fused_computation.16 | output fusion | flops 3674239 | bytes 5259264 | tf_op jit(solution)/shard_map/sub | solution.py:248
  47.4 0.8 fusion.19
  48.2 0.8 fusion.20
  52.5 3.2 %collective-permute-start.4 = (bf16[4,64,256]{2,1,0:T(8,128)(2,1)S(1)}, bf16[4,64,256]{2,1,0:T(8,128)(2,1)S(1)}, u32[]{:S(2)}, u32[]{:S(2)}) collective-permute-start(bf16[4,64,256]{2,1,0:T(8,128)(2,1)S(1)} %bitcast.201), channel_id=1, source_target_pairs={{0,8},{8,16},{16,24},{24,0},{1,9},{9,17},{17,25},{25,1},{2,10},{10... | collective-permute-start | bytes 393224 | tf_op jit(solution)/shard_map/ppermute | solution.py:97
  55.7 1.4 %collective-permute-start.5 = (bf16[4,64,256]{2,1,0:T(8,128)(2,1)S(1)}, bf16[4,64,256]{2,1,0:T(8,128)(2,1)S(1)}, u32[]{:S(2)}, u32[]{:S(2)}) collective-permute-start(bf16[4,64,256]{2,1,0:T(8,128)(2,1)S(1)} %bitcast.202), channel_id=1, source_target_pairs={{0,16},{8,24},{16,0},{24,8},{1,17},{9,25},{17,1},{25,9},{2,18},{10... | collective-permute-start | bytes 393224 | tf_op jit(solution)/shard_map/ppermute | solution.py:97
  57.1 1.3 %collective-permute-start.6 = (bf16[4,64,256]{2,1,0:T(8,128)(2,1)S(1)}, bf16[4,64,256]{2,1,0:T(8,128)(2,1)S(1)}, u32[]{:S(2)}, u32[]{:S(2)}) collective-permute-start(bf16[4,64,256]{2,1,0:T(8,128)(2,1)S(1)} %bitcast.203), channel_id=1, source_target_pairs={{0,24},{8,0},{16,8},{24,16},{1,25},{9,1},{17,9},{25,17},{2,26},{10... | collective-permute-start | bytes 393224 | tf_op jit(solution)/shard_map/ppermute | solution.py:97
  59.3 1.6 %collective-permute-done.4 = bf16[4,64,256]{2,1,0:T(8,128)(2,1)S(1)} collective-permute-done((bf16[4,64,256]{2,1,0:T(8,128)(2,1)S(1)}, bf16[4,64,256]{2,1,0:T(8,128)(2,1)S(1)}, u32[]{:S(2)}, u32[]{:S(2)}) %collective-permute-start.4) | collective-permute-done | bytes 131104 | tf_op jit(solution)/shard_map/ppermute | solution.py:97
  60.8 5.3 %collective-permute-done.5 = bf16[4,64,256]{2,1,0:T(8,128)(2,1)S(1)} collective-permute-done((bf16[4,64,256]{2,1,0:T(8,128)(2,1)S(1)}, bf16[4,64,256]{2,1,0:T(8,128)(2,1)S(1)}, u32[]{:S(2)}, u32[]{:S(2)}) %collective-permute-start.5) | collective-permute-done | bytes 131104 | tf_op jit(solution)/shard_map/ppermute | solution.py:97
  67.0 1.6 %fusion.26 = bf16[4,256,256]{2,1,0:T(8,128)(2,1)S(1)} fusion(f32[4,256,256]{2,1,0:T(8,128)} %get-tuple-element.41, bf16[4,64,256]{2,1,0:T(8,128)(2,1)S(1)} %get-tuple-element.19, bf16[4,64,256]{2,1,0:T(8,128)(2,1)S(1)} %get-tuple-element.20, bf16[4,64,256]{2,1,0:T(8,128)(2,1)S(1)} %get-tuple-element.21, bf16[4,64,256]{2,1,0:T(8,128)(2,1)S(1)} %get-tuple-element.18), kind=kLoop, calls=%fused_computation.57 | loop fusion | flops 4456448 | bytes 2097152 | tf_op jit(solution)/shard_map/convert_element_type | solution.py:330
  70.2 0.9 convolution_add_fusion
  72.1 2.1 %collective-permute-start.10 = (f32[32768]{0:T(1024)S(1)}, f32[32768]{0:T(1024)S(1)}, u32[]{:S(2)}, u32[]{:S(2)}) collective-permute-start(f32[32768]{0:T(1024)S(1)} %bitcast.214), channel_id=1, source_target_pairs={{0,6},{1,7},{2,0},{3,1},{4,2},{5,3},{6,4},{7,5},{8,14},{9,15},{10,... | collective-permute-start | bytes 393224 | tf_op jit(solution)/shard_map/ppermute | solution.py:37
  74.2 1.5 %collective-permute-start.9 = (f32[32768]{0:T(1024)S(1)}, f32[32768]{0:T(1024)S(1)}, u32[]{:S(2)}, u32[]{:S(2)}) collective-permute-start(f32[32768]{0:T(1024)S(1)} %bitcast.211), channel_id=1, source_target_pairs={{0,4},{1,5},{2,6},{3,7},{4,0},{5,1},{6,2},{7,3},{8,12},{9,13},{10,... | collective-permute-start | bytes 393224 | tf_op jit(solution)/shard_map/ppermute | solution.py:37
  76.2 1.3 %collective-permute-start.14 = (bf16[4,128,256]{2,1,0:T(8,128)(2,1)S(1)}, bf16[4,128,256]{2,1,0:T(8,128)(2,1)S(1)}, u32[]{:S(2)}, u32[]{:S(2)}) collective-permute-start(bf16[4,128,256]{2,1,0:T(8,128)(2,1)S(1)} %convolution_convert_fusion.6), channel_id=1, source_target_pairs={{0,7},{1,0},{2,1},{3,2},{4,3},{5,4},{6,5},{7,6},{8,15},{9,8},{10,9... | collective-permute-start | bytes 786440 | tf_op jit(solution)/shard_map/ppermute | solution.py:12
  77.5 0.8 collective-permute-done.10
  78.3 3.2 %collective-permute-done.8 = f32[32768]{0:T(1024)S(1)} collective-permute-done((f32[32768]{0:T(1024)S(1)}, f32[32768]{0:T(1024)S(1)}, u32[]{:S(2)}, u32[]{:S(2)}) %collective-permute-start.8) | collective-permute-done | bytes 131104 | tf_op jit(solution)/shard_map/ppermute | solution.py:37
  82.5 3.3 %collective-permute-start.11 = (f32[8192]{0:T(1024)S(1)}, f32[8192]{0:T(1024)S(1)}, u32[]{:S(2)}, u32[]{:S(2)}) collective-permute-start(f32[8192]{0:T(1024)S(1)} %bitcast.220), channel_id=1, source_target_pairs={{0,8},{8,16},{16,24},{24,0},{1,9},{9,17},{17,25},{25,1},{2,10},{10... | collective-permute-start | bytes 98312 | tf_op jit(solution)/shard_map/ppermute | solution.py:37
  85.8 1.5 %collective-permute-start.12 = (f32[8192]{0:T(1024)S(1)}, f32[8192]{0:T(1024)S(1)}, u32[]{:S(2)}, u32[]{:S(2)}) collective-permute-start(f32[8192]{0:T(1024)S(1)} %bitcast.219), channel_id=1, source_target_pairs={{0,16},{8,24},{16,0},{24,8},{1,17},{9,25},{17,1},{25,9},{2,18},{10... | collective-permute-start | bytes 98312 | tf_op jit(solution)/shard_map/ppermute | solution.py:37
  87.3 0.9 collective-permute-start.13
  88.3 1.3 %convolution_add_fusion.4 = f32[4,256,256]{2,1,0:T(8,128)} fusion(f32[4,256,256]{2,1,0:T(8,128)S(1)} %convolution_add_fusion, bf16[4,128,256]{2,1,0:T(8,128)(2,1)S(1)} %collective-permute-done.14, s32[4,128]{1,0:T(4,128)S(1)} %copy-done.19, pred[4,128]{1,0:T(4,128)(4,1)S(1)} %copy-done.22), kind=kOutput, calls=%fused_computation.29 | convolution fusion | flops 67633152 | bytes 2361856 | tf_op jit(solution)/shard_map/dsn,dsh->dnh/dot_general | solution.py:354
  89.5 1.1 collective-permute-done.12
  91.6 3.0 %collective-permute-start.16 = (f32[8192]{0:T(1024)S(1)}, f32[8192]{0:T(1024)S(1)}, u32[]{:S(2)}, u32[]{:S(2)}) collective-permute-start(f32[8192]{0:T(1024)S(1)} %add_add_fusion.1), channel_id=1, source_target_pairs={{0,16},{8,24},{16,0},{24,8},{1,17},{9,25},{17,1},{25,9},{2,18},{10... | collective-permute-start | bytes 98312 | tf_op jit(solution)/shard_map/ppermute | solution.py:49
  94.6 1.0 collective-permute-start.17
  95.7 1.4 %collective-permute-done.15 = f32[8192]{0:T(1024)S(1)} collective-permute-done((f32[8192]{0:T(1024)S(1)}, f32[8192]{0:T(1024)S(1)}, u32[]{:S(2)}, u32[]{:S(2)}) %collective-permute-start.15) | collective-permute-done | bytes 32800 | tf_op jit(solution)/shard_map/ppermute | solution.py:49
  97.0 1.5 %collective-permute-done.17 = f32[8192]{0:T(1024)S(1)} collective-permute-done((f32[8192]{0:T(1024)S(1)}, f32[8192]{0:T(1024)S(1)}, u32[]{:S(2)}, u32[]{:S(2)}) %collective-permute-start.17) | collective-permute-done | bytes 32800 | tf_op jit(solution)/shard_map/ppermute | solution.py:49
  100.0 1.1 %collective-permute-start.19 = (f32[32768]{0:T(1024)S(1)}, f32[32768]{0:T(1024)S(1)}, u32[]{:S(2)}, u32[]{:S(2)}) collective-permute-start(f32[32768]{0:T(1024)S(1)} %bitcast.205), channel_id=1, source_target_pairs={{0,4},{1,5},{2,6},{3,7},{4,0},{5,1},{6,2},{7,3},{8,12},{9,13},{10,... | collective-permute-start | bytes 393224 | tf_op jit(solution)/shard_map/ppermute | solution.py:49
  101.2 2.5 %collective-permute-start.20 = (f32[32768]{0:T(1024)S(1)}, f32[32768]{0:T(1024)S(1)}, u32[]{:S(2)}, u32[]{:S(2)}) collective-permute-start(f32[32768]{0:T(1024)S(1)} %bitcast.206), channel_id=1, source_target_pairs={{0,6},{1,7},{2,0},{3,1},{4,2},{5,3},{6,4},{7,5},{8,14},{9,15},{10,... | collective-permute-start | bytes 393224 | tf_op jit(solution)/shard_map/ppermute | solution.py:49
  103.8 1.6 %collective-permute-done.18 = f32[32768]{0:T(1024)S(1)} collective-permute-done((f32[32768]{0:T(1024)S(1)}, f32[32768]{0:T(1024)S(1)}, u32[]{:S(2)}, u32[]{:S(2)}) %collective-permute-start.18) | collective-permute-done | bytes 131104 | tf_op jit(solution)/shard_map/ppermute | solution.py:49
  105.4 1.0 collective-permute-done.19
  107.1 0.8 gather_fusion.1
  108.8 1.3 %collective-permute-done.21 = f32[131072]{0:T(1024)S(1)} collective-permute-done((f32[131072]{0:T(1024)S(1)}, f32[131072]{0:T(1024)S(1)}, u32[]{:S(2)}, u32[]{:S(2)}) %collective-permute-start.21) | collective-permute-done | bytes 524320 | tf_op jit(solution)/shard_map/ppermute | solution.py:44
  110.4 1.0 fusion.69
  (151 shorter events, 23.8 us)
Async XLA Ops:
  0.6 12.4 %copy-start = (bf16[256,256]{1,0:T(8,128)(2,1)S(1)}, bf16[256,256]{1,0:T(8,128)(2,1)}, u32[]{:S(2)}) copy-start(bf16[256,256]{1,0:T(8,128)(2,1)} %param.17) | copy-start | bytes 393220
  4.0 7.7 %collective-permute-start = (bf16[4,128,256]{2,1,0:T(8,128)(2,1)}, bf16[4,128,256]{2,1,0:T(8,128)(2,1)}, u32[]{:S(2)}, u32[]{:S(2)}) collective-permute-start(bf16[4,128,256]{2,1,0:T(8,128)(2,1)} %convolution_convert_fusion.7), channel_id=1, source_target_pairs={{0,1},{1,2},{2,3},{3,4},{4,5},{5,6},{6,7},{7,0},{8,9},{9,10},{10,1... | collective-permute-start | bytes 786440 | tf_op jit(solution)/shard_map/ppermute | solution.py:12
  6.3 2.4 %copy-start.1 = (bf16[4,256,256]{2,1,0:T(8,128)(2,1)S(1)}, bf16[4,256,256]{2,1,0:T(8,128)(2,1)}, u32[]{:S(2)}) copy-start(bf16[4,256,256]{2,1,0:T(8,128)(2,1)} %param.12) | copy-start | bytes 1572868
  8.7 2.2 %copy-start.9 = (bf16[4,256,256]{2,1,0:T(8,128)(2,1)}, bf16[4,256,256]{2,1,0:T(8,128)(2,1)S(1)}, u32[]{:S(2)}) copy-start(bf16[4,256,256]{2,1,0:T(8,128)(2,1)S(1)} %fusion.17) | copy-start | bytes 1572868
  8.7 0.7 copy-start.18
  8.7 0.8 copy-start.24
  9.5 2.1 %copy-start.4 = (bf16[16,1,1,64,256]{4,3,2,1,0:T(8,128)(2,1)S(1)}, bf16[16,1,1,64,256]{4,3,2,1,0:T(8,128)(2,1)}, u32[]{:S(2)}) copy-start(bf16[16,1,1,64,256]{4,3,2,1,0:T(8,128)(2,1)} %param.21) | copy-start | bytes 1572868
  13.0 1.4 %copy-start.5 = (bf16[4,256,256]{2,1,0:T(8,128)(2,1)}, bf16[4,256,256]{2,1,0:T(8,128)(2,1)S(1)}, u32[]{:S(2)}) copy-start(bf16[4,256,256]{2,1,0:T(8,128)(2,1)S(1)} %fusion.15) | copy-start | bytes 1572868
  15.2 10.0 %collective-permute-start.1 = (bf16[4,64,256]{2,1,0:T(8,128)(2,1)}, bf16[4,64,256]{2,1,0:T(8,128)(2,1)}, u32[]{:S(2)}, u32[]{:S(2)}) collective-permute-start(bf16[4,64,256]{2,1,0:T(8,128)(2,1)} %get-tuple-element.33), channel_id=1, source_target_pairs={{0,8},{8,16},{16,24},{24,0},{1,9},{9,17},{17,25},{25,1},{2,10},{10... | collective-permute-start | bytes 393224 | tf_op jit(solution)/shard_map/ppermute | solution.py:97
  17.7 12.4 %collective-permute-start.2 = (bf16[4,64,256]{2,1,0:T(8,128)(2,1)}, bf16[4,64,256]{2,1,0:T(8,128)(2,1)}, u32[]{:S(2)}, u32[]{:S(2)}) collective-permute-start(bf16[4,64,256]{2,1,0:T(8,128)(2,1)} %get-tuple-element.32), channel_id=1, source_target_pairs={{0,16},{8,24},{16,0},{24,8},{1,17},{9,25},{17,1},{25,9},{2,18},{10... | collective-permute-start | bytes 393224 | tf_op jit(solution)/shard_map/ppermute | solution.py:97
  20.3 10.0 %collective-permute-start.3 = (bf16[4,64,256]{2,1,0:T(8,128)(2,1)}, bf16[4,64,256]{2,1,0:T(8,128)(2,1)}, u32[]{:S(2)}, u32[]{:S(2)}) collective-permute-start(bf16[4,64,256]{2,1,0:T(8,128)(2,1)} %get-tuple-element.31), channel_id=1, source_target_pairs={{0,24},{8,0},{16,8},{24,16},{1,25},{9,1},{17,9},{25,17},{2,26},{10... | collective-permute-start | bytes 393224 | tf_op jit(solution)/shard_map/ppermute | solution.py:97
  22.9 2.2 %copy-start.23 = (s32[4]{0:T(128)S(1)}, s32[4]{0:T(128)}, u32[]{:S(2)}) copy-start(s32[4]{0:T(128)} %fusion.65) | copy-start | bytes 52
  22.9 7.4 %copy-start.17 = (bf16[1,4,64,256]{3,2,1,0:T(8,128)(2,1)S(1)}, bf16[1,4,64,256]{3,2,1,0:T(8,128)(2,1)}, u32[]{:S(2)}) copy-start(bf16[1,4,64,256]{3,2,1,0:T(8,128)(2,1)} %get-tuple-element.30) | copy-start | bytes 393220
  32.0 0.9 copy-start.13
  32.9 1.9 %copy-start.15 = (bf16[256,256]{1,0:T(8,128)(2,1)S(1)}, bf16[256,256]{1,0:T(8,128)(2,1)}, u32[]{:S(2)}) copy-start(bf16[256,256]{1,0:T(8,128)(2,1)} %param.19) | copy-start | bytes 393220
  34.8 1.9 %copy-start.11 = (bf16[256,256]{1,0:T(8,128)(2,1)S(1)}, bf16[256,256]{1,0:T(8,128)(2,1)}, u32[]{:S(2)}) copy-start(bf16[256,256]{1,0:T(8,128)(2,1)} %param.20) | copy-start | bytes 393220
  39.2 4.1 %copy-start.3 = (f32[8,4,128,128]{3,2,1,0:T(8,128)S(1)}, f32[8,4,128,128]{3,2,1,0:T(8,128)}, u32[]{:S(2)}) copy-start(f32[8,4,128,128]{3,2,1,0:T(8,128)} %fusion.27) | copy-start | bytes 6291460
  43.4 2.9 %copy-start.8 = (bf16[8,128,4,64]{1,3,2,0:T(8,128)(2,1)S(1)}, bf16[8,128,4,64]{1,3,2,0:T(8,128)(2,1)}, u32[]{:S(2)}) copy-start(bf16[8,128,4,64]{1,3,2,0:T(8,128)(2,1)} %copy.36) | copy-start | bytes 1572868
  46.3 1.0 copy-start.7
  46.3 1.9 %copy-start.25 = (f32[8,4,128,128]{2,3,1,0:T(8,128)S(1)}, f32[8,4,128,128]{2,3,1,0:T(8,128)}, u32[]{:S(2)}) copy-start(f32[8,4,128,128]{2,3,1,0:T(8,128)} %get-tuple-element.43) | copy-start | bytes 6291460
  46.3 1.9 %copy-start.26 = (f32[8,4,128]{2,1,0:T(4,128)S(1)}, f32[8,4,128]{2,1,0:T(4,128)}, u32[]{:S(2)}) copy-start(f32[8,4,128]{2,1,0:T(4,128)} %get-tuple-element.42) | copy-start | bytes 49156
  49.0 1.2 %copy-start.2 = (f32[64,16,256]{2,1,0:T(8,128)S(1)}, f32[64,16,256]{2,1,0:T(8,128)}, u32[]{:S(2)}) copy-start(f32[64,16,256]{2,1,0:T(8,128)} %copy.26) | copy-start | bytes 3145732
  49.0 1.2 %copy-start.14 = (bf16[256,256]{1,0:T(8,128)(2,1)S(1)}, bf16[256,256]{1,0:T(8,128)(2,1)}, u32[]{:S(2)}) copy-start(bf16[256,256]{1,0:T(8,128)(2,1)} %param.18) | copy-start | bytes 393220
  49.7 1.0 copy-start.16
  50.7 1.1 copy-start.12
  52.5 8.4 %collective-permute-start.4 = (bf16[4,64,256]{2,1,0:T(8,128)(2,1)S(1)}, bf16[4,64,256]{2,1,0:T(8,128)(2,1)S(1)}, u32[]{:S(2)}, u32[]{:S(2)}) collective-permute-start(bf16[4,64,256]{2,1,0:T(8,128)(2,1)S(1)} %bitcast.201), channel_id=1, source_target_pairs={{0,8},{8,16},{16,24},{24,0},{1,9},{9,17},{17,25},{25,1},{2,10},{10... | collective-permute-start | bytes 393224 | tf_op jit(solution)/shard_map/ppermute | solution.py:97
  55.7 10.5 %collective-permute-start.5 = (bf16[4,64,256]{2,1,0:T(8,128)(2,1)S(1)}, bf16[4,64,256]{2,1,0:T(8,128)(2,1)S(1)}, u32[]{:S(2)}, u32[]{:S(2)}) collective-permute-start(bf16[4,64,256]{2,1,0:T(8,128)(2,1)S(1)} %bitcast.202), channel_id=1, source_target_pairs={{0,16},{8,24},{16,0},{24,8},{1,17},{9,25},{17,1},{25,9},{2,18},{10... | collective-permute-start | bytes 393224 | tf_op jit(solution)/shard_map/ppermute | solution.py:97
  57.1 9.1 %collective-permute-start.6 = (bf16[4,64,256]{2,1,0:T(8,128)(2,1)S(1)}, bf16[4,64,256]{2,1,0:T(8,128)(2,1)S(1)}, u32[]{:S(2)}, u32[]{:S(2)}) collective-permute-start(bf16[4,64,256]{2,1,0:T(8,128)(2,1)S(1)} %bitcast.203), channel_id=1, source_target_pairs={{0,24},{8,0},{16,8},{24,16},{1,25},{9,1},{17,9},{25,17},{2,26},{10... | collective-permute-start | bytes 393224 | tf_op jit(solution)/shard_map/ppermute | solution.py:97
  66.8 1.8 %copy-start.6 = (bf16[4,256,256]{2,1,0:T(8,128)(2,1)S(1)}, bf16[4,256,256]{2,1,0:T(8,128)(2,1)}, u32[]{:S(2)}) copy-start(bf16[4,256,256]{2,1,0:T(8,128)(2,1)} %copy-done.5) | copy-start | bytes 1572868
  69.1 1.0 copy-start.10
  69.3 2.0 %collective-permute-start.7 = (f32[131072]{0:T(1024)S(1)}, f32[131072]{0:T(1024)S(1)}, u32[]{:S(2)}, u32[]{:S(2)}) collective-permute-start(f32[131072]{0:T(1024)S(1)} %broadcast_select_fusion.3), channel_id=1, source_target_pairs={{0,1},{1,0},{2,3},{3,2},{4,5},{5,4},{6,7},{7,6},{8,9},{9,8},{10,11... | collective-permute-start | bytes 1572872 | tf_op jit(solution)/shard_map/ppermute | solution.py:33
  71.6 16.7 %copy-start.19 = (s32[4,128]{1,0:T(4,128)S(1)}, s32[4,128]{1,0:T(4,128)}, u32[]{:S(2)}) copy-start(s32[4,128]{1,0:T(4,128)} %param.15) | copy-start | bytes 6148
  71.6 16.7 %copy-start.22 = (pred[4,128]{1,0:T(4,128)(4,1)S(1)}, pred[4,128]{1,0:T(4,128)(4,1)}, u32[]{:S(2)}) copy-start(pred[4,128]{1,0:T(4,128)(4,1)} %copy-done.21) | copy-start | bytes 1540
  72.1 6.2 %collective-permute-start.10 = (f32[32768]{0:T(1024)S(1)}, f32[32768]{0:T(1024)S(1)}, u32[]{:S(2)}, u32[]{:S(2)}) collective-permute-start(f32[32768]{0:T(1024)S(1)} %bitcast.214), channel_id=1, source_target_pairs={{0,6},{1,7},{2,0},{3,1},{4,2},{5,3},{6,4},{7,5},{8,14},{9,15},{10,... | collective-permute-start | bytes 393224 | tf_op jit(solution)/shard_map/ppermute | solution.py:37
  74.2 7.3 %collective-permute-start.8 = (f32[32768]{0:T(1024)S(1)}, f32[32768]{0:T(1024)S(1)}, u32[]{:S(2)}, u32[]{:S(2)}) collective-permute-start(f32[32768]{0:T(1024)S(1)} %bitcast.213), channel_id=1, source_target_pairs={{0,2},{1,3},{2,4},{3,5},{4,6},{5,7},{6,0},{7,1},{8,10},{9,11},{10,... | collective-permute-start | bytes 393224 | tf_op jit(solution)/shard_map/ppermute | solution.py:37
  74.2 8.1 %collective-permute-start.9 = (f32[32768]{0:T(1024)S(1)}, f32[32768]{0:T(1024)S(1)}, u32[]{:S(2)}, u32[]{:S(2)}) collective-permute-start(f32[32768]{0:T(1024)S(1)} %bitcast.211), channel_id=1, source_target_pairs={{0,4},{1,5},{2,6},{3,7},{4,0},{5,1},{6,2},{7,3},{8,12},{9,13},{10,... | collective-permute-start | bytes 393224 | tf_op jit(solution)/shard_map/ppermute | solution.py:37
  76.2 12.0 %collective-permute-start.14 = (bf16[4,128,256]{2,1,0:T(8,128)(2,1)S(1)}, bf16[4,128,256]{2,1,0:T(8,128)(2,1)S(1)}, u32[]{:S(2)}, u32[]{:S(2)}) collective-permute-start(bf16[4,128,256]{2,1,0:T(8,128)(2,1)S(1)} %convolution_convert_fusion.6), channel_id=1, source_target_pairs={{0,7},{1,0},{2,1},{3,2},{4,3},{5,4},{6,5},{7,6},{8,15},{9,8},{10,9... | collective-permute-start | bytes 786440 | tf_op jit(solution)/shard_map/ppermute | solution.py:12
  82.3 16.9 %copy-start.20 = (pred[4]{0:T(512)(128)(4,1)S(1)}, pred[4]{0:T(512)(128)(4,1)}, u32[]{:S(2)}) copy-start(pred[4]{0:T(512)(128)(4,1)} %get-tuple-element.45) | copy-start | bytes 16
  82.5 7.0 %collective-permute-start.11 = (f32[8192]{0:T(1024)S(1)}, f32[8192]{0:T(1024)S(1)}, u32[]{:S(2)}, u32[]{:S(2)}) collective-permute-start(f32[8192]{0:T(1024)S(1)} %bitcast.220), channel_id=1, source_target_pairs={{0,8},{8,16},{16,24},{24,0},{1,9},{9,17},{17,25},{25,1},{2,10},{10... | collective-permute-start | bytes 98312 | tf_op jit(solution)/shard_map/ppermute | solution.py:37
  85.8 4.8 %collective-permute-start.12 = (f32[8192]{0:T(1024)S(1)}, f32[8192]{0:T(1024)S(1)}, u32[]{:S(2)}, u32[]{:S(2)}) collective-permute-start(f32[8192]{0:T(1024)S(1)} %bitcast.219), channel_id=1, source_target_pairs={{0,16},{8,24},{16,0},{24,8},{1,17},{9,25},{17,1},{25,9},{2,18},{10... | collective-permute-start | bytes 98312 | tf_op jit(solution)/shard_map/ppermute | solution.py:37
  87.3 3.9 %collective-permute-start.13 = (f32[8192]{0:T(1024)S(1)}, f32[8192]{0:T(1024)S(1)}, u32[]{:S(2)}, u32[]{:S(2)}) collective-permute-start(f32[8192]{0:T(1024)S(1)} %bitcast.218), channel_id=1, source_target_pairs={{0,24},{8,0},{16,8},{24,16},{1,25},{9,1},{17,9},{25,17},{2,26},{10... | collective-permute-start | bytes 98312 | tf_op jit(solution)/shard_map/ppermute | solution.py:37
  91.2 5.8 %collective-permute-start.15 = (f32[8192]{0:T(1024)S(1)}, f32[8192]{0:T(1024)S(1)}, u32[]{:S(2)}, u32[]{:S(2)}) collective-permute-start(f32[8192]{0:T(1024)S(1)} %add_add_fusion.1), channel_id=1, source_target_pairs={{0,8},{8,16},{16,24},{24,0},{1,9},{9,17},{17,25},{25,1},{2,10},{10... | collective-permute-start | bytes 98312 | tf_op jit(solution)/shard_map/ppermute | solution.py:49
  91.6 5.4 %collective-permute-start.16 = (f32[8192]{0:T(1024)S(1)}, f32[8192]{0:T(1024)S(1)}, u32[]{:S(2)}, u32[]{:S(2)}) collective-permute-start(f32[8192]{0:T(1024)S(1)} %add_add_fusion.1), channel_id=1, source_target_pairs={{0,16},{8,24},{16,0},{24,8},{1,17},{9,25},{17,1},{25,9},{2,18},{10... | collective-permute-start | bytes 98312 | tf_op jit(solution)/shard_map/ppermute | solution.py:49
  94.6 3.9 %collective-permute-start.17 = (f32[8192]{0:T(1024)S(1)}, f32[8192]{0:T(1024)S(1)}, u32[]{:S(2)}, u32[]{:S(2)}) collective-permute-start(f32[8192]{0:T(1024)S(1)} %add_add_fusion.1), channel_id=1, source_target_pairs={{0,24},{8,0},{16,8},{24,16},{1,25},{9,1},{17,9},{25,17},{2,26},{10... | collective-permute-start | bytes 98312 | tf_op jit(solution)/shard_map/ppermute | solution.py:49
  99.4 6.0 %collective-permute-start.18 = (f32[32768]{0:T(1024)S(1)}, f32[32768]{0:T(1024)S(1)}, u32[]{:S(2)}, u32[]{:S(2)}) collective-permute-start(f32[32768]{0:T(1024)S(1)} %bitcast.204), channel_id=1, source_target_pairs={{0,2},{1,3},{2,4},{3,5},{4,6},{5,7},{6,0},{7,1},{8,10},{9,11},{10,... | collective-permute-start | bytes 393224 | tf_op jit(solution)/shard_map/ppermute | solution.py:49
  100.0 6.4 %collective-permute-start.19 = (f32[32768]{0:T(1024)S(1)}, f32[32768]{0:T(1024)S(1)}, u32[]{:S(2)}, u32[]{:S(2)}) collective-permute-start(f32[32768]{0:T(1024)S(1)} %bitcast.205), channel_id=1, source_target_pairs={{0,4},{1,5},{2,6},{3,7},{4,0},{5,1},{6,2},{7,3},{8,12},{9,13},{10,... | collective-permute-start | bytes 393224 | tf_op jit(solution)/shard_map/ppermute | solution.py:49
  101.2 5.4 %collective-permute-start.20 = (f32[32768]{0:T(1024)S(1)}, f32[32768]{0:T(1024)S(1)}, u32[]{:S(2)}, u32[]{:S(2)}) collective-permute-start(f32[32768]{0:T(1024)S(1)} %bitcast.206), channel_id=1, source_target_pairs={{0,6},{1,7},{2,0},{3,1},{4,2},{5,3},{6,4},{7,5},{8,14},{9,15},{10,... | collective-permute-start | bytes 393224 | tf_op jit(solution)/shard_map/ppermute | solution.py:49
  108.1 2.0 %collective-permute-start.21 = (f32[131072]{0:T(1024)S(1)}, f32[131072]{0:T(1024)S(1)}, u32[]{:S(2)}, u32[]{:S(2)}) collective-permute-start(f32[131072]{0:T(1024)S(1)} %bitcast.197), channel_id=1, source_target_pairs={{0,1},{1,0},{2,3},{3,2},{4,5},{5,4},{6,7},{7,6},{8,9},{9,8},{10,11... | collective-permute-start | bytes 1572872 | tf_op jit(solution)/shard_map/ppermute | solution.py:44
  (1 other events, 0.5 us)

commit v13 on v12

--- a/solution.py
+++ b/solution.py
@@ -216,62 +216,53 @@
         per_group = 1
     groups = nodes_here // per_group
     block = per_group * steps_all
-    flat = jnp.swapaxes(states, 0, 1).reshape(nodes_here * steps_all, width)
-    up_flat = jnp.swapaxes(upstream, 0, 1).reshape(nodes_here * steps_all, width)
-
-    def project(weight):
-        return jnp.dot(flat, weight, preferred_element_type=jnp.float32).astype(jnp.bfloat16)
-
-    def blocks(matrix):
-        return matrix.reshape(groups, block, HEADS, head_dim)
-
-    queries = blocks(project(w_query))
-    key_rows = blocks(project(w_key))
-    value_rows = blocks(project(w_value))
-    up_heads = blocks(up_flat)
+    flat = jnp.swapaxes(states, 0, 1).reshape(groups, block, width)
+    up_flat = jnp.swapaxes(upstream, 0, 1).reshape(groups, block, width)
+    heads_of = {
+        name: weight.reshape(width, HEADS, head_dim)
+        for name, weight in (("q", w_query), ("k", w_key), ("v", w_value))
+    }
+
+    def contract(spec, left, right):
+        return jnp.einsum(spec, left, right, preferred_element_type=jnp.float32)
+
+    queries = contract("gic,chd->ghid", flat, heads_of["q"]).astype(jnp.bfloat16)
+    key_rows = contract("gic,chd->ghid", flat, heads_of["k"]).astype(jnp.bfloat16)
+    value_rows = contract("gic,chd->ghid", flat, heads_of["v"]).astype(jnp.bfloat16)
+    up_heads = up_flat.reshape(groups, block, HEADS, head_dim)
     position = jnp.arange(block)
     same = (position[:, None] // steps_all) == (position[None, :] // steps_all)
     causal = jnp.logical_and(same, (position[:, None] % steps_all) >= (position[None, :] % steps_all))
 
-    def contract(spec, left, right):
-        return jnp.einsum(spec, left, right, preferred_element_type=jnp.float32)
-
-    scores = contract("gihd,gjhd->ghij", queries, key_rows) * scale_factor
+    scores = contract("ghid,ghjd->ghij", queries, key_rows) * scale_factor
     scores = jnp.where(causal, scores, -jnp.inf)
     highest = jnp.max(scores, axis=-1, keepdims=True)
     exponent = jnp.exp(scores - highest)
     probs = exponent / jnp.sum(exponent, axis=-1, keepdims=True)
     probs_low = probs.astype(jnp.bfloat16)
-    value_grad = contract("ghij,gihd->gjhd", probs_low, up_heads).astype(jnp.bfloat16)
-    prob_grad = contract("gihd,gjhd->ghij", up_heads, value_rows)
+    value_grad = contract("ghij,gihd->ghjd", probs_low, up_heads).astype(jnp.bfloat16)
+    prob_grad = contract("gihd,ghjd->ghij", up_heads, value_rows)
     score_grad = (
         probs * (prob_grad - jnp.sum(prob_grad * probs, axis=-1, keepdims=True)) * scale_factor
     ).astype(jnp.bfloat16)
     score_grad = lax.optimization_barrier(score_grad)
-    query_grad = contract("ghij,gjhd->gihd", score_grad, key_rows).astype(jnp.bfloat16)
-    key_grad = contract("ghij,gihd->gjhd", score_grad, queries).astype(jnp.bfloat16)
-    query_flat = query_grad.reshape(-1, width)
-    key_flat = key_grad.reshape(-1, width)
-    value_flat = value_grad.reshape(-1, width)
+    query_grad = contract("ghij,ghjd->ghid", score_grad, key_rows).astype(jnp.bfloat16)
+    key_grad = contract("ghij,ghid->ghjd", score_grad, queries).astype(jnp.bfloat16)
 
     def weight_grad(grad_rows):
-        return lax.dot_general(
-            flat, grad_rows, (((0,), (0,)), ((), ())), preferred_element_type=jnp.float32
-        )
-
-    def input_grad(grad_rows, weight):
-        return lax.dot_general(
-            grad_rows, weight, (((1,), (1,)), ((), ())), preferred_element_type=jnp.float32
-        )
+        return contract("gic,ghid->chd", flat, grad_rows).reshape(width, width)
+
+    def input_grad(grad_rows, name):
+        return contract("ghid,chd->gic", grad_rows, heads_of[name])
 
     back = (
         up_flat.astype(jnp.float32)
-        + input_grad(query_flat, w_query)
-        + input_grad(key_flat, w_key)
-        + input_grad(value_flat, w_value)
+        + input_grad(query_grad, "q")
+        + input_grad(key_grad, "k")
+        + input_grad(value_grad, "v")
     )
     back = jnp.swapaxes(back.astype(jnp.bfloat16).reshape(nodes_here, steps_all, width), 0, 1)
-    return ((weight_grad(query_flat), weight_grad(key_flat), weight_grad(value_flat)), back)
+    return ((weight_grad(query_grad), weight_grad(key_grad), weight_grad(value_grad)), back)
 
 
 def local(

time: 112 us -> 108 us (0.964)
  matrix products: 23 us -> 25.9 us
  local copies, waits for them, and re-layouts: 17.6 us -> 14.9 us
  other arithmetic: 11.3 us -> 8.82 us
  waiting for transfers between devices: 25.7 us -> 24 us
    dot_general x4 -> x12, matrix products: 3.8 us -> 10.3 us  [contract(): return jnp.einsum(spec, left, right, preferred_element_type=jnp.float32)]
    reshape x5 -> x0, local copies, waits for them, and re-layouts: 3.61 us -> none  [blocks(): return matrix.reshape(groups, block, HEADS, head_dim)]
    dot_general x9 -> x0, matrix products: 2.93 us -> none  [the longest x3 1.04 us: input_grad(): lax.dot_general(grad_rows, weight, (((1,), (1,)), ((), ())), preferred_el...]
    sub x1, other arithmetic: 2.94 us -> 0.61 us  [attend_blocked(): prob_grad - jnp.sum(prob_grad * probs, axis=-1, keepdims=True)]
    convert_element_type x4 -> x1, local copies, waits for them, and re-layouts: 2.64 us -> 0.61 us  [attend_blocked(): up_flat.astype(jnp.float32) + input_grad(query_grad, 'q')]
    ppermute x6, waiting for transfers between devices: 12.1 us -> 10.4 us  [exchange(): lax.ppermute(send, axis, [(i, (i + shift) % count) for i in range(count)])]
    unnamed x67, local copies, waits for them, and re-layouts: 3.64 us -> 5.08 us
    convert_element_type x1, other arithmetic: 1.63 us -> 0.43 us  [local(): pre_grad = (back_days.astype(jnp.float32) * sigmoid_val * (1.0 + preact *...]
  transfers between devices with their start and end apart: 22 -> 22, of which waited for: 16 -> 16; matrix products, arithmetic and copies ran while one was open for 13% -> 16% of each run, Pallas kernels for 0% -> 0%
where the time goes in v13:
time: 108 us; the launch traced here: 107 us
  starting transfers between devices  32.2 us (30%)
  matrix products  25.9 us (24%)
  waiting for transfers between devices  24 us (22%)
  local copies, waits for them, and re-layouts  14.9 us (14%)
  other arithmetic  8.82 us (8%)
  between operations  1.54 us (1%)
    ppermute x6, starting transfers between devices, exchange(): lax.ppermute(send, axis, [(i, (i + shift) % count) for i in range(count)])  12.4 us
    ppermute x6, waiting for transfers between devices, exchange(): lax.ppermute(send, axis, [(i, (i + shift) % count) for i in range(count)])  10.4 us
    dot_general x12, matrix products, contract(): return jnp.einsum(spec, left, right, preferred_element_type=jnp.float32)  10.3 us
    ppermute x6, starting transfers between devices, _scatter_step(): lax.ppermute(send, axis, _group_pairs(axis, stride, group, shift))  9.36 us
    ppermute x6, starting transfers between devices, _gather_step(): lax.ppermute(flat, axis, _group_pairs(axis, stride, group, shift))  8.64 us
    ppermute x6, waiting for transfers between devices, _scatter_step(): lax.ppermute(send, axis, _group_pairs(axis, stride, group, shift))  6.45 us
    ppermute x6, waiting for transfers between devices, _gather_step(): lax.ppermute(flat, axis, _group_pairs(axis, stride, group, shift))  5.63 us
    unnamed x67, local copies, waits for them, and re-layouts  5.08 us
  transfers between devices with their start and end apart: 22, of which 16 were waited for; matrix products, arithmetic and copies ran while one was open for 16% of the time, Pallas kernels for 0%

profile of v13, /device:TPU:0, one launch (start us, length us, event | category | flops | bytes accessed | tf_op | source)
XLA Modules:
  0.0 107.4 jit_solution(8485745825143821206)
XLA Ops:
  0.6 0.8 iota_compare_fusion.12
  2.0 2.1 %convolution_convert_fusion.7 = bf16[4,128,256]{2,1,0:T(8,128)(2,1)} fusion(bf16[4,256,256]{2,1,0:T(8,128)(2,1)} %param.12, s32[4,128]{1,0:T(4,128)} %param.15, pred[4,128]{1,0:T(4,128)(4,1)S(1)} %iota_compare_fusion.12), kind=kOutput, calls=%fused_computation.54 | convolution fusion | flops 67502080 | bytes 788992 | tf_op jit(solution)/shard_map/dsn,dnh->dsh/dot_general | solution.py:287
  5.1 1.2 %convert_reduce_fusion = f32[4,256]{1,0:T(4,128)S(1)} fusion(s32[4,1024]{1,0:T(4,128)} %param.14), kind=kLoop, calls=%fused_computation.6 | loop fusion | flops 4193280 | bytes 20480 | tf_op jit(solution)/shard_map/reduce_sum | solution.py:302
  6.3 2.4 %fusion.20 = bf16[4,256,256]{2,1,0:T(8,128)(2,1)S(1)} fusion(s32[4,1024]{1,0:T(4,128)} %param.13, s32[4,1024]{1,0:T(4,128)} %param.14), kind=kOutput, calls=%fused_computation.47 | convolution fusion | flops 539230208 | bytes 557056 | tf_op jit(solution)/shard_map/der,des->drs/dot_general | solution.py:296
  9.6 1.3 %fusion.25 = bf16[4,256,128]{2,1,0:T(8,128)(2,1)S(1)} fusion(s32[4,1024]{1,0:T(4,128)S(1)} %copy-done.18, s32[128]{0:T(128)S(1)} %iota_add_fusion, s32[4,1024]{1,0:T(4,128)S(1)} %copy-done.24), kind=kOutput, calls=%fused_computation.52 | convolution fusion | flops 270139392 | bytes 295424 | tf_op jit(solution)/shard_map/der,des->drs/dot_general | solution.py:299
  11.8 1.3 %fusion.18 = bf16[4,256,256]{2,1,0:T(8,128)(2,1)S(1)} fusion(f32[4,256,256]{2,1,0:T(8,128)S(1)} %fusion.61, bf16[4,256,128]{2,1,0:T(8,128)(2,1)S(1)} %fusion.25, bf16[4,128,256]{2,1,0:T(8,128)(2,1)} %collective-permute-done, bf16[4,256,256]{2,1,0:T(8,128)(2,1)S(1)} %copy-done.1, f32[4,256]{1,0:T(4,128)S(1)} %add_divide_fusion.1), kind=kOutput, calls=%fused_computation.39 | convolution fusion | flops 68419584 | bytes 2625536 | tf_op jit(solution)/shard_map/drs,dsh->drh/dot_general | solution.py:308
  13.2 1.3 %fusion.28 = (bf16[4,256,256]{2,1,0:T(8,128)(2,1)S(1)}, f32[4,256,256]{2,1,0:T(8,128)}) fusion(bf16[4,256,256]{2,1,0:T(8,128)(2,1)S(1)} %copy-done.1, bf16[4,256,256]{2,1,0:T(8,128)(2,1)S(1)} %fusion.18, bf16[256,256]{1,0:T(8,128)(2,1)S(1)} %copy-done), kind=kOutput, calls=%fused_computation.59 | convolution fusion | flops 136052736 | bytes 2752512 | tf_op jit(solution)/shard_map/drh,hk->drk/dot_general | solution.py:310
  14.5 0.8 dynamic-slice_bitcast_fusion
  15.3 2.6 %collective-permute-start.1 = (bf16[4,64,256]{2,1,0:T(8,128)(2,1)}, bf16[4,64,256]{2,1,0:T(8,128)(2,1)}, u32[]{:S(2)}, u32[]{:S(2)}) collective-permute-start(bf16[4,64,256]{2,1,0:T(8,128)(2,1)} %get-tuple-element.33), channel_id=1, source_target_pairs={{0,8},{8,16},{16,24},{24,0},{1,9},{9,17},{17,25},{25,1},{2,10},{10... | collective-permute-start | bytes 393224 | tf_op jit(solution)/shard_map/ppermute | solution.py:97
  17.9 2.6 %collective-permute-start.2 = (bf16[4,64,256]{2,1,0:T(8,128)(2,1)}, bf16[4,64,256]{2,1,0:T(8,128)(2,1)}, u32[]{:S(2)}, u32[]{:S(2)}) collective-permute-start(bf16[4,64,256]{2,1,0:T(8,128)(2,1)} %get-tuple-element.32), channel_id=1, source_target_pairs={{0,16},{8,24},{16,0},{24,8},{1,17},{9,25},{17,1},{25,9},{2,18},{10... | collective-permute-start | bytes 393224 | tf_op jit(solution)/shard_map/ppermute | solution.py:97
  20.5 1.4 %collective-permute-start.3 = (bf16[4,64,256]{2,1,0:T(8,128)(2,1)}, bf16[4,64,256]{2,1,0:T(8,128)(2,1)}, u32[]{:S(2)}, u32[]{:S(2)}) collective-permute-start(bf16[4,64,256]{2,1,0:T(8,128)(2,1)} %get-tuple-element.31), channel_id=1, source_target_pairs={{0,24},{8,0},{16,8},{24,16},{1,25},{9,1},{17,9},{25,17},{2,26},{10... | collective-permute-start | bytes 393224 | tf_op jit(solution)/shard_map/ppermute | solution.py:97
  23.9 1.7 %copy.33 = bf16[256,256]{0,1:T(8,128)(2,1)} copy(bf16[256,256]{1,0:T(8,128)(2,1)} %param.20) | data formatting | bytes 262144 | tf_op args[8]
  26.3 4.0 %collective-permute-done.2 = bf16[4,64,256]{2,1,0:T(8,128)(2,1)} collective-permute-done((bf16[4,64,256]{2,1,0:T(8,128)(2,1)}, bf16[4,64,256]{2,1,0:T(8,128)(2,1)}, u32[]{:S(2)}, u32[]{:S(2)}) %collective-permute-start.2) | collective-permute-done | bytes 131104 | tf_op jit(solution)/shard_map/ppermute | solution.py:97
  30.4 1.1 %pad_maximum_fusion = bf16[4,4,64,256]{3,2,1,0:T(8,128)(2,1)S(1)} fusion(bf16[1,4,64,256]{3,2,1,0:T(8,128)(2,1)} %bitcast.5, bf16[1,4,64,256]{3,2,1,0:T(8,128)(2,1)} %bitcast.4, bf16[1,4,64,256]{3,2,1,0:T(8,128)(2,1)} %bitcast.3, bf16[1,4,64,256]{3,2,1,0:T(8,128)(2,1)S(1)} %copy-done.14), kind=kLoop, calls=%fused_computation.72 | loop fusion | flops 786432 | bytes 1048576 | tf_op jit(solution)/shard_map/stack | solution.py:99
  33.4 3.1 %fusion.24 = f32[8,4,128,128]{3,2,1,0:T(8,128)} fusion(bf16[8,128,4,64]{1,3,2,0:T(8,128)(2,1)S(1)} %copy.35, bf16[8,128,256,1]{2,1,3,0:T(8,128)(2,1)S(1)} %bitcast.204, bf16[256,4,64,1]{0,2,1,3:T(8,128)(2,1)} %bitcast.215), kind=kOutput, calls=%fused_computation.51 | convolution fusion | flops 201588736 | bytes 3276800 | tf_op jit(solution)/shard_map/gihd,ghjd->ghij/dot_general | solution.py:227
  36.5 3.5 %fusion.60 = (f32[8,4,128]{2,1,0:T(4,128)}, f32[8,4,128,128]{2,3,1,0:T(8,128)}) fusion(pred[128,128]{0,1:T(8,128)(4,1)} %compare_and_fusion, bf16[8,4,128,64]{2,3,1,0:T(8,128)(2,1)S(1)} %fusion.21, bf16[8,4,128,64]{2,3,1,0:T(8,128)(2,1)S(1)} %fusion.22), kind=kOutput, calls=%fused_computation.177 | convolution fusion | flops 69206144 | bytes 3178496 | tf_op jit(solution)/shard_map/sub | solution.py:240
  40.0 2.6 %convolution_convert_fusion.4 = bf16[8,4,128,64]{2,3,1,0:T(8,128)(2,1)S(1)} fusion(bf16[8,128,4,64]{1,3,2,0:T(8,128)(2,1)S(1)} %copy.35, f32[8,4,128,128]{2,3,1,0:T(8,128)} %get-tuple-element.43, f32[8,4,128]{2,1,0:T(4,128)} %get-tuple-element.42), kind=kOutput, calls=%fused_computation.44 | convolution fusion | flops 68419584 | bytes 3162112 | tf_op jit(solution)/shard_map/ghij,gihd->ghjd/dot_general | solution.py:227
  44.3 0.8 convolution_convert_fusion.5
  46.1 1.0 convolution_bitcast_fusion.4
  47.9 3.4 %collective-permute-start.4 = (bf16[4,64,256]{2,1,0:T(8,128)(2,1)S(1)}, bf16[4,64,256]{2,1,0:T(8,128)(2,1)S(1)}, u32[]{:S(2)}, u32[]{:S(2)}) collective-permute-start(bf16[4,64,256]{2,1,0:T(8,128)(2,1)S(1)} %bitcast.222), channel_id=1, source_target_pairs={{0,8},{8,16},{16,24},{24,0},{1,9},{9,17},{17,25},{25,1},{2,10},{10... | collective-permute-start | bytes 393224 | tf_op jit(solution)/shard_map/ppermute | solution.py:97
  51.3 1.4 %collective-permute-start.5 = (bf16[4,64,256]{2,1,0:T(8,128)(2,1)S(1)}, bf16[4,64,256]{2,1,0:T(8,128)(2,1)}, u32[]{:S(2)}, u32[]{:S(2)}) collective-permute-start(bf16[4,64,256]{2,1,0:T(8,128)(2,1)S(1)} %bitcast.223), channel_id=1, source_target_pairs={{0,16},{8,24},{16,0},{24,8},{1,17},{9,25},{17,1},{25,9},{2,18},{10... | collective-permute-start | bytes 393224 | tf_op jit(solution)/shard_map/ppermute | solution.py:97
  52.7 1.1 %collective-permute-start.6 = (bf16[4,64,256]{2,1,0:T(8,128)(2,1)S(1)}, bf16[4,64,256]{2,1,0:T(8,128)(2,1)}, u32[]{:S(2)}, u32[]{:S(2)}) collective-permute-start(bf16[4,64,256]{2,1,0:T(8,128)(2,1)S(1)} %bitcast.224), channel_id=1, source_target_pairs={{0,24},{8,0},{16,8},{24,16},{1,25},{9,1},{17,9},{25,17},{2,26},{10... | collective-permute-start | bytes 393224 | tf_op jit(solution)/shard_map/ppermute | solution.py:97
  55.7 0.8 collective-permute-done.4
  56.5 5.4 %collective-permute-done.5 = bf16[4,64,256]{2,1,0:T(8,128)(2,1)} collective-permute-done((bf16[4,64,256]{2,1,0:T(8,128)(2,1)S(1)}, bf16[4,64,256]{2,1,0:T(8,128)(2,1)}, u32[]{:S(2)}, u32[]{:S(2)}) %collective-permute-start.5) | collective-permute-done | bytes 131104 | tf_op jit(solution)/shard_map/ppermute | solution.py:97
  61.9 1.1 %pad_maximum_fusion.1 = bf16[4,4,64,256]{3,2,1,0:T(8,128)(2,1)S(1)} fusion(bf16[1,4,64,256]{3,2,1,0:T(8,128)(2,1)} %bitcast.50, bf16[1,4,64,256]{3,2,1,0:T(8,128)(2,1)} %bitcast.48, bf16[1,4,64,256]{3,2,1,0:T(8,128)(2,1)S(1)} %bitcast.230, bf16[1,4,64,256]{3,2,1,0:T(8,128)(2,1)S(1)} %bitcast.220), kind=kLoop, calls=%fused_computation.74 | loop fusion | flops 786432 | bytes 1048576 | tf_op jit(solution)/shard_map/stack | solution.py:99
  66.2 0.9 convolution_add_fusion
  68.1 2.1 %collective-permute-start.10 = (f32[32768]{0:T(1024)S(1)}, f32[32768]{0:T(1024)S(1)}, u32[]{:S(2)}, u32[]{:S(2)}) collective-permute-start(f32[32768]{0:T(1024)S(1)} %bitcast.233), channel_id=1, source_target_pairs={{0,6},{1,7},{2,0},{3,1},{4,2},{5,3},{6,4},{7,5},{8,14},{9,15},{10,... | collective-permute-start | bytes 393224 | tf_op jit(solution)/shard_map/ppermute | solution.py:37
  70.2 1.5 %collective-permute-start.9 = (f32[32768]{0:T(1024)S(1)}, f32[32768]{0:T(1024)S(1)}, u32[]{:S(2)}, u32[]{:S(2)}) collective-permute-start(f32[32768]{0:T(1024)S(1)} %bitcast.231), channel_id=1, source_target_pairs={{0,4},{1,5},{2,6},{3,7},{4,0},{5,1},{6,2},{7,3},{8,12},{9,13},{10,... | collective-permute-start | bytes 393224 | tf_op jit(solution)/shard_map/ppermute | solution.py:37
  72.3 1.3 %collective-permute-start.14 = (bf16[4,128,256]{2,1,0:T(8,128)(2,1)S(1)}, bf16[4,128,256]{2,1,0:T(8,128)(2,1)S(1)}, u32[]{:S(2)}, u32[]{:S(2)}) collective-permute-start(bf16[4,128,256]{2,1,0:T(8,128)(2,1)S(1)} %convolution_convert_fusion.6), channel_id=1, source_target_pairs={{0,7},{1,0},{2,1},{3,2},{4,3},{5,4},{6,5},{7,6},{8,15},{9,8},{10,9... | collective-permute-start | bytes 786440 | tf_op jit(solution)/shard_map/ppermute | solution.py:12
  73.6 0.8 collective-permute-done.10
  74.4 3.2 %collective-permute-done.8 = f32[32768]{0:T(1024)S(1)} collective-permute-done((f32[32768]{0:T(1024)S(1)}, f32[32768]{0:T(1024)S(1)}, u32[]{:S(2)}, u32[]{:S(2)}) %collective-permute-start.8) | collective-permute-done | bytes 131104 | tf_op jit(solution)/shard_map/ppermute | solution.py:37
  77.6 0.7 collective-permute-done.9
  78.5 3.3 %collective-permute-start.11 = (f32[8192]{0:T(1024)S(1)}, f32[8192]{0:T(1024)S(1)}, u32[]{:S(2)}, u32[]{:S(2)}) collective-permute-start(f32[8192]{0:T(1024)S(1)} %bitcast.239), channel_id=1, source_target_pairs={{0,8},{8,16},{16,24},{24,0},{1,9},{9,17},{17,25},{25,1},{2,10},{10... | collective-permute-start | bytes 98312 | tf_op jit(solution)/shard_map/ppermute | solution.py:37
  81.8 1.5 %collective-permute-start.12 = (f32[8192]{0:T(1024)S(1)}, f32[8192]{0:T(1024)S(1)}, u32[]{:S(2)}, u32[]{:S(2)}) collective-permute-start(f32[8192]{0:T(1024)S(1)} %bitcast.238), channel_id=1, source_target_pairs={{0,16},{8,24},{16,0},{24,8},{1,17},{9,25},{17,1},{25,9},{2,18},{10... | collective-permute-start | bytes 98312 | tf_op jit(solution)/shard_map/ppermute | solution.py:37
  83.4 0.9 collective-permute-start.13
  84.3 1.3 %convolution_add_fusion.1 = f32[4,256,256]{2,1,0:T(8,128)} fusion(f32[4,256,256]{2,1,0:T(8,128)S(1)} %convolution_add_fusion, bf16[4,128,256]{2,1,0:T(8,128)(2,1)S(1)} %collective-permute-done.14, s32[4,128]{1,0:T(4,128)S(1)} %copy-done.19, pred[4,128]{1,0:T(4,128)(4,1)S(1)} %copy-done.22), kind=kOutput, calls=%fused_computation.29 | convolution fusion | flops 67633152 | bytes 2361856 | tf_op jit(solution)/shard_map/dsn,dsh->dnh/dot_general | solution.py:345
  85.6 1.1 %collective-permute-done.12 = f32[8192]{0:T(1024)S(1)} collective-permute-done((f32[8192]{0:T(1024)S(1)}, f32[8192]{0:T(1024)S(1)}, u32[]{:S(2)}, u32[]{:S(2)}) %collective-permute-start.12) | collective-permute-done | bytes 32800 | tf_op jit(solution)/shard_map/ppermute | solution.py:37
  87.6 3.0 %collective-permute-start.16 = (f32[8192]{0:T(1024)S(1)}, f32[8192]{0:T(1024)S(1)}, u32[]{:S(2)}, u32[]{:S(2)}) collective-permute-start(f32[8192]{0:T(1024)S(1)} %add_add_fusion.1), channel_id=1, source_target_pairs={{0,16},{8,24},{16,0},{24,8},{1,17},{9,25},{17,1},{25,9},{2,18},{10... | collective-permute-start | bytes 98312 | tf_op jit(solution)/shard_map/ppermute | solution.py:49
  90.6 1.0 collective-permute-start.17
  91.7 1.4 %collective-permute-done.15 = f32[8192]{0:T(1024)S(1)} collective-permute-done((f32[8192]{0:T(1024)S(1)}, f32[8192]{0:T(1024)S(1)}, u32[]{:S(2)}, u32[]{:S(2)}) %collective-permute-start.15) | collective-permute-done | bytes 32800 | tf_op jit(solution)/shard_map/ppermute | solution.py:49
  93.1 1.5 %collective-permute-done.17 = f32[8192]{0:T(1024)S(1)} collective-permute-done((f32[8192]{0:T(1024)S(1)}, f32[8192]{0:T(1024)S(1)}, u32[]{:S(2)}, u32[]{:S(2)}) %collective-permute-start.17) | collective-permute-done | bytes 32800 | tf_op jit(solution)/shard_map/ppermute | solution.py:49
  96.1 1.1 %collective-permute-start.19 = (f32[32768]{0:T(1024)S(1)}, f32[32768]{0:T(1024)S(1)}, u32[]{:S(2)}, u32[]{:S(2)}) collective-permute-start(f32[32768]{0:T(1024)S(1)} %bitcast.226), channel_id=1, source_target_pairs={{0,4},{1,5},{2,6},{3,7},{4,0},{5,1},{6,2},{7,3},{8,12},{9,13},{10,... | collective-permute-start | bytes 393224 | tf_op jit(solution)/shard_map/ppermute | solution.py:49
  97.2 2.5 %collective-permute-start.20 = (f32[32768]{0:T(1024)S(1)}, f32[32768]{0:T(1024)S(1)}, u32[]{:S(2)}, u32[]{:S(2)}) collective-permute-start(f32[32768]{0:T(1024)S(1)} %bitcast.227), channel_id=1, source_target_pairs={{0,6},{1,7},{2,0},{3,1},{4,2},{5,3},{6,4},{7,5},{8,14},{9,15},{10,... | collective-permute-start | bytes 393224 | tf_op jit(solution)/shard_map/ppermute | solution.py:49
  99.9 1.6 %collective-permute-done.18 = f32[32768]{0:T(1024)S(1)} collective-permute-done((f32[32768]{0:T(1024)S(1)}, f32[32768]{0:T(1024)S(1)}, u32[]{:S(2)}, u32[]{:S(2)}) %collective-permute-start.18) | collective-permute-done | bytes 131104 | tf_op jit(solution)/shard_map/ppermute | solution.py:49
  101.5 1.0 collective-permute-done.19
  103.1 0.8 gather_fusion.1
  104.8 1.3 %collective-permute-done.21 = f32[131072]{0:T(1024)S(1)} collective-permute-done((f32[131072]{0:T(1024)S(1)}, f32[131072]{0:T(1024)S(1)}, u32[]{:S(2)}, u32[]{:S(2)}) %collective-permute-start.21) | collective-permute-done | bytes 524320 | tf_op jit(solution)/shard_map/ppermute | solution.py:44
  106.4 1.0 fusion.59
  (148 shorter events, 22.4 us)
Async XLA Ops:
  0.6 12.5 %copy-start = (bf16[256,256]{1,0:T(8,128)(2,1)S(1)}, bf16[256,256]{1,0:T(8,128)(2,1)}, u32[]{:S(2)}) copy-start(bf16[256,256]{1,0:T(8,128)(2,1)} %param.17) | copy-start | bytes 393220
  4.1 7.7 %collective-permute-start = (bf16[4,128,256]{2,1,0:T(8,128)(2,1)}, bf16[4,128,256]{2,1,0:T(8,128)(2,1)}, u32[]{:S(2)}, u32[]{:S(2)}) collective-permute-start(bf16[4,128,256]{2,1,0:T(8,128)(2,1)} %convolution_convert_fusion.7), channel_id=1, source_target_pairs={{0,1},{1,2},{2,3},{3,4},{4,5},{5,6},{6,7},{7,0},{8,9},{9,10},{10,1... | collective-permute-start | bytes 786440 | tf_op jit(solution)/shard_map/ppermute | solution.py:12
  6.3 2.4 %copy-start.1 = (bf16[4,256,256]{2,1,0:T(8,128)(2,1)S(1)}, bf16[4,256,256]{2,1,0:T(8,128)(2,1)}, u32[]{:S(2)}) copy-start(bf16[4,256,256]{2,1,0:T(8,128)(2,1)} %param.12) | copy-start | bytes 1572868
  8.8 2.2 %copy-start.8 = (bf16[4,256,256]{2,1,0:T(8,128)(2,1)}, bf16[4,256,256]{2,1,0:T(8,128)(2,1)S(1)}, u32[]{:S(2)}) copy-start(bf16[4,256,256]{2,1,0:T(8,128)(2,1)S(1)} %fusion.20) | copy-start | bytes 1572868
  8.8 0.7 copy-start.18
  8.8 0.8 copy-start.24
  9.6 2.1 %copy-start.2 = (bf16[16,1,1,64,256]{4,3,2,1,0:T(8,128)(2,1)S(1)}, bf16[16,1,1,64,256]{4,3,2,1,0:T(8,128)(2,1)}, u32[]{:S(2)}) copy-start(bf16[16,1,1,64,256]{4,3,2,1,0:T(8,128)(2,1)} %param.21) | copy-start | bytes 1572868
  10.9 2.2 %copy-start.12 = (bf16[4,256,128]{2,1,0:T(8,128)(2,1)}, bf16[4,256,128]{2,1,0:T(8,128)(2,1)S(1)}, u32[]{:S(2)}) copy-start(bf16[4,256,128]{2,1,0:T(8,128)(2,1)S(1)} %fusion.25) | copy-start | bytes 786436
  13.1 1.4 %copy-start.3 = (bf16[4,256,256]{2,1,0:T(8,128)(2,1)}, bf16[4,256,256]{2,1,0:T(8,128)(2,1)S(1)}, u32[]{:S(2)}) copy-start(bf16[4,256,256]{2,1,0:T(8,128)(2,1)S(1)} %fusion.18) | copy-start | bytes 1572868
  13.1 9.2 %copy-start.16 = (bf16[256,256]{1,0:T(8,128)(2,1)S(1)}, bf16[256,256]{1,0:T(8,128)(2,1)}, u32[]{:S(2)}) copy-start(bf16[256,256]{1,0:T(8,128)(2,1)} %param.18) | copy-start | bytes 393220
  13.1 9.3 %copy-start.17 = (bf16[256,256]{1,0:T(8,128)(2,1)S(1)}, bf16[256,256]{1,0:T(8,128)(2,1)}, u32[]{:S(2)}) copy-start(bf16[256,256]{1,0:T(8,128)(2,1)} %param.19) | copy-start | bytes 393220
  15.3 11.0 %collective-permute-start.1 = (bf16[4,64,256]{2,1,0:T(8,128)(2,1)}, bf16[4,64,256]{2,1,0:T(8,128)(2,1)}, u32[]{:S(2)}, u32[]{:S(2)}) collective-permute-start(bf16[4,64,256]{2,1,0:T(8,128)(2,1)} %get-tuple-element.33), channel_id=1, source_target_pairs={{0,8},{8,16},{16,24},{24,0},{1,9},{9,17},{17,25},{25,1},{2,10},{10... | collective-permute-start | bytes 393224 | tf_op jit(solution)/shard_map/ppermute | solution.py:97
  17.9 12.4 %collective-permute-start.2 = (bf16[4,64,256]{2,1,0:T(8,128)(2,1)}, bf16[4,64,256]{2,1,0:T(8,128)(2,1)}, u32[]{:S(2)}, u32[]{:S(2)}) collective-permute-start(bf16[4,64,256]{2,1,0:T(8,128)(2,1)} %get-tuple-element.32), channel_id=1, source_target_pairs={{0,16},{8,24},{16,0},{24,8},{1,17},{9,25},{17,1},{25,9},{2,18},{10... | collective-permute-start | bytes 393224 | tf_op jit(solution)/shard_map/ppermute | solution.py:97
  20.5 10.0 %collective-permute-start.3 = (bf16[4,64,256]{2,1,0:T(8,128)(2,1)}, bf16[4,64,256]{2,1,0:T(8,128)(2,1)}, u32[]{:S(2)}, u32[]{:S(2)}) collective-permute-start(bf16[4,64,256]{2,1,0:T(8,128)(2,1)} %get-tuple-element.31), channel_id=1, source_target_pairs={{0,24},{8,0},{16,8},{24,16},{1,25},{9,1},{17,9},{25,17},{2,26},{10... | collective-permute-start | bytes 393224 | tf_op jit(solution)/shard_map/ppermute | solution.py:97
  23.3 2.9 %copy-start.23 = (s32[4]{0:T(128)S(1)}, s32[4]{0:T(128)}, u32[]{:S(2)}) copy-start(s32[4]{0:T(128)} %fusion.55) | copy-start | bytes 52
  23.3 7.1 %copy-start.14 = (bf16[1,4,64,256]{3,2,1,0:T(8,128)(2,1)S(1)}, bf16[1,4,64,256]{3,2,1,0:T(8,128)(2,1)}, u32[]{:S(2)}) copy-start(bf16[1,4,64,256]{3,2,1,0:T(8,128)(2,1)} %get-tuple-element.30) | copy-start | bytes 393220
  33.3 6.6 %copy-start.6 = (bf16[8,4,128,64]{2,3,1,0:T(8,128)(2,1)}, bf16[8,4,128,64]{2,3,1,0:T(8,128)(2,1)S(1)}, u32[]{:S(2)}) copy-start(bf16[8,4,128,64]{2,3,1,0:T(8,128)(2,1)S(1)} %fusion.22) | copy-start | bytes 1572868
  40.0 2.6 %copy-start.5 = (f32[8,4,128,128]{3,2,1,0:T(8,128)S(1)}, f32[8,4,128,128]{3,2,1,0:T(8,128)}, u32[]{:S(2)}) copy-start(f32[8,4,128,128]{3,2,1,0:T(8,128)} %fusion.24) | copy-start | bytes 6291460
  40.0 2.9 %copy-start.25 = (f32[8,4,128,128]{2,3,1,0:T(8,128)S(1)}, f32[8,4,128,128]{2,3,1,0:T(8,128)}, u32[]{:S(2)}) copy-start(f32[8,4,128,128]{2,3,1,0:T(8,128)} %get-tuple-element.43) | copy-start | bytes 6291460
  40.0 2.9 %copy-start.26 = (f32[8,4,128]{2,1,0:T(4,128)S(1)}, f32[8,4,128]{2,1,0:T(4,128)}, u32[]{:S(2)}) copy-start(f32[8,4,128]{2,1,0:T(4,128)} %get-tuple-element.42) | copy-start | bytes 49156
  42.8 1.0 copy-start.7
  43.9 1.2 %copy-start.10 = (bf16[256,256]{0,1:T(8,128)(2,1)S(1)}, bf16[256,256]{0,1:T(8,128)(2,1)}, u32[]{:S(2)}) copy-start(bf16[256,256]{0,1:T(8,128)(2,1)} %copy.33) | copy-start | bytes 393220
  47.6 6.7 %copy-start.15 = (f32[256,4,64]{0,2,1:T(8,128)S(1)}, f32[256,4,64]{0,2,1:T(8,128)}, u32[]{:S(2)}) copy-start(f32[256,4,64]{0,2,1:T(8,128)} %convolution_bitcast_fusion.4) | copy-start | bytes 786436
  47.9 8.6 %collective-permute-start.4 = (bf16[4,64,256]{2,1,0:T(8,128)(2,1)S(1)}, bf16[4,64,256]{2,1,0:T(8,128)(2,1)S(1)}, u32[]{:S(2)}, u32[]{:S(2)}) collective-permute-start(bf16[4,64,256]{2,1,0:T(8,128)(2,1)S(1)} %bitcast.222), channel_id=1, source_target_pairs={{0,8},{8,16},{16,24},{24,0},{1,9},{9,17},{17,25},{25,1},{2,10},{10... | collective-permute-start | bytes 393224 | tf_op jit(solution)/shard_map/ppermute | solution.py:97
  51.3 10.6 %collective-permute-start.5 = (bf16[4,64,256]{2,1,0:T(8,128)(2,1)S(1)}, bf16[4,64,256]{2,1,0:T(8,128)(2,1)}, u32[]{:S(2)}, u32[]{:S(2)}) collective-permute-start(bf16[4,64,256]{2,1,0:T(8,128)(2,1)S(1)} %bitcast.223), channel_id=1, source_target_pairs={{0,16},{8,24},{16,0},{24,8},{1,17},{9,25},{17,1},{25,9},{2,18},{10... | collective-permute-start | bytes 393224 | tf_op jit(solution)/shard_map/ppermute | solution.py:97
  52.7 9.2 %collective-permute-start.6 = (bf16[4,64,256]{2,1,0:T(8,128)(2,1)S(1)}, bf16[4,64,256]{2,1,0:T(8,128)(2,1)}, u32[]{:S(2)}, u32[]{:S(2)}) collective-permute-start(bf16[4,64,256]{2,1,0:T(8,128)(2,1)S(1)} %bitcast.224), channel_id=1, source_target_pairs={{0,24},{8,0},{16,8},{24,16},{1,25},{9,1},{17,9},{25,17},{2,26},{10... | collective-permute-start | bytes 393224 | tf_op jit(solution)/shard_map/ppermute | solution.py:97
  61.9 1.9 %copy-start.11 = (f32[4,256,256]{2,1,0:T(8,128)S(1)}, f32[4,256,256]{2,1,0:T(8,128)}, u32[]{:S(2)}) copy-start(f32[4,256,256]{2,1,0:T(8,128)} %get-tuple-element.41) | copy-start | bytes 3145732
  63.7 1.0 copy-start.4
  65.2 1.0 copy-start.9
  65.3 2.0 %collective-permute-start.7 = (f32[131072]{0:T(1024)S(1)}, f32[131072]{0:T(1024)S(1)}, u32[]{:S(2)}, u32[]{:S(2)}) collective-permute-start(f32[131072]{0:T(1024)S(1)} %broadcast_select_fusion.3), channel_id=1, source_target_pairs={{0,1},{1,0},{2,3},{3,2},{4,5},{5,4},{6,7},{7,6},{8,9},{9,8},{10,11... | collective-permute-start | bytes 1572872 | tf_op jit(solution)/shard_map/ppermute | solution.py:33
  67.1 4.6 %copy-start.13 = (bf16[4,256,128]{2,1,0:T(8,128)(2,1)S(1)}, bf16[4,256,128]{2,1,0:T(8,128)(2,1)}, u32[]{:S(2)}) copy-start(bf16[4,256,128]{2,1,0:T(8,128)(2,1)} %copy-done.12) | copy-start | bytes 786436
  67.6 16.7 %copy-start.19 = (s32[4,128]{1,0:T(4,128)S(1)}, s32[4,128]{1,0:T(4,128)}, u32[]{:S(2)}) copy-start(s32[4,128]{1,0:T(4,128)} %param.15) | copy-start | bytes 6148
  67.6 16.7 %copy-start.22 = (pred[4,128]{1,0:T(4,128)(4,1)S(1)}, pred[4,128]{1,0:T(4,128)(4,1)}, u32[]{:S(2)}) copy-start(pred[4,128]{1,0:T(4,128)(4,1)} %copy-done.21) | copy-start | bytes 1540
  68.1 6.3 %collective-permute-start.10 = (f32[32768]{0:T(1024)S(1)}, f32[32768]{0:T(1024)S(1)}, u32[]{:S(2)}, u32[]{:S(2)}) collective-permute-start(f32[32768]{0:T(1024)S(1)} %bitcast.233), channel_id=1, source_target_pairs={{0,6},{1,7},{2,0},{3,1},{4,2},{5,3},{6,4},{7,5},{8,14},{9,15},{10,... | collective-permute-start | bytes 393224 | tf_op jit(solution)/shard_map/ppermute | solution.py:37
  70.2 7.3 %collective-permute-start.8 = (f32[32768]{0:T(1024)S(1)}, f32[32768]{0:T(1024)S(1)}, u32[]{:S(2)}, u32[]{:S(2)}) collective-permute-start(f32[32768]{0:T(1024)S(1)} %bitcast.232), channel_id=1, source_target_pairs={{0,2},{1,3},{2,4},{3,5},{4,6},{5,7},{6,0},{7,1},{8,10},{9,11},{10,... | collective-permute-start | bytes 393224 | tf_op jit(solution)/shard_map/ppermute | solution.py:37
  70.2 8.1 %collective-permute-start.9 = (f32[32768]{0:T(1024)S(1)}, f32[32768]{0:T(1024)S(1)}, u32[]{:S(2)}, u32[]{:S(2)}) collective-permute-start(f32[32768]{0:T(1024)S(1)} %bitcast.231), channel_id=1, source_target_pairs={{0,4},{1,5},{2,6},{3,7},{4,0},{5,1},{6,2},{7,3},{8,12},{9,13},{10,... | collective-permute-start | bytes 393224 | tf_op jit(solution)/shard_map/ppermute | solution.py:37
  72.3 12.0 %collective-permute-start.14 = (bf16[4,128,256]{2,1,0:T(8,128)(2,1)S(1)}, bf16[4,128,256]{2,1,0:T(8,128)(2,1)S(1)}, u32[]{:S(2)}, u32[]{:S(2)}) collective-permute-start(bf16[4,128,256]{2,1,0:T(8,128)(2,1)S(1)} %convolution_convert_fusion.6), channel_id=1, source_target_pairs={{0,7},{1,0},{2,1},{3,2},{4,3},{5,4},{6,5},{7,6},{8,15},{9,8},{10,9... | collective-permute-start | bytes 786440 | tf_op jit(solution)/shard_map/ppermute | solution.py:12
  78.4 16.9 %copy-start.20 = (pred[4]{0:T(512)(128)(4,1)S(1)}, pred[4]{0:T(512)(128)(4,1)}, u32[]{:S(2)}) copy-start(pred[4]{0:T(512)(128)(4,1)} %get-tuple-element.45) | copy-start | bytes 16
  78.5 7.1 %collective-permute-start.11 = (f32[8192]{0:T(1024)S(1)}, f32[8192]{0:T(1024)S(1)}, u32[]{:S(2)}, u32[]{:S(2)}) collective-permute-start(f32[8192]{0:T(1024)S(1)} %bitcast.239), channel_id=1, source_target_pairs={{0,8},{8,16},{16,24},{24,0},{1,9},{9,17},{17,25},{25,1},{2,10},{10... | collective-permute-start | bytes 98312 | tf_op jit(solution)/shard_map/ppermute | solution.py:37
  81.8 4.8 %collective-permute-start.12 = (f32[8192]{0:T(1024)S(1)}, f32[8192]{0:T(1024)S(1)}, u32[]{:S(2)}, u32[]{:S(2)}) collective-permute-start(f32[8192]{0:T(1024)S(1)} %bitcast.238), channel_id=1, source_target_pairs={{0,16},{8,24},{16,0},{24,8},{1,17},{9,25},{17,1},{25,9},{2,18},{10... | collective-permute-start | bytes 98312 | tf_op jit(solution)/shard_map/ppermute | solution.py:37
  83.4 3.9 %collective-permute-start.13 = (f32[8192]{0:T(1024)S(1)}, f32[8192]{0:T(1024)S(1)}, u32[]{:S(2)}, u32[]{:S(2)}) collective-permute-start(f32[8192]{0:T(1024)S(1)} %bitcast.237), channel_id=1, source_target_pairs={{0,24},{8,0},{16,8},{24,16},{1,25},{9,1},{17,9},{25,17},{2,26},{10... | collective-permute-start | bytes 98312 | tf_op jit(solution)/shard_map/ppermute | solution.py:37
  87.3 5.8 %collective-permute-start.15 = (f32[8192]{0:T(1024)S(1)}, f32[8192]{0:T(1024)S(1)}, u32[]{:S(2)}, u32[]{:S(2)}) collective-permute-start(f32[8192]{0:T(1024)S(1)} %add_add_fusion.1), channel_id=1, source_target_pairs={{0,8},{8,16},{16,24},{24,0},{1,9},{9,17},{17,25},{25,1},{2,10},{10... | collective-permute-start | bytes 98312 | tf_op jit(solution)/shard_map/ppermute | solution.py:49
  87.6 5.4 %collective-permute-start.16 = (f32[8192]{0:T(1024)S(1)}, f32[8192]{0:T(1024)S(1)}, u32[]{:S(2)}, u32[]{:S(2)}) collective-permute-start(f32[8192]{0:T(1024)S(1)} %add_add_fusion.1), channel_id=1, source_target_pairs={{0,16},{8,24},{16,0},{24,8},{1,17},{9,25},{17,1},{25,9},{2,18},{10... | collective-permute-start | bytes 98312 | tf_op jit(solution)/shard_map/ppermute | solution.py:49
  90.6 3.9 %collective-permute-start.17 = (f32[8192]{0:T(1024)S(1)}, f32[8192]{0:T(1024)S(1)}, u32[]{:S(2)}, u32[]{:S(2)}) collective-permute-start(f32[8192]{0:T(1024)S(1)} %add_add_fusion.1), channel_id=1, source_target_pairs={{0,24},{8,0},{16,8},{24,16},{1,25},{9,1},{17,9},{25,17},{2,26},{10... | collective-permute-start | bytes 98312 | tf_op jit(solution)/shard_map/ppermute | solution.py:49
  95.4 6.0 %collective-permute-start.18 = (f32[32768]{0:T(1024)S(1)}, f32[32768]{0:T(1024)S(1)}, u32[]{:S(2)}, u32[]{:S(2)}) collective-permute-start(f32[32768]{0:T(1024)S(1)} %bitcast.225), channel_id=1, source_target_pairs={{0,2},{1,3},{2,4},{3,5},{4,6},{5,7},{6,0},{7,1},{8,10},{9,11},{10,... | collective-permute-start | bytes 393224 | tf_op jit(solution)/shard_map/ppermute | solution.py:49
  96.1 6.4 %collective-permute-start.19 = (f32[32768]{0:T(1024)S(1)}, f32[32768]{0:T(1024)S(1)}, u32[]{:S(2)}, u32[]{:S(2)}) collective-permute-start(f32[32768]{0:T(1024)S(1)} %bitcast.226), channel_id=1, source_target_pairs={{0,4},{1,5},{2,6},{3,7},{4,0},{5,1},{6,2},{7,3},{8,12},{9,13},{10,... | collective-permute-start | bytes 393224 | tf_op jit(solution)/shard_map/ppermute | solution.py:49
  97.2 5.4 %collective-permute-start.20 = (f32[32768]{0:T(1024)S(1)}, f32[32768]{0:T(1024)S(1)}, u32[]{:S(2)}, u32[]{:S(2)}) collective-permute-start(f32[32768]{0:T(1024)S(1)} %bitcast.227), channel_id=1, source_target_pairs={{0,6},{1,7},{2,0},{3,1},{4,2},{5,3},{6,4},{7,5},{8,14},{9,15},{10,... | collective-permute-start | bytes 393224 | tf_op jit(solution)/shard_map/ppermute | solution.py:49
  104.2 2.0 %collective-permute-start.21 = (f32[131072]{0:T(1024)S(1)}, f32[131072]{0:T(1024)S(1)}, u32[]{:S(2)}, u32[]{:S(2)}) collective-permute-start(f32[131072]{0:T(1024)S(1)} %bitcast.218), channel_id=1, source_target_pairs={{0,1},{1,0},{2,3},{3,2},{4,5},{5,4},{6,7},{7,6},{8,9},{9,8},{10,11... | collective-permute-start | bytes 1572872 | tf_op jit(solution)/shard_map/ppermute | solution.py:44
  (1 other events, 0.6 us)

commit v14 on v13

--- a/solution.py
+++ b/solution.py
@@ -86,6 +86,51 @@
     return tuple(results), companion
 
 
+def early_late_sum(early, late_fn, axes, companion_fn):
+    sizes = [lax.axis_size(axis) for axis in axes]
+    total = 1
+    for size in sizes:
+        total *= size
+    head = jnp.concatenate([value.reshape(-1) for value in early])
+    usable = all(_power_of_two(size) for size in sizes) and sizes[0] > 1
+    if not usable or head.shape[0] % (2 * total):
+        late = late_fn()
+        companion = companion_fn()
+        results, companion = tree_sum(tuple(late) + tuple(early), axes, companion)
+        return results, companion
+    head = _scatter_step(head, axes[0], 1, 2)
+    late = late_fn()
+    tail = jnp.concatenate([value.reshape(-1) for value in late])
+    tail = _scatter_step(tail, axes[0], 1, 2)
+    companion = companion_fn()
+    flat = jnp.concatenate([tail, head])
+    steps = []
+    for axis, size in zip(axes, sizes):
+        stride = 2 if axis == axes[0] else 1
+        rest = size // 2 if axis == axes[0] else size
+        for group in _factors(rest) if rest > 1 else []:
+            if group > 1:
+                steps.append((axis, stride, group))
+            stride *= group
+    for axis, stride, group in steps:
+        flat = _scatter_step(flat, axis, stride, group)
+    flat, companion = lax.optimization_barrier((flat, companion))
+    for axis, stride, group in reversed(steps):
+        flat = _gather_step(flat, axis, stride, group)
+    whole = _gather_step(flat, axes[0], 1, 2)
+    half = flat.shape[0]
+    cut = tail.shape[0]
+    tail_all = jnp.concatenate([whole[:cut], whole[half : half + cut]])
+    head_all = jnp.concatenate([whole[cut:half], whole[half + cut :]])
+    results = []
+    for values, joined in ((late, tail_all), (early, head_all)):
+        start = 0
+        for value in values:
+            results.append(joined[start : start + value.size].reshape(value.shape))
+            start += value.size
+    return tuple(results), companion
+
+
 def exchange(value, axis, split_axis, concat_axis):
     count = lax.axis_size(axis)
     mine = lax.axis_index(axis)
@@ -319,33 +364,44 @@
     pre_grad = (
         back_days.astype(jnp.float32) * sigmoid_val * (1.0 + preact * (1.0 - sigmoid_val))
     ).astype(jnp.bfloat16)
-    grad_message = lax.dot_general(
-        aggregate.reshape(-1, width),
-        pre_grad.reshape(-1, width),
-        (((0,), (0,)), ((), ())),
-        preferred_element_type=jnp.float32,
-    )
-    agg_grad = jnp.einsum("drk,hk->drh", pre_grad, w_message, preferred_element_type=jnp.float32)
-    term_grad = agg_grad * inverse[:, :, None]
-    halo_grad = jnp.einsum(
-        "drs,drh->dsh",
-        adjacent_halo.astype(jnp.float32),
-        term_grad,
-        precision=lax.Precision.HIGHEST,
-        preferred_element_type=jnp.float32,
-    ).astype(jnp.bfloat16)
-    returned = from_behind(halo_grad, "dom", -1)
-    own_grad = jnp.einsum(
-        "drs,drh->dsh",
-        adjacent_local.astype(jnp.float32),
-        term_grad,
-        precision=lax.Precision.HIGHEST,
-        preferred_element_type=jnp.float32,
-    )
-    scattered = jnp.einsum("dsn,dsh->dnh", slot_hot, returned, preferred_element_type=jnp.float32)
-    state_grad = back_days.astype(jnp.float32) + term_grad + own_grad + scattered
-    (grad_message, grad_query, grad_key, grad_value), state_grad = tree_sum(
-        (grad_message, attn_grads[0], attn_grads[1], attn_grads[2]), ("dom", "day"), state_grad
+
+    def message_grad():
+        return (
+            lax.dot_general(
+                aggregate.reshape(-1, width),
+                pre_grad.reshape(-1, width),
+                (((0,), (0,)), ((), ())),
+                preferred_element_type=jnp.float32,
+            ),
+        )
+
+    def state_part():
+        agg_grad = jnp.einsum(
+            "drk,hk->drh", pre_grad, w_message, preferred_element_type=jnp.float32
+        )
+        term_grad = agg_grad * inverse[:, :, None]
+        halo_grad = jnp.einsum(
+            "drs,drh->dsh",
+            adjacent_halo.astype(jnp.float32),
+            term_grad,
+            precision=lax.Precision.HIGHEST,
+            preferred_element_type=jnp.float32,
+        ).astype(jnp.bfloat16)
+        returned = from_behind(halo_grad, "dom", -1)
+        own_grad = jnp.einsum(
+            "drs,drh->dsh",
+            adjacent_local.astype(jnp.float32),
+            term_grad,
+            precision=lax.Precision.HIGHEST,
+            preferred_element_type=jnp.float32,
+        )
+        scattered = jnp.einsum(
+            "dsn,dsh->dnh", slot_hot, returned, preferred_element_type=jnp.float32
+        )
+        return back_days.astype(jnp.float32) + term_grad + own_grad + scattered
+
+    (grad_message, grad_query, grad_key, grad_value), state_grad = early_late_sum(
+        attn_grads, message_grad, ("dom", "day"), state_part
     )
     return (state_grad, grad_message, grad_query, grad_key, grad_value)
 

time: 108 us -> 126 us (1.17)
  waiting for transfers between devices: 24 us -> 34.1 us
  starting transfers between devices: 32.2 us -> 24.6 us
  other arithmetic: 8.82 us -> 15.2 us
  local copies, waits for them, and re-layouts: 14.9 us -> 20.1 us
  matrix products: 25.9 us -> 29.4 us
    ppermute x6, waiting for transfers between devices: 10.4 us -> 17.3 us  [exchange(): lax.ppermute(send, axis, [(i, (i + shift) % count) for i in range(count)])]
    dot_general x3, local copies, waits for them, and re-layouts: 0.69 us -> 5.19 us  [contract(): return jnp.einsum(spec, left, right, preferred_element_type=jnp.float32)]
    ppermute x6, waiting for transfers between devices: 5.63 us -> 9.53 us  [_gather_step(): lax.ppermute(flat, axis, _group_pairs(axis, stride, group, shift))]
    sub x1, other arithmetic: 0.61 us -> 4.17 us  [attend_blocked(): prob_grad - jnp.sum(prob_grad * probs, axis=-1, keepdims=True)]
    another operation x4, local copies, waits for them, and re-layouts: 1.07 us -> 4.55 us  [the longest x3 4.26 us: early_late_sum(): head = jnp.concatenate([value.reshape(-1) for value in early])]
    ppermute x6, starting transfers between devices: 8.64 us -> 5.28 us  [_gather_step(): lax.ppermute(flat, axis, _group_pairs(axis, stride, group, shift))]
    unnamed x67 -> x70, local copies, waits for them, and re-layouts: 5.08 us -> 2.46 us
    dot_general x12, matrix products: 10.3 us -> 12.8 us  [contract(): return jnp.einsum(spec, left, right, preferred_element_type=jnp.float32)]
  transfers between devices with their start and end apart: 22 -> 23, of which waited for: 16 -> 13; matrix products, arithmetic and copies ran while one was open for 16% -> 14% of each run, Pallas kernels for 0% -> 0%
where the time goes in v14:
time: 126 us; the launch traced here: 125 us
  waiting for transfers between devices  34.1 us (27%)
  matrix products  29.4 us (23%)
  starting transfers between devices  24.6 us (20%)
  local copies, waits for them, and re-layouts  20.1 us (16%)
  other arithmetic  15.2 us (12%)
  between operations  1.51 us (1%)
    ppermute x6, waiting for transfers between devices, exchange(): lax.ppermute(send, axis, [(i, (i + shift) % count) for i in range(count)])  17.3 us
    dot_general x12, matrix products, contract(): return jnp.einsum(spec, left, right, preferred_element_type=jnp.float32)  12.8 us
    ppermute x6, starting transfers between devices, exchange(): lax.ppermute(send, axis, [(i, (i + shift) % count) for i in range(count)])  10.4 us
    ppermute x6, waiting for transfers between devices, _gather_step(): lax.ppermute(flat, axis, _group_pairs(axis, stride, group, shift))  9.53 us
    ppermute x6, starting transfers between devices, _scatter_step(): lax.ppermute(send, axis, _group_pairs(axis, stride, group, shift))  7.03 us
    ppermute x6, waiting for transfers between devices, _scatter_step(): lax.ppermute(send, axis, _group_pairs(axis, stride, group, shift))  5.73 us
    ppermute x6, starting transfers between devices, _gather_step(): lax.ppermute(flat, axis, _group_pairs(axis, stride, group, shift))  5.28 us
    dot_general x3, local copies, waits for them, and re-layouts, contract(): return jnp.einsum(spec, left, right, preferred_element_type=jnp.float32)  5.19 us
  transfers between devices with their start and end apart: 23, of which 13 were waited for; matrix products, arithmetic and copies ran while one was open for 14% of the time, Pallas kernels for 0%

profile of v14, /device:TPU:0, one launch (start us, length us, event | category | flops | bytes accessed | tf_op | source)
XLA Modules:
  0.0 125.1 jit_solution(10907718222470441215)
XLA Ops:
  1.9 2.1 %convolution_convert_fusion.7 = bf16[4,128,256]{2,1,0:T(8,128)(2,1)} fusion(bf16[4,256,256]{2,1,0:T(8,128)(2,1)} %param.12, s32[4,128]{1,0:T(4,128)} %param.15, pred[4,128]{1,0:T(4,128)(4,1)S(1)} %iota_compare_fusion.12), kind=kOutput, calls=%fused_computation.54 | convolution fusion | flops 67502080 | bytes 788992 | tf_op jit(solution)/shard_map/dsn,dnh->dsh/dot_general | solution.py:332
  5.1 1.2 convert_reduce_fusion
  6.3 2.4 %fusion.20 = bf16[4,256,256]{2,1,0:T(8,128)(2,1)S(1)} fusion(s32[4,1024]{1,0:T(4,128)} %param.13, s32[4,1024]{1,0:T(4,128)} %param.14), kind=kOutput, calls=%fused_computation.47 | convolution fusion | flops 539230208 | bytes 557056 | tf_op jit(solution)/shard_map/der,des->drs/dot_general | solution.py:341
  9.6 1.3 %fusion.25 = bf16[4,256,128]{2,1,0:T(8,128)(2,1)S(1)} fusion(s32[4,1024]{1,0:T(4,128)S(1)} %copy-done.21, s32[128]{0:T(128)S(1)} %iota_add_fusion, s32[4,1024]{1,0:T(4,128)S(1)} %copy-done.26), kind=kOutput, calls=%fused_computation.52 | convolution fusion | flops 270139392 | bytes 295424 | tf_op jit(solution)/shard_map/der,des->drs/dot_general | solution.py:344
  11.8 1.3 %fusion.18 = bf16[4,256,256]{2,1,0:T(8,128)(2,1)S(1)} fusion(f32[4,256,256]{2,1,0:T(8,128)S(1)} %fusion.64, bf16[4,256,128]{2,1,0:T(8,128)(2,1)S(1)} %fusion.25, bf16[4,128,256]{2,1,0:T(8,128)(2,1)} %collective-permute-done, bf16[4,256,256]{2,1,0:T(8,128)(2,1)S(1)} %copy-done.1, f32[4,256]{1,0:T(4,128)S(1)} %add_divide_fusion.1), kind=kOutput, calls=%fused_computation.39 | convolution fusion | flops 68419584 | bytes 2625536 | tf_op jit(solution)/shard_map/drs,dsh->drh/dot_general | solution.py:353
  13.1 1.3 %fusion.28 = (bf16[4,256,256]{2,1,0:T(8,128)(2,1)S(1)}, f32[4,256,256]{2,1,0:T(8,128)}) fusion(bf16[4,256,256]{2,1,0:T(8,128)(2,1)S(1)} %copy-done.1, bf16[4,256,256]{2,1,0:T(8,128)(2,1)S(1)} %fusion.18, bf16[256,256]{1,0:T(8,128)(2,1)S(1)} %copy-done), kind=kOutput, calls=%fused_computation.59 | convolution fusion | flops 136052736 | bytes 2752512 | tf_op jit(solution)/shard_map/drh,hk->drk/dot_general | solution.py:355
  15.2 4.6 %collective-permute-start.3 = (bf16[4,64,256]{2,1,0:T(8,128)(2,1)}, bf16[4,64,256]{2,1,0:T(8,128)(2,1)}, u32[]{:S(2)}, u32[]{:S(2)}) collective-permute-start(bf16[4,64,256]{2,1,0:T(8,128)(2,1)} %get-tuple-element.33), channel_id=1, source_target_pairs={{0,24},{8,0},{16,8},{24,16},{1,25},{9,1},{17,9},{25,17},{2,26},{10... | collective-permute-start | bytes 393224 | tf_op jit(solution)/shard_map/ppermute | solution.py:142
  19.8 1.0 collective-permute-start.1
  24.4 8.3 %collective-permute-done.2 = bf16[4,64,256]{2,1,0:T(8,128)(2,1)} collective-permute-done((bf16[4,64,256]{2,1,0:T(8,128)(2,1)}, bf16[4,64,256]{2,1,0:T(8,128)(2,1)}, u32[]{:S(2)}, u32[]{:S(2)}) %collective-permute-start.2) | collective-permute-done | bytes 131104 | tf_op jit(solution)/shard_map/ppermute | solution.py:142
  32.7 1.1 pad_maximum_fusion
  35.7 2.1 %fusion.24 = f32[8,4,128,128]{3,2,1,0:T(8,128)} fusion(bf16[8,128,4,64]{1,3,2,0:T(8,128)(2,1)S(1)} %copy.35, bf16[8,128,256,1]{2,1,3,0:T(8,128)(2,1)S(1)} %bitcast.208, bf16[256,4,64,1]{0,2,1,3:T(8,128)(2,1)S(1)} %bitcast.219), kind=kOutput, calls=%fused_computation.51 | convolution fusion | flops 201588736 | bytes 3276800 | tf_op jit(solution)/shard_map/gihd,ghjd->ghij/dot_general | solution.py:272
  37.7 3.5 %fusion.63 = (f32[8,4,128]{2,1,0:T(4,128)}, f32[8,4,128,128]{2,3,1,0:T(8,128)}) fusion(pred[128,128]{0,1:T(8,128)(4,1)} %compare_and_fusion, bf16[8,4,128,64]{2,3,1,0:T(8,128)(2,1)S(1)} %fusion.21, bf16[8,4,128,64]{2,3,1,0:T(8,128)(2,1)S(1)} %fusion.22), kind=kOutput, calls=%fused_computation.182 | convolution fusion | flops 69206144 | bytes 3178496 | tf_op jit(solution)/shard_map/sub | solution.py:285
  41.3 4.2 %fusion.7 = bf16[8,4,128,128]{2,3,1,0:T(8,128)(2,1)S(1)} fusion(f32[8,4,128,128]{3,2,1,0:T(8,128)} %fusion.24, f32[8,4,128,128]{2,3,1,0:T(8,128)} %get-tuple-element.47, f32[8,4,128]{2,1,0:T(4,128)} %get-tuple-element.46), kind=kOutput, calls=%fused_computation.16 | output fusion | flops 3674239 | bytes 5259264 | tf_op jit(solution)/shard_map/sub | solution.py:291
  46.3 1.2 convolution_convert_fusion.3
  48.3 1.0 convolution_bitcast_fusion.3
  49.7 1.0 convolution_bitcast_fusion.4
  50.7 1.4 %convolution_bitcast_fusion.1 = f32[8,128,256]{2,1,0:T(8,128)} fusion(bf16[8,4,128,64]{2,3,1,0:T(8,128)(2,1)S(1)} %convolution_convert_fusion.5, bf16[256,4,64,1]{0,2,1,3:T(8,128)(2,1)S(1)} %bitcast.218), kind=kOutput, calls=%fused_computation.27 | convolution fusion | flops 134217728 | bytes 1703936 | tf_op jit(solution)/shard_map/ghid,chd->gic/dot_general | solution.py:272
  52.1 1.2 copy.48
  53.5 2.1 %convolution_bitcast_fusion.5 = f32[256,4,64]{0,2,1:T(8,128)} fusion(bf16[8,128,256,1]{2,1,3,0:T(8,128)(2,1)S(1)} %bitcast.211, bf16[8,4,128,64]{2,3,1,0:T(8,128)(2,1)} %convolution_convert_fusion.3), kind=kOutput, calls=%fused_computation.57 | convolution fusion | flops 134217728 | bytes 1310720 | tf_op jit(solution)/shard_map/gic,ghid->chd/dot_general | solution.py:272
  55.6 2.1 %copy.46 = f32[256,4,64]{2,1,0:T(4,128)} copy(f32[256,4,64]{0,2,1:T(8,128)} %convolution_bitcast_fusion.5) | data formatting | bytes 524288 | tf_op jit(solution)/shard_map/gic,ghid->chd/dot_general | solution.py:272
  57.6 2.0 %reshape_reshape.14 = f32[65536]{0:T(1024)} reshape(f32[256,4,64]{2,1,0:T(4,128)} %copy.46) | data formatting | bytes 524288 | tf_op jit(solution)/shard_map/reshape;reshape | solution.py:94
  59.6 2.0 %copy.50 = f32[256,4,64]{2,1,0:T(4,128)} copy(f32[256,4,64]{0,2,1:T(8,128)} %convolution_bitcast_fusion.3) | data formatting | bytes 524288 | tf_op jit(solution)/shard_map/gic,ghid->chd/dot_general | solution.py:272
  61.6 2.0 %reshape_reshape.16 = f32[65536]{0:T(1024)} reshape(f32[256,4,64]{2,1,0:T(4,128)} %copy.50) | data formatting | bytes 524288 | tf_op jit(solution)/shard_map/reshape;reshape | solution.py:94
  63.6 1.5 %fusion.19 = bf16[8,128,256]{2,1,0:T(8,128)(2,1)S(1)} fusion(f32[8,128,256]{2,1,0:T(8,128)S(1)} %convolution_bitcast_fusion, f32[8,128,256]{2,1,0:T(8,128)S(1)} %copy-done.2, f32[8,128,256]{2,1,0:T(8,128)S(1)} %bitcast.212, bf16[8,4,128,64]{2,3,1,0:T(8,128)(2,1)} %convolution_convert_fusion.3, bf16[256,4,64,1]{0,2,1,3:T(8,128)(2,1)} %bitcast.216), kind=kOutput, calls=%fused_computation.46 | convolution fusion | flops 135266304 | bytes 4325376 | tf_op jit(solution)/shard_map/ghid,chd->gic/dot_general | solution.py:272
  66.0 2.0 %collective-permute-start.5 = (bf16[4,64,256]{2,1,0:T(8,128)(2,1)S(1)}, bf16[4,64,256]{2,1,0:T(8,128)(2,1)S(1)}, u32[]{:S(2)}, u32[]{:S(2)}) collective-permute-start(bf16[4,64,256]{2,1,0:T(8,128)(2,1)S(1)} %bitcast.230), channel_id=1, source_target_pairs={{0,16},{8,24},{16,0},{24,8},{1,17},{9,25},{17,1},{25,9},{2,18},{10... | collective-permute-start | bytes 393224 | tf_op jit(solution)/shard_map/ppermute | solution.py:142
  68.0 2.3 %collective-permute-start.4 = (bf16[4,64,256]{2,1,0:T(8,128)(2,1)S(1)}, bf16[4,64,256]{2,1,0:T(8,128)(2,1)S(1)}, u32[]{:S(2)}, u32[]{:S(2)}) collective-permute-start(bf16[4,64,256]{2,1,0:T(8,128)(2,1)S(1)} %bitcast.231), channel_id=1, source_target_pairs={{0,8},{8,16},{16,24},{24,0},{1,9},{9,17},{17,25},{25,1},{2,10},{10... | collective-permute-start | bytes 393224 | tf_op jit(solution)/shard_map/ppermute | solution.py:142
  71.1 9.0 %collective-permute-done.5 = bf16[4,64,256]{2,1,0:T(8,128)(2,1)S(1)} collective-permute-done((bf16[4,64,256]{2,1,0:T(8,128)(2,1)S(1)}, bf16[4,64,256]{2,1,0:T(8,128)(2,1)S(1)}, u32[]{:S(2)}, u32[]{:S(2)}) %collective-permute-start.5) | collective-permute-done | bytes 131104 | tf_op jit(solution)/shard_map/ppermute | solution.py:142
  82.9 0.9 convolution_add_fusion
  84.1 1.1 select_add_fusion
  86.0 1.5 %collective-permute-start.11 = (f32[32768]{0:T(1024)S(1)}, f32[32768]{0:T(1024)S(1)}, u32[]{:S(2)}, u32[]{:S(2)}) collective-permute-start(f32[32768]{0:T(1024)S(1)} %bitcast.239), channel_id=1, source_target_pairs={{0,6},{1,7},{2,0},{3,1},{4,2},{5,3},{6,4},{7,5},{8,14},{9,15},{10,... | collective-permute-start | bytes 393224 | tf_op jit(solution)/shard_map/ppermute | solution.py:37
  87.5 1.5 %collective-permute-start.10 = (f32[32768]{0:T(1024)S(1)}, f32[32768]{0:T(1024)S(1)}, u32[]{:S(2)}, u32[]{:S(2)}) collective-permute-start(f32[32768]{0:T(1024)S(1)} %bitcast.237), channel_id=1, source_target_pairs={{0,4},{1,5},{2,6},{3,7},{4,0},{5,1},{6,2},{7,3},{8,12},{9,13},{10,... | collective-permute-start | bytes 393224 | tf_op jit(solution)/shard_map/ppermute | solution.py:37
  89.6 1.5 %convolution_convert_fusion.6 = bf16[4,128,256]{2,1,0:T(8,128)(2,1)S(1)} fusion(bf16[4,256,128]{2,1,0:T(8,128)(2,1)} %copy-done.16, f32[4,256,256]{2,1,0:T(8,128)S(1)} %convolution_multiply_fusion), kind=kOutput, calls=%fused_computation.53 | convolution fusion | flops 402784256 | bytes 1572864 | tf_op jit(solution)/shard_map/drs,drh->dsh/dot_general | solution.py:383
  91.1 1.3 %collective-permute-start.15 = (bf16[4,128,256]{2,1,0:T(8,128)(2,1)S(1)}, bf16[4,128,256]{2,1,0:T(8,128)(2,1)S(1)}, u32[]{:S(2)}, u32[]{:S(2)}) collective-permute-start(bf16[4,128,256]{2,1,0:T(8,128)(2,1)S(1)} %convolution_convert_fusion.6), channel_id=1, source_target_pairs={{0,7},{1,0},{2,1},{3,2},{4,3},{5,4},{6,5},{7,6},{8,15},{9,8},{10,9... | collective-permute-start | bytes 786440 | tf_op jit(solution)/shard_map/ppermute | solution.py:12
  92.4 3.2 %collective-permute-done.10 = f32[32768]{0:T(1024)S(1)} collective-permute-done((f32[32768]{0:T(1024)S(1)}, f32[32768]{0:T(1024)S(1)}, u32[]{:S(2)}, u32[]{:S(2)}) %collective-permute-start.10) | collective-permute-done | bytes 131104 | tf_op jit(solution)/shard_map/ppermute | solution.py:37
  95.9 1.4 %collective-permute-start.13 = (f32[8192]{0:T(1024)S(1)}, f32[8192]{0:T(1024)S(1)}, u32[]{:S(2)}, u32[]{:S(2)}) collective-permute-start(f32[8192]{0:T(1024)S(1)} %bitcast.245), channel_id=1, source_target_pairs={{0,16},{8,24},{16,0},{24,8},{1,17},{9,25},{17,1},{25,9},{2,18},{10... | collective-permute-start | bytes 98312 | tf_op jit(solution)/shard_map/ppermute | solution.py:37
  97.3 1.9 %collective-permute-start.12 = (f32[8192]{0:T(1024)S(1)}, f32[8192]{0:T(1024)S(1)}, u32[]{:S(2)}, u32[]{:S(2)}) collective-permute-start(f32[8192]{0:T(1024)S(1)} %bitcast.244), channel_id=1, source_target_pairs={{0,8},{8,16},{16,24},{24,0},{1,9},{9,17},{17,25},{25,1},{2,10},{10... | collective-permute-start | bytes 98312 | tf_op jit(solution)/shard_map/ppermute | solution.py:37
  99.2 1.3 %convolution_add_fusion.1 = f32[4,256,256]{2,1,0:T(8,128)} fusion(f32[4,256,256]{2,1,0:T(8,128)S(1)} %convolution_add_fusion, bf16[4,128,256]{2,1,0:T(8,128)(2,1)S(1)} %collective-permute-done.15, s32[4,128]{1,0:T(4,128)S(1)} %copy-done.22, pred[4,128]{1,0:T(4,128)(4,1)S(1)} %copy-done.25), kind=kOutput, calls=%fused_computation.29 | convolution fusion | flops 67633152 | bytes 2361856 | tf_op jit(solution)/shard_map/dsn,dsh->dnh/dot_general | solution.py:398
  100.8 2.3 %collective-permute-done.12 = f32[8192]{0:T(1024)S(1)} collective-permute-done((f32[8192]{0:T(1024)S(1)}, f32[8192]{0:T(1024)S(1)}, u32[]{:S(2)}, u32[]{:S(2)}) %collective-permute-start.12) | collective-permute-done | bytes 32800 | tf_op jit(solution)/shard_map/ppermute | solution.py:37
  103.1 1.1 collective-permute-start.18
  105.2 1.9 %collective-permute-done.18 = f32[8192]{0:T(1024)S(1)} collective-permute-done((f32[8192]{0:T(1024)S(1)}, f32[8192]{0:T(1024)S(1)}, u32[]{:S(2)}, u32[]{:S(2)}) %collective-permute-start.18) | collective-permute-done | bytes 32800 | tf_op jit(solution)/shard_map/ppermute | solution.py:49
  107.0 2.0 %collective-permute-done.17 = f32[8192]{0:T(1024)S(1)} collective-permute-done((f32[8192]{0:T(1024)S(1)}, f32[8192]{0:T(1024)S(1)}, u32[]{:S(2)}, u32[]{:S(2)}) %collective-permute-start.17) | collective-permute-done | bytes 32800 | tf_op jit(solution)/shard_map/ppermute | solution.py:49
  109.0 1.3 %collective-permute-done.16 = f32[8192]{0:T(1024)S(1)} collective-permute-done((f32[8192]{0:T(1024)S(1)}, f32[8192]{0:T(1024)S(1)}, u32[]{:S(2)}, u32[]{:S(2)}) %collective-permute-start.16) | collective-permute-done | bytes 32800 | tf_op jit(solution)/shard_map/ppermute | solution.py:49
  111.2 1.2 collective-permute-start.21
  113.1 1.4 %collective-permute-start.19 = (f32[32768]{0:T(1024)S(1)}, f32[32768]{0:T(1024)S(1)}, u32[]{:S(2)}, u32[]{:S(2)}) collective-permute-start(f32[32768]{0:T(1024)S(1)} %bitcast.228), channel_id=1, source_target_pairs={{0,2},{1,3},{2,4},{3,5},{4,6},{5,7},{6,0},{7,1},{8,10},{9,11},{10,... | collective-permute-start | bytes 393224 | tf_op jit(solution)/shard_map/ppermute | solution.py:49
  114.6 1.6 %collective-permute-done.21 = f32[32768]{0:T(1024)S(1)} collective-permute-done((f32[32768]{0:T(1024)S(1)}, f32[32768]{0:T(1024)S(1)}, u32[]{:S(2)}, u32[]{:S(2)}) %collective-permute-start.21) | collective-permute-done | bytes 131104 | tf_op jit(solution)/shard_map/ppermute | solution.py:49
  116.3 1.2 collective-permute-done.20
  117.4 1.5 %collective-permute-done.19 = f32[32768]{0:T(1024)S(1)} collective-permute-done((f32[32768]{0:T(1024)S(1)}, f32[32768]{0:T(1024)S(1)}, u32[]{:S(2)}, u32[]{:S(2)}) %collective-permute-start.19) | collective-permute-done | bytes 131104 | tf_op jit(solution)/shard_map/ppermute | solution.py:49
  121.1 1.3 %collective-permute-done.22 = f32[131072]{0:T(1024)S(1)} collective-permute-done((f32[131072]{0:T(1024)S(1)}, f32[131072]{0:T(1024)S(1)}, u32[]{:S(2)}, u32[]{:S(2)}) %collective-permute-start.22) | collective-permute-done | bytes 524320 | tf_op jit(solution)/shard_map/ppermute | solution.py:44
  (158 shorter events, 26.2 us)
Async XLA Ops:
  0.6 12.4 %copy-start = (bf16[256,256]{1,0:T(8,128)(2,1)S(1)}, bf16[256,256]{1,0:T(8,128)(2,1)}, u32[]{:S(2)}) copy-start(bf16[256,256]{1,0:T(8,128)(2,1)} %param.17) | copy-start | bytes 393220
  4.0 7.7 %collective-permute-start = (bf16[4,128,256]{2,1,0:T(8,128)(2,1)}, bf16[4,128,256]{2,1,0:T(8,128)(2,1)}, u32[]{:S(2)}, u32[]{:S(2)}) collective-permute-start(bf16[4,128,256]{2,1,0:T(8,128)(2,1)} %convolution_convert_fusion.7), channel_id=1, source_target_pairs={{0,1},{1,2},{2,3},{3,4},{4,5},{5,6},{6,7},{7,0},{8,9},{9,10},{10,1... | collective-permute-start | bytes 786440 | tf_op jit(solution)/shard_map/ppermute | solution.py:12
  6.3 2.4 %copy-start.1 = (bf16[4,256,256]{2,1,0:T(8,128)(2,1)S(1)}, bf16[4,256,256]{2,1,0:T(8,128)(2,1)}, u32[]{:S(2)}) copy-start(bf16[4,256,256]{2,1,0:T(8,128)(2,1)} %param.12) | copy-start | bytes 1572868
  8.7 2.2 %copy-start.12 = (bf16[4,256,256]{2,1,0:T(8,128)(2,1)}, bf16[4,256,256]{2,1,0:T(8,128)(2,1)S(1)}, u32[]{:S(2)}) copy-start(bf16[4,256,256]{2,1,0:T(8,128)(2,1)S(1)} %fusion.20) | copy-start | bytes 1572868
  9.6 2.1 %copy-start.7 = (bf16[16,1,1,64,256]{4,3,2,1,0:T(8,128)(2,1)S(1)}, bf16[16,1,1,64,256]{4,3,2,1,0:T(8,128)(2,1)}, u32[]{:S(2)}) copy-start(bf16[16,1,1,64,256]{4,3,2,1,0:T(8,128)(2,1)} %param.21) | copy-start | bytes 1572868
  10.9 2.2 %copy-start.16 = (bf16[4,256,128]{2,1,0:T(8,128)(2,1)}, bf16[4,256,128]{2,1,0:T(8,128)(2,1)S(1)}, u32[]{:S(2)}) copy-start(bf16[4,256,128]{2,1,0:T(8,128)(2,1)S(1)} %fusion.25) | copy-start | bytes 786436
  13.1 1.4 %copy-start.8 = (bf16[4,256,256]{2,1,0:T(8,128)(2,1)}, bf16[4,256,256]{2,1,0:T(8,128)(2,1)S(1)}, u32[]{:S(2)}) copy-start(bf16[4,256,256]{2,1,0:T(8,128)(2,1)S(1)} %fusion.18) | copy-start | bytes 1572868
  15.2 9.2 %collective-permute-start.3 = (bf16[4,64,256]{2,1,0:T(8,128)(2,1)}, bf16[4,64,256]{2,1,0:T(8,128)(2,1)}, u32[]{:S(2)}, u32[]{:S(2)}) collective-permute-start(bf16[4,64,256]{2,1,0:T(8,128)(2,1)} %get-tuple-element.33), channel_id=1, source_target_pairs={{0,24},{8,0},{16,8},{24,16},{1,25},{9,1},{17,9},{25,17},{2,26},{10... | collective-permute-start | bytes 393224 | tf_op jit(solution)/shard_map/ppermute | solution.py:142
  19.8 12.9 %collective-permute-start.2 = (bf16[4,64,256]{2,1,0:T(8,128)(2,1)}, bf16[4,64,256]{2,1,0:T(8,128)(2,1)}, u32[]{:S(2)}, u32[]{:S(2)}) collective-permute-start(bf16[4,64,256]{2,1,0:T(8,128)(2,1)} %get-tuple-element.34), channel_id=1, source_target_pairs={{0,16},{8,24},{16,0},{24,8},{1,17},{9,25},{17,1},{25,9},{2,18},{10... | collective-permute-start | bytes 393224 | tf_op jit(solution)/shard_map/ppermute | solution.py:142
  19.8 12.9 %collective-permute-start.1 = (bf16[4,64,256]{2,1,0:T(8,128)(2,1)}, bf16[4,64,256]{2,1,0:T(8,128)(2,1)}, u32[]{:S(2)}, u32[]{:S(2)}) collective-permute-start(bf16[4,64,256]{2,1,0:T(8,128)(2,1)} %get-tuple-element.35), channel_id=1, source_target_pairs={{0,8},{8,16},{16,24},{24,0},{1,9},{9,17},{17,25},{25,1},{2,10},{10... | collective-permute-start | bytes 393224 | tf_op jit(solution)/shard_map/ppermute | solution.py:142
  21.4 1.3 %copy-start.18 = (bf16[256,256]{1,0:T(8,128)(2,1)S(1)}, bf16[256,256]{1,0:T(8,128)(2,1)}, u32[]{:S(2)}) copy-start(bf16[256,256]{1,0:T(8,128)(2,1)} %param.20) | copy-start | bytes 393220
  21.7 1.1 copy-start.19
  21.7 1.2 copy-start.20
  22.1 10.6 %copy-start.17 = (bf16[1,4,64,256]{3,2,1,0:T(8,128)(2,1)S(1)}, bf16[1,4,64,256]{3,2,1,0:T(8,128)(2,1)}, u32[]{:S(2)}) copy-start(bf16[1,4,64,256]{3,2,1,0:T(8,128)(2,1)} %get-tuple-element.32) | copy-start | bytes 393220
  22.9 12.0 %copy-start.14 = (bf16[256,256]{0,1:T(8,128)(2,1)}, bf16[256,256]{0,1:T(8,128)(2,1)S(1)}, u32[]{:S(2)}) copy-start(bf16[256,256]{0,1:T(8,128)(2,1)S(1)} %copy.31) | copy-start | bytes 393220
  35.3 2.4 %copy-start.10 = (bf16[8,4,128,64]{2,3,1,0:T(8,128)(2,1)}, bf16[8,4,128,64]{2,3,1,0:T(8,128)(2,1)S(1)}, u32[]{:S(2)}) copy-start(bf16[8,4,128,64]{2,3,1,0:T(8,128)(2,1)S(1)} %fusion.21) | copy-start | bytes 1572868
  41.3 4.2 %copy-start.11 = (bf16[8,4,128,64]{2,3,1,0:T(8,128)(2,1)S(1)}, bf16[8,4,128,64]{2,3,1,0:T(8,128)(2,1)}, u32[]{:S(2)}) copy-start(bf16[8,4,128,64]{2,3,1,0:T(8,128)(2,1)} %copy-done.10) | copy-start | bytes 1572868
  45.4 2.0 %copy-start.27 = (f32[8,4,128,128]{2,3,1,0:T(8,128)S(1)}, f32[8,4,128,128]{2,3,1,0:T(8,128)}, u32[]{:S(2)}) copy-start(f32[8,4,128,128]{2,3,1,0:T(8,128)} %get-tuple-element.47) | copy-start | bytes 6291460
  45.5 2.0 %copy-start.28 = (f32[8,4,128]{2,1,0:T(4,128)S(1)}, f32[8,4,128]{2,1,0:T(4,128)}, u32[]{:S(2)}) copy-start(f32[8,4,128]{2,1,0:T(4,128)} %get-tuple-element.46) | copy-start | bytes 49156
  55.6 8.0 %copy-start.2 = (f32[8,128,256]{2,1,0:T(8,128)S(1)}, f32[8,128,256]{2,1,0:T(8,128)}, u32[]{:S(2)}) copy-start(f32[8,128,256]{2,1,0:T(8,128)} %convolution_bitcast_fusion.1) | copy-start | bytes 3145732
  63.6 6.7 %copy-start.3 = (f32[65536]{0:T(1024)S(1)}, f32[65536]{0:T(1024)}, u32[]{:S(2)}) copy-start(f32[65536]{0:T(1024)} %reshape_reshape.14) | copy-start | bytes 786436
  63.6 6.7 %copy-start.5 = (f32[65536]{0:T(1024)S(1)}, f32[65536]{0:T(1024)}, u32[]{:S(2)}) copy-start(f32[65536]{0:T(1024)} %reshape_reshape.16) | copy-start | bytes 786436
  65.4 5.7 %collective-permute-start.6 = (bf16[4,64,256]{2,1,0:T(8,128)(2,1)S(1)}, bf16[4,64,256]{2,1,0:T(8,128)(2,1)S(1)}, u32[]{:S(2)}, u32[]{:S(2)}) collective-permute-start(bf16[4,64,256]{2,1,0:T(8,128)(2,1)S(1)} %bitcast.229), channel_id=1, source_target_pairs={{0,24},{8,0},{16,8},{24,16},{1,25},{9,1},{17,9},{25,17},{2,26},{10... | collective-permute-start | bytes 393224 | tf_op jit(solution)/shard_map/ppermute | solution.py:142
  66.0 14.1 %collective-permute-start.5 = (bf16[4,64,256]{2,1,0:T(8,128)(2,1)S(1)}, bf16[4,64,256]{2,1,0:T(8,128)(2,1)S(1)}, u32[]{:S(2)}, u32[]{:S(2)}) collective-permute-start(bf16[4,64,256]{2,1,0:T(8,128)(2,1)S(1)} %bitcast.230), channel_id=1, source_target_pairs={{0,16},{8,24},{16,0},{24,8},{1,17},{9,25},{17,1},{25,9},{2,18},{10... | collective-permute-start | bytes 393224 | tf_op jit(solution)/shard_map/ppermute | solution.py:142
  68.0 12.1 %collective-permute-start.4 = (bf16[4,64,256]{2,1,0:T(8,128)(2,1)S(1)}, bf16[4,64,256]{2,1,0:T(8,128)(2,1)S(1)}, u32[]{:S(2)}, u32[]{:S(2)}) collective-permute-start(bf16[4,64,256]{2,1,0:T(8,128)(2,1)S(1)} %bitcast.231), channel_id=1, source_target_pairs={{0,8},{8,16},{16,24},{24,0},{1,9},{9,17},{17,25},{25,1},{2,10},{10... | collective-permute-start | bytes 393224 | tf_op jit(solution)/shard_map/ppermute | solution.py:142
  71.1 13.0 %collective-permute-start.8 = (f32[98304]{0:T(1024)}, f32[98304]{0:T(1024)}, u32[]{:S(2)}, u32[]{:S(2)}) collective-permute-start(f32[98304]{0:T(1024)} %fusion.45), channel_id=1, source_target_pairs={{0,1},{1,0},{2,3},{3,2},{4,5},{5,4},{6,7},{7,6},{8,9},{9,8},{10,11... | collective-permute-start | bytes 1179656 | tf_op jit(solution)/shard_map/ppermute | solution.py:33
  80.1 1.2 copy-start.15
  80.7 1.1 copy-start.9
  82.6 1.5 %copy-start.4 = (f32[65536]{0:T(1024)S(1)}, f32[65536]{0:T(1024)}, u32[]{:S(2)}) copy-start(f32[65536]{0:T(1024)} %reshape_reshape.14) | copy-start | bytes 786436
  82.6 1.5 %copy-start.6 = (f32[65536]{0:T(1024)S(1)}, f32[65536]{0:T(1024)}, u32[]{:S(2)}) copy-start(f32[65536]{0:T(1024)} %reshape_reshape.16) | copy-start | bytes 786436
  82.7 1.4 %collective-permute-start.7 = (f32[32768]{0:T(1024)S(1)}, f32[32768]{0:T(1024)S(1)}, u32[]{:S(2)}, u32[]{:S(2)}) collective-permute-start(f32[32768]{0:T(1024)S(1)} %bitcast.232), channel_id=1, source_target_pairs={{0,1},{1,0},{2,3},{3,2},{4,5},{5,4},{6,7},{7,6},{8,9},{9,8},{10,11... | collective-permute-start | bytes 393224 | tf_op jit(solution)/shard_map/ppermute | solution.py:33
  85.5 13.7 %copy-start.22 = (s32[4,128]{1,0:T(4,128)S(1)}, s32[4,128]{1,0:T(4,128)}, u32[]{:S(2)}) copy-start(s32[4,128]{1,0:T(4,128)} %param.15) | copy-start | bytes 6148
  85.5 13.7 %copy-start.25 = (pred[4,128]{1,0:T(4,128)(4,1)S(1)}, pred[4,128]{1,0:T(4,128)(4,1)}, u32[]{:S(2)}) copy-start(pred[4,128]{1,0:T(4,128)(4,1)} %copy-done.24) | copy-start | bytes 1540
  86.0 6.4 %collective-permute-start.11 = (f32[32768]{0:T(1024)S(1)}, f32[32768]{0:T(1024)S(1)}, u32[]{:S(2)}, u32[]{:S(2)}) collective-permute-start(f32[32768]{0:T(1024)S(1)} %bitcast.239), channel_id=1, source_target_pairs={{0,6},{1,7},{2,0},{3,1},{4,2},{5,3},{6,4},{7,5},{8,14},{9,15},{10,... | collective-permute-start | bytes 393224 | tf_op jit(solution)/shard_map/ppermute | solution.py:37
  87.5 8.1 %collective-permute-start.10 = (f32[32768]{0:T(1024)S(1)}, f32[32768]{0:T(1024)S(1)}, u32[]{:S(2)}, u32[]{:S(2)}) collective-permute-start(f32[32768]{0:T(1024)S(1)} %bitcast.237), channel_id=1, source_target_pairs={{0,4},{1,5},{2,6},{3,7},{4,0},{5,1},{6,2},{7,3},{8,12},{9,13},{10,... | collective-permute-start | bytes 393224 | tf_op jit(solution)/shard_map/ppermute | solution.py:37
  89.0 6.6 %collective-permute-start.9 = (f32[32768]{0:T(1024)S(1)}, f32[32768]{0:T(1024)S(1)}, u32[]{:S(2)}, u32[]{:S(2)}) collective-permute-start(f32[32768]{0:T(1024)S(1)} %bitcast.235), channel_id=1, source_target_pairs={{0,2},{1,3},{2,4},{3,5},{4,6},{5,7},{6,0},{7,1},{8,10},{9,11},{10,... | collective-permute-start | bytes 393224 | tf_op jit(solution)/shard_map/ppermute | solution.py:37
  91.1 8.1 %collective-permute-start.15 = (bf16[4,128,256]{2,1,0:T(8,128)(2,1)S(1)}, bf16[4,128,256]{2,1,0:T(8,128)(2,1)S(1)}, u32[]{:S(2)}, u32[]{:S(2)}) collective-permute-start(bf16[4,128,256]{2,1,0:T(8,128)(2,1)S(1)} %convolution_convert_fusion.6), channel_id=1, source_target_pairs={{0,7},{1,0},{2,1},{3,2},{4,3},{5,4},{6,5},{7,6},{8,15},{9,8},{10,9... | collective-permute-start | bytes 786440 | tf_op jit(solution)/shard_map/ppermute | solution.py:12
  95.6 15.5 %copy-start.23 = (pred[4]{0:T(512)(128)(4,1)S(1)}, pred[4]{0:T(512)(128)(4,1)}, u32[]{:S(2)}) copy-start(pred[4]{0:T(512)(128)(4,1)} %get-tuple-element.49) | copy-start | bytes 16
  95.8 4.7 %collective-permute-start.14 = (f32[8192]{0:T(1024)S(1)}, f32[8192]{0:T(1024)S(1)}, u32[]{:S(2)}, u32[]{:S(2)}) collective-permute-start(f32[8192]{0:T(1024)S(1)} %bitcast.246), channel_id=1, source_target_pairs={{0,24},{8,0},{16,8},{24,16},{1,25},{9,1},{17,9},{25,17},{2,26},{10... | collective-permute-start | bytes 98312 | tf_op jit(solution)/shard_map/ppermute | solution.py:37
  95.9 4.9 %collective-permute-start.13 = (f32[8192]{0:T(1024)S(1)}, f32[8192]{0:T(1024)S(1)}, u32[]{:S(2)}, u32[]{:S(2)}) collective-permute-start(f32[8192]{0:T(1024)S(1)} %bitcast.245), channel_id=1, source_target_pairs={{0,16},{8,24},{16,0},{24,8},{1,17},{9,25},{17,1},{25,9},{2,18},{10... | collective-permute-start | bytes 98312 | tf_op jit(solution)/shard_map/ppermute | solution.py:37
  97.3 5.8 %collective-permute-start.12 = (f32[8192]{0:T(1024)S(1)}, f32[8192]{0:T(1024)S(1)}, u32[]{:S(2)}, u32[]{:S(2)}) collective-permute-start(f32[8192]{0:T(1024)S(1)} %bitcast.244), channel_id=1, source_target_pairs={{0,8},{8,16},{16,24},{24,0},{1,9},{9,17},{17,25},{25,1},{2,10},{10... | collective-permute-start | bytes 98312 | tf_op jit(solution)/shard_map/ppermute | solution.py:37
  103.1 4.0 %collective-permute-start.18 = (f32[8192]{0:T(1024)S(1)}, f32[8192]{0:T(1024)S(1)}, u32[]{:S(2)}, u32[]{:S(2)}) collective-permute-start(f32[8192]{0:T(1024)S(1)} %add_add_fusion.1), channel_id=1, source_target_pairs={{0,24},{8,0},{16,8},{24,16},{1,25},{9,1},{17,9},{25,17},{2,26},{10... | collective-permute-start | bytes 98312 | tf_op jit(solution)/shard_map/ppermute | solution.py:49
  104.2 4.8 %collective-permute-start.17 = (f32[8192]{0:T(1024)S(1)}, f32[8192]{0:T(1024)S(1)}, u32[]{:S(2)}, u32[]{:S(2)}) collective-permute-start(f32[8192]{0:T(1024)S(1)} %add_add_fusion.1), channel_id=1, source_target_pairs={{0,16},{8,24},{16,0},{24,8},{1,17},{9,25},{17,1},{25,9},{2,18},{10... | collective-permute-start | bytes 98312 | tf_op jit(solution)/shard_map/ppermute | solution.py:49
  104.6 5.7 %collective-permute-start.16 = (f32[8192]{0:T(1024)S(1)}, f32[8192]{0:T(1024)S(1)}, u32[]{:S(2)}, u32[]{:S(2)}) collective-permute-start(f32[8192]{0:T(1024)S(1)} %add_add_fusion.1), channel_id=1, source_target_pairs={{0,8},{8,16},{16,24},{24,0},{1,9},{9,17},{17,25},{25,1},{2,10},{10... | collective-permute-start | bytes 98312 | tf_op jit(solution)/shard_map/ppermute | solution.py:49
  111.2 5.0 %collective-permute-start.21 = (f32[32768]{0:T(1024)S(1)}, f32[32768]{0:T(1024)S(1)}, u32[]{:S(2)}, u32[]{:S(2)}) collective-permute-start(f32[32768]{0:T(1024)S(1)} %bitcast.226), channel_id=1, source_target_pairs={{0,6},{1,7},{2,0},{3,1},{4,2},{5,3},{6,4},{7,5},{8,14},{9,15},{10,... | collective-permute-start | bytes 393224 | tf_op jit(solution)/shard_map/ppermute | solution.py:49
  112.4 5.0 %collective-permute-start.20 = (f32[32768]{0:T(1024)S(1)}, f32[32768]{0:T(1024)S(1)}, u32[]{:S(2)}, u32[]{:S(2)}) collective-permute-start(f32[32768]{0:T(1024)S(1)} %bitcast.227), channel_id=1, source_target_pairs={{0,4},{1,5},{2,6},{3,7},{4,0},{5,1},{6,2},{7,3},{8,12},{9,13},{10,... | collective-permute-start | bytes 393224 | tf_op jit(solution)/shard_map/ppermute | solution.py:49
  113.1 5.9 %collective-permute-start.19 = (f32[32768]{0:T(1024)S(1)}, f32[32768]{0:T(1024)S(1)}, u32[]{:S(2)}, u32[]{:S(2)}) collective-permute-start(f32[32768]{0:T(1024)S(1)} %bitcast.228), channel_id=1, source_target_pairs={{0,2},{1,3},{2,4},{3,5},{4,6},{5,7},{6,0},{7,1},{8,10},{9,11},{10,... | collective-permute-start | bytes 393224 | tf_op jit(solution)/shard_map/ppermute | solution.py:49
  120.5 2.0 %collective-permute-start.22 = (f32[131072]{0:T(1024)S(1)}, f32[131072]{0:T(1024)S(1)}, u32[]{:S(2)}, u32[]{:S(2)}) collective-permute-start(f32[131072]{0:T(1024)S(1)} %bitcast.222), channel_id=1, source_target_pairs={{0,1},{1,0},{2,3},{3,2},{4,5},{5,4},{6,7},{7,6},{8,9},{9,8},{10,11... | collective-permute-start | bytes 1572872 | tf_op jit(solution)/shard_map/ppermute | solution.py:44
  (4 other events, 3.1 us)

commit v15 on v13

--- a/solution.py
+++ b/solution.py
@@ -290,22 +290,22 @@
     received = from_behind(sent, "dom", 1)
 
     target_hot = (edge_target[:, :, None] == rows[None, None, :]).astype(jnp.bfloat16)
-    local_hot = (edge_source[:, :, None] == rows[None, None, :]).astype(jnp.bfloat16)
-    halo_ids = node_local + jnp.arange(halo_slots, dtype=jnp.int32)
-    halo_hot = (edge_source[:, :, None] == halo_ids[None, None, :]).astype(jnp.bfloat16)
-    adjacent_local = jnp.einsum(
-        "der,des->drs", target_hot, local_hot, preferred_element_type=jnp.float32
-    ).astype(jnp.bfloat16)
-    adjacent_halo = jnp.einsum(
-        "der,des->drs", target_hot, halo_hot, preferred_element_type=jnp.float32
-    ).astype(jnp.bfloat16)
-    counted = jnp.sum(target_hot.astype(jnp.float32), axis=1)
+    extended_ids = jnp.arange(node_local + halo_slots, dtype=jnp.int32)
+    source_hot = (edge_source[:, :, None] == extended_ids[None, None, :]).astype(jnp.bfloat16)
+    adjacent = jnp.einsum(
+        "der,des->drs", target_hot, source_hot, preferred_element_type=jnp.float32
+    ).astype(jnp.bfloat16)
+    counted = jnp.einsum(
+        "der,e->dr",
+        target_hot,
+        jnp.ones(target_hot.shape[1], jnp.bfloat16),
+        preferred_element_type=jnp.float32,
+    )
     inverse = 1.0 / (counted + 1.0)
 
     states_f = node_states.astype(jnp.float32)
-    neighbours = jnp.einsum(
-        "drs,dsh->drh", adjacent_local, node_states, preferred_element_type=jnp.float32
-    ) + jnp.einsum("drs,dsh->drh", adjacent_halo, received, preferred_element_type=jnp.float32)
+    extended = jnp.concatenate([node_states, received], axis=1)
+    neighbours = jnp.einsum("drs,dsh->drh", adjacent, extended, preferred_element_type=jnp.float32)
     aggregate = ((states_f + neighbours) * inverse[:, :, None]).astype(jnp.bfloat16)
     preact = jnp.einsum("drh,hk->drk", aggregate, w_message, preferred_element_type=jnp.float32)
     hidden = (states_f + jax.nn.silu(preact)).astype(jnp.bfloat16)
@@ -327,21 +327,16 @@
     )
     agg_grad = jnp.einsum("drk,hk->drh", pre_grad, w_message, preferred_element_type=jnp.float32)
     term_grad = agg_grad * inverse[:, :, None]
-    halo_grad = jnp.einsum(
+    ext_grad = jnp.einsum(
         "drs,drh->dsh",
-        adjacent_halo.astype(jnp.float32),
+        adjacent.astype(jnp.float32),
         term_grad,
         precision=lax.Precision.HIGHEST,
         preferred_element_type=jnp.float32,
-    ).astype(jnp.bfloat16)
+    )
+    halo_grad = ext_grad[:, node_local:].astype(jnp.bfloat16)
     returned = from_behind(halo_grad, "dom", -1)
-    own_grad = jnp.einsum(
-        "drs,drh->dsh",
-        adjacent_local.astype(jnp.float32),
-        term_grad,
-        precision=lax.Precision.HIGHEST,
-        preferred_element_type=jnp.float32,
-    )
+    own_grad = ext_grad[:, :node_local]
     scattered = jnp.einsum("dsn,dsh->dnh", slot_hot, returned, preferred_element_type=jnp.float32)
     state_grad = back_days.astype(jnp.float32) + term_grad + own_grad + scattered
     (grad_message, grad_query, grad_key, grad_value), state_grad = tree_sum(

time: 108 us -> 106 us (0.981)
  waiting for transfers between devices: 24 us -> 22.3 us
    ppermute x6, waiting for transfers between devices: 6.45 us -> 3.41 us  [_scatter_step(): lax.ppermute(send, axis, _group_pairs(axis, stride, group, shift))]
    ppermute x6, waiting for transfers between devices: 10.4 us -> 8.5 us  [exchange(): lax.ppermute(send, axis, [(i, (i + shift) % count) for i in range(count)])]
    unnamed x67 -> x59, local copies, waits for them, and re-layouts: 5.08 us -> 3.36 us
    ppermute x1, waiting for transfers between devices: 0.18 us -> 1.88 us  [_scatter_step(): return keep + lax.ppermute(send, axis, _group_pairs(axis, stride, group, 1))]
    ppermute x2, waiting for transfers between devices: 0.01 us -> 1.67 us  [from_behind(): return lax.ppermute(value, axis, pairs)]
    reduce_sum x1 -> x0, other arithmetic: 1.22 us -> none  [local(): counted = jnp.sum(target_hot.astype(jnp.float32), axis=1)]
    dot_general x6 -> x4, matrix products: 6.72 us -> 7.87 us  [the longest x1 2.9 us: local(): jnp.einsum('der,des->drs', target_hot, source_hot, preferred_element_type...]
  transfers between devices with their start and end apart: 22 -> 22, of which waited for: 16 -> 16; matrix products, arithmetic and copies ran while one was open for 16% -> 17% of each run, Pallas kernels for 0% -> 0%
where the time goes in v15:
time: 106 us
  starting transfers between devices  31.7 us (30%)
  matrix products  26.4 us (25%)
  waiting for transfers between devices  22.3 us (21%)
  local copies, waits for them, and re-layouts  14.5 us (14%)
  other arithmetic  9.11 us (9%)
  between operations  1.4 us (1%)
    ppermute x6, starting transfers between devices, exchange(): lax.ppermute(send, axis, [(i, (i + shift) % count) for i in range(count)])  12.3 us
    dot_general x12, matrix products, contract(): return jnp.einsum(spec, left, right, preferred_element_type=jnp.float32)  9.44 us
    ppermute x6, starting transfers between devices, _scatter_step(): lax.ppermute(send, axis, _group_pairs(axis, stride, group, shift))  8.82 us
    ppermute x6, waiting for transfers between devices, exchange(): lax.ppermute(send, axis, [(i, (i + shift) % count) for i in range(count)])  8.5 us
    ppermute x6, starting transfers between devices, _gather_step(): lax.ppermute(flat, axis, _group_pairs(axis, stride, group, shift))  8.38 us
    ppermute x6, waiting for transfers between devices, _gather_step(): lax.ppermute(flat, axis, _group_pairs(axis, stride, group, shift))  5.55 us
    sub x1, matrix products, attend_blocked(): exponent = jnp.exp(scores - highest)  3.51 us
    ppermute x6, waiting for transfers between devices, _scatter_step(): lax.ppermute(send, axis, _group_pairs(axis, stride, group, shift))  3.41 us
  transfers between devices with their start and end apart: 22, of which 16 were waited for; matrix products, arithmetic and copies ran while one was open for 17% of the time, Pallas kernels for 0%

profile of v15, /device:TPU:0, one launch (start us, length us, event | category | flops | bytes accessed | tf_op | source)
XLA Modules:
  0.0 105.5 jit_solution(12492735210627894066)
XLA Ops:
  0.6 0.8 iota_compare_fusion.10
  1.4 1.4 %convolution_convert_fusion.6 = bf16[4,128,256]{2,1,0:T(8,128)(2,1)S(1)} fusion(bf16[4,256,256]{2,1,0:T(8,128)(2,1)} %param.12, s32[4,128]{1,0:T(4,128)} %param.15, pred[4,128]{1,0:T(4,128)(4,1)S(1)} %iota_compare_fusion.10), kind=kOutput, calls=%fused_computation.47 | convolution fusion | flops 67502080 | bytes 788992 | tf_op jit(solution)/shard_map/dsn,dnh->dsh/dot_general | solution.py:287
  3.4 1.4 %fusion.3 = f32[1,4,256]{2,0,1:T(1,128)S(1)} fusion(s32[4,1024]{1,0:T(4,128)} %param.14), kind=kOutput, calls=%fused_computation.9 | convolution fusion | flops 3145728 | bytes 20480 | tf_op jit(solution)/shard_map/der,e->dr/dot_general | solution.py:298
  4.8 2.9 %fusion.11 = bf16[4,256,384]{2,1,0:T(8,128)(2,1)S(1)} fusion(s32[4,1024]{1,0:T(4,128)} %param.13, s32[4,1024]{1,0:T(4,128)} %param.14), kind=kOutput, calls=%fused_computation.21 | convolution fusion | flops 808321024 | bytes 819200 | tf_op jit(solution)/shard_map/der,des->drs/dot_general | solution.py:295
  7.8 0.8 compare_and_fusion
  8.7 1.7 %collective-permute-done = bf16[4,128,256]{2,1,0:T(8,128)(2,1)} collective-permute-done((bf16[4,128,256]{2,1,0:T(8,128)(2,1)S(1)}, bf16[4,128,256]{2,1,0:T(8,128)(2,1)}, u32[]{:S(2)}, u32[]{:S(2)}) %collective-permute-start) | collective-permute-done | bytes 262176 | tf_op jit(solution)/shard_map/ppermute | solution.py:12
  10.4 1.4 %fusion.16 = bf16[4,256,256]{2,1,0:T(8,128)(2,1)S(1)} fusion(bf16[4,256,384]{2,1,0:T(8,128)(2,1)S(1)} %fusion.11, bf16[4,256,256]{2,1,0:T(8,128)(2,1)S(1)} %copy-done.9, bf16[4,128,256]{2,1,0:T(8,128)(2,1)} %collective-permute-done, f32[4,256]{1,0:T(4,128)S(1)} %fusion.46), kind=kOutput, calls=%fused_computation.35 | convolution fusion | flops 203948032 | bytes 2101248 | tf_op jit(solution)/shard_map/drs,dsh->drh/dot_general | solution.py:308
  11.8 1.3 %fusion.22 = (bf16[4,256,256]{2,1,0:T(8,128)(2,1)S(1)}, f32[4,256,256]{2,1,0:T(8,128)}) fusion(bf16[4,256,256]{2,1,0:T(8,128)(2,1)S(1)} %copy-done.9, bf16[4,256,256]{2,1,0:T(8,128)(2,1)S(1)} %fusion.16, bf16[256,256]{1,0:T(8,128)(2,1)S(1)} %copy-done), kind=kOutput, calls=%fused_computation.52 | convolution fusion | flops 136052736 | bytes 2752512 | tf_op jit(solution)/shard_map/drh,hk->drk/dot_general | solution.py:310
  13.2 0.7 dynamic-slice_bitcast_fusion
  13.9 2.3 %collective-permute-start.1 = (bf16[4,64,256]{2,1,0:T(8,128)(2,1)}, bf16[4,64,256]{2,1,0:T(8,128)(2,1)}, u32[]{:S(2)}, u32[]{:S(2)}) collective-permute-start(bf16[4,64,256]{2,1,0:T(8,128)(2,1)} %get-tuple-element.33), channel_id=1, source_target_pairs={{0,8},{8,16},{16,24},{24,0},{1,9},{9,17},{17,25},{25,1},{2,10},{10... | collective-permute-start | bytes 393224 | tf_op jit(solution)/shard_map/ppermute | solution.py:97
  16.2 2.6 %collective-permute-start.2 = (bf16[4,64,256]{2,1,0:T(8,128)(2,1)}, bf16[4,64,256]{2,1,0:T(8,128)(2,1)}, u32[]{:S(2)}, u32[]{:S(2)}) collective-permute-start(bf16[4,64,256]{2,1,0:T(8,128)(2,1)} %get-tuple-element.32), channel_id=1, source_target_pairs={{0,16},{8,24},{16,0},{24,8},{1,17},{9,25},{17,1},{25,9},{2,18},{10... | collective-permute-start | bytes 393224 | tf_op jit(solution)/shard_map/ppermute | solution.py:97
  18.8 1.3 %collective-permute-start.3 = (bf16[4,64,256]{2,1,0:T(8,128)(2,1)S(1)}, bf16[4,64,256]{2,1,0:T(8,128)(2,1)}, u32[]{:S(2)}, u32[]{:S(2)}) collective-permute-start(bf16[4,64,256]{2,1,0:T(8,128)(2,1)S(1)} %get-tuple-element.31), channel_id=1, source_target_pairs={{0,24},{8,0},{16,8},{24,16},{1,25},{9,1},{17,9},{25,17},{2,26},{10... | collective-permute-start | bytes 393224 | tf_op jit(solution)/shard_map/ppermute | solution.py:97
  21.7 1.2 %copy.35 = bf16[8,128,4,64]{1,3,2,0:T(8,128)(2,1)} copy(bf16[8,128,4,64]{3,2,1,0:T(4,128)(2,1)S(1)} %reshape_reshape.12) | data formatting | bytes 1048576 | tf_op jit(solution)/shard_map/reshape;reshape | solution.py:232
  22.9 0.8 copy.33
  24.4 3.8 %collective-permute-done.2 = bf16[4,64,256]{2,1,0:T(8,128)(2,1)} collective-permute-done((bf16[4,64,256]{2,1,0:T(8,128)(2,1)}, bf16[4,64,256]{2,1,0:T(8,128)(2,1)}, u32[]{:S(2)}, u32[]{:S(2)}) %collective-permute-start.2) | collective-permute-done | bytes 131104 | tf_op jit(solution)/shard_map/ppermute | solution.py:97
  28.2 1.1 %pad_maximum_fusion = bf16[4,4,64,256]{3,2,1,0:T(8,128)(2,1)S(1)} fusion(bf16[1,4,64,256]{3,2,1,0:T(8,128)(2,1)} %bitcast.6, bf16[1,4,64,256]{3,2,1,0:T(8,128)(2,1)} %bitcast.5, bf16[1,4,64,256]{3,2,1,0:T(8,128)(2,1)} %bitcast.4, bf16[1,4,64,256]{3,2,1,0:T(8,128)(2,1)S(1)} %get-tuple-element.30), kind=kLoop, calls=%fused_computation.68 | loop fusion | flops 786432 | bytes 1048576 | tf_op jit(solution)/shard_map/stack | solution.py:99
  31.1 3.0 %fusion.21 = f32[8,4,128,128]{3,2,1,0:T(8,128)} fusion(bf16[8,128,4,64]{1,3,2,0:T(8,128)(2,1)S(1)} %copy-done.1, bf16[8,128,256,1]{2,1,3,0:T(8,128)(2,1)S(1)} %bitcast.203, bf16[256,4,64,1]{0,2,1,3:T(8,128)(2,1)} %bitcast.214), kind=kOutput, calls=%fused_computation.46 | convolution fusion | flops 201588736 | bytes 3276800 | tf_op jit(solution)/shard_map/gihd,ghjd->ghij/dot_general | solution.py:227
  34.1 3.5 %fusion.60 = (f32[8,4,128]{2,1,0:T(4,128)}, f32[8,4,128,128]{2,3,1,0:T(8,128)}) fusion(pred[128,128]{0,1:T(8,128)(4,1)} %compare_and_fusion, bf16[8,4,128,64]{2,3,1,0:T(8,128)(2,1)S(1)} %fusion.18, bf16[8,4,128,64]{2,3,1,0:T(8,128)(2,1)S(1)} %fusion.19), kind=kOutput, calls=%fused_computation.176 | convolution fusion | flops 69206144 | bytes 3178496 | tf_op jit(solution)/shard_map/sub | solution.py:240
  37.6 2.6 %convolution_convert_fusion.4 = bf16[8,4,128,64]{2,3,1,0:T(8,128)(2,1)S(1)} fusion(bf16[8,128,4,64]{1,3,2,0:T(8,128)(2,1)S(1)} %copy-done.1, f32[8,4,128,128]{2,3,1,0:T(8,128)} %get-tuple-element.43, f32[8,4,128]{2,1,0:T(4,128)} %get-tuple-element.42), kind=kOutput, calls=%fused_computation.40 | convolution fusion | flops 68419584 | bytes 3162112 | tf_op jit(solution)/shard_map/ghij,gihd->ghjd/dot_general | solution.py:227
  41.5 0.8 convolution_convert_fusion.5
  44.4 3.3 %collective-permute-start.4 = (bf16[4,64,256]{2,1,0:T(8,128)(2,1)S(1)}, bf16[4,64,256]{2,1,0:T(8,128)(2,1)}, u32[]{:S(2)}, u32[]{:S(2)}) collective-permute-start(bf16[4,64,256]{2,1,0:T(8,128)(2,1)S(1)} %bitcast.221), channel_id=1, source_target_pairs={{0,8},{8,16},{16,24},{24,0},{1,9},{9,17},{17,25},{25,1},{2,10},{10... | collective-permute-start | bytes 393224 | tf_op jit(solution)/shard_map/ppermute | solution.py:97
  47.8 1.7 %collective-permute-start.5 = (bf16[4,64,256]{2,1,0:T(8,128)(2,1)S(1)}, bf16[4,64,256]{2,1,0:T(8,128)(2,1)S(1)}, u32[]{:S(2)}, u32[]{:S(2)}) collective-permute-start(bf16[4,64,256]{2,1,0:T(8,128)(2,1)S(1)} %bitcast.222), channel_id=1, source_target_pairs={{0,16},{8,24},{16,0},{24,8},{1,17},{9,25},{17,1},{25,9},{2,18},{10... | collective-permute-start | bytes 393224 | tf_op jit(solution)/shard_map/ppermute | solution.py:97
  49.5 1.0 collective-permute-start.6
  53.1 4.5 %collective-permute-done.5 = bf16[4,64,256]{2,1,0:T(8,128)(2,1)S(1)} collective-permute-done((bf16[4,64,256]{2,1,0:T(8,128)(2,1)S(1)}, bf16[4,64,256]{2,1,0:T(8,128)(2,1)S(1)}, u32[]{:S(2)}, u32[]{:S(2)}) %collective-permute-start.5) | collective-permute-done | bytes 131104 | tf_op jit(solution)/shard_map/ppermute | solution.py:97
  58.3 1.2 %pad_maximum_fusion.1 = bf16[4,4,64,256]{3,2,1,0:T(8,128)(2,1)S(1)} fusion(bf16[1,4,64,256]{3,2,1,0:T(8,128)(2,1)} %bitcast.51, bf16[1,4,64,256]{3,2,1,0:T(8,128)(2,1)} %bitcast.229, bf16[1,4,64,256]{3,2,1,0:T(8,128)(2,1)} %bitcast.47, bf16[1,4,64,256]{3,2,1,0:T(8,128)(2,1)S(1)} %bitcast.219), kind=kLoop, calls=%fused_computation.70 | loop fusion | flops 786432 | bytes 1048576 | tf_op jit(solution)/shard_map/stack | solution.py:99
  61.6 0.9 broadcast_select_fusion.3
  62.9 1.9 %collective-permute-done.7 = f32[131072]{0:T(1024)} collective-permute-done((f32[131072]{0:T(1024)}, f32[131072]{0:T(1024)}, u32[]{:S(2)}, u32[]{:S(2)}) %collective-permute-start.7) | collective-permute-done | bytes 524320 | tf_op jit(solution)/shard_map/ppermute | solution.py:33
  64.7 1.1 %select_add_fusion = f32[131072]{0:T(1024)S(1)} fusion(f32[131072]{0:T(1024)} %collective-permute-done.7, f32[131072]{0:T(1024)S(1)} %constant_dynamic-update-slice_fusion, f32[131072]{0:T(1024)S(1)} %constant_dynamic-update-slice_fusion.1, pred[]{:T(512)S(6)} %eq.87), kind=kLoop, calls=%fused_computation.74 | loop fusion | flops 262144 | bytes 2097153 | tf_op jit(solution)/shard_map/add | solution.py:33
  66.6 1.4 %collective-permute-start.10 = (f32[32768]{0:T(1024)S(1)}, f32[32768]{0:T(1024)S(1)}, u32[]{:S(2)}, u32[]{:S(2)}) collective-permute-start(f32[32768]{0:T(1024)S(1)} %bitcast.232), channel_id=1, source_target_pairs={{0,6},{1,7},{2,0},{3,1},{4,2},{5,3},{6,4},{7,5},{8,14},{9,15},{10,... | collective-permute-start | bytes 393224 | tf_op jit(solution)/shard_map/ppermute | solution.py:37
  68.6 1.5 %collective-permute-start.9 = (f32[32768]{0:T(1024)S(1)}, f32[32768]{0:T(1024)S(1)}, u32[]{:S(2)}, u32[]{:S(2)}) collective-permute-start(f32[32768]{0:T(1024)S(1)} %bitcast.230), channel_id=1, source_target_pairs={{0,4},{1,5},{2,6},{3,7},{4,0},{5,1},{6,2},{7,3},{8,12},{9,13},{10,... | collective-permute-start | bytes 393224 | tf_op jit(solution)/shard_map/ppermute | solution.py:37
  70.2 2.1 %fusion.61 = f32[4,384,256]{2,1,0:T(8,128)S(1)} fusion(bf16[4,256,384]{2,1,0:T(8,128)(2,1)} %copy-done.8, f32[4,256,256]{2,1,0:T(8,128)S(1)} %convolution_multiply_fusion), kind=kOutput, calls=%fused_computation.177 | convolution fusion | flops 1207959552 | bytes 3407872 | tf_op jit(solution)/shard_map/drs,drh->dsh/dot_general | solution.py:330
  73.0 1.7 %collective-permute-start.14 = (bf16[4,128,256]{2,1,0:T(8,128)(2,1)}, bf16[4,128,256]{2,1,0:T(8,128)(2,1)}, u32[]{:S(2)}, u32[]{:S(2)}) collective-permute-start(bf16[4,128,256]{2,1,0:T(8,128)(2,1)} %slice.101), channel_id=1, source_target_pairs={{0,7},{1,0},{2,1},{3,2},{4,3},{5,4},{6,5},{7,6},{8,15},{9,8},{10,9... | collective-permute-start | bytes 786440 | tf_op jit(solution)/shard_map/ppermute | solution.py:12
  74.7 1.3 %collective-permute-done.8 = f32[32768]{0:T(1024)S(1)} collective-permute-done((f32[32768]{0:T(1024)S(1)}, f32[32768]{0:T(1024)S(1)}, u32[]{:S(2)}, u32[]{:S(2)}) %collective-permute-start.8) | collective-permute-done | bytes 131104 | tf_op jit(solution)/shard_map/ppermute | solution.py:37
  76.9 2.8 %collective-permute-start.11 = (f32[8192]{0:T(1024)S(1)}, f32[8192]{0:T(1024)S(1)}, u32[]{:S(2)}, u32[]{:S(2)}) collective-permute-start(f32[8192]{0:T(1024)S(1)} %bitcast.238), channel_id=1, source_target_pairs={{0,8},{8,16},{16,24},{24,0},{1,9},{9,17},{17,25},{25,1},{2,10},{10... | collective-permute-start | bytes 98312 | tf_op jit(solution)/shard_map/ppermute | solution.py:37
  79.7 2.2 %collective-permute-start.12 = (f32[8192]{0:T(1024)S(1)}, f32[8192]{0:T(1024)S(1)}, u32[]{:S(2)}, u32[]{:S(2)}) collective-permute-start(f32[8192]{0:T(1024)S(1)} %bitcast.237), channel_id=1, source_target_pairs={{0,16},{8,24},{16,0},{24,8},{1,17},{9,25},{17,1},{25,9},{2,18},{10... | collective-permute-start | bytes 98312 | tf_op jit(solution)/shard_map/ppermute | solution.py:37
  82.1 2.2 %convolution_add_fusion.1 = f32[4,256,256]{2,1,0:T(8,128)} fusion(bf16[4,128,256]{2,1,0:T(8,128)(2,1)} %collective-permute-done.14, f32[4,256,256]{2,1,0:T(8,128)S(1)} %convolution_multiply_fusion, f32[4,384,256]{2,1,0:T(8,128)S(1)} %fusion.61, s32[4,128]{1,0:T(4,128)S(1)} %copy-done.17, pred[4,128]{1,0:T(4,128)(4,1)S(1)} %copy-done.19, ...), kind=kOutput, calls=%fused_computation.27 | convolution fusion | flops 70254592 | bytes 3934720 | tf_op jit(solution)/shard_map/dsn,dsh->dnh/dot_general | solution.py:340
  84.5 1.3 %collective-permute-done.13 = f32[8192]{0:T(1024)S(1)} collective-permute-done((f32[8192]{0:T(1024)S(1)}, f32[8192]{0:T(1024)S(1)}, u32[]{:S(2)}, u32[]{:S(2)}) %collective-permute-start.13) | collective-permute-done | bytes 32800 | tf_op jit(solution)/shard_map/ppermute | solution.py:37
  86.2 2.4 %collective-permute-start.16 = (f32[8192]{0:T(1024)S(1)}, f32[8192]{0:T(1024)S(1)}, u32[]{:S(2)}, u32[]{:S(2)}) collective-permute-start(f32[8192]{0:T(1024)S(1)} %add_add_fusion.1), channel_id=1, source_target_pairs={{0,16},{8,24},{16,0},{24,8},{1,17},{9,25},{17,1},{25,9},{2,18},{10... | collective-permute-start | bytes 98312 | tf_op jit(solution)/shard_map/ppermute | solution.py:49
  88.6 1.1 %collective-permute-start.17 = (f32[8192]{0:T(1024)S(1)}, f32[8192]{0:T(1024)S(1)}, u32[]{:S(2)}, u32[]{:S(2)}) collective-permute-start(f32[8192]{0:T(1024)S(1)} %add_add_fusion.1), channel_id=1, source_target_pairs={{0,24},{8,0},{16,8},{24,16},{1,25},{9,1},{17,9},{25,17},{2,26},{10... | collective-permute-start | bytes 98312 | tf_op jit(solution)/shard_map/ppermute | solution.py:49
  89.7 1.9 %collective-permute-done.15 = f32[8192]{0:T(1024)S(1)} collective-permute-done((f32[8192]{0:T(1024)S(1)}, f32[8192]{0:T(1024)S(1)}, u32[]{:S(2)}, u32[]{:S(2)}) %collective-permute-start.15) | collective-permute-done | bytes 32800 | tf_op jit(solution)/shard_map/ppermute | solution.py:49
  91.6 0.9 collective-permute-done.17
  93.3 1.1 %collective-permute-start.18 = (f32[32768]{0:T(1024)S(1)}, f32[32768]{0:T(1024)S(1)}, u32[]{:S(2)}, u32[]{:S(2)}) collective-permute-start(f32[32768]{0:T(1024)S(1)} %bitcast.224), channel_id=1, source_target_pairs={{0,2},{1,3},{2,4},{3,5},{4,6},{5,7},{6,0},{7,1},{8,10},{9,11},{10,... | collective-permute-start | bytes 393224 | tf_op jit(solution)/shard_map/ppermute | solution.py:49
  95.0 2.8 %collective-permute-start.20 = (f32[32768]{0:T(1024)S(1)}, f32[32768]{0:T(1024)S(1)}, u32[]{:S(2)}, u32[]{:S(2)}) collective-permute-start(f32[32768]{0:T(1024)S(1)} %bitcast.226), channel_id=1, source_target_pairs={{0,6},{1,7},{2,0},{3,1},{4,2},{5,3},{6,4},{7,5},{8,14},{9,15},{10,... | collective-permute-start | bytes 393224 | tf_op jit(solution)/shard_map/ppermute | solution.py:49
  98.0 1.4 %collective-permute-done.18 = f32[32768]{0:T(1024)S(1)} collective-permute-done((f32[32768]{0:T(1024)S(1)}, f32[32768]{0:T(1024)S(1)}, u32[]{:S(2)}, u32[]{:S(2)}) %collective-permute-start.18) | collective-permute-done | bytes 131104 | tf_op jit(solution)/shard_map/ppermute | solution.py:49
  99.4 1.3 %collective-permute-done.19 = f32[32768]{0:T(1024)S(1)} collective-permute-done((f32[32768]{0:T(1024)S(1)}, f32[32768]{0:T(1024)S(1)}, u32[]{:S(2)}, u32[]{:S(2)}) %collective-permute-start.19) | collective-permute-done | bytes 131104 | tf_op jit(solution)/shard_map/ppermute | solution.py:49
  101.3 0.8 gather_fusion.1
  103.0 1.3 %collective-permute-done.21 = f32[131072]{0:T(1024)S(1)} collective-permute-done((f32[131072]{0:T(1024)S(1)}, f32[131072]{0:T(1024)S(1)}, u32[]{:S(2)}, u32[]{:S(2)}) %collective-permute-start.21) | collective-permute-done | bytes 524320 | tf_op jit(solution)/shard_map/ppermute | solution.py:44
  104.5 1.0 fusion.59
  (137 shorter events, 20.7 us)
Async XLA Ops:
  0.6 11.2 %copy-start = (bf16[256,256]{1,0:T(8,128)(2,1)S(1)}, bf16[256,256]{1,0:T(8,128)(2,1)}, u32[]{:S(2)}) copy-start(bf16[256,256]{1,0:T(8,128)(2,1)} %param.17) | copy-start | bytes 393220
  1.4 1.9 %copy-start.18 = (pred[4,128]{1,0:T(4,128)(4,1)}, pred[4,128]{1,0:T(4,128)(4,1)S(1)}, u32[]{:S(2)}) copy-start(pred[4,128]{1,0:T(4,128)(4,1)S(1)} %iota_compare_fusion.10) | copy-start | bytes 1540
  2.8 7.5 %collective-permute-start = (bf16[4,128,256]{2,1,0:T(8,128)(2,1)S(1)}, bf16[4,128,256]{2,1,0:T(8,128)(2,1)}, u32[]{:S(2)}, u32[]{:S(2)}) collective-permute-start(bf16[4,128,256]{2,1,0:T(8,128)(2,1)S(1)} %convolution_convert_fusion.6), channel_id=1, source_target_pairs={{0,1},{1,2},{2,3},{3,4},{4,5},{5,6},{6,7},{7,0},{8,9},{9,10},{10,1... | collective-permute-start | bytes 786440 | tf_op jit(solution)/shard_map/ppermute | solution.py:12
  4.8 3.8 %copy-start.2 = (bf16[16,1,1,64,256]{4,3,2,1,0:T(8,128)(2,1)S(1)}, bf16[16,1,1,64,256]{4,3,2,1,0:T(8,128)(2,1)}, u32[]{:S(2)}) copy-start(bf16[16,1,1,64,256]{4,3,2,1,0:T(8,128)(2,1)} %param.21) | copy-start | bytes 1572868
  4.8 5.6 %copy-start.9 = (bf16[4,256,256]{2,1,0:T(8,128)(2,1)S(1)}, bf16[4,256,256]{2,1,0:T(8,128)(2,1)}, u32[]{:S(2)}) copy-start(bf16[4,256,256]{2,1,0:T(8,128)(2,1)} %param.12) | copy-start | bytes 1572868
  7.7 4.1 %copy-start.8 = (bf16[4,256,384]{2,1,0:T(8,128)(2,1)}, bf16[4,256,384]{2,1,0:T(8,128)(2,1)S(1)}, u32[]{:S(2)}) copy-start(bf16[4,256,384]{2,1,0:T(8,128)(2,1)S(1)} %fusion.11) | copy-start | bytes 2359300
  11.8 1.4 %copy-start.10 = (bf16[4,256,256]{2,1,0:T(8,128)(2,1)}, bf16[4,256,256]{2,1,0:T(8,128)(2,1)S(1)}, u32[]{:S(2)}) copy-start(bf16[4,256,256]{2,1,0:T(8,128)(2,1)S(1)} %fusion.16) | copy-start | bytes 1572868
  11.8 9.0 %copy-start.13 = (bf16[256,256]{1,0:T(8,128)(2,1)S(1)}, bf16[256,256]{1,0:T(8,128)(2,1)}, u32[]{:S(2)}) copy-start(bf16[256,256]{1,0:T(8,128)(2,1)} %param.18) | copy-start | bytes 393220
  11.8 9.1 %copy-start.14 = (bf16[256,256]{1,0:T(8,128)(2,1)S(1)}, bf16[256,256]{1,0:T(8,128)(2,1)}, u32[]{:S(2)}) copy-start(bf16[256,256]{1,0:T(8,128)(2,1)} %param.19) | copy-start | bytes 393220
  13.9 10.5 %collective-permute-start.1 = (bf16[4,64,256]{2,1,0:T(8,128)(2,1)}, bf16[4,64,256]{2,1,0:T(8,128)(2,1)}, u32[]{:S(2)}, u32[]{:S(2)}) collective-permute-start(bf16[4,64,256]{2,1,0:T(8,128)(2,1)} %get-tuple-element.33), channel_id=1, source_target_pairs={{0,8},{8,16},{16,24},{24,0},{1,9},{9,17},{17,25},{25,1},{2,10},{10... | collective-permute-start | bytes 393224 | tf_op jit(solution)/shard_map/ppermute | solution.py:97
  16.2 11.9 %collective-permute-start.2 = (bf16[4,64,256]{2,1,0:T(8,128)(2,1)}, bf16[4,64,256]{2,1,0:T(8,128)(2,1)}, u32[]{:S(2)}, u32[]{:S(2)}) collective-permute-start(bf16[4,64,256]{2,1,0:T(8,128)(2,1)} %get-tuple-element.32), channel_id=1, source_target_pairs={{0,16},{8,24},{16,0},{24,8},{1,17},{9,25},{17,1},{25,9},{2,18},{10... | collective-permute-start | bytes 393224 | tf_op jit(solution)/shard_map/ppermute | solution.py:97
  18.8 9.3 %collective-permute-start.3 = (bf16[4,64,256]{2,1,0:T(8,128)(2,1)S(1)}, bf16[4,64,256]{2,1,0:T(8,128)(2,1)}, u32[]{:S(2)}, u32[]{:S(2)}) collective-permute-start(bf16[4,64,256]{2,1,0:T(8,128)(2,1)S(1)} %get-tuple-element.31), channel_id=1, source_target_pairs={{0,24},{8,0},{16,8},{24,16},{1,25},{9,1},{17,9},{25,17},{2,26},{10... | collective-permute-start | bytes 393224 | tf_op jit(solution)/shard_map/ppermute | solution.py:97
  21.0 1.9 %copy-start.15 = (bf16[256,256]{1,0:T(8,128)(2,1)S(1)}, bf16[256,256]{1,0:T(8,128)(2,1)}, u32[]{:S(2)}) copy-start(bf16[256,256]{1,0:T(8,128)(2,1)} %param.20) | copy-start | bytes 393220
  21.7 2.6 %copy-start.20 = (s32[4]{0:T(128)S(1)}, s32[4]{0:T(128)}, u32[]{:S(2)}) copy-start(s32[4]{0:T(128)} %compare_select_fusion) | copy-start | bytes 52
  30.0 1.1 %copy-start.1 = (bf16[8,128,4,64]{1,3,2,0:T(8,128)(2,1)S(1)}, bf16[8,128,4,64]{1,3,2,0:T(8,128)(2,1)}, u32[]{:S(2)}) copy-start(bf16[8,128,4,64]{1,3,2,0:T(8,128)(2,1)} %copy.35) | copy-start | bytes 1572868
  37.6 2.6 %copy-start.3 = (f32[8,4,128,128]{3,2,1,0:T(8,128)S(1)}, f32[8,4,128,128]{3,2,1,0:T(8,128)}, u32[]{:S(2)}) copy-start(f32[8,4,128,128]{3,2,1,0:T(8,128)} %fusion.21) | copy-start | bytes 6291460
  37.6 2.9 %copy-start.21 = (f32[8,4,128,128]{2,3,1,0:T(8,128)S(1)}, f32[8,4,128,128]{2,3,1,0:T(8,128)}, u32[]{:S(2)}) copy-start(f32[8,4,128,128]{2,3,1,0:T(8,128)} %get-tuple-element.43) | copy-start | bytes 6291460
  37.6 2.9 %copy-start.22 = (f32[8,4,128]{2,1,0:T(4,128)S(1)}, f32[8,4,128]{2,1,0:T(4,128)}, u32[]{:S(2)}) copy-start(f32[8,4,128]{2,1,0:T(4,128)} %get-tuple-element.42) | copy-start | bytes 49156
  41.0 1.2 %copy-start.6 = (bf16[256,256]{0,1:T(8,128)(2,1)S(1)}, bf16[256,256]{0,1:T(8,128)(2,1)}, u32[]{:S(2)}) copy-start(bf16[256,256]{0,1:T(8,128)(2,1)} %copy.33) | copy-start | bytes 393220
  41.5 2.2 %copy-start.4 = (bf16[8,4,128,64]{2,3,1,0:T(8,128)(2,1)}, bf16[8,4,128,64]{2,3,1,0:T(8,128)(2,1)S(1)}, u32[]{:S(2)}) copy-start(bf16[8,4,128,64]{2,3,1,0:T(8,128)(2,1)S(1)} %convolution_convert_fusion.3) | copy-start | bytes 1572868
  44.4 8.7 %collective-permute-start.4 = (bf16[4,64,256]{2,1,0:T(8,128)(2,1)S(1)}, bf16[4,64,256]{2,1,0:T(8,128)(2,1)}, u32[]{:S(2)}, u32[]{:S(2)}) collective-permute-start(bf16[4,64,256]{2,1,0:T(8,128)(2,1)S(1)} %bitcast.221), channel_id=1, source_target_pairs={{0,8},{8,16},{16,24},{24,0},{1,9},{9,17},{17,25},{25,1},{2,10},{10... | collective-permute-start | bytes 393224 | tf_op jit(solution)/shard_map/ppermute | solution.py:97
  47.8 9.9 %collective-permute-start.5 = (bf16[4,64,256]{2,1,0:T(8,128)(2,1)S(1)}, bf16[4,64,256]{2,1,0:T(8,128)(2,1)S(1)}, u32[]{:S(2)}, u32[]{:S(2)}) collective-permute-start(bf16[4,64,256]{2,1,0:T(8,128)(2,1)S(1)} %bitcast.222), channel_id=1, source_target_pairs={{0,16},{8,24},{16,0},{24,8},{1,17},{9,25},{17,1},{25,9},{2,18},{10... | collective-permute-start | bytes 393224 | tf_op jit(solution)/shard_map/ppermute | solution.py:97
  49.5 8.3 %collective-permute-start.6 = (bf16[4,64,256]{2,1,0:T(8,128)(2,1)S(1)}, bf16[4,64,256]{2,1,0:T(8,128)(2,1)}, u32[]{:S(2)}, u32[]{:S(2)}) collective-permute-start(bf16[4,64,256]{2,1,0:T(8,128)(2,1)S(1)} %bitcast.223), channel_id=1, source_target_pairs={{0,24},{8,0},{16,8},{24,16},{1,25},{9,1},{17,9},{25,17},{2,26},{10... | collective-permute-start | bytes 393224 | tf_op jit(solution)/shard_map/ppermute | solution.py:97
  51.1 1.1 %copy-start.5 = (bf16[8,4,128,64]{2,3,1,0:T(8,128)(2,1)S(1)}, bf16[8,4,128,64]{2,3,1,0:T(8,128)(2,1)}, u32[]{:S(2)}) copy-start(bf16[8,4,128,64]{2,3,1,0:T(8,128)(2,1)} %copy-done.4) | copy-start | bytes 1572868
  52.2 6.1 %copy-start.12 = (bf16[64,4,256]{2,0,1:T(8,128)(2,1)S(1)}, bf16[64,4,256]{2,0,1:T(8,128)(2,1)}, u32[]{:S(2)}) copy-start(bf16[64,4,256]{2,0,1:T(8,128)(2,1)} %copy.81) | copy-start | bytes 393220
  57.6 0.7 copy-start.16
  58.3 2.0 %copy-start.7 = (f32[4,256,256]{2,1,0:T(8,128)S(1)}, f32[4,256,256]{2,1,0:T(8,128)}, u32[]{:S(2)}) copy-start(f32[4,256,256]{2,1,0:T(8,128)} %get-tuple-element.41) | copy-start | bytes 3145732
  60.1 1.0 copy-start.11
  62.5 2.3 %collective-permute-start.7 = (f32[131072]{0:T(1024)}, f32[131072]{0:T(1024)}, u32[]{:S(2)}, u32[]{:S(2)}) collective-permute-start(f32[131072]{0:T(1024)} %broadcast_select_fusion.3), channel_id=1, source_target_pairs={{0,1},{1,0},{2,3},{3,2},{4,5},{5,4},{6,7},{7,6},{8,9},{9,8},{10,11... | collective-permute-start | bytes 1572872 | tf_op jit(solution)/shard_map/ppermute | solution.py:33
  66.6 8.1 %collective-permute-start.10 = (f32[32768]{0:T(1024)S(1)}, f32[32768]{0:T(1024)S(1)}, u32[]{:S(2)}, u32[]{:S(2)}) collective-permute-start(f32[32768]{0:T(1024)S(1)} %bitcast.232), channel_id=1, source_target_pairs={{0,6},{1,7},{2,0},{3,1},{4,2},{5,3},{6,4},{7,5},{8,14},{9,15},{10,... | collective-permute-start | bytes 393224 | tf_op jit(solution)/shard_map/ppermute | solution.py:37
  67.9 8.1 %collective-permute-start.8 = (f32[32768]{0:T(1024)S(1)}, f32[32768]{0:T(1024)S(1)}, u32[]{:S(2)}, u32[]{:S(2)}) collective-permute-start(f32[32768]{0:T(1024)S(1)} %bitcast.231), channel_id=1, source_target_pairs={{0,2},{1,3},{2,4},{3,5},{4,6},{5,7},{6,0},{7,1},{8,10},{9,11},{10,... | collective-permute-start | bytes 393224 | tf_op jit(solution)/shard_map/ppermute | solution.py:37
  68.6 13.5 %copy-start.17 = (s32[4,128]{1,0:T(4,128)S(1)}, s32[4,128]{1,0:T(4,128)}, u32[]{:S(2)}) copy-start(s32[4,128]{1,0:T(4,128)} %param.15) | copy-start | bytes 6148
  68.6 13.5 %copy-start.19 = (pred[4,128]{1,0:T(4,128)(4,1)S(1)}, pred[4,128]{1,0:T(4,128)(4,1)}, u32[]{:S(2)}) copy-start(pred[4,128]{1,0:T(4,128)(4,1)} %copy-done.18) | copy-start | bytes 1540
  68.6 8.0 %collective-permute-start.9 = (f32[32768]{0:T(1024)S(1)}, f32[32768]{0:T(1024)S(1)}, u32[]{:S(2)}, u32[]{:S(2)}) collective-permute-start(f32[32768]{0:T(1024)S(1)} %bitcast.230), channel_id=1, source_target_pairs={{0,4},{1,5},{2,6},{3,7},{4,0},{5,1},{6,2},{7,3},{8,12},{9,13},{10,... | collective-permute-start | bytes 393224 | tf_op jit(solution)/shard_map/ppermute | solution.py:37
  73.0 9.1 %collective-permute-start.14 = (bf16[4,128,256]{2,1,0:T(8,128)(2,1)}, bf16[4,128,256]{2,1,0:T(8,128)(2,1)}, u32[]{:S(2)}, u32[]{:S(2)}) collective-permute-start(bf16[4,128,256]{2,1,0:T(8,128)(2,1)} %slice.101), channel_id=1, source_target_pairs={{0,7},{1,0},{2,1},{3,2},{4,3},{5,4},{6,5},{7,6},{8,15},{9,8},{10,9... | collective-permute-start | bytes 786440 | tf_op jit(solution)/shard_map/ppermute | solution.py:12
  76.9 7.5 %collective-permute-start.11 = (f32[8192]{0:T(1024)S(1)}, f32[8192]{0:T(1024)S(1)}, u32[]{:S(2)}, u32[]{:S(2)}) collective-permute-start(f32[8192]{0:T(1024)S(1)} %bitcast.238), channel_id=1, source_target_pairs={{0,8},{8,16},{16,24},{24,0},{1,9},{9,17},{17,25},{25,1},{2,10},{10... | collective-permute-start | bytes 98312 | tf_op jit(solution)/shard_map/ppermute | solution.py:37
  79.7 4.8 %collective-permute-start.12 = (f32[8192]{0:T(1024)S(1)}, f32[8192]{0:T(1024)S(1)}, u32[]{:S(2)}, u32[]{:S(2)}) collective-permute-start(f32[8192]{0:T(1024)S(1)} %bitcast.237), channel_id=1, source_target_pairs={{0,16},{8,24},{16,0},{24,8},{1,17},{9,25},{17,1},{25,9},{2,18},{10... | collective-permute-start | bytes 98312 | tf_op jit(solution)/shard_map/ppermute | solution.py:37
  81.9 3.9 %collective-permute-start.13 = (f32[8192]{0:T(1024)S(1)}, f32[8192]{0:T(1024)S(1)}, u32[]{:S(2)}, u32[]{:S(2)}) collective-permute-start(f32[8192]{0:T(1024)S(1)} %bitcast.236), channel_id=1, source_target_pairs={{0,24},{8,0},{16,8},{24,16},{1,25},{9,1},{17,9},{25,17},{2,26},{10... | collective-permute-start | bytes 98312 | tf_op jit(solution)/shard_map/ppermute | solution.py:37
  85.8 5.8 %collective-permute-start.15 = (f32[8192]{0:T(1024)S(1)}, f32[8192]{0:T(1024)S(1)}, u32[]{:S(2)}, u32[]{:S(2)}) collective-permute-start(f32[8192]{0:T(1024)S(1)} %add_add_fusion.1), channel_id=1, source_target_pairs={{0,8},{8,16},{16,24},{24,0},{1,9},{9,17},{17,25},{25,1},{2,10},{10... | collective-permute-start | bytes 98312 | tf_op jit(solution)/shard_map/ppermute | solution.py:49
  86.2 5.4 %collective-permute-start.16 = (f32[8192]{0:T(1024)S(1)}, f32[8192]{0:T(1024)S(1)}, u32[]{:S(2)}, u32[]{:S(2)}) collective-permute-start(f32[8192]{0:T(1024)S(1)} %add_add_fusion.1), channel_id=1, source_target_pairs={{0,16},{8,24},{16,0},{24,8},{1,17},{9,25},{17,1},{25,9},{2,18},{10... | collective-permute-start | bytes 98312 | tf_op jit(solution)/shard_map/ppermute | solution.py:49
  88.6 3.9 %collective-permute-start.17 = (f32[8192]{0:T(1024)S(1)}, f32[8192]{0:T(1024)S(1)}, u32[]{:S(2)}, u32[]{:S(2)}) collective-permute-start(f32[8192]{0:T(1024)S(1)} %add_add_fusion.1), channel_id=1, source_target_pairs={{0,24},{8,0},{16,8},{24,16},{1,25},{9,1},{17,9},{25,17},{2,26},{10... | collective-permute-start | bytes 98312 | tf_op jit(solution)/shard_map/ppermute | solution.py:49
  93.3 6.0 %collective-permute-start.18 = (f32[32768]{0:T(1024)S(1)}, f32[32768]{0:T(1024)S(1)}, u32[]{:S(2)}, u32[]{:S(2)}) collective-permute-start(f32[32768]{0:T(1024)S(1)} %bitcast.224), channel_id=1, source_target_pairs={{0,2},{1,3},{2,4},{3,5},{4,6},{5,7},{6,0},{7,1},{8,10},{9,11},{10,... | collective-permute-start | bytes 393224 | tf_op jit(solution)/shard_map/ppermute | solution.py:49
  94.4 6.3 %collective-permute-start.19 = (f32[32768]{0:T(1024)S(1)}, f32[32768]{0:T(1024)S(1)}, u32[]{:S(2)}, u32[]{:S(2)}) collective-permute-start(f32[32768]{0:T(1024)S(1)} %bitcast.225), channel_id=1, source_target_pairs={{0,4},{1,5},{2,6},{3,7},{4,0},{5,1},{6,2},{7,3},{8,12},{9,13},{10,... | collective-permute-start | bytes 393224 | tf_op jit(solution)/shard_map/ppermute | solution.py:49
  95.0 5.8 %collective-permute-start.20 = (f32[32768]{0:T(1024)S(1)}, f32[32768]{0:T(1024)S(1)}, u32[]{:S(2)}, u32[]{:S(2)}) collective-permute-start(f32[32768]{0:T(1024)S(1)} %bitcast.226), channel_id=1, source_target_pairs={{0,6},{1,7},{2,0},{3,1},{4,2},{5,3},{6,4},{7,5},{8,14},{9,15},{10,... | collective-permute-start | bytes 393224 | tf_op jit(solution)/shard_map/ppermute | solution.py:49
  102.3 2.0 %collective-permute-start.21 = (f32[131072]{0:T(1024)S(1)}, f32[131072]{0:T(1024)S(1)}, u32[]{:S(2)}, u32[]{:S(2)}) collective-permute-start(f32[131072]{0:T(1024)S(1)} %bitcast.217), channel_id=1, source_target_pairs={{0,1},{1,0},{2,3},{3,2},{4,5},{5,4},{6,7},{7,6},{8,9},{9,8},{10,11... | collective-permute-start | bytes 1572872 | tf_op jit(solution)/shard_map/ppermute | solution.py:44

commit v16 on v15

--- a/solution.py
+++ b/solution.py
@@ -67,13 +67,15 @@
         total *= size
     if not all(_power_of_two(size) for size in sizes) or flat.shape[0] % total:
         return lax.psum(tuple(values), axes), companion
-    steps = []
+    per_axis = []
     for axis, size in zip(axes, sizes):
-        stride = 1
+        stride, own = 1, []
         for group in _factors(size):
             if group > 1:
-                steps.append((axis, stride, group))
+                own.append((axis, stride, group))
             stride *= group
+        per_axis.append(own)
+    steps = per_axis[0][:1] + [step for own in per_axis[1:] for step in own] + per_axis[0][1:]
     for axis, stride, group in steps:
         flat = _scatter_step(flat, axis, stride, group)
     flat, companion = lax.optimization_barrier((flat, companion))

time: 106 us -> 113 us (1.066)
  waiting for transfers between devices: 22.3 us -> 29.5 us
    ppermute x6, waiting for transfers between devices: 3.41 us -> 7.68 us  [_scatter_step(): lax.ppermute(send, axis, _group_pairs(axis, stride, group, shift))]
    ppermute x6, waiting for transfers between devices: 5.55 us -> 8.5 us  [_gather_step(): lax.ppermute(flat, axis, _group_pairs(axis, stride, group, shift))]
  transfers between devices with their start and end apart: 22 -> 22, of which waited for: 16 -> 14; matrix products, arithmetic and copies ran while one was open for 17% -> 16% of each run, Pallas kernels for 0% -> 0%
where the time goes in v16:
time: 113 us; the launch traced here: 112 us
  starting transfers between devices  31.1 us (28%)
  waiting for transfers between devices  29.5 us (26%)
  matrix products  26.4 us (23%)
  local copies, waits for them, and re-layouts  14.5 us (13%)
  other arithmetic  9.08 us (8%)
  between operations  1.42 us (1%)
    ppermute x6, starting transfers between devices, exchange(): lax.ppermute(send, axis, [(i, (i + shift) % count) for i in range(count)])  12.3 us
    ppermute x6, starting transfers between devices, _scatter_step(): lax.ppermute(send, axis, _group_pairs(axis, stride, group, shift))  9.81 us
    dot_general x12, matrix products, contract(): return jnp.einsum(spec, left, right, preferred_element_type=jnp.float32)  9.44 us
    ppermute x6, waiting for transfers between devices, _gather_step(): lax.ppermute(flat, axis, _group_pairs(axis, stride, group, shift))  8.5 us
    ppermute x6, waiting for transfers between devices, exchange(): lax.ppermute(send, axis, [(i, (i + shift) % count) for i in range(count)])  8.45 us
    ppermute x6, starting transfers between devices, _gather_step(): lax.ppermute(flat, axis, _group_pairs(axis, stride, group, shift))  7.84 us
    ppermute x6, waiting for transfers between devices, _scatter_step(): lax.ppermute(send, axis, _group_pairs(axis, stride, group, shift))  7.68 us
    sub x1, matrix products, attend_blocked(): exponent = jnp.exp(scores - highest)  3.51 us
  transfers between devices with their start and end apart: 22, of which 14 were waited for; matrix products, arithmetic and copies ran while one was open for 16% of the time, Pallas kernels for 0%

profile of v16, /device:TPU:0, one launch (start us, length us, event | category | flops | bytes accessed | tf_op | source)
XLA Modules:
  0.0 112.1 jit_solution(4689770977379688722)
XLA Ops:
  0.6 0.8 iota_compare_fusion.10
  1.4 1.4 %convolution_convert_fusion.6 = bf16[4,128,256]{2,1,0:T(8,128)(2,1)S(1)} fusion(bf16[4,256,256]{2,1,0:T(8,128)(2,1)} %param.12, s32[4,128]{1,0:T(4,128)} %param.15, pred[4,128]{1,0:T(4,128)(4,1)S(1)} %iota_compare_fusion.10), kind=kOutput, calls=%fused_computation.47 | convolution fusion | flops 67502080 | bytes 788992 | tf_op jit(solution)/shard_map/dsn,dnh->dsh/dot_general | solution.py:289
  3.3 1.4 %fusion.3 = f32[1,4,256]{2,0,1:T(1,128)S(1)} fusion(s32[4,1024]{1,0:T(4,128)} %param.14), kind=kOutput, calls=%fused_computation.9 | convolution fusion | flops 3145728 | bytes 20480 | tf_op jit(solution)/shard_map/der,e->dr/dot_general | solution.py:300
  4.8 2.9 %fusion.11 = bf16[4,256,384]{2,1,0:T(8,128)(2,1)S(1)} fusion(s32[4,1024]{1,0:T(4,128)} %param.13, s32[4,1024]{1,0:T(4,128)} %param.14), kind=kOutput, calls=%fused_computation.21 | convolution fusion | flops 808321024 | bytes 819200 | tf_op jit(solution)/shard_map/der,des->drs/dot_general | solution.py:297
  7.8 0.8 compare_and_fusion
  8.7 1.7 %collective-permute-done = bf16[4,128,256]{2,1,0:T(8,128)(2,1)} collective-permute-done((bf16[4,128,256]{2,1,0:T(8,128)(2,1)S(1)}, bf16[4,128,256]{2,1,0:T(8,128)(2,1)}, u32[]{:S(2)}, u32[]{:S(2)}) %collective-permute-start) | collective-permute-done | bytes 262176 | tf_op jit(solution)/shard_map/ppermute | solution.py:12
  10.4 1.4 %fusion.16 = bf16[4,256,256]{2,1,0:T(8,128)(2,1)S(1)} fusion(bf16[4,256,384]{2,1,0:T(8,128)(2,1)S(1)} %fusion.11, bf16[4,256,256]{2,1,0:T(8,128)(2,1)S(1)} %copy-done.9, bf16[4,128,256]{2,1,0:T(8,128)(2,1)} %collective-permute-done, f32[4,256]{1,0:T(4,128)S(1)} %fusion.46), kind=kOutput, calls=%fused_computation.35 | convolution fusion | flops 203948032 | bytes 2101248 | tf_op jit(solution)/shard_map/drs,dsh->drh/dot_general | solution.py:310
  11.8 1.3 %fusion.22 = (bf16[4,256,256]{2,1,0:T(8,128)(2,1)S(1)}, f32[4,256,256]{2,1,0:T(8,128)}) fusion(bf16[4,256,256]{2,1,0:T(8,128)(2,1)S(1)} %copy-done.9, bf16[4,256,256]{2,1,0:T(8,128)(2,1)S(1)} %fusion.16, bf16[256,256]{1,0:T(8,128)(2,1)S(1)} %copy-done), kind=kOutput, calls=%fused_computation.52 | convolution fusion | flops 136052736 | bytes 2752512 | tf_op jit(solution)/shard_map/drh,hk->drk/dot_general | solution.py:312
  13.2 0.7 dynamic-slice_bitcast_fusion
  13.9 2.3 %collective-permute-start.1 = (bf16[4,64,256]{2,1,0:T(8,128)(2,1)}, bf16[4,64,256]{2,1,0:T(8,128)(2,1)}, u32[]{:S(2)}, u32[]{:S(2)}) collective-permute-start(bf16[4,64,256]{2,1,0:T(8,128)(2,1)} %get-tuple-element.33), channel_id=1, source_target_pairs={{0,8},{8,16},{16,24},{24,0},{1,9},{9,17},{17,25},{25,1},{2,10},{10... | collective-permute-start | bytes 393224 | tf_op jit(solution)/shard_map/ppermute | solution.py:99
  16.2 2.6 %collective-permute-start.2 = (bf16[4,64,256]{2,1,0:T(8,128)(2,1)}, bf16[4,64,256]{2,1,0:T(8,128)(2,1)}, u32[]{:S(2)}, u32[]{:S(2)}) collective-permute-start(bf16[4,64,256]{2,1,0:T(8,128)(2,1)} %get-tuple-element.32), channel_id=1, source_target_pairs={{0,16},{8,24},{16,0},{24,8},{1,17},{9,25},{17,1},{25,9},{2,18},{10... | collective-permute-start | bytes 393224 | tf_op jit(solution)/shard_map/ppermute | solution.py:99
  18.8 1.3 %collective-permute-start.3 = (bf16[4,64,256]{2,1,0:T(8,128)(2,1)S(1)}, bf16[4,64,256]{2,1,0:T(8,128)(2,1)}, u32[]{:S(2)}, u32[]{:S(2)}) collective-permute-start(bf16[4,64,256]{2,1,0:T(8,128)(2,1)S(1)} %get-tuple-element.31), channel_id=1, source_target_pairs={{0,24},{8,0},{16,8},{24,16},{1,25},{9,1},{17,9},{25,17},{2,26},{10... | collective-permute-start | bytes 393224 | tf_op jit(solution)/shard_map/ppermute | solution.py:99
  21.7 1.2 %copy.35 = bf16[8,128,4,64]{1,3,2,0:T(8,128)(2,1)} copy(bf16[8,128,4,64]{3,2,1,0:T(4,128)(2,1)S(1)} %reshape_reshape.12) | data formatting | bytes 1048576 | tf_op jit(solution)/shard_map/reshape;reshape | solution.py:234
  22.9 0.8 copy.33
  24.4 3.8 %collective-permute-done.2 = bf16[4,64,256]{2,1,0:T(8,128)(2,1)} collective-permute-done((bf16[4,64,256]{2,1,0:T(8,128)(2,1)}, bf16[4,64,256]{2,1,0:T(8,128)(2,1)}, u32[]{:S(2)}, u32[]{:S(2)}) %collective-permute-start.2) | collective-permute-done | bytes 131104 | tf_op jit(solution)/shard_map/ppermute | solution.py:99
  28.1 1.1 pad_maximum_fusion
  31.1 3.0 %fusion.21 = f32[8,4,128,128]{3,2,1,0:T(8,128)} fusion(bf16[8,128,4,64]{1,3,2,0:T(8,128)(2,1)S(1)} %copy-done.1, bf16[8,128,256,1]{2,1,3,0:T(8,128)(2,1)S(1)} %bitcast.203, bf16[256,4,64,1]{0,2,1,3:T(8,128)(2,1)} %bitcast.214), kind=kOutput, calls=%fused_computation.46 | convolution fusion | flops 201588736 | bytes 3276800 | tf_op jit(solution)/shard_map/gihd,ghjd->ghij/dot_general | solution.py:229
  34.0 3.5 %fusion.60 = (f32[8,4,128]{2,1,0:T(4,128)}, f32[8,4,128,128]{2,3,1,0:T(8,128)}) fusion(pred[128,128]{0,1:T(8,128)(4,1)} %compare_and_fusion, bf16[8,4,128,64]{2,3,1,0:T(8,128)(2,1)S(1)} %fusion.18, bf16[8,4,128,64]{2,3,1,0:T(8,128)(2,1)S(1)} %fusion.19), kind=kOutput, calls=%fused_computation.176 | convolution fusion | flops 69206144 | bytes 3178496 | tf_op jit(solution)/shard_map/sub | solution.py:242
  37.5 2.6 %convolution_convert_fusion.4 = bf16[8,4,128,64]{2,3,1,0:T(8,128)(2,1)S(1)} fusion(bf16[8,128,4,64]{1,3,2,0:T(8,128)(2,1)S(1)} %copy-done.1, f32[8,4,128,128]{2,3,1,0:T(8,128)} %get-tuple-element.43, f32[8,4,128]{2,1,0:T(4,128)} %get-tuple-element.42), kind=kOutput, calls=%fused_computation.40 | convolution fusion | flops 68419584 | bytes 3162112 | tf_op jit(solution)/shard_map/ghij,gihd->ghjd/dot_general | solution.py:229
  41.5 0.8 convolution_convert_fusion.5
  44.4 3.3 %collective-permute-start.4 = (bf16[4,64,256]{2,1,0:T(8,128)(2,1)S(1)}, bf16[4,64,256]{2,1,0:T(8,128)(2,1)}, u32[]{:S(2)}, u32[]{:S(2)}) collective-permute-start(bf16[4,64,256]{2,1,0:T(8,128)(2,1)S(1)} %bitcast.221), channel_id=1, source_target_pairs={{0,8},{8,16},{16,24},{24,0},{1,9},{9,17},{17,25},{25,1},{2,10},{10... | collective-permute-start | bytes 393224 | tf_op jit(solution)/shard_map/ppermute | solution.py:99
  47.7 1.7 %collective-permute-start.5 = (bf16[4,64,256]{2,1,0:T(8,128)(2,1)S(1)}, bf16[4,64,256]{2,1,0:T(8,128)(2,1)S(1)}, u32[]{:S(2)}, u32[]{:S(2)}) collective-permute-start(bf16[4,64,256]{2,1,0:T(8,128)(2,1)S(1)} %bitcast.222), channel_id=1, source_target_pairs={{0,16},{8,24},{16,0},{24,8},{1,17},{9,25},{17,1},{25,9},{2,18},{10... | collective-permute-start | bytes 393224 | tf_op jit(solution)/shard_map/ppermute | solution.py:99
  49.5 1.0 collective-permute-start.6
  53.1 4.4 %collective-permute-done.5 = bf16[4,64,256]{2,1,0:T(8,128)(2,1)S(1)} collective-permute-done((bf16[4,64,256]{2,1,0:T(8,128)(2,1)S(1)}, bf16[4,64,256]{2,1,0:T(8,128)(2,1)S(1)}, u32[]{:S(2)}, u32[]{:S(2)}) %collective-permute-start.5) | collective-permute-done | bytes 131104 | tf_op jit(solution)/shard_map/ppermute | solution.py:99
  58.2 1.2 %pad_maximum_fusion.1 = bf16[4,4,64,256]{3,2,1,0:T(8,128)(2,1)S(1)} fusion(bf16[1,4,64,256]{3,2,1,0:T(8,128)(2,1)} %bitcast.51, bf16[1,4,64,256]{3,2,1,0:T(8,128)(2,1)} %bitcast.229, bf16[1,4,64,256]{3,2,1,0:T(8,128)(2,1)} %bitcast.47, bf16[1,4,64,256]{3,2,1,0:T(8,128)(2,1)S(1)} %bitcast.219), kind=kLoop, calls=%fused_computation.70 | loop fusion | flops 786432 | bytes 1048576 | tf_op jit(solution)/shard_map/stack | solution.py:101
  61.6 0.9 broadcast_select_fusion.3
  62.8 1.9 %collective-permute-done.7 = f32[131072]{0:T(1024)} collective-permute-done((f32[131072]{0:T(1024)}, f32[131072]{0:T(1024)}, u32[]{:S(2)}, u32[]{:S(2)}) %collective-permute-start.7) | collective-permute-done | bytes 524320 | tf_op jit(solution)/shard_map/ppermute | solution.py:33
  64.7 1.1 select_add_fusion
  66.5 4.7 %collective-permute-start.10 = (f32[32768]{0:T(1024)S(1)}, f32[32768]{0:T(1024)S(1)}, u32[]{:S(2)}, u32[]{:S(2)}) collective-permute-start(f32[32768]{0:T(1024)S(1)} %bitcast.232), channel_id=1, source_target_pairs={{0,24},{8,0},{16,8},{24,16},{1,25},{9,1},{17,9},{25,17},{2,26},{10... | collective-permute-start | bytes 393224 | tf_op jit(solution)/shard_map/ppermute | solution.py:37
  71.8 2.1 %fusion.61 = f32[4,384,256]{2,1,0:T(8,128)S(1)} fusion(bf16[4,256,384]{2,1,0:T(8,128)(2,1)} %copy-done.8, f32[4,256,256]{2,1,0:T(8,128)S(1)} %convolution_multiply_fusion), kind=kOutput, calls=%fused_computation.177 | convolution fusion | flops 1207959552 | bytes 3407872 | tf_op jit(solution)/shard_map/drs,drh->dsh/dot_general | solution.py:332
  73.9 0.7 slice.101
  75.3 4.1 %collective-permute-done.8 = f32[32768]{0:T(1024)S(1)} collective-permute-done((f32[32768]{0:T(1024)S(1)}, f32[32768]{0:T(1024)S(1)}, u32[]{:S(2)}, u32[]{:S(2)}) %collective-permute-start.8) | collective-permute-done | bytes 131104 | tf_op jit(solution)/shard_map/ppermute | solution.py:37
  79.4 3.5 %collective-permute-done.9 = f32[32768]{0:T(1024)S(1)} collective-permute-done((f32[32768]{0:T(1024)S(1)}, f32[32768]{0:T(1024)S(1)}, u32[]{:S(2)}, u32[]{:S(2)}) %collective-permute-start.9) | collective-permute-done | bytes 131104 | tf_op jit(solution)/shard_map/ppermute | solution.py:37
  83.2 1.8 %collective-permute-start.11 = (f32[8192]{0:T(1024)S(1)}, f32[8192]{0:T(1024)S(1)}, u32[]{:S(2)}, u32[]{:S(2)}) collective-permute-start(f32[8192]{0:T(1024)S(1)} %bitcast.238), channel_id=1, source_target_pairs={{0,2},{1,3},{2,4},{3,5},{4,6},{5,7},{6,0},{7,1},{8,10},{9,11},{10,... | collective-permute-start | bytes 98312 | tf_op jit(solution)/shard_map/ppermute | solution.py:37
  85.2 2.4 %collective-permute-start.13 = (f32[8192]{0:T(1024)S(1)}, f32[8192]{0:T(1024)S(1)}, u32[]{:S(2)}, u32[]{:S(2)}) collective-permute-start(f32[8192]{0:T(1024)S(1)} %bitcast.236), channel_id=1, source_target_pairs={{0,6},{1,7},{2,0},{3,1},{4,2},{5,3},{6,4},{7,5},{8,14},{9,15},{10,... | collective-permute-start | bytes 98312 | tf_op jit(solution)/shard_map/ppermute | solution.py:37
  87.7 2.2 %convolution_add_fusion.1 = f32[4,256,256]{2,1,0:T(8,128)} fusion(bf16[4,128,256]{2,1,0:T(8,128)(2,1)} %collective-permute-done.14, f32[4,256,256]{2,1,0:T(8,128)S(1)} %convolution_multiply_fusion, f32[4,384,256]{2,1,0:T(8,128)S(1)} %fusion.61, s32[4,128]{1,0:T(4,128)S(1)} %copy-done.17, pred[4,128]{1,0:T(4,128)(4,1)S(1)} %copy-done.19, ...), kind=kOutput, calls=%fused_computation.27 | convolution fusion | flops 70254592 | bytes 3934720 | tf_op jit(solution)/shard_map/dsn,dsh->dnh/dot_general | solution.py:342
  89.9 1.7 %collective-permute-start.15 = (f32[8192]{0:T(1024)S(1)}, f32[8192]{0:T(1024)S(1)}, u32[]{:S(2)}, u32[]{:S(2)}) collective-permute-start(f32[8192]{0:T(1024)S(1)} %add_add_fusion.1), channel_id=1, source_target_pairs={{0,2},{1,3},{2,4},{3,5},{4,6},{5,7},{6,0},{7,1},{8,10},{9,11},{10,... | collective-permute-start | bytes 98312 | tf_op jit(solution)/shard_map/ppermute | solution.py:49
  91.6 1.5 %collective-permute-start.16 = (f32[8192]{0:T(1024)S(1)}, f32[8192]{0:T(1024)S(1)}, u32[]{:S(2)}, u32[]{:S(2)}) collective-permute-start(f32[8192]{0:T(1024)S(1)} %add_add_fusion.1), channel_id=1, source_target_pairs={{0,4},{1,5},{2,6},{3,7},{4,0},{5,1},{6,2},{7,3},{8,12},{9,13},{10,... | collective-permute-start | bytes 98312 | tf_op jit(solution)/shard_map/ppermute | solution.py:49
  93.1 0.8 collective-permute-start.17
  93.9 0.9 collective-permute-done.15
  95.5 1.5 %collective-permute-done.17 = f32[8192]{0:T(1024)S(1)} collective-permute-done((f32[8192]{0:T(1024)S(1)}, f32[8192]{0:T(1024)S(1)}, u32[]{:S(2)}, u32[]{:S(2)}) %collective-permute-start.17) | collective-permute-done | bytes 32800 | tf_op jit(solution)/shard_map/ppermute | solution.py:49
  98.0 2.9 %collective-permute-start.19 = (f32[32768]{0:T(1024)S(1)}, f32[32768]{0:T(1024)S(1)}, u32[]{:S(2)}, u32[]{:S(2)}) collective-permute-start(f32[32768]{0:T(1024)S(1)} %bitcast.225), channel_id=1, source_target_pairs={{0,16},{8,24},{16,0},{24,8},{1,17},{9,25},{17,1},{25,9},{2,18},{10... | collective-permute-start | bytes 393224 | tf_op jit(solution)/shard_map/ppermute | solution.py:49
  100.9 0.9 collective-permute-start.20
  102.0 2.9 %collective-permute-done.18 = f32[32768]{0:T(1024)S(1)} collective-permute-done((f32[32768]{0:T(1024)S(1)}, f32[32768]{0:T(1024)S(1)}, u32[]{:S(2)}, u32[]{:S(2)}) %collective-permute-start.18) | collective-permute-done | bytes 131104 | tf_op jit(solution)/shard_map/ppermute | solution.py:49
  104.9 2.5 %collective-permute-done.19 = f32[32768]{0:T(1024)S(1)} collective-permute-done((f32[32768]{0:T(1024)S(1)}, f32[32768]{0:T(1024)S(1)}, u32[]{:S(2)}, u32[]{:S(2)}) %collective-permute-start.19) | collective-permute-done | bytes 131104 | tf_op jit(solution)/shard_map/ppermute | solution.py:49
  107.8 0.8 gather_fusion.1
  109.5 1.3 %collective-permute-done.21 = f32[131072]{0:T(1024)S(1)} collective-permute-done((f32[131072]{0:T(1024)S(1)}, f32[131072]{0:T(1024)S(1)}, u32[]{:S(2)}, u32[]{:S(2)}) %collective-permute-start.21) | collective-permute-done | bytes 524320 | tf_op jit(solution)/shard_map/ppermute | solution.py:44
  111.1 1.0 fusion.59
  (137 shorter events, 19.4 us)
Async XLA Ops:
  0.6 11.2 %copy-start = (bf16[256,256]{1,0:T(8,128)(2,1)S(1)}, bf16[256,256]{1,0:T(8,128)(2,1)}, u32[]{:S(2)}) copy-start(bf16[256,256]{1,0:T(8,128)(2,1)} %param.17) | copy-start | bytes 393220
  1.4 1.9 %copy-start.18 = (pred[4,128]{1,0:T(4,128)(4,1)}, pred[4,128]{1,0:T(4,128)(4,1)S(1)}, u32[]{:S(2)}) copy-start(pred[4,128]{1,0:T(4,128)(4,1)S(1)} %iota_compare_fusion.10) | copy-start | bytes 1540
  2.8 7.5 %collective-permute-start = (bf16[4,128,256]{2,1,0:T(8,128)(2,1)S(1)}, bf16[4,128,256]{2,1,0:T(8,128)(2,1)}, u32[]{:S(2)}, u32[]{:S(2)}) collective-permute-start(bf16[4,128,256]{2,1,0:T(8,128)(2,1)S(1)} %convolution_convert_fusion.6), channel_id=1, source_target_pairs={{0,1},{1,2},{2,3},{3,4},{4,5},{5,6},{6,7},{7,0},{8,9},{9,10},{10,1... | collective-permute-start | bytes 786440 | tf_op jit(solution)/shard_map/ppermute | solution.py:12
  4.8 3.8 %copy-start.2 = (bf16[16,1,1,64,256]{4,3,2,1,0:T(8,128)(2,1)S(1)}, bf16[16,1,1,64,256]{4,3,2,1,0:T(8,128)(2,1)}, u32[]{:S(2)}) copy-start(bf16[16,1,1,64,256]{4,3,2,1,0:T(8,128)(2,1)} %param.21) | copy-start | bytes 1572868
  4.8 5.6 %copy-start.9 = (bf16[4,256,256]{2,1,0:T(8,128)(2,1)S(1)}, bf16[4,256,256]{2,1,0:T(8,128)(2,1)}, u32[]{:S(2)}) copy-start(bf16[4,256,256]{2,1,0:T(8,128)(2,1)} %param.12) | copy-start | bytes 1572868
  7.7 4.1 %copy-start.8 = (bf16[4,256,384]{2,1,0:T(8,128)(2,1)}, bf16[4,256,384]{2,1,0:T(8,128)(2,1)S(1)}, u32[]{:S(2)}) copy-start(bf16[4,256,384]{2,1,0:T(8,128)(2,1)S(1)} %fusion.11) | copy-start | bytes 2359300
  11.8 1.4 %copy-start.10 = (bf16[4,256,256]{2,1,0:T(8,128)(2,1)}, bf16[4,256,256]{2,1,0:T(8,128)(2,1)S(1)}, u32[]{:S(2)}) copy-start(bf16[4,256,256]{2,1,0:T(8,128)(2,1)S(1)} %fusion.16) | copy-start | bytes 1572868
  11.8 9.0 %copy-start.13 = (bf16[256,256]{1,0:T(8,128)(2,1)S(1)}, bf16[256,256]{1,0:T(8,128)(2,1)}, u32[]{:S(2)}) copy-start(bf16[256,256]{1,0:T(8,128)(2,1)} %param.18) | copy-start | bytes 393220
  11.8 9.1 %copy-start.14 = (bf16[256,256]{1,0:T(8,128)(2,1)S(1)}, bf16[256,256]{1,0:T(8,128)(2,1)}, u32[]{:S(2)}) copy-start(bf16[256,256]{1,0:T(8,128)(2,1)} %param.19) | copy-start | bytes 393220
  13.9 10.5 %collective-permute-start.1 = (bf16[4,64,256]{2,1,0:T(8,128)(2,1)}, bf16[4,64,256]{2,1,0:T(8,128)(2,1)}, u32[]{:S(2)}, u32[]{:S(2)}) collective-permute-start(bf16[4,64,256]{2,1,0:T(8,128)(2,1)} %get-tuple-element.33), channel_id=1, source_target_pairs={{0,8},{8,16},{16,24},{24,0},{1,9},{9,17},{17,25},{25,1},{2,10},{10... | collective-permute-start | bytes 393224 | tf_op jit(solution)/shard_map/ppermute | solution.py:99
  16.2 11.9 %collective-permute-start.2 = (bf16[4,64,256]{2,1,0:T(8,128)(2,1)}, bf16[4,64,256]{2,1,0:T(8,128)(2,1)}, u32[]{:S(2)}, u32[]{:S(2)}) collective-permute-start(bf16[4,64,256]{2,1,0:T(8,128)(2,1)} %get-tuple-element.32), channel_id=1, source_target_pairs={{0,16},{8,24},{16,0},{24,8},{1,17},{9,25},{17,1},{25,9},{2,18},{10... | collective-permute-start | bytes 393224 | tf_op jit(solution)/shard_map/ppermute | solution.py:99
  18.8 9.3 %collective-permute-start.3 = (bf16[4,64,256]{2,1,0:T(8,128)(2,1)S(1)}, bf16[4,64,256]{2,1,0:T(8,128)(2,1)}, u32[]{:S(2)}, u32[]{:S(2)}) collective-permute-start(bf16[4,64,256]{2,1,0:T(8,128)(2,1)S(1)} %get-tuple-element.31), channel_id=1, source_target_pairs={{0,24},{8,0},{16,8},{24,16},{1,25},{9,1},{17,9},{25,17},{2,26},{10... | collective-permute-start | bytes 393224 | tf_op jit(solution)/shard_map/ppermute | solution.py:99
  21.0 1.9 %copy-start.15 = (bf16[256,256]{1,0:T(8,128)(2,1)S(1)}, bf16[256,256]{1,0:T(8,128)(2,1)}, u32[]{:S(2)}) copy-start(bf16[256,256]{1,0:T(8,128)(2,1)} %param.20) | copy-start | bytes 393220
  21.7 2.6 %copy-start.20 = (s32[4]{0:T(128)S(1)}, s32[4]{0:T(128)}, u32[]{:S(2)}) copy-start(s32[4]{0:T(128)} %compare_select_fusion) | copy-start | bytes 52
  30.0 1.1 copy-start.1
  37.5 2.6 %copy-start.3 = (f32[8,4,128,128]{3,2,1,0:T(8,128)S(1)}, f32[8,4,128,128]{3,2,1,0:T(8,128)}, u32[]{:S(2)}) copy-start(f32[8,4,128,128]{3,2,1,0:T(8,128)} %fusion.21) | copy-start | bytes 6291460
  37.5 2.9 %copy-start.21 = (f32[8,4,128,128]{2,3,1,0:T(8,128)S(1)}, f32[8,4,128,128]{2,3,1,0:T(8,128)}, u32[]{:S(2)}) copy-start(f32[8,4,128,128]{2,3,1,0:T(8,128)} %get-tuple-element.43) | copy-start | bytes 6291460
  37.5 2.9 %copy-start.22 = (f32[8,4,128]{2,1,0:T(4,128)S(1)}, f32[8,4,128]{2,1,0:T(4,128)}, u32[]{:S(2)}) copy-start(f32[8,4,128]{2,1,0:T(4,128)} %get-tuple-element.42) | copy-start | bytes 49156
  41.0 1.2 %copy-start.6 = (bf16[256,256]{0,1:T(8,128)(2,1)S(1)}, bf16[256,256]{0,1:T(8,128)(2,1)}, u32[]{:S(2)}) copy-start(bf16[256,256]{0,1:T(8,128)(2,1)} %copy.33) | copy-start | bytes 393220
  41.4 2.2 %copy-start.4 = (bf16[8,4,128,64]{2,3,1,0:T(8,128)(2,1)}, bf16[8,4,128,64]{2,3,1,0:T(8,128)(2,1)S(1)}, u32[]{:S(2)}) copy-start(bf16[8,4,128,64]{2,3,1,0:T(8,128)(2,1)S(1)} %convolution_convert_fusion.3) | copy-start | bytes 1572868
  44.4 8.7 %collective-permute-start.4 = (bf16[4,64,256]{2,1,0:T(8,128)(2,1)S(1)}, bf16[4,64,256]{2,1,0:T(8,128)(2,1)}, u32[]{:S(2)}, u32[]{:S(2)}) collective-permute-start(bf16[4,64,256]{2,1,0:T(8,128)(2,1)S(1)} %bitcast.221), channel_id=1, source_target_pairs={{0,8},{8,16},{16,24},{24,0},{1,9},{9,17},{17,25},{25,1},{2,10},{10... | collective-permute-start | bytes 393224 | tf_op jit(solution)/shard_map/ppermute | solution.py:99
  47.7 9.8 %collective-permute-start.5 = (bf16[4,64,256]{2,1,0:T(8,128)(2,1)S(1)}, bf16[4,64,256]{2,1,0:T(8,128)(2,1)S(1)}, u32[]{:S(2)}, u32[]{:S(2)}) collective-permute-start(bf16[4,64,256]{2,1,0:T(8,128)(2,1)S(1)} %bitcast.222), channel_id=1, source_target_pairs={{0,16},{8,24},{16,0},{24,8},{1,17},{9,25},{17,1},{25,9},{2,18},{10... | collective-permute-start | bytes 393224 | tf_op jit(solution)/shard_map/ppermute | solution.py:99
  49.5 8.3 %collective-permute-start.6 = (bf16[4,64,256]{2,1,0:T(8,128)(2,1)S(1)}, bf16[4,64,256]{2,1,0:T(8,128)(2,1)}, u32[]{:S(2)}, u32[]{:S(2)}) collective-permute-start(bf16[4,64,256]{2,1,0:T(8,128)(2,1)S(1)} %bitcast.223), channel_id=1, source_target_pairs={{0,24},{8,0},{16,8},{24,16},{1,25},{9,1},{17,9},{25,17},{2,26},{10... | collective-permute-start | bytes 393224 | tf_op jit(solution)/shard_map/ppermute | solution.py:99
  51.1 1.1 copy-start.5
  52.1 6.1 %copy-start.12 = (bf16[64,4,256]{2,0,1:T(8,128)(2,1)S(1)}, bf16[64,4,256]{2,0,1:T(8,128)(2,1)}, u32[]{:S(2)}) copy-start(bf16[64,4,256]{2,0,1:T(8,128)(2,1)} %copy.81) | copy-start | bytes 393220
  57.5 0.7 copy-start.16
  58.2 2.0 %copy-start.7 = (f32[4,256,256]{2,1,0:T(8,128)S(1)}, f32[4,256,256]{2,1,0:T(8,128)}, u32[]{:S(2)}) copy-start(f32[4,256,256]{2,1,0:T(8,128)} %get-tuple-element.41) | copy-start | bytes 3145732
  60.0 1.0 copy-start.11
  62.4 2.3 %collective-permute-start.7 = (f32[131072]{0:T(1024)}, f32[131072]{0:T(1024)}, u32[]{:S(2)}, u32[]{:S(2)}) collective-permute-start(f32[131072]{0:T(1024)} %broadcast_select_fusion.3), channel_id=1, source_target_pairs={{0,1},{1,0},{2,3},{3,2},{4,5},{5,4},{6,7},{7,6},{8,9},{9,8},{10,11... | collective-permute-start | bytes 1572872 | tf_op jit(solution)/shard_map/ppermute | solution.py:33
  66.5 8.8 %collective-permute-start.10 = (f32[32768]{0:T(1024)S(1)}, f32[32768]{0:T(1024)S(1)}, u32[]{:S(2)}, u32[]{:S(2)}) collective-permute-start(f32[32768]{0:T(1024)S(1)} %bitcast.232), channel_id=1, source_target_pairs={{0,24},{8,0},{16,8},{24,16},{1,25},{9,1},{17,9},{25,17},{2,26},{10... | collective-permute-start | bytes 393224 | tf_op jit(solution)/shard_map/ppermute | solution.py:37
  71.2 8.2 %collective-permute-start.8 = (f32[32768]{0:T(1024)S(1)}, f32[32768]{0:T(1024)S(1)}, u32[]{:S(2)}, u32[]{:S(2)}) collective-permute-start(f32[32768]{0:T(1024)S(1)} %bitcast.231), channel_id=1, source_target_pairs={{0,8},{8,16},{16,24},{24,0},{1,9},{9,17},{17,25},{25,1},{2,10},{10... | collective-permute-start | bytes 393224 | tf_op jit(solution)/shard_map/ppermute | solution.py:37
  71.2 16.5 %copy-start.17 = (s32[4,128]{1,0:T(4,128)S(1)}, s32[4,128]{1,0:T(4,128)}, u32[]{:S(2)}) copy-start(s32[4,128]{1,0:T(4,128)} %param.15) | copy-start | bytes 6148
  71.2 16.5 %copy-start.19 = (pred[4,128]{1,0:T(4,128)(4,1)S(1)}, pred[4,128]{1,0:T(4,128)(4,1)}, u32[]{:S(2)}) copy-start(pred[4,128]{1,0:T(4,128)(4,1)} %copy-done.18) | copy-start | bytes 1540
  71.2 11.8 %collective-permute-start.9 = (f32[32768]{0:T(1024)S(1)}, f32[32768]{0:T(1024)S(1)}, u32[]{:S(2)}, u32[]{:S(2)}) collective-permute-start(f32[32768]{0:T(1024)S(1)} %bitcast.230), channel_id=1, source_target_pairs={{0,16},{8,24},{16,0},{24,8},{1,17},{9,25},{17,1},{25,9},{2,18},{10... | collective-permute-start | bytes 393224 | tf_op jit(solution)/shard_map/ppermute | solution.py:37
  74.7 13.0 %collective-permute-start.14 = (bf16[4,128,256]{2,1,0:T(8,128)(2,1)}, bf16[4,128,256]{2,1,0:T(8,128)(2,1)}, u32[]{:S(2)}, u32[]{:S(2)}) collective-permute-start(bf16[4,128,256]{2,1,0:T(8,128)(2,1)} %slice.101), channel_id=1, source_target_pairs={{0,7},{1,0},{2,1},{3,2},{4,3},{5,4},{6,5},{7,6},{8,15},{9,8},{10,9... | collective-permute-start | bytes 786440 | tf_op jit(solution)/shard_map/ppermute | solution.py:12
  83.2 6.7 %collective-permute-start.11 = (f32[8192]{0:T(1024)S(1)}, f32[8192]{0:T(1024)S(1)}, u32[]{:S(2)}, u32[]{:S(2)}) collective-permute-start(f32[8192]{0:T(1024)S(1)} %bitcast.238), channel_id=1, source_target_pairs={{0,2},{1,3},{2,4},{3,5},{4,6},{5,7},{6,0},{7,1},{8,10},{9,11},{10,... | collective-permute-start | bytes 98312 | tf_op jit(solution)/shard_map/ppermute | solution.py:37
  85.0 4.9 %collective-permute-start.12 = (f32[8192]{0:T(1024)S(1)}, f32[8192]{0:T(1024)S(1)}, u32[]{:S(2)}, u32[]{:S(2)}) collective-permute-start(f32[8192]{0:T(1024)S(1)} %bitcast.237), channel_id=1, source_target_pairs={{0,4},{1,5},{2,6},{3,7},{4,0},{5,1},{6,2},{7,3},{8,12},{9,13},{10,... | collective-permute-start | bytes 98312 | tf_op jit(solution)/shard_map/ppermute | solution.py:37
  85.2 4.7 %collective-permute-start.13 = (f32[8192]{0:T(1024)S(1)}, f32[8192]{0:T(1024)S(1)}, u32[]{:S(2)}, u32[]{:S(2)}) collective-permute-start(f32[8192]{0:T(1024)S(1)} %bitcast.236), channel_id=1, source_target_pairs={{0,6},{1,7},{2,0},{3,1},{4,2},{5,3},{6,4},{7,5},{8,14},{9,15},{10,... | collective-permute-start | bytes 98312 | tf_op jit(solution)/shard_map/ppermute | solution.py:37
  89.9 4.9 %collective-permute-start.15 = (f32[8192]{0:T(1024)S(1)}, f32[8192]{0:T(1024)S(1)}, u32[]{:S(2)}, u32[]{:S(2)}) collective-permute-start(f32[8192]{0:T(1024)S(1)} %add_add_fusion.1), channel_id=1, source_target_pairs={{0,2},{1,3},{2,4},{3,5},{4,6},{5,7},{6,0},{7,1},{8,10},{9,11},{10,... | collective-permute-start | bytes 98312 | tf_op jit(solution)/shard_map/ppermute | solution.py:49
  91.6 3.9 %collective-permute-start.16 = (f32[8192]{0:T(1024)S(1)}, f32[8192]{0:T(1024)S(1)}, u32[]{:S(2)}, u32[]{:S(2)}) collective-permute-start(f32[8192]{0:T(1024)S(1)} %add_add_fusion.1), channel_id=1, source_target_pairs={{0,4},{1,5},{2,6},{3,7},{4,0},{5,1},{6,2},{7,3},{8,12},{9,13},{10,... | collective-permute-start | bytes 98312 | tf_op jit(solution)/shard_map/ppermute | solution.py:49
  93.1 3.9 %collective-permute-start.17 = (f32[8192]{0:T(1024)S(1)}, f32[8192]{0:T(1024)S(1)}, u32[]{:S(2)}, u32[]{:S(2)}) collective-permute-start(f32[8192]{0:T(1024)S(1)} %add_add_fusion.1), channel_id=1, source_target_pairs={{0,6},{1,7},{2,0},{3,1},{4,2},{5,3},{6,4},{7,5},{8,14},{9,15},{10,... | collective-permute-start | bytes 98312 | tf_op jit(solution)/shard_map/ppermute | solution.py:49
  97.9 7.0 %collective-permute-start.18 = (f32[32768]{0:T(1024)S(1)}, f32[32768]{0:T(1024)S(1)}, u32[]{:S(2)}, u32[]{:S(2)}) collective-permute-start(f32[32768]{0:T(1024)S(1)} %bitcast.224), channel_id=1, source_target_pairs={{0,8},{8,16},{16,24},{24,0},{1,9},{9,17},{17,25},{25,1},{2,10},{10... | collective-permute-start | bytes 393224 | tf_op jit(solution)/shard_map/ppermute | solution.py:49
  98.0 9.4 %collective-permute-start.19 = (f32[32768]{0:T(1024)S(1)}, f32[32768]{0:T(1024)S(1)}, u32[]{:S(2)}, u32[]{:S(2)}) collective-permute-start(f32[32768]{0:T(1024)S(1)} %bitcast.225), channel_id=1, source_target_pairs={{0,16},{8,24},{16,0},{24,8},{1,17},{9,25},{17,1},{25,9},{2,18},{10... | collective-permute-start | bytes 393224 | tf_op jit(solution)/shard_map/ppermute | solution.py:49
  100.9 6.4 %collective-permute-start.20 = (f32[32768]{0:T(1024)S(1)}, f32[32768]{0:T(1024)S(1)}, u32[]{:S(2)}, u32[]{:S(2)}) collective-permute-start(f32[32768]{0:T(1024)S(1)} %bitcast.226), channel_id=1, source_target_pairs={{0,24},{8,0},{16,8},{24,16},{1,25},{9,1},{17,9},{25,17},{2,26},{10... | collective-permute-start | bytes 393224 | tf_op jit(solution)/shard_map/ppermute | solution.py:49
  108.9 2.0 %collective-permute-start.21 = (f32[131072]{0:T(1024)S(1)}, f32[131072]{0:T(1024)S(1)}, u32[]{:S(2)}, u32[]{:S(2)}) collective-permute-start(f32[131072]{0:T(1024)S(1)} %bitcast.217), channel_id=1, source_target_pairs={{0,1},{1,0},{2,3},{3,2},{4,5},{5,4},{6,7},{7,6},{8,9},{9,8},{10,11... | collective-permute-start | bytes 1572872 | tf_op jit(solution)/shard_map/ppermute | solution.py:44

commit v17 on v15

--- a/solution.py
+++ b/solution.py
@@ -304,8 +304,11 @@
     inverse = 1.0 / (counted + 1.0)
 
     states_f = node_states.astype(jnp.float32)
-    extended = jnp.concatenate([node_states, received], axis=1)
-    neighbours = jnp.einsum("drs,dsh->drh", adjacent, extended, preferred_element_type=jnp.float32)
+    neighbours = jnp.einsum(
+        "drs,dsh->drh", adjacent[:, :, :node_local], node_states, preferred_element_type=jnp.float32
+    ) + jnp.einsum(
+        "drs,dsh->drh", adjacent[:, :, node_local:], received, preferred_element_type=jnp.float32
+    )
     aggregate = ((states_f + neighbours) * inverse[:, :, None]).astype(jnp.bfloat16)
     preact = jnp.einsum("drh,hk->drk", aggregate, w_message, preferred_element_type=jnp.float32)
     hidden = (states_f + jax.nn.silu(preact)).astype(jnp.bfloat16)

time: 106 us -> 114 us (1.075)
  local copies, waits for them, and re-layouts: 14.5 us -> 21.6 us
  waiting for transfers between devices: 22.3 us -> 18.9 us
  matrix products: 26.4 us -> 28.8 us
  other arithmetic: 9.11 us -> 11.4 us
    unnamed x59 -> x71, local copies, waits for them, and re-layouts: 3.36 us -> 10.4 us
    ppermute x6, waiting for transfers between devices: 8.5 us -> 4.44 us  [exchange(): lax.ppermute(send, axis, [(i, (i + shift) % count) for i in range(count)])]
    dot_general x12, matrix products: 9.44 us -> 11.6 us  [contract(): return jnp.einsum(spec, left, right, preferred_element_type=jnp.float32)]
    ppermute x6, waiting for transfers between devices: 3.41 us -> 4.94 us  [_scatter_step(): lax.ppermute(send, axis, _group_pairs(axis, stride, group, shift))]
    convert_element_type x1, other arithmetic: 0.42 us -> 1.8 us  [local(): pre_grad = (back_days.astype(jnp.float32) * sigmoid_val * (1.0 + preact *...]
  transfers between devices with their start and end apart: 22 -> 22, of which waited for: 16 -> 15; matrix products, arithmetic and copies ran while one was open for 17% -> 21% of each run, Pallas kernels for 0% -> 0%
where the time goes in v17:
time: 114 us
  starting transfers between devices  31.4 us (28%)
  matrix products  28.8 us (25%)
  local copies, waits for them, and re-layouts  21.6 us (19%)
  waiting for transfers between devices  18.9 us (17%)
  other arithmetic  11.4 us (10%)
  between operations  1.42 us (1%)
    ppermute x6, starting transfers between devices, exchange(): lax.ppermute(send, axis, [(i, (i + shift) % count) for i in range(count)])  12 us
    dot_general x12, matrix products, contract(): return jnp.einsum(spec, left, right, preferred_element_type=jnp.float32)  11.6 us
    unnamed x71, local copies, waits for them, and re-layouts  10.4 us
    ppermute x6, starting transfers between devices, _scatter_step(): lax.ppermute(send, axis, _group_pairs(axis, stride, group, shift))  9.16 us
    ppermute x6, starting transfers between devices, _gather_step(): lax.ppermute(flat, axis, _group_pairs(axis, stride, group, shift))  9.07 us
    ppermute x6, waiting for transfers between devices, _gather_step(): lax.ppermute(flat, axis, _group_pairs(axis, stride, group, shift))  5.69 us
    ppermute x6, waiting for transfers between devices, _scatter_step(): lax.ppermute(send, axis, _group_pairs(axis, stride, group, shift))  4.94 us
    ppermute x6, waiting for transfers between devices, exchange(): lax.ppermute(send, axis, [(i, (i + shift) % count) for i in range(count)])  4.44 us
  transfers between devices with their start and end apart: 22, of which 15 were waited for; matrix products, arithmetic and copies ran while one was open for 21% of the time, Pallas kernels for 0%

profile of v17, /device:TPU:0, one launch (start us, length us, event | category | flops | bytes accessed | tf_op | source)
XLA Modules:
  0.0 113.5 jit_solution(13064590271799891196)
XLA Ops:
  1.9 2.1 %convolution_convert_fusion.6 = bf16[4,128,256]{2,1,0:T(8,128)(2,1)} fusion(bf16[4,256,256]{2,1,0:T(8,128)(2,1)} %param.12, s32[4,128]{1,0:T(4,128)} %param.15, pred[4,128]{1,0:T(4,128)(4,1)S(1)} %iota_compare_fusion.10), kind=kOutput, calls=%fused_computation.48 | convolution fusion | flops 67502080 | bytes 788992 | tf_op jit(solution)/shard_map/dsn,dnh->dsh/dot_general | solution.py:287
  4.5 1.4 %fusion.3 = f32[1,4,256]{2,0,1:T(1,128)S(1)} fusion(s32[4,1024]{1,0:T(4,128)} %param.14), kind=kOutput, calls=%fused_computation.9 | convolution fusion | flops 3145728 | bytes 20480 | tf_op jit(solution)/shard_map/der,e->dr/dot_general | solution.py:298
  6.0 2.9 %fusion.11 = bf16[4,256,384]{2,1,0:T(8,128)(2,1)S(1)} fusion(s32[4,1024]{1,0:T(4,128)} %param.13, s32[4,1024]{1,0:T(4,128)} %param.14), kind=kOutput, calls=%fused_computation.21 | convolution fusion | flops 808321024 | bytes 819200 | tf_op jit(solution)/shard_map/der,des->drs/dot_general | solution.py:295
  9.9 1.1 %bitcast_convert_fusion = f32[64,16,256]{2,0,1:T(8,128)S(1)} fusion(bf16[16,1,1,64,256]{4,3,2,1,0:T(8,128)(2,1)} %param.21), kind=kLoop, calls=%fused_computation.172 | loop fusion | flops 262144 | bytes 1572864 | tf_op jit(solution)/shard_map/convert_element_type | solution.py:259
  11.8 1.3 %fusion.17 = bf16[4,256,256]{2,1,0:T(8,128)(2,1)S(1)} fusion(f32[4,256,256]{2,1,0:T(8,128)S(1)} %fusion.32, bf16[4,128,256]{2,1,0:T(8,128)(2,1)} %collective-permute-done, bf16[4,256,256]{2,1,0:T(8,128)(2,1)S(1)} %copy-done.1, f32[4,256]{1,0:T(4,128)S(1)} %fusion.47, bf16[4,256,384]{2,1,0:T(8,128)(2,1)S(1)} %fusion.11), kind=kOutput, calls=%fused_computation.36 | convolution fusion | flops 68419584 | bytes 2625536 | tf_op jit(solution)/shard_map/drs,dsh->drh/dot_general | solution.py:309
  13.1 1.3 %fusion.23 = (bf16[4,256,256]{2,1,0:T(8,128)(2,1)S(1)}, f32[4,256,256]{2,1,0:T(8,128)}) fusion(bf16[4,256,256]{2,1,0:T(8,128)(2,1)S(1)} %copy-done.1, bf16[4,256,256]{2,1,0:T(8,128)(2,1)S(1)} %fusion.17, bf16[256,256]{1,0:T(8,128)(2,1)S(1)} %copy-done), kind=kOutput, calls=%fused_computation.53 | convolution fusion | flops 136052736 | bytes 2752512 | tf_op jit(solution)/shard_map/drh,hk->drk/dot_general | solution.py:313
  15.2 2.3 %collective-permute-start.1 = (bf16[4,64,256]{2,1,0:T(8,128)(2,1)}, bf16[4,64,256]{2,1,0:T(8,128)(2,1)}, u32[]{:S(2)}, u32[]{:S(2)}) collective-permute-start(bf16[4,64,256]{2,1,0:T(8,128)(2,1)} %get-tuple-element.33), channel_id=1, source_target_pairs={{0,8},{8,16},{16,24},{24,0},{1,9},{9,17},{17,25},{25,1},{2,10},{10... | collective-permute-start | bytes 393224 | tf_op jit(solution)/shard_map/ppermute | solution.py:97
  17.5 2.6 %collective-permute-start.2 = (bf16[4,64,256]{2,1,0:T(8,128)(2,1)}, bf16[4,64,256]{2,1,0:T(8,128)(2,1)}, u32[]{:S(2)}, u32[]{:S(2)}) collective-permute-start(bf16[4,64,256]{2,1,0:T(8,128)(2,1)} %get-tuple-element.32), channel_id=1, source_target_pairs={{0,16},{8,24},{16,0},{24,8},{1,17},{9,25},{17,1},{25,9},{2,18},{10... | collective-permute-start | bytes 393224 | tf_op jit(solution)/shard_map/ppermute | solution.py:97
  20.1 1.3 %collective-permute-start.3 = (bf16[4,64,256]{2,1,0:T(8,128)(2,1)}, bf16[4,64,256]{2,1,0:T(8,128)(2,1)}, u32[]{:S(2)}, u32[]{:S(2)}) collective-permute-start(bf16[4,64,256]{2,1,0:T(8,128)(2,1)} %get-tuple-element.31), channel_id=1, source_target_pairs={{0,24},{8,0},{16,8},{24,16},{1,25},{9,1},{17,9},{25,17},{2,26},{10... | collective-permute-start | bytes 393224 | tf_op jit(solution)/shard_map/ppermute | solution.py:97
  22.0 1.7 %copy.31 = bf16[256,256]{0,1:T(8,128)(2,1)} copy(bf16[256,256]{1,0:T(8,128)(2,1)} %param.18) | data formatting | bytes 262144 | tf_op args[6]
  23.7 1.7 %copy.32 = bf16[256,256]{0,1:T(8,128)(2,1)} copy(bf16[256,256]{1,0:T(8,128)(2,1)} %param.19) | data formatting | bytes 262144 | tf_op args[7]
  26.1 1.2 %copy.35 = bf16[8,128,4,64]{1,3,2,0:T(8,128)(2,1)} copy(bf16[8,128,4,64]{3,2,1,0:T(4,128)(2,1)S(1)} %reshape_reshape.12) | data formatting | bytes 1048576 | tf_op jit(solution)/shard_map/reshape;reshape | solution.py:232
  27.3 1.7 %copy.33 = bf16[256,256]{0,1:T(8,128)(2,1)} copy(bf16[256,256]{1,0:T(8,128)(2,1)} %param.20) | data formatting | bytes 262144 | tf_op args[8]
  29.9 1.2 %pad_maximum_fusion = bf16[4,4,64,256]{3,2,1,0:T(8,128)(2,1)S(1)} fusion(bf16[1,4,64,256]{3,2,1,0:T(8,128)(2,1)} %bitcast.6, bf16[1,4,64,256]{3,2,1,0:T(8,128)(2,1)} %bitcast.5, bf16[1,4,64,256]{3,2,1,0:T(8,128)(2,1)} %bitcast.4, bf16[1,4,64,256]{3,2,1,0:T(8,128)(2,1)} %get-tuple-element.30), kind=kLoop, calls=%fused_computation.68 | loop fusion | flops 786432 | bytes 1048576 | tf_op jit(solution)/shard_map/stack | solution.py:99
  32.9 1.1 %fusion.20 = bf16[8,4,128,64]{2,3,1,0:T(8,128)(2,1)} fusion(bf16[8,128,256,1]{2,1,3,0:T(8,128)(2,1)S(1)} %bitcast.203, bf16[256,4,64,1]{0,2,1,3:T(8,128)(2,1)S(1)} %bitcast.213), kind=kOutput, calls=%fused_computation.45 | convolution fusion | flops 134479872 | bytes 1179648 | tf_op jit(solution)/shard_map/gic,chd->ghid/dot_general | solution.py:227
  34.0 3.0 %fusion.22 = f32[8,4,128,128]{3,2,1,0:T(8,128)} fusion(bf16[8,128,4,64]{1,3,2,0:T(8,128)(2,1)S(1)} %copy-done.2, bf16[8,128,256,1]{2,1,3,0:T(8,128)(2,1)S(1)} %bitcast.204, bf16[256,4,64,1]{0,2,1,3:T(8,128)(2,1)} %bitcast.215), kind=kOutput, calls=%fused_computation.47 | convolution fusion | flops 201588736 | bytes 3276800 | tf_op jit(solution)/shard_map/gihd,ghjd->ghij/dot_general | solution.py:227
  37.0 3.8 %fusion.60 = (f32[8,4,128]{2,1,0:T(4,128)}, f32[8,4,128,128]{2,3,1,0:T(8,128)}) fusion(pred[128,128]{0,1:T(8,128)(4,1)} %compare_and_fusion, bf16[8,4,128,64]{2,3,1,0:T(8,128)(2,1)S(1)} %fusion.19, bf16[8,4,128,64]{2,3,1,0:T(8,128)(2,1)} %fusion.20), kind=kOutput, calls=%fused_computation.176 | convolution fusion | flops 69206144 | bytes 3178496 | tf_op jit(solution)/shard_map/sub | solution.py:240
  40.9 2.6 %convolution_convert_fusion.4 = bf16[8,4,128,64]{2,3,1,0:T(8,128)(2,1)S(1)} fusion(bf16[8,128,4,64]{1,3,2,0:T(8,128)(2,1)S(1)} %copy-done.2, f32[8,4,128,128]{2,3,1,0:T(8,128)} %get-tuple-element.43, f32[8,4,128]{2,1,0:T(4,128)} %get-tuple-element.42), kind=kOutput, calls=%fused_computation.41 | convolution fusion | flops 68419584 | bytes 3162112 | tf_op jit(solution)/shard_map/ghij,gihd->ghjd/dot_general | solution.py:227
  45.8 0.8 convolution_convert_fusion.5
  47.0 1.0 convolution_bitcast_fusion.3
  48.4 1.0 convolution_bitcast_fusion.4
  50.7 3.4 %collective-permute-start.4 = (bf16[4,64,256]{2,1,0:T(8,128)(2,1)}, bf16[4,64,256]{2,1,0:T(8,128)(2,1)}, u32[]{:S(2)}, u32[]{:S(2)}) collective-permute-start(bf16[4,64,256]{2,1,0:T(8,128)(2,1)} %bitcast.200), channel_id=1, source_target_pairs={{0,8},{8,16},{16,24},{24,0},{1,9},{9,17},{17,25},{25,1},{2,10},{10... | collective-permute-start | bytes 393224 | tf_op jit(solution)/shard_map/ppermute | solution.py:97
  54.8 1.7 %collective-permute-start.5 = (bf16[4,64,256]{2,1,0:T(8,128)(2,1)}, bf16[4,64,256]{2,1,0:T(8,128)(2,1)}, u32[]{:S(2)}, u32[]{:S(2)}) collective-permute-start(bf16[4,64,256]{2,1,0:T(8,128)(2,1)} %bitcast.199), channel_id=1, source_target_pairs={{0,16},{8,24},{16,0},{24,8},{1,17},{9,25},{17,1},{25,9},{2,18},{10... | collective-permute-start | bytes 393224 | tf_op jit(solution)/shard_map/ppermute | solution.py:97
  60.1 1.0 reshape_reshape.13
  61.1 4.0 %collective-permute-done.5 = bf16[4,64,256]{2,1,0:T(8,128)(2,1)} collective-permute-done((bf16[4,64,256]{2,1,0:T(8,128)(2,1)}, bf16[4,64,256]{2,1,0:T(8,128)(2,1)}, u32[]{:S(2)}, u32[]{:S(2)}) %collective-permute-start.5) | collective-permute-done | bytes 131104 | tf_op jit(solution)/shard_map/ppermute | solution.py:97
  65.3 1.1 pad_maximum_fusion.1
  67.2 1.8 %fusion.25 = bf16[4,256,256]{2,1,0:T(8,128)(2,1)S(1)} fusion(f32[4,256,256]{2,1,0:T(8,128)} %get-tuple-element.41, bf16[4,64,256]{2,1,0:T(8,128)(2,1)S(1)} %get-tuple-element.19, bf16[4,64,256]{2,1,0:T(8,128)(2,1)S(1)} %get-tuple-element.20, bf16[4,64,256]{2,1,0:T(8,128)(2,1)S(1)} %get-tuple-element.21, bf16[4,64,256]{2,1,0:T(8,128)(2,1)S(1)} %get-tuple-element.18), kind=kLoop, calls=%fused_computation.55 | loop fusion | flops 4456448 | bytes 2097152 | tf_op jit(solution)/shard_map/convert_element_type | solution.py:324
  69.6 0.9 broadcast_select_fusion.3
  70.8 1.9 %collective-permute-done.7 = f32[131072]{0:T(1024)} collective-permute-done((f32[131072]{0:T(1024)}, f32[131072]{0:T(1024)}, u32[]{:S(2)}, u32[]{:S(2)}) %collective-permute-start.7) | collective-permute-done | bytes 524320 | tf_op jit(solution)/shard_map/ppermute | solution.py:33
  72.7 1.1 select_add_fusion
  74.5 1.8 %collective-permute-start.10 = (f32[32768]{0:T(1024)S(1)}, f32[32768]{0:T(1024)S(1)}, u32[]{:S(2)}, u32[]{:S(2)}) collective-permute-start(f32[32768]{0:T(1024)S(1)} %bitcast.229), channel_id=1, source_target_pairs={{0,6},{1,7},{2,0},{3,1},{4,2},{5,3},{6,4},{7,5},{8,14},{9,15},{10,... | collective-permute-start | bytes 393224 | tf_op jit(solution)/shard_map/ppermute | solution.py:37
  76.6 1.5 %collective-permute-start.9 = (f32[32768]{0:T(1024)S(1)}, f32[32768]{0:T(1024)S(1)}, u32[]{:S(2)}, u32[]{:S(2)}) collective-permute-start(f32[32768]{0:T(1024)S(1)} %bitcast.227), channel_id=1, source_target_pairs={{0,4},{1,5},{2,6},{3,7},{4,0},{5,1},{6,2},{7,3},{8,12},{9,13},{10,... | collective-permute-start | bytes 393224 | tf_op jit(solution)/shard_map/ppermute | solution.py:37
  78.1 1.0 fusion.61
  79.8 1.1 collective-permute-done.10
  80.9 3.1 %collective-permute-done.8 = f32[32768]{0:T(1024)S(1)} collective-permute-done((f32[32768]{0:T(1024)S(1)}, f32[32768]{0:T(1024)S(1)}, u32[]{:S(2)}, u32[]{:S(2)}) %collective-permute-start.8) | collective-permute-done | bytes 131104 | tf_op jit(solution)/shard_map/ppermute | solution.py:37
  84.6 3.1 %collective-permute-start.11 = (f32[8192]{0:T(1024)S(1)}, f32[8192]{0:T(1024)S(1)}, u32[]{:S(2)}, u32[]{:S(2)}) collective-permute-start(f32[8192]{0:T(1024)S(1)} %bitcast.235), channel_id=1, source_target_pairs={{0,8},{8,16},{16,24},{24,0},{1,9},{9,17},{17,25},{25,1},{2,10},{10... | collective-permute-start | bytes 98312 | tf_op jit(solution)/shard_map/ppermute | solution.py:37
  87.7 1.3 %collective-permute-start.12 = (f32[8192]{0:T(1024)S(1)}, f32[8192]{0:T(1024)S(1)}, u32[]{:S(2)}, u32[]{:S(2)}) collective-permute-start(f32[8192]{0:T(1024)S(1)} %bitcast.234), channel_id=1, source_target_pairs={{0,16},{8,24},{16,0},{24,8},{1,17},{9,25},{17,1},{25,9},{2,18},{10... | collective-permute-start | bytes 98312 | tf_op jit(solution)/shard_map/ppermute | solution.py:37
  89.0 1.2 %collective-permute-start.13 = (f32[8192]{0:T(1024)S(1)}, f32[8192]{0:T(1024)S(1)}, u32[]{:S(2)}, u32[]{:S(2)}) collective-permute-start(f32[8192]{0:T(1024)S(1)} %bitcast.233), channel_id=1, source_target_pairs={{0,24},{8,0},{16,8},{24,16},{1,25},{9,1},{17,9},{25,17},{2,26},{10... | collective-permute-start | bytes 98312 | tf_op jit(solution)/shard_map/ppermute | solution.py:37
  90.2 2.4 %convolution_add_fusion = f32[4,256,256]{2,1,0:T(8,128)} fusion(bf16[4,128,256]{2,1,0:T(8,128)(2,1)S(1)} %collective-permute-done.14, f32[4,256,256]{2,1,0:T(8,128)S(1)} %convolution_multiply_fusion, f32[4,384,256]{2,1,0:T(8,128)S(1)} %fusion.61, s32[4,128]{1,0:T(4,128)S(1)} %copy-done.23, pred[4,128]{1,0:T(4,128)(4,1)S(1)} %copy-done.25, ...), kind=kOutput, calls=%fused_computation.26 | convolution fusion | flops 70254592 | bytes 3934720 | tf_op jit(solution)/shard_map/dsn,dsh->dnh/dot_general | solution.py:343
  93.5 3.1 %collective-permute-start.16 = (f32[8192]{0:T(1024)S(1)}, f32[8192]{0:T(1024)S(1)}, u32[]{:S(2)}, u32[]{:S(2)}) collective-permute-start(f32[8192]{0:T(1024)S(1)} %add_add_fusion.1), channel_id=1, source_target_pairs={{0,16},{8,24},{16,0},{24,8},{1,17},{9,25},{17,1},{25,9},{2,18},{10... | collective-permute-start | bytes 98312 | tf_op jit(solution)/shard_map/ppermute | solution.py:49
  96.6 1.0 collective-permute-start.17
  97.6 1.2 %collective-permute-done.15 = f32[8192]{0:T(1024)S(1)} collective-permute-done((f32[8192]{0:T(1024)S(1)}, f32[8192]{0:T(1024)S(1)}, u32[]{:S(2)}, u32[]{:S(2)}) %collective-permute-start.15) | collective-permute-done | bytes 32800 | tf_op jit(solution)/shard_map/ppermute | solution.py:49
  98.9 1.7 %collective-permute-done.17 = f32[8192]{0:T(1024)S(1)} collective-permute-done((f32[8192]{0:T(1024)S(1)}, f32[8192]{0:T(1024)S(1)}, u32[]{:S(2)}, u32[]{:S(2)}) %collective-permute-start.17) | collective-permute-done | bytes 32800 | tf_op jit(solution)/shard_map/ppermute | solution.py:49
  101.8 1.2 %collective-permute-start.19 = (f32[32768]{0:T(1024)S(1)}, f32[32768]{0:T(1024)S(1)}, u32[]{:S(2)}, u32[]{:S(2)}) collective-permute-start(f32[32768]{0:T(1024)S(1)} %bitcast.223), channel_id=1, source_target_pairs={{0,4},{1,5},{2,6},{3,7},{4,0},{5,1},{6,2},{7,3},{8,12},{9,13},{10,... | collective-permute-start | bytes 393224 | tf_op jit(solution)/shard_map/ppermute | solution.py:49
  103.0 2.8 %collective-permute-start.20 = (f32[32768]{0:T(1024)S(1)}, f32[32768]{0:T(1024)S(1)}, u32[]{:S(2)}, u32[]{:S(2)}) collective-permute-start(f32[32768]{0:T(1024)S(1)} %bitcast.224), channel_id=1, source_target_pairs={{0,6},{1,7},{2,0},{3,1},{4,2},{5,3},{6,4},{7,5},{8,14},{9,15},{10,... | collective-permute-start | bytes 393224 | tf_op jit(solution)/shard_map/ppermute | solution.py:49
  106.0 1.4 %collective-permute-done.18 = f32[32768]{0:T(1024)S(1)} collective-permute-done((f32[32768]{0:T(1024)S(1)}, f32[32768]{0:T(1024)S(1)}, u32[]{:S(2)}, u32[]{:S(2)}) %collective-permute-start.18) | collective-permute-done | bytes 131104 | tf_op jit(solution)/shard_map/ppermute | solution.py:49
  111.0 1.3 %collective-permute-done.21 = f32[131072]{0:T(1024)S(1)} collective-permute-done((f32[131072]{0:T(1024)S(1)}, f32[131072]{0:T(1024)S(1)}, u32[]{:S(2)}, u32[]{:S(2)}) %collective-permute-start.21) | collective-permute-done | bytes 524320 | tf_op jit(solution)/shard_map/ppermute | solution.py:44
  112.5 1.0 fusion.59
  (150 shorter events, 27.1 us)
Async XLA Ops:
  0.6 12.4 %copy-start = (bf16[256,256]{1,0:T(8,128)(2,1)S(1)}, bf16[256,256]{1,0:T(8,128)(2,1)}, u32[]{:S(2)}) copy-start(bf16[256,256]{1,0:T(8,128)(2,1)} %param.17) | copy-start | bytes 393220
  4.1 7.7 %collective-permute-start = (bf16[4,128,256]{2,1,0:T(8,128)(2,1)}, bf16[4,128,256]{2,1,0:T(8,128)(2,1)}, u32[]{:S(2)}, u32[]{:S(2)}) collective-permute-start(bf16[4,128,256]{2,1,0:T(8,128)(2,1)} %convolution_convert_fusion.6), channel_id=1, source_target_pairs={{0,1},{1,2},{2,3},{3,4},{4,5},{5,6},{6,7},{7,0},{8,9},{9,10},{10,1... | collective-permute-start | bytes 786440 | tf_op jit(solution)/shard_map/ppermute | solution.py:12
  6.0 2.9 %copy-start.1 = (bf16[4,256,256]{2,1,0:T(8,128)(2,1)S(1)}, bf16[4,256,256]{2,1,0:T(8,128)(2,1)}, u32[]{:S(2)}) copy-start(bf16[4,256,256]{2,1,0:T(8,128)(2,1)} %param.12) | copy-start | bytes 1572868
  13.1 1.4 %copy-start.4 = (bf16[4,256,256]{2,1,0:T(8,128)(2,1)}, bf16[4,256,256]{2,1,0:T(8,128)(2,1)S(1)}, u32[]{:S(2)}) copy-start(bf16[4,256,256]{2,1,0:T(8,128)(2,1)S(1)} %fusion.17) | copy-start | bytes 1572868
  13.1 12.3 %copy-start.3 = (bf16[16,1,1,64,256]{4,3,2,1,0:T(8,128)(2,1)S(1)}, bf16[16,1,1,64,256]{4,3,2,1,0:T(8,128)(2,1)}, u32[]{:S(2)}) copy-start(bf16[16,1,1,64,256]{4,3,2,1,0:T(8,128)(2,1)} %param.21) | copy-start | bytes 1572868
  15.2 14.4 %collective-permute-start.1 = (bf16[4,64,256]{2,1,0:T(8,128)(2,1)}, bf16[4,64,256]{2,1,0:T(8,128)(2,1)}, u32[]{:S(2)}, u32[]{:S(2)}) collective-permute-start(bf16[4,64,256]{2,1,0:T(8,128)(2,1)} %get-tuple-element.33), channel_id=1, source_target_pairs={{0,8},{8,16},{16,24},{24,0},{1,9},{9,17},{17,25},{25,1},{2,10},{10... | collective-permute-start | bytes 393224 | tf_op jit(solution)/shard_map/ppermute | solution.py:97
  17.5 12.3 %collective-permute-start.2 = (bf16[4,64,256]{2,1,0:T(8,128)(2,1)}, bf16[4,64,256]{2,1,0:T(8,128)(2,1)}, u32[]{:S(2)}, u32[]{:S(2)}) collective-permute-start(bf16[4,64,256]{2,1,0:T(8,128)(2,1)} %get-tuple-element.32), channel_id=1, source_target_pairs={{0,16},{8,24},{16,0},{24,8},{1,17},{9,25},{17,1},{25,9},{2,18},{10... | collective-permute-start | bytes 393224 | tf_op jit(solution)/shard_map/ppermute | solution.py:97
  20.1 9.7 %collective-permute-start.3 = (bf16[4,64,256]{2,1,0:T(8,128)(2,1)}, bf16[4,64,256]{2,1,0:T(8,128)(2,1)}, u32[]{:S(2)}, u32[]{:S(2)}) collective-permute-start(bf16[4,64,256]{2,1,0:T(8,128)(2,1)} %get-tuple-element.31), channel_id=1, source_target_pairs={{0,24},{8,0},{16,8},{24,16},{1,25},{9,1},{17,9},{25,17},{2,26},{10... | collective-permute-start | bytes 393224 | tf_op jit(solution)/shard_map/ppermute | solution.py:97
  27.3 2.3 %copy-start.26 = (s32[4]{0:T(128)S(1)}, s32[4]{0:T(128)}, u32[]{:S(2)}) copy-start(s32[4]{0:T(128)} %compare_select_fusion) | copy-start | bytes 52
  31.7 1.1 copy-start.12
  31.8 2.2 %copy-start.2 = (bf16[8,128,4,64]{1,3,2,0:T(8,128)(2,1)S(1)}, bf16[8,128,4,64]{1,3,2,0:T(8,128)(2,1)}, u32[]{:S(2)}) copy-start(bf16[8,128,4,64]{1,3,2,0:T(8,128)(2,1)} %copy.35) | copy-start | bytes 1572868
  32.9 4.2 %copy-start.7 = (bf16[8,4,128,64]{2,3,1,0:T(8,128)(2,1)}, bf16[8,4,128,64]{2,3,1,0:T(8,128)(2,1)S(1)}, u32[]{:S(2)}) copy-start(bf16[8,4,128,64]{2,3,1,0:T(8,128)(2,1)S(1)} %fusion.19) | copy-start | bytes 1572868
  40.9 2.6 %copy-start.6 = (f32[8,4,128,128]{3,2,1,0:T(8,128)S(1)}, f32[8,4,128,128]{3,2,1,0:T(8,128)}, u32[]{:S(2)}) copy-start(f32[8,4,128,128]{3,2,1,0:T(8,128)} %fusion.22) | copy-start | bytes 6291460
  40.9 2.9 %copy-start.27 = (f32[8,4,128,128]{2,3,1,0:T(8,128)S(1)}, f32[8,4,128,128]{2,3,1,0:T(8,128)}, u32[]{:S(2)}) copy-start(f32[8,4,128,128]{2,3,1,0:T(8,128)} %get-tuple-element.43) | copy-start | bytes 6291460
  40.9 2.9 %copy-start.28 = (f32[8,4,128]{2,1,0:T(4,128)S(1)}, f32[8,4,128]{2,1,0:T(4,128)}, u32[]{:S(2)}) copy-start(f32[8,4,128]{2,1,0:T(4,128)} %get-tuple-element.42) | copy-start | bytes 49156
  43.7 1.0 copy-start.9
  44.8 1.9 %copy-start.14 = (bf16[256,256]{0,1:T(8,128)(2,1)S(1)}, bf16[256,256]{0,1:T(8,128)(2,1)}, u32[]{:S(2)}) copy-start(bf16[256,256]{0,1:T(8,128)(2,1)} %copy.33) | copy-start | bytes 393220
  46.6 1.4 %copy-start.13 = (bf16[256,256]{0,1:T(8,128)(2,1)S(1)}, bf16[256,256]{0,1:T(8,128)(2,1)}, u32[]{:S(2)}) copy-start(bf16[256,256]{0,1:T(8,128)(2,1)} %copy.32) | copy-start | bytes 393220
  47.0 2.4 %copy-start.11 = (bf16[256,256]{0,1:T(8,128)(2,1)S(1)}, bf16[256,256]{0,1:T(8,128)(2,1)}, u32[]{:S(2)}) copy-start(bf16[256,256]{0,1:T(8,128)(2,1)} %copy.31) | copy-start | bytes 393220
  49.7 8.7 %copy-start.21 = (f32[256,4,64]{0,2,1:T(8,128)S(1)}, f32[256,4,64]{0,2,1:T(8,128)}, u32[]{:S(2)}) copy-start(f32[256,4,64]{0,2,1:T(8,128)} %convolution_bitcast_fusion.3) | copy-start | bytes 786436
  49.8 9.2 %copy-start.22 = (f32[256,4,64]{0,2,1:T(8,128)S(1)}, f32[256,4,64]{0,2,1:T(8,128)}, u32[]{:S(2)}) copy-start(f32[256,4,64]{0,2,1:T(8,128)} %convolution_bitcast_fusion.4) | copy-start | bytes 786436
  50.7 10.4 %collective-permute-start.4 = (bf16[4,64,256]{2,1,0:T(8,128)(2,1)}, bf16[4,64,256]{2,1,0:T(8,128)(2,1)}, u32[]{:S(2)}, u32[]{:S(2)}) collective-permute-start(bf16[4,64,256]{2,1,0:T(8,128)(2,1)} %bitcast.200), channel_id=1, source_target_pairs={{0,8},{8,16},{16,24},{24,0},{1,9},{9,17},{17,25},{25,1},{2,10},{10... | collective-permute-start | bytes 393224 | tf_op jit(solution)/shard_map/ppermute | solution.py:97
  54.8 10.3 %collective-permute-start.5 = (bf16[4,64,256]{2,1,0:T(8,128)(2,1)}, bf16[4,64,256]{2,1,0:T(8,128)(2,1)}, u32[]{:S(2)}, u32[]{:S(2)}) collective-permute-start(bf16[4,64,256]{2,1,0:T(8,128)(2,1)} %bitcast.199), channel_id=1, source_target_pairs={{0,16},{8,24},{16,0},{24,8},{1,17},{9,25},{17,1},{25,9},{2,18},{10... | collective-permute-start | bytes 393224 | tf_op jit(solution)/shard_map/ppermute | solution.py:97
  57.1 8.1 %collective-permute-start.6 = (bf16[4,64,256]{2,1,0:T(8,128)(2,1)}, bf16[4,64,256]{2,1,0:T(8,128)(2,1)}, u32[]{:S(2)}, u32[]{:S(2)}) collective-permute-start(bf16[4,64,256]{2,1,0:T(8,128)(2,1)} %bitcast.198), channel_id=1, source_target_pairs={{0,24},{8,0},{16,8},{24,16},{1,25},{9,1},{17,9},{25,17},{2,26},{10... | collective-permute-start | bytes 393224 | tf_op jit(solution)/shard_map/ppermute | solution.py:97
  59.5 5.8 %copy-start.20 = (bf16[64,4,256]{2,0,1:T(8,128)(2,1)S(1)}, bf16[64,4,256]{2,0,1:T(8,128)(2,1)}, u32[]{:S(2)}) copy-start(bf16[64,4,256]{2,0,1:T(8,128)(2,1)} %copy.81) | copy-start | bytes 393220
  67.0 2.0 %copy-start.5 = (bf16[4,256,256]{2,1,0:T(8,128)(2,1)S(1)}, bf16[4,256,256]{2,1,0:T(8,128)(2,1)}, u32[]{:S(2)}) copy-start(bf16[4,256,256]{2,1,0:T(8,128)(2,1)} %copy-done.4) | copy-start | bytes 1572868
  67.2 2.4 %copy-start.16 = (bf16[4,64,256]{2,1,0:T(8,128)(2,1)}, bf16[4,64,256]{2,1,0:T(8,128)(2,1)S(1)}, u32[]{:S(2)}) copy-start(bf16[4,64,256]{2,1,0:T(8,128)(2,1)S(1)} %get-tuple-element.19) | copy-start | bytes 393220
  67.2 2.4 %copy-start.17 = (bf16[4,64,256]{2,1,0:T(8,128)(2,1)}, bf16[4,64,256]{2,1,0:T(8,128)(2,1)S(1)}, u32[]{:S(2)}) copy-start(bf16[4,64,256]{2,1,0:T(8,128)(2,1)S(1)} %get-tuple-element.20) | copy-start | bytes 393220
  67.2 2.4 %copy-start.18 = (bf16[4,64,256]{2,1,0:T(8,128)(2,1)}, bf16[4,64,256]{2,1,0:T(8,128)(2,1)S(1)}, u32[]{:S(2)}) copy-start(bf16[4,64,256]{2,1,0:T(8,128)(2,1)S(1)} %get-tuple-element.21) | copy-start | bytes 393220
  67.2 3.3 %copy-start.15 = (bf16[4,64,256]{2,1,0:T(8,128)(2,1)}, bf16[4,64,256]{2,1,0:T(8,128)(2,1)S(1)}, u32[]{:S(2)}) copy-start(bf16[4,64,256]{2,1,0:T(8,128)(2,1)S(1)} %get-tuple-element.18) | copy-start | bytes 393220
  67.2 2.4 %copy-start.19 = (f32[65536]{0:T(1024)S(1)}, f32[65536]{0:T(1024)}, u32[]{:S(2)}) copy-start(f32[65536]{0:T(1024)} %reshape_reshape.13) | copy-start | bytes 786436
  70.5 2.3 %collective-permute-start.7 = (f32[131072]{0:T(1024)}, f32[131072]{0:T(1024)}, u32[]{:S(2)}, u32[]{:S(2)}) collective-permute-start(f32[131072]{0:T(1024)} %broadcast_select_fusion.3), channel_id=1, source_target_pairs={{0,1},{1,0},{2,3},{3,2},{4,5},{5,4},{6,7},{7,6},{8,9},{9,8},{10,11... | collective-permute-start | bytes 1572872 | tf_op jit(solution)/shard_map/ppermute | solution.py:33
  74.5 6.4 %collective-permute-start.10 = (f32[32768]{0:T(1024)S(1)}, f32[32768]{0:T(1024)S(1)}, u32[]{:S(2)}, u32[]{:S(2)}) collective-permute-start(f32[32768]{0:T(1024)S(1)} %bitcast.229), channel_id=1, source_target_pairs={{0,6},{1,7},{2,0},{3,1},{4,2},{5,3},{6,4},{7,5},{8,14},{9,15},{10,... | collective-permute-start | bytes 393224 | tf_op jit(solution)/shard_map/ppermute | solution.py:37
  76.3 7.7 %collective-permute-start.8 = (f32[32768]{0:T(1024)S(1)}, f32[32768]{0:T(1024)S(1)}, u32[]{:S(2)}, u32[]{:S(2)}) collective-permute-start(f32[32768]{0:T(1024)S(1)} %bitcast.228), channel_id=1, source_target_pairs={{0,2},{1,3},{2,4},{3,5},{4,6},{5,7},{6,0},{7,1},{8,10},{9,11},{10,... | collective-permute-start | bytes 393224 | tf_op jit(solution)/shard_map/ppermute | solution.py:37
  76.6 13.6 %copy-start.23 = (s32[4,128]{1,0:T(4,128)S(1)}, s32[4,128]{1,0:T(4,128)}, u32[]{:S(2)}) copy-start(s32[4,128]{1,0:T(4,128)} %param.15) | copy-start | bytes 6148
  76.6 13.6 %copy-start.25 = (pred[4,128]{1,0:T(4,128)(4,1)S(1)}, pred[4,128]{1,0:T(4,128)(4,1)}, u32[]{:S(2)}) copy-start(pred[4,128]{1,0:T(4,128)(4,1)} %copy-done.24) | copy-start | bytes 1540
  76.6 7.8 %collective-permute-start.9 = (f32[32768]{0:T(1024)S(1)}, f32[32768]{0:T(1024)S(1)}, u32[]{:S(2)}, u32[]{:S(2)}) collective-permute-start(f32[32768]{0:T(1024)S(1)} %bitcast.227), channel_id=1, source_target_pairs={{0,4},{1,5},{2,6},{3,7},{4,0},{5,1},{6,2},{7,3},{8,12},{9,13},{10,... | collective-permute-start | bytes 393224 | tf_op jit(solution)/shard_map/ppermute | solution.py:37
  79.2 11.0 %collective-permute-start.14 = (bf16[4,128,256]{2,1,0:T(8,128)(2,1)S(1)}, bf16[4,128,256]{2,1,0:T(8,128)(2,1)S(1)}, u32[]{:S(2)}, u32[]{:S(2)}) collective-permute-start(bf16[4,128,256]{2,1,0:T(8,128)(2,1)S(1)} %slice.115), channel_id=1, source_target_pairs={{0,7},{1,0},{2,1},{3,2},{4,3},{5,4},{6,5},{7,6},{8,15},{9,8},{10,9... | collective-permute-start | bytes 786440 | tf_op jit(solution)/shard_map/ppermute | solution.py:12
  84.6 7.9 %collective-permute-start.11 = (f32[8192]{0:T(1024)S(1)}, f32[8192]{0:T(1024)S(1)}, u32[]{:S(2)}, u32[]{:S(2)}) collective-permute-start(f32[8192]{0:T(1024)S(1)} %bitcast.235), channel_id=1, source_target_pairs={{0,8},{8,16},{16,24},{24,0},{1,9},{9,17},{17,25},{25,1},{2,10},{10... | collective-permute-start | bytes 98312 | tf_op jit(solution)/shard_map/ppermute | solution.py:37
  87.7 4.8 %collective-permute-start.12 = (f32[8192]{0:T(1024)S(1)}, f32[8192]{0:T(1024)S(1)}, u32[]{:S(2)}, u32[]{:S(2)}) collective-permute-start(f32[8192]{0:T(1024)S(1)} %bitcast.234), channel_id=1, source_target_pairs={{0,16},{8,24},{16,0},{24,8},{1,17},{9,25},{17,1},{25,9},{2,18},{10... | collective-permute-start | bytes 98312 | tf_op jit(solution)/shard_map/ppermute | solution.py:37
  89.0 3.9 %collective-permute-start.13 = (f32[8192]{0:T(1024)S(1)}, f32[8192]{0:T(1024)S(1)}, u32[]{:S(2)}, u32[]{:S(2)}) collective-permute-start(f32[8192]{0:T(1024)S(1)} %bitcast.233), channel_id=1, source_target_pairs={{0,24},{8,0},{16,8},{24,16},{1,25},{9,1},{17,9},{25,17},{2,26},{10... | collective-permute-start | bytes 98312 | tf_op jit(solution)/shard_map/ppermute | solution.py:37
  93.0 5.9 %collective-permute-start.15 = (f32[8192]{0:T(1024)S(1)}, f32[8192]{0:T(1024)S(1)}, u32[]{:S(2)}, u32[]{:S(2)}) collective-permute-start(f32[8192]{0:T(1024)S(1)} %add_add_fusion.1), channel_id=1, source_target_pairs={{0,8},{8,16},{16,24},{24,0},{1,9},{9,17},{17,25},{25,1},{2,10},{10... | collective-permute-start | bytes 98312 | tf_op jit(solution)/shard_map/ppermute | solution.py:49
  93.5 5.3 %collective-permute-start.16 = (f32[8192]{0:T(1024)S(1)}, f32[8192]{0:T(1024)S(1)}, u32[]{:S(2)}, u32[]{:S(2)}) collective-permute-start(f32[8192]{0:T(1024)S(1)} %add_add_fusion.1), channel_id=1, source_target_pairs={{0,16},{8,24},{16,0},{24,8},{1,17},{9,25},{17,1},{25,9},{2,18},{10... | collective-permute-start | bytes 98312 | tf_op jit(solution)/shard_map/ppermute | solution.py:49
  96.6 3.9 %collective-permute-start.17 = (f32[8192]{0:T(1024)S(1)}, f32[8192]{0:T(1024)S(1)}, u32[]{:S(2)}, u32[]{:S(2)}) collective-permute-start(f32[8192]{0:T(1024)S(1)} %add_add_fusion.1), channel_id=1, source_target_pairs={{0,24},{8,0},{16,8},{24,16},{1,25},{9,1},{17,9},{25,17},{2,26},{10... | collective-permute-start | bytes 98312 | tf_op jit(solution)/shard_map/ppermute | solution.py:49
  101.4 6.0 %collective-permute-start.18 = (f32[32768]{0:T(1024)S(1)}, f32[32768]{0:T(1024)S(1)}, u32[]{:S(2)}, u32[]{:S(2)}) collective-permute-start(f32[32768]{0:T(1024)S(1)} %bitcast.222), channel_id=1, source_target_pairs={{0,2},{1,3},{2,4},{3,5},{4,6},{5,7},{6,0},{7,1},{8,10},{9,11},{10,... | collective-permute-start | bytes 393224 | tf_op jit(solution)/shard_map/ppermute | solution.py:49
  101.8 6.4 %collective-permute-start.19 = (f32[32768]{0:T(1024)S(1)}, f32[32768]{0:T(1024)S(1)}, u32[]{:S(2)}, u32[]{:S(2)}) collective-permute-start(f32[32768]{0:T(1024)S(1)} %bitcast.223), channel_id=1, source_target_pairs={{0,4},{1,5},{2,6},{3,7},{4,0},{5,1},{6,2},{7,3},{8,12},{9,13},{10,... | collective-permute-start | bytes 393224 | tf_op jit(solution)/shard_map/ppermute | solution.py:49
  103.0 5.8 %collective-permute-start.20 = (f32[32768]{0:T(1024)S(1)}, f32[32768]{0:T(1024)S(1)}, u32[]{:S(2)}, u32[]{:S(2)}) collective-permute-start(f32[32768]{0:T(1024)S(1)} %bitcast.224), channel_id=1, source_target_pairs={{0,6},{1,7},{2,0},{3,1},{4,2},{5,3},{6,4},{7,5},{8,14},{9,15},{10,... | collective-permute-start | bytes 393224 | tf_op jit(solution)/shard_map/ppermute | solution.py:49
  110.3 2.0 %collective-permute-start.21 = (f32[131072]{0:T(1024)S(1)}, f32[131072]{0:T(1024)S(1)}, u32[]{:S(2)}, u32[]{:S(2)}) collective-permute-start(f32[131072]{0:T(1024)S(1)} %bitcast.218), channel_id=1, source_target_pairs={{0,1},{1,0},{2,3},{3,2},{4,5},{5,4},{6,7},{7,6},{8,9},{9,8},{10,11... | collective-permute-start | bytes 1572872 | tf_op jit(solution)/shard_map/ppermute | solution.py:44
  (3 other events, 2.5 us)

commit v18 on v15

--- a/solution.py
+++ b/solution.py
@@ -255,13 +255,9 @@
     def input_grad(grad_rows, name):
         return contract("ghid,chd->gic", grad_rows, heads_of[name])
 
-    back = (
-        up_flat.astype(jnp.float32)
-        + input_grad(query_grad, "q")
-        + input_grad(key_grad, "k")
-        + input_grad(value_grad, "v")
-    )
-    back = jnp.swapaxes(back.astype(jnp.bfloat16).reshape(nodes_here, steps_all, width), 0, 1)
+    through = input_grad(query_grad, "q") + input_grad(key_grad, "k") + input_grad(value_grad, "v")
+    through = jnp.swapaxes(through.reshape(nodes_here, steps_all, width), 0, 1)
+    back = (upstream.astype(jnp.float32) + through).astype(jnp.bfloat16)
     return ((weight_grad(query_grad), weight_grad(key_grad), weight_grad(value_grad)), back)
 
 

time: 106 us -> 105 us (level)
  waiting for transfers between devices: 22.3 us -> 26.9 us
  local copies, waits for them, and re-layouts: 14.5 us -> 10.7 us
  matrix products: 26.4 us -> 23.2 us
  other arithmetic: 9.11 us -> 10.5 us
    ppermute x6, waiting for transfers between devices: 8.5 us -> 12.7 us  [exchange(): lax.ppermute(send, axis, [(i, (i + shift) % count) for i in range(count)])]
    unnamed x59 -> x45, local copies, waits for them, and re-layouts: 3.36 us -> 1.02 us
    sub x1, matrix products: 3.51 us -> 2.22 us  [attend_blocked(): exponent = jnp.exp(scores - highest)]
    ppermute x2, starting transfers between devices: 2.18 us -> 0.96 us  [from_behind(): return lax.ppermute(value, axis, pairs)]
    convert_element_type x1, other arithmetic: 0.42 us -> 1.63 us  [local(): pre_grad = (back_days.astype(jnp.float32) * sigmoid_val * (1.0 + preact *...]
  transfers between devices with their start and end apart: 22 -> 22, of which waited for: 16 -> 17; matrix products, arithmetic and copies ran while one was open for 17% -> 15% of each run, Pallas kernels for 0% -> 0%
where the time goes in v18:
time: 105 us; the launch traced here: 104 us
  starting transfers between devices  31.5 us (30%)
  waiting for transfers between devices  26.9 us (26%)
  matrix products  23.2 us (22%)
  local copies, waits for them, and re-layouts  10.7 us (10%)
  other arithmetic  10.5 us (10%)
  between operations  1.34 us (1%)
    ppermute x6, waiting for transfers between devices, exchange(): lax.ppermute(send, axis, [(i, (i + shift) % count) for i in range(count)])  12.7 us
    ppermute x6, starting transfers between devices, exchange(): lax.ppermute(send, axis, [(i, (i + shift) % count) for i in range(count)])  12 us
    ppermute x6, starting transfers between devices, _scatter_step(): lax.ppermute(send, axis, _group_pairs(axis, stride, group, shift))  9.36 us
    ppermute x6, starting transfers between devices, _gather_step(): lax.ppermute(flat, axis, _group_pairs(axis, stride, group, shift))  9.1 us
    dot_general x12, matrix products, contract(): return jnp.einsum(spec, left, right, preferred_element_type=jnp.float32)  8.44 us
    ppermute x6, waiting for transfers between devices, _gather_step(): lax.ppermute(flat, axis, _group_pairs(axis, stride, group, shift))  5.69 us
    ppermute x6, waiting for transfers between devices, _scatter_step(): lax.ppermute(send, axis, _group_pairs(axis, stride, group, shift))  3.45 us
    dot_general x1, matrix products, local(): jnp.einsum('der,des->drs', target_hot, source_hot, preferred_element_type...  2.86 us
  transfers between devices with their start and end apart: 22, of which 17 were waited for; matrix products, arithmetic and copies ran while one was open for 15% of the time, Pallas kernels for 0%

profile of v18, /device:TPU:0, one launch (start us, length us, event | category | flops | bytes accessed | tf_op | source)
XLA Modules:
  0.0 104.1 jit_solution(4315310666943723620)
XLA Ops:
  0.6 0.8 iota_compare_fusion.10
  1.4 1.4 %convolution_convert_fusion.6 = bf16[4,128,256]{2,1,0:T(8,128)(2,1)S(1)} fusion(bf16[4,256,256]{2,1,0:T(8,128)(2,1)} %param.12, s32[4,128]{1,0:T(4,128)} %param.15, pred[4,128]{1,0:T(4,128)(4,1)S(1)} %iota_compare_fusion.10), kind=kOutput, calls=%fused_computation.45 | convolution fusion | flops 67502080 | bytes 788992 | tf_op jit(solution)/shard_map/dsn,dnh->dsh/dot_general | solution.py:283
  3.4 1.4 %fusion.3 = f32[1,4,256]{2,0,1:T(1,128)S(1)} fusion(s32[4,1024]{1,0:T(4,128)} %param.14), kind=kOutput, calls=%fused_computation.9 | convolution fusion | flops 3145728 | bytes 20480 | tf_op jit(solution)/shard_map/der,e->dr/dot_general | solution.py:294
  4.8 0.7 compare_and_fusion
  5.5 2.9 %fusion.11 = bf16[4,256,384]{2,1,0:T(8,128)(2,1)S(1)} fusion(s32[4,1024]{1,0:T(4,128)} %param.13, s32[4,1024]{1,0:T(4,128)} %param.14), kind=kOutput, calls=%fused_computation.21 | convolution fusion | flops 808321024 | bytes 819200 | tf_op jit(solution)/shard_map/der,des->drs/dot_general | solution.py:291
  8.4 1.8 %collective-permute-done = bf16[4,128,256]{2,1,0:T(8,128)(2,1)S(1)} collective-permute-done((bf16[4,128,256]{2,1,0:T(8,128)(2,1)S(1)}, bf16[4,128,256]{2,1,0:T(8,128)(2,1)S(1)}, u32[]{:S(2)}, u32[]{:S(2)}) %collective-permute-start) | collective-permute-done | bytes 262176 | tf_op jit(solution)/shard_map/ppermute | solution.py:12
  10.8 1.3 %fusion.20 = (bf16[4,256,256]{2,1,0:T(8,128)(2,1)S(1)}, f32[4,256,256]{2,1,0:T(8,128)}) fusion(bf16[4,256,256]{2,1,0:T(8,128)(2,1)S(1)} %copy-done.6, bf16[4,256,256]{2,1,0:T(8,128)(2,1)S(1)} %fusion.15, bf16[256,256]{1,0:T(8,128)(2,1)S(1)} %copy-done), kind=kOutput, calls=%fused_computation.50 | convolution fusion | flops 136052736 | bytes 2752512 | tf_op jit(solution)/shard_map/drh,hk->drk/dot_general | solution.py:306
  12.2 2.4 %collective-permute-start.1 = (bf16[4,64,256]{2,1,0:T(8,128)(2,1)S(1)}, bf16[4,64,256]{2,1,0:T(8,128)(2,1)S(1)}, u32[]{:S(2)}, u32[]{:S(2)}) collective-permute-start(bf16[4,64,256]{2,1,0:T(8,128)(2,1)S(1)} %get-tuple-element.33), channel_id=1, source_target_pairs={{0,8},{8,16},{16,24},{24,0},{1,9},{9,17},{17,25},{25,1},{2,10},{10... | collective-permute-start | bytes 393224 | tf_op jit(solution)/shard_map/ppermute | solution.py:97
  14.6 2.6 %collective-permute-start.2 = (bf16[4,64,256]{2,1,0:T(8,128)(2,1)S(1)}, bf16[4,64,256]{2,1,0:T(8,128)(2,1)}, u32[]{:S(2)}, u32[]{:S(2)}) collective-permute-start(bf16[4,64,256]{2,1,0:T(8,128)(2,1)S(1)} %get-tuple-element.32), channel_id=1, source_target_pairs={{0,16},{8,24},{16,0},{24,8},{1,17},{9,25},{17,1},{25,9},{2,18},{10... | collective-permute-start | bytes 393224 | tf_op jit(solution)/shard_map/ppermute | solution.py:97
  17.2 1.4 %collective-permute-start.3 = (bf16[4,64,256]{2,1,0:T(8,128)(2,1)S(1)}, bf16[4,64,256]{2,1,0:T(8,128)(2,1)}, u32[]{:S(2)}, u32[]{:S(2)}) collective-permute-start(bf16[4,64,256]{2,1,0:T(8,128)(2,1)S(1)} %get-tuple-element.31), channel_id=1, source_target_pairs={{0,24},{8,0},{16,8},{24,16},{1,25},{9,1},{17,9},{25,17},{2,26},{10... | collective-permute-start | bytes 393224 | tf_op jit(solution)/shard_map/ppermute | solution.py:97
  20.9 5.8 %collective-permute-done.2 = bf16[4,64,256]{2,1,0:T(8,128)(2,1)} collective-permute-done((bf16[4,64,256]{2,1,0:T(8,128)(2,1)S(1)}, bf16[4,64,256]{2,1,0:T(8,128)(2,1)}, u32[]{:S(2)}, u32[]{:S(2)}) %collective-permute-start.2) | collective-permute-done | bytes 131104 | tf_op jit(solution)/shard_map/ppermute | solution.py:97
  26.7 1.0 pad_maximum_fusion
  29.6 2.0 %fusion.19 = f32[8,4,128,128]{3,2,1,0:T(8,128)} fusion(bf16[8,128,4,64]{1,3,2,0:T(8,128)(2,1)S(1)} %copy.34, bf16[8,128,256,1]{2,1,3,0:T(8,128)(2,1)S(1)} %bitcast.190, bf16[256,4,64,1]{0,2,1,3:T(8,128)(2,1)S(1)} %bitcast.198), kind=kOutput, calls=%fused_computation.44 | convolution fusion | flops 201588736 | bytes 3276800 | tf_op jit(solution)/shard_map/gihd,ghjd->ghij/dot_general | solution.py:227
  31.6 2.2 %fusion.59 = (f32[8,4,128]{2,1,0:T(4,128)S(1)}, f32[8,4,128,128]{2,3,1,0:T(8,128)}) fusion(pred[128,128]{0,1:T(8,128)(4,1)S(1)} %copy-done.12, bf16[8,4,128,64]{2,3,1,0:T(8,128)(2,1)S(1)} %fusion.16, bf16[8,4,128,64]{2,3,1,0:T(8,128)(2,1)S(1)} %fusion.17), kind=kOutput, calls=%fused_computation.171 | convolution fusion | flops 69206144 | bytes 3178496 | tf_op jit(solution)/shard_map/sub | solution.py:240
  33.8 2.6 %convolution_convert_fusion.4 = bf16[8,4,128,64]{2,3,1,0:T(8,128)(2,1)S(1)} fusion(bf16[8,128,4,64]{1,3,2,0:T(8,128)(2,1)S(1)} %copy.34, f32[8,4,128,128]{2,3,1,0:T(8,128)} %get-tuple-element.43, f32[8,4,128]{2,1,0:T(4,128)S(1)} %get-tuple-element.42), kind=kOutput, calls=%fused_computation.39 | convolution fusion | flops 68419584 | bytes 3162112 | tf_op jit(solution)/shard_map/ghij,gihd->ghjd/dot_general | solution.py:227
  37.7 0.8 convolution_convert_fusion.5
  40.2 0.6 fusion.24
  40.9 0.8 dynamic-slice_bitcast_fusion
  41.6 3.3 %collective-permute-start.4 = (bf16[4,64,256]{2,1,0:T(8,128)(2,1)}, bf16[4,64,256]{2,1,0:T(8,128)(2,1)}, u32[]{:S(2)}, u32[]{:S(2)}) collective-permute-start(bf16[4,64,256]{2,1,0:T(8,128)(2,1)} %get-tuple-element.25), channel_id=1, source_target_pairs={{0,8},{8,16},{16,24},{24,0},{1,9},{9,17},{17,25},{25,1},{2,10},{10... | collective-permute-start | bytes 393224 | tf_op jit(solution)/shard_map/ppermute | solution.py:97
  45.0 1.8 %collective-permute-start.5 = (bf16[4,64,256]{2,1,0:T(8,128)(2,1)}, bf16[4,64,256]{2,1,0:T(8,128)(2,1)}, u32[]{:S(2)}, u32[]{:S(2)}) collective-permute-start(bf16[4,64,256]{2,1,0:T(8,128)(2,1)} %get-tuple-element.24), channel_id=1, source_target_pairs={{0,16},{8,24},{16,0},{24,8},{1,17},{9,25},{17,1},{25,9},{2,18},{10... | collective-permute-start | bytes 393224 | tf_op jit(solution)/shard_map/ppermute | solution.py:97
  49.2 1.7 %collective-permute-done.4 = bf16[4,64,256]{2,1,0:T(8,128)(2,1)} collective-permute-done((bf16[4,64,256]{2,1,0:T(8,128)(2,1)}, bf16[4,64,256]{2,1,0:T(8,128)(2,1)}, u32[]{:S(2)}, u32[]{:S(2)}) %collective-permute-start.4) | collective-permute-done | bytes 131104 | tf_op jit(solution)/shard_map/ppermute | solution.py:97
  50.9 5.0 %collective-permute-done.5 = bf16[4,64,256]{2,1,0:T(8,128)(2,1)} collective-permute-done((bf16[4,64,256]{2,1,0:T(8,128)(2,1)}, bf16[4,64,256]{2,1,0:T(8,128)(2,1)}, u32[]{:S(2)}, u32[]{:S(2)}) %collective-permute-start.5) | collective-permute-done | bytes 131104 | tf_op jit(solution)/shard_map/ppermute | solution.py:97
  56.0 1.1 %pad_maximum_fusion.1 = bf16[4,4,64,256]{3,2,1,0:T(8,128)(2,1)S(1)} fusion(bf16[1,4,64,256]{3,2,1,0:T(8,128)(2,1)} %bitcast.46, bf16[1,4,64,256]{3,2,1,0:T(8,128)(2,1)} %bitcast.45, bf16[1,4,64,256]{3,2,1,0:T(8,128)(2,1)} %bitcast.44, bf16[1,4,64,256]{3,2,1,0:T(8,128)(2,1)S(1)} %get-tuple-element.22), kind=kLoop, calls=%fused_computation.70 | loop fusion | flops 786432 | bytes 1048576 | tf_op jit(solution)/shard_map/stack | solution.py:99
  57.8 1.6 %fusion.22 = bf16[4,256,256]{2,1,0:T(8,128)(2,1)S(1)} fusion(f32[4,256,256]{2,1,0:T(8,128)} %get-tuple-element.41, bf16[4,64,256]{2,1,0:T(8,128)(2,1)S(1)} %get-tuple-element.19, bf16[4,64,256]{2,1,0:T(8,128)(2,1)S(1)} %get-tuple-element.20, bf16[4,64,256]{2,1,0:T(8,128)(2,1)S(1)} %get-tuple-element.21, bf16[4,64,256]{2,1,0:T(8,128)(2,1)S(1)} %get-tuple-element.18), kind=kLoop, calls=%fused_computation.52 | loop fusion | flops 4456448 | bytes 2097152 | tf_op jit(solution)/shard_map/convert_element_type | solution.py:317
  60.0 0.9 broadcast_select_fusion.3
  61.2 1.9 %collective-permute-done.7 = f32[131072]{0:T(1024)} collective-permute-done((f32[131072]{0:T(1024)}, f32[131072]{0:T(1024)}, u32[]{:S(2)}, u32[]{:S(2)}) %collective-permute-start.7) | collective-permute-done | bytes 524320 | tf_op jit(solution)/shard_map/ppermute | solution.py:33
  63.1 1.1 %select_add_fusion = f32[131072]{0:T(1024)S(1)} fusion(f32[131072]{0:T(1024)} %collective-permute-done.7, f32[131072]{0:T(1024)S(1)} %constant_dynamic-update-slice_fusion, f32[131072]{0:T(1024)S(1)} %constant_dynamic-update-slice_fusion.1, pred[]{:T(512)S(6)} %eq.87), kind=kLoop, calls=%fused_computation.74 | loop fusion | flops 262144 | bytes 2097153 | tf_op jit(solution)/shard_map/add | solution.py:33
  64.9 1.2 %collective-permute-start.10 = (f32[32768]{0:T(1024)S(1)}, f32[32768]{0:T(1024)S(1)}, u32[]{:S(2)}, u32[]{:S(2)}) collective-permute-start(f32[32768]{0:T(1024)S(1)} %bitcast.214), channel_id=1, source_target_pairs={{0,6},{1,7},{2,0},{3,1},{4,2},{5,3},{6,4},{7,5},{8,14},{9,15},{10,... | collective-permute-start | bytes 393224 | tf_op jit(solution)/shard_map/ppermute | solution.py:37
  66.1 0.9 collective-permute-start.8
  67.0 1.5 %collective-permute-start.9 = (f32[32768]{0:T(1024)S(1)}, f32[32768]{0:T(1024)S(1)}, u32[]{:S(2)}, u32[]{:S(2)}) collective-permute-start(f32[32768]{0:T(1024)S(1)} %bitcast.212), channel_id=1, source_target_pairs={{0,4},{1,5},{2,6},{3,7},{4,0},{5,1},{6,2},{7,3},{8,12},{9,13},{10,... | collective-permute-start | bytes 393224 | tf_op jit(solution)/shard_map/ppermute | solution.py:37
  68.5 2.1 %fusion.60 = f32[4,384,256]{2,1,0:T(8,128)S(1)} fusion(bf16[4,256,384]{2,1,0:T(8,128)(2,1)} %copy-done.5, f32[4,256,256]{2,1,0:T(8,128)S(1)} %convolution_multiply_fusion), kind=kOutput, calls=%fused_computation.172 | convolution fusion | flops 1207959552 | bytes 3407872 | tf_op jit(solution)/shard_map/drs,drh->dsh/dot_general | solution.py:326
  70.7 0.7 slice.101
  71.9 2.5 %collective-permute-done.8 = f32[32768]{0:T(1024)S(1)} collective-permute-done((f32[32768]{0:T(1024)S(1)}, f32[32768]{0:T(1024)S(1)}, u32[]{:S(2)}, u32[]{:S(2)}) %collective-permute-start.8) | collective-permute-done | bytes 131104 | tf_op jit(solution)/shard_map/ppermute | solution.py:37
  75.0 3.3 %collective-permute-start.11 = (f32[8192]{0:T(1024)S(1)}, f32[8192]{0:T(1024)S(1)}, u32[]{:S(2)}, u32[]{:S(2)}) collective-permute-start(f32[8192]{0:T(1024)S(1)} %bitcast.220), channel_id=1, source_target_pairs={{0,8},{8,16},{16,24},{24,0},{1,9},{9,17},{17,25},{25,1},{2,10},{10... | collective-permute-start | bytes 98312 | tf_op jit(solution)/shard_map/ppermute | solution.py:37
  78.4 1.1 %collective-permute-start.12 = (f32[8192]{0:T(1024)S(1)}, f32[8192]{0:T(1024)S(1)}, u32[]{:S(2)}, u32[]{:S(2)}) collective-permute-start(f32[8192]{0:T(1024)S(1)} %bitcast.219), channel_id=1, source_target_pairs={{0,16},{8,24},{16,0},{24,8},{1,17},{9,25},{17,1},{25,9},{2,18},{10... | collective-permute-start | bytes 98312 | tf_op jit(solution)/shard_map/ppermute | solution.py:37
  79.5 1.3 %collective-permute-start.13 = (f32[8192]{0:T(1024)S(1)}, f32[8192]{0:T(1024)S(1)}, u32[]{:S(2)}, u32[]{:S(2)}) collective-permute-start(f32[8192]{0:T(1024)S(1)} %bitcast.218), channel_id=1, source_target_pairs={{0,24},{8,0},{16,8},{24,16},{1,25},{9,1},{17,9},{25,17},{2,26},{10... | collective-permute-start | bytes 98312 | tf_op jit(solution)/shard_map/ppermute | solution.py:37
  80.8 2.2 %convolution_add_fusion.1 = f32[4,256,256]{2,1,0:T(8,128)} fusion(bf16[4,128,256]{2,1,0:T(8,128)(2,1)} %collective-permute-done.14, f32[4,256,256]{2,1,0:T(8,128)S(1)} %convolution_multiply_fusion, f32[4,384,256]{2,1,0:T(8,128)S(1)} %fusion.60, s32[4,128]{1,0:T(4,128)S(1)} %copy-done.13, pred[4,128]{1,0:T(4,128)(4,1)S(1)} %copy-done.15, ...), kind=kOutput, calls=%fused_computation.27 | convolution fusion | flops 70254592 | bytes 3934720 | tf_op jit(solution)/shard_map/dsn,dsh->dnh/dot_general | solution.py:336
  84.1 3.1 %collective-permute-start.16 = (f32[8192]{0:T(1024)S(1)}, f32[8192]{0:T(1024)S(1)}, u32[]{:S(2)}, u32[]{:S(2)}) collective-permute-start(f32[8192]{0:T(1024)S(1)} %add_add_fusion.1), channel_id=1, source_target_pairs={{0,16},{8,24},{16,0},{24,8},{1,17},{9,25},{17,1},{25,9},{2,18},{10... | collective-permute-start | bytes 98312 | tf_op jit(solution)/shard_map/ppermute | solution.py:49
  87.2 1.0 collective-permute-start.17
  88.2 1.2 %collective-permute-done.15 = f32[8192]{0:T(1024)S(1)} collective-permute-done((f32[8192]{0:T(1024)S(1)}, f32[8192]{0:T(1024)S(1)}, u32[]{:S(2)}, u32[]{:S(2)}) %collective-permute-start.15) | collective-permute-done | bytes 32800 | tf_op jit(solution)/shard_map/ppermute | solution.py:49
  89.5 1.7 %collective-permute-done.17 = f32[8192]{0:T(1024)S(1)} collective-permute-done((f32[8192]{0:T(1024)S(1)}, f32[8192]{0:T(1024)S(1)}, u32[]{:S(2)}, u32[]{:S(2)}) %collective-permute-start.17) | collective-permute-done | bytes 32800 | tf_op jit(solution)/shard_map/ppermute | solution.py:49
  92.1 1.5 %collective-permute-start.19 = (f32[32768]{0:T(1024)S(1)}, f32[32768]{0:T(1024)S(1)}, u32[]{:S(2)}, u32[]{:S(2)}) collective-permute-start(f32[32768]{0:T(1024)S(1)} %bitcast.207), channel_id=1, source_target_pairs={{0,4},{1,5},{2,6},{3,7},{4,0},{5,1},{6,2},{7,3},{8,12},{9,13},{10,... | collective-permute-start | bytes 393224 | tf_op jit(solution)/shard_map/ppermute | solution.py:49
  93.6 2.8 %collective-permute-start.20 = (f32[32768]{0:T(1024)S(1)}, f32[32768]{0:T(1024)S(1)}, u32[]{:S(2)}, u32[]{:S(2)}) collective-permute-start(f32[32768]{0:T(1024)S(1)} %bitcast.208), channel_id=1, source_target_pairs={{0,6},{1,7},{2,0},{3,1},{4,2},{5,3},{6,4},{7,5},{8,14},{9,15},{10,... | collective-permute-start | bytes 393224 | tf_op jit(solution)/shard_map/ppermute | solution.py:49
  96.6 1.4 %collective-permute-done.18 = f32[32768]{0:T(1024)S(1)} collective-permute-done((f32[32768]{0:T(1024)S(1)}, f32[32768]{0:T(1024)S(1)}, u32[]{:S(2)}, u32[]{:S(2)}) %collective-permute-start.18) | collective-permute-done | bytes 131104 | tf_op jit(solution)/shard_map/ppermute | solution.py:49
  98.5 0.9 collective-permute-done.20
  99.9 0.8 gather_fusion.1
  101.6 1.3 %collective-permute-done.21 = f32[131072]{0:T(1024)S(1)} collective-permute-done((f32[131072]{0:T(1024)S(1)}, f32[131072]{0:T(1024)S(1)}, u32[]{:S(2)}, u32[]{:S(2)}) %collective-permute-start.21) | collective-permute-done | bytes 524320 | tf_op jit(solution)/shard_map/ppermute | solution.py:44
  103.1 1.0 fusion.58
  (122 shorter events, 18.1 us)
Async XLA Ops:
  0.6 10.1 %copy-start = (bf16[256,256]{1,0:T(8,128)(2,1)S(1)}, bf16[256,256]{1,0:T(8,128)(2,1)}, u32[]{:S(2)}) copy-start(bf16[256,256]{1,0:T(8,128)(2,1)} %param.17) | copy-start | bytes 393220
  1.4 1.9 %copy-start.14 = (pred[4,128]{1,0:T(4,128)(4,1)}, pred[4,128]{1,0:T(4,128)(4,1)S(1)}, u32[]{:S(2)}) copy-start(pred[4,128]{1,0:T(4,128)(4,1)S(1)} %iota_compare_fusion.10) | copy-start | bytes 1540
  2.8 7.4 %collective-permute-start = (bf16[4,128,256]{2,1,0:T(8,128)(2,1)S(1)}, bf16[4,128,256]{2,1,0:T(8,128)(2,1)S(1)}, u32[]{:S(2)}, u32[]{:S(2)}) collective-permute-start(bf16[4,128,256]{2,1,0:T(8,128)(2,1)S(1)} %convolution_convert_fusion.6), channel_id=1, source_target_pairs={{0,1},{1,2},{2,3},{3,4},{4,5},{5,6},{6,7},{7,0},{8,9},{9,10},{10,1... | collective-permute-start | bytes 786440 | tf_op jit(solution)/shard_map/ppermute | solution.py:12
  5.5 4.7 %copy-start.6 = (bf16[4,256,256]{2,1,0:T(8,128)(2,1)S(1)}, bf16[4,256,256]{2,1,0:T(8,128)(2,1)}, u32[]{:S(2)}) copy-start(bf16[4,256,256]{2,1,0:T(8,128)(2,1)} %param.12) | copy-start | bytes 1572868
  8.4 1.9 %copy-start.5 = (bf16[4,256,384]{2,1,0:T(8,128)(2,1)}, bf16[4,256,384]{2,1,0:T(8,128)(2,1)S(1)}, u32[]{:S(2)}) copy-start(bf16[4,256,384]{2,1,0:T(8,128)(2,1)S(1)} %fusion.11) | copy-start | bytes 2359300
  10.7 1.4 %copy-start.7 = (bf16[4,256,256]{2,1,0:T(8,128)(2,1)}, bf16[4,256,256]{2,1,0:T(8,128)(2,1)S(1)}, u32[]{:S(2)}) copy-start(bf16[4,256,256]{2,1,0:T(8,128)(2,1)S(1)} %fusion.15) | copy-start | bytes 1572868
  10.8 8.3 %copy-start.9 = (bf16[256,256]{1,0:T(8,128)(2,1)S(1)}, bf16[256,256]{1,0:T(8,128)(2,1)}, u32[]{:S(2)}) copy-start(bf16[256,256]{1,0:T(8,128)(2,1)} %param.18) | copy-start | bytes 393220
  10.8 8.4 %copy-start.10 = (bf16[256,256]{1,0:T(8,128)(2,1)S(1)}, bf16[256,256]{1,0:T(8,128)(2,1)}, u32[]{:S(2)}) copy-start(bf16[256,256]{1,0:T(8,128)(2,1)} %param.19) | copy-start | bytes 393220
  10.8 8.5 %copy-start.2 = (bf16[16,1,1,64,256]{4,3,2,1,0:T(8,128)(2,1)S(1)}, bf16[16,1,1,64,256]{4,3,2,1,0:T(8,128)(2,1)}, u32[]{:S(2)}) copy-start(bf16[16,1,1,64,256]{4,3,2,1,0:T(8,128)(2,1)} %param.21) | copy-start | bytes 1572868
  12.2 8.7 %collective-permute-start.1 = (bf16[4,64,256]{2,1,0:T(8,128)(2,1)S(1)}, bf16[4,64,256]{2,1,0:T(8,128)(2,1)S(1)}, u32[]{:S(2)}, u32[]{:S(2)}) collective-permute-start(bf16[4,64,256]{2,1,0:T(8,128)(2,1)S(1)} %get-tuple-element.33), channel_id=1, source_target_pairs={{0,8},{8,16},{16,24},{24,0},{1,9},{9,17},{17,25},{25,1},{2,10},{10... | collective-permute-start | bytes 393224 | tf_op jit(solution)/shard_map/ppermute | solution.py:97
  14.6 12.1 %collective-permute-start.2 = (bf16[4,64,256]{2,1,0:T(8,128)(2,1)S(1)}, bf16[4,64,256]{2,1,0:T(8,128)(2,1)}, u32[]{:S(2)}, u32[]{:S(2)}) collective-permute-start(bf16[4,64,256]{2,1,0:T(8,128)(2,1)S(1)} %get-tuple-element.32), channel_id=1, source_target_pairs={{0,16},{8,24},{16,0},{24,8},{1,17},{9,25},{17,1},{25,9},{2,18},{10... | collective-permute-start | bytes 393224 | tf_op jit(solution)/shard_map/ppermute | solution.py:97
  17.2 9.5 %collective-permute-start.3 = (bf16[4,64,256]{2,1,0:T(8,128)(2,1)S(1)}, bf16[4,64,256]{2,1,0:T(8,128)(2,1)}, u32[]{:S(2)}, u32[]{:S(2)}) collective-permute-start(bf16[4,64,256]{2,1,0:T(8,128)(2,1)S(1)} %get-tuple-element.31), channel_id=1, source_target_pairs={{0,24},{8,0},{16,8},{24,16},{1,25},{9,1},{17,9},{25,17},{2,26},{10... | collective-permute-start | bytes 393224 | tf_op jit(solution)/shard_map/ppermute | solution.py:97
  19.2 9.7 %copy-start.3 = (bf16[256,256]{0,1:T(8,128)(2,1)}, bf16[256,256]{0,1:T(8,128)(2,1)S(1)}, u32[]{:S(2)}) copy-start(bf16[256,256]{0,1:T(8,128)(2,1)S(1)} %copy.30) | copy-start | bytes 393220
  19.3 1.3 %copy-start.11 = (bf16[256,256]{1,0:T(8,128)(2,1)S(1)}, bf16[256,256]{1,0:T(8,128)(2,1)}, u32[]{:S(2)}) copy-start(bf16[256,256]{1,0:T(8,128)(2,1)} %param.20) | copy-start | bytes 393220
  19.3 1.4 %copy-start.16 = (s32[4]{0:T(128)S(1)}, s32[4]{0:T(128)}, u32[]{:S(2)}) copy-start(s32[4]{0:T(128)} %compare_select_fusion) | copy-start | bytes 52
  29.2 2.4 %copy-start.12 = (pred[128,128]{0,1:T(8,128)(4,1)S(1)}, pred[128,128]{0,1:T(8,128)(4,1)}, u32[]{:S(2)}) copy-start(pred[128,128]{0,1:T(8,128)(4,1)} %compare_and_fusion) | copy-start | bytes 49156
  33.8 2.6 %copy-start.1 = (f32[8,4,128,128]{3,2,1,0:T(8,128)S(1)}, f32[8,4,128,128]{3,2,1,0:T(8,128)}, u32[]{:S(2)}) copy-start(f32[8,4,128,128]{3,2,1,0:T(8,128)} %fusion.19) | copy-start | bytes 6291460
  33.8 2.9 %copy-start.17 = (f32[8,4,128,128]{2,3,1,0:T(8,128)S(1)}, f32[8,4,128,128]{2,3,1,0:T(8,128)}, u32[]{:S(2)}) copy-start(f32[8,4,128,128]{2,3,1,0:T(8,128)} %get-tuple-element.43) | copy-start | bytes 6291460
  38.9 1.0 copy-start.4
  41.6 9.3 %collective-permute-start.4 = (bf16[4,64,256]{2,1,0:T(8,128)(2,1)}, bf16[4,64,256]{2,1,0:T(8,128)(2,1)}, u32[]{:S(2)}, u32[]{:S(2)}) collective-permute-start(bf16[4,64,256]{2,1,0:T(8,128)(2,1)} %get-tuple-element.25), channel_id=1, source_target_pairs={{0,8},{8,16},{16,24},{24,0},{1,9},{9,17},{17,25},{25,1},{2,10},{10... | collective-permute-start | bytes 393224 | tf_op jit(solution)/shard_map/ppermute | solution.py:97
  45.0 11.0 %collective-permute-start.5 = (bf16[4,64,256]{2,1,0:T(8,128)(2,1)}, bf16[4,64,256]{2,1,0:T(8,128)(2,1)}, u32[]{:S(2)}, u32[]{:S(2)}) collective-permute-start(bf16[4,64,256]{2,1,0:T(8,128)(2,1)} %get-tuple-element.24), channel_id=1, source_target_pairs={{0,16},{8,24},{16,0},{24,8},{1,17},{9,25},{17,1},{25,9},{2,18},{10... | collective-permute-start | bytes 393224 | tf_op jit(solution)/shard_map/ppermute | solution.py:97
  46.8 9.2 %collective-permute-start.6 = (bf16[4,64,256]{2,1,0:T(8,128)(2,1)S(1)}, bf16[4,64,256]{2,1,0:T(8,128)(2,1)}, u32[]{:S(2)}, u32[]{:S(2)}) collective-permute-start(bf16[4,64,256]{2,1,0:T(8,128)(2,1)S(1)} %get-tuple-element.23), channel_id=1, source_target_pairs={{0,24},{8,0},{16,8},{24,16},{1,25},{9,1},{17,9},{25,17},{2,26},{10... | collective-permute-start | bytes 393224 | tf_op jit(solution)/shard_map/ppermute | solution.py:97
  57.7 1.8 %copy-start.8 = (bf16[4,256,256]{2,1,0:T(8,128)(2,1)S(1)}, bf16[4,256,256]{2,1,0:T(8,128)(2,1)}, u32[]{:S(2)}) copy-start(bf16[4,256,256]{2,1,0:T(8,128)(2,1)} %copy-done.7) | copy-start | bytes 1572868
  60.9 2.3 %collective-permute-start.7 = (f32[131072]{0:T(1024)}, f32[131072]{0:T(1024)}, u32[]{:S(2)}, u32[]{:S(2)}) collective-permute-start(f32[131072]{0:T(1024)} %broadcast_select_fusion.3), channel_id=1, source_target_pairs={{0,1},{1,0},{2,3},{3,2},{4,5},{5,4},{6,7},{7,6},{8,9},{9,8},{10,11... | collective-permute-start | bytes 1572872 | tf_op jit(solution)/shard_map/ppermute | solution.py:33
  64.9 6.9 %collective-permute-start.10 = (f32[32768]{0:T(1024)S(1)}, f32[32768]{0:T(1024)S(1)}, u32[]{:S(2)}, u32[]{:S(2)}) collective-permute-start(f32[32768]{0:T(1024)S(1)} %bitcast.214), channel_id=1, source_target_pairs={{0,6},{1,7},{2,0},{3,1},{4,2},{5,3},{6,4},{7,5},{8,14},{9,15},{10,... | collective-permute-start | bytes 393224 | tf_op jit(solution)/shard_map/ppermute | solution.py:37
  66.1 8.3 %collective-permute-start.8 = (f32[32768]{0:T(1024)S(1)}, f32[32768]{0:T(1024)S(1)}, u32[]{:S(2)}, u32[]{:S(2)}) collective-permute-start(f32[32768]{0:T(1024)S(1)} %bitcast.213), channel_id=1, source_target_pairs={{0,2},{1,3},{2,4},{3,5},{4,6},{5,7},{6,0},{7,1},{8,10},{9,11},{10,... | collective-permute-start | bytes 393224 | tf_op jit(solution)/shard_map/ppermute | solution.py:37
  67.0 13.8 %copy-start.13 = (s32[4,128]{1,0:T(4,128)S(1)}, s32[4,128]{1,0:T(4,128)}, u32[]{:S(2)}) copy-start(s32[4,128]{1,0:T(4,128)} %param.15) | copy-start | bytes 6148
  67.0 13.8 %copy-start.15 = (pred[4,128]{1,0:T(4,128)(4,1)S(1)}, pred[4,128]{1,0:T(4,128)(4,1)}, u32[]{:S(2)}) copy-start(pred[4,128]{1,0:T(4,128)(4,1)} %copy-done.14) | copy-start | bytes 1540
  67.0 7.8 %collective-permute-start.9 = (f32[32768]{0:T(1024)S(1)}, f32[32768]{0:T(1024)S(1)}, u32[]{:S(2)}, u32[]{:S(2)}) collective-permute-start(f32[32768]{0:T(1024)S(1)} %bitcast.212), channel_id=1, source_target_pairs={{0,4},{1,5},{2,6},{3,7},{4,0},{5,1},{6,2},{7,3},{8,12},{9,13},{10,... | collective-permute-start | bytes 393224 | tf_op jit(solution)/shard_map/ppermute | solution.py:37
  71.4 9.4 %collective-permute-start.14 = (bf16[4,128,256]{2,1,0:T(8,128)(2,1)}, bf16[4,128,256]{2,1,0:T(8,128)(2,1)}, u32[]{:S(2)}, u32[]{:S(2)}) collective-permute-start(bf16[4,128,256]{2,1,0:T(8,128)(2,1)} %slice.101), channel_id=1, source_target_pairs={{0,7},{1,0},{2,1},{3,2},{4,3},{5,4},{6,5},{7,6},{8,15},{9,8},{10,9... | collective-permute-start | bytes 786440 | tf_op jit(solution)/shard_map/ppermute | solution.py:12
  75.0 8.0 %collective-permute-start.11 = (f32[8192]{0:T(1024)S(1)}, f32[8192]{0:T(1024)S(1)}, u32[]{:S(2)}, u32[]{:S(2)}) collective-permute-start(f32[8192]{0:T(1024)S(1)} %bitcast.220), channel_id=1, source_target_pairs={{0,8},{8,16},{16,24},{24,0},{1,9},{9,17},{17,25},{25,1},{2,10},{10... | collective-permute-start | bytes 98312 | tf_op jit(solution)/shard_map/ppermute | solution.py:37
  78.4 4.8 %collective-permute-start.12 = (f32[8192]{0:T(1024)S(1)}, f32[8192]{0:T(1024)S(1)}, u32[]{:S(2)}, u32[]{:S(2)}) collective-permute-start(f32[8192]{0:T(1024)S(1)} %bitcast.219), channel_id=1, source_target_pairs={{0,16},{8,24},{16,0},{24,8},{1,17},{9,25},{17,1},{25,9},{2,18},{10... | collective-permute-start | bytes 98312 | tf_op jit(solution)/shard_map/ppermute | solution.py:37
  79.5 4.0 %collective-permute-start.13 = (f32[8192]{0:T(1024)S(1)}, f32[8192]{0:T(1024)S(1)}, u32[]{:S(2)}, u32[]{:S(2)}) collective-permute-start(f32[8192]{0:T(1024)S(1)} %bitcast.218), channel_id=1, source_target_pairs={{0,24},{8,0},{16,8},{24,16},{1,25},{9,1},{17,9},{25,17},{2,26},{10... | collective-permute-start | bytes 98312 | tf_op jit(solution)/shard_map/ppermute | solution.py:37
  83.5 5.9 %collective-permute-start.15 = (f32[8192]{0:T(1024)S(1)}, f32[8192]{0:T(1024)S(1)}, u32[]{:S(2)}, u32[]{:S(2)}) collective-permute-start(f32[8192]{0:T(1024)S(1)} %add_add_fusion.1), channel_id=1, source_target_pairs={{0,8},{8,16},{16,24},{24,0},{1,9},{9,17},{17,25},{25,1},{2,10},{10... | collective-permute-start | bytes 98312 | tf_op jit(solution)/shard_map/ppermute | solution.py:49
  84.1 5.3 %collective-permute-start.16 = (f32[8192]{0:T(1024)S(1)}, f32[8192]{0:T(1024)S(1)}, u32[]{:S(2)}, u32[]{:S(2)}) collective-permute-start(f32[8192]{0:T(1024)S(1)} %add_add_fusion.1), channel_id=1, source_target_pairs={{0,16},{8,24},{16,0},{24,8},{1,17},{9,25},{17,1},{25,9},{2,18},{10... | collective-permute-start | bytes 98312 | tf_op jit(solution)/shard_map/ppermute | solution.py:49
  87.2 3.9 %collective-permute-start.17 = (f32[8192]{0:T(1024)S(1)}, f32[8192]{0:T(1024)S(1)}, u32[]{:S(2)}, u32[]{:S(2)}) collective-permute-start(f32[8192]{0:T(1024)S(1)} %add_add_fusion.1), channel_id=1, source_target_pairs={{0,24},{8,0},{16,8},{24,16},{1,25},{9,1},{17,9},{25,17},{2,26},{10... | collective-permute-start | bytes 98312 | tf_op jit(solution)/shard_map/ppermute | solution.py:49
  92.0 6.0 %collective-permute-start.18 = (f32[32768]{0:T(1024)S(1)}, f32[32768]{0:T(1024)S(1)}, u32[]{:S(2)}, u32[]{:S(2)}) collective-permute-start(f32[32768]{0:T(1024)S(1)} %bitcast.206), channel_id=1, source_target_pairs={{0,2},{1,3},{2,4},{3,5},{4,6},{5,7},{6,0},{7,1},{8,10},{9,11},{10,... | collective-permute-start | bytes 393224 | tf_op jit(solution)/shard_map/ppermute | solution.py:49
  92.1 6.4 %collective-permute-start.19 = (f32[32768]{0:T(1024)S(1)}, f32[32768]{0:T(1024)S(1)}, u32[]{:S(2)}, u32[]{:S(2)}) collective-permute-start(f32[32768]{0:T(1024)S(1)} %bitcast.207), channel_id=1, source_target_pairs={{0,4},{1,5},{2,6},{3,7},{4,0},{5,1},{6,2},{7,3},{8,12},{9,13},{10,... | collective-permute-start | bytes 393224 | tf_op jit(solution)/shard_map/ppermute | solution.py:49
  93.6 5.8 %collective-permute-start.20 = (f32[32768]{0:T(1024)S(1)}, f32[32768]{0:T(1024)S(1)}, u32[]{:S(2)}, u32[]{:S(2)}) collective-permute-start(f32[32768]{0:T(1024)S(1)} %bitcast.208), channel_id=1, source_target_pairs={{0,6},{1,7},{2,0},{3,1},{4,2},{5,3},{6,4},{7,5},{8,14},{9,15},{10,... | collective-permute-start | bytes 393224 | tf_op jit(solution)/shard_map/ppermute | solution.py:49
  100.9 2.0 %collective-permute-start.21 = (f32[131072]{0:T(1024)S(1)}, f32[131072]{0:T(1024)S(1)}, u32[]{:S(2)}, u32[]{:S(2)}) collective-permute-start(f32[131072]{0:T(1024)S(1)} %bitcast.203), channel_id=1, source_target_pairs={{0,1},{1,0},{2,3},{3,2},{4,5},{5,4},{6,7},{7,6},{8,9},{9,8},{10,11... | collective-permute-start | bytes 1572872 | tf_op jit(solution)/shard_map/ppermute | solution.py:44

commit v19 on v18

--- a/solution.py
+++ b/solution.py
@@ -216,7 +216,6 @@
         per_group = 1
     groups = nodes_here // per_group
     block = per_group * steps_all
-    flat = jnp.swapaxes(states, 0, 1).reshape(groups, block, width)
     up_flat = jnp.swapaxes(upstream, 0, 1).reshape(groups, block, width)
     heads_of = {
         name: weight.reshape(width, HEADS, head_dim)
@@ -226,9 +225,15 @@
     def contract(spec, left, right):
         return jnp.einsum(spec, left, right, preferred_element_type=jnp.float32)
 
-    queries = contract("gic,chd->ghid", flat, heads_of["q"]).astype(jnp.bfloat16)
-    key_rows = contract("gic,chd->ghid", flat, heads_of["k"]).astype(jnp.bfloat16)
-    value_rows = contract("gic,chd->ghid", flat, heads_of["v"]).astype(jnp.bfloat16)
+    by_day = states.reshape(steps_all, groups, per_group, width)
+
+    def project(name):
+        rows = contract("tgac,chd->ghatd", by_day, heads_of[name]).astype(jnp.bfloat16)
+        return rows.reshape(groups, HEADS, block, head_dim)
+
+    queries = project("q")
+    key_rows = project("k")
+    value_rows = project("v")
     up_heads = up_flat.reshape(groups, block, HEADS, head_dim)
     position = jnp.arange(block)
     same = (position[:, None] // steps_all) == (position[None, :] // steps_all)
@@ -250,7 +255,8 @@
     key_grad = contract("ghij,ghid->ghjd", score_grad, queries).astype(jnp.bfloat16)
 
     def weight_grad(grad_rows):
-        return contract("gic,ghid->chd", flat, grad_rows).reshape(width, width)
+        split_rows = grad_rows.reshape(groups, HEADS, per_group, steps_all, head_dim)
+        return contract("tgac,ghatd->chd", by_day, split_rows).reshape(width, width)
 
     def input_grad(grad_rows, name):
         return contract("ghid,chd->gic", grad_rows, heads_of[name])

time: 105 us -> 118 us (1.12)
  matrix products: 23.2 us -> 33.4 us
  local copies, waits for them, and re-layouts: 10.7 us -> 20.1 us
  waiting for transfers between devices: 26.9 us -> 21.9 us
  other arithmetic: 10.5 us -> 7.3 us
    convert_element_type x0 -> x6, local copies, waits for them, and re-layouts: none -> 7.68 us  [the longest x3 3.66 us: project(): contract('tgac,chd->ghatd', by_day, heads_of[name]).astype(jnp.bfloat16)]
    dot_general x12, matrix products: 8.44 us -> 13 us  [contract(): return jnp.einsum(spec, left, right, preferred_element_type=jnp.float32)]
    sub x0 -> x1, matrix products: none -> 4.34 us  [attend_blocked(): prob_grad - jnp.sum(prob_grad * probs, axis=-1, keepdims=True)]
    ppermute x6, waiting for transfers between devices: 12.7 us -> 8.49 us  [exchange(): lax.ppermute(send, axis, [(i, (i + shift) % count) for i in range(count)])]
    ppermute x2, starting transfers between devices: 0.96 us -> 2.33 us  [from_behind(): return lax.ppermute(value, axis, pairs)]
    sub x1, matrix products: 2.22 us -> 3.56 us  [attend_blocked(): exponent = jnp.exp(scores - highest)]
    unnamed x45 -> x69, local copies, waits for them, and re-layouts: 1.02 us -> 2.32 us
    convert_element_type x1, other arithmetic: 1.63 us -> 0.42 us  [local(): pre_grad = (back_days.astype(jnp.float32) * sigmoid_val * (1.0 + preact *...]
  transfers between devices with their start and end apart: 22 -> 22, of which waited for: 17 -> 13; matrix products, arithmetic and copies ran while one was open for 15% -> 14% of each run, Pallas kernels for 0% -> 0%
where the time goes in v19:
time: 118 us; the launch traced here: 117 us
  matrix products  33.4 us (28%)
  starting transfers between devices  32.6 us (28%)
  waiting for transfers between devices  21.9 us (19%)
  local copies, waits for them, and re-layouts  20.1 us (17%)
  other arithmetic  7.3 us (6%)
  between operations  1.48 us (1%)
    dot_general x12, matrix products, contract(): return jnp.einsum(spec, left, right, preferred_element_type=jnp.float32)  13 us
    ppermute x6, starting transfers between devices, exchange(): lax.ppermute(send, axis, [(i, (i + shift) % count) for i in range(count)])  12 us
    ppermute x6, starting transfers between devices, _scatter_step(): lax.ppermute(send, axis, _group_pairs(axis, stride, group, shift))  9.5 us
    ppermute x6, starting transfers between devices, _gather_step(): lax.ppermute(flat, axis, _group_pairs(axis, stride, group, shift))  8.8 us
    ppermute x6, waiting for transfers between devices, exchange(): lax.ppermute(send, axis, [(i, (i + shift) % count) for i in range(count)])  8.49 us
    ppermute x6, waiting for transfers between devices, _gather_step(): lax.ppermute(flat, axis, _group_pairs(axis, stride, group, shift))  5.64 us
    sub x1, matrix products, attend_blocked(): prob_grad - jnp.sum(prob_grad * probs, axis=-1, keepdims=True)  4.34 us
    convert_element_type x3, local copies, waits for them, and re-layouts, project(): contract('tgac,chd->ghatd', by_day, heads_of[name]).astype(jnp.bfloat16)  3.66 us
  transfers between devices with their start and end apart: 22, of which 13 were waited for; matrix products, arithmetic and copies ran while one was open for 14% of the time, Pallas kernels for 0%

profile of v19, /device:TPU:0, one launch (start us, length us, event | category | flops | bytes accessed | tf_op | source)
XLA Modules:
  0.0 116.9 jit_solution(3290714136825445821)
XLA Ops:
  1.4 1.4 %convolution_convert_fusion.6 = bf16[4,128,256]{2,1,0:T(8,128)(2,1)S(1)} fusion(bf16[4,256,256]{2,1,0:T(8,128)(2,1)} %param.12, s32[4,128]{1,0:T(4,128)} %param.15, pred[4,128]{1,0:T(4,128)(4,1)S(1)} %iota_compare_fusion.10), kind=kOutput, calls=%fused_computation.44 | convolution fusion | flops 67502080 | bytes 788992 | tf_op jit(solution)/shard_map/dsn,dnh->dsh/dot_general | solution.py:289
  3.4 1.4 %fusion.3 = f32[1,4,256]{2,0,1:T(1,128)S(1)} fusion(s32[4,1024]{1,0:T(4,128)} %param.14), kind=kOutput, calls=%fused_computation.9 | convolution fusion | flops 3145728 | bytes 20480 | tf_op jit(solution)/shard_map/der,e->dr/dot_general | solution.py:300
  5.5 2.9 %fusion.11 = bf16[4,256,384]{2,1,0:T(8,128)(2,1)S(1)} fusion(s32[4,1024]{1,0:T(4,128)} %param.13, s32[4,1024]{1,0:T(4,128)} %param.14), kind=kOutput, calls=%fused_computation.24 | convolution fusion | flops 808321024 | bytes 819200 | tf_op jit(solution)/shard_map/der,des->drs/dot_general | solution.py:297
  8.4 1.9 %collective-permute-done = bf16[4,128,256]{2,1,0:T(8,128)(2,1)S(1)} collective-permute-done((bf16[4,128,256]{2,1,0:T(8,128)(2,1)S(1)}, bf16[4,128,256]{2,1,0:T(8,128)(2,1)S(1)}, u32[]{:S(2)}, u32[]{:S(2)}) %collective-permute-start) | collective-permute-done | bytes 262176 | tf_op jit(solution)/shard_map/ppermute | solution.py:12
  10.8 1.3 %fusion.19 = (bf16[4,256,256]{2,1,0:T(8,128)(2,1)S(1)}, f32[4,256,256]{2,1,0:T(8,128)}) fusion(bf16[4,256,256]{2,1,0:T(8,128)(2,1)S(1)} %copy-done.10, bf16[4,256,256]{2,1,0:T(8,128)(2,1)S(1)} %fusion.18, bf16[256,256]{1,0:T(8,128)(2,1)S(1)} %copy-done), kind=kOutput, calls=%fused_computation.49 | convolution fusion | flops 136052736 | bytes 2752512 | tf_op jit(solution)/shard_map/drh,hk->drk/dot_general | solution.py:312
  12.2 2.4 %collective-permute-start.1 = (bf16[4,64,256]{2,1,0:T(8,128)(2,1)S(1)}, bf16[4,64,256]{2,1,0:T(8,128)(2,1)S(1)}, u32[]{:S(2)}, u32[]{:S(2)}) collective-permute-start(bf16[4,64,256]{2,1,0:T(8,128)(2,1)S(1)} %get-tuple-element.33), channel_id=1, source_target_pairs={{0,8},{8,16},{16,24},{24,0},{1,9},{9,17},{17,25},{25,1},{2,10},{10... | collective-permute-start | bytes 393224 | tf_op jit(solution)/shard_map/ppermute | solution.py:97
  14.6 2.6 %collective-permute-start.2 = (bf16[4,64,256]{2,1,0:T(8,128)(2,1)S(1)}, bf16[4,64,256]{2,1,0:T(8,128)(2,1)S(1)}, u32[]{:S(2)}, u32[]{:S(2)}) collective-permute-start(bf16[4,64,256]{2,1,0:T(8,128)(2,1)S(1)} %get-tuple-element.32), channel_id=1, source_target_pairs={{0,16},{8,24},{16,0},{24,8},{1,17},{9,25},{17,1},{25,9},{2,18},{10... | collective-permute-start | bytes 393224 | tf_op jit(solution)/shard_map/ppermute | solution.py:97
  17.1 1.3 %collective-permute-start.3 = (bf16[4,64,256]{2,1,0:T(8,128)(2,1)S(1)}, bf16[4,64,256]{2,1,0:T(8,128)(2,1)S(1)}, u32[]{:S(2)}, u32[]{:S(2)}) collective-permute-start(bf16[4,64,256]{2,1,0:T(8,128)(2,1)S(1)} %get-tuple-element.31), channel_id=1, source_target_pairs={{0,24},{8,0},{16,8},{24,16},{1,25},{9,1},{17,9},{25,17},{2,26},{10... | collective-permute-start | bytes 393224 | tf_op jit(solution)/shard_map/ppermute | solution.py:97
  19.6 1.4 %copy.43 = bf16[8,128,4,64]{1,3,2,0:T(8,128)(2,1)} copy(bf16[8,128,4,64]{3,2,1,0:T(4,128)(2,1)S(1)} %reshape_reshape.12) | data formatting | bytes 1048576 | tf_op jit(solution)/shard_map/reshape;reshape | solution.py:237
  21.0 4.9 %collective-permute-done.2 = bf16[4,64,256]{2,1,0:T(8,128)(2,1)S(1)} collective-permute-done((bf16[4,64,256]{2,1,0:T(8,128)(2,1)S(1)}, bf16[4,64,256]{2,1,0:T(8,128)(2,1)S(1)}, u32[]{:S(2)}, u32[]{:S(2)}) %collective-permute-start.2) | collective-permute-done | bytes 131104 | tf_op jit(solution)/shard_map/ppermute | solution.py:97
  27.3 1.2 %copy.36 = bf16[8,4,8,16,64]{4,3,2,1,0:T(8,128)(2,1)S(1)} copy(bf16[8,4,8,16,64]{4,2,1,0,3:T(8,128)(2,1)S(1)} %fusion.13) | data formatting | bytes 1048576 | tf_op jit(solution)/shard_map/convert_element_type | solution.py:231
  29.0 1.2 %copy.34 = bf16[8,4,8,16,64]{4,3,2,1,0:T(8,128)(2,1)S(1)} copy(bf16[8,4,8,16,64]{4,2,1,0,3:T(8,128)(2,1)S(1)} %fusion.12) | data formatting | bytes 1048576 | tf_op jit(solution)/shard_map/convert_element_type | solution.py:231
  30.7 1.2 %copy.40 = bf16[8,4,8,16,64]{4,3,2,1,0:T(8,128)(2,1)S(1)} copy(bf16[8,4,8,16,64]{4,2,1,0,3:T(8,128)(2,1)S(1)} %fusion.14) | data formatting | bytes 1048576 | tf_op jit(solution)/shard_map/convert_element_type | solution.py:231
  32.0 3.6 %fusion.69 = (f32[8,4,128]{2,1,0:T(4,128)}, f32[8,4,128,128]{2,3,1,0:T(8,128)}) fusion(pred[128,128]{0,1:T(8,128)(4,1)} %compare_and_fusion, bf16[8,4,128,64]{3,2,1,0:T(8,128)(2,1)S(1)} %bitcast.203, bf16[8,4,128,64]{3,2,1,0:T(8,128)(2,1)S(1)} %bitcast.201), kind=kOutput, calls=%fused_computation.180 | convolution fusion | flops 69206144 | bytes 3178496 | tf_op jit(solution)/shard_map/sub | solution.py:245
  35.5 3.3 %convolution_convert_fusion.3 = bf16[8,4,128,64]{2,3,1,0:T(8,128)(2,1)} fusion(bf16[8,128,4,64]{1,3,2,0:T(8,128)(2,1)} %copy.43, f32[8,4,128,128]{2,3,1,0:T(8,128)} %get-tuple-element.43, f32[8,4,128]{2,1,0:T(4,128)} %get-tuple-element.42), kind=kOutput, calls=%fused_computation.41 | convolution fusion | flops 68419584 | bytes 3162112 | tf_op jit(solution)/shard_map/ghij,gihd->ghjd/dot_general | solution.py:226
  38.9 4.3 %fusion.7 = bf16[8,4,128,128]{2,3,1,0:T(8,128)(2,1)} fusion(bf16[8,4,128,64]{3,2,1,0:T(8,128)(2,1)S(1)} %bitcast.210, bf16[8,128,4,64]{1,3,2,0:T(8,128)(2,1)} %copy.43, f32[8,4,128,128]{2,3,1,0:T(8,128)} %get-tuple-element.43, f32[8,4,128]{2,1,0:T(4,128)} %get-tuple-element.42), kind=kOutput, calls=%fused_computation.15 | convolution fusion | flops 137891968 | bytes 4210688 | tf_op jit(solution)/shard_map/sub | solution.py:251
  43.2 1.8 %convolution_convert_fusion.5 = bf16[8,4,128,64]{2,3,1,0:T(8,128)(2,1)S(1)} fusion(bf16[8,4,128,128]{2,3,1,0:T(8,128)(2,1)} %fusion.7, bf16[8,4,128,64]{3,2,1,0:T(8,128)(2,1)S(1)} %bitcast.202), kind=kOutput, calls=%fused_computation.43 | convolution fusion | flops 67371008 | bytes 2097152 | tf_op jit(solution)/shard_map/ghij,ghjd->ghid/dot_general | solution.py:226
  46.0 1.3 %copy.60 = bf16[8,4,128,64]{3,2,1,0:T(8,128)(2,1)} copy(bf16[8,4,128,64]{2,3,1,0:T(8,128)(2,1)S(1)} %copy-done.2) | data formatting | bytes 1048576 | tf_op jit(solution)/shard_map/convert_element_type | solution.py:248
  47.4 1.4 %convolution_bitcast_fusion = f32[8,128,256]{2,1,0:T(8,128)S(1)} fusion(bf16[8,4,128,64]{2,3,1,0:T(8,128)(2,1)} %convolution_convert_fusion.3, bf16[256,4,64,1]{0,2,1,3:T(8,128)(2,1)S(1)} %bitcast.217), kind=kOutput, calls=%fused_computation.30 | convolution fusion | flops 134217728 | bytes 1703936 | tf_op jit(solution)/shard_map/ghid,chd->gic/dot_general | solution.py:226
  48.8 1.4 %copy.56 = bf16[8,4,128,64]{3,2,1,0:T(8,128)(2,1)} copy(bf16[8,4,128,64]{2,3,1,0:T(8,128)(2,1)S(1)} %convolution_convert_fusion.4) | data formatting | bytes 1048576 | tf_op jit(solution)/shard_map/convert_element_type | solution.py:255
  50.1 1.3 %convolution_bitcast_fusion.1 = f32[8,128,256]{2,1,0:T(8,128)} fusion(bf16[8,4,128,64]{2,3,1,0:T(8,128)(2,1)S(1)} %convolution_convert_fusion.4, bf16[256,4,64,1]{0,2,1,3:T(8,128)(2,1)S(1)} %bitcast.215), kind=kOutput, calls=%fused_computation.31 | convolution fusion | flops 134217728 | bytes 1703936 | tf_op jit(solution)/shard_map/ghid,chd->gic/dot_general | solution.py:226
  51.4 1.3 %copy.52 = bf16[8,4,128,64]{3,2,1,0:T(8,128)(2,1)} copy(bf16[8,4,128,64]{2,3,1,0:T(8,128)(2,1)S(1)} %convolution_convert_fusion.5) | data formatting | bytes 1048576 | tf_op jit(solution)/shard_map/convert_element_type | solution.py:254
  52.8 1.6 %fusion.17 = f32[8,128,256]{2,1,0:T(8,128)S(1)} fusion(f32[8,128,256]{2,1,0:T(8,128)S(1)} %convolution_bitcast_fusion, f32[8,128,256]{2,1,0:T(8,128)} %convolution_bitcast_fusion.1, bf16[8,4,128,64]{2,3,1,0:T(8,128)(2,1)S(1)} %convolution_convert_fusion.5, bf16[256,4,64,1]{0,2,1,3:T(8,128)(2,1)S(1)} %bitcast.220), kind=kOutput, calls=%fused_computation.39 | convolution fusion | flops 134742016 | bytes 3801088 | tf_op jit(solution)/shard_map/ghid,chd->gic/dot_general | solution.py:226
  55.8 3.3 %collective-permute-start.4 = (bf16[4,64,256]{2,1,0:T(8,128)(2,1)S(1)}, bf16[4,64,256]{2,1,0:T(8,128)(2,1)S(1)}, u32[]{:S(2)}, u32[]{:S(2)}) collective-permute-start(bf16[4,64,256]{2,1,0:T(8,128)(2,1)S(1)} %get-tuple-element.25), channel_id=1, source_target_pairs={{0,8},{8,16},{16,24},{24,0},{1,9},{9,17},{17,25},{25,1},{2,10},{10... | collective-permute-start | bytes 393224 | tf_op jit(solution)/shard_map/ppermute | solution.py:97
  59.1 1.7 %collective-permute-start.5 = (bf16[4,64,256]{2,1,0:T(8,128)(2,1)S(1)}, bf16[4,64,256]{2,1,0:T(8,128)(2,1)}, u32[]{:S(2)}, u32[]{:S(2)}) collective-permute-start(bf16[4,64,256]{2,1,0:T(8,128)(2,1)S(1)} %get-tuple-element.24), channel_id=1, source_target_pairs={{0,16},{8,24},{16,0},{24,8},{1,17},{9,25},{17,1},{25,9},{2,18},{10... | collective-permute-start | bytes 393224 | tf_op jit(solution)/shard_map/ppermute | solution.py:97
  65.4 3.5 %collective-permute-done.5 = bf16[4,64,256]{2,1,0:T(8,128)(2,1)} collective-permute-done((bf16[4,64,256]{2,1,0:T(8,128)(2,1)S(1)}, bf16[4,64,256]{2,1,0:T(8,128)(2,1)}, u32[]{:S(2)}, u32[]{:S(2)}) %collective-permute-start.5) | collective-permute-done | bytes 131104 | tf_op jit(solution)/shard_map/ppermute | solution.py:97
  69.0 1.3 %pad_maximum_fusion.2 = bf16[4,4,64,256]{3,2,1,0:T(8,128)(2,1)S(1)} fusion(bf16[1,4,64,256]{3,2,1,0:T(8,128)(2,1)} %bitcast.46, bf16[1,4,64,256]{3,2,1,0:T(8,128)(2,1)} %bitcast.45, bf16[1,4,64,256]{3,2,1,0:T(8,128)(2,1)} %bitcast.229, bf16[1,4,64,256]{3,2,1,0:T(8,128)(2,1)} %get-tuple-element.22), kind=kLoop, calls=%fused_computation.72 | loop fusion | flops 786432 | bytes 1048576 | tf_op jit(solution)/shard_map/stack | solution.py:99
  73.6 1.9 %collective-permute-done.7 = f32[131072]{0:T(1024)} collective-permute-done((f32[131072]{0:T(1024)}, f32[131072]{0:T(1024)}, u32[]{:S(2)}, u32[]{:S(2)}) %collective-permute-start.7) | collective-permute-done | bytes 524320 | tf_op jit(solution)/shard_map/ppermute | solution.py:33
  75.5 1.1 select_add_fusion
  77.3 1.5 %collective-permute-start.10 = (f32[32768]{0:T(1024)S(1)}, f32[32768]{0:T(1024)S(1)}, u32[]{:S(2)}, u32[]{:S(2)}) collective-permute-start(f32[32768]{0:T(1024)S(1)} %bitcast.232), channel_id=1, source_target_pairs={{0,6},{1,7},{2,0},{3,1},{4,2},{5,3},{6,4},{7,5},{8,14},{9,15},{10,... | collective-permute-start | bytes 393224 | tf_op jit(solution)/shard_map/ppermute | solution.py:37
  79.7 1.4 %collective-permute-start.9 = (f32[32768]{0:T(1024)S(1)}, f32[32768]{0:T(1024)S(1)}, u32[]{:S(2)}, u32[]{:S(2)}) collective-permute-start(f32[32768]{0:T(1024)S(1)} %bitcast.230), channel_id=1, source_target_pairs={{0,4},{1,5},{2,6},{3,7},{4,0},{5,1},{6,2},{7,3},{8,12},{9,13},{10,... | collective-permute-start | bytes 393224 | tf_op jit(solution)/shard_map/ppermute | solution.py:37
  81.0 2.1 %fusion.70 = f32[4,384,256]{2,1,0:T(8,128)S(1)} fusion(bf16[4,256,384]{2,1,0:T(8,128)(2,1)} %copy-done.9, f32[4,256,256]{2,1,0:T(8,128)S(1)} %convolution_multiply_fusion), kind=kOutput, calls=%fused_computation.181 | convolution fusion | flops 1207959552 | bytes 3407872 | tf_op jit(solution)/shard_map/drs,drh->dsh/dot_general | solution.py:332
  83.9 1.8 %collective-permute-start.14 = (bf16[4,128,256]{2,1,0:T(8,128)(2,1)}, bf16[4,128,256]{2,1,0:T(8,128)(2,1)}, u32[]{:S(2)}, u32[]{:S(2)}) collective-permute-start(bf16[4,128,256]{2,1,0:T(8,128)(2,1)} %slice.101), channel_id=1, source_target_pairs={{0,7},{1,0},{2,1},{3,2},{4,3},{5,4},{6,5},{7,6},{8,15},{9,8},{10,9... | collective-permute-start | bytes 786440 | tf_op jit(solution)/shard_map/ppermute | solution.py:12
  85.7 1.0 collective-permute-done.8
  87.9 3.3 %collective-permute-start.11 = (f32[8192]{0:T(1024)S(1)}, f32[8192]{0:T(1024)S(1)}, u32[]{:S(2)}, u32[]{:S(2)}) collective-permute-start(f32[8192]{0:T(1024)S(1)} %bitcast.238), channel_id=1, source_target_pairs={{0,8},{8,16},{16,24},{24,0},{1,9},{9,17},{17,25},{25,1},{2,10},{10... | collective-permute-start | bytes 98312 | tf_op jit(solution)/shard_map/ppermute | solution.py:37
  91.3 1.5 %collective-permute-start.12 = (f32[8192]{0:T(1024)S(1)}, f32[8192]{0:T(1024)S(1)}, u32[]{:S(2)}, u32[]{:S(2)}) collective-permute-start(f32[8192]{0:T(1024)S(1)} %bitcast.237), channel_id=1, source_target_pairs={{0,16},{8,24},{16,0},{24,8},{1,17},{9,25},{17,1},{25,9},{2,18},{10... | collective-permute-start | bytes 98312 | tf_op jit(solution)/shard_map/ppermute | solution.py:37
  92.7 1.0 collective-permute-start.13
  93.7 2.2 %convolution_add_fusion.1 = f32[4,256,256]{2,1,0:T(8,128)} fusion(bf16[4,128,256]{2,1,0:T(8,128)(2,1)} %collective-permute-done.14, f32[4,256,256]{2,1,0:T(8,128)S(1)} %convolution_multiply_fusion, f32[4,384,256]{2,1,0:T(8,128)S(1)} %fusion.70, s32[4,128]{1,0:T(4,128)S(1)} %copy-done.27, pred[4,128]{1,0:T(4,128)(4,1)S(1)} %copy-done.29, ...), kind=kOutput, calls=%fused_computation.33 | convolution fusion | flops 70254592 | bytes 3934720 | tf_op jit(solution)/shard_map/dsn,dsh->dnh/dot_general | solution.py:342
  97.1 3.0 %collective-permute-start.16 = (f32[8192]{0:T(1024)S(1)}, f32[8192]{0:T(1024)S(1)}, u32[]{:S(2)}, u32[]{:S(2)}) collective-permute-start(f32[8192]{0:T(1024)S(1)} %add_add_fusion.1), channel_id=1, source_target_pairs={{0,16},{8,24},{16,0},{24,8},{1,17},{9,25},{17,1},{25,9},{2,18},{10... | collective-permute-start | bytes 98312 | tf_op jit(solution)/shard_map/ppermute | solution.py:49
  100.1 1.0 collective-permute-start.17
  101.1 1.3 %collective-permute-done.15 = f32[8192]{0:T(1024)S(1)} collective-permute-done((f32[8192]{0:T(1024)S(1)}, f32[8192]{0:T(1024)S(1)}, u32[]{:S(2)}, u32[]{:S(2)}) %collective-permute-start.15) | collective-permute-done | bytes 32800 | tf_op jit(solution)/shard_map/ppermute | solution.py:49
  102.4 1.5 %collective-permute-done.17 = f32[8192]{0:T(1024)S(1)} collective-permute-done((f32[8192]{0:T(1024)S(1)}, f32[8192]{0:T(1024)S(1)}, u32[]{:S(2)}, u32[]{:S(2)}) %collective-permute-start.17) | collective-permute-done | bytes 32800 | tf_op jit(solution)/shard_map/ppermute | solution.py:49
  104.8 1.1 collective-permute-start.18
  106.6 2.7 %collective-permute-start.20 = (f32[32768]{0:T(1024)S(1)}, f32[32768]{0:T(1024)S(1)}, u32[]{:S(2)}, u32[]{:S(2)}) collective-permute-start(f32[32768]{0:T(1024)S(1)} %bitcast.223), channel_id=1, source_target_pairs={{0,6},{1,7},{2,0},{3,1},{4,2},{5,3},{6,4},{7,5},{8,14},{9,15},{10,... | collective-permute-start | bytes 393224 | tf_op jit(solution)/shard_map/ppermute | solution.py:49
  109.4 1.5 %collective-permute-done.18 = f32[32768]{0:T(1024)S(1)} collective-permute-done((f32[32768]{0:T(1024)S(1)}, f32[32768]{0:T(1024)S(1)}, u32[]{:S(2)}, u32[]{:S(2)}) %collective-permute-start.18) | collective-permute-done | bytes 131104 | tf_op jit(solution)/shard_map/ppermute | solution.py:49
  110.9 1.3 %collective-permute-done.19 = f32[32768]{0:T(1024)S(1)} collective-permute-done((f32[32768]{0:T(1024)S(1)}, f32[32768]{0:T(1024)S(1)}, u32[]{:S(2)}, u32[]{:S(2)}) %collective-permute-start.19) | collective-permute-done | bytes 131104 | tf_op jit(solution)/shard_map/ppermute | solution.py:49
  114.4 1.3 %collective-permute-done.21 = f32[131072]{0:T(1024)S(1)} collective-permute-done((f32[131072]{0:T(1024)S(1)}, f32[131072]{0:T(1024)S(1)}, u32[]{:S(2)}, u32[]{:S(2)}) %collective-permute-start.21) | collective-permute-done | bytes 524320 | tf_op jit(solution)/shard_map/ppermute | solution.py:44
  115.9 1.0 fusion.68
  (150 shorter events, 24.5 us)
Async XLA Ops:
  0.6 10.1 %copy-start = (bf16[256,256]{1,0:T(8,128)(2,1)S(1)}, bf16[256,256]{1,0:T(8,128)(2,1)}, u32[]{:S(2)}) copy-start(bf16[256,256]{1,0:T(8,128)(2,1)} %param.17) | copy-start | bytes 393220
  1.4 1.9 %copy-start.28 = (pred[4,128]{1,0:T(4,128)(4,1)}, pred[4,128]{1,0:T(4,128)(4,1)S(1)}, u32[]{:S(2)}) copy-start(pred[4,128]{1,0:T(4,128)(4,1)S(1)} %iota_compare_fusion.10) | copy-start | bytes 1540
  2.8 7.4 %collective-permute-start = (bf16[4,128,256]{2,1,0:T(8,128)(2,1)S(1)}, bf16[4,128,256]{2,1,0:T(8,128)(2,1)S(1)}, u32[]{:S(2)}, u32[]{:S(2)}) collective-permute-start(bf16[4,128,256]{2,1,0:T(8,128)(2,1)S(1)} %convolution_convert_fusion.6), channel_id=1, source_target_pairs={{0,1},{1,2},{2,3},{3,4},{4,5},{5,6},{6,7},{7,0},{8,9},{9,10},{10,1... | collective-permute-start | bytes 786440 | tf_op jit(solution)/shard_map/ppermute | solution.py:12
  5.5 4.7 %copy-start.10 = (bf16[4,256,256]{2,1,0:T(8,128)(2,1)S(1)}, bf16[4,256,256]{2,1,0:T(8,128)(2,1)}, u32[]{:S(2)}) copy-start(bf16[4,256,256]{2,1,0:T(8,128)(2,1)} %param.12) | copy-start | bytes 1572868
  8.4 3.7 %copy-start.9 = (bf16[4,256,384]{2,1,0:T(8,128)(2,1)}, bf16[4,256,384]{2,1,0:T(8,128)(2,1)S(1)}, u32[]{:S(2)}) copy-start(bf16[4,256,384]{2,1,0:T(8,128)(2,1)S(1)} %fusion.11) | copy-start | bytes 2359300
  10.7 1.4 %copy-start.11 = (bf16[4,256,256]{2,1,0:T(8,128)(2,1)}, bf16[4,256,256]{2,1,0:T(8,128)(2,1)S(1)}, u32[]{:S(2)}) copy-start(bf16[4,256,256]{2,1,0:T(8,128)(2,1)S(1)} %fusion.18) | copy-start | bytes 1572868
  10.8 7.8 %copy-start.15 = (bf16[256,256]{1,0:T(8,128)(2,1)S(1)}, bf16[256,256]{1,0:T(8,128)(2,1)}, u32[]{:S(2)}) copy-start(bf16[256,256]{1,0:T(8,128)(2,1)} %param.19) | copy-start | bytes 393220
  10.8 7.9 %copy-start.16 = (bf16[256,256]{1,0:T(8,128)(2,1)S(1)}, bf16[256,256]{1,0:T(8,128)(2,1)}, u32[]{:S(2)}) copy-start(bf16[256,256]{1,0:T(8,128)(2,1)} %param.18) | copy-start | bytes 393220
  10.8 8.0 %copy-start.17 = (bf16[256,256]{1,0:T(8,128)(2,1)S(1)}, bf16[256,256]{1,0:T(8,128)(2,1)}, u32[]{:S(2)}) copy-start(bf16[256,256]{1,0:T(8,128)(2,1)} %param.20) | copy-start | bytes 393220
  12.1 6.8 %copy-start.3 = (bf16[16,1,1,64,256]{4,3,2,1,0:T(8,128)(2,1)S(1)}, bf16[16,1,1,64,256]{4,3,2,1,0:T(8,128)(2,1)}, u32[]{:S(2)}) copy-start(bf16[16,1,1,64,256]{4,3,2,1,0:T(8,128)(2,1)} %param.21) | copy-start | bytes 1572868
  12.2 8.8 %collective-permute-start.1 = (bf16[4,64,256]{2,1,0:T(8,128)(2,1)S(1)}, bf16[4,64,256]{2,1,0:T(8,128)(2,1)S(1)}, u32[]{:S(2)}, u32[]{:S(2)}) collective-permute-start(bf16[4,64,256]{2,1,0:T(8,128)(2,1)S(1)} %get-tuple-element.33), channel_id=1, source_target_pairs={{0,8},{8,16},{16,24},{24,0},{1,9},{9,17},{17,25},{25,1},{2,10},{10... | collective-permute-start | bytes 393224 | tf_op jit(solution)/shard_map/ppermute | solution.py:97
  14.6 11.4 %collective-permute-start.2 = (bf16[4,64,256]{2,1,0:T(8,128)(2,1)S(1)}, bf16[4,64,256]{2,1,0:T(8,128)(2,1)S(1)}, u32[]{:S(2)}, u32[]{:S(2)}) collective-permute-start(bf16[4,64,256]{2,1,0:T(8,128)(2,1)S(1)} %get-tuple-element.32), channel_id=1, source_target_pairs={{0,16},{8,24},{16,0},{24,8},{1,17},{9,25},{17,1},{25,9},{2,18},{10... | collective-permute-start | bytes 393224 | tf_op jit(solution)/shard_map/ppermute | solution.py:97
  17.1 8.8 %collective-permute-start.3 = (bf16[4,64,256]{2,1,0:T(8,128)(2,1)S(1)}, bf16[4,64,256]{2,1,0:T(8,128)(2,1)S(1)}, u32[]{:S(2)}, u32[]{:S(2)}) collective-permute-start(bf16[4,64,256]{2,1,0:T(8,128)(2,1)S(1)} %get-tuple-element.31), channel_id=1, source_target_pairs={{0,24},{8,0},{16,8},{24,16},{1,25},{9,1},{17,9},{25,17},{2,26},{10... | collective-permute-start | bytes 393224 | tf_op jit(solution)/shard_map/ppermute | solution.py:97
  18.8 9.8 %copy-start.13 = (bf16[256,256]{0,1:T(8,128)(2,1)}, bf16[256,256]{0,1:T(8,128)(2,1)S(1)}, u32[]{:S(2)}) copy-start(bf16[256,256]{0,1:T(8,128)(2,1)S(1)} %copy.33) | copy-start | bytes 393220
  26.8 3.4 %copy-start.18 = (bf16[4,8,8,256]{3,2,1,0:T(8,128)(2,1)}, bf16[4,8,8,256]{3,2,1,0:T(8,128)(2,1)S(1)}, u32[]{:S(2)}) copy-start(bf16[4,8,8,256]{3,2,1,0:T(8,128)(2,1)S(1)} %get-tuple-element.26) | copy-start | bytes 393220
  26.8 3.4 %copy-start.20 = (bf16[4,8,8,256]{3,2,1,0:T(8,128)(2,1)}, bf16[4,8,8,256]{3,2,1,0:T(8,128)(2,1)S(1)}, u32[]{:S(2)}) copy-start(bf16[4,8,8,256]{3,2,1,0:T(8,128)(2,1)S(1)} %get-tuple-element.27) | copy-start | bytes 393220
  26.8 3.4 %copy-start.22 = (bf16[4,8,8,256]{3,2,1,0:T(8,128)(2,1)}, bf16[4,8,8,256]{3,2,1,0:T(8,128)(2,1)S(1)}, u32[]{:S(2)}) copy-start(bf16[4,8,8,256]{3,2,1,0:T(8,128)(2,1)S(1)} %get-tuple-element.28) | copy-start | bytes 393220
  26.8 3.4 %copy-start.24 = (bf16[4,8,8,256]{3,2,1,0:T(8,128)(2,1)}, bf16[4,8,8,256]{3,2,1,0:T(8,128)(2,1)S(1)}, u32[]{:S(2)}) copy-start(bf16[4,8,8,256]{3,2,1,0:T(8,128)(2,1)S(1)} %get-tuple-element.29) | copy-start | bytes 393220
  43.2 1.8 %copy-start.1 = (bf16[8,4,128,128]{2,3,1,0:T(8,128)(2,1)S(1)}, bf16[8,4,128,128]{2,3,1,0:T(8,128)(2,1)}, u32[]{:S(2)}) copy-start(bf16[8,4,128,128]{2,3,1,0:T(8,128)(2,1)} %fusion.7) | copy-start | bytes 3145732
  48.7 4.0 %copy-start.14 = (bf16[256,256]{0,1:T(8,128)(2,1)S(1)}, bf16[256,256]{0,1:T(8,128)(2,1)}, u32[]{:S(2)}) copy-start(bf16[256,256]{0,1:T(8,128)(2,1)} %copy-done.13) | copy-start | bytes 393220
  52.8 1.7 %copy-start.4 = (bf16[16,1,1,64,256]{4,3,2,1,0:T(8,128)(2,1)S(1)}, bf16[16,1,1,64,256]{4,3,2,1,0:T(8,128)(2,1)}, u32[]{:S(2)}) copy-start(bf16[16,1,1,64,256]{4,3,2,1,0:T(8,128)(2,1)} %param.21) | copy-start | bytes 1572868
  54.4 7.1 %copy-start.7 = (bf16[8,4,128,64]{3,2,1,0:T(8,128)(2,1)S(1)}, bf16[8,4,128,64]{3,2,1,0:T(8,128)(2,1)}, u32[]{:S(2)}) copy-start(bf16[8,4,128,64]{3,2,1,0:T(8,128)(2,1)} %copy.60) | copy-start | bytes 1572868
  54.4 7.0 %copy-start.19 = (bf16[4,8,8,256]{3,2,1,0:T(8,128)(2,1)S(1)}, bf16[4,8,8,256]{3,2,1,0:T(8,128)(2,1)}, u32[]{:S(2)}) copy-start(bf16[4,8,8,256]{3,2,1,0:T(8,128)(2,1)} %copy-done.18) | copy-start | bytes 393220
  54.4 7.0 %copy-start.21 = (bf16[4,8,8,256]{3,2,1,0:T(8,128)(2,1)S(1)}, bf16[4,8,8,256]{3,2,1,0:T(8,128)(2,1)}, u32[]{:S(2)}) copy-start(bf16[4,8,8,256]{3,2,1,0:T(8,128)(2,1)} %copy-done.20) | copy-start | bytes 393220
  54.5 7.0 %copy-start.23 = (bf16[4,8,8,256]{3,2,1,0:T(8,128)(2,1)S(1)}, bf16[4,8,8,256]{3,2,1,0:T(8,128)(2,1)}, u32[]{:S(2)}) copy-start(bf16[4,8,8,256]{3,2,1,0:T(8,128)(2,1)} %copy-done.22) | copy-start | bytes 393220
  54.5 7.0 %copy-start.25 = (bf16[4,8,8,256]{3,2,1,0:T(8,128)(2,1)S(1)}, bf16[4,8,8,256]{3,2,1,0:T(8,128)(2,1)}, u32[]{:S(2)}) copy-start(bf16[4,8,8,256]{3,2,1,0:T(8,128)(2,1)} %copy-done.24) | copy-start | bytes 393220
  55.8 9.6 %collective-permute-start.4 = (bf16[4,64,256]{2,1,0:T(8,128)(2,1)S(1)}, bf16[4,64,256]{2,1,0:T(8,128)(2,1)S(1)}, u32[]{:S(2)}, u32[]{:S(2)}) collective-permute-start(bf16[4,64,256]{2,1,0:T(8,128)(2,1)S(1)} %get-tuple-element.25), channel_id=1, source_target_pairs={{0,8},{8,16},{16,24},{24,0},{1,9},{9,17},{17,25},{25,1},{2,10},{10... | collective-permute-start | bytes 393224 | tf_op jit(solution)/shard_map/ppermute | solution.py:97
  59.1 9.8 %collective-permute-start.5 = (bf16[4,64,256]{2,1,0:T(8,128)(2,1)S(1)}, bf16[4,64,256]{2,1,0:T(8,128)(2,1)}, u32[]{:S(2)}, u32[]{:S(2)}) collective-permute-start(bf16[4,64,256]{2,1,0:T(8,128)(2,1)S(1)} %get-tuple-element.24), channel_id=1, source_target_pairs={{0,16},{8,24},{16,0},{24,8},{1,17},{9,25},{17,1},{25,9},{2,18},{10... | collective-permute-start | bytes 393224 | tf_op jit(solution)/shard_map/ppermute | solution.py:97
  60.8 8.2 %collective-permute-start.6 = (bf16[4,64,256]{2,1,0:T(8,128)(2,1)S(1)}, bf16[4,64,256]{2,1,0:T(8,128)(2,1)}, u32[]{:S(2)}, u32[]{:S(2)}) collective-permute-start(bf16[4,64,256]{2,1,0:T(8,128)(2,1)S(1)} %get-tuple-element.23), channel_id=1, source_target_pairs={{0,24},{8,0},{16,8},{24,16},{1,25},{9,1},{17,9},{25,17},{2,26},{10... | collective-permute-start | bytes 393224 | tf_op jit(solution)/shard_map/ppermute | solution.py:97
  65.4 3.6 %copy-start.26 = (bf16[4,64,256]{2,1,0:T(8,128)(2,1)}, bf16[4,64,256]{2,1,0:T(8,128)(2,1)S(1)}, u32[]{:S(2)}) copy-start(bf16[4,64,256]{2,1,0:T(8,128)(2,1)S(1)} %collective-permute-done.4) | copy-start | bytes 393220
  69.0 2.0 %copy-start.8 = (f32[4,256,256]{2,1,0:T(8,128)S(1)}, f32[4,256,256]{2,1,0:T(8,128)}, u32[]{:S(2)}) copy-start(f32[4,256,256]{2,1,0:T(8,128)} %get-tuple-element.41) | copy-start | bytes 3145732
  73.2 2.3 %collective-permute-start.7 = (f32[131072]{0:T(1024)}, f32[131072]{0:T(1024)}, u32[]{:S(2)}, u32[]{:S(2)}) collective-permute-start(f32[131072]{0:T(1024)} %broadcast_select_fusion.3), channel_id=1, source_target_pairs={{0,1},{1,0},{2,3},{3,2},{4,5},{5,4},{6,7},{7,6},{8,9},{9,8},{10,11... | collective-permute-start | bytes 1572872 | tf_op jit(solution)/shard_map/ppermute | solution.py:33
  77.3 8.4 %collective-permute-start.10 = (f32[32768]{0:T(1024)S(1)}, f32[32768]{0:T(1024)S(1)}, u32[]{:S(2)}, u32[]{:S(2)}) collective-permute-start(f32[32768]{0:T(1024)S(1)} %bitcast.232), channel_id=1, source_target_pairs={{0,6},{1,7},{2,0},{3,1},{4,2},{5,3},{6,4},{7,5},{8,14},{9,15},{10,... | collective-permute-start | bytes 393224 | tf_op jit(solution)/shard_map/ppermute | solution.py:37
  78.8 8.0 %collective-permute-start.8 = (f32[32768]{0:T(1024)S(1)}, f32[32768]{0:T(1024)S(1)}, u32[]{:S(2)}, u32[]{:S(2)}) collective-permute-start(f32[32768]{0:T(1024)S(1)} %bitcast.231), channel_id=1, source_target_pairs={{0,2},{1,3},{2,4},{3,5},{4,6},{5,7},{6,0},{7,1},{8,10},{9,11},{10,... | collective-permute-start | bytes 393224 | tf_op jit(solution)/shard_map/ppermute | solution.py:37
  79.6 14.1 %copy-start.27 = (s32[4,128]{1,0:T(4,128)S(1)}, s32[4,128]{1,0:T(4,128)}, u32[]{:S(2)}) copy-start(s32[4,128]{1,0:T(4,128)} %param.15) | copy-start | bytes 6148
  79.6 14.1 %copy-start.29 = (pred[4,128]{1,0:T(4,128)(4,1)S(1)}, pred[4,128]{1,0:T(4,128)(4,1)}, u32[]{:S(2)}) copy-start(pred[4,128]{1,0:T(4,128)(4,1)} %copy-done.28) | copy-start | bytes 1540
  79.7 8.1 %collective-permute-start.9 = (f32[32768]{0:T(1024)S(1)}, f32[32768]{0:T(1024)S(1)}, u32[]{:S(2)}, u32[]{:S(2)}) collective-permute-start(f32[32768]{0:T(1024)S(1)} %bitcast.230), channel_id=1, source_target_pairs={{0,4},{1,5},{2,6},{3,7},{4,0},{5,1},{6,2},{7,3},{8,12},{9,13},{10,... | collective-permute-start | bytes 393224 | tf_op jit(solution)/shard_map/ppermute | solution.py:37
  83.9 9.8 %collective-permute-start.14 = (bf16[4,128,256]{2,1,0:T(8,128)(2,1)}, bf16[4,128,256]{2,1,0:T(8,128)(2,1)}, u32[]{:S(2)}, u32[]{:S(2)}) collective-permute-start(bf16[4,128,256]{2,1,0:T(8,128)(2,1)} %slice.101), channel_id=1, source_target_pairs={{0,7},{1,0},{2,1},{3,2},{4,3},{5,4},{6,5},{7,6},{8,15},{9,8},{10,9... | collective-permute-start | bytes 786440 | tf_op jit(solution)/shard_map/ppermute | solution.py:12
  87.9 8.0 %collective-permute-start.11 = (f32[8192]{0:T(1024)S(1)}, f32[8192]{0:T(1024)S(1)}, u32[]{:S(2)}, u32[]{:S(2)}) collective-permute-start(f32[8192]{0:T(1024)S(1)} %bitcast.238), channel_id=1, source_target_pairs={{0,8},{8,16},{16,24},{24,0},{1,9},{9,17},{17,25},{25,1},{2,10},{10... | collective-permute-start | bytes 98312 | tf_op jit(solution)/shard_map/ppermute | solution.py:37
  91.3 4.8 %collective-permute-start.12 = (f32[8192]{0:T(1024)S(1)}, f32[8192]{0:T(1024)S(1)}, u32[]{:S(2)}, u32[]{:S(2)}) collective-permute-start(f32[8192]{0:T(1024)S(1)} %bitcast.237), channel_id=1, source_target_pairs={{0,16},{8,24},{16,0},{24,8},{1,17},{9,25},{17,1},{25,9},{2,18},{10... | collective-permute-start | bytes 98312 | tf_op jit(solution)/shard_map/ppermute | solution.py:37
  92.7 3.9 %collective-permute-start.13 = (f32[8192]{0:T(1024)S(1)}, f32[8192]{0:T(1024)S(1)}, u32[]{:S(2)}, u32[]{:S(2)}) collective-permute-start(f32[8192]{0:T(1024)S(1)} %bitcast.236), channel_id=1, source_target_pairs={{0,24},{8,0},{16,8},{24,16},{1,25},{9,1},{17,9},{25,17},{2,26},{10... | collective-permute-start | bytes 98312 | tf_op jit(solution)/shard_map/ppermute | solution.py:37
  96.7 5.8 %collective-permute-start.15 = (f32[8192]{0:T(1024)S(1)}, f32[8192]{0:T(1024)S(1)}, u32[]{:S(2)}, u32[]{:S(2)}) collective-permute-start(f32[8192]{0:T(1024)S(1)} %add_add_fusion.1), channel_id=1, source_target_pairs={{0,8},{8,16},{16,24},{24,0},{1,9},{9,17},{17,25},{25,1},{2,10},{10... | collective-permute-start | bytes 98312 | tf_op jit(solution)/shard_map/ppermute | solution.py:49
  97.1 5.4 %collective-permute-start.16 = (f32[8192]{0:T(1024)S(1)}, f32[8192]{0:T(1024)S(1)}, u32[]{:S(2)}, u32[]{:S(2)}) collective-permute-start(f32[8192]{0:T(1024)S(1)} %add_add_fusion.1), channel_id=1, source_target_pairs={{0,16},{8,24},{16,0},{24,8},{1,17},{9,25},{17,1},{25,9},{2,18},{10... | collective-permute-start | bytes 98312 | tf_op jit(solution)/shard_map/ppermute | solution.py:49
  100.1 3.9 %collective-permute-start.17 = (f32[8192]{0:T(1024)S(1)}, f32[8192]{0:T(1024)S(1)}, u32[]{:S(2)}, u32[]{:S(2)}) collective-permute-start(f32[8192]{0:T(1024)S(1)} %add_add_fusion.1), channel_id=1, source_target_pairs={{0,24},{8,0},{16,8},{24,16},{1,25},{9,1},{17,9},{25,17},{2,26},{10... | collective-permute-start | bytes 98312 | tf_op jit(solution)/shard_map/ppermute | solution.py:49
  104.8 6.0 %collective-permute-start.18 = (f32[32768]{0:T(1024)S(1)}, f32[32768]{0:T(1024)S(1)}, u32[]{:S(2)}, u32[]{:S(2)}) collective-permute-start(f32[32768]{0:T(1024)S(1)} %bitcast.221), channel_id=1, source_target_pairs={{0,2},{1,3},{2,4},{3,5},{4,6},{5,7},{6,0},{7,1},{8,10},{9,11},{10,... | collective-permute-start | bytes 393224 | tf_op jit(solution)/shard_map/ppermute | solution.py:49
  106.0 6.2 %collective-permute-start.19 = (f32[32768]{0:T(1024)S(1)}, f32[32768]{0:T(1024)S(1)}, u32[]{:S(2)}, u32[]{:S(2)}) collective-permute-start(f32[32768]{0:T(1024)S(1)} %bitcast.222), channel_id=1, source_target_pairs={{0,4},{1,5},{2,6},{3,7},{4,0},{5,1},{6,2},{7,3},{8,12},{9,13},{10,... | collective-permute-start | bytes 393224 | tf_op jit(solution)/shard_map/ppermute | solution.py:49
  106.6 5.6 %collective-permute-start.20 = (f32[32768]{0:T(1024)S(1)}, f32[32768]{0:T(1024)S(1)}, u32[]{:S(2)}, u32[]{:S(2)}) collective-permute-start(f32[32768]{0:T(1024)S(1)} %bitcast.223), channel_id=1, source_target_pairs={{0,6},{1,7},{2,0},{3,1},{4,2},{5,3},{6,4},{7,5},{8,14},{9,15},{10,... | collective-permute-start | bytes 393224 | tf_op jit(solution)/shard_map/ppermute | solution.py:49
  113.7 2.0 %collective-permute-start.21 = (f32[131072]{0:T(1024)S(1)}, f32[131072]{0:T(1024)S(1)}, u32[]{:S(2)}, u32[]{:S(2)}) collective-permute-start(f32[131072]{0:T(1024)S(1)} %bitcast.212), channel_id=1, source_target_pairs={{0,1},{1,0},{2,3},{3,2},{4,5},{5,4},{6,7},{7,6},{8,9},{9,8},{10,11... | collective-permute-start | bytes 1572872 | tf_op jit(solution)/shard_map/ppermute | solution.py:44
  (4 other events, 4.5 us)

commit v20 on v18

--- a/solution.py
+++ b/solution.py
@@ -323,13 +323,17 @@
     )
     agg_grad = jnp.einsum("drk,hk->drh", pre_grad, w_message, preferred_element_type=jnp.float32)
     term_grad = agg_grad * inverse[:, :, None]
+    high = term_grad.astype(jnp.bfloat16)
+    rest = term_grad - high.astype(jnp.float32)
+    middle = rest.astype(jnp.bfloat16)
+    low = (rest - middle.astype(jnp.float32)).astype(jnp.bfloat16)
     ext_grad = jnp.einsum(
         "drs,drh->dsh",
-        adjacent.astype(jnp.float32),
-        term_grad,
-        precision=lax.Precision.HIGHEST,
+        adjacent,
+        jnp.concatenate([high, middle, low], axis=2),
         preferred_element_type=jnp.float32,
     )
+    ext_grad = ext_grad[:, :, :width] + ext_grad[:, :, width : 2 * width] + ext_grad[:, :, 2 * width :]
     halo_grad = ext_grad[:, node_local:].astype(jnp.bfloat16)
     returned = from_behind(halo_grad, "dom", -1)
     own_grad = ext_grad[:, :node_local]

time: 105 us -> 112 us (1.067)
  starting transfers between devices: 31.5 us -> 24.7 us
  local copies, waits for them, and re-layouts: 10.7 us -> 17.2 us
  waiting for transfers between devices: 26.9 us -> 32.6 us
  matrix products: 23.2 us -> 27.4 us
  other arithmetic: 10.5 us -> 8.2 us
    ppermute x6, waiting for transfers between devices: 12.7 us -> 17.9 us  [exchange(): lax.ppermute(send, axis, [(i, (i + shift) % count) for i in range(count)])]
    ppermute x6, waiting for transfers between devices: 5.69 us -> 9.55 us  [_gather_step(): lax.ppermute(flat, axis, _group_pairs(axis, stride, group, shift))]
    ppermute x6, starting transfers between devices: 9.1 us -> 5.75 us  [_gather_step(): lax.ppermute(flat, axis, _group_pairs(axis, stride, group, shift))]
    dot_general x12, matrix products: 8.44 us -> 11.8 us  [contract(): return jnp.einsum(spec, left, right, preferred_element_type=jnp.float32)]
    add x0 -> x1, other arithmetic: none -> 2.68 us  [local(): ext_grad[:, :, :width] + ext_grad[:, :, width:2 * width]]
    dot_general x3, local copies, waits for them, and re-layouts: 0.69 us -> 3.36 us  [contract(): return jnp.einsum(spec, left, right, preferred_element_type=jnp.float32)]
    another operation x3, local copies, waits for them, and re-layouts: 0.78 us -> 3.23 us  [tree_sum(): flat = jnp.concatenate([value.reshape(-1) for value in values])]
    ppermute x6, starting transfers between devices: 9.36 us -> 6.97 us  [_scatter_step(): lax.ppermute(send, axis, _group_pairs(axis, stride, group, shift))]
  transfers between devices with their start and end apart: 22 -> 22, of which waited for: 17 -> 14; matrix products, arithmetic and copies ran while one was open for 15% -> 16% of each run, Pallas kernels for 0% -> 0%
where the time goes in v20:
time: 112 us
  waiting for transfers between devices  32.6 us (29%)
  matrix products  27.4 us (24%)
  starting transfers between devices  24.7 us (22%)
  local copies, waits for them, and re-layouts  17.2 us (15%)
  other arithmetic  8.2 us (7%)
  between operations  1.62 us (1%)
    ppermute x6, waiting for transfers between devices, exchange(): lax.ppermute(send, axis, [(i, (i + shift) % count) for i in range(count)])  17.9 us
    dot_general x12, matrix products, contract(): return jnp.einsum(spec, left, right, preferred_element_type=jnp.float32)  11.8 us
    ppermute x6, starting transfers between devices, exchange(): lax.ppermute(send, axis, [(i, (i + shift) % count) for i in range(count)])  10.1 us
    ppermute x6, waiting for transfers between devices, _gather_step(): lax.ppermute(flat, axis, _group_pairs(axis, stride, group, shift))  9.55 us
    ppermute x6, starting transfers between devices, _scatter_step(): lax.ppermute(send, axis, _group_pairs(axis, stride, group, shift))  6.97 us
    ppermute x6, starting transfers between devices, _gather_step(): lax.ppermute(flat, axis, _group_pairs(axis, stride, group, shift))  5.75 us
    dot_general x3, local copies, waits for them, and re-layouts, contract(): return jnp.einsum(spec, left, right, preferred_element_type=jnp.float32)  3.36 us
    another operation x3, local copies, waits for them, and re-layouts, tree_sum(): flat = jnp.concatenate([value.reshape(-1) for value in values])  3.23 us
  transfers between devices with their start and end apart: 22, of which 14 were waited for; matrix products, arithmetic and copies ran while one was open for 16% of the time, Pallas kernels for 0%

profile of v20, /device:TPU:0, one launch (start us, length us, event | category | flops | bytes accessed | tf_op | source)
XLA Modules:
  0.0 111.8 jit_solution(17954868240374388088)
XLA Ops:
  1.4 1.4 %convolution_convert_fusion.6 = bf16[4,128,256]{2,1,0:T(8,128)(2,1)S(1)} fusion(bf16[4,256,256]{2,1,0:T(8,128)(2,1)} %param.12, s32[4,128]{1,0:T(4,128)} %param.15, pred[4,128]{1,0:T(4,128)(4,1)S(1)} %iota_compare_fusion.10), kind=kOutput, calls=%fused_computation.53 | convolution fusion | flops 67502080 | bytes 788992 | tf_op jit(solution)/shard_map/dsn,dnh->dsh/dot_general | solution.py:283
  3.9 1.4 %fusion.3 = f32[1,4,256]{2,0,1:T(1,128)S(1)} fusion(s32[4,1024]{1,0:T(4,128)} %param.14), kind=kOutput, calls=%fused_computation.9 | convolution fusion | flops 3145728 | bytes 20480 | tf_op jit(solution)/shard_map/der,e->dr/dot_general | solution.py:294
  6.1 2.9 %fusion.17 = bf16[4,256,384]{2,1,0:T(8,128)(2,1)S(1)} fusion(s32[4,1024]{1,0:T(4,128)} %param.13, s32[4,1024]{1,0:T(4,128)} %param.14), kind=kOutput, calls=%fused_computation.29 | convolution fusion | flops 808321024 | bytes 819200 | tf_op jit(solution)/shard_map/der,des->drs/dot_general | solution.py:291
  9.0 1.3 %collective-permute-done = bf16[4,128,256]{2,1,0:T(8,128)(2,1)S(1)} collective-permute-done((bf16[4,128,256]{2,1,0:T(8,128)(2,1)S(1)}, bf16[4,128,256]{2,1,0:T(8,128)(2,1)S(1)}, u32[]{:S(2)}, u32[]{:S(2)}) %collective-permute-start) | collective-permute-done | bytes 262176 | tf_op jit(solution)/shard_map/ppermute | solution.py:12
  10.8 1.3 %fusion.26 = (bf16[4,256,256]{2,1,0:T(8,128)(2,1)S(1)}, f32[4,256,256]{2,1,0:T(8,128)}) fusion(bf16[4,256,256]{2,1,0:T(8,128)(2,1)S(1)} %copy-done.15, bf16[4,256,256]{2,1,0:T(8,128)(2,1)S(1)} %fusion.21, bf16[256,256]{1,0:T(8,128)(2,1)S(1)} %copy-done), kind=kOutput, calls=%fused_computation.58 | convolution fusion | flops 136052736 | bytes 2752512 | tf_op jit(solution)/shard_map/drh,hk->drk/dot_general | solution.py:306
  12.1 4.4 %collective-permute-start.3 = (bf16[4,64,256]{2,1,0:T(8,128)(2,1)S(1)}, bf16[4,64,256]{2,1,0:T(8,128)(2,1)S(1)}, u32[]{:S(2)}, u32[]{:S(2)}) collective-permute-start(bf16[4,64,256]{2,1,0:T(8,128)(2,1)S(1)} %get-tuple-element.34), channel_id=1, source_target_pairs={{0,24},{8,0},{16,8},{24,16},{1,25},{9,1},{17,9},{25,17},{2,26},{10... | collective-permute-start | bytes 393224 | tf_op jit(solution)/shard_map/ppermute | solution.py:97
  16.6 1.0 collective-permute-start.1
  19.5 0.9 collective-permute-done.3
  20.5 8.3 %collective-permute-done.2 = bf16[4,64,256]{2,1,0:T(8,128)(2,1)S(1)} collective-permute-done((bf16[4,64,256]{2,1,0:T(8,128)(2,1)S(1)}, bf16[4,64,256]{2,1,0:T(8,128)(2,1)S(1)}, u32[]{:S(2)}, u32[]{:S(2)}) %collective-permute-start.2) | collective-permute-done | bytes 131104 | tf_op jit(solution)/shard_map/ppermute | solution.py:97
  30.7 2.0 %fusion.25 = f32[8,4,128,128]{3,2,1,0:T(8,128)} fusion(bf16[8,128,4,64]{1,3,2,0:T(8,128)(2,1)S(1)} %copy.35, bf16[8,128,256,1]{2,1,3,0:T(8,128)(2,1)S(1)} %bitcast.191, bf16[256,4,64,1]{0,2,1,3:T(8,128)(2,1)S(1)} %bitcast.199), kind=kOutput, calls=%fused_computation.52 | convolution fusion | flops 201588736 | bytes 3276800 | tf_op jit(solution)/shard_map/gihd,ghjd->ghij/dot_general | solution.py:227
  32.7 2.2 %fusion.68 = (f32[8,4,128]{2,1,0:T(4,128)S(1)}, f32[8,4,128,128]{2,3,1,0:T(8,128)}) fusion(pred[128,128]{0,1:T(8,128)(4,1)S(1)} %copy-done.21, bf16[8,4,128,64]{2,3,1,0:T(8,128)(2,1)S(1)} %fusion.22, bf16[8,4,128,64]{2,3,1,0:T(8,128)(2,1)S(1)} %fusion.23), kind=kOutput, calls=%fused_computation.184 | convolution fusion | flops 69206144 | bytes 3178496 | tf_op jit(solution)/shard_map/sub | solution.py:240
  34.9 2.6 %convolution_convert_fusion.4 = bf16[8,4,128,64]{2,3,1,0:T(8,128)(2,1)S(1)} fusion(bf16[8,128,4,64]{1,3,2,0:T(8,128)(2,1)S(1)} %copy.35, f32[8,4,128,128]{2,3,1,0:T(8,128)} %get-tuple-element.46, f32[8,4,128]{2,1,0:T(4,128)S(1)} %get-tuple-element.45), kind=kOutput, calls=%fused_computation.47 | convolution fusion | flops 68419584 | bytes 3162112 | tf_op jit(solution)/shard_map/ghij,gihd->ghjd/dot_general | solution.py:227
  37.5 1.0 convolution_bitcast_fusion.3
  39.8 0.8 convolution_convert_fusion.5
  40.6 1.0 convolution_bitcast_fusion.4
  42.0 1.2 %convolution_convert_fusion.3 = bf16[8,4,128,64]{2,3,1,0:T(8,128)(2,1)} fusion(bf16[8,4,128,64]{2,3,1,0:T(8,128)(2,1)S(1)} %copy-done.5, bf16[8,4,128,128]{2,3,1,0:T(8,128)(2,1)S(1)} %fusion.7), kind=kOutput, calls=%fused_computation.46 | convolution fusion | flops 67371008 | bytes 2097152 | tf_op jit(solution)/shard_map/ghij,ghjd->ghid/dot_general | solution.py:227
  43.2 1.2 %copy.45 = f32[256,4,64]{2,1,0:T(4,128)S(1)} copy(f32[256,4,64]{0,2,1:T(8,128)} %convolution_bitcast_fusion.4) | data formatting | bytes 524288 | tf_op jit(solution)/shard_map/gic,ghid->chd/dot_general | solution.py:227
  44.4 1.0 reshape_reshape.14
  45.4 1.0 constant_dynamic-update-slice_fusion.3
  46.3 2.0 %copy.47 = f32[256,4,64]{2,1,0:T(4,128)} copy(f32[256,4,64]{0,2,1:T(8,128)} %convolution_bitcast_fusion.3) | data formatting | bytes 524288 | tf_op jit(solution)/shard_map/gic,ghid->chd/dot_general | solution.py:227
  48.3 2.0 %reshape_reshape.15 = f32[65536]{0:T(1024)} reshape(f32[256,4,64]{2,1,0:T(4,128)} %copy.47) | data formatting | bytes 524288 | tf_op jit(solution)/shard_map/reshape;reshape | solution.py:64
  50.3 1.4 %fusion.20 = f32[8,128,256]{2,1,0:T(8,128)S(1)} fusion(f32[8,128,256]{2,1,0:T(8,128)S(1)} %convolution_bitcast_fusion, f32[8,128,256]{2,1,0:T(8,128)S(1)} %convolution_bitcast_fusion.1, bf16[8,4,128,64]{2,3,1,0:T(8,128)(2,1)} %convolution_convert_fusion.3, bf16[256,4,64,1]{0,2,1,3:T(8,128)(2,1)S(1)} %bitcast.202), kind=kOutput, calls=%fused_computation.41 | convolution fusion | flops 134742016 | bytes 3801088 | tf_op jit(solution)/shard_map/ghid,chd->gic/dot_general | solution.py:227
  52.5 1.4 %collective-permute-start.6 = (bf16[4,64,256]{2,1,0:T(8,128)(2,1)S(1)}, bf16[4,64,256]{2,1,0:T(8,128)(2,1)S(1)}, u32[]{:S(2)}, u32[]{:S(2)}) collective-permute-start(bf16[4,64,256]{2,1,0:T(8,128)(2,1)S(1)} %get-tuple-element.26), channel_id=1, source_target_pairs={{0,24},{8,0},{16,8},{24,16},{1,25},{9,1},{17,9},{25,17},{2,26},{10... | collective-permute-start | bytes 393224 | tf_op jit(solution)/shard_map/ppermute | solution.py:97
  53.8 1.4 %collective-permute-start.5 = (bf16[4,64,256]{2,1,0:T(8,128)(2,1)S(1)}, bf16[4,64,256]{2,1,0:T(8,128)(2,1)S(1)}, u32[]{:S(2)}, u32[]{:S(2)}) collective-permute-start(bf16[4,64,256]{2,1,0:T(8,128)(2,1)S(1)} %get-tuple-element.27), channel_id=1, source_target_pairs={{0,16},{8,24},{16,0},{24,8},{1,17},{9,25},{17,1},{25,9},{2,18},{10... | collective-permute-start | bytes 393224 | tf_op jit(solution)/shard_map/ppermute | solution.py:97
  55.2 1.9 %collective-permute-start.4 = (bf16[4,64,256]{2,1,0:T(8,128)(2,1)S(1)}, bf16[4,64,256]{2,1,0:T(8,128)(2,1)S(1)}, u32[]{:S(2)}, u32[]{:S(2)}) collective-permute-start(bf16[4,64,256]{2,1,0:T(8,128)(2,1)S(1)} %get-tuple-element.28), channel_id=1, source_target_pairs={{0,8},{8,16},{16,24},{24,0},{1,9},{9,17},{17,25},{25,1},{2,10},{10... | collective-permute-start | bytes 393224 | tf_op jit(solution)/shard_map/ppermute | solution.py:97
  58.3 8.4 %collective-permute-done.5 = bf16[4,64,256]{2,1,0:T(8,128)(2,1)S(1)} collective-permute-done((bf16[4,64,256]{2,1,0:T(8,128)(2,1)S(1)}, bf16[4,64,256]{2,1,0:T(8,128)(2,1)S(1)}, u32[]{:S(2)}, u32[]{:S(2)}) %collective-permute-start.5) | collective-permute-done | bytes 131104 | tf_op jit(solution)/shard_map/ppermute | solution.py:97
  70.2 3.0 %fusion.11 = f32[4,384,768]{2,1,0:T(8,128)} fusion(bf16[4,256,384]{2,1,0:T(8,128)(2,1)S(1)} %copy-done.14, bf16[4,256,256]{2,1,0:T(8,128)(2,1)S(1)} %get-tuple-element.15, bf16[4,256,256]{2,1,0:T(8,128)(2,1)S(1)} %get-tuple-element.16, bf16[4,256,256]{2,1,0:T(8,128)(2,1)S(1)} %get-tuple-element.14), kind=kOutput, calls=%fused_computation.23 | convolution fusion | flops 608698368 | bytes 7077888 | tf_op jit(solution)/shard_map/drs,drh->dsh/dot_general | solution.py:330
  74.0 1.4 %collective-permute-start.10 = (f32[32768]{0:T(1024)S(1)}, f32[32768]{0:T(1024)S(1)}, u32[]{:S(2)}, u32[]{:S(2)}) collective-permute-start(f32[32768]{0:T(1024)S(1)} %bitcast.219), channel_id=1, source_target_pairs={{0,6},{1,7},{2,0},{3,1},{4,2},{5,3},{6,4},{7,5},{8,14},{9,15},{10,... | collective-permute-start | bytes 393224 | tf_op jit(solution)/shard_map/ppermute | solution.py:37
  75.3 1.9 %collective-permute-start.9 = (f32[32768]{0:T(1024)S(1)}, f32[32768]{0:T(1024)S(1)}, u32[]{:S(2)}, u32[]{:S(2)}) collective-permute-start(f32[32768]{0:T(1024)S(1)} %bitcast.217), channel_id=1, source_target_pairs={{0,4},{1,5},{2,6},{3,7},{4,0},{5,1},{6,2},{7,3},{8,12},{9,13},{10,... | collective-permute-start | bytes 393224 | tf_op jit(solution)/shard_map/ppermute | solution.py:37
  77.6 2.7 %slice_add_fusion = f32[4,384,256]{2,1,0:T(8,128)S(1)} fusion(f32[4,384,768]{2,1,0:T(8,128)} %fusion.11), kind=kLoop, calls=%fused_computation.21 | loop fusion | flops 786432 | bytes 6291456 | tf_op jit(solution)/shard_map/add | solution.py:336
  81.0 1.3 %collective-permute-start.14 = (bf16[4,128,256]{2,1,0:T(8,128)(2,1)}, bf16[4,128,256]{2,1,0:T(8,128)(2,1)}, u32[]{:S(2)}, u32[]{:S(2)}) collective-permute-start(bf16[4,128,256]{2,1,0:T(8,128)(2,1)} %slice.121), channel_id=1, source_target_pairs={{0,7},{1,0},{2,1},{3,2},{4,3},{5,4},{6,5},{7,6},{8,15},{9,8},{10,9... | collective-permute-start | bytes 786440 | tf_op jit(solution)/shard_map/ppermute | solution.py:12
  82.3 1.0 collective-permute-done.9
  83.6 1.3 %collective-permute-start.12 = (f32[8192]{0:T(1024)S(1)}, f32[8192]{0:T(1024)S(1)}, u32[]{:S(2)}, u32[]{:S(2)}) collective-permute-start(f32[8192]{0:T(1024)S(1)} %bitcast.225), channel_id=1, source_target_pairs={{0,16},{8,24},{16,0},{24,8},{1,17},{9,25},{17,1},{25,9},{2,18},{10... | collective-permute-start | bytes 98312 | tf_op jit(solution)/shard_map/ppermute | solution.py:37
  84.9 1.9 %collective-permute-start.11 = (f32[8192]{0:T(1024)S(1)}, f32[8192]{0:T(1024)S(1)}, u32[]{:S(2)}, u32[]{:S(2)}) collective-permute-start(f32[8192]{0:T(1024)S(1)} %bitcast.224), channel_id=1, source_target_pairs={{0,8},{8,16},{16,24},{24,0},{1,9},{9,17},{17,25},{25,1},{2,10},{10... | collective-permute-start | bytes 98312 | tf_op jit(solution)/shard_map/ppermute | solution.py:37
  86.9 2.2 %convolution_add_fusion.1 = f32[4,256,256]{2,1,0:T(8,128)} fusion(bf16[4,128,256]{2,1,0:T(8,128)(2,1)} %collective-permute-done.14, f32[4,256,256]{2,1,0:T(8,128)S(1)} %get-tuple-element.47, f32[4,384,256]{2,1,0:T(8,128)S(1)} %slice_add_fusion, s32[4,128]{1,0:T(4,128)S(1)} %copy-done.22, pred[4,128]{1,0:T(4,128)(4,1)S(1)} %copy-done.25, ...), kind=kOutput, calls=%fused_computation.35 | convolution fusion | flops 70254592 | bytes 3934720 | tf_op jit(solution)/shard_map/dsn,dsh->dnh/dot_general | solution.py:340
  89.1 1.5 %collective-permute-done.11 = f32[8192]{0:T(1024)S(1)} collective-permute-done((f32[8192]{0:T(1024)S(1)}, f32[8192]{0:T(1024)S(1)}, u32[]{:S(2)}, u32[]{:S(2)}) %collective-permute-start.11) | collective-permute-done | bytes 32800 | tf_op jit(solution)/shard_map/ppermute | solution.py:37
  90.7 1.3 %collective-permute-start.17 = (f32[8192]{0:T(1024)S(1)}, f32[8192]{0:T(1024)S(1)}, u32[]{:S(2)}, u32[]{:S(2)}) collective-permute-start(f32[8192]{0:T(1024)S(1)} %add_add_fusion.1), channel_id=1, source_target_pairs={{0,24},{8,0},{16,8},{24,16},{1,25},{9,1},{17,9},{25,17},{2,26},{10... | collective-permute-start | bytes 98312 | tf_op jit(solution)/shard_map/ppermute | solution.py:49
  92.9 1.7 %collective-permute-done.17 = f32[8192]{0:T(1024)S(1)} collective-permute-done((f32[8192]{0:T(1024)S(1)}, f32[8192]{0:T(1024)S(1)}, u32[]{:S(2)}, u32[]{:S(2)}) %collective-permute-start.17) | collective-permute-done | bytes 32800 | tf_op jit(solution)/shard_map/ppermute | solution.py:49
  94.6 2.5 %collective-permute-done.16 = f32[8192]{0:T(1024)S(1)} collective-permute-done((f32[8192]{0:T(1024)S(1)}, f32[8192]{0:T(1024)S(1)}, u32[]{:S(2)}, u32[]{:S(2)}) %collective-permute-start.16) | collective-permute-done | bytes 32800 | tf_op jit(solution)/shard_map/ppermute | solution.py:49
  97.1 0.9 collective-permute-done.15
  98.9 1.2 %collective-permute-start.20 = (f32[32768]{0:T(1024)S(1)}, f32[32768]{0:T(1024)S(1)}, u32[]{:S(2)}, u32[]{:S(2)}) collective-permute-start(f32[32768]{0:T(1024)S(1)} %bitcast.207), channel_id=1, source_target_pairs={{0,6},{1,7},{2,0},{3,1},{4,2},{5,3},{6,4},{7,5},{8,14},{9,15},{10,... | collective-permute-start | bytes 393224 | tf_op jit(solution)/shard_map/ppermute | solution.py:49
  100.2 1.0 collective-permute-start.19
  101.2 1.2 %collective-permute-start.18 = (f32[32768]{0:T(1024)S(1)}, f32[32768]{0:T(1024)S(1)}, u32[]{:S(2)}, u32[]{:S(2)}) collective-permute-start(f32[32768]{0:T(1024)S(1)} %bitcast.209), channel_id=1, source_target_pairs={{0,2},{1,3},{2,4},{3,5},{4,6},{5,7},{6,0},{7,1},{8,10},{9,11},{10,... | collective-permute-start | bytes 393224 | tf_op jit(solution)/shard_map/ppermute | solution.py:49
  102.6 2.2 %collective-permute-done.20 = f32[32768]{0:T(1024)S(1)} collective-permute-done((f32[32768]{0:T(1024)S(1)}, f32[32768]{0:T(1024)S(1)}, u32[]{:S(2)}, u32[]{:S(2)}) %collective-permute-start.20) | collective-permute-done | bytes 131104 | tf_op jit(solution)/shard_map/ppermute | solution.py:49
  105.1 1.9 %collective-permute-done.18 = f32[32768]{0:T(1024)S(1)} collective-permute-done((f32[32768]{0:T(1024)S(1)}, f32[32768]{0:T(1024)S(1)}, u32[]{:S(2)}, u32[]{:S(2)}) %collective-permute-start.18) | collective-permute-done | bytes 131104 | tf_op jit(solution)/shard_map/ppermute | solution.py:49
  107.5 0.8 gather_fusion.1
  109.2 1.3 %collective-permute-done.21 = f32[131072]{0:T(1024)S(1)} collective-permute-done((f32[131072]{0:T(1024)S(1)}, f32[131072]{0:T(1024)S(1)}, u32[]{:S(2)}, u32[]{:S(2)}) %collective-permute-start.21) | collective-permute-done | bytes 524320 | tf_op jit(solution)/shard_map/ppermute | solution.py:44
  110.8 1.0 fusion.66
  (141 shorter events, 19.5 us)
Async XLA Ops:
  0.6 10.1 %copy-start = (bf16[256,256]{1,0:T(8,128)(2,1)S(1)}, bf16[256,256]{1,0:T(8,128)(2,1)}, u32[]{:S(2)}) copy-start(bf16[256,256]{1,0:T(8,128)(2,1)} %param.17) | copy-start | bytes 393220
  1.4 1.9 %copy-start.24 = (pred[4,128]{1,0:T(4,128)(4,1)}, pred[4,128]{1,0:T(4,128)(4,1)S(1)}, u32[]{:S(2)}) copy-start(pred[4,128]{1,0:T(4,128)(4,1)S(1)} %iota_compare_fusion.10) | copy-start | bytes 1540
  2.8 7.4 %collective-permute-start = (bf16[4,128,256]{2,1,0:T(8,128)(2,1)S(1)}, bf16[4,128,256]{2,1,0:T(8,128)(2,1)S(1)}, u32[]{:S(2)}, u32[]{:S(2)}) collective-permute-start(bf16[4,128,256]{2,1,0:T(8,128)(2,1)S(1)} %convolution_convert_fusion.6), channel_id=1, source_target_pairs={{0,1},{1,2},{2,3},{3,4},{4,5},{5,6},{6,7},{7,0},{8,9},{9,10},{10,1... | collective-permute-start | bytes 786440 | tf_op jit(solution)/shard_map/ppermute | solution.py:12
  6.1 4.2 %copy-start.15 = (bf16[4,256,256]{2,1,0:T(8,128)(2,1)S(1)}, bf16[4,256,256]{2,1,0:T(8,128)(2,1)}, u32[]{:S(2)}) copy-start(bf16[4,256,256]{2,1,0:T(8,128)(2,1)} %param.12) | copy-start | bytes 1572868
  8.9 3.2 %copy-start.13 = (bf16[4,256,384]{2,1,0:T(8,128)(2,1)}, bf16[4,256,384]{2,1,0:T(8,128)(2,1)S(1)}, u32[]{:S(2)}) copy-start(bf16[4,256,384]{2,1,0:T(8,128)(2,1)S(1)} %fusion.17) | copy-start | bytes 2359300
  10.7 1.4 %copy-start.16 = (bf16[4,256,256]{2,1,0:T(8,128)(2,1)}, bf16[4,256,256]{2,1,0:T(8,128)(2,1)S(1)}, u32[]{:S(2)}) copy-start(bf16[4,256,256]{2,1,0:T(8,128)(2,1)S(1)} %fusion.21) | copy-start | bytes 1572868
  10.8 7.0 %copy-start.2 = (bf16[16,1,1,64,256]{4,3,2,1,0:T(8,128)(2,1)S(1)}, bf16[16,1,1,64,256]{4,3,2,1,0:T(8,128)(2,1)}, u32[]{:S(2)}) copy-start(bf16[16,1,1,64,256]{4,3,2,1,0:T(8,128)(2,1)} %param.21) | copy-start | bytes 1572868
  12.1 8.3 %collective-permute-start.3 = (bf16[4,64,256]{2,1,0:T(8,128)(2,1)S(1)}, bf16[4,64,256]{2,1,0:T(8,128)(2,1)S(1)}, u32[]{:S(2)}, u32[]{:S(2)}) collective-permute-start(bf16[4,64,256]{2,1,0:T(8,128)(2,1)S(1)} %get-tuple-element.34), channel_id=1, source_target_pairs={{0,24},{8,0},{16,8},{24,16},{1,25},{9,1},{17,9},{25,17},{2,26},{10... | collective-permute-start | bytes 393224 | tf_op jit(solution)/shard_map/ppermute | solution.py:97
  16.6 12.2 %collective-permute-start.2 = (bf16[4,64,256]{2,1,0:T(8,128)(2,1)S(1)}, bf16[4,64,256]{2,1,0:T(8,128)(2,1)S(1)}, u32[]{:S(2)}, u32[]{:S(2)}) collective-permute-start(bf16[4,64,256]{2,1,0:T(8,128)(2,1)S(1)} %get-tuple-element.35), channel_id=1, source_target_pairs={{0,16},{8,24},{16,0},{24,8},{1,17},{9,25},{17,1},{25,9},{2,18},{10... | collective-permute-start | bytes 393224 | tf_op jit(solution)/shard_map/ppermute | solution.py:97
  16.6 12.2 %collective-permute-start.1 = (bf16[4,64,256]{2,1,0:T(8,128)(2,1)S(1)}, bf16[4,64,256]{2,1,0:T(8,128)(2,1)S(1)}, u32[]{:S(2)}, u32[]{:S(2)}) collective-permute-start(bf16[4,64,256]{2,1,0:T(8,128)(2,1)S(1)} %get-tuple-element.36), channel_id=1, source_target_pairs={{0,8},{8,16},{16,24},{24,0},{1,9},{9,17},{17,25},{25,1},{2,10},{10... | collective-permute-start | bytes 393224 | tf_op jit(solution)/shard_map/ppermute | solution.py:97
  17.8 1.3 %copy-start.18 = (bf16[256,256]{1,0:T(8,128)(2,1)S(1)}, bf16[256,256]{1,0:T(8,128)(2,1)}, u32[]{:S(2)}) copy-start(bf16[256,256]{1,0:T(8,128)(2,1)} %param.20) | copy-start | bytes 393220
  17.8 1.4 %copy-start.19 = (bf16[256,256]{1,0:T(8,128)(2,1)S(1)}, bf16[256,256]{1,0:T(8,128)(2,1)}, u32[]{:S(2)}) copy-start(bf16[256,256]{1,0:T(8,128)(2,1)} %param.18) | copy-start | bytes 393220
  18.1 1.2 %copy-start.20 = (bf16[256,256]{1,0:T(8,128)(2,1)S(1)}, bf16[256,256]{1,0:T(8,128)(2,1)}, u32[]{:S(2)}) copy-start(bf16[256,256]{1,0:T(8,128)(2,1)} %param.19) | copy-start | bytes 393220
  30.3 2.4 %copy-start.21 = (pred[128,128]{0,1:T(8,128)(4,1)S(1)}, pred[128,128]{0,1:T(8,128)(4,1)}, u32[]{:S(2)}) copy-start(pred[128,128]{0,1:T(8,128)(4,1)} %compare_and_fusion) | copy-start | bytes 49156
  30.6 4.3 %copy-start.4 = (bf16[8,4,128,64]{2,3,1,0:T(8,128)(2,1)}, bf16[8,4,128,64]{2,3,1,0:T(8,128)(2,1)S(1)}, u32[]{:S(2)}) copy-start(bf16[8,4,128,64]{2,3,1,0:T(8,128)(2,1)S(1)} %fusion.23) | copy-start | bytes 1572868
  34.9 3.9 %copy-start.26 = (f32[8,4,128,128]{2,3,1,0:T(8,128)S(1)}, f32[8,4,128,128]{2,3,1,0:T(8,128)}, u32[]{:S(2)}) copy-start(f32[8,4,128,128]{2,3,1,0:T(8,128)} %get-tuple-element.46) | copy-start | bytes 6291460
  37.5 1.7 %copy-start.1 = (f32[8,4,128,128]{3,2,1,0:T(8,128)S(1)}, f32[8,4,128,128]{3,2,1,0:T(8,128)}, u32[]{:S(2)}) copy-start(f32[8,4,128,128]{3,2,1,0:T(8,128)} %fusion.25) | copy-start | bytes 6291460
  40.6 1.4 %copy-start.5 = (bf16[8,4,128,64]{2,3,1,0:T(8,128)(2,1)S(1)}, bf16[8,4,128,64]{2,3,1,0:T(8,128)(2,1)}, u32[]{:S(2)}) copy-start(bf16[8,4,128,64]{2,3,1,0:T(8,128)(2,1)} %copy-done.4) | copy-start | bytes 1572868
  50.3 1.5 %copy-start.3 = (bf16[16,1,1,64,256]{4,3,2,1,0:T(8,128)(2,1)S(1)}, bf16[16,1,1,64,256]{4,3,2,1,0:T(8,128)(2,1)}, u32[]{:S(2)}) copy-start(bf16[16,1,1,64,256]{4,3,2,1,0:T(8,128)(2,1)} %param.21) | copy-start | bytes 1572868
  51.7 5.4 %copy-start.11 = (f32[65536]{0:T(1024)S(1)}, f32[65536]{0:T(1024)}, u32[]{:S(2)}) copy-start(f32[65536]{0:T(1024)} %reshape_reshape.15) | copy-start | bytes 786436
  51.7 5.4 %copy-start.6 = (bf16[8,4,128,64]{2,3,1,0:T(8,128)(2,1)S(1)}, bf16[8,4,128,64]{2,3,1,0:T(8,128)(2,1)}, u32[]{:S(2)}) copy-start(bf16[8,4,128,64]{2,3,1,0:T(8,128)(2,1)} %convolution_convert_fusion.3) | copy-start | bytes 1572868
  52.5 5.8 %collective-permute-start.6 = (bf16[4,64,256]{2,1,0:T(8,128)(2,1)S(1)}, bf16[4,64,256]{2,1,0:T(8,128)(2,1)S(1)}, u32[]{:S(2)}, u32[]{:S(2)}) collective-permute-start(bf16[4,64,256]{2,1,0:T(8,128)(2,1)S(1)} %get-tuple-element.26), channel_id=1, source_target_pairs={{0,24},{8,0},{16,8},{24,16},{1,25},{9,1},{17,9},{25,17},{2,26},{10... | collective-permute-start | bytes 393224 | tf_op jit(solution)/shard_map/ppermute | solution.py:97
  53.8 12.8 %collective-permute-start.5 = (bf16[4,64,256]{2,1,0:T(8,128)(2,1)S(1)}, bf16[4,64,256]{2,1,0:T(8,128)(2,1)S(1)}, u32[]{:S(2)}, u32[]{:S(2)}) collective-permute-start(bf16[4,64,256]{2,1,0:T(8,128)(2,1)S(1)} %get-tuple-element.27), channel_id=1, source_target_pairs={{0,16},{8,24},{16,0},{24,8},{1,17},{9,25},{17,1},{25,9},{2,18},{10... | collective-permute-start | bytes 393224 | tf_op jit(solution)/shard_map/ppermute | solution.py:97
  55.2 11.5 %collective-permute-start.4 = (bf16[4,64,256]{2,1,0:T(8,128)(2,1)S(1)}, bf16[4,64,256]{2,1,0:T(8,128)(2,1)S(1)}, u32[]{:S(2)}, u32[]{:S(2)}) collective-permute-start(bf16[4,64,256]{2,1,0:T(8,128)(2,1)S(1)} %get-tuple-element.28), channel_id=1, source_target_pairs={{0,8},{8,16},{16,24},{24,0},{1,9},{9,17},{17,25},{25,1},{2,10},{10... | collective-permute-start | bytes 393224 | tf_op jit(solution)/shard_map/ppermute | solution.py:97
  66.7 1.2 %copy-start.12 = (f32[4,256,256]{2,1,0:T(8,128)S(1)}, f32[4,256,256]{2,1,0:T(8,128)}, u32[]{:S(2)}) copy-start(f32[4,256,256]{2,1,0:T(8,128)} %get-tuple-element.44) | copy-start | bytes 3145732
  67.5 1.5 %copy-start.7 = (bf16[4,64,256]{2,1,0:T(8,128)(2,1)}, bf16[4,64,256]{2,1,0:T(8,128)(2,1)S(1)}, u32[]{:S(2)}) copy-start(bf16[4,64,256]{2,1,0:T(8,128)(2,1)S(1)} %get-tuple-element.23) | copy-start | bytes 393220
  67.5 1.5 %copy-start.9 = (bf16[4,64,256]{2,1,0:T(8,128)(2,1)}, bf16[4,64,256]{2,1,0:T(8,128)(2,1)S(1)}, u32[]{:S(2)}) copy-start(bf16[4,64,256]{2,1,0:T(8,128)(2,1)S(1)} %get-tuple-element.24) | copy-start | bytes 393220
  69.0 1.1 %copy-start.14 = (bf16[4,256,384]{2,1,0:T(8,128)(2,1)S(1)}, bf16[4,256,384]{2,1,0:T(8,128)(2,1)}, u32[]{:S(2)}) copy-start(bf16[4,256,384]{2,1,0:T(8,128)(2,1)} %copy-done.13) | copy-start | bytes 2359300
  69.1 4.1 %collective-permute-start.7 = (f32[131072]{0:T(1024)S(1)}, f32[131072]{0:T(1024)S(1)}, u32[]{:S(2)}, u32[]{:S(2)}) collective-permute-start(f32[131072]{0:T(1024)S(1)} %broadcast_select_fusion.3), channel_id=1, source_target_pairs={{0,1},{1,0},{2,3},{3,2},{4,5},{5,4},{6,7},{7,6},{8,9},{9,8},{10,11... | collective-permute-start | bytes 1572872 | tf_op jit(solution)/shard_map/ppermute | solution.py:33
  74.0 8.3 %collective-permute-start.10 = (f32[32768]{0:T(1024)S(1)}, f32[32768]{0:T(1024)S(1)}, u32[]{:S(2)}, u32[]{:S(2)}) collective-permute-start(f32[32768]{0:T(1024)S(1)} %bitcast.219), channel_id=1, source_target_pairs={{0,6},{1,7},{2,0},{3,1},{4,2},{5,3},{6,4},{7,5},{8,14},{9,15},{10,... | collective-permute-start | bytes 393224 | tf_op jit(solution)/shard_map/ppermute | solution.py:37
  75.3 8.0 %collective-permute-start.9 = (f32[32768]{0:T(1024)S(1)}, f32[32768]{0:T(1024)S(1)}, u32[]{:S(2)}, u32[]{:S(2)}) collective-permute-start(f32[32768]{0:T(1024)S(1)} %bitcast.217), channel_id=1, source_target_pairs={{0,4},{1,5},{2,6},{3,7},{4,0},{5,1},{6,2},{7,3},{8,12},{9,13},{10,... | collective-permute-start | bytes 393224 | tf_op jit(solution)/shard_map/ppermute | solution.py:37
  77.2 9.7 %copy-start.8 = (bf16[4,64,256]{2,1,0:T(8,128)(2,1)S(1)}, bf16[4,64,256]{2,1,0:T(8,128)(2,1)}, u32[]{:S(2)}) copy-start(bf16[4,64,256]{2,1,0:T(8,128)(2,1)} %copy-done.7) | copy-start | bytes 393220
  77.2 9.7 %copy-start.10 = (bf16[4,64,256]{2,1,0:T(8,128)(2,1)S(1)}, bf16[4,64,256]{2,1,0:T(8,128)(2,1)}, u32[]{:S(2)}) copy-start(bf16[4,64,256]{2,1,0:T(8,128)(2,1)} %copy-done.9) | copy-start | bytes 393220
  77.2 9.7 %copy-start.22 = (s32[4,128]{1,0:T(4,128)S(1)}, s32[4,128]{1,0:T(4,128)}, u32[]{:S(2)}) copy-start(s32[4,128]{1,0:T(4,128)} %param.15) | copy-start | bytes 6148
  77.2 9.7 %copy-start.25 = (pred[4,128]{1,0:T(4,128)(4,1)S(1)}, pred[4,128]{1,0:T(4,128)(4,1)}, u32[]{:S(2)}) copy-start(pred[4,128]{1,0:T(4,128)(4,1)} %copy-done.24) | copy-start | bytes 1540
  77.2 6.1 %collective-permute-start.8 = (f32[32768]{0:T(1024)S(1)}, f32[32768]{0:T(1024)S(1)}, u32[]{:S(2)}, u32[]{:S(2)}) collective-permute-start(f32[32768]{0:T(1024)S(1)} %bitcast.215), channel_id=1, source_target_pairs={{0,2},{1,3},{2,4},{3,5},{4,6},{5,7},{6,0},{7,1},{8,10},{9,11},{10,... | collective-permute-start | bytes 393224 | tf_op jit(solution)/shard_map/ppermute | solution.py:37
  81.0 5.9 %collective-permute-start.14 = (bf16[4,128,256]{2,1,0:T(8,128)(2,1)}, bf16[4,128,256]{2,1,0:T(8,128)(2,1)}, u32[]{:S(2)}, u32[]{:S(2)}) collective-permute-start(bf16[4,128,256]{2,1,0:T(8,128)(2,1)} %slice.121), channel_id=1, source_target_pairs={{0,7},{1,0},{2,1},{3,2},{4,3},{5,4},{6,5},{7,6},{8,15},{9,8},{10,9... | collective-permute-start | bytes 786440 | tf_op jit(solution)/shard_map/ppermute | solution.py:12
  83.5 5.6 %collective-permute-start.13 = (f32[8192]{0:T(1024)S(1)}, f32[8192]{0:T(1024)S(1)}, u32[]{:S(2)}, u32[]{:S(2)}) collective-permute-start(f32[8192]{0:T(1024)S(1)} %bitcast.226), channel_id=1, source_target_pairs={{0,24},{8,0},{16,8},{24,16},{1,25},{9,1},{17,9},{25,17},{2,26},{10... | collective-permute-start | bytes 98312 | tf_op jit(solution)/shard_map/ppermute | solution.py:37
  83.6 5.5 %collective-permute-start.12 = (f32[8192]{0:T(1024)S(1)}, f32[8192]{0:T(1024)S(1)}, u32[]{:S(2)}, u32[]{:S(2)}) collective-permute-start(f32[8192]{0:T(1024)S(1)} %bitcast.225), channel_id=1, source_target_pairs={{0,16},{8,24},{16,0},{24,8},{1,17},{9,25},{17,1},{25,9},{2,18},{10... | collective-permute-start | bytes 98312 | tf_op jit(solution)/shard_map/ppermute | solution.py:37
  84.9 5.7 %collective-permute-start.11 = (f32[8192]{0:T(1024)S(1)}, f32[8192]{0:T(1024)S(1)}, u32[]{:S(2)}, u32[]{:S(2)}) collective-permute-start(f32[8192]{0:T(1024)S(1)} %bitcast.224), channel_id=1, source_target_pairs={{0,8},{8,16},{16,24},{24,0},{1,9},{9,17},{17,25},{25,1},{2,10},{10... | collective-permute-start | bytes 98312 | tf_op jit(solution)/shard_map/ppermute | solution.py:37
  86.9 11.9 %copy-start.23 = (pred[4]{0:T(512)(128)(4,1)S(1)}, pred[4]{0:T(512)(128)(4,1)}, u32[]{:S(2)}) copy-start(pred[4]{0:T(512)(128)(4,1)} %get-tuple-element.49) | copy-start | bytes 16
  90.7 4.0 %collective-permute-start.17 = (f32[8192]{0:T(1024)S(1)}, f32[8192]{0:T(1024)S(1)}, u32[]{:S(2)}, u32[]{:S(2)}) collective-permute-start(f32[8192]{0:T(1024)S(1)} %add_add_fusion.1), channel_id=1, source_target_pairs={{0,24},{8,0},{16,8},{24,16},{1,25},{9,1},{17,9},{25,17},{2,26},{10... | collective-permute-start | bytes 98312 | tf_op jit(solution)/shard_map/ppermute | solution.py:49
  92.0 5.2 %collective-permute-start.16 = (f32[8192]{0:T(1024)S(1)}, f32[8192]{0:T(1024)S(1)}, u32[]{:S(2)}, u32[]{:S(2)}) collective-permute-start(f32[8192]{0:T(1024)S(1)} %add_add_fusion.1), channel_id=1, source_target_pairs={{0,16},{8,24},{16,0},{24,8},{1,17},{9,25},{17,1},{25,9},{2,18},{10... | collective-permute-start | bytes 98312 | tf_op jit(solution)/shard_map/ppermute | solution.py:49
  92.3 5.7 %collective-permute-start.15 = (f32[8192]{0:T(1024)S(1)}, f32[8192]{0:T(1024)S(1)}, u32[]{:S(2)}, u32[]{:S(2)}) collective-permute-start(f32[8192]{0:T(1024)S(1)} %add_add_fusion.1), channel_id=1, source_target_pairs={{0,8},{8,16},{16,24},{24,0},{1,9},{9,17},{17,25},{25,1},{2,10},{10... | collective-permute-start | bytes 98312 | tf_op jit(solution)/shard_map/ppermute | solution.py:49
  98.9 5.8 %collective-permute-start.20 = (f32[32768]{0:T(1024)S(1)}, f32[32768]{0:T(1024)S(1)}, u32[]{:S(2)}, u32[]{:S(2)}) collective-permute-start(f32[32768]{0:T(1024)S(1)} %bitcast.207), channel_id=1, source_target_pairs={{0,6},{1,7},{2,0},{3,1},{4,2},{5,3},{6,4},{7,5},{8,14},{9,15},{10,... | collective-permute-start | bytes 393224 | tf_op jit(solution)/shard_map/ppermute | solution.py:49
  100.2 5.0 %collective-permute-start.19 = (f32[32768]{0:T(1024)S(1)}, f32[32768]{0:T(1024)S(1)}, u32[]{:S(2)}, u32[]{:S(2)}) collective-permute-start(f32[32768]{0:T(1024)S(1)} %bitcast.208), channel_id=1, source_target_pairs={{0,4},{1,5},{2,6},{3,7},{4,0},{5,1},{6,2},{7,3},{8,12},{9,13},{10,... | collective-permute-start | bytes 393224 | tf_op jit(solution)/shard_map/ppermute | solution.py:49
  101.2 5.9 %collective-permute-start.18 = (f32[32768]{0:T(1024)S(1)}, f32[32768]{0:T(1024)S(1)}, u32[]{:S(2)}, u32[]{:S(2)}) collective-permute-start(f32[32768]{0:T(1024)S(1)} %bitcast.209), channel_id=1, source_target_pairs={{0,2},{1,3},{2,4},{3,5},{4,6},{5,7},{6,0},{7,1},{8,10},{9,11},{10,... | collective-permute-start | bytes 393224 | tf_op jit(solution)/shard_map/ppermute | solution.py:49
  108.6 2.0 %collective-permute-start.21 = (f32[131072]{0:T(1024)S(1)}, f32[131072]{0:T(1024)S(1)}, u32[]{:S(2)}, u32[]{:S(2)}) collective-permute-start(f32[131072]{0:T(1024)S(1)} %bitcast.204), channel_id=1, source_target_pairs={{0,1},{1,0},{2,3},{3,2},{4,5},{5,4},{6,7},{7,6},{8,9},{9,8},{10,11... | collective-permute-start | bytes 1572872 | tf_op jit(solution)/shard_map/ppermute | solution.py:44
  (1 other events, 1.1 us)

commit v21 on v18

--- a/solution.py
+++ b/solution.py
@@ -238,7 +238,7 @@
     scores = jnp.where(causal, scores, -jnp.inf)
     highest = jnp.max(scores, axis=-1, keepdims=True)
     exponent = jnp.exp(scores - highest)
-    probs = exponent / jnp.sum(exponent, axis=-1, keepdims=True)
+    probs = lax.optimization_barrier(exponent / jnp.sum(exponent, axis=-1, keepdims=True))
     probs_low = probs.astype(jnp.bfloat16)
     value_grad = contract("ghij,gihd->ghjd", probs_low, up_heads).astype(jnp.bfloat16)
     prob_grad = contract("gihd,ghjd->ghij", up_heads, value_rows)

time: 105 us -> 108 us (1.029)
  other arithmetic: 10.5 us -> 14.4 us
  matrix products: 23.2 us -> 21.4 us
  local copies, waits for them, and re-layouts: 10.7 us -> 11.9 us
    sub x1, other arithmetic: 0.61 us -> 2.76 us  [attend_blocked(): prob_grad - jnp.sum(prob_grad * probs, axis=-1, keepdims=True)]
    div x0 -> x1, other arithmetic: none -> 1.75 us  [attend_blocked(): exponent / jnp.sum(exponent, axis=-1, keepdims=True)]
    dot_general x12, matrix products: 8.44 us -> 6.72 us  [contract(): return jnp.einsum(spec, left, right, preferred_element_type=jnp.float32)]
  transfers between devices with their start and end apart: 22 -> 22, of which waited for: 17 -> 16; matrix products, arithmetic and copies ran while one was open for 15% -> 14% of each run, Pallas kernels for 0% -> 0%
where the time goes in v21:
time: 108 us; the launch traced here: 107 us
  starting transfers between devices  31.8 us (29%)
  waiting for transfers between devices  26.3 us (24%)
  matrix products  21.4 us (20%)
  other arithmetic  14.4 us (13%)
  local copies, waits for them, and re-layouts  11.9 us (11%)
  between operations  1.51 us (1%)
    ppermute x6, waiting for transfers between devices, exchange(): lax.ppermute(send, axis, [(i, (i + shift) % count) for i in range(count)])  12.8 us
    ppermute x6, starting transfers between devices, exchange(): lax.ppermute(send, axis, [(i, (i + shift) % count) for i in range(count)])  12.1 us
    ppermute x6, starting transfers between devices, _scatter_step(): lax.ppermute(send, axis, _group_pairs(axis, stride, group, shift))  9.36 us
    ppermute x6, starting transfers between devices, _gather_step(): lax.ppermute(flat, axis, _group_pairs(axis, stride, group, shift))  8.69 us
    dot_general x12, matrix products, contract(): return jnp.einsum(spec, left, right, preferred_element_type=jnp.float32)  6.72 us
    ppermute x6, waiting for transfers between devices, _gather_step(): lax.ppermute(flat, axis, _group_pairs(axis, stride, group, shift))  5.62 us
    ppermute x6, waiting for transfers between devices, _scatter_step(): lax.ppermute(send, axis, _group_pairs(axis, stride, group, shift))  3.29 us
    dot_general x1, matrix products, local(): jnp.einsum('der,des->drs', target_hot, source_hot, preferred_element_type...  2.86 us
  transfers between devices with their start and end apart: 22, of which 16 were waited for; matrix products, arithmetic and copies ran while one was open for 14% of the time, Pallas kernels for 0%

profile of v21, /device:TPU:0, one launch (start us, length us, event | category | flops | bytes accessed | tf_op | source)
XLA Modules:
  0.0 107.2 jit_solution(12369598856411228309)
XLA Ops:
  0.6 0.8 iota_compare_fusion.10
  1.4 1.4 %convolution_convert_fusion.6 = bf16[4,128,256]{2,1,0:T(8,128)(2,1)S(1)} fusion(bf16[4,256,256]{2,1,0:T(8,128)(2,1)} %param.12, s32[4,128]{1,0:T(4,128)} %param.15, pred[4,128]{1,0:T(4,128)(4,1)S(1)} %iota_compare_fusion.10), kind=kOutput, calls=%fused_computation.45 | convolution fusion | flops 67502080 | bytes 788992 | tf_op jit(solution)/shard_map/dsn,dnh->dsh/dot_general | solution.py:283
  3.9 1.4 %fusion.3 = f32[1,4,256]{2,0,1:T(1,128)S(1)} fusion(s32[4,1024]{1,0:T(4,128)} %param.14), kind=kOutput, calls=%fused_computation.9 | convolution fusion | flops 3145728 | bytes 20480 | tf_op jit(solution)/shard_map/der,e->dr/dot_general | solution.py:294
  6.1 2.9 %fusion.11 = bf16[4,256,384]{2,1,0:T(8,128)(2,1)S(1)} fusion(s32[4,1024]{1,0:T(4,128)} %param.13, s32[4,1024]{1,0:T(4,128)} %param.14), kind=kOutput, calls=%fused_computation.21 | convolution fusion | flops 808321024 | bytes 819200 | tf_op jit(solution)/shard_map/der,des->drs/dot_general | solution.py:291
  8.9 1.3 %collective-permute-done = bf16[4,128,256]{2,1,0:T(8,128)(2,1)S(1)} collective-permute-done((bf16[4,128,256]{2,1,0:T(8,128)(2,1)S(1)}, bf16[4,128,256]{2,1,0:T(8,128)(2,1)S(1)}, u32[]{:S(2)}, u32[]{:S(2)}) %collective-permute-start) | collective-permute-done | bytes 262176 | tf_op jit(solution)/shard_map/ppermute | solution.py:12
  10.8 1.4 %fusion.20 = (bf16[4,256,256]{2,1,0:T(8,128)(2,1)S(1)}, f32[4,256,256]{2,1,0:T(8,128)}) fusion(bf16[4,256,256]{2,1,0:T(8,128)(2,1)S(1)} %copy-done.12, bf16[4,256,256]{2,1,0:T(8,128)(2,1)S(1)} %fusion.15, bf16[256,256]{1,0:T(8,128)(2,1)S(1)} %copy-done), kind=kOutput, calls=%fused_computation.50 | convolution fusion | flops 136052736 | bytes 2752512 | tf_op jit(solution)/shard_map/drh,hk->drk/dot_general | solution.py:306
  12.2 2.4 %collective-permute-start.1 = (bf16[4,64,256]{2,1,0:T(8,128)(2,1)S(1)}, bf16[4,64,256]{2,1,0:T(8,128)(2,1)S(1)}, u32[]{:S(2)}, u32[]{:S(2)}) collective-permute-start(bf16[4,64,256]{2,1,0:T(8,128)(2,1)S(1)} %get-tuple-element.33), channel_id=1, source_target_pairs={{0,8},{8,16},{16,24},{24,0},{1,9},{9,17},{17,25},{25,1},{2,10},{10... | collective-permute-start | bytes 393224 | tf_op jit(solution)/shard_map/ppermute | solution.py:97
  14.6 2.6 %collective-permute-start.2 = (bf16[4,64,256]{2,1,0:T(8,128)(2,1)S(1)}, bf16[4,64,256]{2,1,0:T(8,128)(2,1)S(1)}, u32[]{:S(2)}, u32[]{:S(2)}) collective-permute-start(bf16[4,64,256]{2,1,0:T(8,128)(2,1)S(1)} %get-tuple-element.32), channel_id=1, source_target_pairs={{0,16},{8,24},{16,0},{24,8},{1,17},{9,25},{17,1},{25,9},{2,18},{10... | collective-permute-start | bytes 393224 | tf_op jit(solution)/shard_map/ppermute | solution.py:97
  17.2 1.3 %collective-permute-start.3 = (bf16[4,64,256]{2,1,0:T(8,128)(2,1)S(1)}, bf16[4,64,256]{2,1,0:T(8,128)(2,1)}, u32[]{:S(2)}, u32[]{:S(2)}) collective-permute-start(bf16[4,64,256]{2,1,0:T(8,128)(2,1)S(1)} %get-tuple-element.31), channel_id=1, source_target_pairs={{0,24},{8,0},{16,8},{24,16},{1,25},{9,1},{17,9},{25,17},{2,26},{10... | collective-permute-start | bytes 393224 | tf_op jit(solution)/shard_map/ppermute | solution.py:97
  20.4 6.3 %collective-permute-done.2 = bf16[4,64,256]{2,1,0:T(8,128)(2,1)S(1)} collective-permute-done((bf16[4,64,256]{2,1,0:T(8,128)(2,1)S(1)}, bf16[4,64,256]{2,1,0:T(8,128)(2,1)S(1)}, u32[]{:S(2)}, u32[]{:S(2)}) %collective-permute-start.2) | collective-permute-done | bytes 131104 | tf_op jit(solution)/shard_map/ppermute | solution.py:97
  26.6 1.0 pad_maximum_fusion
  29.5 2.2 %fusion.59 = (f32[8,4,128]{2,1,0:T(4,128)S(1)}, f32[8,4,128,128]{2,3,1,0:T(8,128)}) fusion(pred[128,128]{0,1:T(8,128)(4,1)S(1)} %copy-done.20, bf16[8,4,128,64]{2,3,1,0:T(8,128)(2,1)S(1)} %fusion.16, bf16[8,4,128,64]{2,3,1,0:T(8,128)(2,1)S(1)} %fusion.17), kind=kOutput, calls=%fused_computation.171 | convolution fusion | flops 69206144 | bytes 3178496 | tf_op jit(solution)/shard_map/sub | solution.py:240
  31.7 1.8 %broadcast_divide_fusion = f32[8,4,128,128]{2,3,1,0:T(8,128)S(1)} fusion(f32[8,4,128,128]{2,3,1,0:T(8,128)} %get-tuple-element.43, f32[8,4,128]{2,1,0:T(4,128)S(1)} %get-tuple-element.42), kind=kLoop, calls=%fused_computation.58 | loop fusion | flops 524288 | bytes 4210688 | tf_op jit(solution)/shard_map/div | solution.py:241
  33.5 2.0 %fusion.19 = f32[8,4,128,128]{3,2,1,0:T(8,128)} fusion(bf16[8,128,4,64]{1,3,2,0:T(8,128)(2,1)S(1)} %copy.34, bf16[8,128,256,1]{2,1,3,0:T(8,128)(2,1)S(1)} %bitcast.190, bf16[256,4,64,1]{0,2,1,3:T(8,128)(2,1)S(1)} %bitcast.198), kind=kOutput, calls=%fused_computation.44 | convolution fusion | flops 201588736 | bytes 3276800 | tf_op jit(solution)/shard_map/gihd,ghjd->ghij/dot_general | solution.py:227
  35.5 2.8 %fusion.7 = bf16[8,4,128,128]{2,3,1,0:T(8,128)(2,1)S(1)} fusion(f32[8,4,128,128]{2,3,1,0:T(8,128)S(1)} %broadcast_divide_fusion, f32[8,4,128,128]{3,2,1,0:T(8,128)} %fusion.19), kind=kOutput, calls=%fused_computation.15 | output fusion | flops 2625663 | bytes 5242880 | tf_op jit(solution)/shard_map/sub | solution.py:246
  39.3 0.8 convolution_convert_fusion.5
  40.2 0.8 convolution_convert_fusion.4
  44.8 3.4 %collective-permute-start.4 = (bf16[4,64,256]{2,1,0:T(8,128)(2,1)}, bf16[4,64,256]{2,1,0:T(8,128)(2,1)}, u32[]{:S(2)}, u32[]{:S(2)}) collective-permute-start(bf16[4,64,256]{2,1,0:T(8,128)(2,1)} %get-tuple-element.25), channel_id=1, source_target_pairs={{0,8},{8,16},{16,24},{24,0},{1,9},{9,17},{17,25},{25,1},{2,10},{10... | collective-permute-start | bytes 393224 | tf_op jit(solution)/shard_map/ppermute | solution.py:97
  48.2 1.5 %collective-permute-start.5 = (bf16[4,64,256]{2,1,0:T(8,128)(2,1)}, bf16[4,64,256]{2,1,0:T(8,128)(2,1)}, u32[]{:S(2)}, u32[]{:S(2)}) collective-permute-start(bf16[4,64,256]{2,1,0:T(8,128)(2,1)} %get-tuple-element.24), channel_id=1, source_target_pairs={{0,16},{8,24},{16,0},{24,8},{1,17},{9,25},{17,1},{25,9},{2,18},{10... | collective-permute-start | bytes 393224 | tf_op jit(solution)/shard_map/ppermute | solution.py:97
  49.7 0.9 collective-permute-start.6
  52.5 1.3 %collective-permute-done.4 = bf16[4,64,256]{2,1,0:T(8,128)(2,1)} collective-permute-done((bf16[4,64,256]{2,1,0:T(8,128)(2,1)}, bf16[4,64,256]{2,1,0:T(8,128)(2,1)}, u32[]{:S(2)}, u32[]{:S(2)}) %collective-permute-start.4) | collective-permute-done | bytes 131104 | tf_op jit(solution)/shard_map/ppermute | solution.py:97
  53.8 5.1 %collective-permute-done.5 = bf16[4,64,256]{2,1,0:T(8,128)(2,1)} collective-permute-done((bf16[4,64,256]{2,1,0:T(8,128)(2,1)}, bf16[4,64,256]{2,1,0:T(8,128)(2,1)}, u32[]{:S(2)}, u32[]{:S(2)}) %collective-permute-start.5) | collective-permute-done | bytes 131104 | tf_op jit(solution)/shard_map/ppermute | solution.py:97
  58.9 1.1 %pad_maximum_fusion.1 = bf16[4,4,64,256]{3,2,1,0:T(8,128)(2,1)S(1)} fusion(bf16[1,4,64,256]{3,2,1,0:T(8,128)(2,1)} %bitcast.46, bf16[1,4,64,256]{3,2,1,0:T(8,128)(2,1)} %bitcast.45, bf16[1,4,64,256]{3,2,1,0:T(8,128)(2,1)} %bitcast.44, bf16[1,4,64,256]{3,2,1,0:T(8,128)(2,1)S(1)} %get-tuple-element.22), kind=kLoop, calls=%fused_computation.70 | loop fusion | flops 786432 | bytes 1048576 | tf_op jit(solution)/shard_map/stack | solution.py:99
  60.9 1.6 %fusion.22 = bf16[4,256,256]{2,1,0:T(8,128)(2,1)S(1)} fusion(f32[4,256,256]{2,1,0:T(8,128)} %get-tuple-element.41, bf16[4,64,256]{2,1,0:T(8,128)(2,1)S(1)} %get-tuple-element.19, bf16[4,64,256]{2,1,0:T(8,128)(2,1)S(1)} %get-tuple-element.20, bf16[4,64,256]{2,1,0:T(8,128)(2,1)S(1)} %get-tuple-element.21, bf16[4,64,256]{2,1,0:T(8,128)(2,1)S(1)} %get-tuple-element.18), kind=kLoop, calls=%fused_computation.52 | loop fusion | flops 4456448 | bytes 2097152 | tf_op jit(solution)/shard_map/convert_element_type | solution.py:317
  63.1 0.9 broadcast_select_fusion.3
  64.4 1.9 %collective-permute-done.7 = f32[131072]{0:T(1024)} collective-permute-done((f32[131072]{0:T(1024)}, f32[131072]{0:T(1024)}, u32[]{:S(2)}, u32[]{:S(2)}) %collective-permute-start.7) | collective-permute-done | bytes 524320 | tf_op jit(solution)/shard_map/ppermute | solution.py:33
  66.2 1.1 %select_add_fusion = f32[131072]{0:T(1024)S(1)} fusion(f32[131072]{0:T(1024)} %collective-permute-done.7, f32[131072]{0:T(1024)S(1)} %constant_dynamic-update-slice_fusion, f32[131072]{0:T(1024)S(1)} %constant_dynamic-update-slice_fusion.1, pred[]{:T(512)S(6)} %eq.87), kind=kLoop, calls=%fused_computation.74 | loop fusion | flops 262144 | bytes 2097153 | tf_op jit(solution)/shard_map/add | solution.py:33
  68.0 1.8 %collective-permute-start.10 = (f32[32768]{0:T(1024)S(1)}, f32[32768]{0:T(1024)S(1)}, u32[]{:S(2)}, u32[]{:S(2)}) collective-permute-start(f32[32768]{0:T(1024)S(1)} %bitcast.215), channel_id=1, source_target_pairs={{0,6},{1,7},{2,0},{3,1},{4,2},{5,3},{6,4},{7,5},{8,14},{9,15},{10,... | collective-permute-start | bytes 393224 | tf_op jit(solution)/shard_map/ppermute | solution.py:37
  70.1 1.5 %collective-permute-start.9 = (f32[32768]{0:T(1024)S(1)}, f32[32768]{0:T(1024)S(1)}, u32[]{:S(2)}, u32[]{:S(2)}) collective-permute-start(f32[32768]{0:T(1024)S(1)} %bitcast.213), channel_id=1, source_target_pairs={{0,4},{1,5},{2,6},{3,7},{4,0},{5,1},{6,2},{7,3},{8,12},{9,13},{10,... | collective-permute-start | bytes 393224 | tf_op jit(solution)/shard_map/ppermute | solution.py:37
  71.6 2.1 %fusion.60 = f32[4,384,256]{2,1,0:T(8,128)S(1)} fusion(bf16[4,256,384]{2,1,0:T(8,128)(2,1)} %copy-done.11, f32[4,256,256]{2,1,0:T(8,128)S(1)} %convolution_multiply_fusion), kind=kOutput, calls=%fused_computation.172 | convolution fusion | flops 1207959552 | bytes 3407872 | tf_op jit(solution)/shard_map/drs,drh->dsh/dot_general | solution.py:326
  74.5 1.1 %collective-permute-start.14 = (bf16[4,128,256]{2,1,0:T(8,128)(2,1)}, bf16[4,128,256]{2,1,0:T(8,128)(2,1)}, u32[]{:S(2)}, u32[]{:S(2)}) collective-permute-start(bf16[4,128,256]{2,1,0:T(8,128)(2,1)} %slice.101), channel_id=1, source_target_pairs={{0,7},{1,0},{2,1},{3,2},{4,3},{5,4},{6,5},{7,6},{8,15},{9,8},{10,9... | collective-permute-start | bytes 786440 | tf_op jit(solution)/shard_map/ppermute | solution.py:12
  75.6 1.9 %collective-permute-done.8 = f32[32768]{0:T(1024)S(1)} collective-permute-done((f32[32768]{0:T(1024)S(1)}, f32[32768]{0:T(1024)S(1)}, u32[]{:S(2)}, u32[]{:S(2)}) %collective-permute-start.8) | collective-permute-done | bytes 131104 | tf_op jit(solution)/shard_map/ppermute | solution.py:37
  78.1 3.3 %collective-permute-start.11 = (f32[8192]{0:T(1024)S(1)}, f32[8192]{0:T(1024)S(1)}, u32[]{:S(2)}, u32[]{:S(2)}) collective-permute-start(f32[8192]{0:T(1024)S(1)} %bitcast.221), channel_id=1, source_target_pairs={{0,8},{8,16},{16,24},{24,0},{1,9},{9,17},{17,25},{25,1},{2,10},{10... | collective-permute-start | bytes 98312 | tf_op jit(solution)/shard_map/ppermute | solution.py:37
  81.5 1.7 %collective-permute-start.12 = (f32[8192]{0:T(1024)S(1)}, f32[8192]{0:T(1024)S(1)}, u32[]{:S(2)}, u32[]{:S(2)}) collective-permute-start(f32[8192]{0:T(1024)S(1)} %bitcast.220), channel_id=1, source_target_pairs={{0,16},{8,24},{16,0},{24,8},{1,17},{9,25},{17,1},{25,9},{2,18},{10... | collective-permute-start | bytes 98312 | tf_op jit(solution)/shard_map/ppermute | solution.py:37
  83.9 2.2 %convolution_add_fusion.1 = f32[4,256,256]{2,1,0:T(8,128)} fusion(bf16[4,128,256]{2,1,0:T(8,128)(2,1)} %collective-permute-done.14, f32[4,256,256]{2,1,0:T(8,128)S(1)} %convolution_multiply_fusion, f32[4,384,256]{2,1,0:T(8,128)S(1)} %fusion.60, s32[4,128]{1,0:T(4,128)S(1)} %copy-done.21, pred[4,128]{1,0:T(4,128)(4,1)S(1)} %copy-done.27, ...), kind=kOutput, calls=%fused_computation.27 | convolution fusion | flops 70254592 | bytes 3934720 | tf_op jit(solution)/shard_map/dsn,dsh->dnh/dot_general | solution.py:336
  86.3 0.8 collective-permute-done.13
  87.5 2.7 %collective-permute-start.16 = (f32[8192]{0:T(1024)S(1)}, f32[8192]{0:T(1024)S(1)}, u32[]{:S(2)}, u32[]{:S(2)}) collective-permute-start(f32[8192]{0:T(1024)S(1)} %add_add_fusion.1), channel_id=1, source_target_pairs={{0,16},{8,24},{16,0},{24,8},{1,17},{9,25},{17,1},{25,9},{2,18},{10... | collective-permute-start | bytes 98312 | tf_op jit(solution)/shard_map/ppermute | solution.py:49
  90.3 1.0 collective-permute-start.17
  91.3 1.6 %collective-permute-done.15 = f32[8192]{0:T(1024)S(1)} collective-permute-done((f32[8192]{0:T(1024)S(1)}, f32[8192]{0:T(1024)S(1)}, u32[]{:S(2)}, u32[]{:S(2)}) %collective-permute-start.15) | collective-permute-done | bytes 32800 | tf_op jit(solution)/shard_map/ppermute | solution.py:49
  92.9 1.3 %collective-permute-done.17 = f32[8192]{0:T(1024)S(1)} collective-permute-done((f32[8192]{0:T(1024)S(1)}, f32[8192]{0:T(1024)S(1)}, u32[]{:S(2)}, u32[]{:S(2)}) %collective-permute-start.17) | collective-permute-done | bytes 32800 | tf_op jit(solution)/shard_map/ppermute | solution.py:49
  95.0 0.8 collective-permute-start.18
  95.9 1.0 collective-permute-start.19
  96.8 2.7 %collective-permute-start.20 = (f32[32768]{0:T(1024)S(1)}, f32[32768]{0:T(1024)S(1)}, u32[]{:S(2)}, u32[]{:S(2)}) collective-permute-start(f32[32768]{0:T(1024)S(1)} %bitcast.208), channel_id=1, source_target_pairs={{0,6},{1,7},{2,0},{3,1},{4,2},{5,3},{6,4},{7,5},{8,14},{9,15},{10,... | collective-permute-start | bytes 393224 | tf_op jit(solution)/shard_map/ppermute | solution.py:49
  99.7 1.3 %collective-permute-done.18 = f32[32768]{0:T(1024)S(1)} collective-permute-done((f32[32768]{0:T(1024)S(1)}, f32[32768]{0:T(1024)S(1)}, u32[]{:S(2)}, u32[]{:S(2)}) %collective-permute-start.18) | collective-permute-done | bytes 131104 | tf_op jit(solution)/shard_map/ppermute | solution.py:49
  101.1 1.2 %collective-permute-done.19 = f32[32768]{0:T(1024)S(1)} collective-permute-done((f32[32768]{0:T(1024)S(1)}, f32[32768]{0:T(1024)S(1)}, u32[]{:S(2)}, u32[]{:S(2)}) %collective-permute-start.19) | collective-permute-done | bytes 131104 | tf_op jit(solution)/shard_map/ppermute | solution.py:49
  103.0 0.8 gather_fusion.1
  104.7 1.3 %collective-permute-done.21 = f32[131072]{0:T(1024)S(1)} collective-permute-done((f32[131072]{0:T(1024)S(1)}, f32[131072]{0:T(1024)S(1)}, u32[]{:S(2)}, u32[]{:S(2)}) %collective-permute-start.21) | collective-permute-done | bytes 524320 | tf_op jit(solution)/shard_map/ppermute | solution.py:44
  106.3 1.0 fusion.58
  (143 shorter events, 20.6 us)
Async XLA Ops:
  0.6 10.1 %copy-start = (bf16[256,256]{1,0:T(8,128)(2,1)S(1)}, bf16[256,256]{1,0:T(8,128)(2,1)}, u32[]{:S(2)}) copy-start(bf16[256,256]{1,0:T(8,128)(2,1)} %param.17) | copy-start | bytes 393220
  1.4 1.9 %copy-start.26 = (pred[4,128]{1,0:T(4,128)(4,1)}, pred[4,128]{1,0:T(4,128)(4,1)S(1)}, u32[]{:S(2)}) copy-start(pred[4,128]{1,0:T(4,128)(4,1)S(1)} %iota_compare_fusion.10) | copy-start | bytes 1540
  2.8 7.4 %collective-permute-start = (bf16[4,128,256]{2,1,0:T(8,128)(2,1)S(1)}, bf16[4,128,256]{2,1,0:T(8,128)(2,1)S(1)}, u32[]{:S(2)}, u32[]{:S(2)}) collective-permute-start(bf16[4,128,256]{2,1,0:T(8,128)(2,1)S(1)} %convolution_convert_fusion.6), channel_id=1, source_target_pairs={{0,1},{1,2},{2,3},{3,4},{4,5},{5,6},{6,7},{7,0},{8,9},{9,10},{10,1... | collective-permute-start | bytes 786440 | tf_op jit(solution)/shard_map/ppermute | solution.py:12
  3.9 24.3 %copy-start.23 = (pred[4]{0:T(512)(128)(4,1)}, pred[4]{0:T(512)(128)(4,1)S(1)}, u32[]{:S(2)}) copy-start(pred[4]{0:T(512)(128)(4,1)S(1)} %get-tuple-element.44) | copy-start | bytes 16
  5.3 4.9 %copy-start.18 = (f32[4,256]{1,0:T(4,128)}, f32[4,256]{1,0:T(4,128)S(1)}, u32[]{:S(2)}) copy-start(f32[4,256]{1,0:T(4,128)S(1)} %fusion.45) | copy-start | bytes 12292
  6.1 4.2 %copy-start.12 = (bf16[4,256,256]{2,1,0:T(8,128)(2,1)S(1)}, bf16[4,256,256]{2,1,0:T(8,128)(2,1)}, u32[]{:S(2)}) copy-start(bf16[4,256,256]{2,1,0:T(8,128)(2,1)} %param.12) | copy-start | bytes 1572868
  8.9 1.3 %copy-start.11 = (bf16[4,256,384]{2,1,0:T(8,128)(2,1)}, bf16[4,256,384]{2,1,0:T(8,128)(2,1)S(1)}, u32[]{:S(2)}) copy-start(bf16[4,256,384]{2,1,0:T(8,128)(2,1)S(1)} %fusion.11) | copy-start | bytes 2359300
  10.7 1.4 %copy-start.13 = (bf16[4,256,256]{2,1,0:T(8,128)(2,1)}, bf16[4,256,256]{2,1,0:T(8,128)(2,1)S(1)}, u32[]{:S(2)}) copy-start(bf16[4,256,256]{2,1,0:T(8,128)(2,1)S(1)} %fusion.15) | copy-start | bytes 1572868
  10.8 7.8 %copy-start.15 = (bf16[256,256]{1,0:T(8,128)(2,1)S(1)}, bf16[256,256]{1,0:T(8,128)(2,1)}, u32[]{:S(2)}) copy-start(bf16[256,256]{1,0:T(8,128)(2,1)} %param.18) | copy-start | bytes 393220
  10.8 7.9 %copy-start.16 = (bf16[256,256]{1,0:T(8,128)(2,1)S(1)}, bf16[256,256]{1,0:T(8,128)(2,1)}, u32[]{:S(2)}) copy-start(bf16[256,256]{1,0:T(8,128)(2,1)} %param.19) | copy-start | bytes 393220
  10.8 8.0 %copy-start.1 = (bf16[16,1,1,64,256]{4,3,2,1,0:T(8,128)(2,1)S(1)}, bf16[16,1,1,64,256]{4,3,2,1,0:T(8,128)(2,1)}, u32[]{:S(2)}) copy-start(bf16[16,1,1,64,256]{4,3,2,1,0:T(8,128)(2,1)} %param.21) | copy-start | bytes 1572868
  12.2 8.2 %collective-permute-start.1 = (bf16[4,64,256]{2,1,0:T(8,128)(2,1)S(1)}, bf16[4,64,256]{2,1,0:T(8,128)(2,1)S(1)}, u32[]{:S(2)}, u32[]{:S(2)}) collective-permute-start(bf16[4,64,256]{2,1,0:T(8,128)(2,1)S(1)} %get-tuple-element.33), channel_id=1, source_target_pairs={{0,8},{8,16},{16,24},{24,0},{1,9},{9,17},{17,25},{25,1},{2,10},{10... | collective-permute-start | bytes 393224 | tf_op jit(solution)/shard_map/ppermute | solution.py:97
  14.6 12.1 %collective-permute-start.2 = (bf16[4,64,256]{2,1,0:T(8,128)(2,1)S(1)}, bf16[4,64,256]{2,1,0:T(8,128)(2,1)S(1)}, u32[]{:S(2)}, u32[]{:S(2)}) collective-permute-start(bf16[4,64,256]{2,1,0:T(8,128)(2,1)S(1)} %get-tuple-element.32), channel_id=1, source_target_pairs={{0,16},{8,24},{16,0},{24,8},{1,17},{9,25},{17,1},{25,9},{2,18},{10... | collective-permute-start | bytes 393224 | tf_op jit(solution)/shard_map/ppermute | solution.py:97
  17.2 9.5 %collective-permute-start.3 = (bf16[4,64,256]{2,1,0:T(8,128)(2,1)S(1)}, bf16[4,64,256]{2,1,0:T(8,128)(2,1)}, u32[]{:S(2)}, u32[]{:S(2)}) collective-permute-start(bf16[4,64,256]{2,1,0:T(8,128)(2,1)S(1)} %get-tuple-element.31), channel_id=1, source_target_pairs={{0,24},{8,0},{16,8},{24,16},{1,25},{9,1},{17,9},{25,17},{2,26},{10... | collective-permute-start | bytes 393224 | tf_op jit(solution)/shard_map/ppermute | solution.py:97
  18.7 10.1 %copy-start.9 = (bf16[256,256]{0,1:T(8,128)(2,1)}, bf16[256,256]{0,1:T(8,128)(2,1)S(1)}, u32[]{:S(2)}) copy-start(bf16[256,256]{0,1:T(8,128)(2,1)S(1)} %copy.30) | copy-start | bytes 393220
  18.8 1.3 %copy-start.17 = (bf16[256,256]{1,0:T(8,128)(2,1)S(1)}, bf16[256,256]{1,0:T(8,128)(2,1)}, u32[]{:S(2)}) copy-start(bf16[256,256]{1,0:T(8,128)(2,1)} %param.20) | copy-start | bytes 393220
  20.3 8.1 %copy-start.22 = (s32[1024]{0:T(1024)}, s32[1024]{0:T(1024)S(1)}, u32[]{:S(2)}) copy-start(s32[1024]{0:T(1024)S(1)} %pad_clamp_fusion.2) | copy-start | bytes 12292
  28.4 1.1 %copy-start.20 = (pred[128,128]{0,1:T(8,128)(4,1)S(1)}, pred[128,128]{0,1:T(8,128)(4,1)}, u32[]{:S(2)}) copy-start(pred[128,128]{0,1:T(8,128)(4,1)} %compare_and_fusion) | copy-start | bytes 49156
  29.1 2.6 %copy-start.3 = (bf16[8,4,128,64]{2,3,1,0:T(8,128)(2,1)}, bf16[8,4,128,64]{2,3,1,0:T(8,128)(2,1)S(1)}, u32[]{:S(2)}) copy-start(bf16[8,4,128,64]{2,3,1,0:T(8,128)(2,1)S(1)} %fusion.16) | copy-start | bytes 1572868
  29.5 2.2 %copy-start.5 = (bf16[8,4,128,64]{2,3,1,0:T(8,128)(2,1)}, bf16[8,4,128,64]{2,3,1,0:T(8,128)(2,1)S(1)}, u32[]{:S(2)}) copy-start(bf16[8,4,128,64]{2,3,1,0:T(8,128)(2,1)S(1)} %fusion.17) | copy-start | bytes 1572868
  35.5 2.8 %copy-start.6 = (bf16[8,4,128,64]{2,3,1,0:T(8,128)(2,1)S(1)}, bf16[8,4,128,64]{2,3,1,0:T(8,128)(2,1)}, u32[]{:S(2)}) copy-start(bf16[8,4,128,64]{2,3,1,0:T(8,128)(2,1)} %copy-done.5) | copy-start | bytes 1572868
  39.3 3.0 %copy-start.7 = (bf16[8,4,128,64]{2,3,1,0:T(8,128)(2,1)}, bf16[8,4,128,64]{2,3,1,0:T(8,128)(2,1)S(1)}, u32[]{:S(2)}) copy-start(bf16[8,4,128,64]{2,3,1,0:T(8,128)(2,1)S(1)} %convolution_convert_fusion.3) | copy-start | bytes 1572868
  42.4 1.0 copy-start.2
  44.8 9.0 %collective-permute-start.4 = (bf16[4,64,256]{2,1,0:T(8,128)(2,1)}, bf16[4,64,256]{2,1,0:T(8,128)(2,1)}, u32[]{:S(2)}, u32[]{:S(2)}) collective-permute-start(bf16[4,64,256]{2,1,0:T(8,128)(2,1)} %get-tuple-element.25), channel_id=1, source_target_pairs={{0,8},{8,16},{16,24},{24,0},{1,9},{9,17},{17,25},{25,1},{2,10},{10... | collective-permute-start | bytes 393224 | tf_op jit(solution)/shard_map/ppermute | solution.py:97
  48.2 10.7 %collective-permute-start.5 = (bf16[4,64,256]{2,1,0:T(8,128)(2,1)}, bf16[4,64,256]{2,1,0:T(8,128)(2,1)}, u32[]{:S(2)}, u32[]{:S(2)}) collective-permute-start(bf16[4,64,256]{2,1,0:T(8,128)(2,1)} %get-tuple-element.24), channel_id=1, source_target_pairs={{0,16},{8,24},{16,0},{24,8},{1,17},{9,25},{17,1},{25,9},{2,18},{10... | collective-permute-start | bytes 393224 | tf_op jit(solution)/shard_map/ppermute | solution.py:97
  49.7 2.0 %copy-start.8 = (bf16[8,4,128,64]{2,3,1,0:T(8,128)(2,1)S(1)}, bf16[8,4,128,64]{2,3,1,0:T(8,128)(2,1)}, u32[]{:S(2)}) copy-start(bf16[8,4,128,64]{2,3,1,0:T(8,128)(2,1)} %copy-done.7) | copy-start | bytes 1572868
  49.7 9.3 %collective-permute-start.6 = (bf16[4,64,256]{2,1,0:T(8,128)(2,1)S(1)}, bf16[4,64,256]{2,1,0:T(8,128)(2,1)}, u32[]{:S(2)}, u32[]{:S(2)}) collective-permute-start(bf16[4,64,256]{2,1,0:T(8,128)(2,1)S(1)} %get-tuple-element.23), channel_id=1, source_target_pairs={{0,24},{8,0},{16,8},{24,16},{1,25},{9,1},{17,9},{25,17},{2,26},{10... | collective-permute-start | bytes 393224 | tf_op jit(solution)/shard_map/ppermute | solution.py:97
  51.9 8.8 %copy-start.24 = (pred[4]{0:T(512)(128)(4,1)S(1)}, pred[4]{0:T(512)(128)(4,1)}, u32[]{:S(2)}) copy-start(pred[4]{0:T(512)(128)(4,1)} %copy-done.23) | copy-start | bytes 16
  60.7 1.8 %copy-start.14 = (bf16[4,256,256]{2,1,0:T(8,128)(2,1)S(1)}, bf16[4,256,256]{2,1,0:T(8,128)(2,1)}, u32[]{:S(2)}) copy-start(bf16[4,256,256]{2,1,0:T(8,128)(2,1)} %copy-done.13) | copy-start | bytes 1572868
  62.6 1.4 %copy-start.19 = (f32[4,256]{1,0:T(4,128)S(1)}, f32[4,256]{1,0:T(4,128)}, u32[]{:S(2)}) copy-start(f32[4,256]{1,0:T(4,128)} %copy-done.18) | copy-start | bytes 12292
  64.0 2.3 %collective-permute-start.7 = (f32[131072]{0:T(1024)}, f32[131072]{0:T(1024)}, u32[]{:S(2)}, u32[]{:S(2)}) collective-permute-start(f32[131072]{0:T(1024)} %broadcast_select_fusion.3), channel_id=1, source_target_pairs={{0,1},{1,0},{2,3},{3,2},{4,5},{5,4},{6,7},{7,6},{8,9},{9,8},{10,11... | collective-permute-start | bytes 1572872 | tf_op jit(solution)/shard_map/ppermute | solution.py:33
  68.0 7.6 %collective-permute-start.10 = (f32[32768]{0:T(1024)S(1)}, f32[32768]{0:T(1024)S(1)}, u32[]{:S(2)}, u32[]{:S(2)}) collective-permute-start(f32[32768]{0:T(1024)S(1)} %bitcast.215), channel_id=1, source_target_pairs={{0,6},{1,7},{2,0},{3,1},{4,2},{5,3},{6,4},{7,5},{8,14},{9,15},{10,... | collective-permute-start | bytes 393224 | tf_op jit(solution)/shard_map/ppermute | solution.py:37
  69.8 7.7 %collective-permute-start.8 = (f32[32768]{0:T(1024)S(1)}, f32[32768]{0:T(1024)S(1)}, u32[]{:S(2)}, u32[]{:S(2)}) collective-permute-start(f32[32768]{0:T(1024)S(1)} %bitcast.214), channel_id=1, source_target_pairs={{0,2},{1,3},{2,4},{3,5},{4,6},{5,7},{6,0},{7,1},{8,10},{9,11},{10,... | collective-permute-start | bytes 393224 | tf_op jit(solution)/shard_map/ppermute | solution.py:37
  70.1 13.8 %copy-start.21 = (s32[4,128]{1,0:T(4,128)S(1)}, s32[4,128]{1,0:T(4,128)}, u32[]{:S(2)}) copy-start(s32[4,128]{1,0:T(4,128)} %param.15) | copy-start | bytes 6148
  70.1 13.8 %copy-start.27 = (pred[4,128]{1,0:T(4,128)(4,1)S(1)}, pred[4,128]{1,0:T(4,128)(4,1)}, u32[]{:S(2)}) copy-start(pred[4,128]{1,0:T(4,128)(4,1)} %copy-done.26) | copy-start | bytes 1540
  70.1 7.8 %collective-permute-start.9 = (f32[32768]{0:T(1024)S(1)}, f32[32768]{0:T(1024)S(1)}, u32[]{:S(2)}, u32[]{:S(2)}) collective-permute-start(f32[32768]{0:T(1024)S(1)} %bitcast.213), channel_id=1, source_target_pairs={{0,4},{1,5},{2,6},{3,7},{4,0},{5,1},{6,2},{7,3},{8,12},{9,13},{10,... | collective-permute-start | bytes 393224 | tf_op jit(solution)/shard_map/ppermute | solution.py:37
  74.5 9.4 %collective-permute-start.14 = (bf16[4,128,256]{2,1,0:T(8,128)(2,1)}, bf16[4,128,256]{2,1,0:T(8,128)(2,1)}, u32[]{:S(2)}, u32[]{:S(2)}) collective-permute-start(bf16[4,128,256]{2,1,0:T(8,128)(2,1)} %slice.101), channel_id=1, source_target_pairs={{0,7},{1,0},{2,1},{3,2},{4,3},{5,4},{6,5},{7,6},{8,15},{9,8},{10,9... | collective-permute-start | bytes 786440 | tf_op jit(solution)/shard_map/ppermute | solution.py:12
  78.1 8.0 %collective-permute-start.11 = (f32[8192]{0:T(1024)S(1)}, f32[8192]{0:T(1024)S(1)}, u32[]{:S(2)}, u32[]{:S(2)}) collective-permute-start(f32[8192]{0:T(1024)S(1)} %bitcast.221), channel_id=1, source_target_pairs={{0,8},{8,16},{16,24},{24,0},{1,9},{9,17},{17,25},{25,1},{2,10},{10... | collective-permute-start | bytes 98312 | tf_op jit(solution)/shard_map/ppermute | solution.py:37
  81.5 4.8 %collective-permute-start.12 = (f32[8192]{0:T(1024)S(1)}, f32[8192]{0:T(1024)S(1)}, u32[]{:S(2)}, u32[]{:S(2)}) collective-permute-start(f32[8192]{0:T(1024)S(1)} %bitcast.220), channel_id=1, source_target_pairs={{0,16},{8,24},{16,0},{24,8},{1,17},{9,25},{17,1},{25,9},{2,18},{10... | collective-permute-start | bytes 98312 | tf_op jit(solution)/shard_map/ppermute | solution.py:37
  83.2 11.7 %copy-start.25 = (pred[4]{0:T(512)(128)(4,1)S(1)}, pred[4]{0:T(512)(128)(4,1)}, u32[]{:S(2)}) copy-start(pred[4]{0:T(512)(128)(4,1)} %get-tuple-element.45) | copy-start | bytes 16
  83.2 3.9 %collective-permute-start.13 = (f32[8192]{0:T(1024)S(1)}, f32[8192]{0:T(1024)S(1)}, u32[]{:S(2)}, u32[]{:S(2)}) collective-permute-start(f32[8192]{0:T(1024)S(1)} %bitcast.219), channel_id=1, source_target_pairs={{0,24},{8,0},{16,8},{24,16},{1,25},{9,1},{17,9},{25,17},{2,26},{10... | collective-permute-start | bytes 98312 | tf_op jit(solution)/shard_map/ppermute | solution.py:37
  87.1 5.8 %collective-permute-start.15 = (f32[8192]{0:T(1024)S(1)}, f32[8192]{0:T(1024)S(1)}, u32[]{:S(2)}, u32[]{:S(2)}) collective-permute-start(f32[8192]{0:T(1024)S(1)} %add_add_fusion.1), channel_id=1, source_target_pairs={{0,8},{8,16},{16,24},{24,0},{1,9},{9,17},{17,25},{25,1},{2,10},{10... | collective-permute-start | bytes 98312 | tf_op jit(solution)/shard_map/ppermute | solution.py:49
  87.5 5.4 %collective-permute-start.16 = (f32[8192]{0:T(1024)S(1)}, f32[8192]{0:T(1024)S(1)}, u32[]{:S(2)}, u32[]{:S(2)}) collective-permute-start(f32[8192]{0:T(1024)S(1)} %add_add_fusion.1), channel_id=1, source_target_pairs={{0,16},{8,24},{16,0},{24,8},{1,17},{9,25},{17,1},{25,9},{2,18},{10... | collective-permute-start | bytes 98312 | tf_op jit(solution)/shard_map/ppermute | solution.py:49
  90.3 3.9 %collective-permute-start.17 = (f32[8192]{0:T(1024)S(1)}, f32[8192]{0:T(1024)S(1)}, u32[]{:S(2)}, u32[]{:S(2)}) collective-permute-start(f32[8192]{0:T(1024)S(1)} %add_add_fusion.1), channel_id=1, source_target_pairs={{0,24},{8,0},{16,8},{24,16},{1,25},{9,1},{17,9},{25,17},{2,26},{10... | collective-permute-start | bytes 98312 | tf_op jit(solution)/shard_map/ppermute | solution.py:49
  95.0 6.0 %collective-permute-start.18 = (f32[32768]{0:T(1024)S(1)}, f32[32768]{0:T(1024)S(1)}, u32[]{:S(2)}, u32[]{:S(2)}) collective-permute-start(f32[32768]{0:T(1024)S(1)} %bitcast.206), channel_id=1, source_target_pairs={{0,2},{1,3},{2,4},{3,5},{4,6},{5,7},{6,0},{7,1},{8,10},{9,11},{10,... | collective-permute-start | bytes 393224 | tf_op jit(solution)/shard_map/ppermute | solution.py:49
  95.9 6.4 %collective-permute-start.19 = (f32[32768]{0:T(1024)S(1)}, f32[32768]{0:T(1024)S(1)}, u32[]{:S(2)}, u32[]{:S(2)}) collective-permute-start(f32[32768]{0:T(1024)S(1)} %bitcast.207), channel_id=1, source_target_pairs={{0,4},{1,5},{2,6},{3,7},{4,0},{5,1},{6,2},{7,3},{8,12},{9,13},{10,... | collective-permute-start | bytes 393224 | tf_op jit(solution)/shard_map/ppermute | solution.py:49
  96.8 5.7 %collective-permute-start.20 = (f32[32768]{0:T(1024)S(1)}, f32[32768]{0:T(1024)S(1)}, u32[]{:S(2)}, u32[]{:S(2)}) collective-permute-start(f32[32768]{0:T(1024)S(1)} %bitcast.208), channel_id=1, source_target_pairs={{0,6},{1,7},{2,0},{3,1},{4,2},{5,3},{6,4},{7,5},{8,14},{9,15},{10,... | collective-permute-start | bytes 393224 | tf_op jit(solution)/shard_map/ppermute | solution.py:49
  104.0 2.0 %collective-permute-start.21 = (f32[131072]{0:T(1024)S(1)}, f32[131072]{0:T(1024)S(1)}, u32[]{:S(2)}, u32[]{:S(2)}) collective-permute-start(f32[131072]{0:T(1024)S(1)} %bitcast.203), channel_id=1, source_target_pairs={{0,1},{1,0},{2,3},{3,2},{4,5},{5,4},{6,7},{7,6},{8,9},{9,8},{10,11... | collective-permute-start | bytes 1572872 | tf_op jit(solution)/shard_map/ppermute | solution.py:44
  (2 other events, 2.1 us)

commit v22 on v18

--- a/solution.py
+++ b/solution.py
@@ -245,7 +245,6 @@
     score_grad = (
         probs * (prob_grad - jnp.sum(prob_grad * probs, axis=-1, keepdims=True)) * scale_factor
     ).astype(jnp.bfloat16)
-    score_grad = lax.optimization_barrier(score_grad)
     query_grad = contract("ghij,ghjd->ghid", score_grad, key_rows).astype(jnp.bfloat16)
     key_grad = contract("ghij,ghid->ghjd", score_grad, queries).astype(jnp.bfloat16)
 

time: 105 us -> 120 us (1.14)
  matrix products: 23.2 us -> 36.8 us
  waiting for transfers between devices: 26.9 us -> 35.3 us
  starting transfers between devices: 31.5 us -> 26.2 us
  other arithmetic: 10.5 us -> 5.85 us
  local copies, waits for them, and re-layouts: 10.7 us -> 14 us
    dot_general x12, matrix products: 8.44 us -> 22 us  [contract(): return jnp.einsum(spec, left, right, preferred_element_type=jnp.float32)]
    ppermute x6, waiting for transfers between devices: 12.7 us -> 16.9 us  [exchange(): lax.ppermute(send, axis, [(i, (i + shift) % count) for i in range(count)])]
    ppermute x6, waiting for transfers between devices: 5.69 us -> 9.44 us  [_gather_step(): lax.ppermute(flat, axis, _group_pairs(axis, stride, group, shift))]
    ppermute x6, starting transfers between devices: 9.36 us -> 6.78 us  [_scatter_step(): lax.ppermute(send, axis, _group_pairs(axis, stride, group, shift))]
    ppermute x6, starting transfers between devices: 9.1 us -> 6.8 us  [_gather_step(): lax.ppermute(flat, axis, _group_pairs(axis, stride, group, shift))]
    another operation x2, other arithmetic: 2.13 us -> 0.14 us  [exchange(): jnp.stack(got)]
    dot_general x3, local copies, waits for them, and re-layouts: 0.69 us -> 2.59 us  [contract(): return jnp.einsum(spec, left, right, preferred_element_type=jnp.float32)]
    ppermute x6, starting transfers between devices: 12 us -> 10.3 us  [exchange(): lax.ppermute(send, axis, [(i, (i + shift) % count) for i in range(count)])]
  transfers between devices with their start and end apart: 22 -> 22, of which waited for: 17 -> 17; matrix products, arithmetic and copies ran while one was open for 15% -> 11% of each run, Pallas kernels for 0% -> 0%
where the time goes in v22:
time: 120 us
  matrix products  36.8 us (31%)
  waiting for transfers between devices  35.3 us (29%)
  starting transfers between devices  26.2 us (22%)
  local copies, waits for them, and re-layouts  14 us (12%)
  other arithmetic  5.85 us (5%)
  between operations  1.4 us (1%)
    dot_general x12, matrix products, contract(): return jnp.einsum(spec, left, right, preferred_element_type=jnp.float32)  22 us
    ppermute x6, waiting for transfers between devices, exchange(): lax.ppermute(send, axis, [(i, (i + shift) % count) for i in range(count)])  16.9 us
    ppermute x6, starting transfers between devices, exchange(): lax.ppermute(send, axis, [(i, (i + shift) % count) for i in range(count)])  10.3 us
    ppermute x6, waiting for transfers between devices, _gather_step(): lax.ppermute(flat, axis, _group_pairs(axis, stride, group, shift))  9.44 us
    ppermute x6, starting transfers between devices, _gather_step(): lax.ppermute(flat, axis, _group_pairs(axis, stride, group, shift))  6.8 us
    ppermute x6, starting transfers between devices, _scatter_step(): lax.ppermute(send, axis, _group_pairs(axis, stride, group, shift))  6.78 us
    ppermute x6, waiting for transfers between devices, _scatter_step(): lax.ppermute(send, axis, _group_pairs(axis, stride, group, shift))  3.49 us
    dot_general x1, matrix products, local(): jnp.einsum('der,des->drs', target_hot, source_hot, preferred_element_type...  2.87 us
  transfers between devices with their start and end apart: 22, of which 17 were waited for; matrix products, arithmetic and copies ran while one was open for 11% of the time, Pallas kernels for 0%

profile of v22, /device:TPU:0, one launch (start us, length us, event | category | flops | bytes accessed | tf_op | source)
XLA Modules:
  0.0 119.5 jit_solution(7366211719708998139)
XLA Ops:
  1.4 1.4 %convolution_convert_fusion.6 = bf16[4,128,256]{2,1,0:T(8,128)(2,1)S(1)} fusion(bf16[4,256,256]{2,1,0:T(8,128)(2,1)} %param.12, s32[4,128]{1,0:T(4,128)} %param.15, pred[4,128]{1,0:T(4,128)(4,1)S(1)} %iota_compare_fusion.10), kind=kOutput, calls=%fused_computation.45 | convolution fusion | flops 67502080 | bytes 788992 | tf_op jit(solution)/shard_map/dsn,dnh->dsh/dot_general | solution.py:282
  3.4 1.4 %fusion.3 = f32[1,4,256]{2,0,1:T(1,128)S(1)} fusion(s32[4,1024]{1,0:T(4,128)} %param.14), kind=kOutput, calls=%fused_computation.9 | convolution fusion | flops 3145728 | bytes 20480 | tf_op jit(solution)/shard_map/der,e->dr/dot_general | solution.py:293
  4.9 2.9 %fusion.11 = bf16[4,256,384]{2,1,0:T(8,128)(2,1)S(1)} fusion(s32[4,1024]{1,0:T(4,128)} %param.13, s32[4,1024]{1,0:T(4,128)} %param.14), kind=kOutput, calls=%fused_computation.21 | convolution fusion | flops 808321024 | bytes 819200 | tf_op jit(solution)/shard_map/der,des->drs/dot_general | solution.py:290
  7.8 2.4 %collective-permute-done = bf16[4,128,256]{2,1,0:T(8,128)(2,1)S(1)} collective-permute-done((bf16[4,128,256]{2,1,0:T(8,128)(2,1)S(1)}, bf16[4,128,256]{2,1,0:T(8,128)(2,1)S(1)}, u32[]{:S(2)}, u32[]{:S(2)}) %collective-permute-start) | collective-permute-done | bytes 262176 | tf_op jit(solution)/shard_map/ppermute | solution.py:12
  10.8 1.3 %fusion.20 = (bf16[4,256,256]{2,1,0:T(8,128)(2,1)S(1)}, f32[4,256,256]{2,1,0:T(8,128)}) fusion(bf16[4,256,256]{2,1,0:T(8,128)(2,1)S(1)} %copy-done.9, bf16[4,256,256]{2,1,0:T(8,128)(2,1)S(1)} %fusion.15, bf16[256,256]{1,0:T(8,128)(2,1)S(1)} %copy-done), kind=kOutput, calls=%fused_computation.50 | convolution fusion | flops 136052736 | bytes 2752512 | tf_op jit(solution)/shard_map/drh,hk->drk/dot_general | solution.py:305
  12.2 4.4 %collective-permute-start.3 = (bf16[4,64,256]{2,1,0:T(8,128)(2,1)S(1)}, bf16[4,64,256]{2,1,0:T(8,128)(2,1)S(1)}, u32[]{:S(2)}, u32[]{:S(2)}) collective-permute-start(bf16[4,64,256]{2,1,0:T(8,128)(2,1)S(1)} %get-tuple-element.31), channel_id=1, source_target_pairs={{0,24},{8,0},{16,8},{24,16},{1,25},{9,1},{17,9},{25,17},{2,26},{10... | collective-permute-start | bytes 393224 | tf_op jit(solution)/shard_map/ppermute | solution.py:97
  16.6 1.0 collective-permute-start.1
  19.3 1.2 collective-permute-done.3
  20.5 7.3 %collective-permute-done.2 = bf16[4,64,256]{2,1,0:T(8,128)(2,1)S(1)} collective-permute-done((bf16[4,64,256]{2,1,0:T(8,128)(2,1)S(1)}, bf16[4,64,256]{2,1,0:T(8,128)(2,1)S(1)}, u32[]{:S(2)}, u32[]{:S(2)}) %collective-permute-start.2) | collective-permute-done | bytes 131104 | tf_op jit(solution)/shard_map/ppermute | solution.py:97
  29.7 2.0 %fusion.19 = f32[8,4,128,128]{3,2,1,0:T(8,128)} fusion(bf16[8,128,4,64]{1,3,2,0:T(8,128)(2,1)S(1)} %copy.34, bf16[8,128,256,1]{2,1,3,0:T(8,128)(2,1)S(1)} %bitcast.195, bf16[256,4,64,1]{0,2,1,3:T(8,128)(2,1)S(1)} %bitcast.203), kind=kOutput, calls=%fused_computation.44 | convolution fusion | flops 201588736 | bytes 3276800 | tf_op jit(solution)/shard_map/gihd,ghjd->ghij/dot_general | solution.py:227
  31.7 2.2 %fusion.63 = (f32[8,4,128]{2,1,0:T(4,128)S(1)}, f32[8,4,128,128]{2,3,1,0:T(8,128)}) fusion(pred[128,128]{0,1:T(8,128)(4,1)S(1)} %compare_and_fusion, bf16[8,4,128,64]{2,3,1,0:T(8,128)(2,1)S(1)} %fusion.16, bf16[8,4,128,64]{2,3,1,0:T(8,128)(2,1)S(1)} %fusion.17), kind=kOutput, calls=%fused_computation.175 | convolution fusion | flops 69206144 | bytes 3178496 | tf_op jit(solution)/shard_map/sub | solution.py:240
  33.9 3.2 %convolution_convert_fusion.4 = bf16[8,4,128,64]{2,3,1,0:T(8,128)(2,1)} fusion(bf16[8,128,4,64]{1,3,2,0:T(8,128)(2,1)S(1)} %copy.34, f32[8,4,128,128]{2,3,1,0:T(8,128)} %get-tuple-element.43, f32[8,4,128]{2,1,0:T(4,128)S(1)} %get-tuple-element.42), kind=kOutput, calls=%fused_computation.39 | convolution fusion | flops 68419584 | bytes 3162112 | tf_op jit(solution)/shard_map/ghij,gihd->ghjd/dot_general | solution.py:227
  37.2 4.4 %convolution_convert_fusion.5 = bf16[8,4,128,64]{2,3,1,0:T(8,128)(2,1)S(1)} fusion(bf16[8,4,128,64]{2,3,1,0:T(8,128)(2,1)} %copy-done.14, f32[8,4,128,128]{3,2,1,0:T(8,128)} %fusion.19, f32[8,4,128,128]{2,3,1,0:T(8,128)} %get-tuple-element.43, f32[8,4,128]{2,1,0:T(4,128)S(1)} %get-tuple-element.42), kind=kOutput, calls=%fused_computation.40 | convolution fusion | flops 71045248 | bytes 5259264 | tf_op jit(solution)/shard_map/ghij,ghid->ghjd/dot_general | solution.py:227
  41.6 5.2 %convolution_convert_fusion.3 = bf16[8,4,128,64]{2,3,1,0:T(8,128)(2,1)} fusion(bf16[8,4,128,64]{2,3,1,0:T(8,128)(2,1)S(1)} %fusion.17, f32[8,4,128,128]{3,2,1,0:T(8,128)} %fusion.19, f32[8,4,128,128]{2,3,1,0:T(8,128)} %get-tuple-element.43, f32[8,4,128]{2,1,0:T(4,128)S(1)} %get-tuple-element.42), kind=kOutput, calls=%fused_computation.38 | convolution fusion | flops 71045248 | bytes 5259264 | tf_op jit(solution)/shard_map/ghij,ghjd->ghid/dot_general | solution.py:227
  46.8 1.0 convolution_bitcast_fusion.3
  47.8 1.4 %convolution_bitcast_fusion = f32[8,128,256]{2,1,0:T(8,128)S(1)} fusion(bf16[8,4,128,64]{2,3,1,0:T(8,128)(2,1)} %convolution_convert_fusion.4, bf16[256,4,64,1]{0,2,1,3:T(8,128)(2,1)S(1)} %bitcast.204), kind=kOutput, calls=%fused_computation.24 | convolution fusion | flops 134217728 | bytes 1703936 | tf_op jit(solution)/shard_map/ghid,chd->gic/dot_general | solution.py:227
  49.2 1.0 convolution_bitcast_fusion.4
  50.2 1.4 %convolution_bitcast_fusion.1 = f32[8,128,256]{2,1,0:T(8,128)S(1)} fusion(bf16[8,4,128,64]{2,3,1,0:T(8,128)(2,1)} %copy-done.12, bf16[256,4,64,1]{0,2,1,3:T(8,128)(2,1)S(1)} %bitcast.202), kind=kOutput, calls=%fused_computation.25 | convolution fusion | flops 134217728 | bytes 1703936 | tf_op jit(solution)/shard_map/ghid,chd->gic/dot_general | solution.py:227
  51.6 1.2 copy.46
  53.8 1.2 copy.44
  55.9 1.0 constant_dynamic-update-slice_fusion.3
  57.0 1.4 %fusion.14 = f32[8,128,256]{2,1,0:T(8,128)S(1)} fusion(f32[8,128,256]{2,1,0:T(8,128)S(1)} %convolution_bitcast_fusion, f32[8,128,256]{2,1,0:T(8,128)S(1)} %convolution_bitcast_fusion.1, bf16[8,4,128,64]{2,3,1,0:T(8,128)(2,1)} %convolution_convert_fusion.3, bf16[256,4,64,1]{0,2,1,3:T(8,128)(2,1)S(1)} %bitcast.206), kind=kOutput, calls=%fused_computation.33 | convolution fusion | flops 134742016 | bytes 3801088 | tf_op jit(solution)/shard_map/ghid,chd->gic/dot_general | solution.py:227
  59.1 1.9 %collective-permute-start.6 = (bf16[4,64,256]{2,1,0:T(8,128)(2,1)S(1)}, bf16[4,64,256]{2,1,0:T(8,128)(2,1)S(1)}, u32[]{:S(2)}, u32[]{:S(2)}) collective-permute-start(bf16[4,64,256]{2,1,0:T(8,128)(2,1)S(1)} %get-tuple-element.23), channel_id=1, source_target_pairs={{0,24},{8,0},{16,8},{24,16},{1,25},{9,1},{17,9},{25,17},{2,26},{10... | collective-permute-start | bytes 393224 | tf_op jit(solution)/shard_map/ppermute | solution.py:97
  60.9 1.1 collective-permute-start.5
  62.0 1.9 %collective-permute-start.4 = (bf16[4,64,256]{2,1,0:T(8,128)(2,1)S(1)}, bf16[4,64,256]{2,1,0:T(8,128)(2,1)S(1)}, u32[]{:S(2)}, u32[]{:S(2)}) collective-permute-start(bf16[4,64,256]{2,1,0:T(8,128)(2,1)S(1)} %get-tuple-element.25), channel_id=1, source_target_pairs={{0,8},{8,16},{16,24},{24,0},{1,9},{9,17},{17,25},{25,1},{2,10},{10... | collective-permute-start | bytes 393224 | tf_op jit(solution)/shard_map/ppermute | solution.py:97
  65.0 8.3 %collective-permute-done.5 = bf16[4,64,256]{2,1,0:T(8,128)(2,1)S(1)} collective-permute-done((bf16[4,64,256]{2,1,0:T(8,128)(2,1)S(1)}, bf16[4,64,256]{2,1,0:T(8,128)(2,1)S(1)}, u32[]{:S(2)}, u32[]{:S(2)}) %collective-permute-start.5) | collective-permute-done | bytes 131104 | tf_op jit(solution)/shard_map/ppermute | solution.py:97
  74.1 1.7 %fusion.22 = bf16[4,256,256]{2,1,0:T(8,128)(2,1)S(1)} fusion(f32[4,256,256]{2,1,0:T(8,128)} %get-tuple-element.41, bf16[4,64,256]{2,1,0:T(8,128)(2,1)S(1)} %get-tuple-element.19, bf16[4,64,256]{2,1,0:T(8,128)(2,1)S(1)} %get-tuple-element.20, bf16[4,64,256]{2,1,0:T(8,128)(2,1)S(1)} %get-tuple-element.21, bf16[4,64,256]{2,1,0:T(8,128)(2,1)S(1)} %get-tuple-element.18), kind=kLoop, calls=%fused_computation.52 | loop fusion | flops 4456448 | bytes 2097152 | tf_op jit(solution)/shard_map/convert_element_type | solution.py:316
  77.6 1.8 %collective-permute-done.7 = f32[131072]{0:T(1024)S(1)} collective-permute-done((f32[131072]{0:T(1024)}, f32[131072]{0:T(1024)S(1)}, u32[]{:S(2)}, u32[]{:S(2)}) %collective-permute-start.7) | collective-permute-done | bytes 524320 | tf_op jit(solution)/shard_map/ppermute | solution.py:33
  80.2 1.5 %collective-permute-start.10 = (f32[32768]{0:T(1024)S(1)}, f32[32768]{0:T(1024)S(1)}, u32[]{:S(2)}, u32[]{:S(2)}) collective-permute-start(f32[32768]{0:T(1024)S(1)} %bitcast.223), channel_id=1, source_target_pairs={{0,6},{1,7},{2,0},{3,1},{4,2},{5,3},{6,4},{7,5},{8,14},{9,15},{10,... | collective-permute-start | bytes 393224 | tf_op jit(solution)/shard_map/ppermute | solution.py:37
  82.3 1.5 %collective-permute-start.9 = (f32[32768]{0:T(1024)S(1)}, f32[32768]{0:T(1024)S(1)}, u32[]{:S(2)}, u32[]{:S(2)}) collective-permute-start(f32[32768]{0:T(1024)S(1)} %bitcast.219), channel_id=1, source_target_pairs={{0,4},{1,5},{2,6},{3,7},{4,0},{5,1},{6,2},{7,3},{8,12},{9,13},{10,... | collective-permute-start | bytes 393224 | tf_op jit(solution)/shard_map/ppermute | solution.py:37
  83.8 2.1 %fusion.64 = f32[4,384,256]{2,1,0:T(8,128)S(1)} fusion(bf16[4,256,384]{2,1,0:T(8,128)(2,1)} %copy-done.8, f32[4,256,256]{2,1,0:T(8,128)S(1)} %convolution_multiply_fusion), kind=kOutput, calls=%fused_computation.176 | convolution fusion | flops 1207959552 | bytes 3407872 | tf_op jit(solution)/shard_map/drs,drh->dsh/dot_general | solution.py:325
  86.6 1.7 %collective-permute-start.14 = (bf16[4,128,256]{2,1,0:T(8,128)(2,1)}, bf16[4,128,256]{2,1,0:T(8,128)(2,1)}, u32[]{:S(2)}, u32[]{:S(2)}) collective-permute-start(bf16[4,128,256]{2,1,0:T(8,128)(2,1)} %slice.101), channel_id=1, source_target_pairs={{0,7},{1,0},{2,1},{3,2},{4,3},{5,4},{6,5},{7,6},{8,15},{9,8},{10,9... | collective-permute-start | bytes 786440 | tf_op jit(solution)/shard_map/ppermute | solution.py:12
  88.4 1.3 %collective-permute-done.8 = f32[32768]{0:T(1024)S(1)} collective-permute-done((f32[32768]{0:T(1024)S(1)}, f32[32768]{0:T(1024)S(1)}, u32[]{:S(2)}, u32[]{:S(2)}) %collective-permute-start.8) | collective-permute-done | bytes 131104 | tf_op jit(solution)/shard_map/ppermute | solution.py:37
  90.6 2.0 %collective-permute-start.11 = (f32[8192]{0:T(1024)S(1)}, f32[8192]{0:T(1024)S(1)}, u32[]{:S(2)}, u32[]{:S(2)}) collective-permute-start(f32[8192]{0:T(1024)S(1)} %bitcast.229), channel_id=1, source_target_pairs={{0,8},{8,16},{16,24},{24,0},{1,9},{9,17},{17,25},{25,1},{2,10},{10... | collective-permute-start | bytes 98312 | tf_op jit(solution)/shard_map/ppermute | solution.py:37
  92.6 1.1 collective-permute-start.12
  93.8 2.2 %convolution_add_fusion.1 = f32[4,256,256]{2,1,0:T(8,128)} fusion(bf16[4,128,256]{2,1,0:T(8,128)(2,1)} %collective-permute-done.14, f32[4,256,256]{2,1,0:T(8,128)S(1)} %convolution_multiply_fusion, f32[4,384,256]{2,1,0:T(8,128)S(1)} %fusion.64, s32[4,128]{1,0:T(4,128)S(1)} %copy-done.19, pred[4,128]{1,0:T(4,128)(4,1)S(1)} %iota_compare_fusion.10, ...), kind=kOutput, calls=%fused_computation.27 | convolution fusion | flops 70254592 | bytes 3934720 | tf_op jit(solution)/shard_map/dsn,dsh->dnh/dot_general | solution.py:335
  96.4 1.1 collective-permute-done.12
  97.5 2.2 %collective-permute-start.17 = (f32[8192]{0:T(1024)S(1)}, f32[8192]{0:T(1024)S(1)}, u32[]{:S(2)}, u32[]{:S(2)}) collective-permute-start(f32[8192]{0:T(1024)S(1)} %add_add_fusion.1), channel_id=1, source_target_pairs={{0,24},{8,0},{16,8},{24,16},{1,25},{9,1},{17,9},{25,17},{2,26},{10... | collective-permute-start | bytes 98312 | tf_op jit(solution)/shard_map/ppermute | solution.py:49
  99.7 1.0 collective-permute-start.15
  100.8 1.1 collective-permute-done.17
  101.8 2.7 %collective-permute-done.16 = f32[8192]{0:T(1024)S(1)} collective-permute-done((f32[8192]{0:T(1024)S(1)}, f32[8192]{0:T(1024)S(1)}, u32[]{:S(2)}, u32[]{:S(2)}) %collective-permute-start.16) | collective-permute-done | bytes 32800 | tf_op jit(solution)/shard_map/ppermute | solution.py:49
  106.3 1.2 collective-permute-start.20
  107.5 1.5 %collective-permute-start.19 = (f32[32768]{0:T(1024)S(1)}, f32[32768]{0:T(1024)S(1)}, u32[]{:S(2)}, u32[]{:S(2)}) collective-permute-start(f32[32768]{0:T(1024)S(1)} %bitcast.212), channel_id=1, source_target_pairs={{0,4},{1,5},{2,6},{3,7},{4,0},{5,1},{6,2},{7,3},{8,12},{9,13},{10,... | collective-permute-start | bytes 393224 | tf_op jit(solution)/shard_map/ppermute | solution.py:49
  110.0 1.3 %collective-permute-done.20 = f32[32768]{0:T(1024)S(1)} collective-permute-done((f32[32768]{0:T(1024)S(1)}, f32[32768]{0:T(1024)S(1)}, u32[]{:S(2)}, u32[]{:S(2)}) %collective-permute-start.20) | collective-permute-done | bytes 131104 | tf_op jit(solution)/shard_map/ppermute | solution.py:49
  111.3 1.1 collective-permute-done.19
  112.4 2.4 %collective-permute-done.18 = f32[32768]{0:T(1024)S(1)} collective-permute-done((f32[32768]{0:T(1024)S(1)}, f32[32768]{0:T(1024)S(1)}, u32[]{:S(2)}, u32[]{:S(2)}) %collective-permute-start.18) | collective-permute-done | bytes 131104 | tf_op jit(solution)/shard_map/ppermute | solution.py:49
  117.0 1.3 %collective-permute-done.21 = f32[131072]{0:T(1024)S(1)} collective-permute-done((f32[131072]{0:T(1024)S(1)}, f32[131072]{0:T(1024)S(1)}, u32[]{:S(2)}, u32[]{:S(2)}) %collective-permute-start.21) | collective-permute-done | bytes 524320 | tf_op jit(solution)/shard_map/ppermute | solution.py:44
  118.6 1.0 fusion.62
  (125 shorter events, 20.2 us)
Async XLA Ops:
  0.6 10.1 %copy-start = (bf16[256,256]{1,0:T(8,128)(2,1)S(1)}, bf16[256,256]{1,0:T(8,128)(2,1)}, u32[]{:S(2)}) copy-start(bf16[256,256]{1,0:T(8,128)(2,1)} %param.17) | copy-start | bytes 393220
  2.8 7.4 %collective-permute-start = (bf16[4,128,256]{2,1,0:T(8,128)(2,1)S(1)}, bf16[4,128,256]{2,1,0:T(8,128)(2,1)S(1)}, u32[]{:S(2)}, u32[]{:S(2)}) collective-permute-start(bf16[4,128,256]{2,1,0:T(8,128)(2,1)S(1)} %convolution_convert_fusion.6), channel_id=1, source_target_pairs={{0,1},{1,2},{2,3},{3,4},{4,5},{5,6},{6,7},{7,0},{8,9},{9,10},{10,1... | collective-permute-start | bytes 786440 | tf_op jit(solution)/shard_map/ppermute | solution.py:12
  4.9 5.3 %copy-start.9 = (bf16[4,256,256]{2,1,0:T(8,128)(2,1)S(1)}, bf16[4,256,256]{2,1,0:T(8,128)(2,1)}, u32[]{:S(2)}) copy-start(bf16[4,256,256]{2,1,0:T(8,128)(2,1)} %param.12) | copy-start | bytes 1572868
  7.8 2.9 %copy-start.8 = (bf16[4,256,384]{2,1,0:T(8,128)(2,1)}, bf16[4,256,384]{2,1,0:T(8,128)(2,1)S(1)}, u32[]{:S(2)}) copy-start(bf16[4,256,384]{2,1,0:T(8,128)(2,1)S(1)} %fusion.11) | copy-start | bytes 2359300
  10.7 1.4 %copy-start.10 = (bf16[4,256,256]{2,1,0:T(8,128)(2,1)}, bf16[4,256,256]{2,1,0:T(8,128)(2,1)S(1)}, u32[]{:S(2)}) copy-start(bf16[4,256,256]{2,1,0:T(8,128)(2,1)S(1)} %fusion.15) | copy-start | bytes 1572868
  10.8 6.9 %copy-start.16 = (bf16[256,256]{1,0:T(8,128)(2,1)S(1)}, bf16[256,256]{1,0:T(8,128)(2,1)}, u32[]{:S(2)}) copy-start(bf16[256,256]{1,0:T(8,128)(2,1)} %param.18) | copy-start | bytes 393220
  10.8 7.0 %copy-start.17 = (bf16[256,256]{1,0:T(8,128)(2,1)S(1)}, bf16[256,256]{1,0:T(8,128)(2,1)}, u32[]{:S(2)}) copy-start(bf16[256,256]{1,0:T(8,128)(2,1)} %param.19) | copy-start | bytes 393220
  10.8 7.1 %copy-start.18 = (bf16[256,256]{1,0:T(8,128)(2,1)S(1)}, bf16[256,256]{1,0:T(8,128)(2,1)}, u32[]{:S(2)}) copy-start(bf16[256,256]{1,0:T(8,128)(2,1)} %param.20) | copy-start | bytes 393220
  12.1 5.9 %copy-start.1 = (bf16[16,1,1,64,256]{4,3,2,1,0:T(8,128)(2,1)S(1)}, bf16[16,1,1,64,256]{4,3,2,1,0:T(8,128)(2,1)}, u32[]{:S(2)}) copy-start(bf16[16,1,1,64,256]{4,3,2,1,0:T(8,128)(2,1)} %param.21) | copy-start | bytes 1572868
  12.2 8.3 %collective-permute-start.3 = (bf16[4,64,256]{2,1,0:T(8,128)(2,1)S(1)}, bf16[4,64,256]{2,1,0:T(8,128)(2,1)S(1)}, u32[]{:S(2)}, u32[]{:S(2)}) collective-permute-start(bf16[4,64,256]{2,1,0:T(8,128)(2,1)S(1)} %get-tuple-element.31), channel_id=1, source_target_pairs={{0,24},{8,0},{16,8},{24,16},{1,25},{9,1},{17,9},{25,17},{2,26},{10... | collective-permute-start | bytes 393224 | tf_op jit(solution)/shard_map/ppermute | solution.py:97
  16.6 11.2 %collective-permute-start.2 = (bf16[4,64,256]{2,1,0:T(8,128)(2,1)S(1)}, bf16[4,64,256]{2,1,0:T(8,128)(2,1)S(1)}, u32[]{:S(2)}, u32[]{:S(2)}) collective-permute-start(bf16[4,64,256]{2,1,0:T(8,128)(2,1)S(1)} %get-tuple-element.32), channel_id=1, source_target_pairs={{0,16},{8,24},{16,0},{24,8},{1,17},{9,25},{17,1},{25,9},{2,18},{10... | collective-permute-start | bytes 393224 | tf_op jit(solution)/shard_map/ppermute | solution.py:97
  16.6 11.2 %collective-permute-start.1 = (bf16[4,64,256]{2,1,0:T(8,128)(2,1)S(1)}, bf16[4,64,256]{2,1,0:T(8,128)(2,1)S(1)}, u32[]{:S(2)}, u32[]{:S(2)}) collective-permute-start(bf16[4,64,256]{2,1,0:T(8,128)(2,1)S(1)} %get-tuple-element.33), channel_id=1, source_target_pairs={{0,8},{8,16},{16,24},{24,0},{1,9},{9,17},{17,25},{25,1},{2,10},{10... | collective-permute-start | bytes 393224 | tf_op jit(solution)/shard_map/ppermute | solution.py:97
  29.6 4.3 %copy-start.14 = (bf16[8,4,128,64]{2,3,1,0:T(8,128)(2,1)}, bf16[8,4,128,64]{2,3,1,0:T(8,128)(2,1)S(1)}, u32[]{:S(2)}) copy-start(bf16[8,4,128,64]{2,3,1,0:T(8,128)(2,1)S(1)} %fusion.16) | copy-start | bytes 1572868
  41.6 7.6 %copy-start.12 = (bf16[8,4,128,64]{2,3,1,0:T(8,128)(2,1)}, bf16[8,4,128,64]{2,3,1,0:T(8,128)(2,1)S(1)}, u32[]{:S(2)}) copy-start(bf16[8,4,128,64]{2,3,1,0:T(8,128)(2,1)S(1)} %convolution_convert_fusion.5) | copy-start | bytes 1572868
  41.6 5.2 %copy-start.13 = (bf16[8,4,128,64]{2,3,1,0:T(8,128)(2,1)S(1)}, bf16[8,4,128,64]{2,3,1,0:T(8,128)(2,1)}, u32[]{:S(2)}) copy-start(bf16[8,4,128,64]{2,3,1,0:T(8,128)(2,1)} %convolution_convert_fusion.4) | copy-start | bytes 1572868
  55.9 2.5 %copy-start.2 = (bf16[16,1,1,64,256]{4,3,2,1,0:T(8,128)(2,1)S(1)}, bf16[16,1,1,64,256]{4,3,2,1,0:T(8,128)(2,1)}, u32[]{:S(2)}) copy-start(bf16[16,1,1,64,256]{4,3,2,1,0:T(8,128)(2,1)} %param.21) | copy-start | bytes 1572868
  58.4 5.6 %copy-start.7 = (f32[65536]{0:T(1024)S(1)}, f32[65536]{0:T(1024)}, u32[]{:S(2)}) copy-start(f32[65536]{0:T(1024)} %reshape_reshape.15) | copy-start | bytes 786436
  58.4 5.6 %copy-start.15 = (bf16[8,4,128,64]{2,3,1,0:T(8,128)(2,1)S(1)}, bf16[8,4,128,64]{2,3,1,0:T(8,128)(2,1)}, u32[]{:S(2)}) copy-start(bf16[8,4,128,64]{2,3,1,0:T(8,128)(2,1)} %convolution_convert_fusion.3) | copy-start | bytes 1572868
  59.1 5.9 %collective-permute-start.6 = (bf16[4,64,256]{2,1,0:T(8,128)(2,1)S(1)}, bf16[4,64,256]{2,1,0:T(8,128)(2,1)S(1)}, u32[]{:S(2)}, u32[]{:S(2)}) collective-permute-start(bf16[4,64,256]{2,1,0:T(8,128)(2,1)S(1)} %get-tuple-element.23), channel_id=1, source_target_pairs={{0,24},{8,0},{16,8},{24,16},{1,25},{9,1},{17,9},{25,17},{2,26},{10... | collective-permute-start | bytes 393224 | tf_op jit(solution)/shard_map/ppermute | solution.py:97
  60.9 12.3 %collective-permute-start.5 = (bf16[4,64,256]{2,1,0:T(8,128)(2,1)S(1)}, bf16[4,64,256]{2,1,0:T(8,128)(2,1)S(1)}, u32[]{:S(2)}, u32[]{:S(2)}) collective-permute-start(bf16[4,64,256]{2,1,0:T(8,128)(2,1)S(1)} %get-tuple-element.24), channel_id=1, source_target_pairs={{0,16},{8,24},{16,0},{24,8},{1,17},{9,25},{17,1},{25,9},{2,18},{10... | collective-permute-start | bytes 393224 | tf_op jit(solution)/shard_map/ppermute | solution.py:97
  62.0 11.2 %collective-permute-start.4 = (bf16[4,64,256]{2,1,0:T(8,128)(2,1)S(1)}, bf16[4,64,256]{2,1,0:T(8,128)(2,1)S(1)}, u32[]{:S(2)}, u32[]{:S(2)}) collective-permute-start(bf16[4,64,256]{2,1,0:T(8,128)(2,1)S(1)} %get-tuple-element.25), channel_id=1, source_target_pairs={{0,8},{8,16},{16,24},{24,0},{1,9},{9,17},{17,25},{25,1},{2,10},{10... | collective-permute-start | bytes 393224 | tf_op jit(solution)/shard_map/ppermute | solution.py:97
  73.9 1.9 %copy-start.11 = (bf16[4,256,256]{2,1,0:T(8,128)(2,1)S(1)}, bf16[4,256,256]{2,1,0:T(8,128)(2,1)}, u32[]{:S(2)}) copy-start(bf16[4,256,256]{2,1,0:T(8,128)(2,1)} %copy-done.10) | copy-start | bytes 1572868
  74.1 2.3 %copy-start.3 = (bf16[4,64,256]{2,1,0:T(8,128)(2,1)}, bf16[4,64,256]{2,1,0:T(8,128)(2,1)S(1)}, u32[]{:S(2)}) copy-start(bf16[4,64,256]{2,1,0:T(8,128)(2,1)S(1)} %get-tuple-element.20) | copy-start | bytes 393220
  74.1 2.3 %copy-start.5 = (bf16[4,64,256]{2,1,0:T(8,128)(2,1)}, bf16[4,64,256]{2,1,0:T(8,128)(2,1)S(1)}, u32[]{:S(2)}) copy-start(bf16[4,64,256]{2,1,0:T(8,128)(2,1)S(1)} %get-tuple-element.21) | copy-start | bytes 393220
  77.3 2.1 %collective-permute-start.7 = (f32[131072]{0:T(1024)}, f32[131072]{0:T(1024)S(1)}, u32[]{:S(2)}, u32[]{:S(2)}) collective-permute-start(f32[131072]{0:T(1024)} %broadcast_select_fusion.3), channel_id=1, source_target_pairs={{0,1},{1,0},{2,3},{3,2},{4,5},{5,4},{6,7},{7,6},{8,9},{9,8},{10,11... | collective-permute-start | bytes 1572872 | tf_op jit(solution)/shard_map/ppermute | solution.py:33
  80.2 8.2 %collective-permute-start.10 = (f32[32768]{0:T(1024)S(1)}, f32[32768]{0:T(1024)S(1)}, u32[]{:S(2)}, u32[]{:S(2)}) collective-permute-start(f32[32768]{0:T(1024)S(1)} %bitcast.223), channel_id=1, source_target_pairs={{0,6},{1,7},{2,0},{3,1},{4,2},{5,3},{6,4},{7,5},{8,14},{9,15},{10,... | collective-permute-start | bytes 393224 | tf_op jit(solution)/shard_map/ppermute | solution.py:37
  81.7 8.0 %collective-permute-start.8 = (f32[32768]{0:T(1024)S(1)}, f32[32768]{0:T(1024)S(1)}, u32[]{:S(2)}, u32[]{:S(2)}) collective-permute-start(f32[32768]{0:T(1024)S(1)} %bitcast.221), channel_id=1, source_target_pairs={{0,2},{1,3},{2,4},{3,5},{4,6},{5,7},{6,0},{7,1},{8,10},{9,11},{10,... | collective-permute-start | bytes 393224 | tf_op jit(solution)/shard_map/ppermute | solution.py:37
  82.3 11.5 %copy-start.4 = (bf16[4,64,256]{2,1,0:T(8,128)(2,1)S(1)}, bf16[4,64,256]{2,1,0:T(8,128)(2,1)}, u32[]{:S(2)}) copy-start(bf16[4,64,256]{2,1,0:T(8,128)(2,1)} %copy-done.3) | copy-start | bytes 393220
  82.3 11.5 %copy-start.6 = (bf16[4,64,256]{2,1,0:T(8,128)(2,1)S(1)}, bf16[4,64,256]{2,1,0:T(8,128)(2,1)}, u32[]{:S(2)}) copy-start(bf16[4,64,256]{2,1,0:T(8,128)(2,1)} %copy-done.5) | copy-start | bytes 393220
  82.3 11.5 %copy-start.19 = (s32[4,128]{1,0:T(4,128)S(1)}, s32[4,128]{1,0:T(4,128)}, u32[]{:S(2)}) copy-start(s32[4,128]{1,0:T(4,128)} %param.15) | copy-start | bytes 6148
  82.3 8.1 %collective-permute-start.9 = (f32[32768]{0:T(1024)S(1)}, f32[32768]{0:T(1024)S(1)}, u32[]{:S(2)}, u32[]{:S(2)}) collective-permute-start(f32[32768]{0:T(1024)S(1)} %bitcast.219), channel_id=1, source_target_pairs={{0,4},{1,5},{2,6},{3,7},{4,0},{5,1},{6,2},{7,3},{8,12},{9,13},{10,... | collective-permute-start | bytes 393224 | tf_op jit(solution)/shard_map/ppermute | solution.py:37
  86.6 7.1 %collective-permute-start.14 = (bf16[4,128,256]{2,1,0:T(8,128)(2,1)}, bf16[4,128,256]{2,1,0:T(8,128)(2,1)}, u32[]{:S(2)}, u32[]{:S(2)}) collective-permute-start(bf16[4,128,256]{2,1,0:T(8,128)(2,1)} %slice.101), channel_id=1, source_target_pairs={{0,7},{1,0},{2,1},{3,2},{4,3},{5,4},{6,5},{7,6},{8,15},{9,8},{10,9... | collective-permute-start | bytes 786440 | tf_op jit(solution)/shard_map/ppermute | solution.py:12
  90.6 5.4 %collective-permute-start.13 = (f32[8192]{0:T(1024)S(1)}, f32[8192]{0:T(1024)S(1)}, u32[]{:S(2)}, u32[]{:S(2)}) collective-permute-start(f32[8192]{0:T(1024)S(1)} %bitcast.230), channel_id=1, source_target_pairs={{0,24},{8,0},{16,8},{24,16},{1,25},{9,1},{17,9},{25,17},{2,26},{10... | collective-permute-start | bytes 98312 | tf_op jit(solution)/shard_map/ppermute | solution.py:37
  90.6 5.8 %collective-permute-start.11 = (f32[8192]{0:T(1024)S(1)}, f32[8192]{0:T(1024)S(1)}, u32[]{:S(2)}, u32[]{:S(2)}) collective-permute-start(f32[8192]{0:T(1024)S(1)} %bitcast.229), channel_id=1, source_target_pairs={{0,8},{8,16},{16,24},{24,0},{1,9},{9,17},{17,25},{25,1},{2,10},{10... | collective-permute-start | bytes 98312 | tf_op jit(solution)/shard_map/ppermute | solution.py:37
  92.6 4.9 %collective-permute-start.12 = (f32[8192]{0:T(1024)S(1)}, f32[8192]{0:T(1024)S(1)}, u32[]{:S(2)}, u32[]{:S(2)}) collective-permute-start(f32[8192]{0:T(1024)S(1)} %bitcast.228), channel_id=1, source_target_pairs={{0,16},{8,24},{16,0},{24,8},{1,17},{9,25},{17,1},{25,9},{2,18},{10... | collective-permute-start | bytes 98312 | tf_op jit(solution)/shard_map/ppermute | solution.py:37
  97.5 4.3 %collective-permute-start.17 = (f32[8192]{0:T(1024)S(1)}, f32[8192]{0:T(1024)S(1)}, u32[]{:S(2)}, u32[]{:S(2)}) collective-permute-start(f32[8192]{0:T(1024)S(1)} %add_add_fusion.1), channel_id=1, source_target_pairs={{0,24},{8,0},{16,8},{24,16},{1,25},{9,1},{17,9},{25,17},{2,26},{10... | collective-permute-start | bytes 98312 | tf_op jit(solution)/shard_map/ppermute | solution.py:49
  99.7 4.8 %collective-permute-start.16 = (f32[8192]{0:T(1024)S(1)}, f32[8192]{0:T(1024)S(1)}, u32[]{:S(2)}, u32[]{:S(2)}) collective-permute-start(f32[8192]{0:T(1024)S(1)} %add_add_fusion.1), channel_id=1, source_target_pairs={{0,16},{8,24},{16,0},{24,8},{1,17},{9,25},{17,1},{25,9},{2,18},{10... | collective-permute-start | bytes 98312 | tf_op jit(solution)/shard_map/ppermute | solution.py:49
  99.7 5.7 %collective-permute-start.15 = (f32[8192]{0:T(1024)S(1)}, f32[8192]{0:T(1024)S(1)}, u32[]{:S(2)}, u32[]{:S(2)}) collective-permute-start(f32[8192]{0:T(1024)S(1)} %add_add_fusion.1), channel_id=1, source_target_pairs={{0,8},{8,16},{16,24},{24,0},{1,9},{9,17},{17,25},{25,1},{2,10},{10... | collective-permute-start | bytes 98312 | tf_op jit(solution)/shard_map/ppermute | solution.py:49
  106.3 5.0 %collective-permute-start.20 = (f32[32768]{0:T(1024)S(1)}, f32[32768]{0:T(1024)S(1)}, u32[]{:S(2)}, u32[]{:S(2)}) collective-permute-start(f32[32768]{0:T(1024)S(1)} %bitcast.211), channel_id=1, source_target_pairs={{0,6},{1,7},{2,0},{3,1},{4,2},{5,3},{6,4},{7,5},{8,14},{9,15},{10,... | collective-permute-start | bytes 393224 | tf_op jit(solution)/shard_map/ppermute | solution.py:49
  107.5 5.0 %collective-permute-start.19 = (f32[32768]{0:T(1024)S(1)}, f32[32768]{0:T(1024)S(1)}, u32[]{:S(2)}, u32[]{:S(2)}) collective-permute-start(f32[32768]{0:T(1024)S(1)} %bitcast.212), channel_id=1, source_target_pairs={{0,4},{1,5},{2,6},{3,7},{4,0},{5,1},{6,2},{7,3},{8,12},{9,13},{10,... | collective-permute-start | bytes 393224 | tf_op jit(solution)/shard_map/ppermute | solution.py:49
  108.9 5.9 %collective-permute-start.18 = (f32[32768]{0:T(1024)S(1)}, f32[32768]{0:T(1024)S(1)}, u32[]{:S(2)}, u32[]{:S(2)}) collective-permute-start(f32[32768]{0:T(1024)S(1)} %bitcast.213), channel_id=1, source_target_pairs={{0,2},{1,3},{2,4},{3,5},{4,6},{5,7},{6,0},{7,1},{8,10},{9,11},{10,... | collective-permute-start | bytes 393224 | tf_op jit(solution)/shard_map/ppermute | solution.py:49
  116.3 2.0 %collective-permute-start.21 = (f32[131072]{0:T(1024)S(1)}, f32[131072]{0:T(1024)S(1)}, u32[]{:S(2)}, u32[]{:S(2)}) collective-permute-start(f32[131072]{0:T(1024)S(1)} %bitcast.208), channel_id=1, source_target_pairs={{0,1},{1,0},{2,3},{3,2},{4,5},{5,4},{6,7},{7,6},{8,9},{9,8},{10,11... | collective-permute-start | bytes 1572872 | tf_op jit(solution)/shard_map/ppermute | solution.py:44
